TPU v7x, 32 devices: a whole 2x2x4 slice. The times are simulated.
32 devices in a mesh: grp: 2 (over y), aux: 16 (over z, x, core).
Axes of the slice: x: 2, y: 2, z: 4, core: 2. Of those that a mesh axis runs over, the one named last changes fastest.
Arguments:
- rhs: float32 [512, 2, 1024], P(('grp', 'aux')), parts along dimension 0, may hold values from -6 to 6
- occ_energy: float32 [512], P('grp'), parts along dimension 0, may hold values from -1.5 to -0.3
- vir_energy: float32 [2048], P('grp'), parts along dimension 0, may hold values from 0.2 to 3
- occ_ints: bfloat16 [128, 256, 256], P(('grp', 'aux')), parts along dimension 0, may hold values from -0.046875 to 0.046875
- vir_ints: bfloat16 [128, 1024, 1024], P(('grp', 'aux')), parts along dimension 0, may hold values from -0.1875 to 0.1875
Outputs:
- response: float32 [512, 2, 1024], P(('grp', 'aux')), parts along dimension 0
There are 2 independent parts, one for each index of `grp`. A program takes and returns all parts, laid end to end along the dimension named above; each array names one. Nothing has to cross between parts.
All inputs are finite; a program needn't handle non-finite values.
Results may differ from a plain program's by a relative error of at most 0.0015.
Values may be sent and summed in bfloat16 or wider, within the bound.
No kernel may reach another device: no remote copies, remote signals or barrier semaphores. Data moves between devices by JAX's collectives and lax.ppermute only.
A program may use at most 64 MiB of HBM per device.

v0:
```python
import jax
import jax.numpy as jnp
from jax import lax
from jax.sharding import PartitionSpec as P

ITERS = 2


def shards(rhs, occ_energy, vir_energy, occ_ints, vir_ints):
    own_rows = rhs.shape[0]
    states = rhs.shape[1]
    nvir = rhs.shape[2]
    local_aux = occ_ints.shape[0]
    nocc = occ_ints.shape[1]
    position = lax.axis_index("aux")
    my_occ = lax.dynamic_slice_in_dim(occ_energy, position * own_rows, own_rows, 0)
    denom = vir_energy[None, None, :] - my_occ[:, None, None]
    response = rhs / denom
    for step in range(ITERS):
        rounded = response.astype(jnp.bfloat16)
        piece = lax.all_gather(rounded, "aux", axis=0, tiled=True)
        count = piece.shape[0]
        flat = piece.reshape(count, states * nvir)
        half = jnp.einsum("pij,jk->pik", occ_ints, flat, preferred_element_type=jnp.float32)
        half = half.astype(jnp.bfloat16).reshape(local_aux, nocc, states, nvir)
        exchange = lax.psum_scatter(
            lax.dot_general(
                half, vir_ints, (((0, 3), (0, 2)), ((), ())), preferred_element_type=jnp.float32
            ),
            "aux",
            scatter_dimension=0,
            tiled=True,
        )
        response = 0.4 * response + 0.6 * (rhs - exchange) / denom
    return response


def solution(mesh):
    in_specs = (
        P(("grp", "aux"), None, None),
        P("grp"),
        P("grp"),
        P(("grp", "aux"), None, None),
        P(("grp", "aux"), None, None),
    )
    out_specs = P(("grp", "aux"), None, None)
    return jax.shard_map(shards, mesh=mesh, in_specs=in_specs, out_specs=out_specs, check_vma=False)
```

profile of v0, /device:TPU:0, one launch (start us, length us, event | category | flops | bytes accessed | tf_op | source)
XLA Modules:
  0.0 241.8 jit_solution(5597992553866525456)
XLA Ops:
  6.5 0.0 copy-start
  6.5 0.0 all-gather.3.cloned.1.call-start
  6.5 0.8 dynamic_slice.3
  7.3 0.8 broadcast_subtract_fusion
  8.1 1.6 fusion.10
  9.7 0.0 all-gather.3.cloned.1.call-update
  9.7 0.0 reduce-scatter.3.cloned.1.call-start
  9.8 40.8 %all-gather.3.cloned.1.call-done = bf16[256,2,1024]{2,0,1:T(8,128)(2,1)} async-done(((bf16[16,2,1024]{2,0,1:T(8,128)(2,1)}), bf16[256,2,1024]{2,0,1:T(8,128)(2,1)}) %all-gather.3.cloned.1.call-update) | async-done | bytes 1048592 | tf_op jit(solution)/shard_map/all_gather | solution.py:21
  50.5 1.5 copy.14
  52.0 0.0 copy-done
  52.0 1.3 convolution_convert_fusion.1
  53.3 0.0 copy-start.1
  53.3 8.4 %fusion.4 = f32[256,2,1024]{2,0,1:T(8,128)} fusion(bf16[4,256,2,1024]{1,3,2,0:T(8,128)(2,1)S(1)} %bitcast.33, bf16[4,1024,1024]{2,1,0:T(8,128)(2,1)} %param.9), kind=kOutput, calls=%fused_computation.6 | convolution fusion | flops 4294967296 | bytes 14680064 | tf_op jit(solution)/shard_map/dot_general | solution.py:27
  61.7 0.0 reduce-scatter.3.cloned.1.call-update
  61.7 0.0 all-gather.5.cloned.1.call-start
  61.8 60.6 %reduce-scatter.3.cloned.1.call-done = f32[16,2,1024]{2,0,1:T(8,128)} async-done(((f32[256,2,1024]{2,0,1:T(8,128)}), f32[16,2,1024]{2,0,1:T(8,128)}) %reduce-scatter.3.cloned.1.call-update) | async-done | bytes 131088 | tf_op jit(solution)/shard_map/reduce_scatter | solution.py:26
  122.3 0.0 copy-done.1
  122.3 1.6 fusion.11
  123.9 0.0 all-gather.5.cloned.1.call-update
  124.0 0.0 reduce-scatter.5.cloned.1.call-start
  124.0 37.8 %all-gather.5.cloned.1.call-done = bf16[256,2,1024]{2,0,1:T(8,128)(2,1)} async-done(((bf16[16,2,1024]{2,0,1:T(8,128)(2,1)}), bf16[256,2,1024]{2,0,1:T(8,128)(2,1)}) %all-gather.5.cloned.1.call-update) | async-done | bytes 1048592 | tf_op jit(solution)/shard_map/all_gather | solution.py:21
  161.8 1.5 copy.17
  163.3 1.3 convolution_convert_fusion
  164.5 0.0 copy-start.2
  164.6 8.4 %fusion.7 = f32[256,2,1024]{2,0,1:T(8,128)} fusion(bf16[4,256,2,1024]{1,3,2,0:T(8,128)(2,1)S(1)} %bitcast.34, bf16[4,1024,1024]{2,1,0:T(8,128)(2,1)} %param.9), kind=kOutput, calls=%fused_computation.7 | convolution fusion | flops 4294967296 | bytes 14680064 | tf_op jit(solution)/shard_map/dot_general | solution.py:27
  172.9 0.0 reduce-scatter.5.cloned.1.call-update
  172.9 60.6 %reduce-scatter.5.cloned.1.call-done = f32[16,2,1024]{2,0,1:T(8,128)} async-done(((f32[256,2,1024]{2,0,1:T(8,128)}), f32[16,2,1024]{2,0,1:T(8,128)}) %reduce-scatter.5.cloned.1.call-update) | async-done | bytes 131088 | tf_op jit(solution)/shard_map/reduce_scatter | solution.py:26
  233.5 0.0 copy-done.2
  233.5 1.0 divide_add_fusion
  234.5 0.8 copy.20
Async XLA Ops:
  6.5 45.5 %copy-start = (bf16[4,256,256]{2,1,0:T(8,128)(2,1)S(1)}, bf16[4,256,256]{2,1,0:T(8,128)(2,1)}, u32[]{:S(2)}) copy-start(bf16[4,256,256]{2,1,0:T(8,128)(2,1)} %param.8) | copy-start | bytes 1572868
  6.5 44.0 %all-gather.3.cloned.1.call-start = ((), (), s32[]{:S(2)}) async-start(), calls=%async_computation.2 | async-start | bytes 1114112 | tf_op jit(solution)/shard_map/all_gather | solution.py:21
  9.7 112.6 %reduce-scatter.3.cloned.1.call-start = ((), (), s32[]{:S(2)}) async-start(), calls=%async_computation.3 | async-start | bytes 2228224 | tf_op jit(solution)/shard_map/reduce_scatter | solution.py:26
  53.3 69.0 %copy-start.1 = (f32[16,2,1024]{2,1,0:T(2,128)S(1)}, f32[16,2,1024]{2,1,0:T(2,128)}, u32[]{:S(2)}) copy-start(f32[16,2,1024]{2,1,0:T(2,128)} %param.5) | copy-start | bytes 393220
  61.7 100.1 %all-gather.5.cloned.1.call-start = ((), (), s32[]{:S(2)}) async-start(), calls=%async_computation.4 | async-start | bytes 1114112 | tf_op jit(solution)/shard_map/all_gather | solution.py:21
  124.0 109.6 %reduce-scatter.5.cloned.1.call-start = ((), (), s32[]{:S(2)}) async-start(), calls=%async_computation.5 | async-start | bytes 2228224 | tf_op jit(solution)/shard_map/reduce_scatter | solution.py:26
  164.5 69.0 %copy-start.2 = (f32[16,2,1024]{2,0,1:T(8,128)S(1)}, f32[16,2,1024]{2,0,1:T(8,128)}, u32[]{:S(2)}) copy-start(f32[16,2,1024]{2,0,1:T(8,128)} %reduce-scatter.3.cloned.1.call-done) | copy-start | bytes 393220
Sparse Core Ops, SparseCore 0:
  9.8 40.6 all-gather.2
  61.8 60.4 reduce-scatter.2
  124.8 36.9 all-gather.4
  173.1 60.4 reduce-scatter.4
where the time goes:
time: 242 us
  waiting for transfers between devices  200 us (83%)
  matrix products  19.3 us (8%)
  between operations  13.2 us (5%)
  other arithmetic  4.91 us (2%)
  local copies, waits for them, and re-layouts  4.53 us (2%)
    reduce_scatter x2, waiting for transfers between devices, shards(): lax.psum_scatter(lax.dot_general(half, vir_ints, (((0, 3), (0, 2)), ((),...  121 us
    all_gather x2, waiting for transfers between devices, shards(): piece = lax.all_gather(rounded, 'aux', axis=0, tiled=True)  78.5 us
    dot_general x2, matrix products, shards(): lax.dot_general(half, vir_ints, (((0, 3), (0, 2)), ((), ())), preferred_e...  16.7 us
  transfers between devices with their start and end apart: 4, of which 4 were waited for; matrix products, arithmetic and copies ran while one was open for 0% of the time, Pallas kernels for 0%

commit v1 on v0

v1 whole, which is shorter than its diff:
```python
import jax
import jax.numpy as jnp
from jax import lax
from jax.sharding import PartitionSpec as P

ITERS = 2


def gather_rows(x, n):
    me = lax.axis_index("aux")
    acc = x[None]
    k = n.bit_length() - 2
    while k >= 0:
        bit = (me >> k) & 1
        theirs = lax.ppermute(acc, "aux", [(d, d ^ (1 << k)) for d in range(n)])
        lo = jnp.where(bit == 0, acc, theirs)
        hi = jnp.where(bit == 0, theirs, acc)
        acc = jnp.stack([lo, hi], axis=1).reshape((-1,) + x.shape)
        k -= 1
    return acc.reshape((n * x.shape[0],) + x.shape[1:])


def scatter_sum(part, n):
    me = lax.axis_index("aux")
    rows = part.shape[0] // n
    acc = part.reshape((n, rows) + part.shape[1:])
    k = 0
    while (1 << k) < n:
        bit = (me >> k) & 1
        pairs = acc.reshape((acc.shape[0] // 2, 2) + acc.shape[1:])
        keep = lax.dynamic_index_in_dim(pairs, bit, axis=1, keepdims=False)
        send = lax.dynamic_index_in_dim(pairs, 1 - bit, axis=1, keepdims=False)
        acc = keep + lax.ppermute(send, "aux", [(d, d ^ (1 << k)) for d in range(n)])
        k += 1
    return acc[0]


def shards(rhs, occ_energy, vir_energy, occ_ints, vir_ints):
    own_rows = rhs.shape[0]
    states = rhs.shape[1]
    nvir = rhs.shape[2]
    local_aux = occ_ints.shape[0]
    nocc = occ_ints.shape[1]
    n = nocc // own_rows
    assert n & (n - 1) == 0
    position = lax.axis_index("aux")
    my_occ = lax.dynamic_slice_in_dim(occ_energy, position * own_rows, own_rows, 0)
    denom = vir_energy[None, None, :] - my_occ[:, None, None]
    response = rhs / denom
    for step in range(ITERS):
        rounded = response.astype(jnp.bfloat16)
        piece = gather_rows(rounded, n)
        flat = piece.reshape(nocc, states * nvir)
        half = jnp.einsum("pij,jk->pik", occ_ints, flat, preferred_element_type=jnp.float32)
        half = half.astype(jnp.bfloat16).reshape(local_aux, nocc, states, nvir)
        part = lax.dot_general(
            half, vir_ints, (((0, 3), (0, 2)), ((), ())), preferred_element_type=jnp.float32
        )
        exchange = scatter_sum(part, n)
        response = 0.4 * response + 0.6 * (rhs - exchange) / denom
    return response


def solution(mesh):
    in_specs = (
        P(("grp", "aux"), None, None),
        P("grp"),
        P("grp"),
        P(("grp", "aux"), None, None),
        P(("grp", "aux"), None, None),
    )
    out_specs = P(("grp", "aux"), None, None)
    return jax.shard_map(shards, mesh=mesh, in_specs=in_specs, out_specs=out_specs, check_vma=False)
```

time: 242 us -> 153 us (0.63)
  waiting for transfers between devices: 200 us -> 80.9 us
  starting transfers between devices: 0.13 us -> 24.1 us
  local copies, waits for them, and re-layouts: 4.53 us -> 18.7 us
  between operations: 13.2 us -> 0.32 us
  matrix products: 19.3 us -> 23 us
    reduce_scatter x2 -> x0, waiting for transfers between devices: 121 us -> none  [shards(): lax.psum_scatter(lax.dot_general(half, vir_ints, (((0, 3), (0, 2)), ((),...]
    ppermute x0 -> x16, waiting for transfers between devices: none -> 80.9 us  [the longest x8 52.3 us: scatter_sum(): acc = keep + lax.ppermute(send, 'aux', [(d, d ^ 1 << k) for d in range(n)])]
    all_gather x2 -> x0, waiting for transfers between devices: 78.5 us -> none  [shards(): piece = lax.all_gather(rounded, 'aux', axis=0, tiled=True)]
    ppermute x0 -> x16, starting transfers between devices: none -> 24.1 us  [the longest x8 12.8 us: scatter_sum(): acc = keep + lax.ppermute(send, 'aux', [(d, d ^ 1 << k) for d in range(n)])]
    reshape x0 -> x2, local copies, waits for them, and re-layouts: none -> 12.6 us  [shards(): half = half.astype(jnp.bfloat16).reshape(local_aux, nocc, states, nvir)]
    dot_general x2, matrix products: 2.57 us -> 6.53 us  [shards(): jnp.einsum('pij,jk->pik', occ_ints, flat, preferred_element_type=jnp.floa...]
    convert_element_type x2 -> x0, other arithmetic: 3.17 us -> none  [shards(): rounded = response.astype(jnp.bfloat16)]
    all_gather x2 -> x0, local copies, waits for them, and re-layouts: 2.95 us -> none  [shards(): piece = lax.all_gather(rounded, 'aux', axis=0, tiled=True)]
  transfers between devices with their start and end apart: 4 -> 16, of which waited for: 4 -> 16; matrix products, arithmetic and copies ran while one was open for 0% -> 0% of each run, Pallas kernels for 0% -> 0%
where the time goes in v1:
time: 153 us; the launch traced here: 152 us
  waiting for transfers between devices  80.9 us (53%)
  starting transfers between devices  24.1 us (16%)
  matrix products  23 us (15%)
  local copies, waits for them, and re-layouts  18.7 us (12%)
  other arithmetic  5.3 us (3%)
    ppermute x8, waiting for transfers between devices, scatter_sum(): acc = keep + lax.ppermute(send, 'aux', [(d, d ^ 1 << k) for d in range(n)])  52.3 us
    ppermute x8, waiting for transfers between devices, gather_rows(): theirs = lax.ppermute(acc, 'aux', [(d, d ^ 1 << k) for d in range(n)])  28.6 us
    dot_general x2, matrix products, shards(): lax.dot_general(half, vir_ints, (((0, 3), (0, 2)), ((), ())), preferred_e...  16.4 us
    ppermute x8, starting transfers between devices, scatter_sum(): acc = keep + lax.ppermute(send, 'aux', [(d, d ^ 1 << k) for d in range(n)])  12.8 us
    reshape x2, local copies, waits for them, and re-layouts, shards(): half = half.astype(jnp.bfloat16).reshape(local_aux, nocc, states, nvir)  12.6 us
    ppermute x8, starting transfers between devices, gather_rows(): theirs = lax.ppermute(acc, 'aux', [(d, d ^ 1 << k) for d in range(n)])  11.3 us
    dot_general x2, matrix products, shards(): jnp.einsum('pij,jk->pik', occ_ints, flat, preferred_element_type=jnp.floa...  6.53 us
  transfers between devices with their start and end apart: 16, of which 16 were waited for; matrix products, arithmetic and copies ran while one was open for 0% of the time, Pallas kernels for 0%

profile of v1, /device:TPU:0, one launch (start us, length us, event | category | flops | bytes accessed | tf_op | source)
XLA Modules:
  0.0 152.2 jit_solution(15131103735064309912)
XLA Ops:
  0.0 0.8 dynamic_slice.47
  0.8 0.8 broadcast_subtract_fusion
  1.6 0.9 fusion.25
  2.5 4.1 %collective-permute-start = (bf16[1,16,2,1024]{3,1,2,0:T(8,128)(2,1)S(1)}, bf16[1,16,2,1024]{3,1,2,0:T(8,128)(2,1)S(1)}, u32[]{:S(2)}, u32[]{:S(2)}) collective-permute-start(bf16[1,16,2,1024]{3,1,2,0:T(8,128)(2,1)S(1)} %fusion.25), channel_id=1, source_target_pairs={{0,8},{1,9},{2,10},{3,11},{4,12},{5,13},{6,14},{7,15},{8,0},{9,1},... | collective-permute-start | bytes 196616 | tf_op jit(solution)/shard_map/ppermute | solution.py:15
  6.6 3.6 %collective-permute-done = bf16[1,16,2,1024]{3,1,2,0:T(8,128)(2,1)S(1)} collective-permute-done((bf16[1,16,2,1024]{3,1,2,0:T(8,128)(2,1)S(1)}, bf16[1,16,2,1024]{3,1,2,0:T(8,128)(2,1)S(1)}, u32[]{:S(2)}, u32[]{:S(2)}) %collective-permute-start) | collective-permute-done | bytes 65568 | tf_op jit(solution)/shard_map/ppermute | solution.py:15
  10.3 1.0 select_bitcast_fusion.15
  11.3 0.6 collective-permute-start.1
  11.9 4.4 %collective-permute-done.1 = bf16[2,16,2,1024]{3,1,2,0:T(8,128)(2,1)S(1)} collective-permute-done((bf16[2,16,2,1024]{3,1,2,0:T(8,128)(2,1)S(1)}, bf16[2,16,2,1024]{3,1,2,0:T(8,128)(2,1)S(1)}, u32[]{:S(2)}, u32[]{:S(2)}) %collective-permute-start.1) | collective-permute-done | bytes 131104 | tf_op jit(solution)/shard_map/ppermute | solution.py:15
  16.3 1.8 %collective-permute-start.2 = (bf16[4,16,2,1024]{3,1,2,0:T(8,128)(2,1)S(1)}, bf16[4,16,2,1024]{3,1,2,0:T(8,128)(2,1)S(1)}, u32[]{:S(2)}, u32[]{:S(2)}) collective-permute-start(bf16[4,16,2,1024]{3,1,2,0:T(8,128)(2,1)S(1)} %bitcast.174), channel_id=1, source_target_pairs={{0,2},{1,3},{2,0},{3,1},{4,6},{5,7},{6,4},{7,5},{8,10},{9,11},{10,... | collective-permute-start | bytes 786440 | tf_op jit(solution)/shard_map/ppermute | solution.py:15
  18.1 4.7 %collective-permute-done.2 = bf16[4,16,2,1024]{3,1,2,0:T(8,128)(2,1)S(1)} collective-permute-done((bf16[4,16,2,1024]{3,1,2,0:T(8,128)(2,1)S(1)}, bf16[4,16,2,1024]{3,1,2,0:T(8,128)(2,1)S(1)}, u32[]{:S(2)}, u32[]{:S(2)}) %collective-permute-start.2) | collective-permute-done | bytes 262176 | tf_op jit(solution)/shard_map/ppermute | solution.py:15
  22.8 0.1 select_bitcast_fusion.7
  22.8 0.1 pad_maximum_fusion.2
  23.0 0.1 collective-permute-start.3
  23.0 1.9 %collective-permute-done.3 = bf16[8,16,2,1024]{3,1,2,0:T(8,128)(2,1)S(1)} collective-permute-done((bf16[8,16,2,1024]{3,1,2,0:T(8,128)(2,1)S(1)}, bf16[8,16,2,1024]{3,1,2,0:T(8,128)(2,1)S(1)}, u32[]{:S(2)}, u32[]{:S(2)}) %collective-permute-start.3) | collective-permute-done | bytes 524320 | tf_op jit(solution)/shard_map/ppermute | solution.py:15
  24.9 0.1 select_bitcast_fusion.3
  25.0 0.1 pad_maximum_fusion
  25.1 1.1 copy.30
  26.2 0.3 copy.50
  26.5 3.3 %convolution_convert_fusion.1 = bf16[2048,4,256]{2,0,1:T(8,128)(2,1)} fusion(bf16[4,256,256]{2,1,0:T(8,128)(2,1)S(1)} %copy-done, bf16[256,2048]{1,0:T(8,128)(2,1)S(1)} %bitcast.166), kind=kOutput, calls=%fused_computation.7 | convolution fusion | flops 1075838976 | bytes 5767168 | tf_op jit(solution)/shard_map/pij,jk->pik/dot_general | solution.py:54
  29.8 6.3 %copy.32 = bf16[4,256,2,1024]{3,1,0,2:T(8,128)(2,1)} copy(bf16[4,256,2,1024]{1,3,2,0:T(8,128)(2,1)} %bitcast.156) | data formatting | bytes 8388608 | tf_op jit(solution)/shard_map/reshape | solution.py:55
  36.1 8.2 %fusion.6 = f32[8,2,16,2,1024]{4,2,3,1,0:T(8,128)S(1)} fusion(bf16[4,1024,1024]{2,1,0:T(8,128)(2,1)} %param.9, bf16[8,2,16,2,4,1024]{5,2,1,0,4,3:T(8,128)(2,1)} %bitcast.158), kind=kOutput, calls=%fused_computation.8 | convolution fusion | flops 4294967296 | bytes 14680064 | tf_op jit(solution)/shard_map/dot_general | solution.py:56
  44.3 1.3 copy-done.1
  45.6 0.1 dynamic-slice_bitcast_fusion.1
  45.7 0.2 collective-permute-start.4
  45.9 2.5 %collective-permute-done.4 = f32[8,16,2,1024]{3,1,2,0:T(8,128)S(1)} collective-permute-done((f32[8,16,2,1024]{3,1,2,0:T(8,128)S(1)}, f32[8,16,2,1024]{3,1,2,0:T(8,128)S(1)}, u32[]{:S(2)}, u32[]{:S(2)}) %collective-permute-start.4) | collective-permute-done | bytes 1048608 | tf_op jit(solution)/shard_map/ppermute | solution.py:33
  48.4 1.4 bitcast_add_fusion.1
  49.9 1.8 %collective-permute-start.5 = (f32[4,16,2,1024]{3,1,2,0:T(8,128)S(1)}, f32[4,16,2,1024]{3,1,2,0:T(8,128)S(1)}, u32[]{:S(2)}, u32[]{:S(2)}) collective-permute-start(f32[4,16,2,1024]{3,1,2,0:T(8,128)S(1)} %dynamic-slice_bitcast_fusion.3), channel_id=1, source_target_pairs={{0,2},{1,3},{2,0},{3,1},{4,6},{5,7},{6,4},{7,5},{8,10},{9,11},{10,... | collective-permute-start | bytes 1572872 | tf_op jit(solution)/shard_map/ppermute | solution.py:33
  51.6 12.3 %collective-permute-done.5 = f32[4,16,2,1024]{3,1,2,0:T(8,128)S(1)} collective-permute-done((f32[4,16,2,1024]{3,1,2,0:T(8,128)S(1)}, f32[4,16,2,1024]{3,1,2,0:T(8,128)S(1)}, u32[]{:S(2)}, u32[]{:S(2)}) %collective-permute-start.5) | collective-permute-done | bytes 524320 | tf_op jit(solution)/shard_map/ppermute | solution.py:33
  63.9 0.1 bitcast_add_fusion.3
  64.0 0.8 collective-permute-start.6
  64.9 6.7 %collective-permute-done.6 = f32[2,16,2,1024]{3,1,2,0:T(8,128)S(1)} collective-permute-done((f32[2,16,2,1024]{3,1,2,0:T(8,128)S(1)}, f32[2,16,2,1024]{3,1,2,0:T(8,128)S(1)}, u32[]{:S(2)}, u32[]{:S(2)}) %collective-permute-start.6) | collective-permute-done | bytes 262176 | tf_op jit(solution)/shard_map/ppermute | solution.py:33
  71.7 3.3 %collective-permute-start.7 = (f32[1,16,2,1024]{3,1,2,0:T(8,128)S(1)}, f32[1,16,2,1024]{3,1,2,0:T(8,128)S(1)}, u32[]{:S(2)}, u32[]{:S(2)}) collective-permute-start(f32[1,16,2,1024]{3,1,2,0:T(8,128)S(1)} %constant_dynamic-slice_fusion.1), channel_id=1, source_target_pairs={{0,8},{1,9},{2,10},{3,11},{4,12},{5,13},{6,14},{7,15},{8,0},{9,1},... | collective-permute-start | bytes 393224 | tf_op jit(solution)/shard_map/ppermute | solution.py:33
  75.0 4.9 %collective-permute-done.7 = f32[1,16,2,1024]{3,1,2,0:T(8,128)S(1)} collective-permute-done((f32[1,16,2,1024]{3,1,2,0:T(8,128)S(1)}, f32[1,16,2,1024]{3,1,2,0:T(8,128)S(1)}, u32[]{:S(2)}, u32[]{:S(2)}) %collective-permute-start.7) | collective-permute-done | bytes 131104 | tf_op jit(solution)/shard_map/ppermute | solution.py:33
  79.8 0.1 convert_bitcast_fusion
  79.9 1.2 collective-permute-start.8
  81.1 4.1 %collective-permute-done.8 = bf16[1,16,2,1024]{3,1,2,0:T(8,128)(2,1)S(1)} collective-permute-done((bf16[1,16,2,1024]{3,1,2,0:T(8,128)(2,1)S(1)}, bf16[1,16,2,1024]{3,1,2,0:T(8,128)(2,1)S(1)}, u32[]{:S(2)}, u32[]{:S(2)}) %collective-permute-start.8) | collective-permute-done | bytes 65568 | tf_op jit(solution)/shard_map/ppermute | solution.py:15
  85.2 1.9 %collective-permute-start.9 = (bf16[2,16,2,1024]{3,1,2,0:T(8,128)(2,1)S(1)}, bf16[2,16,2,1024]{3,1,2,0:T(8,128)(2,1)S(1)}, u32[]{:S(2)}, u32[]{:S(2)}) collective-permute-start(bf16[2,16,2,1024]{3,1,2,0:T(8,128)(2,1)S(1)} %maximum_bitcast_fusion.1), channel_id=1, source_target_pairs={{0,4},{1,5},{2,6},{3,7},{4,0},{5,1},{6,2},{7,3},{8,12},{9,13},{10,... | collective-permute-start | bytes 393224 | tf_op jit(solution)/shard_map/ppermute | solution.py:15
  87.1 3.1 %collective-permute-done.9 = bf16[2,16,2,1024]{3,1,2,0:T(8,128)(2,1)S(1)} collective-permute-done((bf16[2,16,2,1024]{3,1,2,0:T(8,128)(2,1)S(1)}, bf16[2,16,2,1024]{3,1,2,0:T(8,128)(2,1)S(1)}, u32[]{:S(2)}, u32[]{:S(2)}) %collective-permute-start.9) | collective-permute-done | bytes 131104 | tf_op jit(solution)/shard_map/ppermute | solution.py:15
  90.3 1.6 %collective-permute-start.10 = (bf16[4,16,2,1024]{3,1,2,0:T(8,128)(2,1)S(1)}, bf16[4,16,2,1024]{3,1,2,0:T(8,128)(2,1)S(1)}, u32[]{:S(2)}, u32[]{:S(2)}) collective-permute-start(bf16[4,16,2,1024]{3,1,2,0:T(8,128)(2,1)S(1)} %bitcast.175), channel_id=1, source_target_pairs={{0,2},{1,3},{2,0},{3,1},{4,6},{5,7},{6,4},{7,5},{8,10},{9,11},{10,... | collective-permute-start | bytes 786440 | tf_op jit(solution)/shard_map/ppermute | solution.py:15
  91.9 4.9 %collective-permute-done.10 = bf16[4,16,2,1024]{3,1,2,0:T(8,128)(2,1)S(1)} collective-permute-done((bf16[4,16,2,1024]{3,1,2,0:T(8,128)(2,1)S(1)}, bf16[4,16,2,1024]{3,1,2,0:T(8,128)(2,1)S(1)}, u32[]{:S(2)}, u32[]{:S(2)}) %collective-permute-start.10) | collective-permute-done | bytes 262176 | tf_op jit(solution)/shard_map/ppermute | solution.py:15
  96.7 0.1 select_bitcast_fusion.5
  96.8 0.1 pad_maximum_fusion.3
  96.9 0.1 collective-permute-start.11
  97.0 1.9 %collective-permute-done.11 = bf16[8,16,2,1024]{3,1,2,0:T(8,128)(2,1)S(1)} collective-permute-done((bf16[8,16,2,1024]{3,1,2,0:T(8,128)(2,1)S(1)}, bf16[8,16,2,1024]{3,1,2,0:T(8,128)(2,1)S(1)}, u32[]{:S(2)}, u32[]{:S(2)}) %collective-permute-start.11) | collective-permute-done | bytes 524320 | tf_op jit(solution)/shard_map/ppermute | solution.py:15
  98.9 0.1 select_bitcast_fusion.1
  99.0 0.1 pad_maximum_fusion.1
  99.1 1.1 copy.37
  100.2 0.3 copy.51
  100.5 3.3 %convolution_convert_fusion = bf16[2048,4,256]{2,0,1:T(8,128)(2,1)} fusion(bf16[4,256,256]{2,1,0:T(8,128)(2,1)S(1)} %copy-done, bf16[256,2048]{1,0:T(8,128)(2,1)S(1)} %bitcast.167), kind=kOutput, calls=%fused_computation.6 | convolution fusion | flops 1075838976 | bytes 5767168 | tf_op jit(solution)/shard_map/pij,jk->pik/dot_general | solution.py:54
  103.7 6.3 %copy.39 = bf16[4,256,2,1024]{3,1,0,2:T(8,128)(2,1)} copy(bf16[4,256,2,1024]{1,3,2,0:T(8,128)(2,1)} %bitcast.157) | data formatting | bytes 8388608 | tf_op jit(solution)/shard_map/reshape | solution.py:55
  110.0 8.2 %fusion.11 = f32[8,2,16,2,1024]{4,2,3,1,0:T(8,128)S(1)} fusion(bf16[4,1024,1024]{2,1,0:T(8,128)(2,1)} %param.9, bf16[8,2,16,2,4,1024]{5,2,1,0,4,3:T(8,128)(2,1)} %bitcast.159), kind=kOutput, calls=%fused_computation.9 | convolution fusion | flops 4294967296 | bytes 14680064 | tf_op jit(solution)/shard_map/dot_general | solution.py:56
  118.3 0.1 dynamic-slice_bitcast_fusion
  118.4 0.2 collective-permute-start.12
  118.6 2.5 %collective-permute-done.12 = f32[8,16,2,1024]{3,1,2,0:T(8,128)S(1)} collective-permute-done((f32[8,16,2,1024]{3,1,2,0:T(8,128)S(1)}, f32[8,16,2,1024]{3,1,2,0:T(8,128)S(1)}, u32[]{:S(2)}, u32[]{:S(2)}) %collective-permute-start.12) | collective-permute-done | bytes 1048608 | tf_op jit(solution)/shard_map/ppermute | solution.py:33
  121.1 0.1 bitcast_add_fusion
  121.3 1.6 %collective-permute-start.13 = (f32[4,16,2,1024]{3,1,2,0:T(8,128)S(1)}, f32[4,16,2,1024]{3,1,2,0:T(8,128)S(1)}, u32[]{:S(2)}, u32[]{:S(2)}) collective-permute-start(f32[4,16,2,1024]{3,1,2,0:T(8,128)S(1)} %dynamic-slice_bitcast_fusion.2), channel_id=1, source_target_pairs={{0,2},{1,3},{2,0},{3,1},{4,6},{5,7},{6,4},{7,5},{8,10},{9,11},{10,... | collective-permute-start | bytes 1572872 | tf_op jit(solution)/shard_map/ppermute | solution.py:33
  122.9 12.5 %collective-permute-done.13 = f32[4,16,2,1024]{3,1,2,0:T(8,128)S(1)} collective-permute-done((f32[4,16,2,1024]{3,1,2,0:T(8,128)S(1)}, f32[4,16,2,1024]{3,1,2,0:T(8,128)S(1)}, u32[]{:S(2)}, u32[]{:S(2)}) %collective-permute-start.13) | collective-permute-done | bytes 524320 | tf_op jit(solution)/shard_map/ppermute | solution.py:33
  135.3 0.1 bitcast_add_fusion.2
  135.5 1.9 %collective-permute-start.14 = (f32[2,16,2,1024]{3,1,2,0:T(8,128)S(1)}, f32[2,16,2,1024]{3,1,2,0:T(8,128)S(1)}, u32[]{:S(2)}, u32[]{:S(2)}) collective-permute-start(f32[2,16,2,1024]{3,1,2,0:T(8,128)S(1)} %dynamic-slice_bitcast_fusion.4), channel_id=1, source_target_pairs={{0,4},{1,5},{2,6},{3,7},{4,0},{5,1},{6,2},{7,3},{8,12},{9,13},{10,... | collective-permute-start | bytes 786440 | tf_op jit(solution)/shard_map/ppermute | solution.py:33
  137.4 5.8 %collective-permute-done.14 = f32[2,16,2,1024]{3,1,2,0:T(8,128)S(1)} collective-permute-done((f32[2,16,2,1024]{3,1,2,0:T(8,128)S(1)}, f32[2,16,2,1024]{3,1,2,0:T(8,128)S(1)}, u32[]{:S(2)}, u32[]{:S(2)}) %collective-permute-start.14) | collective-permute-done | bytes 262176 | tf_op jit(solution)/shard_map/ppermute | solution.py:33
  143.2 3.0 %collective-permute-start.15 = (f32[1,16,2,1024]{3,1,2,0:T(8,128)S(1)}, f32[1,16,2,1024]{3,1,2,0:T(8,128)S(1)}, u32[]{:S(2)}, u32[]{:S(2)}) collective-permute-start(f32[1,16,2,1024]{3,1,2,0:T(8,128)S(1)} %constant_dynamic-slice_fusion), channel_id=1, source_target_pairs={{0,8},{1,9},{2,10},{3,11},{4,12},{5,13},{6,14},{7,15},{8,0},{9,1},... | collective-permute-start | bytes 393224 | tf_op jit(solution)/shard_map/ppermute | solution.py:33
  146.2 5.2 %collective-permute-done.15 = f32[1,16,2,1024]{3,1,2,0:T(8,128)S(1)} collective-permute-done((f32[1,16,2,1024]{3,1,2,0:T(8,128)S(1)}, f32[1,16,2,1024]{3,1,2,0:T(8,128)S(1)}, u32[]{:S(2)}, u32[]{:S(2)}) %collective-permute-start.15) | collective-permute-done | bytes 131104 | tf_op jit(solution)/shard_map/ppermute | solution.py:33
  151.4 0.1 fusion.20
  151.5 0.8 copy.42
  (23 shorter events, 0.5 us)
Async XLA Ops:
  0.0 26.5 %copy-start = (bf16[4,256,256]{2,1,0:T(8,128)(2,1)S(1)}, bf16[4,256,256]{2,1,0:T(8,128)(2,1)}, u32[]{:S(2)}) copy-start(bf16[4,256,256]{2,1,0:T(8,128)(2,1)} %param.8) | copy-start | bytes 1572868
  2.5 7.8 %collective-permute-start = (bf16[1,16,2,1024]{3,1,2,0:T(8,128)(2,1)S(1)}, bf16[1,16,2,1024]{3,1,2,0:T(8,128)(2,1)S(1)}, u32[]{:S(2)}, u32[]{:S(2)}) collective-permute-start(bf16[1,16,2,1024]{3,1,2,0:T(8,128)(2,1)S(1)} %fusion.25), channel_id=1, source_target_pairs={{0,8},{1,9},{2,10},{3,11},{4,12},{5,13},{6,14},{7,15},{8,0},{9,1},... | collective-permute-start | bytes 196616 | tf_op jit(solution)/shard_map/ppermute | solution.py:15
  11.3 5.0 %collective-permute-start.1 = (bf16[2,16,2,1024]{3,1,2,0:T(8,128)(2,1)S(1)}, bf16[2,16,2,1024]{3,1,2,0:T(8,128)(2,1)S(1)}, u32[]{:S(2)}, u32[]{:S(2)}) collective-permute-start(bf16[2,16,2,1024]{3,1,2,0:T(8,128)(2,1)S(1)} %maximum_bitcast_fusion), channel_id=1, source_target_pairs={{0,4},{1,5},{2,6},{3,7},{4,0},{5,1},{6,2},{7,3},{8,12},{9,13},{10,... | collective-permute-start | bytes 393224 | tf_op jit(solution)/shard_map/ppermute | solution.py:15
  16.3 6.4 %collective-permute-start.2 = (bf16[4,16,2,1024]{3,1,2,0:T(8,128)(2,1)S(1)}, bf16[4,16,2,1024]{3,1,2,0:T(8,128)(2,1)S(1)}, u32[]{:S(2)}, u32[]{:S(2)}) collective-permute-start(bf16[4,16,2,1024]{3,1,2,0:T(8,128)(2,1)S(1)} %bitcast.174), channel_id=1, source_target_pairs={{0,2},{1,3},{2,0},{3,1},{4,6},{5,7},{6,4},{7,5},{8,10},{9,11},{10,... | collective-permute-start | bytes 786440 | tf_op jit(solution)/shard_map/ppermute | solution.py:15
  23.0 2.0 %collective-permute-start.3 = (bf16[8,16,2,1024]{3,1,2,0:T(8,128)(2,1)S(1)}, bf16[8,16,2,1024]{3,1,2,0:T(8,128)(2,1)S(1)}, u32[]{:S(2)}, u32[]{:S(2)}) collective-permute-start(bf16[8,16,2,1024]{3,1,2,0:T(8,128)(2,1)S(1)} %bitcast.168), channel_id=1, source_target_pairs={{0,1},{1,0},{2,3},{3,2},{4,5},{5,4},{6,7},{7,6},{8,9},{9,8},{10,11... | collective-permute-start | bytes 1572872 | tf_op jit(solution)/shard_map/ppermute | solution.py:15
  44.3 1.3 copy-start.1
  45.7 34.1 %copy-start.2 = (f32[16,2,1024]{2,1,0:T(2,128)S(1)}, f32[16,2,1024]{2,1,0:T(2,128)}, u32[]{:S(2)}) copy-start(f32[16,2,1024]{2,1,0:T(2,128)} %param.5) | copy-start | bytes 393220
  45.7 2.7 %collective-permute-start.4 = (f32[8,16,2,1024]{3,1,2,0:T(8,128)S(1)}, f32[8,16,2,1024]{3,1,2,0:T(8,128)S(1)}, u32[]{:S(2)}, u32[]{:S(2)}) collective-permute-start(f32[8,16,2,1024]{3,1,2,0:T(8,128)S(1)} %dynamic-slice_bitcast_fusion.1), channel_id=1, source_target_pairs={{0,1},{1,0},{2,3},{3,2},{4,5},{5,4},{6,7},{7,6},{8,9},{9,8},{10,11... | collective-permute-start | bytes 3145736 | tf_op jit(solution)/shard_map/ppermute | solution.py:33
  49.9 14.0 %collective-permute-start.5 = (f32[4,16,2,1024]{3,1,2,0:T(8,128)S(1)}, f32[4,16,2,1024]{3,1,2,0:T(8,128)S(1)}, u32[]{:S(2)}, u32[]{:S(2)}) collective-permute-start(f32[4,16,2,1024]{3,1,2,0:T(8,128)S(1)} %dynamic-slice_bitcast_fusion.3), channel_id=1, source_target_pairs={{0,2},{1,3},{2,0},{3,1},{4,6},{5,7},{6,4},{7,5},{8,10},{9,11},{10,... | collective-permute-start | bytes 1572872 | tf_op jit(solution)/shard_map/ppermute | solution.py:33
  64.0 7.6 %collective-permute-start.6 = (f32[2,16,2,1024]{3,1,2,0:T(8,128)S(1)}, f32[2,16,2,1024]{3,1,2,0:T(8,128)S(1)}, u32[]{:S(2)}, u32[]{:S(2)}) collective-permute-start(f32[2,16,2,1024]{3,1,2,0:T(8,128)S(1)} %dynamic-slice_bitcast_fusion.5), channel_id=1, source_target_pairs={{0,4},{1,5},{2,6},{3,7},{4,0},{5,1},{6,2},{7,3},{8,12},{9,13},{10,... | collective-permute-start | bytes 786440 | tf_op jit(solution)/shard_map/ppermute | solution.py:33
  71.7 8.2 %collective-permute-start.7 = (f32[1,16,2,1024]{3,1,2,0:T(8,128)S(1)}, f32[1,16,2,1024]{3,1,2,0:T(8,128)S(1)}, u32[]{:S(2)}, u32[]{:S(2)}) collective-permute-start(f32[1,16,2,1024]{3,1,2,0:T(8,128)S(1)} %constant_dynamic-slice_fusion.1), channel_id=1, source_target_pairs={{0,8},{1,9},{2,10},{3,11},{4,12},{5,13},{6,14},{7,15},{8,0},{9,1},... | collective-permute-start | bytes 393224 | tf_op jit(solution)/shard_map/ppermute | solution.py:33
  79.9 5.2 %collective-permute-start.8 = (bf16[1,16,2,1024]{3,1,2,0:T(8,128)(2,1)S(1)}, bf16[1,16,2,1024]{3,1,2,0:T(8,128)(2,1)S(1)}, u32[]{:S(2)}, u32[]{:S(2)}) collective-permute-start(bf16[1,16,2,1024]{3,1,2,0:T(8,128)(2,1)S(1)} %get-tuple-element.5), channel_id=1, source_target_pairs={{0,8},{1,9},{2,10},{3,11},{4,12},{5,13},{6,14},{7,15},{8,0},{9,1},... | collective-permute-start | bytes 196616 | tf_op jit(solution)/shard_map/ppermute | solution.py:15
  85.2 5.0 %collective-permute-start.9 = (bf16[2,16,2,1024]{3,1,2,0:T(8,128)(2,1)S(1)}, bf16[2,16,2,1024]{3,1,2,0:T(8,128)(2,1)S(1)}, u32[]{:S(2)}, u32[]{:S(2)}) collective-permute-start(bf16[2,16,2,1024]{3,1,2,0:T(8,128)(2,1)S(1)} %maximum_bitcast_fusion.1), channel_id=1, source_target_pairs={{0,4},{1,5},{2,6},{3,7},{4,0},{5,1},{6,2},{7,3},{8,12},{9,13},{10,... | collective-permute-start | bytes 393224 | tf_op jit(solution)/shard_map/ppermute | solution.py:15
  90.3 6.4 %collective-permute-start.10 = (bf16[4,16,2,1024]{3,1,2,0:T(8,128)(2,1)S(1)}, bf16[4,16,2,1024]{3,1,2,0:T(8,128)(2,1)S(1)}, u32[]{:S(2)}, u32[]{:S(2)}) collective-permute-start(bf16[4,16,2,1024]{3,1,2,0:T(8,128)(2,1)S(1)} %bitcast.175), channel_id=1, source_target_pairs={{0,2},{1,3},{2,0},{3,1},{4,6},{5,7},{6,4},{7,5},{8,10},{9,11},{10,... | collective-permute-start | bytes 786440 | tf_op jit(solution)/shard_map/ppermute | solution.py:15
  96.9 2.0 %collective-permute-start.11 = (bf16[8,16,2,1024]{3,1,2,0:T(8,128)(2,1)S(1)}, bf16[8,16,2,1024]{3,1,2,0:T(8,128)(2,1)S(1)}, u32[]{:S(2)}, u32[]{:S(2)}) collective-permute-start(bf16[8,16,2,1024]{3,1,2,0:T(8,128)(2,1)S(1)} %bitcast.169), channel_id=1, source_target_pairs={{0,1},{1,0},{2,3},{3,2},{4,5},{5,4},{6,7},{7,6},{8,9},{9,8},{10,11... | collective-permute-start | bytes 1572872 | tf_op jit(solution)/shard_map/ppermute | solution.py:15
  118.4 2.7 %collective-permute-start.12 = (f32[8,16,2,1024]{3,1,2,0:T(8,128)S(1)}, f32[8,16,2,1024]{3,1,2,0:T(8,128)S(1)}, u32[]{:S(2)}, u32[]{:S(2)}) collective-permute-start(f32[8,16,2,1024]{3,1,2,0:T(8,128)S(1)} %dynamic-slice_bitcast_fusion), channel_id=1, source_target_pairs={{0,1},{1,0},{2,3},{3,2},{4,5},{5,4},{6,7},{7,6},{8,9},{9,8},{10,11... | collective-permute-start | bytes 3145736 | tf_op jit(solution)/shard_map/ppermute | solution.py:33
  121.3 14.0 %collective-permute-start.13 = (f32[4,16,2,1024]{3,1,2,0:T(8,128)S(1)}, f32[4,16,2,1024]{3,1,2,0:T(8,128)S(1)}, u32[]{:S(2)}, u32[]{:S(2)}) collective-permute-start(f32[4,16,2,1024]{3,1,2,0:T(8,128)S(1)} %dynamic-slice_bitcast_fusion.2), channel_id=1, source_target_pairs={{0,2},{1,3},{2,0},{3,1},{4,6},{5,7},{6,4},{7,5},{8,10},{9,11},{10,... | collective-permute-start | bytes 1572872 | tf_op jit(solution)/shard_map/ppermute | solution.py:33
  135.5 7.7 %collective-permute-start.14 = (f32[2,16,2,1024]{3,1,2,0:T(8,128)S(1)}, f32[2,16,2,1024]{3,1,2,0:T(8,128)S(1)}, u32[]{:S(2)}, u32[]{:S(2)}) collective-permute-start(f32[2,16,2,1024]{3,1,2,0:T(8,128)S(1)} %dynamic-slice_bitcast_fusion.4), channel_id=1, source_target_pairs={{0,4},{1,5},{2,6},{3,7},{4,0},{5,1},{6,2},{7,3},{8,12},{9,13},{10,... | collective-permute-start | bytes 786440 | tf_op jit(solution)/shard_map/ppermute | solution.py:33
  143.2 8.2 %collective-permute-start.15 = (f32[1,16,2,1024]{3,1,2,0:T(8,128)S(1)}, f32[1,16,2,1024]{3,1,2,0:T(8,128)S(1)}, u32[]{:S(2)}, u32[]{:S(2)}) collective-permute-start(f32[1,16,2,1024]{3,1,2,0:T(8,128)S(1)} %constant_dynamic-slice_fusion), channel_id=1, source_target_pairs={{0,8},{1,9},{2,10},{3,11},{4,12},{5,13},{6,14},{7,15},{8,0},{9,1},... | collective-permute-start | bytes 393224 | tf_op jit(solution)/shard_map/ppermute | solution.py:33

commit v2 on v1

--- a/solution.py
+++ b/solution.py
@@ -1,6 +1,10 @@
+import functools
+
 import jax
 import jax.numpy as jnp
 from jax import lax
+from jax.experimental import pallas as pl
+from jax.experimental.pallas import tpu as pltpu
 from jax.sharding import PartitionSpec as P
 
 ITERS = 2
@@ -35,11 +39,43 @@
     return acc[0]
 
 
+def exchange_kernel(states, occ_ref, r_ref, vir_ref, out_ref):
+    @pl.when(pl.program_id(0) == 0)
+    def _():
+        out_ref[...] = jnp.zeros_like(out_ref)
+
+    half = jnp.dot(occ_ref[0], r_ref[...], preferred_element_type=jnp.float32).astype(jnp.bfloat16)
+    nvir = vir_ref.shape[1]
+    vir = vir_ref[0]
+    for s in range(states):
+        cols = slice(s * nvir, (s + 1) * nvir)
+        out_ref[:, cols] += lax.dot_general(
+            half[:, cols], vir, (((1,), (1,)), ((), ())), preferred_element_type=jnp.float32
+        )
+
+
+def exchange_part(occ_ints, flat, vir_ints, states):
+    local_aux, nocc, _ = occ_ints.shape
+    nvir = vir_ints.shape[1]
+    width = states * nvir
+    return pl.pallas_call(
+        functools.partial(exchange_kernel, states),
+        grid=(local_aux,),
+        in_specs=[
+            pl.BlockSpec((1, nocc, nocc), lambda p: (p, 0, 0)),
+            pl.BlockSpec((nocc, width), lambda p: (0, 0)),
+            pl.BlockSpec((1, nvir, nvir), lambda p: (p, 0, 0)),
+        ],
+        out_specs=pl.BlockSpec((nocc, width), lambda p: (0, 0)),
+        out_shape=jax.ShapeDtypeStruct((nocc, width), jnp.float32),
+        compiler_params=pltpu.CompilerParams(dimension_semantics=("arbitrary",)),
+    )(occ_ints, flat, vir_ints)
+
+
 def shards(rhs, occ_energy, vir_energy, occ_ints, vir_ints):
     own_rows = rhs.shape[0]
     states = rhs.shape[1]
     nvir = rhs.shape[2]
-    local_aux = occ_ints.shape[0]
     nocc = occ_ints.shape[1]
     n = nocc // own_rows
     assert n & (n - 1) == 0
@@ -48,15 +84,10 @@
     denom = vir_energy[None, None, :] - my_occ[:, None, None]
     response = rhs / denom
     for step in range(ITERS):
-        rounded = response.astype(jnp.bfloat16)
-        piece = gather_rows(rounded, n)
-        flat = piece.reshape(nocc, states * nvir)
-        half = jnp.einsum("pij,jk->pik", occ_ints, flat, preferred_element_type=jnp.float32)
-        half = half.astype(jnp.bfloat16).reshape(local_aux, nocc, states, nvir)
-        part = lax.dot_general(
-            half, vir_ints, (((0, 3), (0, 2)), ((), ())), preferred_element_type=jnp.float32
-        )
-        exchange = scatter_sum(part, n)
+        rounded = response.astype(jnp.bfloat16).reshape(own_rows, states * nvir)
+        flat = gather_rows(rounded, n)
+        part = exchange_part(occ_ints, flat, vir_ints, states)
+        exchange = scatter_sum(part, n).reshape(own_rows, states, nvir)
         response = 0.4 * response + 0.6 * (rhs - exchange) / denom
     return response
 

time: 153 us -> 137 us (0.90)
  matrix products: 23 us -> 0 us
  Pallas kernels: 0 us -> 19.4 us
  local copies, waits for them, and re-layouts: 18.7 us -> 6.36 us
    dot_general x4 -> x0, matrix products: 23 us -> none  [the longest x2 16.4 us: shards(): lax.dot_general(half, vir_ints, (((0, 3), (0, 2)), ((), ())), preferred_e...]
    pallas_call x0 -> x2, Pallas kernels: none -> 19.4 us  [exchange_part(): pl.pallas_call(functools.partial(exchange_kernel, states), grid=(local_au...]
    reshape x2 -> x0, local copies, waits for them, and re-layouts: 12.6 us -> none  [shards(): half = half.astype(jnp.bfloat16).reshape(local_aux, nocc, states, nvir)]
    squeeze x8, local copies, waits for them, and re-layouts: 0.37 us -> 3.09 us  [scatter_sum(): send = lax.dynamic_index_in_dim(pairs, 1 - bit, axis=1, keepdims=False)]
    unnamed x8 -> x6, local copies, waits for them, and re-layouts: 1.86 us -> 0.01 us
where the time goes in v2:
time: 137 us; the launch traced here: 136 us
  waiting for transfers between devices  81 us (59%)
  starting transfers between devices  24.1 us (18%)
  Pallas kernels  19.4 us (14%)
  local copies, waits for them, and re-layouts  6.36 us (5%)
  other arithmetic  5.17 us (4%)
    ppermute x8, waiting for transfers between devices, scatter_sum(): acc = keep + lax.ppermute(send, 'aux', [(d, d ^ 1 << k) for d in range(n)])  52.4 us
    ppermute x8, waiting for transfers between devices, gather_rows(): theirs = lax.ppermute(acc, 'aux', [(d, d ^ 1 << k) for d in range(n)])  28.6 us
    pallas_call x2, Pallas kernels, exchange_part(): pl.pallas_call(functools.partial(exchange_kernel, states), grid=(local_au...  19.4 us
    ppermute x8, starting transfers between devices, scatter_sum(): acc = keep + lax.ppermute(send, 'aux', [(d, d ^ 1 << k) for d in range(n)])  12.8 us
    ppermute x8, starting transfers between devices, gather_rows(): theirs = lax.ppermute(acc, 'aux', [(d, d ^ 1 << k) for d in range(n)])  11.3 us
    squeeze x8, local copies, waits for them, and re-layouts, scatter_sum(): send = lax.dynamic_index_in_dim(pairs, 1 - bit, axis=1, keepdims=False)  3.09 us
  transfers between devices with their start and end apart: 16, of which 16 were waited for; matrix products, arithmetic and copies ran while one was open for 0% of the time, Pallas kernels for 0%

profile of v2, /device:TPU:0, one launch (start us, length us, event | category | flops | bytes accessed | tf_op | source)
XLA Modules:
  0.0 136.3 jit_solution(14280521919857561706)
XLA Ops:
  0.0 0.8 dynamic_slice.47
  0.8 0.8 broadcast_subtract_fusion
  1.5 1.0 fusion
  2.5 4.1 %collective-permute-start = (bf16[1,16,2048]{2,1,0:T(8,128)(2,1)S(1)}, bf16[1,16,2048]{2,1,0:T(8,128)(2,1)S(1)}, u32[]{:S(2)}, u32[]{:S(2)}) collective-permute-start(bf16[1,16,2048]{2,1,0:T(8,128)(2,1)S(1)} %broadcast_in_dim_reshape.6), channel_id=1, source_target_pairs={{0,8},{1,9},{2,10},{3,11},{4,12},{5,13},{6,14},{7,15},{8,0},{9,1},... | collective-permute-start | bytes 196616 | tf_op jit(solution)/shard_map/ppermute | solution.py:19
  6.6 3.6 %collective-permute-done = bf16[1,16,2048]{2,1,0:T(8,128)(2,1)S(1)} collective-permute-done((bf16[1,16,2048]{2,1,0:T(8,128)(2,1)S(1)}, bf16[1,16,2048]{2,1,0:T(8,128)(2,1)S(1)}, u32[]{:S(2)}, u32[]{:S(2)}) %collective-permute-start) | collective-permute-done | bytes 65568 | tf_op jit(solution)/shard_map/ppermute | solution.py:19
  10.3 0.6 collective-permute-start.1
  11.0 4.4 %collective-permute-done.1 = bf16[2,16,2048]{2,1,0:T(8,128)(2,1)S(1)} collective-permute-done((bf16[2,16,2048]{2,1,0:T(8,128)(2,1)S(1)}, bf16[2,16,2048]{2,1,0:T(8,128)(2,1)S(1)}, u32[]{:S(2)}, u32[]{:S(2)}) %collective-permute-start.1) | collective-permute-done | bytes 131104 | tf_op jit(solution)/shard_map/ppermute | solution.py:19
  15.4 1.8 %collective-permute-start.2 = (bf16[4,16,2048]{2,1,0:T(8,128)(2,1)S(1)}, bf16[4,16,2048]{2,1,0:T(8,128)(2,1)S(1)}, u32[]{:S(2)}, u32[]{:S(2)}) collective-permute-start(bf16[4,16,2048]{2,1,0:T(8,128)(2,1)S(1)} %bitcast.106), channel_id=1, source_target_pairs={{0,2},{1,3},{2,0},{3,1},{4,6},{5,7},{6,4},{7,5},{8,10},{9,11},{10,... | collective-permute-start | bytes 786440 | tf_op jit(solution)/shard_map/ppermute | solution.py:19
  17.2 4.7 %collective-permute-done.2 = bf16[4,16,2048]{2,1,0:T(8,128)(2,1)S(1)} collective-permute-done((bf16[4,16,2048]{2,1,0:T(8,128)(2,1)S(1)}, bf16[4,16,2048]{2,1,0:T(8,128)(2,1)S(1)}, u32[]{:S(2)}, u32[]{:S(2)}) %collective-permute-start.2) | collective-permute-done | bytes 262176 | tf_op jit(solution)/shard_map/ppermute | solution.py:19
  21.9 0.1 select_bitcast_fusion.7
  21.9 0.1 pad_maximum_fusion.2
  22.0 0.1 collective-permute-start.3
  22.1 1.9 %collective-permute-done.3 = bf16[8,16,2048]{2,1,0:T(8,128)(2,1)S(1)} collective-permute-done((bf16[8,16,2048]{2,1,0:T(8,128)(2,1)S(1)}, bf16[8,16,2048]{2,1,0:T(8,128)(2,1)S(1)}, u32[]{:S(2)}, u32[]{:S(2)}) %collective-permute-start.3) | collective-permute-done | bytes 524320 | tf_op jit(solution)/shard_map/ppermute | solution.py:19
  24.0 0.1 select_bitcast_fusion.3
  24.1 0.1 pad_maximum_fusion
  24.2 1.1 copy.16
  25.3 9.7 %shard_map.55 = f32[256,2048]{1,0:T(8,128)} custom-call(bf16[4,256,256]{2,1,0:T(8,128)(2,1)} %occ_ref.3, bf16[256,2048]{1,0:T(8,128)(2,1)} %bitcast.94, bf16[4,1024,1024]{2,1,0:T(8,128)(2,1)} %vir_ref.3), custom_call_target="tpu_custom_call" | custom-call | tf_op jit(solution)/shard_map/pallas_call | solution.py:61
  35.0 0.0 copy-start
  35.0 1.4 %dynamic-slice_bitcast_fusion.1 = f32[8,16,2048]{2,1,0:T(8,128)S(1)} fusion(f32[8,2,16,2048]{3,2,1,0:T(8,128)} %bitcast.90, s32[]{:T(128)S(6)} %select_n.133), kind=kLoop, calls=%fused_computation.5 | loop fusion | bytes 2097156 | tf_op jit(solution)/shard_map/jit(dynamic_index_in_dim)/squeeze | solution.py:36
  36.4 0.2 collective-permute-start.4
  36.6 2.7 %collective-permute-done.4 = f32[8,16,2048]{2,1,0:T(8,128)} collective-permute-done((f32[8,16,2048]{2,1,0:T(8,128)S(1)}, f32[8,16,2048]{2,1,0:T(8,128)}, u32[]{:S(2)}, u32[]{:S(2)}) %collective-permute-start.4) | collective-permute-done | bytes 1048608 | tf_op jit(solution)/shard_map/ppermute | solution.py:37
  39.3 0.0 copy-done
  39.3 1.3 bitcast_add_fusion.1
  40.7 0.0 copy-start.2
  40.7 1.8 %collective-permute-start.5 = (f32[4,16,2048]{2,1,0:T(8,128)S(1)}, f32[4,16,2048]{2,1,0:T(8,128)S(1)}, u32[]{:S(2)}, u32[]{:S(2)}) collective-permute-start(f32[4,16,2048]{2,1,0:T(8,128)S(1)} %dynamic-slice_bitcast_fusion.3), channel_id=1, source_target_pairs={{0,2},{1,3},{2,0},{3,1},{4,6},{5,7},{6,4},{7,5},{8,10},{9,11},{10,... | collective-permute-start | bytes 1572872 | tf_op jit(solution)/shard_map/ppermute | solution.py:37
  42.5 12.3 %collective-permute-done.5 = f32[4,16,2048]{2,1,0:T(8,128)S(1)} collective-permute-done((f32[4,16,2048]{2,1,0:T(8,128)S(1)}, f32[4,16,2048]{2,1,0:T(8,128)S(1)}, u32[]{:S(2)}, u32[]{:S(2)}) %collective-permute-start.5) | collective-permute-done | bytes 524320 | tf_op jit(solution)/shard_map/ppermute | solution.py:37
  54.7 0.1 bitcast_add_fusion.3
  54.8 0.8 collective-permute-start.6
  55.7 6.7 %collective-permute-done.6 = f32[2,16,2048]{2,1,0:T(8,128)S(1)} collective-permute-done((f32[2,16,2048]{2,1,0:T(8,128)S(1)}, f32[2,16,2048]{2,1,0:T(8,128)S(1)}, u32[]{:S(2)}, u32[]{:S(2)}) %collective-permute-start.6) | collective-permute-done | bytes 262176 | tf_op jit(solution)/shard_map/ppermute | solution.py:37
  62.5 3.3 %collective-permute-start.7 = (f32[1,16,2048]{2,1,0:T(8,128)S(1)}, f32[1,16,2048]{2,1,0:T(8,128)S(1)}, u32[]{:S(2)}, u32[]{:S(2)}) collective-permute-start(f32[1,16,2048]{2,1,0:T(8,128)S(1)} %constant_dynamic-slice_fusion.1), channel_id=1, source_target_pairs={{0,8},{1,9},{2,10},{3,11},{4,12},{5,13},{6,14},{7,15},{8,0},{9,1},... | collective-permute-start | bytes 393224 | tf_op jit(solution)/shard_map/ppermute | solution.py:37
  65.8 4.9 %collective-permute-done.7 = f32[1,16,2048]{2,1,0:T(8,128)S(1)} collective-permute-done((f32[1,16,2048]{2,1,0:T(8,128)S(1)}, f32[1,16,2048]{2,1,0:T(8,128)S(1)}, u32[]{:S(2)}, u32[]{:S(2)}) %collective-permute-start.7) | collective-permute-done | bytes 131104 | tf_op jit(solution)/shard_map/ppermute | solution.py:37
  70.7 0.1 reshape_squeeze.6
  70.8 0.0 copy-done.2
  70.8 0.2 fusion.1
  71.0 1.2 collective-permute-start.8
  72.2 4.1 %collective-permute-done.8 = bf16[1,16,2048]{2,1,0:T(8,128)(2,1)S(1)} collective-permute-done((bf16[1,16,2048]{2,1,0:T(8,128)(2,1)S(1)}, bf16[1,16,2048]{2,1,0:T(8,128)(2,1)S(1)}, u32[]{:S(2)}, u32[]{:S(2)}) %collective-permute-start.8) | collective-permute-done | bytes 65568 | tf_op jit(solution)/shard_map/ppermute | solution.py:19
  76.3 1.9 %collective-permute-start.9 = (bf16[2,16,2048]{2,1,0:T(8,128)(2,1)S(1)}, bf16[2,16,2048]{2,1,0:T(8,128)(2,1)S(1)}, u32[]{:S(2)}, u32[]{:S(2)}) collective-permute-start(bf16[2,16,2048]{2,1,0:T(8,128)(2,1)S(1)} %maximum_bitcast_fusion.1), channel_id=1, source_target_pairs={{0,4},{1,5},{2,6},{3,7},{4,0},{5,1},{6,2},{7,3},{8,12},{9,13},{10,... | collective-permute-start | bytes 393224 | tf_op jit(solution)/shard_map/ppermute | solution.py:19
  78.2 3.1 %collective-permute-done.9 = bf16[2,16,2048]{2,1,0:T(8,128)(2,1)S(1)} collective-permute-done((bf16[2,16,2048]{2,1,0:T(8,128)(2,1)S(1)}, bf16[2,16,2048]{2,1,0:T(8,128)(2,1)S(1)}, u32[]{:S(2)}, u32[]{:S(2)}) %collective-permute-start.9) | collective-permute-done | bytes 131104 | tf_op jit(solution)/shard_map/ppermute | solution.py:19
  81.4 1.6 %collective-permute-start.10 = (bf16[4,16,2048]{2,1,0:T(8,128)(2,1)S(1)}, bf16[4,16,2048]{2,1,0:T(8,128)(2,1)S(1)}, u32[]{:S(2)}, u32[]{:S(2)}) collective-permute-start(bf16[4,16,2048]{2,1,0:T(8,128)(2,1)S(1)} %bitcast.107), channel_id=1, source_target_pairs={{0,2},{1,3},{2,0},{3,1},{4,6},{5,7},{6,4},{7,5},{8,10},{9,11},{10,... | collective-permute-start | bytes 786440 | tf_op jit(solution)/shard_map/ppermute | solution.py:19
  82.9 4.9 %collective-permute-done.10 = bf16[4,16,2048]{2,1,0:T(8,128)(2,1)S(1)} collective-permute-done((bf16[4,16,2048]{2,1,0:T(8,128)(2,1)S(1)}, bf16[4,16,2048]{2,1,0:T(8,128)(2,1)S(1)}, u32[]{:S(2)}, u32[]{:S(2)}) %collective-permute-start.10) | collective-permute-done | bytes 262176 | tf_op jit(solution)/shard_map/ppermute | solution.py:19
  87.8 0.1 select_bitcast_fusion.5
  87.9 0.1 pad_maximum_fusion.3
  88.0 0.1 collective-permute-start.11
  88.1 1.9 %collective-permute-done.11 = bf16[8,16,2048]{2,1,0:T(8,128)(2,1)S(1)} collective-permute-done((bf16[8,16,2048]{2,1,0:T(8,128)(2,1)S(1)}, bf16[8,16,2048]{2,1,0:T(8,128)(2,1)S(1)}, u32[]{:S(2)}, u32[]{:S(2)}) %collective-permute-start.11) | collective-permute-done | bytes 524320 | tf_op jit(solution)/shard_map/ppermute | solution.py:19
  90.0 0.1 select_bitcast_fusion.1
  90.1 0.1 pad_maximum_fusion.1
  90.2 1.1 copy.19
  91.2 9.7 %shard_map.56 = f32[256,2048]{1,0:T(8,128)} custom-call(bf16[4,256,256]{2,1,0:T(8,128)(2,1)} %occ_ref.3, bf16[256,2048]{1,0:T(8,128)(2,1)} %bitcast.95, bf16[4,1024,1024]{2,1,0:T(8,128)(2,1)} %vir_ref.3), custom_call_target="tpu_custom_call" | custom-call | tf_op jit(solution)/shard_map/pallas_call | solution.py:61
  100.9 0.0 copy-start.1
  101.0 1.5 %dynamic-slice_bitcast_fusion = f32[8,16,2048]{2,1,0:T(8,128)S(1)} fusion(f32[8,2,16,2048]{3,2,1,0:T(8,128)} %bitcast.92, s32[]{:T(128)S(6)} %select_n.133), kind=kLoop, calls=%fused_computation.4 | loop fusion | bytes 2097156 | tf_op jit(solution)/shard_map/jit(dynamic_index_in_dim)/squeeze | solution.py:36
  102.4 0.2 collective-permute-start.12
  102.6 2.5 %collective-permute-done.12 = f32[8,16,2048]{2,1,0:T(8,128)S(1)} collective-permute-done((f32[8,16,2048]{2,1,0:T(8,128)S(1)}, f32[8,16,2048]{2,1,0:T(8,128)S(1)}, u32[]{:S(2)}, u32[]{:S(2)}) %collective-permute-start.12) | collective-permute-done | bytes 1048608 | tf_op jit(solution)/shard_map/ppermute | solution.py:37
  105.2 0.0 copy-done.1
  105.2 0.1 bitcast_add_fusion
  105.3 1.6 %collective-permute-start.13 = (f32[4,16,2048]{2,1,0:T(8,128)S(1)}, f32[4,16,2048]{2,1,0:T(8,128)S(1)}, u32[]{:S(2)}, u32[]{:S(2)}) collective-permute-start(f32[4,16,2048]{2,1,0:T(8,128)S(1)} %dynamic-slice_bitcast_fusion.2), channel_id=1, source_target_pairs={{0,2},{1,3},{2,0},{3,1},{4,6},{5,7},{6,4},{7,5},{8,10},{9,11},{10,... | collective-permute-start | bytes 1572872 | tf_op jit(solution)/shard_map/ppermute | solution.py:37
  106.9 12.5 %collective-permute-done.13 = f32[4,16,2048]{2,1,0:T(8,128)S(1)} collective-permute-done((f32[4,16,2048]{2,1,0:T(8,128)S(1)}, f32[4,16,2048]{2,1,0:T(8,128)S(1)}, u32[]{:S(2)}, u32[]{:S(2)}) %collective-permute-start.13) | collective-permute-done | bytes 524320 | tf_op jit(solution)/shard_map/ppermute | solution.py:37
  119.4 0.1 bitcast_add_fusion.2
  119.5 1.9 %collective-permute-start.14 = (f32[2,16,2048]{2,1,0:T(8,128)S(1)}, f32[2,16,2048]{2,1,0:T(8,128)S(1)}, u32[]{:S(2)}, u32[]{:S(2)}) collective-permute-start(f32[2,16,2048]{2,1,0:T(8,128)S(1)} %dynamic-slice_bitcast_fusion.4), channel_id=1, source_target_pairs={{0,4},{1,5},{2,6},{3,7},{4,0},{5,1},{6,2},{7,3},{8,12},{9,13},{10,... | collective-permute-start | bytes 786440 | tf_op jit(solution)/shard_map/ppermute | solution.py:37
  121.4 5.8 %collective-permute-done.14 = f32[2,16,2048]{2,1,0:T(8,128)S(1)} collective-permute-done((f32[2,16,2048]{2,1,0:T(8,128)S(1)}, f32[2,16,2048]{2,1,0:T(8,128)S(1)}, u32[]{:S(2)}, u32[]{:S(2)}) %collective-permute-start.14) | collective-permute-done | bytes 262176 | tf_op jit(solution)/shard_map/ppermute | solution.py:37
  127.2 3.0 %collective-permute-start.15 = (f32[1,16,2048]{2,1,0:T(8,128)S(1)}, f32[1,16,2048]{2,1,0:T(8,128)S(1)}, u32[]{:S(2)}, u32[]{:S(2)}) collective-permute-start(f32[1,16,2048]{2,1,0:T(8,128)S(1)} %constant_dynamic-slice_fusion), channel_id=1, source_target_pairs={{0,8},{1,9},{2,10},{3,11},{4,12},{5,13},{6,14},{7,15},{8,0},{9,1},... | collective-permute-start | bytes 393224 | tf_op jit(solution)/shard_map/ppermute | solution.py:37
  130.2 5.2 %collective-permute-done.15 = f32[1,16,2048]{2,1,0:T(8,128)S(1)} collective-permute-done((f32[1,16,2048]{2,1,0:T(8,128)S(1)}, f32[1,16,2048]{2,1,0:T(8,128)S(1)}, u32[]{:S(2)}, u32[]{:S(2)}) %collective-permute-start.15) | collective-permute-done | bytes 131104 | tf_op jit(solution)/shard_map/ppermute | solution.py:37
  135.4 0.1 reshape_squeeze.7
  135.5 0.8 divide_add_fusion
  (23 shorter events, 0.6 us)
Async XLA Ops:
  2.5 7.8 %collective-permute-start = (bf16[1,16,2048]{2,1,0:T(8,128)(2,1)S(1)}, bf16[1,16,2048]{2,1,0:T(8,128)(2,1)S(1)}, u32[]{:S(2)}, u32[]{:S(2)}) collective-permute-start(bf16[1,16,2048]{2,1,0:T(8,128)(2,1)S(1)} %broadcast_in_dim_reshape.6), channel_id=1, source_target_pairs={{0,8},{1,9},{2,10},{3,11},{4,12},{5,13},{6,14},{7,15},{8,0},{9,1},... | collective-permute-start | bytes 196616 | tf_op jit(solution)/shard_map/ppermute | solution.py:19
  10.3 5.0 %collective-permute-start.1 = (bf16[2,16,2048]{2,1,0:T(8,128)(2,1)S(1)}, bf16[2,16,2048]{2,1,0:T(8,128)(2,1)S(1)}, u32[]{:S(2)}, u32[]{:S(2)}) collective-permute-start(bf16[2,16,2048]{2,1,0:T(8,128)(2,1)S(1)} %maximum_bitcast_fusion), channel_id=1, source_target_pairs={{0,4},{1,5},{2,6},{3,7},{4,0},{5,1},{6,2},{7,3},{8,12},{9,13},{10,... | collective-permute-start | bytes 393224 | tf_op jit(solution)/shard_map/ppermute | solution.py:19
  15.4 6.4 %collective-permute-start.2 = (bf16[4,16,2048]{2,1,0:T(8,128)(2,1)S(1)}, bf16[4,16,2048]{2,1,0:T(8,128)(2,1)S(1)}, u32[]{:S(2)}, u32[]{:S(2)}) collective-permute-start(bf16[4,16,2048]{2,1,0:T(8,128)(2,1)S(1)} %bitcast.106), channel_id=1, source_target_pairs={{0,2},{1,3},{2,0},{3,1},{4,6},{5,7},{6,4},{7,5},{8,10},{9,11},{10,... | collective-permute-start | bytes 786440 | tf_op jit(solution)/shard_map/ppermute | solution.py:19
  22.0 2.0 %collective-permute-start.3 = (bf16[8,16,2048]{2,1,0:T(8,128)(2,1)S(1)}, bf16[8,16,2048]{2,1,0:T(8,128)(2,1)S(1)}, u32[]{:S(2)}, u32[]{:S(2)}) collective-permute-start(bf16[8,16,2048]{2,1,0:T(8,128)(2,1)S(1)} %bitcast.100), channel_id=1, source_target_pairs={{0,1},{1,0},{2,3},{3,2},{4,5},{5,4},{6,7},{7,6},{8,9},{9,8},{10,11... | collective-permute-start | bytes 1572872 | tf_op jit(solution)/shard_map/ppermute | solution.py:19
  35.0 4.3 %copy-start = (f32[256,2048]{1,0:T(8,128)S(1)}, f32[256,2048]{1,0:T(8,128)}, u32[]{:S(2)}) copy-start(f32[256,2048]{1,0:T(8,128)} %shard_map.55) | copy-start | bytes 6291460
  36.4 2.9 %collective-permute-start.4 = (f32[8,16,2048]{2,1,0:T(8,128)S(1)}, f32[8,16,2048]{2,1,0:T(8,128)}, u32[]{:S(2)}, u32[]{:S(2)}) collective-permute-start(f32[8,16,2048]{2,1,0:T(8,128)S(1)} %dynamic-slice_bitcast_fusion.1), channel_id=1, source_target_pairs={{0,1},{1,0},{2,3},{3,2},{4,5},{5,4},{6,7},{7,6},{8,9},{9,8},{10,11... | collective-permute-start | bytes 3145736 | tf_op jit(solution)/shard_map/ppermute | solution.py:37
  40.7 30.1 %copy-start.2 = (f32[16,2,1024]{2,1,0:T(2,128)S(1)}, f32[16,2,1024]{2,1,0:T(2,128)}, u32[]{:S(2)}) copy-start(f32[16,2,1024]{2,1,0:T(2,128)} %param.5) | copy-start | bytes 393220
  40.7 14.0 %collective-permute-start.5 = (f32[4,16,2048]{2,1,0:T(8,128)S(1)}, f32[4,16,2048]{2,1,0:T(8,128)S(1)}, u32[]{:S(2)}, u32[]{:S(2)}) collective-permute-start(f32[4,16,2048]{2,1,0:T(8,128)S(1)} %dynamic-slice_bitcast_fusion.3), channel_id=1, source_target_pairs={{0,2},{1,3},{2,0},{3,1},{4,6},{5,7},{6,4},{7,5},{8,10},{9,11},{10,... | collective-permute-start | bytes 1572872 | tf_op jit(solution)/shard_map/ppermute | solution.py:37
  54.8 7.6 %collective-permute-start.6 = (f32[2,16,2048]{2,1,0:T(8,128)S(1)}, f32[2,16,2048]{2,1,0:T(8,128)S(1)}, u32[]{:S(2)}, u32[]{:S(2)}) collective-permute-start(f32[2,16,2048]{2,1,0:T(8,128)S(1)} %dynamic-slice_bitcast_fusion.5), channel_id=1, source_target_pairs={{0,4},{1,5},{2,6},{3,7},{4,0},{5,1},{6,2},{7,3},{8,12},{9,13},{10,... | collective-permute-start | bytes 786440 | tf_op jit(solution)/shard_map/ppermute | solution.py:37
  62.5 8.2 %collective-permute-start.7 = (f32[1,16,2048]{2,1,0:T(8,128)S(1)}, f32[1,16,2048]{2,1,0:T(8,128)S(1)}, u32[]{:S(2)}, u32[]{:S(2)}) collective-permute-start(f32[1,16,2048]{2,1,0:T(8,128)S(1)} %constant_dynamic-slice_fusion.1), channel_id=1, source_target_pairs={{0,8},{1,9},{2,10},{3,11},{4,12},{5,13},{6,14},{7,15},{8,0},{9,1},... | collective-permute-start | bytes 393224 | tf_op jit(solution)/shard_map/ppermute | solution.py:37
  71.0 5.2 %collective-permute-start.8 = (bf16[1,16,2048]{2,1,0:T(8,128)(2,1)S(1)}, bf16[1,16,2048]{2,1,0:T(8,128)(2,1)S(1)}, u32[]{:S(2)}, u32[]{:S(2)}) collective-permute-start(bf16[1,16,2048]{2,1,0:T(8,128)(2,1)S(1)} %broadcast_in_dim_reshape.7), channel_id=1, source_target_pairs={{0,8},{1,9},{2,10},{3,11},{4,12},{5,13},{6,14},{7,15},{8,0},{9,1},... | collective-permute-start | bytes 196616 | tf_op jit(solution)/shard_map/ppermute | solution.py:19
  76.3 5.0 %collective-permute-start.9 = (bf16[2,16,2048]{2,1,0:T(8,128)(2,1)S(1)}, bf16[2,16,2048]{2,1,0:T(8,128)(2,1)S(1)}, u32[]{:S(2)}, u32[]{:S(2)}) collective-permute-start(bf16[2,16,2048]{2,1,0:T(8,128)(2,1)S(1)} %maximum_bitcast_fusion.1), channel_id=1, source_target_pairs={{0,4},{1,5},{2,6},{3,7},{4,0},{5,1},{6,2},{7,3},{8,12},{9,13},{10,... | collective-permute-start | bytes 393224 | tf_op jit(solution)/shard_map/ppermute | solution.py:19
  81.4 6.4 %collective-permute-start.10 = (bf16[4,16,2048]{2,1,0:T(8,128)(2,1)S(1)}, bf16[4,16,2048]{2,1,0:T(8,128)(2,1)S(1)}, u32[]{:S(2)}, u32[]{:S(2)}) collective-permute-start(bf16[4,16,2048]{2,1,0:T(8,128)(2,1)S(1)} %bitcast.107), channel_id=1, source_target_pairs={{0,2},{1,3},{2,0},{3,1},{4,6},{5,7},{6,4},{7,5},{8,10},{9,11},{10,... | collective-permute-start | bytes 786440 | tf_op jit(solution)/shard_map/ppermute | solution.py:19
  88.0 2.0 %collective-permute-start.11 = (bf16[8,16,2048]{2,1,0:T(8,128)(2,1)S(1)}, bf16[8,16,2048]{2,1,0:T(8,128)(2,1)S(1)}, u32[]{:S(2)}, u32[]{:S(2)}) collective-permute-start(bf16[8,16,2048]{2,1,0:T(8,128)(2,1)S(1)} %bitcast.101), channel_id=1, source_target_pairs={{0,1},{1,0},{2,3},{3,2},{4,5},{5,4},{6,7},{7,6},{8,9},{9,8},{10,11... | collective-permute-start | bytes 1572872 | tf_op jit(solution)/shard_map/ppermute | solution.py:19
  100.9 4.2 %copy-start.1 = (f32[256,2048]{1,0:T(8,128)S(1)}, f32[256,2048]{1,0:T(8,128)}, u32[]{:S(2)}) copy-start(f32[256,2048]{1,0:T(8,128)} %shard_map.56) | copy-start | bytes 6291460
  102.4 2.7 %collective-permute-start.12 = (f32[8,16,2048]{2,1,0:T(8,128)S(1)}, f32[8,16,2048]{2,1,0:T(8,128)S(1)}, u32[]{:S(2)}, u32[]{:S(2)}) collective-permute-start(f32[8,16,2048]{2,1,0:T(8,128)S(1)} %dynamic-slice_bitcast_fusion), channel_id=1, source_target_pairs={{0,1},{1,0},{2,3},{3,2},{4,5},{5,4},{6,7},{7,6},{8,9},{9,8},{10,11... | collective-permute-start | bytes 3145736 | tf_op jit(solution)/shard_map/ppermute | solution.py:37
  105.3 14.0 %collective-permute-start.13 = (f32[4,16,2048]{2,1,0:T(8,128)S(1)}, f32[4,16,2048]{2,1,0:T(8,128)S(1)}, u32[]{:S(2)}, u32[]{:S(2)}) collective-permute-start(f32[4,16,2048]{2,1,0:T(8,128)S(1)} %dynamic-slice_bitcast_fusion.2), channel_id=1, source_target_pairs={{0,2},{1,3},{2,0},{3,1},{4,6},{5,7},{6,4},{7,5},{8,10},{9,11},{10,... | collective-permute-start | bytes 1572872 | tf_op jit(solution)/shard_map/ppermute | solution.py:37
  119.5 7.7 %collective-permute-start.14 = (f32[2,16,2048]{2,1,0:T(8,128)S(1)}, f32[2,16,2048]{2,1,0:T(8,128)S(1)}, u32[]{:S(2)}, u32[]{:S(2)}) collective-permute-start(f32[2,16,2048]{2,1,0:T(8,128)S(1)} %dynamic-slice_bitcast_fusion.4), channel_id=1, source_target_pairs={{0,4},{1,5},{2,6},{3,7},{4,0},{5,1},{6,2},{7,3},{8,12},{9,13},{10,... | collective-permute-start | bytes 786440 | tf_op jit(solution)/shard_map/ppermute | solution.py:37
  127.2 8.2 %collective-permute-start.15 = (f32[1,16,2048]{2,1,0:T(8,128)S(1)}, f32[1,16,2048]{2,1,0:T(8,128)S(1)}, u32[]{:S(2)}, u32[]{:S(2)}) collective-permute-start(f32[1,16,2048]{2,1,0:T(8,128)S(1)} %constant_dynamic-slice_fusion), channel_id=1, source_target_pairs={{0,8},{1,9},{2,10},{3,11},{4,12},{5,13},{6,14},{7,15},{8,0},{9,1},... | collective-permute-start | bytes 393224 | tf_op jit(solution)/shard_map/ppermute | solution.py:37

commit v3 on v2

--- a/solution.py
+++ b/solution.py
@@ -10,33 +10,79 @@
 ITERS = 2
 
 
+def bit_orders(m, descending):
+    order0 = list(range(1, m))
+    order1 = list(order0)
+    if len(order1) >= 2:
+        order1[0], order1[1] = order1[1], order1[0]
+    if descending:
+        return order0[::-1] + [0], order1[::-1] + [0]
+    return [0] + order0, [0] + order1
+
+
+def partners(n, b0, b1):
+    return [(d, d ^ (1 << (b1 if d & 1 else b0))) for d in range(n)]
+
+
 def gather_rows(x, n):
+    m = n.bit_length() - 1
     me = lax.axis_index("aux")
+    odd = (me & 1) == 1
+    order0, order1 = bit_orders(m, True)
     acc = x[None]
-    k = n.bit_length() - 2
-    while k >= 0:
-        bit = (me >> k) & 1
-        theirs = lax.ppermute(acc, "aux", [(d, d ^ (1 << k)) for d in range(n)])
+    have0, have1 = [], []
+    for b0, b1 in zip(order0, order1):
+        bit = jnp.where(odd, (me >> b1) & 1, (me >> b0) & 1)
+        theirs = lax.ppermute(acc, "aux", partners(n, b0, b1))
         lo = jnp.where(bit == 0, acc, theirs)
         hi = jnp.where(bit == 0, theirs, acc)
-        acc = jnp.stack([lo, hi], axis=1).reshape((-1,) + x.shape)
-        k -= 1
+        at0 = sum(1 for b in have0 if b > b0)
+        at1 = sum(1 for b in have1 if b > b1)
+        lead = len(have0)
+        lo = lo.reshape((2,) * lead + x.shape) if lead else lo[0]
+        hi = hi.reshape((2,) * lead + x.shape) if lead else hi[0]
+        new0 = jnp.stack([lo, hi], axis=at0)
+        if at1 == at0:
+            acc = new0
+        else:
+            acc = jnp.where(odd, jnp.stack([lo, hi], axis=at1), new0)
+        have0 = sorted(have0 + [b0], reverse=True)
+        have1 = sorted(have1 + [b1], reverse=True)
+        acc = acc.reshape((-1,) + x.shape)
     return acc.reshape((n * x.shape[0],) + x.shape[1:])
 
 
 def scatter_sum(part, n):
+    m = n.bit_length() - 1
     me = lax.axis_index("aux")
+    odd = (me & 1) == 1
     rows = part.shape[0] // n
-    acc = part.reshape((n, rows) + part.shape[1:])
-    k = 0
-    while (1 << k) < n:
-        bit = (me >> k) & 1
-        pairs = acc.reshape((acc.shape[0] // 2, 2) + acc.shape[1:])
-        keep = lax.dynamic_index_in_dim(pairs, bit, axis=1, keepdims=False)
-        send = lax.dynamic_index_in_dim(pairs, 1 - bit, axis=1, keepdims=False)
-        acc = keep + lax.ppermute(send, "aux", [(d, d ^ (1 << k)) for d in range(n)])
-        k += 1
-    return acc[0]
+    order0, order1 = bit_orders(m, False)
+    acc = part.reshape((2,) * m + (rows,) + part.shape[1:])
+    axes0 = list(range(m - 1, -1, -1))
+    axes1 = list(axes0)
+    for b0, b1 in zip(order0, order1):
+        at0, at1 = axes0.index(b0), axes1.index(b1)
+        bit0, bit1 = (me >> b0) & 1, (me >> b1) & 1
+        if at0 == at1:
+            bit = jnp.where(odd, bit1, bit0)
+            keep = lax.dynamic_index_in_dim(acc, bit, axis=at0, keepdims=False)
+            send = lax.dynamic_index_in_dim(acc, 1 - bit, axis=at0, keepdims=False)
+        else:
+            keep = jnp.where(
+                odd,
+                lax.dynamic_index_in_dim(acc, bit1, axis=at1, keepdims=False),
+                lax.dynamic_index_in_dim(acc, bit0, axis=at0, keepdims=False),
+            )
+            send = jnp.where(
+                odd,
+                lax.dynamic_index_in_dim(acc, 1 - bit1, axis=at1, keepdims=False),
+                lax.dynamic_index_in_dim(acc, 1 - bit0, axis=at0, keepdims=False),
+            )
+        acc = keep + lax.ppermute(send, "aux", partners(n, b0, b1))
+        axes0.pop(at0)
+        axes1.pop(at1)
+    return acc
 
 
 def exchange_kernel(states, occ_ref, r_ref, vir_ref, out_ref):

time: 137 us -> 125 us (0.912)
  starting transfers between devices: 24.1 us -> 15.5 us
  waiting for transfers between devices: 81 us -> 77.5 us
  other arithmetic: 5.17 us -> 7.41 us
  local copies, waits for them, and re-layouts: 6.36 us -> 4.45 us
    ppermute x16, starting transfers between devices: 24.1 us -> 15.5 us  [the longest x8 8.62 us: gather_rows(): theirs = lax.ppermute(acc, 'aux', partners(n, b0, b1))]
    ppermute x16, waiting for transfers between devices: 81 us -> 77.5 us  [the longest x8 45.1 us: scatter_sum(): acc = keep + lax.ppermute(send, 'aux', partners(n, b0, b1))]
    another operation x7 -> x1, local copies, waits for them, and re-layouts: 2.44 us -> 0.02 us  [gather_rows(): new0 = jnp.stack([lo, hi], axis=at0)]
    dynamic_slice x0 -> x3, local copies, waits for them, and re-layouts: none -> 1.85 us  [the longest x1 1.68 us: scatter_sum(): keep = lax.dynamic_index_in_dim(acc, bit, axis=at0, keepdims=False)]
    another operation x14 -> x8, other arithmetic: 0.74 us -> 2.3 us  [gather_rows(): new0 = jnp.stack([lo, hi], axis=at0)]
    squeeze x8 -> x5, local copies, waits for them, and re-layouts: 3.09 us -> 1.54 us  [scatter_sum(): send = lax.dynamic_index_in_dim(acc, 1 - bit, axis=at0, keepdims=False)]
where the time goes in v3:
time: 125 us
  waiting for transfers between devices  77.5 us (62%)
  Pallas kernels  19.4 us (16%)
  starting transfers between devices  15.5 us (12%)
  other arithmetic  7.41 us (6%)
  local copies, waits for them, and re-layouts  4.45 us (4%)
    ppermute x8, waiting for transfers between devices, scatter_sum(): acc = keep + lax.ppermute(send, 'aux', partners(n, b0, b1))  45.1 us
    ppermute x8, waiting for transfers between devices, gather_rows(): theirs = lax.ppermute(acc, 'aux', partners(n, b0, b1))  32.4 us
    pallas_call x2, Pallas kernels, exchange_part(): pl.pallas_call(functools.partial(exchange_kernel, states), grid=(local_au...  19.4 us
    ppermute x8, starting transfers between devices, gather_rows(): theirs = lax.ppermute(acc, 'aux', partners(n, b0, b1))  8.62 us
    ppermute x8, starting transfers between devices, scatter_sum(): acc = keep + lax.ppermute(send, 'aux', partners(n, b0, b1))  6.9 us
  transfers between devices with their start and end apart: 16, of which 16 were waited for; matrix products, arithmetic and copies ran while one was open for 0% of the time, Pallas kernels for 0%

profile of v3, /device:TPU:0, one launch (start us, length us, event | category | flops | bytes accessed | tf_op | source)
XLA Modules:
  0.0 124.6 jit_solution(4250986216010067286)
XLA Ops:
  0.0 0.8 dynamic_slice.68
  0.8 0.8 broadcast_subtract_fusion
  1.5 1.0 fusion.2
  2.5 4.1 %collective-permute-start = (bf16[1,16,2048]{2,1,0:T(8,128)(2,1)S(1)}, bf16[1,16,2048]{2,1,0:T(8,128)(2,1)S(1)}, u32[]{:S(2)}, u32[]{:S(2)}) collective-permute-start(bf16[1,16,2048]{2,1,0:T(8,128)(2,1)S(1)} %broadcast_in_dim_reshape.6), channel_id=1, source_target_pairs={{0,8},{1,9},{2,10},{3,11},{4,12},{5,13},{6,14},{7,15},{8,0},{9,1},... | collective-permute-start | bytes 196616 | tf_op jit(solution)/shard_map/ppermute | solution.py:36
  6.6 3.6 %collective-permute-done = bf16[1,16,2048]{2,1,0:T(8,128)(2,1)S(1)} collective-permute-done((bf16[1,16,2048]{2,1,0:T(8,128)(2,1)S(1)}, bf16[1,16,2048]{2,1,0:T(8,128)(2,1)S(1)}, u32[]{:S(2)}, u32[]{:S(2)}) %collective-permute-start) | collective-permute-done | bytes 65568 | tf_op jit(solution)/shard_map/ppermute | solution.py:36
  10.3 0.6 collective-permute-start.1
  11.0 4.4 %collective-permute-done.1 = bf16[2,16,2048]{2,1,0:T(8,128)(2,1)S(1)} collective-permute-done((bf16[2,16,2048]{2,1,0:T(8,128)(2,1)S(1)}, bf16[2,16,2048]{2,1,0:T(8,128)(2,1)S(1)}, u32[]{:S(2)}, u32[]{:S(2)}) %collective-permute-start.1) | collective-permute-done | bytes 131104 | tf_op jit(solution)/shard_map/ppermute | solution.py:36
  15.5 2.0 %collective-permute-start.2 = (bf16[4,16,2048]{2,1,0:T(8,128)(2,1)S(1)}, bf16[4,16,2048]{2,1,0:T(8,128)(2,1)S(1)}, u32[]{:S(2)}, u32[]{:S(2)}) collective-permute-start(bf16[4,16,2048]{2,1,0:T(8,128)(2,1)S(1)} %bitcast.131), channel_id=1, source_target_pairs={{0,2},{1,5},{2,0},{3,7},{4,6},{5,1},{6,4},{7,3},{8,10},{9,13},{10,... | collective-permute-start | bytes 786440 | tf_op jit(solution)/shard_map/ppermute | solution.py:36
  17.5 4.4 %collective-permute-done.2 = bf16[4,16,2048]{2,1,0:T(8,128)(2,1)S(1)} collective-permute-done((bf16[4,16,2048]{2,1,0:T(8,128)(2,1)S(1)}, bf16[4,16,2048]{2,1,0:T(8,128)(2,1)S(1)}, u32[]{:S(2)}, u32[]{:S(2)}) %collective-permute-start.2) | collective-permute-done | bytes 262176 | tf_op jit(solution)/shard_map/ppermute | solution.py:36
  21.9 0.1 broadcast_select_fusion.7
  22.0 0.1 maximum_select_fusion
  22.0 0.1 collective-permute-start.3
  22.1 1.9 %collective-permute-done.3 = bf16[8,16,2048]{2,1,0:T(8,128)(2,1)S(1)} collective-permute-done((bf16[8,16,2048]{2,1,0:T(8,128)(2,1)S(1)}, bf16[8,16,2048]{2,1,0:T(8,128)(2,1)S(1)}, u32[]{:S(2)}, u32[]{:S(2)}) %collective-permute-start.3) | collective-permute-done | bytes 524320 | tf_op jit(solution)/shard_map/ppermute | solution.py:36
  24.0 0.1 broadcast_select_fusion.3
  24.1 1.1 pad_maximum_fusion
  25.2 9.7 %shard_map.55 = f32[256,2048]{1,0:T(8,128)} custom-call(bf16[4,256,256]{2,1,0:T(8,128)(2,1)} %occ_ref.3, bf16[256,2048]{1,0:T(8,128)(2,1)} %bitcast.114, bf16[4,1024,1024]{2,1,0:T(8,128)(2,1)} %vir_ref.3), custom_call_target="tpu_custom_call" | custom-call | tf_op jit(solution)/shard_map/pallas_call | solution.py:107
  34.9 0.0 copy-start
  34.9 1.4 %dynamic-slice_bitcast_fusion = f32[2,2,2,16,2048]{4,3,2,1,0:T(8,128)S(1)} fusion(f32[2,2,2,2,16,2048]{5,4,3,2,1,0:T(8,128)} %bitcast.111, s32[]{:T(128)S(6)} %select_n.207), kind=kLoop, calls=%fused_computation.5 | loop fusion | bytes 2097156 | tf_op jit(solution)/shard_map/jit(dynamic_index_in_dim)/squeeze | solution.py:70
  36.4 0.2 collective-permute-start.4
  36.6 2.7 %collective-permute-done.4 = f32[2,2,2,16,2048]{4,3,2,1,0:T(8,128)} collective-permute-done((f32[2,2,2,16,2048]{4,3,2,1,0:T(8,128)S(1)}, f32[2,2,2,16,2048]{4,3,2,1,0:T(8,128)}, u32[]{:S(2)}, u32[]{:S(2)}) %collective-permute-start.4) | collective-permute-done | bytes 1048608 | tf_op jit(solution)/shard_map/ppermute | solution.py:82
  39.2 0.0 copy-done
  39.2 1.3 %bitcast_add_fusion = f32[2,2,2,16,2048]{4,3,2,1,0:T(8,128)S(1)} fusion(f32[2,2,2,16,2048]{4,3,2,1,0:T(8,128)} %collective-permute-done.4, f32[2,2,2,2,16,2048]{5,4,3,2,1,0:T(8,128)S(1)} %bitcast.112, s32[]{:T(128)S(6)} %select_n.206), kind=kLoop, calls=%fused_computation.2 | loop fusion | flops 262144 | bytes 3145732 | tf_op jit(solution)/shard_map/add | solution.py:82
  40.6 0.1 bitcast_select_fusion.2
  40.7 2.0 %collective-permute-start.5 = (f32[2,2,16,2048]{3,2,1,0:T(8,128)S(1)}, f32[2,2,16,2048]{3,2,1,0:T(8,128)S(1)}, u32[]{:S(2)}, u32[]{:S(2)}) collective-permute-start(f32[2,2,16,2048]{3,2,1,0:T(8,128)S(1)} %bitcast_select_fusion.2), channel_id=1, source_target_pairs={{0,2},{1,5},{2,0},{3,7},{4,6},{5,1},{6,4},{7,3},{8,10},{9,13},{10,... | collective-permute-start | bytes 1572872 | tf_op jit(solution)/shard_map/ppermute | solution.py:82
  42.7 0.0 copy-start.1
  42.7 7.2 %collective-permute-done.5 = f32[2,2,16,2048]{3,2,1,0:T(8,128)S(1)} collective-permute-done((f32[2,2,16,2048]{3,2,1,0:T(8,128)S(1)}, f32[2,2,16,2048]{3,2,1,0:T(8,128)S(1)}, u32[]{:S(2)}, u32[]{:S(2)}) %collective-permute-start.5) | collective-permute-done | bytes 524320 | tf_op jit(solution)/shard_map/ppermute | solution.py:82
  49.9 0.1 fusion.1
  50.0 0.6 collective-permute-start.6
  50.6 5.8 %collective-permute-done.6 = f32[2,16,2048]{2,1,0:T(8,128)S(1)} collective-permute-done((f32[2,16,2048]{2,1,0:T(8,128)S(1)}, f32[2,16,2048]{2,1,0:T(8,128)S(1)}, u32[]{:S(2)}, u32[]{:S(2)}) %collective-permute-start.6) | collective-permute-done | bytes 262176 | tf_op jit(solution)/shard_map/ppermute | solution.py:82
  56.5 2.0 %collective-permute-start.7 = (f32[16,2048]{1,0:T(8,128)S(1)}, f32[16,2048]{1,0:T(8,128)S(1)}, u32[]{:S(2)}, u32[]{:S(2)}) collective-permute-start(f32[16,2048]{1,0:T(8,128)S(1)} %dynamic-slice_bitcast_fusion.4), channel_id=1, source_target_pairs={{0,8},{1,9},{2,10},{3,11},{4,12},{5,13},{6,14},{7,15},{8,0},{9,1},... | collective-permute-start | bytes 393224 | tf_op jit(solution)/shard_map/ppermute | solution.py:82
  58.5 5.8 %collective-permute-done.7 = f32[16,2048]{1,0:T(8,128)S(1)} collective-permute-done((f32[16,2048]{1,0:T(8,128)S(1)}, f32[16,2048]{1,0:T(8,128)S(1)}, u32[]{:S(2)}, u32[]{:S(2)}) %collective-permute-start.7) | collective-permute-done | bytes 131104 | tf_op jit(solution)/shard_map/ppermute | solution.py:82
  64.3 0.1 reshape.58
  64.5 0.0 copy-done.1
  64.5 0.2 fusion.3
  64.7 0.2 collective-permute-start.8
  64.9 5.7 %collective-permute-done.8 = bf16[1,16,2048]{2,1,0:T(8,128)(2,1)S(1)} collective-permute-done((bf16[1,16,2048]{2,1,0:T(8,128)(2,1)S(1)}, bf16[1,16,2048]{2,1,0:T(8,128)(2,1)S(1)}, u32[]{:S(2)}, u32[]{:S(2)}) %collective-permute-start.8) | collective-permute-done | bytes 65568 | tf_op jit(solution)/shard_map/ppermute | solution.py:36
  70.6 0.1 collective-permute-start.9
  70.7 5.4 %collective-permute-done.9 = bf16[2,16,2048]{2,1,0:T(8,128)(2,1)S(1)} collective-permute-done((bf16[2,16,2048]{2,1,0:T(8,128)(2,1)S(1)}, bf16[2,16,2048]{2,1,0:T(8,128)(2,1)S(1)}, u32[]{:S(2)}, u32[]{:S(2)}) %collective-permute-start.9) | collective-permute-done | bytes 131104 | tf_op jit(solution)/shard_map/ppermute | solution.py:36
  76.2 1.5 %collective-permute-start.10 = (bf16[4,16,2048]{2,1,0:T(8,128)(2,1)S(1)}, bf16[4,16,2048]{2,1,0:T(8,128)(2,1)S(1)}, u32[]{:S(2)}, u32[]{:S(2)}) collective-permute-start(bf16[4,16,2048]{2,1,0:T(8,128)(2,1)S(1)} %bitcast.132), channel_id=1, source_target_pairs={{0,2},{1,5},{2,0},{3,7},{4,6},{5,1},{6,4},{7,3},{8,10},{9,13},{10,... | collective-permute-start | bytes 786440 | tf_op jit(solution)/shard_map/ppermute | solution.py:36
  77.6 5.0 %collective-permute-done.10 = bf16[4,16,2048]{2,1,0:T(8,128)(2,1)S(1)} collective-permute-done((bf16[4,16,2048]{2,1,0:T(8,128)(2,1)S(1)}, bf16[4,16,2048]{2,1,0:T(8,128)(2,1)S(1)}, u32[]{:S(2)}, u32[]{:S(2)}) %collective-permute-start.10) | collective-permute-done | bytes 262176 | tf_op jit(solution)/shard_map/ppermute | solution.py:36
  82.6 0.1 broadcast_select_fusion.5
  82.7 0.1 maximum_select_fusion.1
  82.8 0.1 collective-permute-start.11
  82.8 1.9 %collective-permute-done.11 = bf16[8,16,2048]{2,1,0:T(8,128)(2,1)S(1)} collective-permute-done((bf16[8,16,2048]{2,1,0:T(8,128)(2,1)S(1)}, bf16[8,16,2048]{2,1,0:T(8,128)(2,1)S(1)}, u32[]{:S(2)}, u32[]{:S(2)}) %collective-permute-start.11) | collective-permute-done | bytes 524320 | tf_op jit(solution)/shard_map/ppermute | solution.py:36
  84.7 0.1 broadcast_select_fusion.1
  84.8 1.1 pad_maximum_fusion.1
  85.9 9.7 %shard_map.56 = f32[256,2048]{1,0:T(8,128)} custom-call(bf16[4,256,256]{2,1,0:T(8,128)(2,1)} %occ_ref.3, bf16[256,2048]{1,0:T(8,128)(2,1)} %bitcast.115, bf16[4,1024,1024]{2,1,0:T(8,128)(2,1)} %vir_ref.3), custom_call_target="tpu_custom_call" | custom-call | tf_op jit(solution)/shard_map/pallas_call | solution.py:107
  95.6 1.7 %constant_dynamic-slice_fusion.3 = (f32[2,2,2,1,16,2048]{5,4,3,2,1,0:T(8,128)S(1)}, f32[2,2,2,1,16,2048]{5,4,3,2,1,0:T(8,128)S(1)}) fusion(f32[2,2,2,2,16,2048]{5,4,3,2,1,0:T(8,128)} %bitcast.113, s32[]{:T(128)S(6)} %select_n.206, s32[]{:T(128)S(6)} %select_n.207), kind=kLoop, calls=%fused_computation.49 | loop fusion | bytes 4194312 | tf_op jit(solution)/shard_map/jit(dynamic_index_in_dim)/dynamic_slice | solution.py:69
  97.3 0.1 copy.46
  97.4 0.2 collective-permute-start.12
  97.6 2.5 %collective-permute-done.12 = f32[2,2,2,16,2048]{4,3,2,0,1:T(8,128)S(1)} collective-permute-done((f32[2,2,2,16,2048]{4,3,2,0,1:T(8,128)S(1)}, f32[2,2,2,16,2048]{4,3,2,0,1:T(8,128)S(1)}, u32[]{:S(2)}, u32[]{:S(2)}) %collective-permute-start.12) | collective-permute-done | bytes 1048608 | tf_op jit(solution)/shard_map/ppermute | solution.py:82
  100.2 0.2 bitcast_add_fusion.1
  100.3 0.1 constant_dynamic-slice_fusion.1
  100.4 0.1 bitcast_select_fusion
  100.5 1.5 %collective-permute-start.13 = (f32[2,2,16,2048]{3,2,1,0:T(8,128)S(1)}, f32[2,2,16,2048]{3,2,1,0:T(8,128)S(1)}, u32[]{:S(2)}, u32[]{:S(2)}) collective-permute-start(f32[2,2,16,2048]{3,2,1,0:T(8,128)S(1)} %bitcast_select_fusion), channel_id=1, source_target_pairs={{0,2},{1,5},{2,0},{3,7},{4,6},{5,1},{6,4},{7,3},{8,10},{9,13},{10,... | collective-permute-start | bytes 1572872 | tf_op jit(solution)/shard_map/ppermute | solution.py:82
  101.9 7.8 %collective-permute-done.13 = f32[2,2,16,2048]{3,2,1,0:T(8,128)S(1)} collective-permute-done((f32[2,2,16,2048]{3,2,1,0:T(8,128)S(1)}, f32[2,2,16,2048]{3,2,1,0:T(8,128)S(1)}, u32[]{:S(2)}, u32[]{:S(2)}) %collective-permute-start.13) | collective-permute-done | bytes 524320 | tf_op jit(solution)/shard_map/ppermute | solution.py:82
  109.7 0.1 fusion
  109.8 0.1 collective-permute-start.14
  109.9 6.4 %collective-permute-done.14 = f32[2,16,2048]{2,1,0:T(8,128)S(1)} collective-permute-done((f32[2,16,2048]{2,1,0:T(8,128)S(1)}, f32[2,16,2048]{2,1,0:T(8,128)S(1)}, u32[]{:S(2)}, u32[]{:S(2)}) %collective-permute-start.14) | collective-permute-done | bytes 262176 | tf_op jit(solution)/shard_map/ppermute | solution.py:82
  116.3 0.4 collective-permute-start.15
  116.7 6.9 %collective-permute-done.15 = f32[16,2048]{1,0:T(8,128)S(1)} collective-permute-done((f32[16,2048]{1,0:T(8,128)S(1)}, f32[16,2048]{1,0:T(8,128)S(1)}, u32[]{:S(2)}, u32[]{:S(2)}) %collective-permute-start.15) | collective-permute-done | bytes 131104 | tf_op jit(solution)/shard_map/ppermute | solution.py:82
  123.7 0.1 reshape.61
  123.8 0.8 divide_add_fusion
  (19 shorter events, 0.4 us)
Async XLA Ops:
  2.5 7.8 %collective-permute-start = (bf16[1,16,2048]{2,1,0:T(8,128)(2,1)S(1)}, bf16[1,16,2048]{2,1,0:T(8,128)(2,1)S(1)}, u32[]{:S(2)}, u32[]{:S(2)}) collective-permute-start(bf16[1,16,2048]{2,1,0:T(8,128)(2,1)S(1)} %broadcast_in_dim_reshape.6), channel_id=1, source_target_pairs={{0,8},{1,9},{2,10},{3,11},{4,12},{5,13},{6,14},{7,15},{8,0},{9,1},... | collective-permute-start | bytes 196616 | tf_op jit(solution)/shard_map/ppermute | solution.py:36
  10.3 5.1 %collective-permute-start.1 = (bf16[2,16,2048]{2,1,0:T(8,128)(2,1)S(1)}, bf16[2,16,2048]{2,1,0:T(8,128)(2,1)S(1)}, u32[]{:S(2)}, u32[]{:S(2)}) collective-permute-start(bf16[2,16,2048]{2,1,0:T(8,128)(2,1)S(1)} %pad_maximum_fusion.4), channel_id=1, source_target_pairs={{0,4},{1,3},{2,6},{3,1},{4,0},{5,7},{6,2},{7,5},{8,12},{9,11},{10,... | collective-permute-start | bytes 393224 | tf_op jit(solution)/shard_map/ppermute | solution.py:36
  15.5 6.4 %collective-permute-start.2 = (bf16[4,16,2048]{2,1,0:T(8,128)(2,1)S(1)}, bf16[4,16,2048]{2,1,0:T(8,128)(2,1)S(1)}, u32[]{:S(2)}, u32[]{:S(2)}) collective-permute-start(bf16[4,16,2048]{2,1,0:T(8,128)(2,1)S(1)} %bitcast.131), channel_id=1, source_target_pairs={{0,2},{1,5},{2,0},{3,7},{4,6},{5,1},{6,4},{7,3},{8,10},{9,13},{10,... | collective-permute-start | bytes 786440 | tf_op jit(solution)/shard_map/ppermute | solution.py:36
  22.0 2.0 %collective-permute-start.3 = (bf16[8,16,2048]{2,1,0:T(8,128)(2,1)S(1)}, bf16[8,16,2048]{2,1,0:T(8,128)(2,1)S(1)}, u32[]{:S(2)}, u32[]{:S(2)}) collective-permute-start(bf16[8,16,2048]{2,1,0:T(8,128)(2,1)S(1)} %bitcast.124), channel_id=1, source_target_pairs={{0,1},{1,0},{2,3},{3,2},{4,5},{5,4},{6,7},{7,6},{8,9},{9,8},{10,11... | collective-permute-start | bytes 1572872 | tf_op jit(solution)/shard_map/ppermute | solution.py:36
  34.9 4.3 %copy-start = (f32[256,2048]{1,0:T(8,128)S(1)}, f32[256,2048]{1,0:T(8,128)}, u32[]{:S(2)}) copy-start(f32[256,2048]{1,0:T(8,128)} %shard_map.55) | copy-start | bytes 6291460
  36.4 2.9 %collective-permute-start.4 = (f32[2,2,2,16,2048]{4,3,2,1,0:T(8,128)S(1)}, f32[2,2,2,16,2048]{4,3,2,1,0:T(8,128)}, u32[]{:S(2)}, u32[]{:S(2)}) collective-permute-start(f32[2,2,2,16,2048]{4,3,2,1,0:T(8,128)S(1)} %dynamic-slice_bitcast_fusion), channel_id=1, source_target_pairs={{0,1},{1,0},{2,3},{3,2},{4,5},{5,4},{6,7},{7,6},{8,9},{9,8},{10,11... | collective-permute-start | bytes 3145736 | tf_op jit(solution)/shard_map/ppermute | solution.py:82
  40.7 9.2 %collective-permute-start.5 = (f32[2,2,16,2048]{3,2,1,0:T(8,128)S(1)}, f32[2,2,16,2048]{3,2,1,0:T(8,128)S(1)}, u32[]{:S(2)}, u32[]{:S(2)}) collective-permute-start(f32[2,2,16,2048]{3,2,1,0:T(8,128)S(1)} %bitcast_select_fusion.2), channel_id=1, source_target_pairs={{0,2},{1,5},{2,0},{3,7},{4,6},{5,1},{6,4},{7,3},{8,10},{9,13},{10,... | collective-permute-start | bytes 1572872 | tf_op jit(solution)/shard_map/ppermute | solution.py:82
  42.7 21.8 %copy-start.1 = (f32[16,2,1024]{2,1,0:T(2,128)S(1)}, f32[16,2,1024]{2,1,0:T(2,128)}, u32[]{:S(2)}) copy-start(f32[16,2,1024]{2,1,0:T(2,128)} %param.5) | copy-start | bytes 393220
  50.0 6.4 %collective-permute-start.6 = (f32[2,16,2048]{2,1,0:T(8,128)S(1)}, f32[2,16,2048]{2,1,0:T(8,128)S(1)}, u32[]{:S(2)}, u32[]{:S(2)}) collective-permute-start(f32[2,16,2048]{2,1,0:T(8,128)S(1)} %dynamic-slice_bitcast_fusion.2), channel_id=1, source_target_pairs={{0,4},{1,3},{2,6},{3,1},{4,0},{5,7},{6,2},{7,5},{8,12},{9,11},{10,... | collective-permute-start | bytes 786440 | tf_op jit(solution)/shard_map/ppermute | solution.py:82
  56.5 7.8 %collective-permute-start.7 = (f32[16,2048]{1,0:T(8,128)S(1)}, f32[16,2048]{1,0:T(8,128)S(1)}, u32[]{:S(2)}, u32[]{:S(2)}) collective-permute-start(f32[16,2048]{1,0:T(8,128)S(1)} %dynamic-slice_bitcast_fusion.4), channel_id=1, source_target_pairs={{0,8},{1,9},{2,10},{3,11},{4,12},{5,13},{6,14},{7,15},{8,0},{9,1},... | collective-permute-start | bytes 393224 | tf_op jit(solution)/shard_map/ppermute | solution.py:82
  64.7 5.9 %collective-permute-start.8 = (bf16[1,16,2048]{2,1,0:T(8,128)(2,1)S(1)}, bf16[1,16,2048]{2,1,0:T(8,128)(2,1)S(1)}, u32[]{:S(2)}, u32[]{:S(2)}) collective-permute-start(bf16[1,16,2048]{2,1,0:T(8,128)(2,1)S(1)} %broadcast_in_dim_reshape.7), channel_id=1, source_target_pairs={{0,8},{1,9},{2,10},{3,11},{4,12},{5,13},{6,14},{7,15},{8,0},{9,1},... | collective-permute-start | bytes 196616 | tf_op jit(solution)/shard_map/ppermute | solution.py:36
  70.6 5.5 %collective-permute-start.9 = (bf16[2,16,2048]{2,1,0:T(8,128)(2,1)S(1)}, bf16[2,16,2048]{2,1,0:T(8,128)(2,1)S(1)}, u32[]{:S(2)}, u32[]{:S(2)}) collective-permute-start(bf16[2,16,2048]{2,1,0:T(8,128)(2,1)S(1)} %pad_maximum_fusion.5), channel_id=1, source_target_pairs={{0,4},{1,3},{2,6},{3,1},{4,0},{5,7},{6,2},{7,5},{8,12},{9,11},{10,... | collective-permute-start | bytes 393224 | tf_op jit(solution)/shard_map/ppermute | solution.py:36
  76.2 6.4 %collective-permute-start.10 = (bf16[4,16,2048]{2,1,0:T(8,128)(2,1)S(1)}, bf16[4,16,2048]{2,1,0:T(8,128)(2,1)S(1)}, u32[]{:S(2)}, u32[]{:S(2)}) collective-permute-start(bf16[4,16,2048]{2,1,0:T(8,128)(2,1)S(1)} %bitcast.132), channel_id=1, source_target_pairs={{0,2},{1,5},{2,0},{3,7},{4,6},{5,1},{6,4},{7,3},{8,10},{9,13},{10,... | collective-permute-start | bytes 786440 | tf_op jit(solution)/shard_map/ppermute | solution.py:36
  82.8 2.0 %collective-permute-start.11 = (bf16[8,16,2048]{2,1,0:T(8,128)(2,1)S(1)}, bf16[8,16,2048]{2,1,0:T(8,128)(2,1)S(1)}, u32[]{:S(2)}, u32[]{:S(2)}) collective-permute-start(bf16[8,16,2048]{2,1,0:T(8,128)(2,1)S(1)} %bitcast.125), channel_id=1, source_target_pairs={{0,1},{1,0},{2,3},{3,2},{4,5},{5,4},{6,7},{7,6},{8,9},{9,8},{10,11... | collective-permute-start | bytes 1572872 | tf_op jit(solution)/shard_map/ppermute | solution.py:36
  97.4 2.7 %collective-permute-start.12 = (f32[2,2,2,16,2048]{4,3,2,0,1:T(8,128)S(1)}, f32[2,2,2,16,2048]{4,3,2,0,1:T(8,128)S(1)}, u32[]{:S(2)}, u32[]{:S(2)}) collective-permute-start(f32[2,2,2,16,2048]{4,3,2,0,1:T(8,128)S(1)} %bitcast.130), channel_id=1, source_target_pairs={{0,1},{1,0},{2,3},{3,2},{4,5},{5,4},{6,7},{7,6},{8,9},{9,8},{10,11... | collective-permute-start | bytes 3145736 | tf_op jit(solution)/shard_map/ppermute | solution.py:82
  100.5 9.2 %collective-permute-start.13 = (f32[2,2,16,2048]{3,2,1,0:T(8,128)S(1)}, f32[2,2,16,2048]{3,2,1,0:T(8,128)S(1)}, u32[]{:S(2)}, u32[]{:S(2)}) collective-permute-start(f32[2,2,16,2048]{3,2,1,0:T(8,128)S(1)} %bitcast_select_fusion), channel_id=1, source_target_pairs={{0,2},{1,5},{2,0},{3,7},{4,6},{5,1},{6,4},{7,3},{8,10},{9,13},{10,... | collective-permute-start | bytes 1572872 | tf_op jit(solution)/shard_map/ppermute | solution.py:82
  109.8 6.4 %collective-permute-start.14 = (f32[2,16,2048]{2,1,0:T(8,128)S(1)}, f32[2,16,2048]{2,1,0:T(8,128)S(1)}, u32[]{:S(2)}, u32[]{:S(2)}) collective-permute-start(f32[2,16,2048]{2,1,0:T(8,128)S(1)} %dynamic-slice_bitcast_fusion.1), channel_id=1, source_target_pairs={{0,4},{1,3},{2,6},{3,1},{4,0},{5,7},{6,2},{7,5},{8,12},{9,11},{10,... | collective-permute-start | bytes 786440 | tf_op jit(solution)/shard_map/ppermute | solution.py:82
  116.3 7.3 %collective-permute-start.15 = (f32[16,2048]{1,0:T(8,128)S(1)}, f32[16,2048]{1,0:T(8,128)S(1)}, u32[]{:S(2)}, u32[]{:S(2)}) collective-permute-start(f32[16,2048]{1,0:T(8,128)S(1)} %dynamic-slice_bitcast_fusion.3), channel_id=1, source_target_pairs={{0,8},{1,9},{2,10},{3,11},{4,12},{5,13},{6,14},{7,15},{8,0},{9,1},... | collective-permute-start | bytes 393224 | tf_op jit(solution)/shard_map/ppermute | solution.py:82

commit v4 on v3

--- a/solution.py
+++ b/solution.py
@@ -128,13 +128,19 @@
     position = lax.axis_index("aux")
     my_occ = lax.dynamic_slice_in_dim(occ_energy, position * own_rows, own_rows, 0)
     denom = vir_energy[None, None, :] - my_occ[:, None, None]
-    response = rhs / denom
-    for step in range(ITERS):
-        rounded = response.astype(jnp.bfloat16).reshape(own_rows, states * nvir)
-        flat = gather_rows(rounded, n)
-        part = exchange_part(occ_ints, flat, vir_ints, states)
-        exchange = scatter_sum(part, n).reshape(own_rows, states, nvir)
-        response = 0.4 * response + 0.6 * (rhs - exchange) / denom
+    finals = []
+    for state in range(states):
+        own_rhs = rhs[:, state, :]
+        own_denom = denom[:, 0, :]
+        resp = own_rhs / own_denom
+        for step in range(ITERS):
+            rounded = resp.astype(jnp.bfloat16)
+            flat = gather_rows(rounded, n)
+            part = exchange_part(occ_ints, flat, vir_ints, 1)
+            exchange = scatter_sum(part, n)
+            resp = 0.4 * resp + 0.6 * (own_rhs - exchange) / own_denom
+        finals.append(resp)
+    response = jnp.stack(finals, axis=1)
     return response
 
 

time: 125 us -> 122 us (0.976)
  waiting for transfers between devices: 77.5 us -> 41.2 us
  starting transfers between devices: 15.5 us -> 38.1 us
  Pallas kernels: 19.4 us -> 28.8 us
  local copies, waits for them, and re-layouts: 4.45 us -> 7.09 us
  other arithmetic: 7.41 us -> 5.71 us
    ppermute x8 -> x16, waiting for transfers between devices: 45.1 us -> 23.7 us  [scatter_sum(): acc = keep + lax.ppermute(send, 'aux', partners(n, b0, b1))]
    ppermute x8 -> x16, waiting for transfers between devices: 32.4 us -> 17.5 us  [gather_rows(): theirs = lax.ppermute(acc, 'aux', partners(n, b0, b1))]
    ppermute x8 -> x16, starting transfers between devices: 6.9 us -> 20.4 us  [scatter_sum(): acc = keep + lax.ppermute(send, 'aux', partners(n, b0, b1))]
    pallas_call x2 -> x4, Pallas kernels: 19.4 us -> 28.8 us  [exchange_part(): pl.pallas_call(functools.partial(exchange_kernel, states), grid=(local_au...]
    ppermute x8 -> x16, starting transfers between devices: 8.62 us -> 17.8 us  [gather_rows(): theirs = lax.ppermute(acc, 'aux', partners(n, b0, b1))]
    dynamic_slice x1 -> x3, local copies, waits for them, and re-layouts: 1.68 us -> 3.98 us  [scatter_sum(): keep = lax.dynamic_index_in_dim(acc, bit, axis=at0, keepdims=False)]
    squeeze x5 -> x8, local copies, waits for them, and re-layouts: 1.54 us -> 0.13 us  [scatter_sum(): send = lax.dynamic_index_in_dim(acc, 1 - bit, axis=at0, keepdims=False)]
    another operation x8 -> x16, other arithmetic: 2.3 us -> 3.52 us  [gather_rows(): new0 = jnp.stack([lo, hi], axis=at0)]
  transfers between devices with their start and end apart: 16 -> 32, of which waited for: 16 -> 26; matrix products, arithmetic and copies ran while one was open for 0% -> 6% of each run, Pallas kernels for 0% -> 18%
where the time goes in v4:
time: 122 us; the launch traced here: 121 us
  waiting for transfers between devices  41.2 us (34%)
  starting transfers between devices  38.1 us (31%)
  Pallas kernels  28.8 us (24%)
  local copies, waits for them, and re-layouts  7.09 us (6%)
  other arithmetic  5.71 us (5%)
    pallas_call x4, Pallas kernels, exchange_part(): pl.pallas_call(functools.partial(exchange_kernel, states), grid=(local_au...  28.8 us
    ppermute x16, waiting for transfers between devices, scatter_sum(): acc = keep + lax.ppermute(send, 'aux', partners(n, b0, b1))  23.7 us
    ppermute x16, starting transfers between devices, scatter_sum(): acc = keep + lax.ppermute(send, 'aux', partners(n, b0, b1))  20.4 us
    ppermute x16, starting transfers between devices, gather_rows(): theirs = lax.ppermute(acc, 'aux', partners(n, b0, b1))  17.8 us
    ppermute x16, waiting for transfers between devices, gather_rows(): theirs = lax.ppermute(acc, 'aux', partners(n, b0, b1))  17.5 us
    dynamic_slice x3, local copies, waits for them, and re-layouts, scatter_sum(): keep = lax.dynamic_index_in_dim(acc, bit, axis=at0, keepdims=False)  3.98 us
    another operation x16, other arithmetic, gather_rows(): new0 = jnp.stack([lo, hi], axis=at0)  3.52 us
  transfers between devices with their start and end apart: 32, of which 26 were waited for; matrix products, arithmetic and copies ran while one was open for 6% of the time, Pallas kernels for 18%

profile of v4, /device:TPU:0, one launch (start us, length us, event | category | flops | bytes accessed | tf_op | source)
XLA Modules:
  0.0 121.5 jit_solution(8325356184727498418)
XLA Ops:
  0.0 1.1 fusion.24
  1.1 0.8 dynamic_slice.128
  1.9 0.8 fusion.4
  2.6 4.1 %collective-permute-start = (bf16[1,16,1024]{2,1,0:T(8,128)(2,1)S(1)}, bf16[1,16,1024]{2,1,0:T(8,128)(2,1)S(1)}, u32[]{:S(2)}, u32[]{:S(2)}) collective-permute-start(bf16[1,16,1024]{2,1,0:T(8,128)(2,1)S(1)} %get-tuple-element.63), channel_id=1, source_target_pairs={{0,8},{1,9},{2,10},{3,11},{4,12},{5,13},{6,14},{7,15},{8,0},{9,1},... | collective-permute-start | bytes 98312 | tf_op jit(solution)/shard_map/ppermute | solution.py:36
  6.8 2.2 %collective-permute-done = bf16[1,16,1024]{2,1,0:T(8,128)(2,1)S(1)} collective-permute-done((bf16[1,16,1024]{2,1,0:T(8,128)(2,1)S(1)}, bf16[1,16,1024]{2,1,0:T(8,128)(2,1)S(1)}, u32[]{:S(2)}, u32[]{:S(2)}) %collective-permute-start) | collective-permute-done | bytes 32800 | tf_op jit(solution)/shard_map/ppermute | solution.py:36
  9.0 1.7 %collective-permute-start.1 = (bf16[2,16,1024]{2,1,0:T(8,128)(2,1)S(1)}, bf16[2,16,1024]{2,1,0:T(8,128)(2,1)S(1)}, u32[]{:S(2)}, u32[]{:S(2)}) collective-permute-start(bf16[2,16,1024]{2,1,0:T(8,128)(2,1)S(1)} %pad_maximum_fusion.9), channel_id=1, source_target_pairs={{0,4},{1,3},{2,6},{3,1},{4,0},{5,7},{6,2},{7,5},{8,12},{9,11},{10,... | collective-permute-start | bytes 196616 | tf_op jit(solution)/shard_map/ppermute | solution.py:36
  10.7 0.9 collective-permute-done.16
  11.6 1.6 %collective-permute-start.17 = (bf16[2,16,1024]{2,1,0:T(8,128)(2,1)S(1)}, bf16[2,16,1024]{2,1,0:T(8,128)(2,1)S(1)}, u32[]{:S(2)}, u32[]{:S(2)}) collective-permute-start(bf16[2,16,1024]{2,1,0:T(8,128)(2,1)S(1)} %pad_maximum_fusion.11), channel_id=1, source_target_pairs={{0,4},{1,3},{2,6},{3,1},{4,0},{5,7},{6,2},{7,5},{8,12},{9,11},{10,... | collective-permute-start | bytes 196616 | tf_op jit(solution)/shard_map/ppermute | solution.py:36
  13.4 1.8 %collective-permute-start.2 = (bf16[4,16,1024]{2,1,0:T(8,128)(2,1)S(1)}, bf16[4,16,1024]{2,1,0:T(8,128)(2,1)S(1)}, u32[]{:S(2)}, u32[]{:S(2)}) collective-permute-start(bf16[4,16,1024]{2,1,0:T(8,128)(2,1)S(1)} %bitcast.296), channel_id=1, source_target_pairs={{0,2},{1,5},{2,0},{3,7},{4,6},{5,1},{6,4},{7,3},{8,10},{9,13},{10,... | collective-permute-start | bytes 393224 | tf_op jit(solution)/shard_map/ppermute | solution.py:36
  15.1 1.2 collective-permute-done.17
  16.4 1.1 collective-permute-start.18
  17.5 0.9 collective-permute-done.2
  18.6 2.9 %collective-permute-done.18 = bf16[4,16,1024]{2,1,0:T(8,128)(2,1)S(1)} collective-permute-done((bf16[4,16,1024]{2,1,0:T(8,128)(2,1)S(1)}, bf16[4,16,1024]{2,1,0:T(8,128)(2,1)S(1)}, u32[]{:S(2)}, u32[]{:S(2)}) %collective-permute-start.18) | collective-permute-done | bytes 131104 | tf_op jit(solution)/shard_map/ppermute | solution.py:36
  21.7 0.8 pad_maximum_fusion
  22.5 7.2 %shard_map.55 = f32[256,1024]{1,0:T(8,128)} custom-call(bf16[4,256,256]{2,1,0:T(8,128)(2,1)} %occ_ref.7, bf16[256,1024]{1,0:T(8,128)(2,1)} %bitcast.264, bf16[4,1024,1024]{2,1,0:T(8,128)(2,1)} %vir_ref.7), custom_call_target="tpu_custom_call" | custom-call | tf_op jit(solution)/shard_map/pallas_call | solution.py:107
  29.7 1.3 %constant_dynamic-slice_fusion.15 = (f32[2,2,2,1,16,1024]{5,4,3,2,1,0:T(8,128)S(1)}, f32[2,2,2,1,16,1024]{5,4,3,2,1,0:T(8,128)S(1)}) fusion(f32[2,2,2,2,16,1024]{5,4,3,2,1,0:T(8,128)} %bitcast.262, s32[]{:T(128)S(6)} %select_n.336, s32[]{:T(128)S(6)} %select_n.337), kind=kLoop, calls=%fused_computation.128 | loop fusion | bytes 2097160 | tf_op jit(solution)/shard_map/jit(dynamic_index_in_dim)/dynamic_slice | solution.py:69
  31.1 0.6 collective-permute-start.4
  31.7 0.8 pad_maximum_fusion.2
  32.5 7.2 %shard_map.57 = f32[256,1024]{1,0:T(8,128)} custom-call(bf16[4,256,256]{2,1,0:T(8,128)(2,1)} %occ_ref.7, bf16[256,1024]{1,0:T(8,128)(2,1)} %bitcast.265, bf16[4,1024,1024]{2,1,0:T(8,128)(2,1)} %vir_ref.7), custom_call_target="tpu_custom_call" | custom-call | tf_op jit(solution)/shard_map/pallas_call | solution.py:107
  39.7 1.3 %constant_dynamic-slice_fusion.7 = (f32[2,2,2,1,16,1024]{5,4,3,2,1,0:T(8,128)S(1)}, f32[2,2,2,1,16,1024]{5,4,3,2,1,0:T(8,128)S(1)}) fusion(f32[2,2,2,2,16,1024]{5,4,3,2,1,0:T(8,128)} %bitcast.263, s32[]{:T(128)S(6)} %select_n.336, s32[]{:T(128)S(6)} %select_n.337), kind=kLoop, calls=%fused_computation.120 | loop fusion | bytes 2097160 | tf_op jit(solution)/shard_map/jit(dynamic_index_in_dim)/dynamic_slice | solution.py:69
  41.4 1.1 collective-permute-start.5
  42.5 0.6 collective-permute-done.20
  43.2 1.1 collective-permute-start.21
  44.4 3.5 %collective-permute-done.5 = f32[2,2,16,1024]{3,2,1,0:T(8,128)S(1)} collective-permute-done((f32[2,2,16,1024]{3,2,1,0:T(8,128)S(1)}, f32[2,2,16,1024]{3,2,1,0:T(8,128)S(1)}, u32[]{:S(2)}, u32[]{:S(2)}) %collective-permute-start.5) | collective-permute-done | bytes 262176 | tf_op jit(solution)/shard_map/ppermute | solution.py:82
  47.9 1.4 %collective-permute-start.6 = (f32[2,16,1024]{2,1,0:T(8,128)S(1)}, f32[2,16,1024]{2,1,0:T(8,128)S(1)}, u32[]{:S(2)}, u32[]{:S(2)}) collective-permute-start(f32[2,16,1024]{2,1,0:T(8,128)S(1)} %dynamic-slice_bitcast_fusion.3), channel_id=1, source_target_pairs={{0,4},{1,3},{2,6},{3,1},{4,0},{5,7},{6,2},{7,5},{8,12},{9,11},{10,... | collective-permute-start | bytes 393224 | tf_op jit(solution)/shard_map/ppermute | solution.py:82
  49.3 1.7 %collective-permute-done.21 = f32[2,2,16,1024]{3,2,1,0:T(8,128)S(1)} collective-permute-done((f32[2,2,16,1024]{3,2,1,0:T(8,128)S(1)}, f32[2,2,16,1024]{3,2,1,0:T(8,128)S(1)}, u32[]{:S(2)}, u32[]{:S(2)}) %collective-permute-start.21) | collective-permute-done | bytes 262176 | tf_op jit(solution)/shard_map/ppermute | solution.py:82
  51.1 1.4 %collective-permute-start.22 = (f32[2,16,1024]{2,1,0:T(8,128)S(1)}, f32[2,16,1024]{2,1,0:T(8,128)S(1)}, u32[]{:S(2)}, u32[]{:S(2)}) collective-permute-start(f32[2,16,1024]{2,1,0:T(8,128)S(1)} %dynamic-slice_bitcast_fusion.1), channel_id=1, source_target_pairs={{0,4},{1,3},{2,6},{3,1},{4,0},{5,7},{6,2},{7,5},{8,12},{9,11},{10,... | collective-permute-start | bytes 393224 | tf_op jit(solution)/shard_map/ppermute | solution.py:82
  52.4 0.5 collective-permute-done.6
  53.0 2.9 %collective-permute-start.7 = (f32[16,1024]{1,0:T(8,128)S(1)}, f32[16,1024]{1,0:T(8,128)S(1)}, u32[]{:S(2)}, u32[]{:S(2)}) collective-permute-start(f32[16,1024]{1,0:T(8,128)S(1)} %dynamic-slice_bitcast_fusion.7), channel_id=1, source_target_pairs={{0,8},{1,9},{2,10},{3,11},{4,12},{5,13},{6,14},{7,15},{8,0},{9,1},... | collective-permute-start | bytes 196616 | tf_op jit(solution)/shard_map/ppermute | solution.py:82
  55.9 0.9 collective-permute-done.22
  56.8 2.4 %collective-permute-start.23 = (f32[16,1024]{1,0:T(8,128)S(1)}, f32[16,1024]{1,0:T(8,128)S(1)}, u32[]{:S(2)}, u32[]{:S(2)}) collective-permute-start(f32[16,1024]{1,0:T(8,128)S(1)} %dynamic-slice_bitcast_fusion.5), channel_id=1, source_target_pairs={{0,8},{1,9},{2,10},{3,11},{4,12},{5,13},{6,14},{7,15},{8,0},{9,1},... | collective-permute-start | bytes 196616 | tf_op jit(solution)/shard_map/ppermute | solution.py:82
  59.3 3.5 %collective-permute-done.23 = f32[16,1024]{1,0:T(8,128)S(1)} collective-permute-done((f32[16,1024]{1,0:T(8,128)S(1)}, f32[16,1024]{1,0:T(8,128)S(1)}, u32[]{:S(2)}, u32[]{:S(2)}) %collective-permute-start.23) | collective-permute-done | bytes 65568 | tf_op jit(solution)/shard_map/ppermute | solution.py:82
  62.9 1.8 %collective-permute-start.24 = (bf16[1,16,1024]{2,1,0:T(8,128)(2,1)S(1)}, bf16[1,16,1024]{2,1,0:T(8,128)(2,1)S(1)}, u32[]{:S(2)}, u32[]{:S(2)}) collective-permute-start(bf16[1,16,1024]{2,1,0:T(8,128)(2,1)S(1)} %get-tuple-element.61), channel_id=1, source_target_pairs={{0,8},{1,9},{2,10},{3,11},{4,12},{5,13},{6,14},{7,15},{8,0},{9,1},... | collective-permute-start | bytes 98312 | tf_op jit(solution)/shard_map/ppermute | solution.py:36
  64.7 1.2 collective-permute-start.8
  65.9 2.2 %collective-permute-done.24 = bf16[1,16,1024]{2,1,0:T(8,128)(2,1)S(1)} collective-permute-done((bf16[1,16,1024]{2,1,0:T(8,128)(2,1)S(1)}, bf16[1,16,1024]{2,1,0:T(8,128)(2,1)S(1)}, u32[]{:S(2)}, u32[]{:S(2)}) %collective-permute-start.24) | collective-permute-done | bytes 32800 | tf_op jit(solution)/shard_map/ppermute | solution.py:36
  68.1 0.6 collective-permute-start.25
  68.7 0.8 collective-permute-done.8
  69.5 2.0 %collective-permute-start.9 = (bf16[2,16,1024]{2,1,0:T(8,128)(2,1)S(1)}, bf16[2,16,1024]{2,1,0:T(8,128)(2,1)S(1)}, u32[]{:S(2)}, u32[]{:S(2)}) collective-permute-start(bf16[2,16,1024]{2,1,0:T(8,128)(2,1)S(1)} %pad_maximum_fusion.10), channel_id=1, source_target_pairs={{0,4},{1,3},{2,6},{3,1},{4,0},{5,7},{6,2},{7,5},{8,12},{9,11},{10,... | collective-permute-start | bytes 196616 | tf_op jit(solution)/shard_map/ppermute | solution.py:36
  71.6 1.6 %collective-permute-done.25 = bf16[2,16,1024]{2,1,0:T(8,128)(2,1)S(1)} collective-permute-done((bf16[2,16,1024]{2,1,0:T(8,128)(2,1)S(1)}, bf16[2,16,1024]{2,1,0:T(8,128)(2,1)S(1)}, u32[]{:S(2)}, u32[]{:S(2)}) %collective-permute-start.25) | collective-permute-done | bytes 65568 | tf_op jit(solution)/shard_map/ppermute | solution.py:36
  73.3 1.3 %collective-permute-done.9 = bf16[2,16,1024]{2,1,0:T(8,128)(2,1)S(1)} collective-permute-done((bf16[2,16,1024]{2,1,0:T(8,128)(2,1)S(1)}, bf16[2,16,1024]{2,1,0:T(8,128)(2,1)S(1)}, u32[]{:S(2)}, u32[]{:S(2)}) %collective-permute-start.9) | collective-permute-done | bytes 65568 | tf_op jit(solution)/shard_map/ppermute | solution.py:36
  74.6 1.4 %collective-permute-start.10 = (bf16[4,16,1024]{2,1,0:T(8,128)(2,1)S(1)}, bf16[4,16,1024]{2,1,0:T(8,128)(2,1)S(1)}, u32[]{:S(2)}, u32[]{:S(2)}) collective-permute-start(bf16[4,16,1024]{2,1,0:T(8,128)(2,1)S(1)} %bitcast.298), channel_id=1, source_target_pairs={{0,2},{1,5},{2,0},{3,7},{4,6},{5,1},{6,4},{7,3},{8,10},{9,13},{10,... | collective-permute-start | bytes 393224 | tf_op jit(solution)/shard_map/ppermute | solution.py:36
  76.1 2.2 %collective-permute-done.26 = bf16[4,16,1024]{2,1,0:T(8,128)(2,1)S(1)} collective-permute-done((bf16[4,16,1024]{2,1,0:T(8,128)(2,1)S(1)}, bf16[4,16,1024]{2,1,0:T(8,128)(2,1)S(1)}, u32[]{:S(2)}, u32[]{:S(2)}) %collective-permute-start.26) | collective-permute-done | bytes 131104 | tf_op jit(solution)/shard_map/ppermute | solution.py:36
  78.4 1.3 %collective-permute-done.10 = bf16[4,16,1024]{2,1,0:T(8,128)(2,1)S(1)} collective-permute-done((bf16[4,16,1024]{2,1,0:T(8,128)(2,1)S(1)}, bf16[4,16,1024]{2,1,0:T(8,128)(2,1)S(1)}, u32[]{:S(2)}, u32[]{:S(2)}) %collective-permute-start.10) | collective-permute-done | bytes 131104 | tf_op jit(solution)/shard_map/ppermute | solution.py:36
  80.0 0.8 pad_maximum_fusion.3
  80.8 7.2 %shard_map.58 = f32[256,1024]{1,0:T(8,128)} custom-call(bf16[4,256,256]{2,1,0:T(8,128)(2,1)} %occ_ref.7, bf16[256,1024]{1,0:T(8,128)(2,1)} %bitcast.266, bf16[4,1024,1024]{2,1,0:T(8,128)(2,1)} %vir_ref.7), custom_call_target="tpu_custom_call" | custom-call | tf_op jit(solution)/shard_map/pallas_call | solution.py:107
  88.1 0.9 pad_maximum_fusion.1
  88.9 7.2 %shard_map.56 = f32[256,1024]{1,0:T(8,128)} custom-call(bf16[4,256,256]{2,1,0:T(8,128)(2,1)} %occ_ref.7, bf16[256,1024]{1,0:T(8,128)(2,1)} %bitcast.267, bf16[4,1024,1024]{2,1,0:T(8,128)(2,1)} %vir_ref.7), custom_call_target="tpu_custom_call" | custom-call | tf_op jit(solution)/shard_map/pallas_call | solution.py:107
  96.1 1.4 %constant_dynamic-slice_fusion.3 = (f32[2,2,2,1,16,1024]{5,4,3,2,1,0:T(8,128)S(1)}, f32[2,2,2,1,16,1024]{5,4,3,2,1,0:T(8,128)S(1)}, f32[2,2,2,1,16,1024]{5,4,3,2,1,0:T(8,128)S(1)}, f32[2,2,2,1,16,1024]{5,4,3,2,1,0:T(8,128)S(1)}) fusion(f32[2,2,2,2,16,1024]{5,4,3,2,1,0:T(8,128)S(1)} %bitcast.260, s32[]{:T(128)S(6)} %select_n.336, s32[]{:T(128)S(6)} %select_n.337, ...), kind=kLoop, calls=%fused_computation.116 | loop fusion | bytes 4194312 | tf_op jit(solution)/shard_map/jit(dynamic_index_in_dim)/dynamic_slice | solution.py:69
  97.6 0.5 collective-permute-start.12
  98.1 0.1 collective-permute-start.28
  98.2 1.4 %collective-permute-done.12 = f32[2,2,2,16,1024]{4,3,2,0,1:T(8,128)S(1)} collective-permute-done((f32[2,2,2,16,1024]{4,3,2,0,1:T(8,128)S(1)}, f32[2,2,2,16,1024]{4,3,2,0,1:T(8,128)S(1)}, u32[]{:S(2)}, u32[]{:S(2)}) %collective-permute-start.12) | collective-permute-done | bytes 524320 | tf_op jit(solution)/shard_map/ppermute | solution.py:82
  99.8 1.4 %collective-permute-start.13 = (f32[2,2,16,1024]{3,2,1,0:T(8,128)S(1)}, f32[2,2,16,1024]{3,2,1,0:T(8,128)S(1)}, u32[]{:S(2)}, u32[]{:S(2)}) collective-permute-start(f32[2,2,16,1024]{3,2,1,0:T(8,128)S(1)} %bitcast_select_fusion.4), channel_id=1, source_target_pairs={{0,2},{1,5},{2,0},{3,7},{4,6},{5,1},{6,4},{7,3},{8,10},{9,13},{10,... | collective-permute-start | bytes 786440 | tf_op jit(solution)/shard_map/ppermute | solution.py:82
  101.4 0.7 collective-permute-start.29
  102.1 4.1 %collective-permute-done.13 = f32[2,2,16,1024]{3,2,1,0:T(8,128)S(1)} collective-permute-done((f32[2,2,16,1024]{3,2,1,0:T(8,128)S(1)}, f32[2,2,16,1024]{3,2,1,0:T(8,128)S(1)}, u32[]{:S(2)}, u32[]{:S(2)}) %collective-permute-start.13) | collective-permute-done | bytes 262176 | tf_op jit(solution)/shard_map/ppermute | solution.py:82
  106.3 1.3 %collective-permute-start.14 = (f32[2,16,1024]{2,1,0:T(8,128)S(1)}, f32[2,16,1024]{2,1,0:T(8,128)S(1)}, u32[]{:S(2)}, u32[]{:S(2)}) collective-permute-start(f32[2,16,1024]{2,1,0:T(8,128)S(1)} %dynamic-slice_bitcast_fusion.2), channel_id=1, source_target_pairs={{0,4},{1,3},{2,6},{3,1},{4,0},{5,7},{6,2},{7,5},{8,12},{9,11},{10,... | collective-permute-start | bytes 393224 | tf_op jit(solution)/shard_map/ppermute | solution.py:82
  107.6 1.9 %collective-permute-done.29 = f32[2,2,16,1024]{3,2,1,0:T(8,128)S(1)} collective-permute-done((f32[2,2,16,1024]{3,2,1,0:T(8,128)S(1)}, f32[2,2,16,1024]{3,2,1,0:T(8,128)S(1)}, u32[]{:S(2)}, u32[]{:S(2)}) %collective-permute-start.29) | collective-permute-done | bytes 262176 | tf_op jit(solution)/shard_map/ppermute | solution.py:82
  109.6 1.3 %collective-permute-start.30 = (f32[2,16,1024]{2,1,0:T(8,128)S(1)}, f32[2,16,1024]{2,1,0:T(8,128)S(1)}, u32[]{:S(2)}, u32[]{:S(2)}) collective-permute-start(f32[2,16,1024]{2,1,0:T(8,128)S(1)} %dynamic-slice_bitcast_fusion), channel_id=1, source_target_pairs={{0,4},{1,3},{2,6},{3,1},{4,0},{5,7},{6,2},{7,5},{8,12},{9,11},{10,... | collective-permute-start | bytes 393224 | tf_op jit(solution)/shard_map/ppermute | solution.py:82
  110.9 0.4 collective-permute-done.14
  111.4 2.2 %collective-permute-start.15 = (f32[16,1024]{1,0:T(8,128)S(1)}, f32[16,1024]{1,0:T(8,128)S(1)}, u32[]{:S(2)}, u32[]{:S(2)}) collective-permute-start(f32[16,1024]{1,0:T(8,128)S(1)} %dynamic-slice_bitcast_fusion.6), channel_id=1, source_target_pairs={{0,8},{1,9},{2,10},{3,11},{4,12},{5,13},{6,14},{7,15},{8,0},{9,1},... | collective-permute-start | bytes 196616 | tf_op jit(solution)/shard_map/ppermute | solution.py:82
  113.6 1.7 %collective-permute-done.30 = f32[2,16,1024]{2,1,0:T(8,128)S(1)} collective-permute-done((f32[2,16,1024]{2,1,0:T(8,128)S(1)}, f32[2,16,1024]{2,1,0:T(8,128)S(1)}, u32[]{:S(2)}, u32[]{:S(2)}) %collective-permute-start.30) | collective-permute-done | bytes 131104 | tf_op jit(solution)/shard_map/ppermute | solution.py:82
  115.4 1.9 %collective-permute-start.31 = (f32[16,1024]{1,0:T(8,128)S(1)}, f32[16,1024]{1,0:T(8,128)S(1)}, u32[]{:S(2)}, u32[]{:S(2)}) collective-permute-start(f32[16,1024]{1,0:T(8,128)S(1)} %dynamic-slice_bitcast_fusion.4), channel_id=1, source_target_pairs={{0,8},{1,9},{2,10},{3,11},{4,12},{5,13},{6,14},{7,15},{8,0},{9,1},... | collective-permute-start | bytes 196616 | tf_op jit(solution)/shard_map/ppermute | solution.py:82
  117.2 1.5 %collective-permute-done.15 = f32[16,1024]{1,0:T(8,128)S(1)} collective-permute-done((f32[16,1024]{1,0:T(8,128)S(1)}, f32[16,1024]{1,0:T(8,128)S(1)}, u32[]{:S(2)}, u32[]{:S(2)}) %collective-permute-start.15) | collective-permute-done | bytes 65568 | tf_op jit(solution)/shard_map/ppermute | solution.py:82
  118.7 1.9 %collective-permute-done.31 = f32[16,1024]{1,0:T(8,128)S(1)} collective-permute-done((f32[16,1024]{1,0:T(8,128)S(1)}, f32[16,1024]{1,0:T(8,128)S(1)}, u32[]{:S(2)}, u32[]{:S(2)}) %collective-permute-start.31) | collective-permute-done | bytes 65568 | tf_op jit(solution)/shard_map/ppermute | solution.py:82
  120.7 0.8 copy.86
  (85 shorter events, 2.8 us)
Async XLA Ops:
  2.6 6.3 %collective-permute-start = (bf16[1,16,1024]{2,1,0:T(8,128)(2,1)S(1)}, bf16[1,16,1024]{2,1,0:T(8,128)(2,1)S(1)}, u32[]{:S(2)}, u32[]{:S(2)}) collective-permute-start(bf16[1,16,1024]{2,1,0:T(8,128)(2,1)S(1)} %get-tuple-element.63), channel_id=1, source_target_pairs={{0,8},{1,9},{2,10},{3,11},{4,12},{5,13},{6,14},{7,15},{8,0},{9,1},... | collective-permute-start | bytes 98312 | tf_op jit(solution)/shard_map/ppermute | solution.py:36
  6.7 4.8 %collective-permute-start.16 = (bf16[1,16,1024]{2,1,0:T(8,128)(2,1)S(1)}, bf16[1,16,1024]{2,1,0:T(8,128)(2,1)S(1)}, u32[]{:S(2)}, u32[]{:S(2)}) collective-permute-start(bf16[1,16,1024]{2,1,0:T(8,128)(2,1)S(1)} %get-tuple-element.64), channel_id=1, source_target_pairs={{0,8},{1,9},{2,10},{3,11},{4,12},{5,13},{6,14},{7,15},{8,0},{9,1},... | collective-permute-start | bytes 98312 | tf_op jit(solution)/shard_map/ppermute | solution.py:36
  9.0 4.3 %collective-permute-start.1 = (bf16[2,16,1024]{2,1,0:T(8,128)(2,1)S(1)}, bf16[2,16,1024]{2,1,0:T(8,128)(2,1)S(1)}, u32[]{:S(2)}, u32[]{:S(2)}) collective-permute-start(bf16[2,16,1024]{2,1,0:T(8,128)(2,1)S(1)} %pad_maximum_fusion.9), channel_id=1, source_target_pairs={{0,4},{1,3},{2,6},{3,1},{4,0},{5,7},{6,2},{7,5},{8,12},{9,11},{10,... | collective-permute-start | bytes 196616 | tf_op jit(solution)/shard_map/ppermute | solution.py:36
  11.6 4.8 %collective-permute-start.17 = (bf16[2,16,1024]{2,1,0:T(8,128)(2,1)S(1)}, bf16[2,16,1024]{2,1,0:T(8,128)(2,1)S(1)}, u32[]{:S(2)}, u32[]{:S(2)}) collective-permute-start(bf16[2,16,1024]{2,1,0:T(8,128)(2,1)S(1)} %pad_maximum_fusion.11), channel_id=1, source_target_pairs={{0,4},{1,3},{2,6},{3,1},{4,0},{5,7},{6,2},{7,5},{8,12},{9,11},{10,... | collective-permute-start | bytes 196616 | tf_op jit(solution)/shard_map/ppermute | solution.py:36
  13.4 5.0 %collective-permute-start.2 = (bf16[4,16,1024]{2,1,0:T(8,128)(2,1)S(1)}, bf16[4,16,1024]{2,1,0:T(8,128)(2,1)S(1)}, u32[]{:S(2)}, u32[]{:S(2)}) collective-permute-start(bf16[4,16,1024]{2,1,0:T(8,128)(2,1)S(1)} %bitcast.296), channel_id=1, source_target_pairs={{0,2},{1,5},{2,0},{3,7},{4,6},{5,1},{6,4},{7,3},{8,10},{9,13},{10,... | collective-permute-start | bytes 393224 | tf_op jit(solution)/shard_map/ppermute | solution.py:36
  16.4 5.0 %collective-permute-start.18 = (bf16[4,16,1024]{2,1,0:T(8,128)(2,1)S(1)}, bf16[4,16,1024]{2,1,0:T(8,128)(2,1)S(1)}, u32[]{:S(2)}, u32[]{:S(2)}) collective-permute-start(bf16[4,16,1024]{2,1,0:T(8,128)(2,1)S(1)} %bitcast.299), channel_id=1, source_target_pairs={{0,2},{1,5},{2,0},{3,7},{4,6},{5,1},{6,4},{7,3},{8,10},{9,13},{10,... | collective-permute-start | bytes 393224 | tf_op jit(solution)/shard_map/ppermute | solution.py:36
  18.5 3.1 %collective-permute-start.3 = (bf16[8,16,1024]{2,1,0:T(8,128)(2,1)S(1)}, bf16[8,16,1024]{2,1,0:T(8,128)(2,1)S(1)}, u32[]{:S(2)}, u32[]{:S(2)}) collective-permute-start(bf16[8,16,1024]{2,1,0:T(8,128)(2,1)S(1)} %bitcast.286), channel_id=1, source_target_pairs={{0,1},{1,0},{2,3},{3,2},{4,5},{5,4},{6,7},{7,6},{8,9},{9,8},{10,11... | collective-permute-start | bytes 786440 | tf_op jit(solution)/shard_map/ppermute | solution.py:36
  21.5 10.1 %collective-permute-start.19 = (bf16[8,16,1024]{2,1,0:T(8,128)(2,1)S(1)}, bf16[8,16,1024]{2,1,0:T(8,128)(2,1)S(1)}, u32[]{:S(2)}, u32[]{:S(2)}) collective-permute-start(bf16[8,16,1024]{2,1,0:T(8,128)(2,1)S(1)} %bitcast.284), channel_id=1, source_target_pairs={{0,1},{1,0},{2,3},{3,2},{4,5},{5,4},{6,7},{7,6},{8,9},{9,8},{10,11... | collective-permute-start | bytes 786440 | tf_op jit(solution)/shard_map/ppermute | solution.py:36
  31.1 10.1 %collective-permute-start.4 = (f32[2,2,2,16,1024]{4,3,2,0,1:T(8,128)S(1)}, f32[2,2,2,16,1024]{4,3,2,0,1:T(8,128)S(1)}, u32[]{:S(2)}, u32[]{:S(2)}) collective-permute-start(f32[2,2,2,16,1024]{4,3,2,0,1:T(8,128)S(1)} %bitcast.300), channel_id=1, source_target_pairs={{0,1},{1,0},{2,3},{3,2},{4,5},{5,4},{6,7},{7,6},{8,9},{9,8},{10,11... | collective-permute-start | bytes 1572872 | tf_op jit(solution)/shard_map/ppermute | solution.py:82
  39.7 23.0 %copy-start.1 = (f32[1024]{0:T(1024)S(1)}, f32[1024]{0:T(1024)}, u32[]{:S(2)}) copy-start(f32[1024]{0:T(1024)} %param.7) | copy-start | bytes 12292
  41.1 2.0 %collective-permute-start.20 = (f32[2,2,2,16,1024]{4,3,2,0,1:T(8,128)S(1)}, f32[2,2,2,16,1024]{4,3,2,0,1:T(8,128)S(1)}, u32[]{:S(2)}, u32[]{:S(2)}) collective-permute-start(f32[2,2,2,16,1024]{4,3,2,0,1:T(8,128)S(1)} %bitcast.301), channel_id=1, source_target_pairs={{0,1},{1,0},{2,3},{3,2},{4,5},{5,4},{6,7},{7,6},{8,9},{9,8},{10,11... | collective-permute-start | bytes 1572872 | tf_op jit(solution)/shard_map/ppermute | solution.py:82
  41.4 6.4 %collective-permute-start.5 = (f32[2,2,16,1024]{3,2,1,0:T(8,128)S(1)}, f32[2,2,16,1024]{3,2,1,0:T(8,128)S(1)}, u32[]{:S(2)}, u32[]{:S(2)}) collective-permute-start(f32[2,2,16,1024]{3,2,1,0:T(8,128)S(1)} %bitcast_select_fusion.6), channel_id=1, source_target_pairs={{0,2},{1,5},{2,0},{3,7},{4,6},{5,1},{6,4},{7,3},{8,10},{9,13},{10,... | collective-permute-start | bytes 786440 | tf_op jit(solution)/shard_map/ppermute | solution.py:82
  43.2 7.8 %collective-permute-start.21 = (f32[2,2,16,1024]{3,2,1,0:T(8,128)S(1)}, f32[2,2,16,1024]{3,2,1,0:T(8,128)S(1)}, u32[]{:S(2)}, u32[]{:S(2)}) collective-permute-start(f32[2,2,16,1024]{3,2,1,0:T(8,128)S(1)} %bitcast_select_fusion.2), channel_id=1, source_target_pairs={{0,2},{1,5},{2,0},{3,7},{4,6},{5,1},{6,4},{7,3},{8,10},{9,13},{10,... | collective-permute-start | bytes 786440 | tf_op jit(solution)/shard_map/ppermute | solution.py:82
  47.9 5.0 %collective-permute-start.6 = (f32[2,16,1024]{2,1,0:T(8,128)S(1)}, f32[2,16,1024]{2,1,0:T(8,128)S(1)}, u32[]{:S(2)}, u32[]{:S(2)}) collective-permute-start(f32[2,16,1024]{2,1,0:T(8,128)S(1)} %dynamic-slice_bitcast_fusion.3), channel_id=1, source_target_pairs={{0,4},{1,3},{2,6},{3,1},{4,0},{5,7},{6,2},{7,5},{8,12},{9,11},{10,... | collective-permute-start | bytes 393224 | tf_op jit(solution)/shard_map/ppermute | solution.py:82
  51.1 5.7 %collective-permute-start.22 = (f32[2,16,1024]{2,1,0:T(8,128)S(1)}, f32[2,16,1024]{2,1,0:T(8,128)S(1)}, u32[]{:S(2)}, u32[]{:S(2)}) collective-permute-start(f32[2,16,1024]{2,1,0:T(8,128)S(1)} %dynamic-slice_bitcast_fusion.1), channel_id=1, source_target_pairs={{0,4},{1,3},{2,6},{3,1},{4,0},{5,7},{6,2},{7,5},{8,12},{9,11},{10,... | collective-permute-start | bytes 393224 | tf_op jit(solution)/shard_map/ppermute | solution.py:82
  53.0 6.3 %collective-permute-start.7 = (f32[16,1024]{1,0:T(8,128)S(1)}, f32[16,1024]{1,0:T(8,128)S(1)}, u32[]{:S(2)}, u32[]{:S(2)}) collective-permute-start(f32[16,1024]{1,0:T(8,128)S(1)} %dynamic-slice_bitcast_fusion.7), channel_id=1, source_target_pairs={{0,8},{1,9},{2,10},{3,11},{4,12},{5,13},{6,14},{7,15},{8,0},{9,1},... | collective-permute-start | bytes 196616 | tf_op jit(solution)/shard_map/ppermute | solution.py:82
  56.8 5.9 %collective-permute-start.23 = (f32[16,1024]{1,0:T(8,128)S(1)}, f32[16,1024]{1,0:T(8,128)S(1)}, u32[]{:S(2)}, u32[]{:S(2)}) collective-permute-start(f32[16,1024]{1,0:T(8,128)S(1)} %dynamic-slice_bitcast_fusion.5), channel_id=1, source_target_pairs={{0,8},{1,9},{2,10},{3,11},{4,12},{5,13},{6,14},{7,15},{8,0},{9,1},... | collective-permute-start | bytes 196616 | tf_op jit(solution)/shard_map/ppermute | solution.py:82
  62.9 5.2 %collective-permute-start.24 = (bf16[1,16,1024]{2,1,0:T(8,128)(2,1)S(1)}, bf16[1,16,1024]{2,1,0:T(8,128)(2,1)S(1)}, u32[]{:S(2)}, u32[]{:S(2)}) collective-permute-start(bf16[1,16,1024]{2,1,0:T(8,128)(2,1)S(1)} %get-tuple-element.61), channel_id=1, source_target_pairs={{0,8},{1,9},{2,10},{3,11},{4,12},{5,13},{6,14},{7,15},{8,0},{9,1},... | collective-permute-start | bytes 98312 | tf_op jit(solution)/shard_map/ppermute | solution.py:36
  64.7 4.8 %collective-permute-start.8 = (bf16[1,16,1024]{2,1,0:T(8,128)(2,1)S(1)}, bf16[1,16,1024]{2,1,0:T(8,128)(2,1)S(1)}, u32[]{:S(2)}, u32[]{:S(2)}) collective-permute-start(bf16[1,16,1024]{2,1,0:T(8,128)(2,1)S(1)} %get-tuple-element.5), channel_id=1, source_target_pairs={{0,8},{1,9},{2,10},{3,11},{4,12},{5,13},{6,14},{7,15},{8,0},{9,1},... | collective-permute-start | bytes 98312 | tf_op jit(solution)/shard_map/ppermute | solution.py:36
  68.1 5.0 %collective-permute-start.25 = (bf16[2,16,1024]{2,1,0:T(8,128)(2,1)S(1)}, bf16[2,16,1024]{2,1,0:T(8,128)(2,1)S(1)}, u32[]{:S(2)}, u32[]{:S(2)}) collective-permute-start(bf16[2,16,1024]{2,1,0:T(8,128)(2,1)S(1)} %pad_maximum_fusion.12), channel_id=1, source_target_pairs={{0,4},{1,3},{2,6},{3,1},{4,0},{5,7},{6,2},{7,5},{8,12},{9,11},{10,... | collective-permute-start | bytes 196616 | tf_op jit(solution)/shard_map/ppermute | solution.py:36
  69.5 5.0 %collective-permute-start.9 = (bf16[2,16,1024]{2,1,0:T(8,128)(2,1)S(1)}, bf16[2,16,1024]{2,1,0:T(8,128)(2,1)S(1)}, u32[]{:S(2)}, u32[]{:S(2)}) collective-permute-start(bf16[2,16,1024]{2,1,0:T(8,128)(2,1)S(1)} %pad_maximum_fusion.10), channel_id=1, source_target_pairs={{0,4},{1,3},{2,6},{3,1},{4,0},{5,7},{6,2},{7,5},{8,12},{9,11},{10,... | collective-permute-start | bytes 196616 | tf_op jit(solution)/shard_map/ppermute | solution.py:36
  73.2 5.0 %collective-permute-start.26 = (bf16[4,16,1024]{2,1,0:T(8,128)(2,1)S(1)}, bf16[4,16,1024]{2,1,0:T(8,128)(2,1)S(1)}, u32[]{:S(2)}, u32[]{:S(2)}) collective-permute-start(bf16[4,16,1024]{2,1,0:T(8,128)(2,1)S(1)} %bitcast.297), channel_id=1, source_target_pairs={{0,2},{1,5},{2,0},{3,7},{4,6},{5,1},{6,4},{7,3},{8,10},{9,13},{10,... | collective-permute-start | bytes 393224 | tf_op jit(solution)/shard_map/ppermute | solution.py:36
  74.6 5.0 %collective-permute-start.10 = (bf16[4,16,1024]{2,1,0:T(8,128)(2,1)S(1)}, bf16[4,16,1024]{2,1,0:T(8,128)(2,1)S(1)}, u32[]{:S(2)}, u32[]{:S(2)}) collective-permute-start(bf16[4,16,1024]{2,1,0:T(8,128)(2,1)S(1)} %bitcast.298), channel_id=1, source_target_pairs={{0,2},{1,5},{2,0},{3,7},{4,6},{5,1},{6,4},{7,3},{8,10},{9,13},{10,... | collective-permute-start | bytes 393224 | tf_op jit(solution)/shard_map/ppermute | solution.py:36
  78.3 1.6 %collective-permute-start.27 = (bf16[8,16,1024]{2,1,0:T(8,128)(2,1)S(1)}, bf16[8,16,1024]{2,1,0:T(8,128)(2,1)S(1)}, u32[]{:S(2)}, u32[]{:S(2)}) collective-permute-start(bf16[8,16,1024]{2,1,0:T(8,128)(2,1)S(1)} %bitcast.285), channel_id=1, source_target_pairs={{0,1},{1,0},{2,3},{3,2},{4,5},{5,4},{6,7},{7,6},{8,9},{9,8},{10,11... | collective-permute-start | bytes 786440 | tf_op jit(solution)/shard_map/ppermute | solution.py:36
  79.8 8.3 %collective-permute-start.11 = (bf16[8,16,1024]{2,1,0:T(8,128)(2,1)S(1)}, bf16[8,16,1024]{2,1,0:T(8,128)(2,1)S(1)}, u32[]{:S(2)}, u32[]{:S(2)}) collective-permute-start(bf16[8,16,1024]{2,1,0:T(8,128)(2,1)S(1)} %bitcast.287), channel_id=1, source_target_pairs={{0,1},{1,0},{2,3},{3,2},{4,5},{5,4},{6,7},{7,6},{8,9},{9,8},{10,11... | collective-permute-start | bytes 786440 | tf_op jit(solution)/shard_map/ppermute | solution.py:36
  88.0 8.1 %copy-start = (f32[256,1024]{1,0:T(8,128)S(1)}, f32[256,1024]{1,0:T(8,128)}, u32[]{:S(2)}) copy-start(f32[256,1024]{1,0:T(8,128)} %shard_map.58) | copy-start | bytes 3145732
  97.6 2.0 %collective-permute-start.12 = (f32[2,2,2,16,1024]{4,3,2,0,1:T(8,128)S(1)}, f32[2,2,2,16,1024]{4,3,2,0,1:T(8,128)S(1)}, u32[]{:S(2)}, u32[]{:S(2)}) collective-permute-start(f32[2,2,2,16,1024]{4,3,2,0,1:T(8,128)S(1)} %bitcast.303), channel_id=1, source_target_pairs={{0,1},{1,0},{2,3},{3,2},{4,5},{5,4},{6,7},{7,6},{8,9},{9,8},{10,11... | collective-permute-start | bytes 1572872 | tf_op jit(solution)/shard_map/ppermute | solution.py:82
  98.1 3.1 %collective-permute-start.28 = (f32[2,2,2,16,1024]{4,3,2,0,1:T(8,128)S(1)}, f32[2,2,2,16,1024]{4,3,2,0,1:T(8,128)S(1)}, u32[]{:S(2)}, u32[]{:S(2)}) collective-permute-start(f32[2,2,2,16,1024]{4,3,2,0,1:T(8,128)S(1)} %bitcast.302), channel_id=1, source_target_pairs={{0,1},{1,0},{2,3},{3,2},{4,5},{5,4},{6,7},{7,6},{8,9},{9,8},{10,11... | collective-permute-start | bytes 1572872 | tf_op jit(solution)/shard_map/ppermute | solution.py:82
  99.8 6.4 %collective-permute-start.13 = (f32[2,2,16,1024]{3,2,1,0:T(8,128)S(1)}, f32[2,2,16,1024]{3,2,1,0:T(8,128)S(1)}, u32[]{:S(2)}, u32[]{:S(2)}) collective-permute-start(f32[2,2,16,1024]{3,2,1,0:T(8,128)S(1)} %bitcast_select_fusion.4), channel_id=1, source_target_pairs={{0,2},{1,5},{2,0},{3,7},{4,6},{5,1},{6,4},{7,3},{8,10},{9,13},{10,... | collective-permute-start | bytes 786440 | tf_op jit(solution)/shard_map/ppermute | solution.py:82
  101.4 8.1 %collective-permute-start.29 = (f32[2,2,16,1024]{3,2,1,0:T(8,128)S(1)}, f32[2,2,16,1024]{3,2,1,0:T(8,128)S(1)}, u32[]{:S(2)}, u32[]{:S(2)}) collective-permute-start(f32[2,2,16,1024]{3,2,1,0:T(8,128)S(1)} %bitcast_select_fusion), channel_id=1, source_target_pairs={{0,2},{1,5},{2,0},{3,7},{4,6},{5,1},{6,4},{7,3},{8,10},{9,13},{10,... | collective-permute-start | bytes 786440 | tf_op jit(solution)/shard_map/ppermute | solution.py:82
  106.3 5.0 %collective-permute-start.14 = (f32[2,16,1024]{2,1,0:T(8,128)S(1)}, f32[2,16,1024]{2,1,0:T(8,128)S(1)}, u32[]{:S(2)}, u32[]{:S(2)}) collective-permute-start(f32[2,16,1024]{2,1,0:T(8,128)S(1)} %dynamic-slice_bitcast_fusion.2), channel_id=1, source_target_pairs={{0,4},{1,3},{2,6},{3,1},{4,0},{5,7},{6,2},{7,5},{8,12},{9,11},{10,... | collective-permute-start | bytes 393224 | tf_op jit(solution)/shard_map/ppermute | solution.py:82
  109.6 5.7 %collective-permute-start.30 = (f32[2,16,1024]{2,1,0:T(8,128)S(1)}, f32[2,16,1024]{2,1,0:T(8,128)S(1)}, u32[]{:S(2)}, u32[]{:S(2)}) collective-permute-start(f32[2,16,1024]{2,1,0:T(8,128)S(1)} %dynamic-slice_bitcast_fusion), channel_id=1, source_target_pairs={{0,4},{1,3},{2,6},{3,1},{4,0},{5,7},{6,2},{7,5},{8,12},{9,11},{10,... | collective-permute-start | bytes 393224 | tf_op jit(solution)/shard_map/ppermute | solution.py:82
  111.4 7.3 %collective-permute-start.15 = (f32[16,1024]{1,0:T(8,128)S(1)}, f32[16,1024]{1,0:T(8,128)S(1)}, u32[]{:S(2)}, u32[]{:S(2)}) collective-permute-start(f32[16,1024]{1,0:T(8,128)S(1)} %dynamic-slice_bitcast_fusion.6), channel_id=1, source_target_pairs={{0,8},{1,9},{2,10},{3,11},{4,12},{5,13},{6,14},{7,15},{8,0},{9,1},... | collective-permute-start | bytes 196616 | tf_op jit(solution)/shard_map/ppermute | solution.py:82
  115.4 5.2 %collective-permute-start.31 = (f32[16,1024]{1,0:T(8,128)S(1)}, f32[16,1024]{1,0:T(8,128)S(1)}, u32[]{:S(2)}, u32[]{:S(2)}) collective-permute-start(f32[16,1024]{1,0:T(8,128)S(1)} %dynamic-slice_bitcast_fusion.4), channel_id=1, source_target_pairs={{0,8},{1,9},{2,10},{3,11},{4,12},{5,13},{6,14},{7,15},{8,0},{9,1},... | collective-permute-start | bytes 196616 | tf_op jit(solution)/shard_map/ppermute | solution.py:82

commit v5 on v4

--- a/solution.py
+++ b/solution.py
@@ -31,7 +31,7 @@
     order0, order1 = bit_orders(m, True)
     acc = x[None]
     have0, have1 = [], []
-    for b0, b1 in zip(order0, order1):
+    for b0, b1 in zip(order0[:-1], order1[:-1]):
         bit = jnp.where(odd, (me >> b1) & 1, (me >> b0) & 1)
         theirs = lax.ppermute(acc, "aux", partners(n, b0, b1))
         lo = jnp.where(bit == 0, acc, theirs)
@@ -49,19 +49,22 @@
         have0 = sorted(have0 + [b0], reverse=True)
         have1 = sorted(have1 + [b1], reverse=True)
         acc = acc.reshape((-1,) + x.shape)
-    return acc.reshape((n * x.shape[0],) + x.shape[1:])
+    theirs = lax.ppermute(acc, "aux", partners(n, 0, 0))
+    return jnp.concatenate([acc, theirs], axis=0).reshape((n * x.shape[0],) + x.shape[1:])
 
 
 def scatter_sum(part, n):
     m = n.bit_length() - 1
     me = lax.axis_index("aux")
     odd = (me & 1) == 1
+    half = part.shape[0] // 2
     rows = part.shape[0] // n
     order0, order1 = bit_orders(m, False)
-    acc = part.reshape((2,) * m + (rows,) + part.shape[1:])
-    axes0 = list(range(m - 1, -1, -1))
+    shape = (2,) * (m - 1) + (rows,) + part.shape[1:]
+    acc = part[:half].reshape(shape) + lax.ppermute(part[half:].reshape(shape), "aux", partners(n, 0, 0))
+    axes0 = list(range(m - 1, 0, -1))
     axes1 = list(axes0)
-    for b0, b1 in zip(order0, order1):
+    for b0, b1 in zip(order0[1:], order1[1:]):
         at0, at1 = axes0.index(b0), axes1.index(b1)
         bit0, bit1 = (me >> b0) & 1, (me >> b1) & 1
         if at0 == at1:
@@ -83,6 +86,19 @@
         axes0.pop(at0)
         axes1.pop(at1)
     return acc
+
+
+def order_occ_ints(occ_ints, n, core):
+    local_aux, nocc, _ = occ_ints.shape
+    rows = nocc // n
+    o = occ_ints.reshape(local_aux, n // 2, 2, rows, nocc)
+    even, odd = o[:, :, 0], o[:, :, 1]
+    mine = core == 0
+    o = jnp.stack([jnp.where(mine, even, odd), jnp.where(mine, odd, even)], axis=1)
+    o = o.reshape(local_aux, nocc, n // 2, 2, rows)
+    even, odd = o[:, :, :, 0], o[:, :, :, 1]
+    o = jnp.stack([jnp.where(mine, even, odd), jnp.where(mine, odd, even)], axis=2)
+    return o.reshape(local_aux, nocc, nocc)
 
 
 def exchange_kernel(states, occ_ref, r_ref, vir_ref, out_ref):
@@ -128,6 +144,7 @@
     position = lax.axis_index("aux")
     my_occ = lax.dynamic_slice_in_dim(occ_energy, position * own_rows, own_rows, 0)
     denom = vir_energy[None, None, :] - my_occ[:, None, None]
+    ordered_occ = order_occ_ints(occ_ints, n, position & 1)
     finals = []
     for state in range(states):
         own_rhs = rhs[:, state, :]
@@ -136,7 +153,7 @@
         for step in range(ITERS):
             rounded = resp.astype(jnp.bfloat16)
             flat = gather_rows(rounded, n)
-            part = exchange_part(occ_ints, flat, vir_ints, 1)
+            part = exchange_part(ordered_occ, flat, vir_ints, 1)
             exchange = scatter_sum(part, n)
             resp = 0.4 * resp + 0.6 * (own_rhs - exchange) / own_denom
         finals.append(resp)

time: 122 us -> 133 us (1.090)
  local copies, waits for them, and re-layouts: 7.09 us -> 20 us
  waiting for transfers between devices: 41.2 us -> 37.6 us
  other arithmetic: 5.71 us -> 7.88 us
    reshape x0 -> x2, local copies, waits for them, and re-layouts: none -> 6.51 us  [the longest x1 5.48 us: order_occ_ints(): o = o.reshape(local_aux, nocc, n // 2, 2, rows)]
    slice x0 -> x4, local copies, waits for them, and re-layouts: none -> 5.92 us  [scatter_sum(): part[half:].reshape(shape)]
    another operation x0 -> x2, local copies, waits for them, and re-layouts: none -> 4.7 us  [the longest x1 4.67 us: order_occ_ints(): jnp.stack([jnp.where(mine, even, odd), jnp.where(mine, odd, even)], axis=1)]
    dynamic_slice x11 -> x0, local copies, waits for them, and re-layouts: 4.32 us -> none  [the longest x3 3.98 us: scatter_sum(): keep = lax.dynamic_index_in_dim(acc, bit, axis=at0, keepdims=False)]
    another operation x16 -> x12, other arithmetic: 3.52 us -> 0.15 us  [gather_rows(): new0 = jnp.stack([lo, hi], axis=at0)]
    concatenate x0 -> x4, other arithmetic: none -> 3.37 us  [gather_rows(): jnp.concatenate([acc, theirs], axis=0)]
    ppermute x16 -> x12, waiting for transfers between devices: 17.5 us -> 14.2 us  [gather_rows(): theirs = lax.ppermute(acc, 'aux', partners(n, b0, b1))]
    select_n x0 -> x4, other arithmetic: none -> 2.2 us  [the longest x2 1.1 us: order_occ_ints(): jnp.where(mine, even, odd)]
  transfers between devices with their start and end apart: 32 -> 32, of which waited for: 26 -> 25; matrix products, arithmetic and copies ran while one was open for 6% -> 18% of each run, Pallas kernels for 18% -> 22%
where the time goes in v5:
time: 133 us
  starting transfers between devices  38.2 us (29%)
  waiting for transfers between devices  37.6 us (28%)
  Pallas kernels  28.8 us (22%)
  local copies, waits for them, and re-layouts  20 us (15%)
  other arithmetic  7.88 us (6%)
    pallas_call x4, Pallas kernels, exchange_part(): pl.pallas_call(functools.partial(exchange_kernel, states), grid=(local_au...  28.8 us
    ppermute x12, waiting for transfers between devices, scatter_sum(): acc = keep + lax.ppermute(send, 'aux', partners(n, b0, b1))  22.9 us
    ppermute x12, starting transfers between devices, scatter_sum(): acc = keep + lax.ppermute(send, 'aux', partners(n, b0, b1))  18.6 us
    ppermute x12, starting transfers between devices, gather_rows(): theirs = lax.ppermute(acc, 'aux', partners(n, b0, b1))  18.1 us
    ppermute x12, waiting for transfers between devices, gather_rows(): theirs = lax.ppermute(acc, 'aux', partners(n, b0, b1))  14.2 us
    slice x4, local copies, waits for them, and re-layouts, scatter_sum(): part[half:].reshape(shape)  5.92 us
    reshape x1, local copies, waits for them, and re-layouts, order_occ_ints(): o = o.reshape(local_aux, nocc, n // 2, 2, rows)  5.48 us
    another operation x1, local copies, waits for them, and re-layouts, order_occ_ints(): jnp.stack([jnp.where(mine, even, odd), jnp.where(mine, odd, even)], axis=1)  4.67 us
  transfers between devices with their start and end apart: 32, of which 25 were waited for; matrix products, arithmetic and copies ran while one was open for 18% of the time, Pallas kernels for 22%

profile of v5, /device:TPU:0, one launch (start us, length us, event | category | flops | bytes accessed | tf_op | source)
XLA Modules:
  0.0 132.9 jit_solution(1341064910029612714)
XLA Ops:
  0.0 1.1 fusion.32
  1.1 0.8 dynamic_slice.103
  1.9 0.8 fusion.8
  2.6 4.1 %collective-permute-start = (bf16[1,16,1024]{2,1,0:T(8,128)(2,1)S(1)}, bf16[1,16,1024]{2,1,0:T(8,128)(2,1)S(1)}, u32[]{:S(2)}, u32[]{:S(2)}) collective-permute-start(bf16[1,16,1024]{2,1,0:T(8,128)(2,1)S(1)} %get-tuple-element.47), channel_id=1, source_target_pairs={{0,8},{1,9},{2,10},{3,11},{4,12},{5,13},{6,14},{7,15},{8,0},{9,1},... | collective-permute-start | bytes 98312 | tf_op jit(solution)/shard_map/ppermute | solution.py:36
  6.8 1.1 fusion
  7.9 1.1 fusion.3
  9.0 4.7 %copy.111 = bf16[4,2,8,16,256]{3,2,1,4,0:T(8,128)(2,1)} copy(bf16[4,2,8,16,256]{4,3,2,0,1:T(8,128)(2,1)S(1)} %pad_maximum_fusion) | data formatting | bytes 1048576 | tf_op jit(solution)/shard_map/stack | solution.py:97
  13.7 5.5 %reshape.268 = bf16[4,256,8,2,16]{1,4,3,2,0:T(8,128)(2,1)S(1)} reshape(bf16[4,2,8,16,256]{3,2,1,4,0:T(8,128)(2,1)} %copy.111) | data formatting | bytes 1048576 | tf_op jit(solution)/shard_map/reshape | solution.py:98
  19.4 1.0 copy.121.occ_ref
  20.4 1.9 %collective-permute-start.1 = (bf16[2,16,1024]{2,1,0:T(8,128)(2,1)S(1)}, bf16[2,16,1024]{2,1,0:T(8,128)(2,1)S(1)}, u32[]{:S(2)}, u32[]{:S(2)}) collective-permute-start(bf16[2,16,1024]{2,1,0:T(8,128)(2,1)S(1)} %pad_maximum_fusion.15), channel_id=1, source_target_pairs={{0,4},{1,3},{2,6},{3,1},{4,0},{5,7},{6,2},{7,5},{8,12},{9,11},{10,... | collective-permute-start | bytes 196616 | tf_op jit(solution)/shard_map/ppermute | solution.py:36
  22.6 2.1 %collective-permute-done.1 = bf16[2,16,1024]{2,1,0:T(8,128)(2,1)S(1)} collective-permute-done((bf16[2,16,1024]{2,1,0:T(8,128)(2,1)S(1)}, bf16[2,16,1024]{2,1,0:T(8,128)(2,1)S(1)}, u32[]{:S(2)}, u32[]{:S(2)}) %collective-permute-start.1) | collective-permute-done | bytes 65568 | tf_op jit(solution)/shard_map/ppermute | solution.py:36
  24.8 1.8 %collective-permute-start.2 = (bf16[4,16,1024]{2,1,0:T(8,128)(2,1)S(1)}, bf16[4,16,1024]{2,1,0:T(8,128)(2,1)S(1)}, u32[]{:S(2)}, u32[]{:S(2)}) collective-permute-start(bf16[4,16,1024]{2,1,0:T(8,128)(2,1)S(1)} %bitcast.253), channel_id=1, source_target_pairs={{0,2},{1,5},{2,0},{3,7},{4,6},{5,1},{6,4},{7,3},{8,10},{9,13},{10,... | collective-permute-start | bytes 393224 | tf_op jit(solution)/shard_map/ppermute | solution.py:36
  26.6 0.8 collective-permute-done.17
  27.4 1.6 %collective-permute-start.18 = (bf16[4,16,1024]{2,1,0:T(8,128)(2,1)S(1)}, bf16[4,16,1024]{2,1,0:T(8,128)(2,1)S(1)}, u32[]{:S(2)}, u32[]{:S(2)}) collective-permute-start(bf16[4,16,1024]{2,1,0:T(8,128)(2,1)S(1)} %bitcast.256), channel_id=1, source_target_pairs={{0,2},{1,5},{2,0},{3,7},{4,6},{5,1},{6,4},{7,3},{8,10},{9,13},{10,... | collective-permute-start | bytes 393224 | tf_op jit(solution)/shard_map/ppermute | solution.py:36
  29.0 0.8 collective-permute-done.2
  30.0 2.4 %collective-permute-done.18 = bf16[4,16,1024]{2,1,0:T(8,128)(2,1)S(1)} collective-permute-done((bf16[4,16,1024]{2,1,0:T(8,128)(2,1)S(1)}, bf16[4,16,1024]{2,1,0:T(8,128)(2,1)S(1)}, u32[]{:S(2)}, u32[]{:S(2)}) %collective-permute-start.18) | collective-permute-done | bytes 131104 | tf_op jit(solution)/shard_map/ppermute | solution.py:36
  32.7 0.8 pad_maximum_fusion.2
  33.5 7.2 %shard_map.55 = f32[256,1024]{1,0:T(8,128)} custom-call(bf16[4,256,256]{2,1,0:T(8,128)(2,1)} %copy.121.occ_ref, bf16[256,1024]{1,0:T(8,128)(2,1)} %bitcast.219, bf16[4,1024,1024]{2,1,0:T(8,128)(2,1)} %vir_ref.7), custom_call_target="tpu_custom_call" | custom-call | tf_op jit(solution)/shard_map/pallas_call | solution.py:123
  40.7 2.1 %fusion.29 = (f32[128,1024]{1,0:T(8,128)}, f32[128,1024]{1,0:T(8,128)S(1)}) fusion(f32[256,1024]{1,0:T(8,128)} %shard_map.55), kind=kLoop, calls=%fused_computation.112 | loop fusion | bytes 2097152 | tf_op jit(solution)/shard_map/slice | solution.py:64
  43.3 0.8 pad_maximum_fusion.4
  44.2 7.2 %shard_map.57 = f32[256,1024]{1,0:T(8,128)} custom-call(bf16[4,256,256]{2,1,0:T(8,128)(2,1)} %copy.121.occ_ref, bf16[256,1024]{1,0:T(8,128)(2,1)} %bitcast.220, bf16[4,1024,1024]{2,1,0:T(8,128)(2,1)} %vir_ref.7), custom_call_target="tpu_custom_call" | custom-call | tf_op jit(solution)/shard_map/pallas_call | solution.py:123
  51.4 1.3 fusion.31
  52.9 1.6 %collective-permute-start.5 = (f32[2,2,16,1024]{3,2,1,0:T(8,128)S(1)}, f32[2,2,16,1024]{3,2,1,0:T(8,128)S(1)}, u32[]{:S(2)}, u32[]{:S(2)}) collective-permute-start(f32[2,2,16,1024]{3,2,1,0:T(8,128)S(1)} %bitcast_select_fusion.10), channel_id=1, source_target_pairs={{0,2},{1,5},{2,0},{3,7},{4,6},{5,1},{6,4},{7,3},{8,10},{9,13},{10,... | collective-permute-start | bytes 786440 | tf_op jit(solution)/shard_map/ppermute | solution.py:85
  54.7 1.6 %collective-permute-start.21 = (f32[2,2,16,1024]{3,2,1,0:T(8,128)S(1)}, f32[2,2,16,1024]{3,2,1,0:T(8,128)S(1)}, u32[]{:S(2)}, u32[]{:S(2)}) collective-permute-start(f32[2,2,16,1024]{3,2,1,0:T(8,128)S(1)} %bitcast_select_fusion.6), channel_id=1, source_target_pairs={{0,2},{1,5},{2,0},{3,7},{4,6},{5,1},{6,4},{7,3},{8,10},{9,13},{10,... | collective-permute-start | bytes 786440 | tf_op jit(solution)/shard_map/ppermute | solution.py:85
  56.3 3.0 %collective-permute-done.5 = f32[2,2,16,1024]{3,2,1,0:T(8,128)S(1)} collective-permute-done((f32[2,2,16,1024]{3,2,1,0:T(8,128)S(1)}, f32[2,2,16,1024]{3,2,1,0:T(8,128)S(1)}, u32[]{:S(2)}, u32[]{:S(2)}) %collective-permute-start.5) | collective-permute-done | bytes 262176 | tf_op jit(solution)/shard_map/ppermute | solution.py:85
  59.4 0.9 collective-permute-start.6
  60.2 2.2 %collective-permute-done.21 = f32[2,2,16,1024]{3,2,1,0:T(8,128)S(1)} collective-permute-done((f32[2,2,16,1024]{3,2,1,0:T(8,128)S(1)}, f32[2,2,16,1024]{3,2,1,0:T(8,128)S(1)}, u32[]{:S(2)}, u32[]{:S(2)}) %collective-permute-start.21) | collective-permute-done | bytes 262176 | tf_op jit(solution)/shard_map/ppermute | solution.py:85
  62.6 0.9 collective-permute-start.22
  63.5 1.0 collective-permute-done.6
  64.5 2.7 %collective-permute-start.7 = (f32[16,1024]{1,0:T(8,128)S(1)}, f32[16,1024]{1,0:T(8,128)S(1)}, u32[]{:S(2)}, u32[]{:S(2)}) collective-permute-start(f32[16,1024]{1,0:T(8,128)S(1)} %dynamic-slice_bitcast_fusion.7), channel_id=1, source_target_pairs={{0,8},{1,9},{2,10},{3,11},{4,12},{5,13},{6,14},{7,15},{8,0},{9,1},... | collective-permute-start | bytes 196616 | tf_op jit(solution)/shard_map/ppermute | solution.py:85
  67.1 0.9 collective-permute-done.22
  68.0 2.3 %collective-permute-start.23 = (f32[16,1024]{1,0:T(8,128)S(1)}, f32[16,1024]{1,0:T(8,128)S(1)}, u32[]{:S(2)}, u32[]{:S(2)}) collective-permute-start(f32[16,1024]{1,0:T(8,128)S(1)} %dynamic-slice_bitcast_fusion.5), channel_id=1, source_target_pairs={{0,8},{1,9},{2,10},{3,11},{4,12},{5,13},{6,14},{7,15},{8,0},{9,1},... | collective-permute-start | bytes 196616 | tf_op jit(solution)/shard_map/ppermute | solution.py:85
  70.3 0.9 collective-permute-done.7
  71.2 2.8 %collective-permute-done.23 = f32[16,1024]{1,0:T(8,128)S(1)} collective-permute-done((f32[16,1024]{1,0:T(8,128)S(1)}, f32[16,1024]{1,0:T(8,128)S(1)}, u32[]{:S(2)}, u32[]{:S(2)}) %collective-permute-start.23) | collective-permute-done | bytes 65568 | tf_op jit(solution)/shard_map/ppermute | solution.py:85
  74.0 1.7 %collective-permute-start.8 = (bf16[1,16,1024]{2,1,0:T(8,128)(2,1)S(1)}, bf16[1,16,1024]{2,1,0:T(8,128)(2,1)S(1)}, u32[]{:S(2)}, u32[]{:S(2)}) collective-permute-start(bf16[1,16,1024]{2,1,0:T(8,128)(2,1)S(1)} %get-tuple-element.5), channel_id=1, source_target_pairs={{0,8},{1,9},{2,10},{3,11},{4,12},{5,13},{6,14},{7,15},{8,0},{9,1},... | collective-permute-start | bytes 98312 | tf_op jit(solution)/shard_map/ppermute | solution.py:36
  75.7 1.3 collective-permute-start.24
  77.0 2.2 %collective-permute-done.8 = bf16[1,16,1024]{2,1,0:T(8,128)(2,1)S(1)} collective-permute-done((bf16[1,16,1024]{2,1,0:T(8,128)(2,1)S(1)}, bf16[1,16,1024]{2,1,0:T(8,128)(2,1)S(1)}, u32[]{:S(2)}, u32[]{:S(2)}) %collective-permute-start.8) | collective-permute-done | bytes 32800 | tf_op jit(solution)/shard_map/ppermute | solution.py:36
  79.3 0.6 collective-permute-start.9
  79.9 0.6 collective-permute-done.24
  80.6 2.2 %collective-permute-start.25 = (bf16[2,16,1024]{2,1,0:T(8,128)(2,1)S(1)}, bf16[2,16,1024]{2,1,0:T(8,128)(2,1)S(1)}, u32[]{:S(2)}, u32[]{:S(2)}) collective-permute-start(bf16[2,16,1024]{2,1,0:T(8,128)(2,1)S(1)} %pad_maximum_fusion.18), channel_id=1, source_target_pairs={{0,4},{1,3},{2,6},{3,1},{4,0},{5,7},{6,2},{7,5},{8,12},{9,11},{10,... | collective-permute-start | bytes 196616 | tf_op jit(solution)/shard_map/ppermute | solution.py:36
  82.7 1.6 %collective-permute-done.9 = bf16[2,16,1024]{2,1,0:T(8,128)(2,1)S(1)} collective-permute-done((bf16[2,16,1024]{2,1,0:T(8,128)(2,1)S(1)}, bf16[2,16,1024]{2,1,0:T(8,128)(2,1)S(1)}, u32[]{:S(2)}, u32[]{:S(2)}) %collective-permute-start.9) | collective-permute-done | bytes 65568 | tf_op jit(solution)/shard_map/ppermute | solution.py:36
  84.4 1.1 collective-permute-start.10
  85.8 1.6 %collective-permute-start.26 = (bf16[4,16,1024]{2,1,0:T(8,128)(2,1)S(1)}, bf16[4,16,1024]{2,1,0:T(8,128)(2,1)S(1)}, u32[]{:S(2)}, u32[]{:S(2)}) collective-permute-start(bf16[4,16,1024]{2,1,0:T(8,128)(2,1)S(1)} %bitcast.255), channel_id=1, source_target_pairs={{0,2},{1,5},{2,0},{3,7},{4,6},{5,1},{6,4},{7,3},{8,10},{9,13},{10,... | collective-permute-start | bytes 393224 | tf_op jit(solution)/shard_map/ppermute | solution.py:36
  87.4 2.1 %collective-permute-done.10 = bf16[4,16,1024]{2,1,0:T(8,128)(2,1)S(1)} collective-permute-done((bf16[4,16,1024]{2,1,0:T(8,128)(2,1)S(1)}, bf16[4,16,1024]{2,1,0:T(8,128)(2,1)S(1)}, u32[]{:S(2)}, u32[]{:S(2)}) %collective-permute-start.10) | collective-permute-done | bytes 131104 | tf_op jit(solution)/shard_map/ppermute | solution.py:36
  89.6 1.2 collective-permute-done.26
  91.1 0.8 pad_maximum_fusion.3
  92.0 7.2 %shard_map.56 = f32[256,1024]{1,0:T(8,128)} custom-call(bf16[4,256,256]{2,1,0:T(8,128)(2,1)} %copy.121.occ_ref, bf16[256,1024]{1,0:T(8,128)(2,1)} %bitcast.221, bf16[4,1024,1024]{2,1,0:T(8,128)(2,1)} %vir_ref.7), custom_call_target="tpu_custom_call" | custom-call | tf_op jit(solution)/shard_map/pallas_call | solution.py:123
  99.2 1.3 fusion.28
  100.9 0.8 pad_maximum_fusion.5
  101.8 7.2 %shard_map.58 = f32[256,1024]{1,0:T(8,128)} custom-call(bf16[4,256,256]{2,1,0:T(8,128)(2,1)} %copy.121.occ_ref, bf16[256,1024]{1,0:T(8,128)(2,1)} %bitcast.218, bf16[4,1024,1024]{2,1,0:T(8,128)(2,1)} %vir_ref.7), custom_call_target="tpu_custom_call" | custom-call | tf_op jit(solution)/shard_map/pallas_call | solution.py:123
  109.0 1.3 fusion.30
  110.6 1.5 %collective-permute-start.13 = (f32[2,2,16,1024]{3,2,1,0:T(8,128)S(1)}, f32[2,2,16,1024]{3,2,1,0:T(8,128)S(1)}, u32[]{:S(2)}, u32[]{:S(2)}) collective-permute-start(f32[2,2,16,1024]{3,2,1,0:T(8,128)S(1)} %bitcast_select_fusion.8), channel_id=1, source_target_pairs={{0,2},{1,5},{2,0},{3,7},{4,6},{5,1},{6,4},{7,3},{8,10},{9,13},{10,... | collective-permute-start | bytes 786440 | tf_op jit(solution)/shard_map/ppermute | solution.py:85
  112.4 1.6 %collective-permute-start.29 = (f32[2,2,16,1024]{3,2,1,0:T(8,128)S(1)}, f32[2,2,16,1024]{3,2,1,0:T(8,128)S(1)}, u32[]{:S(2)}, u32[]{:S(2)}) collective-permute-start(f32[2,2,16,1024]{3,2,1,0:T(8,128)S(1)} %bitcast_select_fusion.4), channel_id=1, source_target_pairs={{0,2},{1,5},{2,0},{3,7},{4,6},{5,1},{6,4},{7,3},{8,10},{9,13},{10,... | collective-permute-start | bytes 786440 | tf_op jit(solution)/shard_map/ppermute | solution.py:85
  113.9 3.1 %collective-permute-done.13 = f32[2,2,16,1024]{3,2,1,0:T(8,128)S(1)} collective-permute-done((f32[2,2,16,1024]{3,2,1,0:T(8,128)S(1)}, f32[2,2,16,1024]{3,2,1,0:T(8,128)S(1)}, u32[]{:S(2)}, u32[]{:S(2)}) %collective-permute-start.13) | collective-permute-done | bytes 262176 | tf_op jit(solution)/shard_map/ppermute | solution.py:85
  117.1 1.2 collective-permute-start.14
  118.3 2.0 %collective-permute-done.29 = f32[2,2,16,1024]{3,2,1,0:T(8,128)S(1)} collective-permute-done((f32[2,2,16,1024]{3,2,1,0:T(8,128)S(1)}, f32[2,2,16,1024]{3,2,1,0:T(8,128)S(1)}, u32[]{:S(2)}, u32[]{:S(2)}) %collective-permute-start.29) | collective-permute-done | bytes 262176 | tf_op jit(solution)/shard_map/ppermute | solution.py:85
  120.4 1.1 collective-permute-start.30
  121.5 0.6 collective-permute-done.14
  122.2 1.8 %collective-permute-start.15 = (f32[16,1024]{1,0:T(8,128)S(1)}, f32[16,1024]{1,0:T(8,128)S(1)}, u32[]{:S(2)}, u32[]{:S(2)}) collective-permute-start(f32[16,1024]{1,0:T(8,128)S(1)} %dynamic-slice_bitcast_fusion.6), channel_id=1, source_target_pairs={{0,8},{1,9},{2,10},{3,11},{4,12},{5,13},{6,14},{7,15},{8,0},{9,1},... | collective-permute-start | bytes 196616 | tf_op jit(solution)/shard_map/ppermute | solution.py:85
  123.9 2.2 %collective-permute-done.30 = f32[2,16,1024]{2,1,0:T(8,128)S(1)} collective-permute-done((f32[2,16,1024]{2,1,0:T(8,128)S(1)}, f32[2,16,1024]{2,1,0:T(8,128)S(1)}, u32[]{:S(2)}, u32[]{:S(2)}) %collective-permute-start.30) | collective-permute-done | bytes 131104 | tf_op jit(solution)/shard_map/ppermute | solution.py:85
  126.1 1.6 %collective-permute-start.31 = (f32[16,1024]{1,0:T(8,128)S(1)}, f32[16,1024]{1,0:T(8,128)S(1)}, u32[]{:S(2)}, u32[]{:S(2)}) collective-permute-start(f32[16,1024]{1,0:T(8,128)S(1)} %dynamic-slice_bitcast_fusion.4), channel_id=1, source_target_pairs={{0,8},{1,9},{2,10},{3,11},{4,12},{5,13},{6,14},{7,15},{8,0},{9,1},... | collective-permute-start | bytes 196616 | tf_op jit(solution)/shard_map/ppermute | solution.py:85
  127.8 1.7 %collective-permute-done.15 = f32[16,1024]{1,0:T(8,128)S(1)} collective-permute-done((f32[16,1024]{1,0:T(8,128)S(1)}, f32[16,1024]{1,0:T(8,128)S(1)}, u32[]{:S(2)}, u32[]{:S(2)}) %collective-permute-start.15) | collective-permute-done | bytes 65568 | tf_op jit(solution)/shard_map/ppermute | solution.py:85
  129.5 2.6 %collective-permute-done.31 = f32[16,1024]{1,0:T(8,128)S(1)} collective-permute-done((f32[16,1024]{1,0:T(8,128)S(1)}, f32[16,1024]{1,0:T(8,128)S(1)}, u32[]{:S(2)}, u32[]{:S(2)}) %collective-permute-start.31) | collective-permute-done | bytes 65568 | tf_op jit(solution)/shard_map/ppermute | solution.py:85
  132.2 0.8 copy.138
  (86 shorter events, 4.5 us)
Async XLA Ops:
  2.6 17.8 %collective-permute-start = (bf16[1,16,1024]{2,1,0:T(8,128)(2,1)S(1)}, bf16[1,16,1024]{2,1,0:T(8,128)(2,1)S(1)}, u32[]{:S(2)}, u32[]{:S(2)}) collective-permute-start(bf16[1,16,1024]{2,1,0:T(8,128)(2,1)S(1)} %get-tuple-element.47), channel_id=1, source_target_pairs={{0,8},{1,9},{2,10},{3,11},{4,12},{5,13},{6,14},{7,15},{8,0},{9,1},... | collective-permute-start | bytes 98312 | tf_op jit(solution)/shard_map/ppermute | solution.py:36
  6.7 15.6 %collective-permute-start.16 = (bf16[1,16,1024]{2,1,0:T(8,128)(2,1)S(1)}, bf16[1,16,1024]{2,1,0:T(8,128)(2,1)S(1)}, u32[]{:S(2)}, u32[]{:S(2)}) collective-permute-start(bf16[1,16,1024]{2,1,0:T(8,128)(2,1)S(1)} %get-tuple-element.48), channel_id=1, source_target_pairs={{0,8},{1,9},{2,10},{3,11},{4,12},{5,13},{6,14},{7,15},{8,0},{9,1},... | collective-permute-start | bytes 98312 | tf_op jit(solution)/shard_map/ppermute | solution.py:36
  20.4 4.3 %collective-permute-start.1 = (bf16[2,16,1024]{2,1,0:T(8,128)(2,1)S(1)}, bf16[2,16,1024]{2,1,0:T(8,128)(2,1)S(1)}, u32[]{:S(2)}, u32[]{:S(2)}) collective-permute-start(bf16[2,16,1024]{2,1,0:T(8,128)(2,1)S(1)} %pad_maximum_fusion.15), channel_id=1, source_target_pairs={{0,4},{1,3},{2,6},{3,1},{4,0},{5,7},{6,2},{7,5},{8,12},{9,11},{10,... | collective-permute-start | bytes 196616 | tf_op jit(solution)/shard_map/ppermute | solution.py:36
  22.4 5.0 %collective-permute-start.17 = (bf16[2,16,1024]{2,1,0:T(8,128)(2,1)S(1)}, bf16[2,16,1024]{2,1,0:T(8,128)(2,1)S(1)}, u32[]{:S(2)}, u32[]{:S(2)}) collective-permute-start(bf16[2,16,1024]{2,1,0:T(8,128)(2,1)S(1)} %pad_maximum_fusion.17), channel_id=1, source_target_pairs={{0,4},{1,3},{2,6},{3,1},{4,0},{5,7},{6,2},{7,5},{8,12},{9,11},{10,... | collective-permute-start | bytes 196616 | tf_op jit(solution)/shard_map/ppermute | solution.py:36
  24.8 5.0 %collective-permute-start.2 = (bf16[4,16,1024]{2,1,0:T(8,128)(2,1)S(1)}, bf16[4,16,1024]{2,1,0:T(8,128)(2,1)S(1)}, u32[]{:S(2)}, u32[]{:S(2)}) collective-permute-start(bf16[4,16,1024]{2,1,0:T(8,128)(2,1)S(1)} %bitcast.253), channel_id=1, source_target_pairs={{0,2},{1,5},{2,0},{3,7},{4,6},{5,1},{6,4},{7,3},{8,10},{9,13},{10,... | collective-permute-start | bytes 393224 | tf_op jit(solution)/shard_map/ppermute | solution.py:36
  27.4 5.0 %collective-permute-start.18 = (bf16[4,16,1024]{2,1,0:T(8,128)(2,1)S(1)}, bf16[4,16,1024]{2,1,0:T(8,128)(2,1)S(1)}, u32[]{:S(2)}, u32[]{:S(2)}) collective-permute-start(bf16[4,16,1024]{2,1,0:T(8,128)(2,1)S(1)} %bitcast.256), channel_id=1, source_target_pairs={{0,2},{1,5},{2,0},{3,7},{4,6},{5,1},{6,4},{7,3},{8,10},{9,13},{10,... | collective-permute-start | bytes 393224 | tf_op jit(solution)/shard_map/ppermute | solution.py:36
  30.0 2.7 %collective-permute-start.3 = (bf16[8,16,1024]{2,1,0:T(8,128)(2,1)S(1)}, bf16[8,16,1024]{2,1,0:T(8,128)(2,1)S(1)}, u32[]{:S(2)}, u32[]{:S(2)}) collective-permute-start(bf16[8,16,1024]{2,1,0:T(8,128)(2,1)S(1)} %bitcast.247), channel_id=1, source_target_pairs={{0,1},{1,0},{2,3},{3,2},{4,5},{5,4},{6,7},{7,6},{8,9},{9,8},{10,11... | collective-permute-start | bytes 786440 | tf_op jit(solution)/shard_map/ppermute | solution.py:52
  32.6 10.7 %collective-permute-start.19 = (bf16[8,16,1024]{2,1,0:T(8,128)(2,1)S(1)}, bf16[8,16,1024]{2,1,0:T(8,128)(2,1)S(1)}, u32[]{:S(2)}, u32[]{:S(2)}) collective-permute-start(bf16[8,16,1024]{2,1,0:T(8,128)(2,1)S(1)} %bitcast.249), channel_id=1, source_target_pairs={{0,1},{1,0},{2,3},{3,2},{4,5},{5,4},{6,7},{7,6},{8,9},{9,8},{10,11... | collective-permute-start | bytes 786440 | tf_op jit(solution)/shard_map/ppermute | solution.py:52
  42.8 9.9 %collective-permute-start.4 = (f32[2,2,2,16,1024]{4,3,2,1,0:T(8,128)}, f32[2,2,2,16,1024]{4,3,2,1,0:T(8,128)S(1)}, u32[]{:S(2)}, u32[]{:S(2)}) collective-permute-start(f32[2,2,2,16,1024]{4,3,2,1,0:T(8,128)} %bitcast.25), channel_id=1, source_target_pairs={{0,1},{1,0},{2,3},{3,2},{4,5},{5,4},{6,7},{7,6},{8,9},{9,8},{10,11... | collective-permute-start | bytes 1572872 | tf_op jit(solution)/shard_map/ppermute | solution.py:64
  44.2 29.8 %copy-start = (f32[1024]{0:T(1024)S(1)}, f32[1024]{0:T(1024)}, u32[]{:S(2)}) copy-start(f32[1024]{0:T(1024)} %param.7) | copy-start | bytes 12292
  52.7 2.0 %collective-permute-start.20 = (f32[2,2,2,16,1024]{4,3,2,1,0:T(8,128)S(1)}, f32[2,2,2,16,1024]{4,3,2,1,0:T(8,128)S(1)}, u32[]{:S(2)}, u32[]{:S(2)}) collective-permute-start(f32[2,2,2,16,1024]{4,3,2,1,0:T(8,128)S(1)} %bitcast.257), channel_id=1, source_target_pairs={{0,1},{1,0},{2,3},{3,2},{4,5},{5,4},{6,7},{7,6},{8,9},{9,8},{10,11... | collective-permute-start | bytes 1572872 | tf_op jit(solution)/shard_map/ppermute | solution.py:64
  52.9 6.4 %collective-permute-start.5 = (f32[2,2,16,1024]{3,2,1,0:T(8,128)S(1)}, f32[2,2,16,1024]{3,2,1,0:T(8,128)S(1)}, u32[]{:S(2)}, u32[]{:S(2)}) collective-permute-start(f32[2,2,16,1024]{3,2,1,0:T(8,128)S(1)} %bitcast_select_fusion.10), channel_id=1, source_target_pairs={{0,2},{1,5},{2,0},{3,7},{4,6},{5,1},{6,4},{7,3},{8,10},{9,13},{10,... | collective-permute-start | bytes 786440 | tf_op jit(solution)/shard_map/ppermute | solution.py:85
  54.7 7.8 %collective-permute-start.21 = (f32[2,2,16,1024]{3,2,1,0:T(8,128)S(1)}, f32[2,2,16,1024]{3,2,1,0:T(8,128)S(1)}, u32[]{:S(2)}, u32[]{:S(2)}) collective-permute-start(f32[2,2,16,1024]{3,2,1,0:T(8,128)S(1)} %bitcast_select_fusion.6), channel_id=1, source_target_pairs={{0,2},{1,5},{2,0},{3,7},{4,6},{5,1},{6,4},{7,3},{8,10},{9,13},{10,... | collective-permute-start | bytes 786440 | tf_op jit(solution)/shard_map/ppermute | solution.py:85
  59.4 5.0 %collective-permute-start.6 = (f32[2,16,1024]{2,1,0:T(8,128)S(1)}, f32[2,16,1024]{2,1,0:T(8,128)S(1)}, u32[]{:S(2)}, u32[]{:S(2)}) collective-permute-start(f32[2,16,1024]{2,1,0:T(8,128)S(1)} %dynamic-slice_bitcast_fusion.3), channel_id=1, source_target_pairs={{0,4},{1,3},{2,6},{3,1},{4,0},{5,7},{6,2},{7,5},{8,12},{9,11},{10,... | collective-permute-start | bytes 393224 | tf_op jit(solution)/shard_map/ppermute | solution.py:85
  62.6 5.4 %collective-permute-start.22 = (f32[2,16,1024]{2,1,0:T(8,128)S(1)}, f32[2,16,1024]{2,1,0:T(8,128)S(1)}, u32[]{:S(2)}, u32[]{:S(2)}) collective-permute-start(f32[2,16,1024]{2,1,0:T(8,128)S(1)} %dynamic-slice_bitcast_fusion.1), channel_id=1, source_target_pairs={{0,4},{1,3},{2,6},{3,1},{4,0},{5,7},{6,2},{7,5},{8,12},{9,11},{10,... | collective-permute-start | bytes 393224 | tf_op jit(solution)/shard_map/ppermute | solution.py:85
  64.5 6.7 %collective-permute-start.7 = (f32[16,1024]{1,0:T(8,128)S(1)}, f32[16,1024]{1,0:T(8,128)S(1)}, u32[]{:S(2)}, u32[]{:S(2)}) collective-permute-start(f32[16,1024]{1,0:T(8,128)S(1)} %dynamic-slice_bitcast_fusion.7), channel_id=1, source_target_pairs={{0,8},{1,9},{2,10},{3,11},{4,12},{5,13},{6,14},{7,15},{8,0},{9,1},... | collective-permute-start | bytes 196616 | tf_op jit(solution)/shard_map/ppermute | solution.py:85
  68.0 5.9 %collective-permute-start.23 = (f32[16,1024]{1,0:T(8,128)S(1)}, f32[16,1024]{1,0:T(8,128)S(1)}, u32[]{:S(2)}, u32[]{:S(2)}) collective-permute-start(f32[16,1024]{1,0:T(8,128)S(1)} %dynamic-slice_bitcast_fusion.5), channel_id=1, source_target_pairs={{0,8},{1,9},{2,10},{3,11},{4,12},{5,13},{6,14},{7,15},{8,0},{9,1},... | collective-permute-start | bytes 196616 | tf_op jit(solution)/shard_map/ppermute | solution.py:85
  74.0 5.2 %collective-permute-start.8 = (bf16[1,16,1024]{2,1,0:T(8,128)(2,1)S(1)}, bf16[1,16,1024]{2,1,0:T(8,128)(2,1)S(1)}, u32[]{:S(2)}, u32[]{:S(2)}) collective-permute-start(bf16[1,16,1024]{2,1,0:T(8,128)(2,1)S(1)} %get-tuple-element.5), channel_id=1, source_target_pairs={{0,8},{1,9},{2,10},{3,11},{4,12},{5,13},{6,14},{7,15},{8,0},{9,1},... | collective-permute-start | bytes 98312 | tf_op jit(solution)/shard_map/ppermute | solution.py:36
  75.7 4.8 %collective-permute-start.24 = (bf16[1,16,1024]{2,1,0:T(8,128)(2,1)S(1)}, bf16[1,16,1024]{2,1,0:T(8,128)(2,1)S(1)}, u32[]{:S(2)}, u32[]{:S(2)}) collective-permute-start(bf16[1,16,1024]{2,1,0:T(8,128)(2,1)S(1)} %get-tuple-element.45), channel_id=1, source_target_pairs={{0,8},{1,9},{2,10},{3,11},{4,12},{5,13},{6,14},{7,15},{8,0},{9,1},... | collective-permute-start | bytes 98312 | tf_op jit(solution)/shard_map/ppermute | solution.py:36
  79.3 5.0 %collective-permute-start.9 = (bf16[2,16,1024]{2,1,0:T(8,128)(2,1)S(1)}, bf16[2,16,1024]{2,1,0:T(8,128)(2,1)S(1)}, u32[]{:S(2)}, u32[]{:S(2)}) collective-permute-start(bf16[2,16,1024]{2,1,0:T(8,128)(2,1)S(1)} %pad_maximum_fusion.16), channel_id=1, source_target_pairs={{0,4},{1,3},{2,6},{3,1},{4,0},{5,7},{6,2},{7,5},{8,12},{9,11},{10,... | collective-permute-start | bytes 196616 | tf_op jit(solution)/shard_map/ppermute | solution.py:36
  80.6 5.2 %collective-permute-start.25 = (bf16[2,16,1024]{2,1,0:T(8,128)(2,1)S(1)}, bf16[2,16,1024]{2,1,0:T(8,128)(2,1)S(1)}, u32[]{:S(2)}, u32[]{:S(2)}) collective-permute-start(bf16[2,16,1024]{2,1,0:T(8,128)(2,1)S(1)} %pad_maximum_fusion.18), channel_id=1, source_target_pairs={{0,4},{1,3},{2,6},{3,1},{4,0},{5,7},{6,2},{7,5},{8,12},{9,11},{10,... | collective-permute-start | bytes 196616 | tf_op jit(solution)/shard_map/ppermute | solution.py:36
  84.4 5.0 %collective-permute-start.10 = (bf16[4,16,1024]{2,1,0:T(8,128)(2,1)S(1)}, bf16[4,16,1024]{2,1,0:T(8,128)(2,1)S(1)}, u32[]{:S(2)}, u32[]{:S(2)}) collective-permute-start(bf16[4,16,1024]{2,1,0:T(8,128)(2,1)S(1)} %bitcast.254), channel_id=1, source_target_pairs={{0,2},{1,5},{2,0},{3,7},{4,6},{5,1},{6,4},{7,3},{8,10},{9,13},{10,... | collective-permute-start | bytes 393224 | tf_op jit(solution)/shard_map/ppermute | solution.py:36
  85.8 5.0 %collective-permute-start.26 = (bf16[4,16,1024]{2,1,0:T(8,128)(2,1)S(1)}, bf16[4,16,1024]{2,1,0:T(8,128)(2,1)S(1)}, u32[]{:S(2)}, u32[]{:S(2)}) collective-permute-start(bf16[4,16,1024]{2,1,0:T(8,128)(2,1)S(1)} %bitcast.255), channel_id=1, source_target_pairs={{0,2},{1,5},{2,0},{3,7},{4,6},{5,1},{6,4},{7,3},{8,10},{9,13},{10,... | collective-permute-start | bytes 393224 | tf_op jit(solution)/shard_map/ppermute | solution.py:36
  89.5 1.6 %collective-permute-start.11 = (bf16[8,16,1024]{2,1,0:T(8,128)(2,1)S(1)}, bf16[8,16,1024]{2,1,0:T(8,128)(2,1)S(1)}, u32[]{:S(2)}, u32[]{:S(2)}) collective-permute-start(bf16[8,16,1024]{2,1,0:T(8,128)(2,1)S(1)} %bitcast.245), channel_id=1, source_target_pairs={{0,1},{1,0},{2,3},{3,2},{4,5},{5,4},{6,7},{7,6},{8,9},{9,8},{10,11... | collective-permute-start | bytes 786440 | tf_op jit(solution)/shard_map/ppermute | solution.py:52
  90.9 10.0 %collective-permute-start.27 = (bf16[8,16,1024]{2,1,0:T(8,128)(2,1)S(1)}, bf16[8,16,1024]{2,1,0:T(8,128)(2,1)S(1)}, u32[]{:S(2)}, u32[]{:S(2)}) collective-permute-start(bf16[8,16,1024]{2,1,0:T(8,128)(2,1)S(1)} %bitcast.251), channel_id=1, source_target_pairs={{0,1},{1,0},{2,3},{3,2},{4,5},{5,4},{6,7},{7,6},{8,9},{9,8},{10,11... | collective-permute-start | bytes 786440 | tf_op jit(solution)/shard_map/ppermute | solution.py:52
  100.5 10.0 %collective-permute-start.12 = (f32[2,2,2,16,1024]{4,3,2,1,0:T(8,128)S(1)}, f32[2,2,2,16,1024]{4,3,2,1,0:T(8,128)S(1)}, u32[]{:S(2)}, u32[]{:S(2)}) collective-permute-start(f32[2,2,2,16,1024]{4,3,2,1,0:T(8,128)S(1)} %bitcast.258), channel_id=1, source_target_pairs={{0,1},{1,0},{2,3},{3,2},{4,5},{5,4},{6,7},{7,6},{8,9},{9,8},{10,11... | collective-permute-start | bytes 1572872 | tf_op jit(solution)/shard_map/ppermute | solution.py:64
  110.3 2.0 %collective-permute-start.28 = (f32[2,2,2,16,1024]{4,3,2,1,0:T(8,128)S(1)}, f32[2,2,2,16,1024]{4,3,2,1,0:T(8,128)S(1)}, u32[]{:S(2)}, u32[]{:S(2)}) collective-permute-start(f32[2,2,2,16,1024]{4,3,2,1,0:T(8,128)S(1)} %bitcast.259), channel_id=1, source_target_pairs={{0,1},{1,0},{2,3},{3,2},{4,5},{5,4},{6,7},{7,6},{8,9},{9,8},{10,11... | collective-permute-start | bytes 1572872 | tf_op jit(solution)/shard_map/ppermute | solution.py:64
  110.6 6.4 %collective-permute-start.13 = (f32[2,2,16,1024]{3,2,1,0:T(8,128)S(1)}, f32[2,2,16,1024]{3,2,1,0:T(8,128)S(1)}, u32[]{:S(2)}, u32[]{:S(2)}) collective-permute-start(f32[2,2,16,1024]{3,2,1,0:T(8,128)S(1)} %bitcast_select_fusion.8), channel_id=1, source_target_pairs={{0,2},{1,5},{2,0},{3,7},{4,6},{5,1},{6,4},{7,3},{8,10},{9,13},{10,... | collective-permute-start | bytes 786440 | tf_op jit(solution)/shard_map/ppermute | solution.py:85
  112.4 7.9 %collective-permute-start.29 = (f32[2,2,16,1024]{3,2,1,0:T(8,128)S(1)}, f32[2,2,16,1024]{3,2,1,0:T(8,128)S(1)}, u32[]{:S(2)}, u32[]{:S(2)}) collective-permute-start(f32[2,2,16,1024]{3,2,1,0:T(8,128)S(1)} %bitcast_select_fusion.4), channel_id=1, source_target_pairs={{0,2},{1,5},{2,0},{3,7},{4,6},{5,1},{6,4},{7,3},{8,10},{9,13},{10,... | collective-permute-start | bytes 786440 | tf_op jit(solution)/shard_map/ppermute | solution.py:85
  117.1 5.0 %collective-permute-start.14 = (f32[2,16,1024]{2,1,0:T(8,128)S(1)}, f32[2,16,1024]{2,1,0:T(8,128)S(1)}, u32[]{:S(2)}, u32[]{:S(2)}) collective-permute-start(f32[2,16,1024]{2,1,0:T(8,128)S(1)} %dynamic-slice_bitcast_fusion.2), channel_id=1, source_target_pairs={{0,4},{1,3},{2,6},{3,1},{4,0},{5,7},{6,2},{7,5},{8,12},{9,11},{10,... | collective-permute-start | bytes 393224 | tf_op jit(solution)/shard_map/ppermute | solution.py:85
  120.4 5.7 %collective-permute-start.30 = (f32[2,16,1024]{2,1,0:T(8,128)S(1)}, f32[2,16,1024]{2,1,0:T(8,128)S(1)}, u32[]{:S(2)}, u32[]{:S(2)}) collective-permute-start(f32[2,16,1024]{2,1,0:T(8,128)S(1)} %dynamic-slice_bitcast_fusion), channel_id=1, source_target_pairs={{0,4},{1,3},{2,6},{3,1},{4,0},{5,7},{6,2},{7,5},{8,12},{9,11},{10,... | collective-permute-start | bytes 393224 | tf_op jit(solution)/shard_map/ppermute | solution.py:85
  122.2 7.3 %collective-permute-start.15 = (f32[16,1024]{1,0:T(8,128)S(1)}, f32[16,1024]{1,0:T(8,128)S(1)}, u32[]{:S(2)}, u32[]{:S(2)}) collective-permute-start(f32[16,1024]{1,0:T(8,128)S(1)} %dynamic-slice_bitcast_fusion.6), channel_id=1, source_target_pairs={{0,8},{1,9},{2,10},{3,11},{4,12},{5,13},{6,14},{7,15},{8,0},{9,1},... | collective-permute-start | bytes 196616 | tf_op jit(solution)/shard_map/ppermute | solution.py:85
  126.1 5.9 %collective-permute-start.31 = (f32[16,1024]{1,0:T(8,128)S(1)}, f32[16,1024]{1,0:T(8,128)S(1)}, u32[]{:S(2)}, u32[]{:S(2)}) collective-permute-start(f32[16,1024]{1,0:T(8,128)S(1)} %dynamic-slice_bitcast_fusion.4), channel_id=1, source_target_pairs={{0,8},{1,9},{2,10},{3,11},{4,12},{5,13},{6,14},{7,15},{8,0},{9,1},... | collective-permute-start | bytes 196616 | tf_op jit(solution)/shard_map/ppermute | solution.py:85

commit v6 on v4

--- a/solution.py
+++ b/solution.py
@@ -128,19 +128,21 @@
     position = lax.axis_index("aux")
     my_occ = lax.dynamic_slice_in_dim(occ_energy, position * own_rows, own_rows, 0)
     denom = vir_energy[None, None, :] - my_occ[:, None, None]
-    finals = []
-    for state in range(states):
-        own_rhs = rhs[:, state, :]
-        own_denom = denom[:, 0, :]
-        resp = own_rhs / own_denom
-        for step in range(ITERS):
-            rounded = resp.astype(jnp.bfloat16)
+    own_denom = denom[:, 0, :]
+    resps = [rhs[:, state, :] / own_denom for state in range(states)]
+    for step in range(ITERS - 1):
+        for state in range(states):
+            rounded = resps[state].astype(jnp.bfloat16)
             flat = gather_rows(rounded, n)
             part = exchange_part(occ_ints, flat, vir_ints, 1)
             exchange = scatter_sum(part, n)
-            resp = 0.4 * resp + 0.6 * (own_rhs - exchange) / own_denom
-        finals.append(resp)
-    response = jnp.stack(finals, axis=1)
+            resps[state] = 0.4 * resps[state] + 0.6 * (rhs[:, state, :] - exchange) / own_denom
+    response = jnp.stack(resps, axis=1)
+    rounded = response.astype(jnp.bfloat16).reshape(own_rows, states * nvir)
+    flat = gather_rows(rounded, n)
+    part = exchange_part(occ_ints, flat, vir_ints, states)
+    exchange = scatter_sum(part, n).reshape(own_rows, states, nvir)
+    response = 0.4 * response + 0.6 * (rhs - exchange) / denom
     return response
 
 

time: 122 us -> 125 us (1.025)
  waiting for transfers between devices: 41.2 us -> 64.5 us
  starting transfers between devices: 38.1 us -> 24.4 us
  Pallas kernels: 28.8 us -> 24.2 us
    ppermute x16 -> x12, waiting for transfers between devices: 23.7 us -> 37 us  [scatter_sum(): acc = keep + lax.ppermute(send, 'aux', partners(n, b0, b1))]
    ppermute x16 -> x12, waiting for transfers between devices: 17.5 us -> 27.6 us  [gather_rows(): theirs = lax.ppermute(acc, 'aux', partners(n, b0, b1))]
    ppermute x16 -> x12, starting transfers between devices: 20.4 us -> 12 us  [scatter_sum(): acc = keep + lax.ppermute(send, 'aux', partners(n, b0, b1))]
    ppermute x16 -> x12, starting transfers between devices: 17.8 us -> 12.4 us  [gather_rows(): theirs = lax.ppermute(acc, 'aux', partners(n, b0, b1))]
    pallas_call x4 -> x3, Pallas kernels: 28.8 us -> 24.2 us  [exchange_part(): pl.pallas_call(functools.partial(exchange_kernel, states), grid=(local_au...]
    dynamic_slice x3 -> x2, local copies, waits for them, and re-layouts: 3.98 us -> 3.06 us  [scatter_sum(): keep = lax.dynamic_index_in_dim(acc, bit, axis=at0, keepdims=False)]
    another operation x16 -> x12, other arithmetic: 3.52 us -> 2.92 us  [gather_rows(): new0 = jnp.stack([lo, hi], axis=at0)]
  transfers between devices with their start and end apart: 32 -> 24, of which waited for: 26 -> 21; matrix products, arithmetic and copies ran while one was open for 6% -> 1% of each run, Pallas kernels for 18% -> 0%
where the time goes in v6:
time: 125 us
  waiting for transfers between devices  64.5 us (52%)
  starting transfers between devices  24.4 us (20%)
  Pallas kernels  24.2 us (19%)
  local copies, waits for them, and re-layouts  6.12 us (5%)
  other arithmetic  5.11 us (4%)
    ppermute x12, waiting for transfers between devices, scatter_sum(): acc = keep + lax.ppermute(send, 'aux', partners(n, b0, b1))  37 us
    ppermute x12, waiting for transfers between devices, gather_rows(): theirs = lax.ppermute(acc, 'aux', partners(n, b0, b1))  27.6 us
    pallas_call x3, Pallas kernels, exchange_part(): pl.pallas_call(functools.partial(exchange_kernel, states), grid=(local_au...  24.2 us
    ppermute x12, starting transfers between devices, gather_rows(): theirs = lax.ppermute(acc, 'aux', partners(n, b0, b1))  12.4 us
    ppermute x12, starting transfers between devices, scatter_sum(): acc = keep + lax.ppermute(send, 'aux', partners(n, b0, b1))  12 us
    dynamic_slice x2, local copies, waits for them, and re-layouts, scatter_sum(): keep = lax.dynamic_index_in_dim(acc, bit, axis=at0, keepdims=False)  3.06 us
    another operation x12, other arithmetic, gather_rows(): new0 = jnp.stack([lo, hi], axis=at0)  2.92 us
  transfers between devices with their start and end apart: 24, of which 21 were waited for; matrix products, arithmetic and copies ran while one was open for 1% of the time, Pallas kernels for 0%

profile of v6, /device:TPU:0, one launch (start us, length us, event | category | flops | bytes accessed | tf_op | source)
XLA Modules:
  0.0 124.8 jit_solution(4458446548349072341)
XLA Ops:
  0.0 0.9 copy.36
  1.0 0.8 dynamic_slice.103
  1.7 0.8 fusion.7
  2.5 4.1 %collective-permute-start = (bf16[1,16,1024]{2,1,0:T(8,128)(2,1)S(1)}, bf16[1,16,1024]{2,1,0:T(8,128)(2,1)S(1)}, u32[]{:S(2)}, u32[]{:S(2)}) collective-permute-start(bf16[1,16,1024]{2,1,0:T(8,128)(2,1)S(1)} %get-tuple-element.33), channel_id=1, source_target_pairs={{0,8},{1,9},{2,10},{3,11},{4,12},{5,13},{6,14},{7,15},{8,0},{9,1},... | collective-permute-start | bytes 98312 | tf_op jit(solution)/shard_map/ppermute | solution.py:36
  6.6 0.1 collective-permute-start.8
  6.7 2.2 %collective-permute-done = bf16[1,16,1024]{2,1,0:T(8,128)(2,1)S(1)} collective-permute-done((bf16[1,16,1024]{2,1,0:T(8,128)(2,1)S(1)}, bf16[1,16,1024]{2,1,0:T(8,128)(2,1)S(1)}, u32[]{:S(2)}, u32[]{:S(2)}) %collective-permute-start) | collective-permute-done | bytes 32800 | tf_op jit(solution)/shard_map/ppermute | solution.py:36
  8.9 1.7 %collective-permute-start.1 = (bf16[2,16,1024]{2,1,0:T(8,128)(2,1)S(1)}, bf16[2,16,1024]{2,1,0:T(8,128)(2,1)S(1)}, u32[]{:S(2)}, u32[]{:S(2)}) collective-permute-start(bf16[2,16,1024]{2,1,0:T(8,128)(2,1)S(1)} %pad_maximum_fusion.8), channel_id=1, source_target_pairs={{0,4},{1,3},{2,6},{3,1},{4,0},{5,7},{6,2},{7,5},{8,12},{9,11},{10,... | collective-permute-start | bytes 196616 | tf_op jit(solution)/shard_map/ppermute | solution.py:36
  10.5 0.9 collective-permute-done.8
  11.4 1.6 %collective-permute-start.9 = (bf16[2,16,1024]{2,1,0:T(8,128)(2,1)S(1)}, bf16[2,16,1024]{2,1,0:T(8,128)(2,1)S(1)}, u32[]{:S(2)}, u32[]{:S(2)}) collective-permute-start(bf16[2,16,1024]{2,1,0:T(8,128)(2,1)S(1)} %pad_maximum_fusion.9), channel_id=1, source_target_pairs={{0,4},{1,3},{2,6},{3,1},{4,0},{5,7},{6,2},{7,5},{8,12},{9,11},{10,... | collective-permute-start | bytes 196616 | tf_op jit(solution)/shard_map/ppermute | solution.py:36
  13.1 0.1 collective-permute-done.1
  13.2 1.8 %collective-permute-start.2 = (bf16[4,16,1024]{2,1,0:T(8,128)(2,1)S(1)}, bf16[4,16,1024]{2,1,0:T(8,128)(2,1)S(1)}, u32[]{:S(2)}, u32[]{:S(2)}) collective-permute-start(bf16[4,16,1024]{2,1,0:T(8,128)(2,1)S(1)} %bitcast.223), channel_id=1, source_target_pairs={{0,2},{1,5},{2,0},{3,7},{4,6},{5,1},{6,4},{7,3},{8,10},{9,13},{10,... | collective-permute-start | bytes 393224 | tf_op jit(solution)/shard_map/ppermute | solution.py:36
  15.0 1.2 collective-permute-done.9
  16.3 1.1 collective-permute-start.10
  17.4 0.9 collective-permute-done.2
  18.4 0.1 collective-permute-start.3
  18.4 2.9 %collective-permute-done.10 = bf16[4,16,1024]{2,1,0:T(8,128)(2,1)S(1)} collective-permute-done((bf16[4,16,1024]{2,1,0:T(8,128)(2,1)S(1)}, bf16[4,16,1024]{2,1,0:T(8,128)(2,1)S(1)}, u32[]{:S(2)}, u32[]{:S(2)}) %collective-permute-start.10) | collective-permute-done | bytes 131104 | tf_op jit(solution)/shard_map/ppermute | solution.py:36
  21.5 0.9 pad_maximum_fusion.1
  22.4 0.6 collective-permute-done.11
  23.0 0.9 pad_maximum_fusion.2
  23.9 7.2 %shard_map.56 = f32[256,1024]{1,0:T(8,128)} custom-call(bf16[4,256,256]{2,1,0:T(8,128)(2,1)} %occ_ref.5, bf16[256,1024]{1,0:T(8,128)(2,1)} %bitcast.204, bf16[4,1024,1024]{2,1,0:T(8,128)(2,1)} %vir_ref.5), custom_call_target="tpu_custom_call" | custom-call | tf_op jit(solution)/shard_map/pallas_call | solution.py:107
  31.1 7.3 %shard_map.55 = f32[256,1024]{1,0:T(8,128)} custom-call(bf16[4,256,256]{2,1,0:T(8,128)(2,1)} %occ_ref.5, bf16[256,1024]{1,0:T(8,128)(2,1)} %bitcast.202, bf16[4,1024,1024]{2,1,0:T(8,128)(2,1)} %vir_ref.5), custom_call_target="tpu_custom_call" | custom-call | tf_op jit(solution)/shard_map/pallas_call | solution.py:107
  38.4 1.4 %constant_dynamic-slice_fusion.7 = (f32[2,2,2,1,16,1024]{5,4,3,2,1,0:T(8,128)S(1)}, f32[2,2,2,1,16,1024]{5,4,3,2,1,0:T(8,128)S(1)}, f32[2,2,2,1,16,1024]{5,4,3,2,1,0:T(8,128)S(1)}, f32[2,2,2,1,16,1024]{5,4,3,2,1,0:T(8,128)S(1)}) fusion(f32[2,2,2,2,16,1024]{5,4,3,2,1,0:T(8,128)S(1)} %bitcast.195, s32[]{:T(128)S(6)} %select_n.300, s32[]{:T(128)S(6)} %select_n.301, ...), kind=kLoop, calls=%fused_computation.95 | loop fusion | bytes 4194312 | tf_op jit(solution)/shard_map/jit(dynamic_index_in_dim)/dynamic_slice | solution.py:69
  39.8 0.2 collective-permute-start.4
  40.1 0.4 collective-permute-start.12
  40.5 1.3 %collective-permute-done.4 = f32[2,2,2,16,1024]{4,3,2,0,1:T(8,128)S(1)} collective-permute-done((f32[2,2,2,16,1024]{4,3,2,0,1:T(8,128)S(1)}, f32[2,2,2,16,1024]{4,3,2,0,1:T(8,128)S(1)}, u32[]{:S(2)}, u32[]{:S(2)}) %collective-permute-start.4) | collective-permute-done | bytes 524320 | tf_op jit(solution)/shard_map/ppermute | solution.py:82
  41.9 1.1 collective-permute-start.5
  43.2 1.0 collective-permute-start.13
  44.3 4.1 %collective-permute-done.5 = f32[2,2,16,1024]{3,2,1,0:T(8,128)S(1)} collective-permute-done((f32[2,2,16,1024]{3,2,1,0:T(8,128)S(1)}, f32[2,2,16,1024]{3,2,1,0:T(8,128)S(1)}, u32[]{:S(2)}, u32[]{:S(2)}) %collective-permute-start.5) | collective-permute-done | bytes 262176 | tf_op jit(solution)/shard_map/ppermute | solution.py:82
  48.5 1.4 %collective-permute-start.6 = (f32[2,16,1024]{2,1,0:T(8,128)S(1)}, f32[2,16,1024]{2,1,0:T(8,128)S(1)}, u32[]{:S(2)}, u32[]{:S(2)}) collective-permute-start(f32[2,16,1024]{2,1,0:T(8,128)S(1)} %dynamic-slice_bitcast_fusion.3), channel_id=1, source_target_pairs={{0,4},{1,3},{2,6},{3,1},{4,0},{5,7},{6,2},{7,5},{8,12},{9,11},{10,... | collective-permute-start | bytes 393224 | tf_op jit(solution)/shard_map/ppermute | solution.py:82
  49.8 2.1 %collective-permute-done.13 = f32[2,2,16,1024]{3,2,1,0:T(8,128)S(1)} collective-permute-done((f32[2,2,16,1024]{3,2,1,0:T(8,128)S(1)}, f32[2,2,16,1024]{3,2,1,0:T(8,128)S(1)}, u32[]{:S(2)}, u32[]{:S(2)}) %collective-permute-start.13) | collective-permute-done | bytes 262176 | tf_op jit(solution)/shard_map/ppermute | solution.py:82
  52.0 1.4 %collective-permute-start.14 = (f32[2,16,1024]{2,1,0:T(8,128)S(1)}, f32[2,16,1024]{2,1,0:T(8,128)S(1)}, u32[]{:S(2)}, u32[]{:S(2)}) collective-permute-start(f32[2,16,1024]{2,1,0:T(8,128)S(1)} %dynamic-slice_bitcast_fusion.2), channel_id=1, source_target_pairs={{0,4},{1,3},{2,6},{3,1},{4,0},{5,7},{6,2},{7,5},{8,12},{9,11},{10,... | collective-permute-start | bytes 393224 | tf_op jit(solution)/shard_map/ppermute | solution.py:82
  53.4 0.1 collective-permute-done.6
  53.5 2.9 %collective-permute-start.7 = (f32[16,1024]{1,0:T(8,128)S(1)}, f32[16,1024]{1,0:T(8,128)S(1)}, u32[]{:S(2)}, u32[]{:S(2)}) collective-permute-start(f32[16,1024]{1,0:T(8,128)S(1)} %dynamic-slice_bitcast_fusion.5), channel_id=1, source_target_pairs={{0,8},{1,9},{2,10},{3,11},{4,12},{5,13},{6,14},{7,15},{8,0},{9,1},... | collective-permute-start | bytes 196616 | tf_op jit(solution)/shard_map/ppermute | solution.py:82
  56.4 1.3 %collective-permute-done.14 = f32[2,16,1024]{2,1,0:T(8,128)S(1)} collective-permute-done((f32[2,16,1024]{2,1,0:T(8,128)S(1)}, f32[2,16,1024]{2,1,0:T(8,128)S(1)}, u32[]{:S(2)}, u32[]{:S(2)}) %collective-permute-start.14) | collective-permute-done | bytes 131104 | tf_op jit(solution)/shard_map/ppermute | solution.py:82
  57.7 2.2 %collective-permute-start.15 = (f32[16,1024]{1,0:T(8,128)S(1)}, f32[16,1024]{1,0:T(8,128)S(1)}, u32[]{:S(2)}, u32[]{:S(2)}) collective-permute-start(f32[16,1024]{1,0:T(8,128)S(1)} %dynamic-slice_bitcast_fusion.4), channel_id=1, source_target_pairs={{0,8},{1,9},{2,10},{3,11},{4,12},{5,13},{6,14},{7,15},{8,0},{9,1},... | collective-permute-start | bytes 196616 | tf_op jit(solution)/shard_map/ppermute | solution.py:82
  59.9 3.7 %collective-permute-done.15 = f32[16,1024]{1,0:T(8,128)S(1)} collective-permute-done((f32[16,1024]{1,0:T(8,128)S(1)}, f32[16,1024]{1,0:T(8,128)S(1)}, u32[]{:S(2)}, u32[]{:S(2)}) %collective-permute-start.15) | collective-permute-done | bytes 65568 | tf_op jit(solution)/shard_map/ppermute | solution.py:82
  63.7 0.1 fusion.11
  63.9 1.6 %collective-permute-start.16 = (bf16[1,16,2048]{2,1,0:T(8,128)(2,1)S(1)}, bf16[1,16,2048]{2,1,0:T(8,128)(2,1)S(1)}, u32[]{:S(2)}, u32[]{:S(2)}) collective-permute-start(bf16[1,16,2048]{2,1,0:T(8,128)(2,1)S(1)} %convert_element_type.36), channel_id=1, source_target_pairs={{0,8},{1,9},{2,10},{3,11},{4,12},{5,13},{6,14},{7,15},{8,0},{9,1},... | collective-permute-start | bytes 196616 | tf_op jit(solution)/shard_map/ppermute | solution.py:36
  65.5 4.4 %collective-permute-done.16 = bf16[1,16,2048]{2,1,0:T(8,128)(2,1)S(1)} collective-permute-done((bf16[1,16,2048]{2,1,0:T(8,128)(2,1)S(1)}, bf16[1,16,2048]{2,1,0:T(8,128)(2,1)S(1)}, u32[]{:S(2)}, u32[]{:S(2)}) %collective-permute-start.16) | collective-permute-done | bytes 65568 | tf_op jit(solution)/shard_map/ppermute | solution.py:36
  69.9 0.2 collective-permute-start.17
  70.0 6.3 %collective-permute-done.17 = bf16[2,16,2048]{2,1,0:T(8,128)(2,1)S(1)} collective-permute-done((bf16[2,16,2048]{2,1,0:T(8,128)(2,1)S(1)}, bf16[2,16,2048]{2,1,0:T(8,128)(2,1)S(1)}, u32[]{:S(2)}, u32[]{:S(2)}) %collective-permute-start.17) | collective-permute-done | bytes 131104 | tf_op jit(solution)/shard_map/ppermute | solution.py:36
  76.4 0.1 collective-permute-start.18
  76.4 6.4 %collective-permute-done.18 = bf16[4,16,2048]{2,1,0:T(8,128)(2,1)S(1)} collective-permute-done((bf16[4,16,2048]{2,1,0:T(8,128)(2,1)S(1)}, bf16[4,16,2048]{2,1,0:T(8,128)(2,1)S(1)}, u32[]{:S(2)}, u32[]{:S(2)}) %collective-permute-start.18) | collective-permute-done | bytes 262176 | tf_op jit(solution)/shard_map/ppermute | solution.py:36
  82.9 0.1 maximum_select_fusion
  83.0 0.1 collective-permute-start.19
  83.0 1.9 %collective-permute-done.19 = bf16[8,16,2048]{2,1,0:T(8,128)(2,1)S(1)} collective-permute-done((bf16[8,16,2048]{2,1,0:T(8,128)(2,1)S(1)}, bf16[8,16,2048]{2,1,0:T(8,128)(2,1)S(1)}, u32[]{:S(2)}, u32[]{:S(2)}) %collective-permute-start.19) | collective-permute-done | bytes 524320 | tf_op jit(solution)/shard_map/ppermute | solution.py:36
  84.9 0.1 broadcast_select_fusion.1
  85.0 1.1 pad_maximum_fusion
  86.1 9.7 %shard_map.57 = f32[256,2048]{1,0:T(8,128)} custom-call(bf16[4,256,256]{2,1,0:T(8,128)(2,1)} %occ_ref.5, bf16[256,2048]{1,0:T(8,128)(2,1)} %bitcast.197, bf16[4,1024,1024]{2,1,0:T(8,128)(2,1)} %vir_ref.5), custom_call_target="tpu_custom_call" | custom-call | tf_op jit(solution)/shard_map/pallas_call | solution.py:107
  95.8 1.7 %constant_dynamic-slice_fusion.3 = (f32[2,2,2,1,16,2048]{5,4,3,2,1,0:T(8,128)S(1)}, f32[2,2,2,1,16,2048]{5,4,3,2,1,0:T(8,128)S(1)}) fusion(f32[2,2,2,2,16,2048]{5,4,3,2,1,0:T(8,128)} %bitcast.194, s32[]{:T(128)S(6)} %select_n.300, s32[]{:T(128)S(6)} %select_n.301), kind=kLoop, calls=%fused_computation.91 | loop fusion | bytes 4194312 | tf_op jit(solution)/shard_map/jit(dynamic_index_in_dim)/dynamic_slice | solution.py:69
  97.5 0.1 copy.90
  97.6 0.2 collective-permute-start.20
  97.8 2.5 %collective-permute-done.20 = f32[2,2,2,16,2048]{4,3,2,0,1:T(8,128)S(1)} collective-permute-done((f32[2,2,2,16,2048]{4,3,2,0,1:T(8,128)S(1)}, f32[2,2,2,16,2048]{4,3,2,0,1:T(8,128)S(1)}, u32[]{:S(2)}, u32[]{:S(2)}) %collective-permute-start.20) | collective-permute-done | bytes 1048608 | tf_op jit(solution)/shard_map/ppermute | solution.py:82
  100.4 0.2 bitcast_add_fusion
  100.5 0.1 constant_dynamic-slice_fusion.1
  100.7 0.1 collective-permute-start.21
  100.8 9.2 %collective-permute-done.21 = f32[2,2,16,2048]{3,2,1,0:T(8,128)S(1)} collective-permute-done((f32[2,2,16,2048]{3,2,1,0:T(8,128)S(1)}, f32[2,2,16,2048]{3,2,1,0:T(8,128)S(1)}, u32[]{:S(2)}, u32[]{:S(2)}) %collective-permute-start.21) | collective-permute-done | bytes 524320 | tf_op jit(solution)/shard_map/ppermute | solution.py:82
  109.9 0.1 fusion
  110.0 0.1 collective-permute-start.22
  110.2 6.3 %collective-permute-done.22 = f32[2,16,2048]{2,1,0:T(8,128)S(1)} collective-permute-done((f32[2,16,2048]{2,1,0:T(8,128)S(1)}, f32[2,16,2048]{2,1,0:T(8,128)S(1)}, u32[]{:S(2)}, u32[]{:S(2)}) %collective-permute-start.22) | collective-permute-done | bytes 262176 | tf_op jit(solution)/shard_map/ppermute | solution.py:82
  116.5 1.0 collective-permute-start.23
  117.6 6.4 %collective-permute-done.23 = f32[16,2048]{1,0:T(8,128)S(1)} collective-permute-done((f32[16,2048]{1,0:T(8,128)S(1)}, f32[16,2048]{1,0:T(8,128)S(1)}, u32[]{:S(2)}, u32[]{:S(2)}) %collective-permute-start.23) | collective-permute-done | bytes 131104 | tf_op jit(solution)/shard_map/ppermute | solution.py:82
  123.9 0.1 fusion.5
  124.0 0.8 copy.74
  (55 shorter events, 1.5 us)
Async XLA Ops:
  2.5 6.3 %collective-permute-start = (bf16[1,16,1024]{2,1,0:T(8,128)(2,1)S(1)}, bf16[1,16,1024]{2,1,0:T(8,128)(2,1)S(1)}, u32[]{:S(2)}, u32[]{:S(2)}) collective-permute-start(bf16[1,16,1024]{2,1,0:T(8,128)(2,1)S(1)} %get-tuple-element.33), channel_id=1, source_target_pairs={{0,8},{1,9},{2,10},{3,11},{4,12},{5,13},{6,14},{7,15},{8,0},{9,1},... | collective-permute-start | bytes 98312 | tf_op jit(solution)/shard_map/ppermute | solution.py:36
  6.6 4.8 %collective-permute-start.8 = (bf16[1,16,1024]{2,1,0:T(8,128)(2,1)S(1)}, bf16[1,16,1024]{2,1,0:T(8,128)(2,1)S(1)}, u32[]{:S(2)}, u32[]{:S(2)}) collective-permute-start(bf16[1,16,1024]{2,1,0:T(8,128)(2,1)S(1)} %get-tuple-element.34), channel_id=1, source_target_pairs={{0,8},{1,9},{2,10},{3,11},{4,12},{5,13},{6,14},{7,15},{8,0},{9,1},... | collective-permute-start | bytes 98312 | tf_op jit(solution)/shard_map/ppermute | solution.py:36
  8.9 4.3 %collective-permute-start.1 = (bf16[2,16,1024]{2,1,0:T(8,128)(2,1)S(1)}, bf16[2,16,1024]{2,1,0:T(8,128)(2,1)S(1)}, u32[]{:S(2)}, u32[]{:S(2)}) collective-permute-start(bf16[2,16,1024]{2,1,0:T(8,128)(2,1)S(1)} %pad_maximum_fusion.8), channel_id=1, source_target_pairs={{0,4},{1,3},{2,6},{3,1},{4,0},{5,7},{6,2},{7,5},{8,12},{9,11},{10,... | collective-permute-start | bytes 196616 | tf_op jit(solution)/shard_map/ppermute | solution.py:36
  11.4 4.8 %collective-permute-start.9 = (bf16[2,16,1024]{2,1,0:T(8,128)(2,1)S(1)}, bf16[2,16,1024]{2,1,0:T(8,128)(2,1)S(1)}, u32[]{:S(2)}, u32[]{:S(2)}) collective-permute-start(bf16[2,16,1024]{2,1,0:T(8,128)(2,1)S(1)} %pad_maximum_fusion.9), channel_id=1, source_target_pairs={{0,4},{1,3},{2,6},{3,1},{4,0},{5,7},{6,2},{7,5},{8,12},{9,11},{10,... | collective-permute-start | bytes 196616 | tf_op jit(solution)/shard_map/ppermute | solution.py:36
  13.2 5.0 %collective-permute-start.2 = (bf16[4,16,1024]{2,1,0:T(8,128)(2,1)S(1)}, bf16[4,16,1024]{2,1,0:T(8,128)(2,1)S(1)}, u32[]{:S(2)}, u32[]{:S(2)}) collective-permute-start(bf16[4,16,1024]{2,1,0:T(8,128)(2,1)S(1)} %bitcast.223), channel_id=1, source_target_pairs={{0,2},{1,5},{2,0},{3,7},{4,6},{5,1},{6,4},{7,3},{8,10},{9,13},{10,... | collective-permute-start | bytes 393224 | tf_op jit(solution)/shard_map/ppermute | solution.py:36
  16.3 5.0 %collective-permute-start.10 = (bf16[4,16,1024]{2,1,0:T(8,128)(2,1)S(1)}, bf16[4,16,1024]{2,1,0:T(8,128)(2,1)S(1)}, u32[]{:S(2)}, u32[]{:S(2)}) collective-permute-start(bf16[4,16,1024]{2,1,0:T(8,128)(2,1)S(1)} %bitcast.224), channel_id=1, source_target_pairs={{0,2},{1,5},{2,0},{3,7},{4,6},{5,1},{6,4},{7,3},{8,10},{9,13},{10,... | collective-permute-start | bytes 393224 | tf_op jit(solution)/shard_map/ppermute | solution.py:36
  18.4 3.1 %collective-permute-start.3 = (bf16[8,16,1024]{2,1,0:T(8,128)(2,1)S(1)}, bf16[8,16,1024]{2,1,0:T(8,128)(2,1)S(1)}, u32[]{:S(2)}, u32[]{:S(2)}) collective-permute-start(bf16[8,16,1024]{2,1,0:T(8,128)(2,1)S(1)} %bitcast.217), channel_id=1, source_target_pairs={{0,1},{1,0},{2,3},{3,2},{4,5},{5,4},{6,7},{7,6},{8,9},{9,8},{10,11... | collective-permute-start | bytes 786440 | tf_op jit(solution)/shard_map/ppermute | solution.py:36
  21.4 1.6 %collective-permute-start.11 = (bf16[8,16,1024]{2,1,0:T(8,128)(2,1)S(1)}, bf16[8,16,1024]{2,1,0:T(8,128)(2,1)S(1)}, u32[]{:S(2)}, u32[]{:S(2)}) collective-permute-start(bf16[8,16,1024]{2,1,0:T(8,128)(2,1)S(1)} %bitcast.218), channel_id=1, source_target_pairs={{0,1},{1,0},{2,3},{3,2},{4,5},{5,4},{6,7},{7,6},{8,9},{9,8},{10,11... | collective-permute-start | bytes 786440 | tf_op jit(solution)/shard_map/ppermute | solution.py:36
  31.1 7.3 %copy-start = (f32[256,1024]{1,0:T(8,128)S(1)}, f32[256,1024]{1,0:T(8,128)}, u32[]{:S(2)}) copy-start(f32[256,1024]{1,0:T(8,128)} %shard_map.56) | copy-start | bytes 3145732
  39.8 2.0 %collective-permute-start.4 = (f32[2,2,2,16,1024]{4,3,2,0,1:T(8,128)S(1)}, f32[2,2,2,16,1024]{4,3,2,0,1:T(8,128)S(1)}, u32[]{:S(2)}, u32[]{:S(2)}) collective-permute-start(f32[2,2,2,16,1024]{4,3,2,0,1:T(8,128)S(1)} %bitcast.225), channel_id=1, source_target_pairs={{0,1},{1,0},{2,3},{3,2},{4,5},{5,4},{6,7},{7,6},{8,9},{9,8},{10,11... | collective-permute-start | bytes 1572872 | tf_op jit(solution)/shard_map/ppermute | solution.py:82
  40.1 3.0 %collective-permute-start.12 = (f32[2,2,2,16,1024]{4,3,2,0,1:T(8,128)S(1)}, f32[2,2,2,16,1024]{4,3,2,0,1:T(8,128)S(1)}, u32[]{:S(2)}, u32[]{:S(2)}) collective-permute-start(f32[2,2,2,16,1024]{4,3,2,0,1:T(8,128)S(1)} %bitcast.226), channel_id=1, source_target_pairs={{0,1},{1,0},{2,3},{3,2},{4,5},{5,4},{6,7},{7,6},{8,9},{9,8},{10,11... | collective-permute-start | bytes 1572872 | tf_op jit(solution)/shard_map/ppermute | solution.py:82
  41.9 6.4 %collective-permute-start.5 = (f32[2,2,16,1024]{3,2,1,0:T(8,128)S(1)}, f32[2,2,16,1024]{3,2,1,0:T(8,128)S(1)}, u32[]{:S(2)}, u32[]{:S(2)}) collective-permute-start(f32[2,2,16,1024]{3,2,1,0:T(8,128)S(1)} %bitcast_select_fusion.4), channel_id=1, source_target_pairs={{0,2},{1,5},{2,0},{3,7},{4,6},{5,1},{6,4},{7,3},{8,10},{9,13},{10,... | collective-permute-start | bytes 786440 | tf_op jit(solution)/shard_map/ppermute | solution.py:82
  43.2 20.5 %copy-start.2 = (f32[1024]{0:T(1024)S(1)}, f32[1024]{0:T(1024)}, u32[]{:S(2)}) copy-start(f32[1024]{0:T(1024)} %param.7) | copy-start | bytes 12292
  43.2 8.7 %collective-permute-start.13 = (f32[2,2,16,1024]{3,2,1,0:T(8,128)S(1)}, f32[2,2,16,1024]{3,2,1,0:T(8,128)S(1)}, u32[]{:S(2)}, u32[]{:S(2)}) collective-permute-start(f32[2,2,16,1024]{3,2,1,0:T(8,128)S(1)} %bitcast_select_fusion.2), channel_id=1, source_target_pairs={{0,2},{1,5},{2,0},{3,7},{4,6},{5,1},{6,4},{7,3},{8,10},{9,13},{10,... | collective-permute-start | bytes 786440 | tf_op jit(solution)/shard_map/ppermute | solution.py:82
  48.5 5.0 %collective-permute-start.6 = (f32[2,16,1024]{2,1,0:T(8,128)S(1)}, f32[2,16,1024]{2,1,0:T(8,128)S(1)}, u32[]{:S(2)}, u32[]{:S(2)}) collective-permute-start(f32[2,16,1024]{2,1,0:T(8,128)S(1)} %dynamic-slice_bitcast_fusion.3), channel_id=1, source_target_pairs={{0,4},{1,3},{2,6},{3,1},{4,0},{5,7},{6,2},{7,5},{8,12},{9,11},{10,... | collective-permute-start | bytes 393224 | tf_op jit(solution)/shard_map/ppermute | solution.py:82
  52.0 5.7 %collective-permute-start.14 = (f32[2,16,1024]{2,1,0:T(8,128)S(1)}, f32[2,16,1024]{2,1,0:T(8,128)S(1)}, u32[]{:S(2)}, u32[]{:S(2)}) collective-permute-start(f32[2,16,1024]{2,1,0:T(8,128)S(1)} %dynamic-slice_bitcast_fusion.2), channel_id=1, source_target_pairs={{0,4},{1,3},{2,6},{3,1},{4,0},{5,7},{6,2},{7,5},{8,12},{9,11},{10,... | collective-permute-start | bytes 393224 | tf_op jit(solution)/shard_map/ppermute | solution.py:82
  53.5 6.4 %collective-permute-start.7 = (f32[16,1024]{1,0:T(8,128)S(1)}, f32[16,1024]{1,0:T(8,128)S(1)}, u32[]{:S(2)}, u32[]{:S(2)}) collective-permute-start(f32[16,1024]{1,0:T(8,128)S(1)} %dynamic-slice_bitcast_fusion.5), channel_id=1, source_target_pairs={{0,8},{1,9},{2,10},{3,11},{4,12},{5,13},{6,14},{7,15},{8,0},{9,1},... | collective-permute-start | bytes 196616 | tf_op jit(solution)/shard_map/ppermute | solution.py:82
  57.7 5.9 %collective-permute-start.15 = (f32[16,1024]{1,0:T(8,128)S(1)}, f32[16,1024]{1,0:T(8,128)S(1)}, u32[]{:S(2)}, u32[]{:S(2)}) collective-permute-start(f32[16,1024]{1,0:T(8,128)S(1)} %dynamic-slice_bitcast_fusion.4), channel_id=1, source_target_pairs={{0,8},{1,9},{2,10},{3,11},{4,12},{5,13},{6,14},{7,15},{8,0},{9,1},... | collective-permute-start | bytes 196616 | tf_op jit(solution)/shard_map/ppermute | solution.py:82
  63.9 5.9 %collective-permute-start.16 = (bf16[1,16,2048]{2,1,0:T(8,128)(2,1)S(1)}, bf16[1,16,2048]{2,1,0:T(8,128)(2,1)S(1)}, u32[]{:S(2)}, u32[]{:S(2)}) collective-permute-start(bf16[1,16,2048]{2,1,0:T(8,128)(2,1)S(1)} %convert_element_type.36), channel_id=1, source_target_pairs={{0,8},{1,9},{2,10},{3,11},{4,12},{5,13},{6,14},{7,15},{8,0},{9,1},... | collective-permute-start | bytes 196616 | tf_op jit(solution)/shard_map/ppermute | solution.py:36
  69.9 6.4 %collective-permute-start.17 = (bf16[2,16,2048]{2,1,0:T(8,128)(2,1)S(1)}, bf16[2,16,2048]{2,1,0:T(8,128)(2,1)S(1)}, u32[]{:S(2)}, u32[]{:S(2)}) collective-permute-start(bf16[2,16,2048]{2,1,0:T(8,128)(2,1)S(1)} %pad_maximum_fusion.7), channel_id=1, source_target_pairs={{0,4},{1,3},{2,6},{3,1},{4,0},{5,7},{6,2},{7,5},{8,12},{9,11},{10,... | collective-permute-start | bytes 393224 | tf_op jit(solution)/shard_map/ppermute | solution.py:36
  76.4 6.4 %collective-permute-start.18 = (bf16[4,16,2048]{2,1,0:T(8,128)(2,1)S(1)}, bf16[4,16,2048]{2,1,0:T(8,128)(2,1)S(1)}, u32[]{:S(2)}, u32[]{:S(2)}) collective-permute-start(bf16[4,16,2048]{2,1,0:T(8,128)(2,1)S(1)} %bitcast.216), channel_id=1, source_target_pairs={{0,2},{1,5},{2,0},{3,7},{4,6},{5,1},{6,4},{7,3},{8,10},{9,13},{10,... | collective-permute-start | bytes 786440 | tf_op jit(solution)/shard_map/ppermute | solution.py:36
  83.0 2.0 %collective-permute-start.19 = (bf16[8,16,2048]{2,1,0:T(8,128)(2,1)S(1)}, bf16[8,16,2048]{2,1,0:T(8,128)(2,1)S(1)}, u32[]{:S(2)}, u32[]{:S(2)}) collective-permute-start(bf16[8,16,2048]{2,1,0:T(8,128)(2,1)S(1)} %bitcast.203), channel_id=1, source_target_pairs={{0,1},{1,0},{2,3},{3,2},{4,5},{5,4},{6,7},{7,6},{8,9},{9,8},{10,11... | collective-permute-start | bytes 1572872 | tf_op jit(solution)/shard_map/ppermute | solution.py:36
  97.6 2.7 %collective-permute-start.20 = (f32[2,2,2,16,2048]{4,3,2,0,1:T(8,128)S(1)}, f32[2,2,2,16,2048]{4,3,2,0,1:T(8,128)S(1)}, u32[]{:S(2)}, u32[]{:S(2)}) collective-permute-start(f32[2,2,2,16,2048]{4,3,2,0,1:T(8,128)S(1)} %bitcast.215), channel_id=1, source_target_pairs={{0,1},{1,0},{2,3},{3,2},{4,5},{5,4},{6,7},{7,6},{8,9},{9,8},{10,11... | collective-permute-start | bytes 3145736 | tf_op jit(solution)/shard_map/ppermute | solution.py:82
  100.7 23.3 %copy-start.1 = (f32[16,2,1024]{2,1,0:T(2,128)S(1)}, f32[16,2,1024]{2,1,0:T(2,128)}, u32[]{:S(2)}) copy-start(f32[16,2,1024]{2,1,0:T(2,128)} %param.5) | copy-start | bytes 393220
  100.7 9.2 %collective-permute-start.21 = (f32[2,2,16,2048]{3,2,1,0:T(8,128)S(1)}, f32[2,2,16,2048]{3,2,1,0:T(8,128)S(1)}, u32[]{:S(2)}, u32[]{:S(2)}) collective-permute-start(f32[2,2,16,2048]{3,2,1,0:T(8,128)S(1)} %bitcast_select_fusion), channel_id=1, source_target_pairs={{0,2},{1,5},{2,0},{3,7},{4,6},{5,1},{6,4},{7,3},{8,10},{9,13},{10,... | collective-permute-start | bytes 1572872 | tf_op jit(solution)/shard_map/ppermute | solution.py:82
  110.0 6.4 %collective-permute-start.22 = (f32[2,16,2048]{2,1,0:T(8,128)S(1)}, f32[2,16,2048]{2,1,0:T(8,128)S(1)}, u32[]{:S(2)}, u32[]{:S(2)}) collective-permute-start(f32[2,16,2048]{2,1,0:T(8,128)S(1)} %dynamic-slice_bitcast_fusion), channel_id=1, source_target_pairs={{0,4},{1,3},{2,6},{3,1},{4,0},{5,7},{6,2},{7,5},{8,12},{9,11},{10,... | collective-permute-start | bytes 786440 | tf_op jit(solution)/shard_map/ppermute | solution.py:82
  116.5 7.4 %collective-permute-start.23 = (f32[16,2048]{1,0:T(8,128)S(1)}, f32[16,2048]{1,0:T(8,128)S(1)}, u32[]{:S(2)}, u32[]{:S(2)}) collective-permute-start(f32[16,2048]{1,0:T(8,128)S(1)} %dynamic-slice_bitcast_fusion.1), channel_id=1, source_target_pairs={{0,8},{1,9},{2,10},{3,11},{4,12},{5,13},{6,14},{7,15},{8,0},{9,1},... | collective-permute-start | bytes 393224 | tf_op jit(solution)/shard_map/ppermute | solution.py:82

commit v7 on v4

--- a/solution.py
+++ b/solution.py
@@ -52,58 +52,64 @@
     return acc.reshape((n * x.shape[0],) + x.shape[1:])
 
 
-def scatter_sum(part, n):
+def scatter_sum(keep, send, n):
     m = n.bit_length() - 1
     me = lax.axis_index("aux")
     odd = (me & 1) == 1
-    rows = part.shape[0] // n
+    rows = 2 * keep.shape[0] // n
     order0, order1 = bit_orders(m, False)
-    acc = part.reshape((2,) * m + (rows,) + part.shape[1:])
-    axes0 = list(range(m - 1, -1, -1))
+    shape = (2,) * (m - 1) + (rows,) + keep.shape[1:]
+    acc = keep.reshape(shape) + lax.ppermute(send, "aux", partners(n, 0, 0)).reshape(shape)
+    axes0 = list(range(m - 1, 0, -1))
     axes1 = list(axes0)
-    for b0, b1 in zip(order0, order1):
+    for b0, b1 in zip(order0[1:], order1[1:]):
         at0, at1 = axes0.index(b0), axes1.index(b1)
         bit0, bit1 = (me >> b0) & 1, (me >> b1) & 1
         if at0 == at1:
             bit = jnp.where(odd, bit1, bit0)
-            keep = lax.dynamic_index_in_dim(acc, bit, axis=at0, keepdims=False)
-            send = lax.dynamic_index_in_dim(acc, 1 - bit, axis=at0, keepdims=False)
+            kept = lax.dynamic_index_in_dim(acc, bit, axis=at0, keepdims=False)
+            sent = lax.dynamic_index_in_dim(acc, 1 - bit, axis=at0, keepdims=False)
         else:
-            keep = jnp.where(
+            kept = jnp.where(
                 odd,
                 lax.dynamic_index_in_dim(acc, bit1, axis=at1, keepdims=False),
                 lax.dynamic_index_in_dim(acc, bit0, axis=at0, keepdims=False),
             )
-            send = jnp.where(
+            sent = jnp.where(
                 odd,
                 lax.dynamic_index_in_dim(acc, 1 - bit1, axis=at1, keepdims=False),
                 lax.dynamic_index_in_dim(acc, 1 - bit0, axis=at0, keepdims=False),
             )
-        acc = keep + lax.ppermute(send, "aux", partners(n, b0, b1))
+        acc = kept + lax.ppermute(sent, "aux", partners(n, b0, b1))
         axes0.pop(at0)
         axes1.pop(at1)
     return acc
 
 
-def exchange_kernel(states, occ_ref, r_ref, vir_ref, out_ref):
+def exchange_kernel(states, occ_ref, r_ref, vir_ref, keep_ref, send_ref):
     @pl.when(pl.program_id(0) == 0)
     def _():
-        out_ref[...] = jnp.zeros_like(out_ref)
+        keep_ref[...] = jnp.zeros_like(keep_ref)
+        send_ref[...] = jnp.zeros_like(send_ref)
 
     half = jnp.dot(occ_ref[0], r_ref[...], preferred_element_type=jnp.float32).astype(jnp.bfloat16)
     nvir = vir_ref.shape[1]
+    split = keep_ref.shape[0]
     vir = vir_ref[0]
     for s in range(states):
         cols = slice(s * nvir, (s + 1) * nvir)
-        out_ref[:, cols] += lax.dot_general(
+        term = lax.dot_general(
             half[:, cols], vir, (((1,), (1,)), ((), ())), preferred_element_type=jnp.float32
         )
+        keep_ref[:, cols] += term[:split]
+        send_ref[:, cols] += term[split:]
 
 
 def exchange_part(occ_ints, flat, vir_ints, states):
     local_aux, nocc, _ = occ_ints.shape
     nvir = vir_ints.shape[1]
     width = states * nvir
+    out = jax.ShapeDtypeStruct((nocc // 2, width), jnp.float32)
     return pl.pallas_call(
         functools.partial(exchange_kernel, states),
         grid=(local_aux,),
@@ -112,10 +118,22 @@
             pl.BlockSpec((nocc, width), lambda p: (0, 0)),
             pl.BlockSpec((1, nvir, nvir), lambda p: (p, 0, 0)),
         ],
-        out_specs=pl.BlockSpec((nocc, width), lambda p: (0, 0)),
-        out_shape=jax.ShapeDtypeStruct((nocc, width), jnp.float32),
+        out_specs=[
+            pl.BlockSpec((nocc // 2, width), lambda p: (0, 0)),
+            pl.BlockSpec((nocc // 2, width), lambda p: (0, 0)),
+        ],
+        out_shape=[out, out],
         compiler_params=pltpu.CompilerParams(dimension_semantics=("arbitrary",)),
     )(occ_ints, flat, vir_ints)
+
+
+def order_rows(occ_ints, n, core):
+    local_aux, nocc, _ = occ_ints.shape
+    o = occ_ints.reshape(local_aux, n // 2, 2, nocc // n, nocc)
+    even, odd = o[:, :, 0], o[:, :, 1]
+    mine = core == 0
+    o = jnp.stack([jnp.where(mine, even, odd), jnp.where(mine, odd, even)], axis=1)
+    return o.reshape(local_aux, nocc, nocc)
 
 
 def shards(rhs, occ_energy, vir_energy, occ_ints, vir_ints):
@@ -128,6 +146,7 @@
     position = lax.axis_index("aux")
     my_occ = lax.dynamic_slice_in_dim(occ_energy, position * own_rows, own_rows, 0)
     denom = vir_energy[None, None, :] - my_occ[:, None, None]
+    ordered_occ = order_rows(occ_ints, n, position & 1)
     finals = []
     for state in range(states):
         own_rhs = rhs[:, state, :]
@@ -136,8 +155,8 @@
         for step in range(ITERS):
             rounded = resp.astype(jnp.bfloat16)
             flat = gather_rows(rounded, n)
-            part = exchange_part(occ_ints, flat, vir_ints, 1)
-            exchange = scatter_sum(part, n)
+            keep, send = exchange_part(ordered_occ, flat, vir_ints, 1)
+            exchange = scatter_sum(keep, send, n)
             resp = 0.4 * resp + 0.6 * (own_rhs - exchange) / own_denom
         finals.append(resp)
     response = jnp.stack(finals, axis=1)

time: 122 us -> 117 us (0.959)
  waiting for transfers between devices: 41.2 us -> 36 us
  local copies, waits for them, and re-layouts: 7.09 us -> 2.78 us
  other arithmetic: 5.71 us -> 9.74 us
  starting transfers between devices: 38.1 us -> 39.4 us
    dynamic_slice x11 -> x0, local copies, waits for them, and re-layouts: 4.32 us -> none  [the longest x3 3.98 us: scatter_sum(): keep = lax.dynamic_index_in_dim(acc, bit, axis=at0, keepdims=False)]
    ppermute x16, waiting for transfers between devices: 23.7 us -> 20.6 us  [the longest x12 19.6 us: scatter_sum(): acc = kept + lax.ppermute(sent, 'aux', partners(n, b0, b1))]
    ppermute x16, waiting for transfers between devices: 17.5 us -> 15.3 us  [gather_rows(): theirs = lax.ppermute(acc, 'aux', partners(n, b0, b1))]
    add x12, other arithmetic: 0.52 us -> 2.58 us  [the longest x4 2.34 us: scatter_sum(): keep.reshape(shape)]
  transfers between devices with their start and end apart: 32 -> 32, of which waited for: 26 -> 24; matrix products, arithmetic and copies ran while one was open for 6% -> 8% of each run, Pallas kernels for 18% -> 24%
where the time goes in v7:
time: 117 us
  starting transfers between devices  39.4 us (34%)
  waiting for transfers between devices  36 us (31%)
  Pallas kernels  28.6 us (24%)
  other arithmetic  9.74 us (8%)
  local copies, waits for them, and re-layouts  2.78 us (2%)
    pallas_call x4, Pallas kernels, exchange_part(): pl.pallas_call(functools.partial(exchange_kernel, states), grid=(local_au...  28.6 us
    ppermute x12, waiting for transfers between devices, scatter_sum(): acc = kept + lax.ppermute(sent, 'aux', partners(n, b0, b1))  19.6 us
    ppermute x12, starting transfers between devices, scatter_sum(): acc = kept + lax.ppermute(sent, 'aux', partners(n, b0, b1))  19.5 us
    ppermute x16, starting transfers between devices, gather_rows(): theirs = lax.ppermute(acc, 'aux', partners(n, b0, b1))  18.9 us
    ppermute x16, waiting for transfers between devices, gather_rows(): theirs = lax.ppermute(acc, 'aux', partners(n, b0, b1))  15.3 us
    another operation x16, other arithmetic, gather_rows(): new0 = jnp.stack([lo, hi], axis=at0)  3.54 us
  transfers between devices with their start and end apart: 32, of which 24 were waited for; matrix products, arithmetic and copies ran while one was open for 8% of the time, Pallas kernels for 24%

profile of v7, /device:TPU:0, one launch (start us, length us, event | category | flops | bytes accessed | tf_op | source)
XLA Modules:
  0.0 116.9 jit_solution(14234572098468285167)
XLA Ops:
  0.0 1.1 fusion.24
  1.1 0.8 dynamic_slice.103
  1.9 0.8 fusion.4
  2.6 4.1 %collective-permute-start.16 = (bf16[1,16,1024]{2,1,0:T(8,128)(2,1)S(1)}, bf16[1,16,1024]{2,1,0:T(8,128)(2,1)S(1)}, u32[]{:S(2)}, u32[]{:S(2)}) collective-permute-start(bf16[1,16,1024]{2,1,0:T(8,128)(2,1)S(1)} %get-tuple-element.66), channel_id=1, source_target_pairs={{0,8},{1,9},{2,10},{3,11},{4,12},{5,13},{6,14},{7,15},{8,0},{9,1},... | collective-permute-start | bytes 98312 | tf_op jit(solution)/shard_map/ppermute | solution.py:36
  6.8 1.1 select_bitcast_fusion.1
  7.9 0.9 pad_maximum_fusion
  8.7 0.2 collective-permute-done.16
  9.0 1.7 %collective-permute-start.17 = (bf16[2,16,1024]{2,1,0:T(8,128)(2,1)S(1)}, bf16[2,16,1024]{2,1,0:T(8,128)(2,1)S(1)}, u32[]{:S(2)}, u32[]{:S(2)}) collective-permute-start(bf16[2,16,1024]{2,1,0:T(8,128)(2,1)S(1)} %pad_maximum_fusion.12), channel_id=1, source_target_pairs={{0,4},{1,3},{2,6},{3,1},{4,0},{5,7},{6,2},{7,5},{8,12},{9,11},{10,... | collective-permute-start | bytes 196616 | tf_op jit(solution)/shard_map/ppermute | solution.py:36
  10.7 0.9 collective-permute-done
  11.6 1.6 %collective-permute-start.1 = (bf16[2,16,1024]{2,1,0:T(8,128)(2,1)S(1)}, bf16[2,16,1024]{2,1,0:T(8,128)(2,1)S(1)}, u32[]{:S(2)}, u32[]{:S(2)}) collective-permute-start(bf16[2,16,1024]{2,1,0:T(8,128)(2,1)S(1)} %pad_maximum_fusion.10), channel_id=1, source_target_pairs={{0,4},{1,3},{2,6},{3,1},{4,0},{5,7},{6,2},{7,5},{8,12},{9,11},{10,... | collective-permute-start | bytes 196616 | tf_op jit(solution)/shard_map/ppermute | solution.py:36
  13.2 0.1 collective-permute-done.17
  13.4 1.8 %collective-permute-start.18 = (bf16[4,16,1024]{2,1,0:T(8,128)(2,1)S(1)}, bf16[4,16,1024]{2,1,0:T(8,128)(2,1)S(1)}, u32[]{:S(2)}, u32[]{:S(2)}) collective-permute-start(bf16[4,16,1024]{2,1,0:T(8,128)(2,1)S(1)} %bitcast.305), channel_id=1, source_target_pairs={{0,2},{1,5},{2,0},{3,7},{4,6},{5,1},{6,4},{7,3},{8,10},{9,13},{10,... | collective-permute-start | bytes 393224 | tf_op jit(solution)/shard_map/ppermute | solution.py:36
  15.2 1.4 %collective-permute-done.1 = bf16[2,16,1024]{2,1,0:T(8,128)(2,1)S(1)} collective-permute-done((bf16[2,16,1024]{2,1,0:T(8,128)(2,1)S(1)}, bf16[2,16,1024]{2,1,0:T(8,128)(2,1)S(1)}, u32[]{:S(2)}, u32[]{:S(2)}) %collective-permute-start.1) | collective-permute-done | bytes 65568 | tf_op jit(solution)/shard_map/ppermute | solution.py:36
  16.6 1.6 %collective-permute-start.2 = (bf16[4,16,1024]{2,1,0:T(8,128)(2,1)S(1)}, bf16[4,16,1024]{2,1,0:T(8,128)(2,1)S(1)}, u32[]{:S(2)}, u32[]{:S(2)}) collective-permute-start(bf16[4,16,1024]{2,1,0:T(8,128)(2,1)S(1)} %bitcast.306), channel_id=1, source_target_pairs={{0,2},{1,5},{2,0},{3,7},{4,6},{5,1},{6,4},{7,3},{8,10},{9,13},{10,... | collective-permute-start | bytes 393224 | tf_op jit(solution)/shard_map/ppermute | solution.py:36
  18.2 0.3 collective-permute-done.18
  18.6 3.1 %collective-permute-done.2 = bf16[4,16,1024]{2,1,0:T(8,128)(2,1)S(1)} collective-permute-done((bf16[4,16,1024]{2,1,0:T(8,128)(2,1)S(1)}, bf16[4,16,1024]{2,1,0:T(8,128)(2,1)S(1)}, u32[]{:S(2)}, u32[]{:S(2)}) %collective-permute-start.2) | collective-permute-done | bytes 131104 | tf_op jit(solution)/shard_map/ppermute | solution.py:36
  21.9 0.8 pad_maximum_fusion.3
  22.7 7.1 %shard_map.57 = (f32[128,1024]{1,0:T(8,128)}, f32[128,1024]{1,0:T(8,128)}) custom-call(bf16[4,256,256]{2,1,0:T(8,128)(2,1)} %bitcast.260, bf16[256,1024]{1,0:T(8,128)(2,1)} %bitcast.273, bf16[4,1024,1024]{2,1,0:T(8,128)(2,1)} %vir_ref.7), custom_call_target="tpu_custom_call" | custom-call | tf_op jit(solution)/shard_map/pallas_call | solution.py:113
  29.9 0.5 collective-permute-start.20
  30.4 0.8 pad_maximum_fusion.1
  31.3 7.2 %shard_map.55 = (f32[128,1024]{1,0:T(8,128)}, f32[128,1024]{1,0:T(8,128)}) custom-call(bf16[4,256,256]{2,1,0:T(8,128)(2,1)} %bitcast.261, bf16[256,1024]{1,0:T(8,128)(2,1)} %bitcast.274, bf16[4,1024,1024]{2,1,0:T(8,128)(2,1)} %vir_ref.7), custom_call_target="tpu_custom_call" | custom-call | tf_op jit(solution)/shard_map/pallas_call | solution.py:113
  38.6 1.6 %collective-permute-start.21 = (f32[2,2,16,1024]{3,2,1,0:T(8,128)S(1)}, f32[2,2,16,1024]{3,2,1,0:T(8,128)S(1)}, u32[]{:S(2)}, u32[]{:S(2)}) collective-permute-start(f32[2,2,16,1024]{3,2,1,0:T(8,128)S(1)} %bitcast_select_fusion.2), channel_id=1, source_target_pairs={{0,2},{1,5},{2,0},{3,7},{4,6},{5,1},{6,4},{7,3},{8,10},{9,13},{10,... | collective-permute-start | bytes 786440 | tf_op jit(solution)/shard_map/ppermute | solution.py:83
  40.1 0.4 collective-permute-done.4
  40.6 1.1 add.132
  41.7 1.6 %collective-permute-start.5 = (f32[2,2,16,1024]{3,2,1,0:T(8,128)S(1)}, f32[2,2,16,1024]{3,2,1,0:T(8,128)S(1)}, u32[]{:S(2)}, u32[]{:S(2)}) collective-permute-start(f32[2,2,16,1024]{3,2,1,0:T(8,128)S(1)} %bitcast_select_fusion.6), channel_id=1, source_target_pairs={{0,2},{1,5},{2,0},{3,7},{4,6},{5,1},{6,4},{7,3},{8,10},{9,13},{10,... | collective-permute-start | bytes 786440 | tf_op jit(solution)/shard_map/ppermute | solution.py:83
  43.3 1.8 %collective-permute-done.21 = f32[2,2,16,1024]{3,2,1,0:T(8,128)S(1)} collective-permute-done((f32[2,2,16,1024]{3,2,1,0:T(8,128)S(1)}, f32[2,2,16,1024]{3,2,1,0:T(8,128)S(1)}, u32[]{:S(2)}, u32[]{:S(2)}) %collective-permute-start.21) | collective-permute-done | bytes 262176 | tf_op jit(solution)/shard_map/ppermute | solution.py:83
  45.1 1.6 %collective-permute-start.22 = (f32[2,16,1024]{2,1,0:T(8,128)S(1)}, f32[2,16,1024]{2,1,0:T(8,128)S(1)}, u32[]{:S(2)}, u32[]{:S(2)}) collective-permute-start(f32[2,16,1024]{2,1,0:T(8,128)S(1)} %dynamic-slice_bitcast_fusion.1), channel_id=1, source_target_pairs={{0,4},{1,3},{2,6},{3,1},{4,0},{5,7},{6,2},{7,5},{8,12},{9,11},{10,... | collective-permute-start | bytes 393224 | tf_op jit(solution)/shard_map/ppermute | solution.py:83
  46.7 2.1 %collective-permute-done.5 = f32[2,2,16,1024]{3,2,1,0:T(8,128)S(1)} collective-permute-done((f32[2,2,16,1024]{3,2,1,0:T(8,128)S(1)}, f32[2,2,16,1024]{3,2,1,0:T(8,128)S(1)}, u32[]{:S(2)}, u32[]{:S(2)}) %collective-permute-start.5) | collective-permute-done | bytes 262176 | tf_op jit(solution)/shard_map/ppermute | solution.py:83
  48.9 1.6 %collective-permute-start.6 = (f32[2,16,1024]{2,1,0:T(8,128)S(1)}, f32[2,16,1024]{2,1,0:T(8,128)S(1)}, u32[]{:S(2)}, u32[]{:S(2)}) collective-permute-start(f32[2,16,1024]{2,1,0:T(8,128)S(1)} %dynamic-slice_bitcast_fusion.3), channel_id=1, source_target_pairs={{0,4},{1,3},{2,6},{3,1},{4,0},{5,7},{6,2},{7,5},{8,12},{9,11},{10,... | collective-permute-start | bytes 393224 | tf_op jit(solution)/shard_map/ppermute | solution.py:83
  50.6 2.2 %collective-permute-start.23 = (f32[16,1024]{1,0:T(8,128)S(1)}, f32[16,1024]{1,0:T(8,128)S(1)}, u32[]{:S(2)}, u32[]{:S(2)}) collective-permute-start(f32[16,1024]{1,0:T(8,128)S(1)} %dynamic-slice_bitcast_fusion.5), channel_id=1, source_target_pairs={{0,8},{1,9},{2,10},{3,11},{4,12},{5,13},{6,14},{7,15},{8,0},{9,1},... | collective-permute-start | bytes 196616 | tf_op jit(solution)/shard_map/ppermute | solution.py:83
  52.8 1.9 %collective-permute-done.6 = f32[2,16,1024]{2,1,0:T(8,128)S(1)} collective-permute-done((f32[2,16,1024]{2,1,0:T(8,128)S(1)}, f32[2,16,1024]{2,1,0:T(8,128)S(1)}, u32[]{:S(2)}, u32[]{:S(2)}) %collective-permute-start.6) | collective-permute-done | bytes 131104 | tf_op jit(solution)/shard_map/ppermute | solution.py:83
  54.7 2.6 %collective-permute-start.7 = (f32[16,1024]{1,0:T(8,128)S(1)}, f32[16,1024]{1,0:T(8,128)S(1)}, u32[]{:S(2)}, u32[]{:S(2)}) collective-permute-start(f32[16,1024]{1,0:T(8,128)S(1)} %dynamic-slice_bitcast_fusion.7), channel_id=1, source_target_pairs={{0,8},{1,9},{2,10},{3,11},{4,12},{5,13},{6,14},{7,15},{8,0},{9,1},... | collective-permute-start | bytes 196616 | tf_op jit(solution)/shard_map/ppermute | solution.py:83
  57.3 2.6 %collective-permute-done.7 = f32[16,1024]{1,0:T(8,128)S(1)} collective-permute-done((f32[16,1024]{1,0:T(8,128)S(1)}, f32[16,1024]{1,0:T(8,128)S(1)}, u32[]{:S(2)}, u32[]{:S(2)}) %collective-permute-start.7) | collective-permute-done | bytes 65568 | tf_op jit(solution)/shard_map/ppermute | solution.py:83
  60.0 3.0 %collective-permute-start.24 = (bf16[1,16,1024]{2,1,0:T(8,128)(2,1)S(1)}, bf16[1,16,1024]{2,1,0:T(8,128)(2,1)S(1)}, u32[]{:S(2)}, u32[]{:S(2)}) collective-permute-start(bf16[1,16,1024]{2,1,0:T(8,128)(2,1)S(1)} %get-tuple-element.63), channel_id=1, source_target_pairs={{0,8},{1,9},{2,10},{3,11},{4,12},{5,13},{6,14},{7,15},{8,0},{9,1},... | collective-permute-start | bytes 98312 | tf_op jit(solution)/shard_map/ppermute | solution.py:36
  63.2 1.8 %collective-permute-done.24 = bf16[1,16,1024]{2,1,0:T(8,128)(2,1)S(1)} collective-permute-done((bf16[1,16,1024]{2,1,0:T(8,128)(2,1)S(1)}, bf16[1,16,1024]{2,1,0:T(8,128)(2,1)S(1)}, u32[]{:S(2)}, u32[]{:S(2)}) %collective-permute-start.24) | collective-permute-done | bytes 32800 | tf_op jit(solution)/shard_map/ppermute | solution.py:36
  65.0 1.5 %collective-permute-start.25 = (bf16[2,16,1024]{2,1,0:T(8,128)(2,1)S(1)}, bf16[2,16,1024]{2,1,0:T(8,128)(2,1)S(1)}, u32[]{:S(2)}, u32[]{:S(2)}) collective-permute-start(bf16[2,16,1024]{2,1,0:T(8,128)(2,1)S(1)} %pad_maximum_fusion.13), channel_id=1, source_target_pairs={{0,4},{1,3},{2,6},{3,1},{4,0},{5,7},{6,2},{7,5},{8,12},{9,11},{10,... | collective-permute-start | bytes 196616 | tf_op jit(solution)/shard_map/ppermute | solution.py:36
  66.5 1.6 %collective-permute-done.8 = bf16[1,16,1024]{2,1,0:T(8,128)(2,1)S(1)} collective-permute-done((bf16[1,16,1024]{2,1,0:T(8,128)(2,1)S(1)}, bf16[1,16,1024]{2,1,0:T(8,128)(2,1)S(1)}, u32[]{:S(2)}, u32[]{:S(2)}) %collective-permute-start.8) | collective-permute-done | bytes 32800 | tf_op jit(solution)/shard_map/ppermute | solution.py:36
  68.1 0.3 collective-permute-start.9
  68.4 1.6 %collective-permute-done.25 = bf16[2,16,1024]{2,1,0:T(8,128)(2,1)S(1)} collective-permute-done((bf16[2,16,1024]{2,1,0:T(8,128)(2,1)S(1)}, bf16[2,16,1024]{2,1,0:T(8,128)(2,1)S(1)}, u32[]{:S(2)}, u32[]{:S(2)}) %collective-permute-start.25) | collective-permute-done | bytes 65568 | tf_op jit(solution)/shard_map/ppermute | solution.py:36
  70.0 1.5 %collective-permute-start.26 = (bf16[4,16,1024]{2,1,0:T(8,128)(2,1)S(1)}, bf16[4,16,1024]{2,1,0:T(8,128)(2,1)S(1)}, u32[]{:S(2)}, u32[]{:S(2)}) collective-permute-start(bf16[4,16,1024]{2,1,0:T(8,128)(2,1)S(1)} %bitcast.304), channel_id=1, source_target_pairs={{0,2},{1,5},{2,0},{3,7},{4,6},{5,1},{6,4},{7,3},{8,10},{9,13},{10,... | collective-permute-start | bytes 393224 | tf_op jit(solution)/shard_map/ppermute | solution.py:36
  71.5 0.9 collective-permute-done.9
  72.5 1.4 %collective-permute-start.10 = (bf16[4,16,1024]{2,1,0:T(8,128)(2,1)S(1)}, bf16[4,16,1024]{2,1,0:T(8,128)(2,1)S(1)}, u32[]{:S(2)}, u32[]{:S(2)}) collective-permute-start(bf16[4,16,1024]{2,1,0:T(8,128)(2,1)S(1)} %bitcast.307), channel_id=1, source_target_pairs={{0,2},{1,5},{2,0},{3,7},{4,6},{5,1},{6,4},{7,3},{8,10},{9,13},{10,... | collective-permute-start | bytes 393224 | tf_op jit(solution)/shard_map/ppermute | solution.py:36
  73.9 1.2 %collective-permute-done.26 = bf16[4,16,1024]{2,1,0:T(8,128)(2,1)S(1)} collective-permute-done((bf16[4,16,1024]{2,1,0:T(8,128)(2,1)S(1)}, bf16[4,16,1024]{2,1,0:T(8,128)(2,1)S(1)}, u32[]{:S(2)}, u32[]{:S(2)}) %collective-permute-start.26) | collective-permute-done | bytes 131104 | tf_op jit(solution)/shard_map/ppermute | solution.py:36
  75.2 2.3 %collective-permute-done.10 = bf16[4,16,1024]{2,1,0:T(8,128)(2,1)S(1)} collective-permute-done((bf16[4,16,1024]{2,1,0:T(8,128)(2,1)S(1)}, bf16[4,16,1024]{2,1,0:T(8,128)(2,1)S(1)}, u32[]{:S(2)}, u32[]{:S(2)}) %collective-permute-start.10) | collective-permute-done | bytes 131104 | tf_op jit(solution)/shard_map/ppermute | solution.py:36
  77.8 0.8 pad_maximum_fusion.4
  78.6 7.1 %shard_map.58 = (f32[128,1024]{1,0:T(8,128)}, f32[128,1024]{1,0:T(8,128)}) custom-call(bf16[4,256,256]{2,1,0:T(8,128)(2,1)} %bitcast.262, bf16[256,1024]{1,0:T(8,128)(2,1)} %bitcast.275, bf16[4,1024,1024]{2,1,0:T(8,128)(2,1)} %vir_ref.7), custom_call_target="tpu_custom_call" | custom-call | tf_op jit(solution)/shard_map/pallas_call | solution.py:113
  85.8 0.5 collective-permute-start.28
  86.3 0.8 pad_maximum_fusion.2
  87.2 7.2 %shard_map.56 = (f32[128,1024]{1,0:T(8,128)}, f32[128,1024]{1,0:T(8,128)}) custom-call(bf16[4,256,256]{2,1,0:T(8,128)(2,1)} %bitcast.263, bf16[256,1024]{1,0:T(8,128)(2,1)} %bitcast.272, bf16[4,1024,1024]{2,1,0:T(8,128)(2,1)} %vir_ref.7), custom_call_target="tpu_custom_call" | custom-call | tf_op jit(solution)/shard_map/pallas_call | solution.py:113
  94.5 1.4 %collective-permute-start.29 = (f32[2,2,16,1024]{3,2,1,0:T(8,128)S(1)}, f32[2,2,16,1024]{3,2,1,0:T(8,128)S(1)}, u32[]{:S(2)}, u32[]{:S(2)}) collective-permute-start(f32[2,2,16,1024]{3,2,1,0:T(8,128)S(1)} %bitcast_select_fusion), channel_id=1, source_target_pairs={{0,2},{1,5},{2,0},{3,7},{4,6},{5,1},{6,4},{7,3},{8,10},{9,13},{10,... | collective-permute-start | bytes 786440 | tf_op jit(solution)/shard_map/ppermute | solution.py:83
  95.8 0.6 collective-permute-done.12
  96.5 1.1 add.146
  97.6 1.4 %collective-permute-start.13 = (f32[2,2,16,1024]{3,2,1,0:T(8,128)S(1)}, f32[2,2,16,1024]{3,2,1,0:T(8,128)S(1)}, u32[]{:S(2)}, u32[]{:S(2)}) collective-permute-start(f32[2,2,16,1024]{3,2,1,0:T(8,128)S(1)} %bitcast_select_fusion.4), channel_id=1, source_target_pairs={{0,2},{1,5},{2,0},{3,7},{4,6},{5,1},{6,4},{7,3},{8,10},{9,13},{10,... | collective-permute-start | bytes 786440 | tf_op jit(solution)/shard_map/ppermute | solution.py:83
  99.0 1.9 %collective-permute-done.29 = f32[2,2,16,1024]{3,2,1,0:T(8,128)S(1)} collective-permute-done((f32[2,2,16,1024]{3,2,1,0:T(8,128)S(1)}, f32[2,2,16,1024]{3,2,1,0:T(8,128)S(1)}, u32[]{:S(2)}, u32[]{:S(2)}) %collective-permute-start.29) | collective-permute-done | bytes 262176 | tf_op jit(solution)/shard_map/ppermute | solution.py:83
  101.0 0.7 collective-permute-start.30
  101.7 3.1 %collective-permute-done.13 = f32[2,2,16,1024]{3,2,1,0:T(8,128)S(1)} collective-permute-done((f32[2,2,16,1024]{3,2,1,0:T(8,128)S(1)}, f32[2,2,16,1024]{3,2,1,0:T(8,128)S(1)}, u32[]{:S(2)}, u32[]{:S(2)}) %collective-permute-start.13) | collective-permute-done | bytes 262176 | tf_op jit(solution)/shard_map/ppermute | solution.py:83
  104.8 0.7 collective-permute-start.14
  105.5 0.5 collective-permute-done.30
  106.1 2.1 %collective-permute-start.31 = (f32[16,1024]{1,0:T(8,128)S(1)}, f32[16,1024]{1,0:T(8,128)S(1)}, u32[]{:S(2)}, u32[]{:S(2)}) collective-permute-start(f32[16,1024]{1,0:T(8,128)S(1)} %dynamic-slice_bitcast_fusion.4), channel_id=1, source_target_pairs={{0,8},{1,9},{2,10},{3,11},{4,12},{5,13},{6,14},{7,15},{8,0},{9,1},... | collective-permute-start | bytes 196616 | tf_op jit(solution)/shard_map/ppermute | solution.py:83
  108.2 1.9 %collective-permute-done.14 = f32[2,16,1024]{2,1,0:T(8,128)S(1)} collective-permute-done((f32[2,16,1024]{2,1,0:T(8,128)S(1)}, f32[2,16,1024]{2,1,0:T(8,128)S(1)}, u32[]{:S(2)}, u32[]{:S(2)}) %collective-permute-start.14) | collective-permute-done | bytes 131104 | tf_op jit(solution)/shard_map/ppermute | solution.py:83
  110.1 2.1 %collective-permute-start.15 = (f32[16,1024]{1,0:T(8,128)S(1)}, f32[16,1024]{1,0:T(8,128)S(1)}, u32[]{:S(2)}, u32[]{:S(2)}) collective-permute-start(f32[16,1024]{1,0:T(8,128)S(1)} %dynamic-slice_bitcast_fusion.6), channel_id=1, source_target_pairs={{0,8},{1,9},{2,10},{3,11},{4,12},{5,13},{6,14},{7,15},{8,0},{9,1},... | collective-permute-start | bytes 196616 | tf_op jit(solution)/shard_map/ppermute | solution.py:83
  112.1 0.9 collective-permute-done.31
  113.0 3.0 %collective-permute-done.15 = f32[16,1024]{1,0:T(8,128)S(1)} collective-permute-done((f32[16,1024]{1,0:T(8,128)S(1)}, f32[16,1024]{1,0:T(8,128)S(1)}, u32[]{:S(2)}, u32[]{:S(2)}) %collective-permute-start.15) | collective-permute-done | bytes 65568 | tf_op jit(solution)/shard_map/ppermute | solution.py:83
  116.1 0.8 copy.63
  (78 shorter events, 2.1 us)
Async XLA Ops:
  2.6 6.3 %collective-permute-start.16 = (bf16[1,16,1024]{2,1,0:T(8,128)(2,1)S(1)}, bf16[1,16,1024]{2,1,0:T(8,128)(2,1)S(1)}, u32[]{:S(2)}, u32[]{:S(2)}) collective-permute-start(bf16[1,16,1024]{2,1,0:T(8,128)(2,1)S(1)} %get-tuple-element.66), channel_id=1, source_target_pairs={{0,8},{1,9},{2,10},{3,11},{4,12},{5,13},{6,14},{7,15},{8,0},{9,1},... | collective-permute-start | bytes 98312 | tf_op jit(solution)/shard_map/ppermute | solution.py:36
  6.7 4.8 %collective-permute-start = (bf16[1,16,1024]{2,1,0:T(8,128)(2,1)S(1)}, bf16[1,16,1024]{2,1,0:T(8,128)(2,1)S(1)}, u32[]{:S(2)}, u32[]{:S(2)}) collective-permute-start(bf16[1,16,1024]{2,1,0:T(8,128)(2,1)S(1)} %get-tuple-element.65), channel_id=1, source_target_pairs={{0,8},{1,9},{2,10},{3,11},{4,12},{5,13},{6,14},{7,15},{8,0},{9,1},... | collective-permute-start | bytes 98312 | tf_op jit(solution)/shard_map/ppermute | solution.py:36
  9.0 4.3 %collective-permute-start.17 = (bf16[2,16,1024]{2,1,0:T(8,128)(2,1)S(1)}, bf16[2,16,1024]{2,1,0:T(8,128)(2,1)S(1)}, u32[]{:S(2)}, u32[]{:S(2)}) collective-permute-start(bf16[2,16,1024]{2,1,0:T(8,128)(2,1)S(1)} %pad_maximum_fusion.12), channel_id=1, source_target_pairs={{0,4},{1,3},{2,6},{3,1},{4,0},{5,7},{6,2},{7,5},{8,12},{9,11},{10,... | collective-permute-start | bytes 196616 | tf_op jit(solution)/shard_map/ppermute | solution.py:36
  11.6 5.0 %collective-permute-start.1 = (bf16[2,16,1024]{2,1,0:T(8,128)(2,1)S(1)}, bf16[2,16,1024]{2,1,0:T(8,128)(2,1)S(1)}, u32[]{:S(2)}, u32[]{:S(2)}) collective-permute-start(bf16[2,16,1024]{2,1,0:T(8,128)(2,1)S(1)} %pad_maximum_fusion.10), channel_id=1, source_target_pairs={{0,4},{1,3},{2,6},{3,1},{4,0},{5,7},{6,2},{7,5},{8,12},{9,11},{10,... | collective-permute-start | bytes 196616 | tf_op jit(solution)/shard_map/ppermute | solution.py:36
  13.4 5.0 %collective-permute-start.18 = (bf16[4,16,1024]{2,1,0:T(8,128)(2,1)S(1)}, bf16[4,16,1024]{2,1,0:T(8,128)(2,1)S(1)}, u32[]{:S(2)}, u32[]{:S(2)}) collective-permute-start(bf16[4,16,1024]{2,1,0:T(8,128)(2,1)S(1)} %bitcast.305), channel_id=1, source_target_pairs={{0,2},{1,5},{2,0},{3,7},{4,6},{5,1},{6,4},{7,3},{8,10},{9,13},{10,... | collective-permute-start | bytes 393224 | tf_op jit(solution)/shard_map/ppermute | solution.py:36
  16.6 5.0 %collective-permute-start.2 = (bf16[4,16,1024]{2,1,0:T(8,128)(2,1)S(1)}, bf16[4,16,1024]{2,1,0:T(8,128)(2,1)S(1)}, u32[]{:S(2)}, u32[]{:S(2)}) collective-permute-start(bf16[4,16,1024]{2,1,0:T(8,128)(2,1)S(1)} %bitcast.306), channel_id=1, source_target_pairs={{0,2},{1,5},{2,0},{3,7},{4,6},{5,1},{6,4},{7,3},{8,10},{9,13},{10,... | collective-permute-start | bytes 393224 | tf_op jit(solution)/shard_map/ppermute | solution.py:36
  18.5 3.3 %collective-permute-start.19 = (bf16[8,16,1024]{2,1,0:T(8,128)(2,1)S(1)}, bf16[8,16,1024]{2,1,0:T(8,128)(2,1)S(1)}, u32[]{:S(2)}, u32[]{:S(2)}) collective-permute-start(bf16[8,16,1024]{2,1,0:T(8,128)(2,1)S(1)} %bitcast.295), channel_id=1, source_target_pairs={{0,1},{1,0},{2,3},{3,2},{4,5},{5,4},{6,7},{7,6},{8,9},{9,8},{10,11... | collective-permute-start | bytes 786440 | tf_op jit(solution)/shard_map/ppermute | solution.py:36
  21.7 8.6 %collective-permute-start.3 = (bf16[8,16,1024]{2,1,0:T(8,128)(2,1)S(1)}, bf16[8,16,1024]{2,1,0:T(8,128)(2,1)S(1)}, u32[]{:S(2)}, u32[]{:S(2)}) collective-permute-start(bf16[8,16,1024]{2,1,0:T(8,128)(2,1)S(1)} %bitcast.293), channel_id=1, source_target_pairs={{0,1},{1,0},{2,3},{3,2},{4,5},{5,4},{6,7},{7,6},{8,9},{9,8},{10,11... | collective-permute-start | bytes 786440 | tf_op jit(solution)/shard_map/ppermute | solution.py:36
  29.9 8.6 %copy-start = (f32[128,1024]{1,0:T(8,128)S(1)}, f32[128,1024]{1,0:T(8,128)}, u32[]{:S(2)}) copy-start(f32[128,1024]{1,0:T(8,128)} %get-tuple-element.17) | copy-start | bytes 1572868
  29.9 8.6 %collective-permute-start.20 = (f32[128,1024]{1,0:T(8,128)}, f32[128,1024]{1,0:T(8,128)S(1)}, u32[]{:S(2)}, u32[]{:S(2)}) collective-permute-start(f32[128,1024]{1,0:T(8,128)} %get-tuple-element.18), channel_id=1, source_target_pairs={{0,1},{1,0},{2,3},{3,2},{4,5},{5,4},{6,7},{7,6},{8,9},{9,8},{10,11... | collective-permute-start | bytes 1572872 | tf_op jit(solution)/shard_map/ppermute | solution.py:62
  31.3 28.7 %copy-start.2 = (f32[1024]{0:T(1024)S(1)}, f32[1024]{0:T(1024)}, u32[]{:S(2)}) copy-start(f32[1024]{0:T(1024)} %param.7) | copy-start | bytes 12292
  38.4 2.1 %collective-permute-start.4 = (f32[128,1024]{1,0:T(8,128)}, f32[128,1024]{1,0:T(8,128)S(1)}, u32[]{:S(2)}, u32[]{:S(2)}) collective-permute-start(f32[128,1024]{1,0:T(8,128)} %get-tuple-element.14), channel_id=1, source_target_pairs={{0,1},{1,0},{2,3},{3,2},{4,5},{5,4},{6,7},{7,6},{8,9},{9,8},{10,11... | collective-permute-start | bytes 1572872 | tf_op jit(solution)/shard_map/ppermute | solution.py:62
  38.6 6.4 %collective-permute-start.21 = (f32[2,2,16,1024]{3,2,1,0:T(8,128)S(1)}, f32[2,2,16,1024]{3,2,1,0:T(8,128)S(1)}, u32[]{:S(2)}, u32[]{:S(2)}) collective-permute-start(f32[2,2,16,1024]{3,2,1,0:T(8,128)S(1)} %bitcast_select_fusion.2), channel_id=1, source_target_pairs={{0,2},{1,5},{2,0},{3,7},{4,6},{5,1},{6,4},{7,3},{8,10},{9,13},{10,... | collective-permute-start | bytes 786440 | tf_op jit(solution)/shard_map/ppermute | solution.py:83
  41.7 7.1 %collective-permute-start.5 = (f32[2,2,16,1024]{3,2,1,0:T(8,128)S(1)}, f32[2,2,16,1024]{3,2,1,0:T(8,128)S(1)}, u32[]{:S(2)}, u32[]{:S(2)}) collective-permute-start(f32[2,2,16,1024]{3,2,1,0:T(8,128)S(1)} %bitcast_select_fusion.6), channel_id=1, source_target_pairs={{0,2},{1,5},{2,0},{3,7},{4,6},{5,1},{6,4},{7,3},{8,10},{9,13},{10,... | collective-permute-start | bytes 786440 | tf_op jit(solution)/shard_map/ppermute | solution.py:83
  45.1 5.5 %collective-permute-start.22 = (f32[2,16,1024]{2,1,0:T(8,128)S(1)}, f32[2,16,1024]{2,1,0:T(8,128)S(1)}, u32[]{:S(2)}, u32[]{:S(2)}) collective-permute-start(f32[2,16,1024]{2,1,0:T(8,128)S(1)} %dynamic-slice_bitcast_fusion.1), channel_id=1, source_target_pairs={{0,4},{1,3},{2,6},{3,1},{4,0},{5,7},{6,2},{7,5},{8,12},{9,11},{10,... | collective-permute-start | bytes 393224 | tf_op jit(solution)/shard_map/ppermute | solution.py:83
  48.9 5.7 %collective-permute-start.6 = (f32[2,16,1024]{2,1,0:T(8,128)S(1)}, f32[2,16,1024]{2,1,0:T(8,128)S(1)}, u32[]{:S(2)}, u32[]{:S(2)}) collective-permute-start(f32[2,16,1024]{2,1,0:T(8,128)S(1)} %dynamic-slice_bitcast_fusion.3), channel_id=1, source_target_pairs={{0,4},{1,3},{2,6},{3,1},{4,0},{5,7},{6,2},{7,5},{8,12},{9,11},{10,... | collective-permute-start | bytes 393224 | tf_op jit(solution)/shard_map/ppermute | solution.py:83
  50.6 6.7 %collective-permute-start.23 = (f32[16,1024]{1,0:T(8,128)S(1)}, f32[16,1024]{1,0:T(8,128)S(1)}, u32[]{:S(2)}, u32[]{:S(2)}) collective-permute-start(f32[16,1024]{1,0:T(8,128)S(1)} %dynamic-slice_bitcast_fusion.5), channel_id=1, source_target_pairs={{0,8},{1,9},{2,10},{3,11},{4,12},{5,13},{6,14},{7,15},{8,0},{9,1},... | collective-permute-start | bytes 196616 | tf_op jit(solution)/shard_map/ppermute | solution.py:83
  54.7 5.2 %collective-permute-start.7 = (f32[16,1024]{1,0:T(8,128)S(1)}, f32[16,1024]{1,0:T(8,128)S(1)}, u32[]{:S(2)}, u32[]{:S(2)}) collective-permute-start(f32[16,1024]{1,0:T(8,128)S(1)} %dynamic-slice_bitcast_fusion.7), channel_id=1, source_target_pairs={{0,8},{1,9},{2,10},{3,11},{4,12},{5,13},{6,14},{7,15},{8,0},{9,1},... | collective-permute-start | bytes 196616 | tf_op jit(solution)/shard_map/ppermute | solution.py:83
  60.0 4.9 %collective-permute-start.24 = (bf16[1,16,1024]{2,1,0:T(8,128)(2,1)S(1)}, bf16[1,16,1024]{2,1,0:T(8,128)(2,1)S(1)}, u32[]{:S(2)}, u32[]{:S(2)}) collective-permute-start(bf16[1,16,1024]{2,1,0:T(8,128)(2,1)S(1)} %get-tuple-element.63), channel_id=1, source_target_pairs={{0,8},{1,9},{2,10},{3,11},{4,12},{5,13},{6,14},{7,15},{8,0},{9,1},... | collective-permute-start | bytes 98312 | tf_op jit(solution)/shard_map/ppermute | solution.py:36
  63.1 5.0 %collective-permute-start.8 = (bf16[1,16,1024]{2,1,0:T(8,128)(2,1)S(1)}, bf16[1,16,1024]{2,1,0:T(8,128)(2,1)S(1)}, u32[]{:S(2)}, u32[]{:S(2)}) collective-permute-start(bf16[1,16,1024]{2,1,0:T(8,128)(2,1)S(1)} %get-tuple-element.21), channel_id=1, source_target_pairs={{0,8},{1,9},{2,10},{3,11},{4,12},{5,13},{6,14},{7,15},{8,0},{9,1},... | collective-permute-start | bytes 98312 | tf_op jit(solution)/shard_map/ppermute | solution.py:36
  65.0 5.0 %collective-permute-start.25 = (bf16[2,16,1024]{2,1,0:T(8,128)(2,1)S(1)}, bf16[2,16,1024]{2,1,0:T(8,128)(2,1)S(1)}, u32[]{:S(2)}, u32[]{:S(2)}) collective-permute-start(bf16[2,16,1024]{2,1,0:T(8,128)(2,1)S(1)} %pad_maximum_fusion.13), channel_id=1, source_target_pairs={{0,4},{1,3},{2,6},{3,1},{4,0},{5,7},{6,2},{7,5},{8,12},{9,11},{10,... | collective-permute-start | bytes 196616 | tf_op jit(solution)/shard_map/ppermute | solution.py:36
  68.1 4.3 %collective-permute-start.9 = (bf16[2,16,1024]{2,1,0:T(8,128)(2,1)S(1)}, bf16[2,16,1024]{2,1,0:T(8,128)(2,1)S(1)}, u32[]{:S(2)}, u32[]{:S(2)}) collective-permute-start(bf16[2,16,1024]{2,1,0:T(8,128)(2,1)S(1)} %pad_maximum_fusion.11), channel_id=1, source_target_pairs={{0,4},{1,3},{2,6},{3,1},{4,0},{5,7},{6,2},{7,5},{8,12},{9,11},{10,... | collective-permute-start | bytes 196616 | tf_op jit(solution)/shard_map/ppermute | solution.py:36
  70.0 5.0 %collective-permute-start.26 = (bf16[4,16,1024]{2,1,0:T(8,128)(2,1)S(1)}, bf16[4,16,1024]{2,1,0:T(8,128)(2,1)S(1)}, u32[]{:S(2)}, u32[]{:S(2)}) collective-permute-start(bf16[4,16,1024]{2,1,0:T(8,128)(2,1)S(1)} %bitcast.304), channel_id=1, source_target_pairs={{0,2},{1,5},{2,0},{3,7},{4,6},{5,1},{6,4},{7,3},{8,10},{9,13},{10,... | collective-permute-start | bytes 393224 | tf_op jit(solution)/shard_map/ppermute | solution.py:36
  72.5 5.0 %collective-permute-start.10 = (bf16[4,16,1024]{2,1,0:T(8,128)(2,1)S(1)}, bf16[4,16,1024]{2,1,0:T(8,128)(2,1)S(1)}, u32[]{:S(2)}, u32[]{:S(2)}) collective-permute-start(bf16[4,16,1024]{2,1,0:T(8,128)(2,1)S(1)} %bitcast.307), channel_id=1, source_target_pairs={{0,2},{1,5},{2,0},{3,7},{4,6},{5,1},{6,4},{7,3},{8,10},{9,13},{10,... | collective-permute-start | bytes 393224 | tf_op jit(solution)/shard_map/ppermute | solution.py:36
  75.2 2.6 %collective-permute-start.27 = (bf16[8,16,1024]{2,1,0:T(8,128)(2,1)S(1)}, bf16[8,16,1024]{2,1,0:T(8,128)(2,1)S(1)}, u32[]{:S(2)}, u32[]{:S(2)}) collective-permute-start(bf16[8,16,1024]{2,1,0:T(8,128)(2,1)S(1)} %bitcast.294), channel_id=1, source_target_pairs={{0,1},{1,0},{2,3},{3,2},{4,5},{5,4},{6,7},{7,6},{8,9},{9,8},{10,11... | collective-permute-start | bytes 786440 | tf_op jit(solution)/shard_map/ppermute | solution.py:36
  77.6 8.6 %collective-permute-start.11 = (bf16[8,16,1024]{2,1,0:T(8,128)(2,1)S(1)}, bf16[8,16,1024]{2,1,0:T(8,128)(2,1)S(1)}, u32[]{:S(2)}, u32[]{:S(2)}) collective-permute-start(bf16[8,16,1024]{2,1,0:T(8,128)(2,1)S(1)} %bitcast.292), channel_id=1, source_target_pairs={{0,1},{1,0},{2,3},{3,2},{4,5},{5,4},{6,7},{7,6},{8,9},{9,8},{10,11... | collective-permute-start | bytes 786440 | tf_op jit(solution)/shard_map/ppermute | solution.py:36
  85.8 8.6 %copy-start.1 = (f32[128,1024]{1,0:T(8,128)S(1)}, f32[128,1024]{1,0:T(8,128)}, u32[]{:S(2)}) copy-start(f32[128,1024]{1,0:T(8,128)} %get-tuple-element.19) | copy-start | bytes 1572868
  85.8 8.6 %collective-permute-start.28 = (f32[128,1024]{1,0:T(8,128)}, f32[128,1024]{1,0:T(8,128)S(1)}, u32[]{:S(2)}, u32[]{:S(2)}) collective-permute-start(f32[128,1024]{1,0:T(8,128)} %get-tuple-element.20), channel_id=1, source_target_pairs={{0,1},{1,0},{2,3},{3,2},{4,5},{5,4},{6,7},{7,6},{8,9},{9,8},{10,11... | collective-permute-start | bytes 1572872 | tf_op jit(solution)/shard_map/ppermute | solution.py:62
  94.3 2.1 %collective-permute-start.12 = (f32[128,1024]{1,0:T(8,128)}, f32[128,1024]{1,0:T(8,128)S(1)}, u32[]{:S(2)}, u32[]{:S(2)}) collective-permute-start(f32[128,1024]{1,0:T(8,128)} %get-tuple-element.16), channel_id=1, source_target_pairs={{0,1},{1,0},{2,3},{3,2},{4,5},{5,4},{6,7},{7,6},{8,9},{9,8},{10,11... | collective-permute-start | bytes 1572872 | tf_op jit(solution)/shard_map/ppermute | solution.py:62
  94.5 6.4 %collective-permute-start.29 = (f32[2,2,16,1024]{3,2,1,0:T(8,128)S(1)}, f32[2,2,16,1024]{3,2,1,0:T(8,128)S(1)}, u32[]{:S(2)}, u32[]{:S(2)}) collective-permute-start(f32[2,2,16,1024]{3,2,1,0:T(8,128)S(1)} %bitcast_select_fusion), channel_id=1, source_target_pairs={{0,2},{1,5},{2,0},{3,7},{4,6},{5,1},{6,4},{7,3},{8,10},{9,13},{10,... | collective-permute-start | bytes 786440 | tf_op jit(solution)/shard_map/ppermute | solution.py:83
  97.6 7.2 %collective-permute-start.13 = (f32[2,2,16,1024]{3,2,1,0:T(8,128)S(1)}, f32[2,2,16,1024]{3,2,1,0:T(8,128)S(1)}, u32[]{:S(2)}, u32[]{:S(2)}) collective-permute-start(f32[2,2,16,1024]{3,2,1,0:T(8,128)S(1)} %bitcast_select_fusion.4), channel_id=1, source_target_pairs={{0,2},{1,5},{2,0},{3,7},{4,6},{5,1},{6,4},{7,3},{8,10},{9,13},{10,... | collective-permute-start | bytes 786440 | tf_op jit(solution)/shard_map/ppermute | solution.py:83
  101.0 5.0 %collective-permute-start.30 = (f32[2,16,1024]{2,1,0:T(8,128)S(1)}, f32[2,16,1024]{2,1,0:T(8,128)S(1)}, u32[]{:S(2)}, u32[]{:S(2)}) collective-permute-start(f32[2,16,1024]{2,1,0:T(8,128)S(1)} %dynamic-slice_bitcast_fusion), channel_id=1, source_target_pairs={{0,4},{1,3},{2,6},{3,1},{4,0},{5,7},{6,2},{7,5},{8,12},{9,11},{10,... | collective-permute-start | bytes 393224 | tf_op jit(solution)/shard_map/ppermute | solution.py:83
  104.8 5.2 %collective-permute-start.14 = (f32[2,16,1024]{2,1,0:T(8,128)S(1)}, f32[2,16,1024]{2,1,0:T(8,128)S(1)}, u32[]{:S(2)}, u32[]{:S(2)}) collective-permute-start(f32[2,16,1024]{2,1,0:T(8,128)S(1)} %dynamic-slice_bitcast_fusion.2), channel_id=1, source_target_pairs={{0,4},{1,3},{2,6},{3,1},{4,0},{5,7},{6,2},{7,5},{8,12},{9,11},{10,... | collective-permute-start | bytes 393224 | tf_op jit(solution)/shard_map/ppermute | solution.py:83
  106.1 7.0 %collective-permute-start.31 = (f32[16,1024]{1,0:T(8,128)S(1)}, f32[16,1024]{1,0:T(8,128)S(1)}, u32[]{:S(2)}, u32[]{:S(2)}) collective-permute-start(f32[16,1024]{1,0:T(8,128)S(1)} %dynamic-slice_bitcast_fusion.4), channel_id=1, source_target_pairs={{0,8},{1,9},{2,10},{3,11},{4,12},{5,13},{6,14},{7,15},{8,0},{9,1},... | collective-permute-start | bytes 196616 | tf_op jit(solution)/shard_map/ppermute | solution.py:83
  110.1 5.9 %collective-permute-start.15 = (f32[16,1024]{1,0:T(8,128)S(1)}, f32[16,1024]{1,0:T(8,128)S(1)}, u32[]{:S(2)}, u32[]{:S(2)}) collective-permute-start(f32[16,1024]{1,0:T(8,128)S(1)} %dynamic-slice_bitcast_fusion.6), channel_id=1, source_target_pairs={{0,8},{1,9},{2,10},{3,11},{4,12},{5,13},{6,14},{7,15},{8,0},{9,1},... | collective-permute-start | bytes 196616 | tf_op jit(solution)/shard_map/ppermute | solution.py:83

commit v8 on v7

--- a/solution.py
+++ b/solution.py
@@ -31,7 +31,7 @@
     order0, order1 = bit_orders(m, True)
     acc = x[None]
     have0, have1 = [], []
-    for b0, b1 in zip(order0, order1):
+    for b0, b1 in zip(order0[:-1], order1[:-1]):
         bit = jnp.where(odd, (me >> b1) & 1, (me >> b0) & 1)
         theirs = lax.ppermute(acc, "aux", partners(n, b0, b1))
         lo = jnp.where(bit == 0, acc, theirs)
@@ -49,7 +49,8 @@
         have0 = sorted(have0 + [b0], reverse=True)
         have1 = sorted(have1 + [b1], reverse=True)
         acc = acc.reshape((-1,) + x.shape)
-    return acc.reshape((n * x.shape[0],) + x.shape[1:])
+    flat = acc.reshape((n // 2 * x.shape[0],) + x.shape[1:])
+    return flat, lax.ppermute(flat, "aux", partners(n, 0, 0))
 
 
 def scatter_sum(keep, send, n):
@@ -86,11 +87,14 @@
     return acc
 
 
-def exchange_kernel(states, occ_ref, r_ref, vir_ref, keep_ref, send_ref):
+def exchange_kernel(states, occ_ref, mine_ref, theirs_ref, vir_ref, keep_ref, send_ref, r_ref):
     @pl.when(pl.program_id(0) == 0)
     def _():
         keep_ref[...] = jnp.zeros_like(keep_ref)
         send_ref[...] = jnp.zeros_like(send_ref)
+        split = mine_ref.shape[0]
+        r_ref[:split] = mine_ref[...]
+        r_ref[split:] = theirs_ref[...]
 
     half = jnp.dot(occ_ref[0], r_ref[...], preferred_element_type=jnp.float32).astype(jnp.bfloat16)
     nvir = vir_ref.shape[1]
@@ -105,7 +109,7 @@
         send_ref[:, cols] += term[split:]
 
 
-def exchange_part(occ_ints, flat, vir_ints, states):
+def exchange_part(occ_ints, mine, theirs, vir_ints, states):
     local_aux, nocc, _ = occ_ints.shape
     nvir = vir_ints.shape[1]
     width = states * nvir
@@ -115,7 +119,8 @@
         grid=(local_aux,),
         in_specs=[
             pl.BlockSpec((1, nocc, nocc), lambda p: (p, 0, 0)),
-            pl.BlockSpec((nocc, width), lambda p: (0, 0)),
+            pl.BlockSpec((nocc // 2, width), lambda p: (0, 0)),
+            pl.BlockSpec((nocc // 2, width), lambda p: (0, 0)),
             pl.BlockSpec((1, nvir, nvir), lambda p: (p, 0, 0)),
         ],
         out_specs=[
@@ -123,8 +128,21 @@
             pl.BlockSpec((nocc // 2, width), lambda p: (0, 0)),
         ],
         out_shape=[out, out],
+        scratch_shapes=[pltpu.VMEM((nocc, width), jnp.bfloat16)],
         compiler_params=pltpu.CompilerParams(dimension_semantics=("arbitrary",)),
-    )(occ_ints, flat, vir_ints)
+    )(occ_ints, mine, theirs, vir_ints)
+
+
+def order_columns(occ_ints, n, core):
+    local_aux, nocc, _ = occ_ints.shape
+    rows = nocc // n
+    dest = jnp.arange(nocc)
+    block, within = dest // rows, dest % rows
+    upper = block // (n // 2)
+    source = ((block % (n // 2)) * 2 + (upper ^ core)) * rows + within
+    select = (jnp.arange(nocc)[:, None] == source[None, :]).astype(occ_ints.dtype)
+    moved = jnp.dot(occ_ints.reshape(local_aux * nocc, nocc), select, preferred_element_type=jnp.float32)
+    return moved.astype(occ_ints.dtype).reshape(local_aux, nocc, nocc)
 
 
 def order_rows(occ_ints, n, core):
@@ -146,7 +164,7 @@
     position = lax.axis_index("aux")
     my_occ = lax.dynamic_slice_in_dim(occ_energy, position * own_rows, own_rows, 0)
     denom = vir_energy[None, None, :] - my_occ[:, None, None]
-    ordered_occ = order_rows(occ_ints, n, position & 1)
+    ordered_occ = order_columns(order_rows(occ_ints, n, position & 1), n, position & 1)
     finals = []
     for state in range(states):
         own_rhs = rhs[:, state, :]
@@ -154,8 +172,8 @@
         resp = own_rhs / own_denom
         for step in range(ITERS):
             rounded = resp.astype(jnp.bfloat16)
-            flat = gather_rows(rounded, n)
-            keep, send = exchange_part(ordered_occ, flat, vir_ints, 1)
+            mine, theirs = gather_rows(rounded, n)
+            keep, send = exchange_part(ordered_occ, mine, theirs, vir_ints, 1)
             exchange = scatter_sum(keep, send, n)
             resp = 0.4 * resp + 0.6 * (own_rhs - exchange) / own_denom
         finals.append(resp)

time: 117 us -> 117 us (level)
  waiting for transfers between devices: 36 us -> 32.2 us
  other arithmetic: 9.74 us -> 6.4 us
  local copies, waits for them, and re-layouts: 2.78 us -> 5.69 us
  starting transfers between devices: 39.4 us -> 41.9 us
    another operation x16 -> x12, other arithmetic: 3.54 us -> 0.15 us  [gather_rows(): new0 = jnp.stack([lo, hi], axis=at0)]
    ppermute x16 -> x12, waiting for transfers between devices: 15.3 us -> 12.1 us  [gather_rows(): theirs = lax.ppermute(acc, 'aux', partners(n, b0, b1))]
    unnamed x6 -> x22, local copies, waits for them, and re-layouts: 0.01 us -> 2.89 us
    ppermute x16 -> x12, starting transfers between devices: 18.9 us -> 20.4 us  [gather_rows(): theirs = lax.ppermute(acc, 'aux', partners(n, b0, b1))]
  transfers between devices with their start and end apart: 32 -> 32, of which waited for: 24 -> 22; matrix products, arithmetic and copies ran while one was open for 8% -> 6% of each run, Pallas kernels for 24% -> 25%
where the time goes in v8:
time: 117 us; the launch traced here: 116 us
  starting transfers between devices  41.9 us (36%)
  waiting for transfers between devices  32.2 us (28%)
  Pallas kernels  28.7 us (25%)
  other arithmetic  6.4 us (5%)
  local copies, waits for them, and re-layouts  5.69 us (5%)
    pallas_call x4, Pallas kernels, exchange_part(): pl.pallas_call(functools.partial(exchange_kernel, states), grid=(local_au...  28.7 us
    ppermute x12, starting transfers between devices, gather_rows(): theirs = lax.ppermute(acc, 'aux', partners(n, b0, b1))  20.4 us
    ppermute x12, starting transfers between devices, scatter_sum(): acc = kept + lax.ppermute(sent, 'aux', partners(n, b0, b1))  20.1 us
    ppermute x12, waiting for transfers between devices, scatter_sum(): acc = kept + lax.ppermute(sent, 'aux', partners(n, b0, b1))  19.1 us
    ppermute x12, waiting for transfers between devices, gather_rows(): theirs = lax.ppermute(acc, 'aux', partners(n, b0, b1))  12.1 us
    unnamed x22, local copies, waits for them, and re-layouts  2.89 us
  transfers between devices with their start and end apart: 32, of which 22 were waited for; matrix products, arithmetic and copies ran while one was open for 6% of the time, Pallas kernels for 25%

profile of v8, /device:TPU:0, one launch (start us, length us, event | category | flops | bytes accessed | tf_op | source)
XLA Modules:
  0.0 116.5 jit_solution(14642340407873982777)
XLA Ops:
  0.0 1.1 fusion.32
  1.1 0.8 dynamic_slice.103
  1.9 0.8 fusion.7
  2.6 4.1 %collective-permute-start.16 = (bf16[1,16,1024]{2,1,0:T(8,128)(2,1)S(1)}, bf16[1,16,1024]{2,1,0:T(8,128)(2,1)S(1)}, u32[]{:S(2)}, u32[]{:S(2)}) collective-permute-start(bf16[1,16,1024]{2,1,0:T(8,128)(2,1)S(1)} %get-tuple-element.56), channel_id=1, source_target_pairs={{0,8},{1,9},{2,10},{3,11},{4,12},{5,13},{6,14},{7,15},{8,0},{9,1},... | collective-permute-start | bytes 98312 | tf_op jit(solution)/shard_map/ppermute | solution.py:36
  6.8 1.1 fusion
  7.9 1.1 fusion.1
  9.1 1.1 convolution_convert_fusion
  10.2 1.9 %collective-permute-start.17 = (bf16[2,16,1024]{2,1,0:T(8,128)(2,1)S(1)}, bf16[2,16,1024]{2,1,0:T(8,128)(2,1)S(1)}, u32[]{:S(2)}, u32[]{:S(2)}) collective-permute-start(bf16[2,16,1024]{2,1,0:T(8,128)(2,1)S(1)} %pad_maximum_fusion.8), channel_id=1, source_target_pairs={{0,4},{1,3},{2,6},{3,1},{4,0},{5,7},{6,2},{7,5},{8,12},{9,11},{10,... | collective-permute-start | bytes 196616 | tf_op jit(solution)/shard_map/ppermute | solution.py:36
  12.2 1.1 collective-permute-start.1
  13.2 1.3 %collective-permute-done.17 = bf16[2,16,1024]{2,1,0:T(8,128)(2,1)S(1)} collective-permute-done((bf16[2,16,1024]{2,1,0:T(8,128)(2,1)S(1)}, bf16[2,16,1024]{2,1,0:T(8,128)(2,1)S(1)}, u32[]{:S(2)}, u32[]{:S(2)}) %collective-permute-start.17) | collective-permute-done | bytes 65568 | tf_op jit(solution)/shard_map/ppermute | solution.py:36
  14.6 1.8 %collective-permute-start.18 = (bf16[4,16,1024]{2,1,0:T(8,128)(2,1)S(1)}, bf16[4,16,1024]{2,1,0:T(8,128)(2,1)S(1)}, u32[]{:S(2)}, u32[]{:S(2)}) collective-permute-start(bf16[4,16,1024]{2,1,0:T(8,128)(2,1)S(1)} %bitcast.264), channel_id=1, source_target_pairs={{0,2},{1,5},{2,0},{3,7},{4,6},{5,1},{6,4},{7,3},{8,10},{9,13},{10,... | collective-permute-start | bytes 393224 | tf_op jit(solution)/shard_map/ppermute | solution.py:36
  16.4 0.8 collective-permute-done.1
  17.2 1.6 %collective-permute-start.2 = (bf16[4,16,1024]{2,1,0:T(8,128)(2,1)S(1)}, bf16[4,16,1024]{2,1,0:T(8,128)(2,1)S(1)}, u32[]{:S(2)}, u32[]{:S(2)}) collective-permute-start(bf16[4,16,1024]{2,1,0:T(8,128)(2,1)S(1)} %bitcast.265), channel_id=1, source_target_pairs={{0,2},{1,5},{2,0},{3,7},{4,6},{5,1},{6,4},{7,3},{8,10},{9,13},{10,... | collective-permute-start | bytes 393224 | tf_op jit(solution)/shard_map/ppermute | solution.py:36
  18.8 0.9 collective-permute-done.18
  19.8 2.4 %collective-permute-done.2 = bf16[4,16,1024]{2,1,0:T(8,128)(2,1)S(1)} collective-permute-done((bf16[4,16,1024]{2,1,0:T(8,128)(2,1)S(1)}, bf16[4,16,1024]{2,1,0:T(8,128)(2,1)S(1)}, u32[]{:S(2)}, u32[]{:S(2)}) %collective-permute-start.2) | collective-permute-done | bytes 131104 | tf_op jit(solution)/shard_map/ppermute | solution.py:36
  22.5 0.7 copy-done.7
  23.2 7.2 %shard_map.57 = (f32[128,1024]{1,0:T(8,128)}, f32[128,1024]{1,0:T(8,128)}) custom-call(bf16[4,256,256]{2,1,0:T(8,128)(2,1)} %bitcast.224, bf16[128,1024]{1,0:T(8,128)(2,1)} %bitcast.258, bf16[128,1024]{1,0:T(8,128)(2,1)} %copy-done.7, bf16[4,1024,1024]{2,1,0:T(8,128)(2,1)} %vir_ref.7), custom_call_target="tpu_custom_call" | custom-call | tf_op jit(solution)/shard_map/pallas_call | solution.py:117
  30.3 0.5 collective-permute-start.20
  30.9 0.7 copy-done.9
  31.6 7.2 %shard_map.55 = (f32[128,1024]{1,0:T(8,128)}, f32[128,1024]{1,0:T(8,128)}) custom-call(bf16[4,256,256]{2,1,0:T(8,128)(2,1)} %bitcast.225, bf16[128,1024]{1,0:T(8,128)(2,1)} %bitcast.262, bf16[128,1024]{1,0:T(8,128)(2,1)} %copy-done.9, bf16[4,1024,1024]{2,1,0:T(8,128)(2,1)} %vir_ref.7), custom_call_target="tpu_custom_call" | custom-call | tf_op jit(solution)/shard_map/pallas_call | solution.py:117
  38.9 1.6 %collective-permute-start.21 = (f32[2,2,16,1024]{3,2,1,0:T(8,128)S(1)}, f32[2,2,16,1024]{3,2,1,0:T(8,128)S(1)}, u32[]{:S(2)}, u32[]{:S(2)}) collective-permute-start(f32[2,2,16,1024]{3,2,1,0:T(8,128)S(1)} %bitcast_select_fusion.4), channel_id=1, source_target_pairs={{0,2},{1,5},{2,0},{3,7},{4,6},{5,1},{6,4},{7,3},{8,10},{9,13},{10,... | collective-permute-start | bytes 786440 | tf_op jit(solution)/shard_map/ppermute | solution.py:84
  40.5 0.4 collective-permute-done.4
  40.9 1.1 add.178
  42.1 1.6 %collective-permute-start.5 = (f32[2,2,16,1024]{3,2,1,0:T(8,128)S(1)}, f32[2,2,16,1024]{3,2,1,0:T(8,128)S(1)}, u32[]{:S(2)}, u32[]{:S(2)}) collective-permute-start(f32[2,2,16,1024]{3,2,1,0:T(8,128)S(1)} %bitcast_select_fusion.8), channel_id=1, source_target_pairs={{0,2},{1,5},{2,0},{3,7},{4,6},{5,1},{6,4},{7,3},{8,10},{9,13},{10,... | collective-permute-start | bytes 786440 | tf_op jit(solution)/shard_map/ppermute | solution.py:84
  43.6 1.8 %collective-permute-done.21 = f32[2,2,16,1024]{3,2,1,0:T(8,128)S(1)} collective-permute-done((f32[2,2,16,1024]{3,2,1,0:T(8,128)S(1)}, f32[2,2,16,1024]{3,2,1,0:T(8,128)S(1)}, u32[]{:S(2)}, u32[]{:S(2)}) %collective-permute-start.21) | collective-permute-done | bytes 262176 | tf_op jit(solution)/shard_map/ppermute | solution.py:84
  45.4 0.9 collective-permute-start.22
  46.3 2.9 %collective-permute-done.5 = f32[2,2,16,1024]{3,2,1,0:T(8,128)S(1)} collective-permute-done((f32[2,2,16,1024]{3,2,1,0:T(8,128)S(1)}, f32[2,2,16,1024]{3,2,1,0:T(8,128)S(1)}, u32[]{:S(2)}, u32[]{:S(2)}) %collective-permute-start.5) | collective-permute-done | bytes 262176 | tf_op jit(solution)/shard_map/ppermute | solution.py:84
  49.3 0.9 collective-permute-start.6
  50.2 0.3 collective-permute-done.22
  50.5 2.7 %collective-permute-start.23 = (f32[16,1024]{1,0:T(8,128)S(1)}, f32[16,1024]{1,0:T(8,128)S(1)}, u32[]{:S(2)}, u32[]{:S(2)}) collective-permute-start(f32[16,1024]{1,0:T(8,128)S(1)} %dynamic-slice_bitcast_fusion.5), channel_id=1, source_target_pairs={{0,8},{1,9},{2,10},{3,11},{4,12},{5,13},{6,14},{7,15},{8,0},{9,1},... | collective-permute-start | bytes 196616 | tf_op jit(solution)/shard_map/ppermute | solution.py:84
  53.2 1.5 %collective-permute-done.6 = f32[2,16,1024]{2,1,0:T(8,128)S(1)} collective-permute-done((f32[2,16,1024]{2,1,0:T(8,128)S(1)}, f32[2,16,1024]{2,1,0:T(8,128)S(1)}, u32[]{:S(2)}, u32[]{:S(2)}) %collective-permute-start.6) | collective-permute-done | bytes 131104 | tf_op jit(solution)/shard_map/ppermute | solution.py:84
  54.7 2.3 %collective-permute-start.7 = (f32[16,1024]{1,0:T(8,128)S(1)}, f32[16,1024]{1,0:T(8,128)S(1)}, u32[]{:S(2)}, u32[]{:S(2)}) collective-permute-start(f32[16,1024]{1,0:T(8,128)S(1)} %dynamic-slice_bitcast_fusion.7), channel_id=1, source_target_pairs={{0,8},{1,9},{2,10},{3,11},{4,12},{5,13},{6,14},{7,15},{8,0},{9,1},... | collective-permute-start | bytes 196616 | tf_op jit(solution)/shard_map/ppermute | solution.py:84
  57.0 3.6 %collective-permute-done.7 = f32[16,1024]{1,0:T(8,128)S(1)} collective-permute-done((f32[16,1024]{1,0:T(8,128)S(1)}, f32[16,1024]{1,0:T(8,128)S(1)}, u32[]{:S(2)}, u32[]{:S(2)}) %collective-permute-start.7) | collective-permute-done | bytes 65568 | tf_op jit(solution)/shard_map/ppermute | solution.py:84
  60.7 1.7 %collective-permute-start.24 = (bf16[1,16,1024]{2,1,0:T(8,128)(2,1)S(1)}, bf16[1,16,1024]{2,1,0:T(8,128)(2,1)S(1)}, u32[]{:S(2)}, u32[]{:S(2)}) collective-permute-start(bf16[1,16,1024]{2,1,0:T(8,128)(2,1)S(1)} %get-tuple-element.53), channel_id=1, source_target_pairs={{0,8},{1,9},{2,10},{3,11},{4,12},{5,13},{6,14},{7,15},{8,0},{9,1},... | collective-permute-start | bytes 98312 | tf_op jit(solution)/shard_map/ppermute | solution.py:36
  62.4 1.3 %collective-permute-start.8 = (bf16[1,16,1024]{2,1,0:T(8,128)(2,1)S(1)}, bf16[1,16,1024]{2,1,0:T(8,128)(2,1)S(1)}, u32[]{:S(2)}, u32[]{:S(2)}) collective-permute-start(bf16[1,16,1024]{2,1,0:T(8,128)(2,1)S(1)} %get-tuple-element.21), channel_id=1, source_target_pairs={{0,8},{1,9},{2,10},{3,11},{4,12},{5,13},{6,14},{7,15},{8,0},{9,1},... | collective-permute-start | bytes 98312 | tf_op jit(solution)/shard_map/ppermute | solution.py:36
  63.7 1.9 %collective-permute-done.24 = bf16[1,16,1024]{2,1,0:T(8,128)(2,1)S(1)} collective-permute-done((bf16[1,16,1024]{2,1,0:T(8,128)(2,1)S(1)}, bf16[1,16,1024]{2,1,0:T(8,128)(2,1)S(1)}, u32[]{:S(2)}, u32[]{:S(2)}) %collective-permute-start.24) | collective-permute-done | bytes 32800 | tf_op jit(solution)/shard_map/ppermute | solution.py:36
  65.7 1.2 %collective-permute-start.25 = (bf16[2,16,1024]{2,1,0:T(8,128)(2,1)S(1)}, bf16[2,16,1024]{2,1,0:T(8,128)(2,1)S(1)}, u32[]{:S(2)}, u32[]{:S(2)}) collective-permute-start(bf16[2,16,1024]{2,1,0:T(8,128)(2,1)S(1)} %pad_maximum_fusion.9), channel_id=1, source_target_pairs={{0,4},{1,3},{2,6},{3,1},{4,0},{5,7},{6,2},{7,5},{8,12},{9,11},{10,... | collective-permute-start | bytes 196616 | tf_op jit(solution)/shard_map/ppermute | solution.py:36
  66.8 0.4 collective-permute-done.8
  67.3 2.9 %collective-permute-start.9 = (bf16[2,16,1024]{2,1,0:T(8,128)(2,1)S(1)}, bf16[2,16,1024]{2,1,0:T(8,128)(2,1)S(1)}, u32[]{:S(2)}, u32[]{:S(2)}) collective-permute-start(bf16[2,16,1024]{2,1,0:T(8,128)(2,1)S(1)} %pad_maximum_fusion.7), channel_id=1, source_target_pairs={{0,4},{1,3},{2,6},{3,1},{4,0},{5,7},{6,2},{7,5},{8,12},{9,11},{10,... | collective-permute-start | bytes 196616 | tf_op jit(solution)/shard_map/ppermute | solution.py:36
  70.1 0.5 collective-permute-done.25
  70.7 1.4 %collective-permute-start.26 = (bf16[4,16,1024]{2,1,0:T(8,128)(2,1)S(1)}, bf16[4,16,1024]{2,1,0:T(8,128)(2,1)S(1)}, u32[]{:S(2)}, u32[]{:S(2)}) collective-permute-start(bf16[4,16,1024]{2,1,0:T(8,128)(2,1)S(1)} %bitcast.263), channel_id=1, source_target_pairs={{0,2},{1,5},{2,0},{3,7},{4,6},{5,1},{6,4},{7,3},{8,10},{9,13},{10,... | collective-permute-start | bytes 393224 | tf_op jit(solution)/shard_map/ppermute | solution.py:36
  72.1 0.5 collective-permute-done.9
  72.6 1.4 %collective-permute-start.10 = (bf16[4,16,1024]{2,1,0:T(8,128)(2,1)S(1)}, bf16[4,16,1024]{2,1,0:T(8,128)(2,1)S(1)}, u32[]{:S(2)}, u32[]{:S(2)}) collective-permute-start(bf16[4,16,1024]{2,1,0:T(8,128)(2,1)S(1)} %bitcast.266), channel_id=1, source_target_pairs={{0,2},{1,5},{2,0},{3,7},{4,6},{5,1},{6,4},{7,3},{8,10},{9,13},{10,... | collective-permute-start | bytes 393224 | tf_op jit(solution)/shard_map/ppermute | solution.py:36
  74.1 1.7 %collective-permute-done.26 = bf16[4,16,1024]{2,1,0:T(8,128)(2,1)S(1)} collective-permute-done((bf16[4,16,1024]{2,1,0:T(8,128)(2,1)S(1)}, bf16[4,16,1024]{2,1,0:T(8,128)(2,1)S(1)}, u32[]{:S(2)}, u32[]{:S(2)}) %collective-permute-start.26) | collective-permute-done | bytes 131104 | tf_op jit(solution)/shard_map/ppermute | solution.py:36
  75.9 1.7 %collective-permute-done.10 = bf16[4,16,1024]{2,1,0:T(8,128)(2,1)S(1)} collective-permute-done((bf16[4,16,1024]{2,1,0:T(8,128)(2,1)S(1)}, bf16[4,16,1024]{2,1,0:T(8,128)(2,1)S(1)}, u32[]{:S(2)}, u32[]{:S(2)}) %collective-permute-start.10) | collective-permute-done | bytes 131104 | tf_op jit(solution)/shard_map/ppermute | solution.py:36
  77.9 0.7 copy-done.6
  78.6 7.2 %shard_map.58 = (f32[128,1024]{1,0:T(8,128)}, f32[128,1024]{1,0:T(8,128)}) custom-call(bf16[4,256,256]{2,1,0:T(8,128)(2,1)} %bitcast.226, bf16[128,1024]{1,0:T(8,128)(2,1)} %bitcast.256, bf16[128,1024]{1,0:T(8,128)(2,1)} %copy-done.6, bf16[4,1024,1024]{2,1,0:T(8,128)(2,1)} %vir_ref.7), custom_call_target="tpu_custom_call" | custom-call | tf_op jit(solution)/shard_map/pallas_call | solution.py:117
  85.7 0.5 collective-permute-start.28
  86.2 0.7 copy-done.8
  87.0 7.2 %shard_map.56 = (f32[128,1024]{1,0:T(8,128)}, f32[128,1024]{1,0:T(8,128)}) custom-call(bf16[4,256,256]{2,1,0:T(8,128)(2,1)} %bitcast.227, bf16[128,1024]{1,0:T(8,128)(2,1)} %bitcast.260, bf16[128,1024]{1,0:T(8,128)(2,1)} %copy-done.8, bf16[4,1024,1024]{2,1,0:T(8,128)(2,1)} %vir_ref.7), custom_call_target="tpu_custom_call" | custom-call | tf_op jit(solution)/shard_map/pallas_call | solution.py:117
  94.3 1.4 %collective-permute-start.29 = (f32[2,2,16,1024]{3,2,1,0:T(8,128)S(1)}, f32[2,2,16,1024]{3,2,1,0:T(8,128)S(1)}, u32[]{:S(2)}, u32[]{:S(2)}) collective-permute-start(f32[2,2,16,1024]{3,2,1,0:T(8,128)S(1)} %bitcast_select_fusion.2), channel_id=1, source_target_pairs={{0,2},{1,5},{2,0},{3,7},{4,6},{5,1},{6,4},{7,3},{8,10},{9,13},{10,... | collective-permute-start | bytes 786440 | tf_op jit(solution)/shard_map/ppermute | solution.py:84
  95.7 0.5 collective-permute-done.12
  96.3 1.1 add.192
  97.4 1.4 %collective-permute-start.13 = (f32[2,2,16,1024]{3,2,1,0:T(8,128)S(1)}, f32[2,2,16,1024]{3,2,1,0:T(8,128)S(1)}, u32[]{:S(2)}, u32[]{:S(2)}) collective-permute-start(f32[2,2,16,1024]{3,2,1,0:T(8,128)S(1)} %bitcast_select_fusion.6), channel_id=1, source_target_pairs={{0,2},{1,5},{2,0},{3,7},{4,6},{5,1},{6,4},{7,3},{8,10},{9,13},{10,... | collective-permute-start | bytes 786440 | tf_op jit(solution)/shard_map/ppermute | solution.py:84
  98.9 1.9 %collective-permute-done.29 = f32[2,2,16,1024]{3,2,1,0:T(8,128)S(1)} collective-permute-done((f32[2,2,16,1024]{3,2,1,0:T(8,128)S(1)}, f32[2,2,16,1024]{3,2,1,0:T(8,128)S(1)}, u32[]{:S(2)}, u32[]{:S(2)}) %collective-permute-start.29) | collective-permute-done | bytes 262176 | tf_op jit(solution)/shard_map/ppermute | solution.py:84
  100.8 1.9 %collective-permute-start.30 = (f32[2,16,1024]{2,1,0:T(8,128)S(1)}, f32[2,16,1024]{2,1,0:T(8,128)S(1)}, u32[]{:S(2)}, u32[]{:S(2)}) collective-permute-start(f32[2,16,1024]{2,1,0:T(8,128)S(1)} %dynamic-slice_bitcast_fusion), channel_id=1, source_target_pairs={{0,4},{1,3},{2,6},{3,1},{4,0},{5,7},{6,2},{7,5},{8,12},{9,11},{10,... | collective-permute-start | bytes 393224 | tf_op jit(solution)/shard_map/ppermute | solution.py:84
  102.7 1.9 %collective-permute-done.13 = f32[2,2,16,1024]{3,2,1,0:T(8,128)S(1)} collective-permute-done((f32[2,2,16,1024]{3,2,1,0:T(8,128)S(1)}, f32[2,2,16,1024]{3,2,1,0:T(8,128)S(1)}, u32[]{:S(2)}, u32[]{:S(2)}) %collective-permute-start.13) | collective-permute-done | bytes 262176 | tf_op jit(solution)/shard_map/ppermute | solution.py:84
  104.6 1.9 %collective-permute-start.14 = (f32[2,16,1024]{2,1,0:T(8,128)S(1)}, f32[2,16,1024]{2,1,0:T(8,128)S(1)}, u32[]{:S(2)}, u32[]{:S(2)}) collective-permute-start(f32[2,16,1024]{2,1,0:T(8,128)S(1)} %dynamic-slice_bitcast_fusion.2), channel_id=1, source_target_pairs={{0,4},{1,3},{2,6},{3,1},{4,0},{5,7},{6,2},{7,5},{8,12},{9,11},{10,... | collective-permute-start | bytes 393224 | tf_op jit(solution)/shard_map/ppermute | solution.py:84
  106.6 2.0 %collective-permute-start.31 = (f32[16,1024]{1,0:T(8,128)S(1)}, f32[16,1024]{1,0:T(8,128)S(1)}, u32[]{:S(2)}, u32[]{:S(2)}) collective-permute-start(f32[16,1024]{1,0:T(8,128)S(1)} %dynamic-slice_bitcast_fusion.4), channel_id=1, source_target_pairs={{0,8},{1,9},{2,10},{3,11},{4,12},{5,13},{6,14},{7,15},{8,0},{9,1},... | collective-permute-start | bytes 196616 | tf_op jit(solution)/shard_map/ppermute | solution.py:84
  108.5 1.8 %collective-permute-done.14 = f32[2,16,1024]{2,1,0:T(8,128)S(1)} collective-permute-done((f32[2,16,1024]{2,1,0:T(8,128)S(1)}, f32[2,16,1024]{2,1,0:T(8,128)S(1)}, u32[]{:S(2)}, u32[]{:S(2)}) %collective-permute-start.14) | collective-permute-done | bytes 131104 | tf_op jit(solution)/shard_map/ppermute | solution.py:84
  110.4 1.7 %collective-permute-start.15 = (f32[16,1024]{1,0:T(8,128)S(1)}, f32[16,1024]{1,0:T(8,128)S(1)}, u32[]{:S(2)}, u32[]{:S(2)}) collective-permute-start(f32[16,1024]{1,0:T(8,128)S(1)} %dynamic-slice_bitcast_fusion.6), channel_id=1, source_target_pairs={{0,8},{1,9},{2,10},{3,11},{4,12},{5,13},{6,14},{7,15},{8,0},{9,1},... | collective-permute-start | bytes 196616 | tf_op jit(solution)/shard_map/ppermute | solution.py:84
  112.1 1.9 %collective-permute-done.31 = f32[16,1024]{1,0:T(8,128)S(1)} collective-permute-done((f32[16,1024]{1,0:T(8,128)S(1)}, f32[16,1024]{1,0:T(8,128)S(1)}, u32[]{:S(2)}, u32[]{:S(2)}) %collective-permute-start.31) | collective-permute-done | bytes 65568 | tf_op jit(solution)/shard_map/ppermute | solution.py:84
  114.0 1.6 %collective-permute-done.15 = f32[16,1024]{1,0:T(8,128)S(1)} collective-permute-done((f32[16,1024]{1,0:T(8,128)S(1)}, f32[16,1024]{1,0:T(8,128)S(1)}, u32[]{:S(2)}, u32[]{:S(2)}) %collective-permute-start.15) | collective-permute-done | bytes 65568 | tf_op jit(solution)/shard_map/ppermute | solution.py:84
  115.7 0.8 copy.64
  (90 shorter events, 1.9 us)
Async XLA Ops:
  2.6 7.6 %collective-permute-start.16 = (bf16[1,16,1024]{2,1,0:T(8,128)(2,1)S(1)}, bf16[1,16,1024]{2,1,0:T(8,128)(2,1)S(1)}, u32[]{:S(2)}, u32[]{:S(2)}) collective-permute-start(bf16[1,16,1024]{2,1,0:T(8,128)(2,1)S(1)} %get-tuple-element.56), channel_id=1, source_target_pairs={{0,8},{1,9},{2,10},{3,11},{4,12},{5,13},{6,14},{7,15},{8,0},{9,1},... | collective-permute-start | bytes 98312 | tf_op jit(solution)/shard_map/ppermute | solution.py:36
  6.7 5.4 %collective-permute-start = (bf16[1,16,1024]{2,1,0:T(8,128)(2,1)S(1)}, bf16[1,16,1024]{2,1,0:T(8,128)(2,1)S(1)}, u32[]{:S(2)}, u32[]{:S(2)}) collective-permute-start(bf16[1,16,1024]{2,1,0:T(8,128)(2,1)S(1)} %get-tuple-element.55), channel_id=1, source_target_pairs={{0,8},{1,9},{2,10},{3,11},{4,12},{5,13},{6,14},{7,15},{8,0},{9,1},... | collective-permute-start | bytes 98312 | tf_op jit(solution)/shard_map/ppermute | solution.py:36
  10.2 4.3 %collective-permute-start.17 = (bf16[2,16,1024]{2,1,0:T(8,128)(2,1)S(1)}, bf16[2,16,1024]{2,1,0:T(8,128)(2,1)S(1)}, u32[]{:S(2)}, u32[]{:S(2)}) collective-permute-start(bf16[2,16,1024]{2,1,0:T(8,128)(2,1)S(1)} %pad_maximum_fusion.8), channel_id=1, source_target_pairs={{0,4},{1,3},{2,6},{3,1},{4,0},{5,7},{6,2},{7,5},{8,12},{9,11},{10,... | collective-permute-start | bytes 196616 | tf_op jit(solution)/shard_map/ppermute | solution.py:36
  12.2 5.0 %collective-permute-start.1 = (bf16[2,16,1024]{2,1,0:T(8,128)(2,1)S(1)}, bf16[2,16,1024]{2,1,0:T(8,128)(2,1)S(1)}, u32[]{:S(2)}, u32[]{:S(2)}) collective-permute-start(bf16[2,16,1024]{2,1,0:T(8,128)(2,1)S(1)} %pad_maximum_fusion.6), channel_id=1, source_target_pairs={{0,4},{1,3},{2,6},{3,1},{4,0},{5,7},{6,2},{7,5},{8,12},{9,11},{10,... | collective-permute-start | bytes 196616 | tf_op jit(solution)/shard_map/ppermute | solution.py:36
  14.6 5.0 %collective-permute-start.18 = (bf16[4,16,1024]{2,1,0:T(8,128)(2,1)S(1)}, bf16[4,16,1024]{2,1,0:T(8,128)(2,1)S(1)}, u32[]{:S(2)}, u32[]{:S(2)}) collective-permute-start(bf16[4,16,1024]{2,1,0:T(8,128)(2,1)S(1)} %bitcast.264), channel_id=1, source_target_pairs={{0,2},{1,5},{2,0},{3,7},{4,6},{5,1},{6,4},{7,3},{8,10},{9,13},{10,... | collective-permute-start | bytes 393224 | tf_op jit(solution)/shard_map/ppermute | solution.py:36
  17.2 5.0 %collective-permute-start.2 = (bf16[4,16,1024]{2,1,0:T(8,128)(2,1)S(1)}, bf16[4,16,1024]{2,1,0:T(8,128)(2,1)S(1)}, u32[]{:S(2)}, u32[]{:S(2)}) collective-permute-start(bf16[4,16,1024]{2,1,0:T(8,128)(2,1)S(1)} %bitcast.265), channel_id=1, source_target_pairs={{0,2},{1,5},{2,0},{3,7},{4,6},{5,1},{6,4},{7,3},{8,10},{9,13},{10,... | collective-permute-start | bytes 393224 | tf_op jit(solution)/shard_map/ppermute | solution.py:36
  19.7 2.7 %copy-start.1 = (bf16[2,2,2,16,1024]{4,3,2,1,0:T(8,128)(2,1)}, bf16[2,2,2,16,1024]{4,3,2,1,0:T(8,128)(2,1)S(1)}, u32[]{:S(2)}) copy-start(bf16[2,2,2,16,1024]{4,3,2,1,0:T(8,128)(2,1)S(1)} %maximum_select_fusion.2) | copy-start | bytes 786436
  19.8 2.7 %collective-permute-start.19 = (bf16[128,1024]{1,0:T(8,128)(2,1)S(1)}, bf16[128,1024]{1,0:T(8,128)(2,1)S(1)}, u32[]{:S(2)}, u32[]{:S(2)}) collective-permute-start(bf16[128,1024]{1,0:T(8,128)(2,1)S(1)} %bitcast.257), channel_id=1, source_target_pairs={{0,1},{1,0},{2,3},{3,2},{4,5},{5,4},{6,7},{7,6},{8,9},{9,8},{10,11... | collective-permute-start | bytes 786440 | tf_op jit(solution)/shard_map/ppermute | solution.py:53
  22.4 8.5 %copy-start.3 = (bf16[2,2,2,16,1024]{4,3,2,1,0:T(8,128)(2,1)}, bf16[2,2,2,16,1024]{4,3,2,1,0:T(8,128)(2,1)S(1)}, u32[]{:S(2)}) copy-start(bf16[2,2,2,16,1024]{4,3,2,1,0:T(8,128)(2,1)S(1)} %maximum_select_fusion) | copy-start | bytes 786436
  22.4 8.5 %collective-permute-start.3 = (bf16[128,1024]{1,0:T(8,128)(2,1)S(1)}, bf16[128,1024]{1,0:T(8,128)(2,1)S(1)}, u32[]{:S(2)}, u32[]{:S(2)}) collective-permute-start(bf16[128,1024]{1,0:T(8,128)(2,1)S(1)} %bitcast.261), channel_id=1, source_target_pairs={{0,1},{1,0},{2,3},{3,2},{4,5},{5,4},{6,7},{7,6},{8,9},{9,8},{10,11... | collective-permute-start | bytes 786440 | tf_op jit(solution)/shard_map/ppermute | solution.py:53
  22.4 0.7 copy-start.7
  30.3 8.5 %copy-start.4 = (f32[128,1024]{1,0:T(8,128)S(1)}, f32[128,1024]{1,0:T(8,128)}, u32[]{:S(2)}) copy-start(f32[128,1024]{1,0:T(8,128)} %get-tuple-element.17) | copy-start | bytes 1572868
  30.3 30.3 %copy-start.10 = (f32[1024]{0:T(1024)S(1)}, f32[1024]{0:T(1024)}, u32[]{:S(2)}) copy-start(f32[1024]{0:T(1024)} %param.7) | copy-start | bytes 12292
  30.3 8.5 %collective-permute-start.20 = (f32[128,1024]{1,0:T(8,128)}, f32[128,1024]{1,0:T(8,128)S(1)}, u32[]{:S(2)}, u32[]{:S(2)}) collective-permute-start(f32[128,1024]{1,0:T(8,128)} %get-tuple-element.18), channel_id=1, source_target_pairs={{0,1},{1,0},{2,3},{3,2},{4,5},{5,4},{6,7},{7,6},{8,9},{9,8},{10,11... | collective-permute-start | bytes 1572872 | tf_op jit(solution)/shard_map/ppermute | solution.py:63
  30.9 0.7 copy-start.9
  38.8 2.1 %collective-permute-start.4 = (f32[128,1024]{1,0:T(8,128)}, f32[128,1024]{1,0:T(8,128)S(1)}, u32[]{:S(2)}, u32[]{:S(2)}) collective-permute-start(f32[128,1024]{1,0:T(8,128)} %get-tuple-element.14), channel_id=1, source_target_pairs={{0,1},{1,0},{2,3},{3,2},{4,5},{5,4},{6,7},{7,6},{8,9},{9,8},{10,11... | collective-permute-start | bytes 1572872 | tf_op jit(solution)/shard_map/ppermute | solution.py:63
  38.9 6.4 %collective-permute-start.21 = (f32[2,2,16,1024]{3,2,1,0:T(8,128)S(1)}, f32[2,2,16,1024]{3,2,1,0:T(8,128)S(1)}, u32[]{:S(2)}, u32[]{:S(2)}) collective-permute-start(f32[2,2,16,1024]{3,2,1,0:T(8,128)S(1)} %bitcast_select_fusion.4), channel_id=1, source_target_pairs={{0,2},{1,5},{2,0},{3,7},{4,6},{5,1},{6,4},{7,3},{8,10},{9,13},{10,... | collective-permute-start | bytes 786440 | tf_op jit(solution)/shard_map/ppermute | solution.py:84
  42.1 7.1 %collective-permute-start.5 = (f32[2,2,16,1024]{3,2,1,0:T(8,128)S(1)}, f32[2,2,16,1024]{3,2,1,0:T(8,128)S(1)}, u32[]{:S(2)}, u32[]{:S(2)}) collective-permute-start(f32[2,2,16,1024]{3,2,1,0:T(8,128)S(1)} %bitcast_select_fusion.8), channel_id=1, source_target_pairs={{0,2},{1,5},{2,0},{3,7},{4,6},{5,1},{6,4},{7,3},{8,10},{9,13},{10,... | collective-permute-start | bytes 786440 | tf_op jit(solution)/shard_map/ppermute | solution.py:84
  45.4 5.0 %collective-permute-start.22 = (f32[2,16,1024]{2,1,0:T(8,128)S(1)}, f32[2,16,1024]{2,1,0:T(8,128)S(1)}, u32[]{:S(2)}, u32[]{:S(2)}) collective-permute-start(f32[2,16,1024]{2,1,0:T(8,128)S(1)} %dynamic-slice_bitcast_fusion.1), channel_id=1, source_target_pairs={{0,4},{1,3},{2,6},{3,1},{4,0},{5,7},{6,2},{7,5},{8,12},{9,11},{10,... | collective-permute-start | bytes 393224 | tf_op jit(solution)/shard_map/ppermute | solution.py:84
  49.3 5.4 %collective-permute-start.6 = (f32[2,16,1024]{2,1,0:T(8,128)S(1)}, f32[2,16,1024]{2,1,0:T(8,128)S(1)}, u32[]{:S(2)}, u32[]{:S(2)}) collective-permute-start(f32[2,16,1024]{2,1,0:T(8,128)S(1)} %dynamic-slice_bitcast_fusion.3), channel_id=1, source_target_pairs={{0,4},{1,3},{2,6},{3,1},{4,0},{5,7},{6,2},{7,5},{8,12},{9,11},{10,... | collective-permute-start | bytes 393224 | tf_op jit(solution)/shard_map/ppermute | solution.py:84
  50.5 6.5 %collective-permute-start.23 = (f32[16,1024]{1,0:T(8,128)S(1)}, f32[16,1024]{1,0:T(8,128)S(1)}, u32[]{:S(2)}, u32[]{:S(2)}) collective-permute-start(f32[16,1024]{1,0:T(8,128)S(1)} %dynamic-slice_bitcast_fusion.5), channel_id=1, source_target_pairs={{0,8},{1,9},{2,10},{3,11},{4,12},{5,13},{6,14},{7,15},{8,0},{9,1},... | collective-permute-start | bytes 196616 | tf_op jit(solution)/shard_map/ppermute | solution.py:84
  54.7 5.9 %collective-permute-start.7 = (f32[16,1024]{1,0:T(8,128)S(1)}, f32[16,1024]{1,0:T(8,128)S(1)}, u32[]{:S(2)}, u32[]{:S(2)}) collective-permute-start(f32[16,1024]{1,0:T(8,128)S(1)} %dynamic-slice_bitcast_fusion.7), channel_id=1, source_target_pairs={{0,8},{1,9},{2,10},{3,11},{4,12},{5,13},{6,14},{7,15},{8,0},{9,1},... | collective-permute-start | bytes 196616 | tf_op jit(solution)/shard_map/ppermute | solution.py:84
  60.7 4.9 %collective-permute-start.24 = (bf16[1,16,1024]{2,1,0:T(8,128)(2,1)S(1)}, bf16[1,16,1024]{2,1,0:T(8,128)(2,1)S(1)}, u32[]{:S(2)}, u32[]{:S(2)}) collective-permute-start(bf16[1,16,1024]{2,1,0:T(8,128)(2,1)S(1)} %get-tuple-element.53), channel_id=1, source_target_pairs={{0,8},{1,9},{2,10},{3,11},{4,12},{5,13},{6,14},{7,15},{8,0},{9,1},... | collective-permute-start | bytes 98312 | tf_op jit(solution)/shard_map/ppermute | solution.py:36
  62.4 4.8 %collective-permute-start.8 = (bf16[1,16,1024]{2,1,0:T(8,128)(2,1)S(1)}, bf16[1,16,1024]{2,1,0:T(8,128)(2,1)S(1)}, u32[]{:S(2)}, u32[]{:S(2)}) collective-permute-start(bf16[1,16,1024]{2,1,0:T(8,128)(2,1)S(1)} %get-tuple-element.21), channel_id=1, source_target_pairs={{0,8},{1,9},{2,10},{3,11},{4,12},{5,13},{6,14},{7,15},{8,0},{9,1},... | collective-permute-start | bytes 98312 | tf_op jit(solution)/shard_map/ppermute | solution.py:36
  65.7 5.0 %collective-permute-start.25 = (bf16[2,16,1024]{2,1,0:T(8,128)(2,1)S(1)}, bf16[2,16,1024]{2,1,0:T(8,128)(2,1)S(1)}, u32[]{:S(2)}, u32[]{:S(2)}) collective-permute-start(bf16[2,16,1024]{2,1,0:T(8,128)(2,1)S(1)} %pad_maximum_fusion.9), channel_id=1, source_target_pairs={{0,4},{1,3},{2,6},{3,1},{4,0},{5,7},{6,2},{7,5},{8,12},{9,11},{10,... | collective-permute-start | bytes 196616 | tf_op jit(solution)/shard_map/ppermute | solution.py:36
  67.3 5.3 %collective-permute-start.9 = (bf16[2,16,1024]{2,1,0:T(8,128)(2,1)S(1)}, bf16[2,16,1024]{2,1,0:T(8,128)(2,1)S(1)}, u32[]{:S(2)}, u32[]{:S(2)}) collective-permute-start(bf16[2,16,1024]{2,1,0:T(8,128)(2,1)S(1)} %pad_maximum_fusion.7), channel_id=1, source_target_pairs={{0,4},{1,3},{2,6},{3,1},{4,0},{5,7},{6,2},{7,5},{8,12},{9,11},{10,... | collective-permute-start | bytes 196616 | tf_op jit(solution)/shard_map/ppermute | solution.py:36
  70.7 5.0 %collective-permute-start.26 = (bf16[4,16,1024]{2,1,0:T(8,128)(2,1)S(1)}, bf16[4,16,1024]{2,1,0:T(8,128)(2,1)S(1)}, u32[]{:S(2)}, u32[]{:S(2)}) collective-permute-start(bf16[4,16,1024]{2,1,0:T(8,128)(2,1)S(1)} %bitcast.263), channel_id=1, source_target_pairs={{0,2},{1,5},{2,0},{3,7},{4,6},{5,1},{6,4},{7,3},{8,10},{9,13},{10,... | collective-permute-start | bytes 393224 | tf_op jit(solution)/shard_map/ppermute | solution.py:36
  72.6 5.0 %collective-permute-start.10 = (bf16[4,16,1024]{2,1,0:T(8,128)(2,1)S(1)}, bf16[4,16,1024]{2,1,0:T(8,128)(2,1)S(1)}, u32[]{:S(2)}, u32[]{:S(2)}) collective-permute-start(bf16[4,16,1024]{2,1,0:T(8,128)(2,1)S(1)} %bitcast.266), channel_id=1, source_target_pairs={{0,2},{1,5},{2,0},{3,7},{4,6},{5,1},{6,4},{7,3},{8,10},{9,13},{10,... | collective-permute-start | bytes 393224 | tf_op jit(solution)/shard_map/ppermute | solution.py:36
  75.8 2.0 %copy-start = (bf16[2,2,2,16,1024]{4,3,2,1,0:T(8,128)(2,1)}, bf16[2,2,2,16,1024]{4,3,2,1,0:T(8,128)(2,1)S(1)}, u32[]{:S(2)}) copy-start(bf16[2,2,2,16,1024]{4,3,2,1,0:T(8,128)(2,1)S(1)} %maximum_select_fusion.3) | copy-start | bytes 786436
  75.9 2.0 %collective-permute-start.27 = (bf16[128,1024]{1,0:T(8,128)(2,1)S(1)}, bf16[128,1024]{1,0:T(8,128)(2,1)S(1)}, u32[]{:S(2)}, u32[]{:S(2)}) collective-permute-start(bf16[128,1024]{1,0:T(8,128)(2,1)S(1)} %bitcast.255), channel_id=1, source_target_pairs={{0,1},{1,0},{2,3},{3,2},{4,5},{5,4},{6,7},{7,6},{8,9},{9,8},{10,11... | collective-permute-start | bytes 786440 | tf_op jit(solution)/shard_map/ppermute | solution.py:53
  77.8 8.5 %copy-start.2 = (bf16[2,2,2,16,1024]{4,3,2,1,0:T(8,128)(2,1)}, bf16[2,2,2,16,1024]{4,3,2,1,0:T(8,128)(2,1)S(1)}, u32[]{:S(2)}) copy-start(bf16[2,2,2,16,1024]{4,3,2,1,0:T(8,128)(2,1)S(1)} %maximum_select_fusion.1) | copy-start | bytes 786436
  77.8 8.5 %collective-permute-start.11 = (bf16[128,1024]{1,0:T(8,128)(2,1)S(1)}, bf16[128,1024]{1,0:T(8,128)(2,1)S(1)}, u32[]{:S(2)}, u32[]{:S(2)}) collective-permute-start(bf16[128,1024]{1,0:T(8,128)(2,1)S(1)} %bitcast.259), channel_id=1, source_target_pairs={{0,1},{1,0},{2,3},{3,2},{4,5},{5,4},{6,7},{7,6},{8,9},{9,8},{10,11... | collective-permute-start | bytes 786440 | tf_op jit(solution)/shard_map/ppermute | solution.py:53
  77.9 0.7 copy-start.6
  85.7 8.4 %copy-start.5 = (f32[128,1024]{1,0:T(8,128)S(1)}, f32[128,1024]{1,0:T(8,128)}, u32[]{:S(2)}) copy-start(f32[128,1024]{1,0:T(8,128)} %get-tuple-element.19) | copy-start | bytes 1572868
  85.7 8.4 %collective-permute-start.28 = (f32[128,1024]{1,0:T(8,128)}, f32[128,1024]{1,0:T(8,128)S(1)}, u32[]{:S(2)}, u32[]{:S(2)}) collective-permute-start(f32[128,1024]{1,0:T(8,128)} %get-tuple-element.20), channel_id=1, source_target_pairs={{0,1},{1,0},{2,3},{3,2},{4,5},{5,4},{6,7},{7,6},{8,9},{9,8},{10,11... | collective-permute-start | bytes 1572872 | tf_op jit(solution)/shard_map/ppermute | solution.py:63
  86.2 0.7 copy-start.8
  94.1 2.1 %collective-permute-start.12 = (f32[128,1024]{1,0:T(8,128)}, f32[128,1024]{1,0:T(8,128)S(1)}, u32[]{:S(2)}, u32[]{:S(2)}) collective-permute-start(f32[128,1024]{1,0:T(8,128)} %get-tuple-element.16), channel_id=1, source_target_pairs={{0,1},{1,0},{2,3},{3,2},{4,5},{5,4},{6,7},{7,6},{8,9},{9,8},{10,11... | collective-permute-start | bytes 1572872 | tf_op jit(solution)/shard_map/ppermute | solution.py:63
  94.3 6.4 %collective-permute-start.29 = (f32[2,2,16,1024]{3,2,1,0:T(8,128)S(1)}, f32[2,2,16,1024]{3,2,1,0:T(8,128)S(1)}, u32[]{:S(2)}, u32[]{:S(2)}) collective-permute-start(f32[2,2,16,1024]{3,2,1,0:T(8,128)S(1)} %bitcast_select_fusion.2), channel_id=1, source_target_pairs={{0,2},{1,5},{2,0},{3,7},{4,6},{5,1},{6,4},{7,3},{8,10},{9,13},{10,... | collective-permute-start | bytes 786440 | tf_op jit(solution)/shard_map/ppermute | solution.py:84
  97.4 7.1 %collective-permute-start.13 = (f32[2,2,16,1024]{3,2,1,0:T(8,128)S(1)}, f32[2,2,16,1024]{3,2,1,0:T(8,128)S(1)}, u32[]{:S(2)}, u32[]{:S(2)}) collective-permute-start(f32[2,2,16,1024]{3,2,1,0:T(8,128)S(1)} %bitcast_select_fusion.6), channel_id=1, source_target_pairs={{0,2},{1,5},{2,0},{3,7},{4,6},{5,1},{6,4},{7,3},{8,10},{9,13},{10,... | collective-permute-start | bytes 786440 | tf_op jit(solution)/shard_map/ppermute | solution.py:84
  100.8 5.7 %collective-permute-start.30 = (f32[2,16,1024]{2,1,0:T(8,128)S(1)}, f32[2,16,1024]{2,1,0:T(8,128)S(1)}, u32[]{:S(2)}, u32[]{:S(2)}) collective-permute-start(f32[2,16,1024]{2,1,0:T(8,128)S(1)} %dynamic-slice_bitcast_fusion), channel_id=1, source_target_pairs={{0,4},{1,3},{2,6},{3,1},{4,0},{5,7},{6,2},{7,5},{8,12},{9,11},{10,... | collective-permute-start | bytes 393224 | tf_op jit(solution)/shard_map/ppermute | solution.py:84
  104.6 5.7 %collective-permute-start.14 = (f32[2,16,1024]{2,1,0:T(8,128)S(1)}, f32[2,16,1024]{2,1,0:T(8,128)S(1)}, u32[]{:S(2)}, u32[]{:S(2)}) collective-permute-start(f32[2,16,1024]{2,1,0:T(8,128)S(1)} %dynamic-slice_bitcast_fusion.2), channel_id=1, source_target_pairs={{0,4},{1,3},{2,6},{3,1},{4,0},{5,7},{6,2},{7,5},{8,12},{9,11},{10,... | collective-permute-start | bytes 393224 | tf_op jit(solution)/shard_map/ppermute | solution.py:84
  106.6 7.4 %collective-permute-start.31 = (f32[16,1024]{1,0:T(8,128)S(1)}, f32[16,1024]{1,0:T(8,128)S(1)}, u32[]{:S(2)}, u32[]{:S(2)}) collective-permute-start(f32[16,1024]{1,0:T(8,128)S(1)} %dynamic-slice_bitcast_fusion.4), channel_id=1, source_target_pairs={{0,8},{1,9},{2,10},{3,11},{4,12},{5,13},{6,14},{7,15},{8,0},{9,1},... | collective-permute-start | bytes 196616 | tf_op jit(solution)/shard_map/ppermute | solution.py:84
  110.4 5.2 %collective-permute-start.15 = (f32[16,1024]{1,0:T(8,128)S(1)}, f32[16,1024]{1,0:T(8,128)S(1)}, u32[]{:S(2)}, u32[]{:S(2)}) collective-permute-start(f32[16,1024]{1,0:T(8,128)S(1)} %dynamic-slice_bitcast_fusion.6), channel_id=1, source_target_pairs={{0,8},{1,9},{2,10},{3,11},{4,12},{5,13},{6,14},{7,15},{8,0},{9,1},... | collective-permute-start | bytes 196616 | tf_op jit(solution)/shard_map/ppermute | solution.py:84

commit v9 on v8

--- a/solution.py
+++ b/solution.py
@@ -8,6 +8,7 @@
 from jax.sharding import PartitionSpec as P
 
 ITERS = 2
+PIECES = 2
 
 
 def bit_orders(m, descending):
@@ -87,50 +88,49 @@
     return acc
 
 
-def exchange_kernel(states, occ_ref, mine_ref, theirs_ref, vir_ref, keep_ref, send_ref, r_ref):
+def exchange_kernel(states, pieces, occ_ref, *refs):
+    mine, theirs = refs[:pieces], refs[pieces:2 * pieces]
+    vir_ref = refs[2 * pieces]
+    keep, send = refs[2 * pieces + 1:3 * pieces + 1], refs[3 * pieces + 1:4 * pieces + 1]
+    r_ref = refs[4 * pieces + 1]
+    split = mine[0].shape[0]
+    width = mine[0].shape[1]
+
     @pl.when(pl.program_id(0) == 0)
     def _():
-        keep_ref[...] = jnp.zeros_like(keep_ref)
-        send_ref[...] = jnp.zeros_like(send_ref)
-        split = mine_ref.shape[0]
-        r_ref[:split] = mine_ref[...]
-        r_ref[split:] = theirs_ref[...]
+        for q in range(pieces):
+            keep[q][...] = jnp.zeros_like(keep[q])
+            send[q][...] = jnp.zeros_like(send[q])
+            r_ref[:split, q * width:(q + 1) * width] = mine[q][...]
+            r_ref[split:, q * width:(q + 1) * width] = theirs[q][...]
 
     half = jnp.dot(occ_ref[0], r_ref[...], preferred_element_type=jnp.float32).astype(jnp.bfloat16)
-    nvir = vir_ref.shape[1]
-    split = keep_ref.shape[0]
     vir = vir_ref[0]
-    for s in range(states):
-        cols = slice(s * nvir, (s + 1) * nvir)
-        term = lax.dot_general(
-            half[:, cols], vir, (((1,), (1,)), ((), ())), preferred_element_type=jnp.float32
-        )
-        keep_ref[:, cols] += term[:split]
-        send_ref[:, cols] += term[split:]
+    term = lax.dot_general(half, vir, (((1,), (1,)), ((), ())), preferred_element_type=jnp.float32)
+    for q in range(pieces):
+        keep[q][...] += term[:split, q * width:(q + 1) * width]
+        send[q][...] += term[split:, q * width:(q + 1) * width]
 
 
-def exchange_part(occ_ints, mine, theirs, vir_ints, states):
+def exchange_part(occ_ints, mine, theirs, vir_ints):
     local_aux, nocc, _ = occ_ints.shape
     nvir = vir_ints.shape[1]
-    width = states * nvir
+    pieces = len(mine)
+    width = nvir // pieces
+    piece = pl.BlockSpec((nocc // 2, width), lambda p: (0, 0))
     out = jax.ShapeDtypeStruct((nocc // 2, width), jnp.float32)
-    return pl.pallas_call(
-        functools.partial(exchange_kernel, states),
+    results = pl.pallas_call(
+        functools.partial(exchange_kernel, 1, pieces),
         grid=(local_aux,),
-        in_specs=[
-            pl.BlockSpec((1, nocc, nocc), lambda p: (p, 0, 0)),
-            pl.BlockSpec((nocc // 2, width), lambda p: (0, 0)),
-            pl.BlockSpec((nocc // 2, width), lambda p: (0, 0)),
-            pl.BlockSpec((1, nvir, nvir), lambda p: (p, 0, 0)),
-        ],
-        out_specs=[
-            pl.BlockSpec((nocc // 2, width), lambda p: (0, 0)),
-            pl.BlockSpec((nocc // 2, width), lambda p: (0, 0)),
-        ],
-        out_shape=[out, out],
-        scratch_shapes=[pltpu.VMEM((nocc, width), jnp.bfloat16)],
+        in_specs=[pl.BlockSpec((1, nocc, nocc), lambda p: (p, 0, 0))]
+        + [piece] * (2 * pieces)
+        + [pl.BlockSpec((1, nvir, nvir), lambda p: (p, 0, 0))],
+        out_specs=[piece] * (2 * pieces),
+        out_shape=[out] * (2 * pieces),
+        scratch_shapes=[pltpu.VMEM((nocc, nvir), jnp.bfloat16)],
         compiler_params=pltpu.CompilerParams(dimension_semantics=("arbitrary",)),
-    )(occ_ints, mine, theirs, vir_ints)
+    )(occ_ints, *mine, *theirs, vir_ints)
+    return results[:pieces], results[pieces:]
 
 
 def order_columns(occ_ints, n, core):
@@ -172,9 +172,10 @@
         resp = own_rhs / own_denom
         for step in range(ITERS):
             rounded = resp.astype(jnp.bfloat16)
-            mine, theirs = gather_rows(rounded, n)
-            keep, send = exchange_part(ordered_occ, mine, theirs, vir_ints, 1)
-            exchange = scatter_sum(keep, send, n)
+            width = nvir // PIECES
+            got = [gather_rows(rounded[:, q * width:(q + 1) * width], n) for q in range(PIECES)]
+            keep, send = exchange_part(ordered_occ, [g[0] for g in got], [g[1] for g in got], vir_ints)
+            exchange = jnp.concatenate([scatter_sum(k, t, n) for k, t in zip(keep, send)], axis=1)
             resp = 0.4 * resp + 0.6 * (own_rhs - exchange) / own_denom
         finals.append(resp)
     response = jnp.stack(finals, axis=1)

time: 117 us -> 131 us (1.12)
  starting transfers between devices: 41.9 us -> 64 us
  waiting for transfers between devices: 32.2 us -> 21.4 us
  other arithmetic: 6.4 us -> 8.46 us
    ppermute x12 -> x24, starting transfers between devices: 20.4 us -> 31.2 us  [gather_rows(): theirs = lax.ppermute(acc, 'aux', partners(n, b0, b1))]
    ppermute x12 -> x24, starting transfers between devices: 20.1 us -> 29.8 us  [scatter_sum(): acc = kept + lax.ppermute(sent, 'aux', partners(n, b0, b1))]
    ppermute x12 -> x24, waiting for transfers between devices: 19.1 us -> 12.2 us  [scatter_sum(): acc = kept + lax.ppermute(sent, 'aux', partners(n, b0, b1))]
    ppermute x12 -> x24, waiting for transfers between devices: 12.1 us -> 7.05 us  [gather_rows(): theirs = lax.ppermute(acc, 'aux', partners(n, b0, b1))]
    ppermute x4 -> x8, waiting for transfers between devices: 0.01 us -> 2.05 us  [gather_rows(): return (flat, lax.ppermute(flat, 'aux', partners(n, 0, 0)))]
    add x4 -> x8, other arithmetic: 2.34 us -> 4.1 us  [scatter_sum(): keep.reshape(shape)]
    ppermute x4 -> x8, starting transfers between devices: 0.28 us -> 1.65 us  [gather_rows(): return (flat, lax.ppermute(flat, 'aux', partners(n, 0, 0)))]
    unnamed x22 -> x42, local copies, waits for them, and re-layouts: 2.89 us -> 3.31 us
  transfers between devices with their start and end apart: 32 -> 64, of which waited for: 22 -> 19; matrix products, arithmetic and copies ran while one was open for 6% -> 7% of each run, Pallas kernels for 25% -> 22%
where the time goes in v9:
time: 131 us; the launch traced here: 130 us
  starting transfers between devices  64 us (49%)
  Pallas kernels  28.3 us (22%)
  waiting for transfers between devices  21.4 us (16%)
  other arithmetic  8.46 us (6%)
  local copies, waits for them, and re-layouts  6.22 us (5%)
    ppermute x24, starting transfers between devices, gather_rows(): theirs = lax.ppermute(acc, 'aux', partners(n, b0, b1))  31.2 us
    ppermute x24, starting transfers between devices, scatter_sum(): acc = kept + lax.ppermute(sent, 'aux', partners(n, b0, b1))  29.8 us
    pallas_call x4, Pallas kernels, exchange_part(): pl.pallas_call(functools.partial(exchange_kernel, 1, pieces), grid=(local...  28.3 us
    ppermute x24, waiting for transfers between devices, scatter_sum(): acc = kept + lax.ppermute(sent, 'aux', partners(n, b0, b1))  12.2 us
    ppermute x24, waiting for transfers between devices, gather_rows(): theirs = lax.ppermute(acc, 'aux', partners(n, b0, b1))  7.05 us
    add x8, other arithmetic, scatter_sum(): keep.reshape(shape)  4.1 us
    unnamed x42, local copies, waits for them, and re-layouts  3.31 us
  transfers between devices with their start and end apart: 64, of which 19 were waited for; matrix products, arithmetic and copies ran while one was open for 7% of the time, Pallas kernels for 22%

profile of v9, /device:TPU:0, one launch (start us, length us, event | category | flops | bytes accessed | tf_op | source)
XLA Modules:
  0.0 130.4 jit_solution(1757635330696467914)
XLA Ops:
  0.0 1.1 fusion.40
  1.1 0.8 dynamic_slice.199
  1.9 0.8 fusion.29
  2.6 4.1 %collective-permute-start.32 = (bf16[1,16,512]{2,1,0:T(8,128)(2,1)S(1)}, bf16[1,16,512]{2,1,0:T(8,128)(2,1)S(1)}, u32[]{:S(2)}, u32[]{:S(2)}) collective-permute-start(bf16[1,16,512]{2,1,0:T(8,128)(2,1)S(1)} %get-tuple-element.102), channel_id=1, source_target_pairs={{0,8},{1,9},{2,10},{3,11},{4,12},{5,13},{6,14},{7,15},{8,0},{9,1},... | collective-permute-start | bytes 49160 | tf_op jit(solution)/shard_map/ppermute | solution.py:37
  6.8 2.8 %collective-permute-start = (bf16[1,16,512]{2,1,0:T(8,128)(2,1)S(1)}, bf16[1,16,512]{2,1,0:T(8,128)(2,1)S(1)}, u32[]{:S(2)}, u32[]{:S(2)}) collective-permute-start(bf16[1,16,512]{2,1,0:T(8,128)(2,1)S(1)} %get-tuple-element.94), channel_id=1, source_target_pairs={{0,8},{1,9},{2,10},{3,11},{4,12},{5,13},{6,14},{7,15},{8,0},{9,1},... | collective-permute-start | bytes 49160 | tf_op jit(solution)/shard_map/ppermute | solution.py:37
  9.8 1.1 fusion
  10.8 1.1 fusion.1
  12.0 1.1 convolution_convert_fusion
  13.2 1.9 %collective-permute-start.36 = (bf16[2,16,512]{2,1,0:T(8,128)(2,1)S(1)}, bf16[2,16,512]{2,1,0:T(8,128)(2,1)S(1)}, u32[]{:S(2)}, u32[]{:S(2)}) collective-permute-start(bf16[2,16,512]{2,1,0:T(8,128)(2,1)S(1)} %pad_maximum_fusion.15), channel_id=1, source_target_pairs={{0,4},{1,3},{2,6},{3,1},{4,0},{5,7},{6,2},{7,5},{8,12},{9,11},{10,... | collective-permute-start | bytes 98312 | tf_op jit(solution)/shard_map/ppermute | solution.py:37
  15.3 1.9 %collective-permute-start.4 = (bf16[2,16,512]{2,1,0:T(8,128)(2,1)S(1)}, bf16[2,16,512]{2,1,0:T(8,128)(2,1)S(1)}, u32[]{:S(2)}, u32[]{:S(2)}) collective-permute-start(bf16[2,16,512]{2,1,0:T(8,128)(2,1)S(1)} %pad_maximum_fusion.11), channel_id=1, source_target_pairs={{0,4},{1,3},{2,6},{3,1},{4,0},{5,7},{6,2},{7,5},{8,12},{9,11},{10,... | collective-permute-start | bytes 98312 | tf_op jit(solution)/shard_map/ppermute | solution.py:37
  17.5 1.8 %collective-permute-start.37 = (bf16[4,16,512]{2,1,0:T(8,128)(2,1)S(1)}, bf16[4,16,512]{2,1,0:T(8,128)(2,1)S(1)}, u32[]{:S(2)}, u32[]{:S(2)}) collective-permute-start(bf16[4,16,512]{2,1,0:T(8,128)(2,1)S(1)} %bitcast.491), channel_id=1, source_target_pairs={{0,2},{1,5},{2,0},{3,7},{4,6},{5,1},{6,4},{7,3},{8,10},{9,13},{10,... | collective-permute-start | bytes 196616 | tf_op jit(solution)/shard_map/ppermute | solution.py:37
  19.3 1.3 %collective-permute-start.34 = (bf16[4,16,512]{2,1,0:T(8,128)(2,1)S(1)}, bf16[4,16,512]{2,1,0:T(8,128)(2,1)S(1)}, u32[]{:S(2)}, u32[]{:S(2)}) collective-permute-start(bf16[4,16,512]{2,1,0:T(8,128)(2,1)S(1)} %bitcast.493), channel_id=1, source_target_pairs={{0,2},{1,5},{2,0},{3,7},{4,6},{5,1},{6,4},{7,3},{8,10},{9,13},{10,... | collective-permute-start | bytes 196616 | tf_op jit(solution)/shard_map/ppermute | solution.py:37
  20.7 0.8 collective-permute-start.5
  21.6 1.6 %collective-permute-start.2 = (bf16[4,16,512]{2,1,0:T(8,128)(2,1)S(1)}, bf16[4,16,512]{2,1,0:T(8,128)(2,1)S(1)}, u32[]{:S(2)}, u32[]{:S(2)}) collective-permute-start(bf16[4,16,512]{2,1,0:T(8,128)(2,1)S(1)} %bitcast.495), channel_id=1, source_target_pairs={{0,2},{1,5},{2,0},{3,7},{4,6},{5,1},{6,4},{7,3},{8,10},{9,13},{10,... | collective-permute-start | bytes 196616 | tf_op jit(solution)/shard_map/ppermute | solution.py:37
  23.9 1.1 collective-permute-done.5
  25.2 0.7 collective-permute-done.2
  26.6 7.1 %shard_map.57 = (f32[128,512]{1,0:T(8,128)}, f32[128,512]{1,0:T(8,128)}, f32[128,512]{1,0:T(8,128)}, f32[128,512]{1,0:T(8,128)}) custom-call(bf16[4,256,256]{2,1,0:T(8,128)(2,1)} %bitcast.416, bf16[128,512]{1,0:T(8,128)(2,1)} %bitcast.482, bf16[128,512]{1,0:T(8,128)(2,1)} %bitcast.476, bf16[128,512]{1,0:T(8,128)(2,1)} %copy-done.17, ...), custom_call_target="tpu_custom_call" | custom-call | tf_op jit(solution)/shard_map/pallas_call | solution.py:122
  34.5 1.0 collective-permute-done.6.refs_2_
  36.2 7.1 %shard_map.55 = (f32[128,512]{1,0:T(8,128)}, f32[128,512]{1,0:T(8,128)}, f32[128,512]{1,0:T(8,128)}, f32[128,512]{1,0:T(8,128)}) custom-call(bf16[4,256,256]{2,1,0:T(8,128)(2,1)} %bitcast.417, bf16[128,512]{1,0:T(8,128)(2,1)} %bitcast.486, bf16[128,512]{1,0:T(8,128)(2,1)} %bitcast.478, bf16[128,512]{1,0:T(8,128)(2,1)} %copy-done.19, ...), custom_call_target="tpu_custom_call" | custom-call | tf_op jit(solution)/shard_map/pallas_call | solution.py:122
  43.9 1.6 %collective-permute-start.41 = (f32[2,2,16,512]{3,2,1,0:T(8,128)S(1)}, f32[2,2,16,512]{3,2,1,0:T(8,128)S(1)}, u32[]{:S(2)}, u32[]{:S(2)}) collective-permute-start(f32[2,2,16,512]{3,2,1,0:T(8,128)S(1)} %bitcast_select_fusion.8), channel_id=1, source_target_pairs={{0,2},{1,5},{2,0},{3,7},{4,6},{5,1},{6,4},{7,3},{8,10},{9,13},{10,... | collective-permute-start | bytes 393224 | tf_op jit(solution)/shard_map/ppermute | solution.py:85
  46.1 1.0 add.278
  47.1 1.6 %collective-permute-start.9 = (f32[2,2,16,512]{3,2,1,0:T(8,128)S(1)}, f32[2,2,16,512]{3,2,1,0:T(8,128)S(1)}, u32[]{:S(2)}, u32[]{:S(2)}) collective-permute-start(f32[2,2,16,512]{3,2,1,0:T(8,128)S(1)} %bitcast_select_fusion.16), channel_id=1, source_target_pairs={{0,2},{1,5},{2,0},{3,7},{4,6},{5,1},{6,4},{7,3},{8,10},{9,13},{10,... | collective-permute-start | bytes 393224 | tf_op jit(solution)/shard_map/ppermute | solution.py:85
  48.7 1.0 add.291
  50.4 1.6 %collective-permute-start.42 = (f32[2,16,512]{2,1,0:T(8,128)S(1)}, f32[2,16,512]{2,1,0:T(8,128)S(1)}, u32[]{:S(2)}, u32[]{:S(2)}) collective-permute-start(f32[2,16,512]{2,1,0:T(8,128)S(1)} %dynamic-slice_bitcast_fusion.3), channel_id=1, source_target_pairs={{0,4},{1,3},{2,6},{3,1},{4,0},{5,7},{6,2},{7,5},{8,12},{9,11},{10,... | collective-permute-start | bytes 196616 | tf_op jit(solution)/shard_map/ppermute | solution.py:85
  52.7 1.6 %collective-permute-start.10 = (f32[2,16,512]{2,1,0:T(8,128)S(1)}, f32[2,16,512]{2,1,0:T(8,128)S(1)}, u32[]{:S(2)}, u32[]{:S(2)}) collective-permute-start(f32[2,16,512]{2,1,0:T(8,128)S(1)} %dynamic-slice_bitcast_fusion.7), channel_id=1, source_target_pairs={{0,4},{1,3},{2,6},{3,1},{4,0},{5,7},{6,2},{7,5},{8,12},{9,11},{10,... | collective-permute-start | bytes 196616 | tf_op jit(solution)/shard_map/ppermute | solution.py:85
  54.3 1.7 %collective-permute-done.13 = f32[2,2,16,512]{3,2,1,0:T(8,128)S(1)} collective-permute-done((f32[2,2,16,512]{3,2,1,0:T(8,128)S(1)}, f32[2,2,16,512]{3,2,1,0:T(8,128)S(1)}, u32[]{:S(2)}, u32[]{:S(2)}) %collective-permute-start.13) | collective-permute-done | bytes 131104 | tf_op jit(solution)/shard_map/ppermute | solution.py:85
  56.1 0.9 collective-permute-start.14
  57.0 2.7 %collective-permute-start.43 = (f32[16,512]{1,0:T(8,128)S(1)}, f32[16,512]{1,0:T(8,128)S(1)}, u32[]{:S(2)}, u32[]{:S(2)}) collective-permute-start(f32[16,512]{1,0:T(8,128)S(1)} %dynamic-slice_bitcast_fusion.11), channel_id=1, source_target_pairs={{0,8},{1,9},{2,10},{3,11},{4,12},{5,13},{6,14},{7,15},{8,0},{9,1},... | collective-permute-start | bytes 98312 | tf_op jit(solution)/shard_map/ppermute | solution.py:85
  60.1 2.7 %collective-permute-start.11 = (f32[16,512]{1,0:T(8,128)S(1)}, f32[16,512]{1,0:T(8,128)S(1)}, u32[]{:S(2)}, u32[]{:S(2)}) collective-permute-start(f32[16,512]{1,0:T(8,128)S(1)} %dynamic-slice_bitcast_fusion.15), channel_id=1, source_target_pairs={{0,8},{1,9},{2,10},{3,11},{4,12},{5,13},{6,14},{7,15},{8,0},{9,1},... | collective-permute-start | bytes 98312 | tf_op jit(solution)/shard_map/ppermute | solution.py:85
  63.5 1.1 collective-permute-done.47
  64.6 1.1 collective-permute-done.11
  65.7 2.3 %collective-permute-done.15 = f32[16,512]{1,0:T(8,128)S(1)} collective-permute-done((f32[16,512]{1,0:T(8,128)S(1)}, f32[16,512]{1,0:T(8,128)S(1)}, u32[]{:S(2)}, u32[]{:S(2)}) %collective-permute-start.15) | collective-permute-done | bytes 32800 | tf_op jit(solution)/shard_map/ppermute | solution.py:85
  68.5 2.6 %collective-permute-start.51 = (bf16[1,16,512]{2,1,0:T(8,128)(2,1)S(1)}, bf16[1,16,512]{2,1,0:T(8,128)(2,1)S(1)}, u32[]{:S(2)}, u32[]{:S(2)}) collective-permute-start(bf16[1,16,512]{2,1,0:T(8,128)(2,1)S(1)} %get-tuple-element.97), channel_id=1, source_target_pairs={{0,8},{1,9},{2,10},{3,11},{4,12},{5,13},{6,14},{7,15},{8,0},{9,1},... | collective-permute-start | bytes 49160 | tf_op jit(solution)/shard_map/ppermute | solution.py:37
  71.4 2.6 %collective-permute-start.19 = (bf16[1,16,512]{2,1,0:T(8,128)(2,1)S(1)}, bf16[1,16,512]{2,1,0:T(8,128)(2,1)S(1)}, u32[]{:S(2)}, u32[]{:S(2)}) collective-permute-start(bf16[1,16,512]{2,1,0:T(8,128)(2,1)S(1)} %get-tuple-element.89), channel_id=1, source_target_pairs={{0,8},{1,9},{2,10},{3,11},{4,12},{5,13},{6,14},{7,15},{8,0},{9,1},... | collective-permute-start | bytes 49160 | tf_op jit(solution)/shard_map/ppermute | solution.py:37
  74.1 1.0 collective-permute-start.49
  75.1 1.1 collective-permute-start.52
  76.2 1.9 %collective-permute-start.17 = (bf16[2,16,512]{2,1,0:T(8,128)(2,1)S(1)}, bf16[2,16,512]{2,1,0:T(8,128)(2,1)S(1)}, u32[]{:S(2)}, u32[]{:S(2)}) collective-permute-start(bf16[2,16,512]{2,1,0:T(8,128)(2,1)S(1)} %pad_maximum_fusion.12), channel_id=1, source_target_pairs={{0,4},{1,3},{2,6},{3,1},{4,0},{5,7},{6,2},{7,5},{8,12},{9,11},{10,... | collective-permute-start | bytes 98312 | tf_op jit(solution)/shard_map/ppermute | solution.py:37
  78.4 1.0 collective-permute-done.52
  79.5 1.4 %collective-permute-start.53 = (bf16[4,16,512]{2,1,0:T(8,128)(2,1)S(1)}, bf16[4,16,512]{2,1,0:T(8,128)(2,1)S(1)}, u32[]{:S(2)}, u32[]{:S(2)}) collective-permute-start(bf16[4,16,512]{2,1,0:T(8,128)(2,1)S(1)} %bitcast.496), channel_id=1, source_target_pairs={{0,2},{1,5},{2,0},{3,7},{4,6},{5,1},{6,4},{7,3},{8,10},{9,13},{10,... | collective-permute-start | bytes 196616 | tf_op jit(solution)/shard_map/ppermute | solution.py:37
  80.9 0.7 collective-permute-start.50
  82.0 1.6 %collective-permute-start.21 = (bf16[4,16,512]{2,1,0:T(8,128)(2,1)S(1)}, bf16[4,16,512]{2,1,0:T(8,128)(2,1)S(1)}, u32[]{:S(2)}, u32[]{:S(2)}) collective-permute-start(bf16[4,16,512]{2,1,0:T(8,128)(2,1)S(1)} %bitcast.498), channel_id=1, source_target_pairs={{0,2},{1,5},{2,0},{3,7},{4,6},{5,1},{6,4},{7,3},{8,10},{9,13},{10,... | collective-permute-start | bytes 196616 | tf_op jit(solution)/shard_map/ppermute | solution.py:37
  84.4 0.8 collective-permute-done.50
  85.4 1.0 collective-permute-done.21
  86.5 1.5 %collective-permute-done.18 = bf16[4,16,512]{2,1,0:T(8,128)(2,1)S(1)} collective-permute-done((bf16[4,16,512]{2,1,0:T(8,128)(2,1)S(1)}, bf16[4,16,512]{2,1,0:T(8,128)(2,1)S(1)}, u32[]{:S(2)}, u32[]{:S(2)}) %collective-permute-start.18) | collective-permute-done | bytes 65568 | tf_op jit(solution)/shard_map/ppermute | solution.py:37
  89.3 7.1 %shard_map.58 = (f32[128,512]{1,0:T(8,128)}, f32[128,512]{1,0:T(8,128)}, f32[128,512]{1,0:T(8,128)}, f32[128,512]{1,0:T(8,128)}) custom-call(bf16[4,256,256]{2,1,0:T(8,128)(2,1)} %bitcast.418, bf16[128,512]{1,0:T(8,128)(2,1)} %bitcast.480, bf16[128,512]{1,0:T(8,128)(2,1)} %bitcast.472, bf16[128,512]{1,0:T(8,128)(2,1)} %copy-done.16, ...), custom_call_target="tpu_custom_call" | custom-call | tf_op jit(solution)/shard_map/pallas_call | solution.py:122
  97.2 1.0 collective-permute-done.22.refs_2_
  98.9 7.1 %shard_map.56 = (f32[128,512]{1,0:T(8,128)}, f32[128,512]{1,0:T(8,128)}, f32[128,512]{1,0:T(8,128)}, f32[128,512]{1,0:T(8,128)}) custom-call(bf16[4,256,256]{2,1,0:T(8,128)(2,1)} %bitcast.419, bf16[128,512]{1,0:T(8,128)(2,1)} %bitcast.484, bf16[128,512]{1,0:T(8,128)(2,1)} %bitcast.474, bf16[128,512]{1,0:T(8,128)(2,1)} %copy-done.18, ...), custom_call_target="tpu_custom_call" | custom-call | tf_op jit(solution)/shard_map/pallas_call | solution.py:122
  107.3 1.5 %collective-permute-start.61 = (f32[2,2,16,512]{3,2,1,0:T(8,128)S(1)}, f32[2,2,16,512]{3,2,1,0:T(8,128)S(1)}, u32[]{:S(2)}, u32[]{:S(2)}) collective-permute-start(f32[2,2,16,512]{3,2,1,0:T(8,128)S(1)} %bitcast_select_fusion.2), channel_id=1, source_target_pairs={{0,2},{1,5},{2,0},{3,7},{4,6},{5,1},{6,4},{7,3},{8,10},{9,13},{10,... | collective-permute-start | bytes 393224 | tf_op jit(solution)/shard_map/ppermute | solution.py:85
  108.8 1.0 add.298
  109.8 0.7 collective-permute-start.25
  110.5 1.0 add.303
  111.5 1.5 %collective-permute-start.29 = (f32[2,2,16,512]{3,2,1,0:T(8,128)S(1)}, f32[2,2,16,512]{3,2,1,0:T(8,128)S(1)}, u32[]{:S(2)}, u32[]{:S(2)}) collective-permute-start(f32[2,2,16,512]{3,2,1,0:T(8,128)S(1)} %bitcast_select_fusion.10), channel_id=1, source_target_pairs={{0,2},{1,5},{2,0},{3,7},{4,6},{5,1},{6,4},{7,3},{8,10},{9,13},{10,... | collective-permute-start | bytes 393224 | tf_op jit(solution)/shard_map/ppermute | solution.py:85
  113.1 0.9 collective-permute-start.58
  114.1 1.2 collective-permute-start.62
  115.3 0.9 collective-permute-start.26
  116.3 1.7 %collective-permute-done.29 = f32[2,2,16,512]{3,2,1,0:T(8,128)S(1)} collective-permute-done((f32[2,2,16,512]{3,2,1,0:T(8,128)S(1)}, f32[2,2,16,512]{3,2,1,0:T(8,128)S(1)}, u32[]{:S(2)}, u32[]{:S(2)}) %collective-permute-start.29) | collective-permute-done | bytes 131104 | tf_op jit(solution)/shard_map/ppermute | solution.py:85
  118.0 0.9 collective-permute-start.30
  119.0 2.1 %collective-permute-start.59 = (f32[16,512]{1,0:T(8,128)S(1)}, f32[16,512]{1,0:T(8,128)S(1)}, u32[]{:S(2)}, u32[]{:S(2)}) collective-permute-start(f32[16,512]{1,0:T(8,128)S(1)} %dynamic-slice_bitcast_fusion.9), channel_id=1, source_target_pairs={{0,8},{1,9},{2,10},{3,11},{4,12},{5,13},{6,14},{7,15},{8,0},{9,1},... | collective-permute-start | bytes 98312 | tf_op jit(solution)/shard_map/ppermute | solution.py:85
  121.2 0.9 collective-permute-start.63
  122.1 2.1 %collective-permute-start.27 = (f32[16,512]{1,0:T(8,128)S(1)}, f32[16,512]{1,0:T(8,128)S(1)}, u32[]{:S(2)}, u32[]{:S(2)}) collective-permute-start(f32[16,512]{1,0:T(8,128)S(1)} %dynamic-slice_bitcast_fusion.13), channel_id=1, source_target_pairs={{0,8},{1,9},{2,10},{3,11},{4,12},{5,13},{6,14},{7,15},{8,0},{9,1},... | collective-permute-start | bytes 98312 | tf_op jit(solution)/shard_map/ppermute | solution.py:85
  124.3 0.9 collective-permute-start.31
  125.2 1.2 collective-permute-done.63
  127.0 2.5 %collective-permute-done.31 = f32[16,512]{1,0:T(8,128)S(1)} collective-permute-done((f32[16,512]{1,0:T(8,128)S(1)}, f32[16,512]{1,0:T(8,128)S(1)}, u32[]{:S(2)}, u32[]{:S(2)}) %collective-permute-start.31) | collective-permute-done | bytes 32800 | tf_op jit(solution)/shard_map/ppermute | solution.py:85
  129.7 0.8 copy.111
  (232 shorter events, 15.1 us)
Async XLA Ops:
  2.6 10.5 %collective-permute-start.32 = (bf16[1,16,512]{2,1,0:T(8,128)(2,1)S(1)}, bf16[1,16,512]{2,1,0:T(8,128)(2,1)S(1)}, u32[]{:S(2)}, u32[]{:S(2)}) collective-permute-start(bf16[1,16,512]{2,1,0:T(8,128)(2,1)S(1)} %get-tuple-element.102), channel_id=1, source_target_pairs={{0,8},{1,9},{2,10},{3,11},{4,12},{5,13},{6,14},{7,15},{8,0},{9,1},... | collective-permute-start | bytes 49160 | tf_op jit(solution)/shard_map/ppermute | solution.py:37
  6.7 6.4 %collective-permute-start.35 = (bf16[1,16,512]{2,1,0:T(8,128)(2,1)S(1)}, bf16[1,16,512]{2,1,0:T(8,128)(2,1)S(1)}, u32[]{:S(2)}, u32[]{:S(2)}) collective-permute-start(bf16[1,16,512]{2,1,0:T(8,128)(2,1)S(1)} %get-tuple-element.101), channel_id=1, source_target_pairs={{0,8},{1,9},{2,10},{3,11},{4,12},{5,13},{6,14},{7,15},{8,0},{9,1},... | collective-permute-start | bytes 49160 | tf_op jit(solution)/shard_map/ppermute | solution.py:37
  6.8 8.5 %collective-permute-start = (bf16[1,16,512]{2,1,0:T(8,128)(2,1)S(1)}, bf16[1,16,512]{2,1,0:T(8,128)(2,1)S(1)}, u32[]{:S(2)}, u32[]{:S(2)}) collective-permute-start(bf16[1,16,512]{2,1,0:T(8,128)(2,1)S(1)} %get-tuple-element.94), channel_id=1, source_target_pairs={{0,8},{1,9},{2,10},{3,11},{4,12},{5,13},{6,14},{7,15},{8,0},{9,1},... | collective-permute-start | bytes 49160 | tf_op jit(solution)/shard_map/ppermute | solution.py:37
  9.7 5.6 %collective-permute-start.3 = (bf16[1,16,512]{2,1,0:T(8,128)(2,1)S(1)}, bf16[1,16,512]{2,1,0:T(8,128)(2,1)S(1)}, u32[]{:S(2)}, u32[]{:S(2)}) collective-permute-start(bf16[1,16,512]{2,1,0:T(8,128)(2,1)S(1)} %get-tuple-element.93), channel_id=1, source_target_pairs={{0,8},{1,9},{2,10},{3,11},{4,12},{5,13},{6,14},{7,15},{8,0},{9,1},... | collective-permute-start | bytes 49160 | tf_op jit(solution)/shard_map/ppermute | solution.py:37
  13.2 4.2 %collective-permute-start.36 = (bf16[2,16,512]{2,1,0:T(8,128)(2,1)S(1)}, bf16[2,16,512]{2,1,0:T(8,128)(2,1)S(1)}, u32[]{:S(2)}, u32[]{:S(2)}) collective-permute-start(bf16[2,16,512]{2,1,0:T(8,128)(2,1)S(1)} %pad_maximum_fusion.15), channel_id=1, source_target_pairs={{0,4},{1,3},{2,6},{3,1},{4,0},{5,7},{6,2},{7,5},{8,12},{9,11},{10,... | collective-permute-start | bytes 98312 | tf_op jit(solution)/shard_map/ppermute | solution.py:37
  15.1 4.2 %collective-permute-start.33 = (bf16[2,16,512]{2,1,0:T(8,128)(2,1)S(1)}, bf16[2,16,512]{2,1,0:T(8,128)(2,1)S(1)}, u32[]{:S(2)}, u32[]{:S(2)}) collective-permute-start(bf16[2,16,512]{2,1,0:T(8,128)(2,1)S(1)} %pad_maximum_fusion.14), channel_id=1, source_target_pairs={{0,4},{1,3},{2,6},{3,1},{4,0},{5,7},{6,2},{7,5},{8,12},{9,11},{10,... | collective-permute-start | bytes 98312 | tf_op jit(solution)/shard_map/ppermute | solution.py:37
  15.3 5.3 %collective-permute-start.4 = (bf16[2,16,512]{2,1,0:T(8,128)(2,1)S(1)}, bf16[2,16,512]{2,1,0:T(8,128)(2,1)S(1)}, u32[]{:S(2)}, u32[]{:S(2)}) collective-permute-start(bf16[2,16,512]{2,1,0:T(8,128)(2,1)S(1)} %pad_maximum_fusion.11), channel_id=1, source_target_pairs={{0,4},{1,3},{2,6},{3,1},{4,0},{5,7},{6,2},{7,5},{8,12},{9,11},{10,... | collective-permute-start | bytes 98312 | tf_op jit(solution)/shard_map/ppermute | solution.py:37
  17.2 4.3 %collective-permute-start.1 = (bf16[2,16,512]{2,1,0:T(8,128)(2,1)S(1)}, bf16[2,16,512]{2,1,0:T(8,128)(2,1)S(1)}, u32[]{:S(2)}, u32[]{:S(2)}) collective-permute-start(bf16[2,16,512]{2,1,0:T(8,128)(2,1)S(1)} %pad_maximum_fusion.10), channel_id=1, source_target_pairs={{0,4},{1,3},{2,6},{3,1},{4,0},{5,7},{6,2},{7,5},{8,12},{9,11},{10,... | collective-permute-start | bytes 98312 | tf_op jit(solution)/shard_map/ppermute | solution.py:37
  17.5 5.7 %collective-permute-start.37 = (bf16[4,16,512]{2,1,0:T(8,128)(2,1)S(1)}, bf16[4,16,512]{2,1,0:T(8,128)(2,1)S(1)}, u32[]{:S(2)}, u32[]{:S(2)}) collective-permute-start(bf16[4,16,512]{2,1,0:T(8,128)(2,1)S(1)} %bitcast.491), channel_id=1, source_target_pairs={{0,2},{1,5},{2,0},{3,7},{4,6},{5,1},{6,4},{7,3},{8,10},{9,13},{10,... | collective-permute-start | bytes 196616 | tf_op jit(solution)/shard_map/ppermute | solution.py:37
  19.3 4.3 %collective-permute-start.34 = (bf16[4,16,512]{2,1,0:T(8,128)(2,1)S(1)}, bf16[4,16,512]{2,1,0:T(8,128)(2,1)S(1)}, u32[]{:S(2)}, u32[]{:S(2)}) collective-permute-start(bf16[4,16,512]{2,1,0:T(8,128)(2,1)S(1)} %bitcast.493), channel_id=1, source_target_pairs={{0,2},{1,5},{2,0},{3,7},{4,6},{5,1},{6,4},{7,3},{8,10},{9,13},{10,... | collective-permute-start | bytes 196616 | tf_op jit(solution)/shard_map/ppermute | solution.py:37
  20.7 4.3 %collective-permute-start.5 = (bf16[4,16,512]{2,1,0:T(8,128)(2,1)S(1)}, bf16[4,16,512]{2,1,0:T(8,128)(2,1)S(1)}, u32[]{:S(2)}, u32[]{:S(2)}) collective-permute-start(bf16[4,16,512]{2,1,0:T(8,128)(2,1)S(1)} %bitcast.494), channel_id=1, source_target_pairs={{0,2},{1,5},{2,0},{3,7},{4,6},{5,1},{6,4},{7,3},{8,10},{9,13},{10,... | collective-permute-start | bytes 196616 | tf_op jit(solution)/shard_map/ppermute | solution.py:37
  21.6 4.3 %collective-permute-start.2 = (bf16[4,16,512]{2,1,0:T(8,128)(2,1)S(1)}, bf16[4,16,512]{2,1,0:T(8,128)(2,1)S(1)}, u32[]{:S(2)}, u32[]{:S(2)}) collective-permute-start(bf16[4,16,512]{2,1,0:T(8,128)(2,1)S(1)} %bitcast.495), channel_id=1, source_target_pairs={{0,2},{1,5},{2,0},{3,7},{4,6},{5,1},{6,4},{7,3},{8,10},{9,13},{10,... | collective-permute-start | bytes 196616 | tf_op jit(solution)/shard_map/ppermute | solution.py:37
  23.2 2.7 %collective-permute-start.39 = (bf16[128,512]{1,0:T(8,128)(2,1)S(1)}, bf16[128,512]{1,0:T(8,128)(2,1)S(1)}, u32[]{:S(2)}, u32[]{:S(2)}) collective-permute-start(bf16[128,512]{1,0:T(8,128)(2,1)S(1)} %bitcast.475), channel_id=1, source_target_pairs={{0,1},{1,0},{2,3},{3,2},{4,5},{5,4},{6,7},{7,6},{8,9},{9,8},{10,11... | collective-permute-start | bytes 393224 | tf_op jit(solution)/shard_map/ppermute | solution.py:54
  23.7 2.2 %collective-permute-start.38 = (bf16[128,512]{1,0:T(8,128)(2,1)S(1)}, bf16[128,512]{1,0:T(8,128)(2,1)S(1)}, u32[]{:S(2)}, u32[]{:S(2)}) collective-permute-start(bf16[128,512]{1,0:T(8,128)(2,1)S(1)} %bitcast.481), channel_id=1, source_target_pairs={{0,1},{1,0},{2,3},{3,2},{4,5},{5,4},{6,7},{7,6},{8,9},{9,8},{10,11... | collective-permute-start | bytes 393224 | tf_op jit(solution)/shard_map/ppermute | solution.py:54
  25.1 9.4 %collective-permute-start.7 = (bf16[128,512]{1,0:T(8,128)(2,1)S(1)}, bf16[128,512]{1,0:T(8,128)(2,1)S(1)}, u32[]{:S(2)}, u32[]{:S(2)}) collective-permute-start(bf16[128,512]{1,0:T(8,128)(2,1)S(1)} %bitcast.477), channel_id=1, source_target_pairs={{0,1},{1,0},{2,3},{3,2},{4,5},{5,4},{6,7},{7,6},{8,9},{9,8},{10,11... | collective-permute-start | bytes 393224 | tf_op jit(solution)/shard_map/ppermute | solution.py:54
  33.7 10.1 %collective-permute-start.40 = (f32[128,512]{1,0:T(8,128)}, f32[128,512]{1,0:T(8,128)S(1)}, u32[]{:S(2)}, u32[]{:S(2)}) collective-permute-start(f32[128,512]{1,0:T(8,128)} %get-tuple-element.30), channel_id=1, source_target_pairs={{0,1},{1,0},{2,3},{3,2},{4,5},{5,4},{6,7},{7,6},{8,9},{9,8},{10,11... | collective-permute-start | bytes 786440 | tf_op jit(solution)/shard_map/ppermute | solution.py:64
  33.9 1.7 %collective-permute-start.6 = (bf16[128,512]{1,0:T(8,128)(2,1)S(1)}, bf16[128,512]{1,0:T(8,128)(2,1)S(1)}, u32[]{:S(2)}, u32[]{:S(2)}) collective-permute-start(bf16[128,512]{1,0:T(8,128)(2,1)S(1)} %bitcast.485), channel_id=1, source_target_pairs={{0,1},{1,0},{2,3},{3,2},{4,5},{5,4},{6,7},{7,6},{8,9},{9,8},{10,11... | collective-permute-start | bytes 393224 | tf_op jit(solution)/shard_map/ppermute | solution.py:54
  34.4 11.0 %collective-permute-start.44 = (f32[128,512]{1,0:T(8,128)}, f32[128,512]{1,0:T(8,128)S(1)}, u32[]{:S(2)}, u32[]{:S(2)}) collective-permute-start(f32[128,512]{1,0:T(8,128)} %get-tuple-element.32), channel_id=1, source_target_pairs={{0,1},{1,0},{2,3},{3,2},{4,5},{5,4},{6,7},{7,6},{8,9},{9,8},{10,11... | collective-permute-start | bytes 786440 | tf_op jit(solution)/shard_map/ppermute | solution.py:64
  43.3 2.8 %collective-permute-start.8 = (f32[128,512]{1,0:T(8,128)}, f32[128,512]{1,0:T(8,128)S(1)}, u32[]{:S(2)}, u32[]{:S(2)}) collective-permute-start(f32[128,512]{1,0:T(8,128)} %get-tuple-element.22), channel_id=1, source_target_pairs={{0,1},{1,0},{2,3},{3,2},{4,5},{5,4},{6,7},{7,6},{8,9},{9,8},{10,11... | collective-permute-start | bytes 786440 | tf_op jit(solution)/shard_map/ppermute | solution.py:64
  43.5 5.2 %collective-permute-start.12 = (f32[128,512]{1,0:T(8,128)}, f32[128,512]{1,0:T(8,128)S(1)}, u32[]{:S(2)}, u32[]{:S(2)}) collective-permute-start(f32[128,512]{1,0:T(8,128)} %get-tuple-element.24), channel_id=1, source_target_pairs={{0,1},{1,0},{2,3},{3,2},{4,5},{5,4},{6,7},{7,6},{8,9},{9,8},{10,11... | collective-permute-start | bytes 786440 | tf_op jit(solution)/shard_map/ppermute | solution.py:64
  43.9 6.5 %collective-permute-start.41 = (f32[2,2,16,512]{3,2,1,0:T(8,128)S(1)}, f32[2,2,16,512]{3,2,1,0:T(8,128)S(1)}, u32[]{:S(2)}, u32[]{:S(2)}) collective-permute-start(f32[2,2,16,512]{3,2,1,0:T(8,128)S(1)} %bitcast_select_fusion.8), channel_id=1, source_target_pairs={{0,2},{1,5},{2,0},{3,7},{4,6},{5,1},{6,4},{7,3},{8,10},{9,13},{10,... | collective-permute-start | bytes 393224 | tf_op jit(solution)/shard_map/ppermute | solution.py:85
  45.5 6.5 %collective-permute-start.45 = (f32[2,2,16,512]{3,2,1,0:T(8,128)S(1)}, f32[2,2,16,512]{3,2,1,0:T(8,128)S(1)}, u32[]{:S(2)}, u32[]{:S(2)}) collective-permute-start(f32[2,2,16,512]{3,2,1,0:T(8,128)S(1)} %bitcast_select_fusion.6), channel_id=1, source_target_pairs={{0,2},{1,5},{2,0},{3,7},{4,6},{5,1},{6,4},{7,3},{8,10},{9,13},{10,... | collective-permute-start | bytes 393224 | tf_op jit(solution)/shard_map/ppermute | solution.py:85
  47.1 5.5 %collective-permute-start.9 = (f32[2,2,16,512]{3,2,1,0:T(8,128)S(1)}, f32[2,2,16,512]{3,2,1,0:T(8,128)S(1)}, u32[]{:S(2)}, u32[]{:S(2)}) collective-permute-start(f32[2,2,16,512]{3,2,1,0:T(8,128)S(1)} %bitcast_select_fusion.16), channel_id=1, source_target_pairs={{0,2},{1,5},{2,0},{3,7},{4,6},{5,1},{6,4},{7,3},{8,10},{9,13},{10,... | collective-permute-start | bytes 393224 | tf_op jit(solution)/shard_map/ppermute | solution.py:85
  49.7 6.3 %collective-permute-start.13 = (f32[2,2,16,512]{3,2,1,0:T(8,128)S(1)}, f32[2,2,16,512]{3,2,1,0:T(8,128)S(1)}, u32[]{:S(2)}, u32[]{:S(2)}) collective-permute-start(f32[2,2,16,512]{3,2,1,0:T(8,128)S(1)} %bitcast_select_fusion.14), channel_id=1, source_target_pairs={{0,2},{1,5},{2,0},{3,7},{4,6},{5,1},{6,4},{7,3},{8,10},{9,13},{10,... | collective-permute-start | bytes 393224 | tf_op jit(solution)/shard_map/ppermute | solution.py:85
  50.4 6.6 %collective-permute-start.42 = (f32[2,16,512]{2,1,0:T(8,128)S(1)}, f32[2,16,512]{2,1,0:T(8,128)S(1)}, u32[]{:S(2)}, u32[]{:S(2)}) collective-permute-start(f32[2,16,512]{2,1,0:T(8,128)S(1)} %dynamic-slice_bitcast_fusion.3), channel_id=1, source_target_pairs={{0,4},{1,3},{2,6},{3,1},{4,0},{5,7},{6,2},{7,5},{8,12},{9,11},{10,... | collective-permute-start | bytes 196616 | tf_op jit(solution)/shard_map/ppermute | solution.py:85
  52.1 7.6 %collective-permute-start.46 = (f32[2,16,512]{2,1,0:T(8,128)S(1)}, f32[2,16,512]{2,1,0:T(8,128)S(1)}, u32[]{:S(2)}, u32[]{:S(2)}) collective-permute-start(f32[2,16,512]{2,1,0:T(8,128)S(1)} %dynamic-slice_bitcast_fusion.2), channel_id=1, source_target_pairs={{0,4},{1,3},{2,6},{3,1},{4,0},{5,7},{6,2},{7,5},{8,12},{9,11},{10,... | collective-permute-start | bytes 196616 | tf_op jit(solution)/shard_map/ppermute | solution.py:85
  52.7 7.4 %collective-permute-start.10 = (f32[2,16,512]{2,1,0:T(8,128)S(1)}, f32[2,16,512]{2,1,0:T(8,128)S(1)}, u32[]{:S(2)}, u32[]{:S(2)}) collective-permute-start(f32[2,16,512]{2,1,0:T(8,128)S(1)} %dynamic-slice_bitcast_fusion.7), channel_id=1, source_target_pairs={{0,4},{1,3},{2,6},{3,1},{4,0},{5,7},{6,2},{7,5},{8,12},{9,11},{10,... | collective-permute-start | bytes 196616 | tf_op jit(solution)/shard_map/ppermute | solution.py:85
  56.1 6.7 %collective-permute-start.14 = (f32[2,16,512]{2,1,0:T(8,128)S(1)}, f32[2,16,512]{2,1,0:T(8,128)S(1)}, u32[]{:S(2)}, u32[]{:S(2)}) collective-permute-start(f32[2,16,512]{2,1,0:T(8,128)S(1)} %dynamic-slice_bitcast_fusion.6), channel_id=1, source_target_pairs={{0,4},{1,3},{2,6},{3,1},{4,0},{5,7},{6,2},{7,5},{8,12},{9,11},{10,... | collective-permute-start | bytes 196616 | tf_op jit(solution)/shard_map/ppermute | solution.py:85
  57.0 6.4 %collective-permute-start.43 = (f32[16,512]{1,0:T(8,128)S(1)}, f32[16,512]{1,0:T(8,128)S(1)}, u32[]{:S(2)}, u32[]{:S(2)}) collective-permute-start(f32[16,512]{1,0:T(8,128)S(1)} %dynamic-slice_bitcast_fusion.11), channel_id=1, source_target_pairs={{0,8},{1,9},{2,10},{3,11},{4,12},{5,13},{6,14},{7,15},{8,0},{9,1},... | collective-permute-start | bytes 98312 | tf_op jit(solution)/shard_map/ppermute | solution.py:85
  59.7 4.9 %collective-permute-start.47 = (f32[16,512]{1,0:T(8,128)S(1)}, f32[16,512]{1,0:T(8,128)S(1)}, u32[]{:S(2)}, u32[]{:S(2)}) collective-permute-start(f32[16,512]{1,0:T(8,128)S(1)} %dynamic-slice_bitcast_fusion.10), channel_id=1, source_target_pairs={{0,8},{1,9},{2,10},{3,11},{4,12},{5,13},{6,14},{7,15},{8,0},{9,1},... | collective-permute-start | bytes 98312 | tf_op jit(solution)/shard_map/ppermute | solution.py:85
  60.1 5.6 %collective-permute-start.11 = (f32[16,512]{1,0:T(8,128)S(1)}, f32[16,512]{1,0:T(8,128)S(1)}, u32[]{:S(2)}, u32[]{:S(2)}) collective-permute-start(f32[16,512]{1,0:T(8,128)S(1)} %dynamic-slice_bitcast_fusion.15), channel_id=1, source_target_pairs={{0,8},{1,9},{2,10},{3,11},{4,12},{5,13},{6,14},{7,15},{8,0},{9,1},... | collective-permute-start | bytes 98312 | tf_op jit(solution)/shard_map/ppermute | solution.py:85
  62.8 5.2 %collective-permute-start.15 = (f32[16,512]{1,0:T(8,128)S(1)}, f32[16,512]{1,0:T(8,128)S(1)}, u32[]{:S(2)}, u32[]{:S(2)}) collective-permute-start(f32[16,512]{1,0:T(8,128)S(1)} %dynamic-slice_bitcast_fusion.14), channel_id=1, source_target_pairs={{0,8},{1,9},{2,10},{3,11},{4,12},{5,13},{6,14},{7,15},{8,0},{9,1},... | collective-permute-start | bytes 98312 | tf_op jit(solution)/shard_map/ppermute | solution.py:85
  68.1 5.9 %collective-permute-start.48 = (bf16[1,16,512]{2,1,0:T(8,128)(2,1)S(1)}, bf16[1,16,512]{2,1,0:T(8,128)(2,1)S(1)}, u32[]{:S(2)}, u32[]{:S(2)}) collective-permute-start(bf16[1,16,512]{2,1,0:T(8,128)(2,1)S(1)} %get-tuple-element.98), channel_id=1, source_target_pairs={{0,8},{1,9},{2,10},{3,11},{4,12},{5,13},{6,14},{7,15},{8,0},{9,1},... | collective-permute-start | bytes 49160 | tf_op jit(solution)/shard_map/ppermute | solution.py:37
  68.5 5.6 %collective-permute-start.51 = (bf16[1,16,512]{2,1,0:T(8,128)(2,1)S(1)}, bf16[1,16,512]{2,1,0:T(8,128)(2,1)S(1)}, u32[]{:S(2)}, u32[]{:S(2)}) collective-permute-start(bf16[1,16,512]{2,1,0:T(8,128)(2,1)S(1)} %get-tuple-element.97), channel_id=1, source_target_pairs={{0,8},{1,9},{2,10},{3,11},{4,12},{5,13},{6,14},{7,15},{8,0},{9,1},... | collective-permute-start | bytes 49160 | tf_op jit(solution)/shard_map/ppermute | solution.py:37
  71.1 5.1 %collective-permute-start.16 = (bf16[1,16,512]{2,1,0:T(8,128)(2,1)S(1)}, bf16[1,16,512]{2,1,0:T(8,128)(2,1)S(1)}, u32[]{:S(2)}, u32[]{:S(2)}) collective-permute-start(bf16[1,16,512]{2,1,0:T(8,128)(2,1)S(1)} %get-tuple-element.90), channel_id=1, source_target_pairs={{0,8},{1,9},{2,10},{3,11},{4,12},{5,13},{6,14},{7,15},{8,0},{9,1},... | collective-permute-start | bytes 49160 | tf_op jit(solution)/shard_map/ppermute | solution.py:37
  71.4 4.8 %collective-permute-start.19 = (bf16[1,16,512]{2,1,0:T(8,128)(2,1)S(1)}, bf16[1,16,512]{2,1,0:T(8,128)(2,1)S(1)}, u32[]{:S(2)}, u32[]{:S(2)}) collective-permute-start(bf16[1,16,512]{2,1,0:T(8,128)(2,1)S(1)} %get-tuple-element.89), channel_id=1, source_target_pairs={{0,8},{1,9},{2,10},{3,11},{4,12},{5,13},{6,14},{7,15},{8,0},{9,1},... | collective-permute-start | bytes 49160 | tf_op jit(solution)/shard_map/ppermute | solution.py:37
  74.1 4.3 %collective-permute-start.49 = (bf16[2,16,512]{2,1,0:T(8,128)(2,1)S(1)}, bf16[2,16,512]{2,1,0:T(8,128)(2,1)S(1)}, u32[]{:S(2)}, u32[]{:S(2)}) collective-permute-start(bf16[2,16,512]{2,1,0:T(8,128)(2,1)S(1)} %pad_maximum_fusion.16), channel_id=1, source_target_pairs={{0,4},{1,3},{2,6},{3,1},{4,0},{5,7},{6,2},{7,5},{8,12},{9,11},{10,... | collective-permute-start | bytes 98312 | tf_op jit(solution)/shard_map/ppermute | solution.py:37
  75.1 4.3 %collective-permute-start.52 = (bf16[2,16,512]{2,1,0:T(8,128)(2,1)S(1)}, bf16[2,16,512]{2,1,0:T(8,128)(2,1)S(1)}, u32[]{:S(2)}, u32[]{:S(2)}) collective-permute-start(bf16[2,16,512]{2,1,0:T(8,128)(2,1)S(1)} %pad_maximum_fusion.17), channel_id=1, source_target_pairs={{0,4},{1,3},{2,6},{3,1},{4,0},{5,7},{6,2},{7,5},{8,12},{9,11},{10,... | collective-permute-start | bytes 98312 | tf_op jit(solution)/shard_map/ppermute | solution.py:37
  76.2 5.4 %collective-permute-start.17 = (bf16[2,16,512]{2,1,0:T(8,128)(2,1)S(1)}, bf16[2,16,512]{2,1,0:T(8,128)(2,1)S(1)}, u32[]{:S(2)}, u32[]{:S(2)}) collective-permute-start(bf16[2,16,512]{2,1,0:T(8,128)(2,1)S(1)} %pad_maximum_fusion.12), channel_id=1, source_target_pairs={{0,4},{1,3},{2,6},{3,1},{4,0},{5,7},{6,2},{7,5},{8,12},{9,11},{10,... | collective-permute-start | bytes 98312 | tf_op jit(solution)/shard_map/ppermute | solution.py:37
  78.1 3.9 %collective-permute-start.20 = (bf16[2,16,512]{2,1,0:T(8,128)(2,1)S(1)}, bf16[2,16,512]{2,1,0:T(8,128)(2,1)S(1)}, u32[]{:S(2)}, u32[]{:S(2)}) collective-permute-start(bf16[2,16,512]{2,1,0:T(8,128)(2,1)S(1)} %pad_maximum_fusion.13), channel_id=1, source_target_pairs={{0,4},{1,3},{2,6},{3,1},{4,0},{5,7},{6,2},{7,5},{8,12},{9,11},{10,... | collective-permute-start | bytes 98312 | tf_op jit(solution)/shard_map/ppermute | solution.py:37
  79.5 4.8 %collective-permute-start.53 = (bf16[4,16,512]{2,1,0:T(8,128)(2,1)S(1)}, bf16[4,16,512]{2,1,0:T(8,128)(2,1)S(1)}, u32[]{:S(2)}, u32[]{:S(2)}) collective-permute-start(bf16[4,16,512]{2,1,0:T(8,128)(2,1)S(1)} %bitcast.496), channel_id=1, source_target_pairs={{0,2},{1,5},{2,0},{3,7},{4,6},{5,1},{6,4},{7,3},{8,10},{9,13},{10,... | collective-permute-start | bytes 196616 | tf_op jit(solution)/shard_map/ppermute | solution.py:37
  80.9 4.3 %collective-permute-start.50 = (bf16[4,16,512]{2,1,0:T(8,128)(2,1)S(1)}, bf16[4,16,512]{2,1,0:T(8,128)(2,1)S(1)}, u32[]{:S(2)}, u32[]{:S(2)}) collective-permute-start(bf16[4,16,512]{2,1,0:T(8,128)(2,1)S(1)} %bitcast.492), channel_id=1, source_target_pairs={{0,2},{1,5},{2,0},{3,7},{4,6},{5,1},{6,4},{7,3},{8,10},{9,13},{10,... | collective-permute-start | bytes 196616 | tf_op jit(solution)/shard_map/ppermute | solution.py:37
  82.0 4.3 %collective-permute-start.21 = (bf16[4,16,512]{2,1,0:T(8,128)(2,1)S(1)}, bf16[4,16,512]{2,1,0:T(8,128)(2,1)S(1)}, u32[]{:S(2)}, u32[]{:S(2)}) collective-permute-start(bf16[4,16,512]{2,1,0:T(8,128)(2,1)S(1)} %bitcast.498), channel_id=1, source_target_pairs={{0,2},{1,5},{2,0},{3,7},{4,6},{5,1},{6,4},{7,3},{8,10},{9,13},{10,... | collective-permute-start | bytes 196616 | tf_op jit(solution)/shard_map/ppermute | solution.py:37
  83.6 4.3 %collective-permute-start.18 = (bf16[4,16,512]{2,1,0:T(8,128)(2,1)S(1)}, bf16[4,16,512]{2,1,0:T(8,128)(2,1)S(1)}, u32[]{:S(2)}, u32[]{:S(2)}) collective-permute-start(bf16[4,16,512]{2,1,0:T(8,128)(2,1)S(1)} %bitcast.497), channel_id=1, source_target_pairs={{0,2},{1,5},{2,0},{3,7},{4,6},{5,1},{6,4},{7,3},{8,10},{9,13},{10,... | collective-permute-start | bytes 196616 | tf_op jit(solution)/shard_map/ppermute | solution.py:37
  84.3 3.7 %collective-permute-start.55 = (bf16[128,512]{1,0:T(8,128)(2,1)S(1)}, bf16[128,512]{1,0:T(8,128)(2,1)S(1)}, u32[]{:S(2)}, u32[]{:S(2)}) collective-permute-start(bf16[128,512]{1,0:T(8,128)(2,1)S(1)} %bitcast.471), channel_id=1, source_target_pairs={{0,1},{1,0},{2,3},{3,2},{4,5},{5,4},{6,7},{7,6},{8,9},{9,8},{10,11... | collective-permute-start | bytes 393224 | tf_op jit(solution)/shard_map/ppermute | solution.py:54
  85.3 2.7 %collective-permute-start.54 = (bf16[128,512]{1,0:T(8,128)(2,1)S(1)}, bf16[128,512]{1,0:T(8,128)(2,1)S(1)}, u32[]{:S(2)}, u32[]{:S(2)}) collective-permute-start(bf16[128,512]{1,0:T(8,128)(2,1)S(1)} %bitcast.479), channel_id=1, source_target_pairs={{0,1},{1,0},{2,3},{3,2},{4,5},{5,4},{6,7},{7,6},{8,9},{9,8},{10,11... | collective-permute-start | bytes 393224 | tf_op jit(solution)/shard_map/ppermute | solution.py:54
  86.4 10.7 %collective-permute-start.23 = (bf16[128,512]{1,0:T(8,128)(2,1)S(1)}, bf16[128,512]{1,0:T(8,128)(2,1)S(1)}, u32[]{:S(2)}, u32[]{:S(2)}) collective-permute-start(bf16[128,512]{1,0:T(8,128)(2,1)S(1)} %bitcast.473), channel_id=1, source_target_pairs={{0,1},{1,0},{2,3},{3,2},{4,5},{5,4},{6,7},{7,6},{8,9},{9,8},{10,11... | collective-permute-start | bytes 393224 | tf_op jit(solution)/shard_map/ppermute | solution.py:54
  96.4 10.1 %collective-permute-start.56 = (f32[128,512]{1,0:T(8,128)}, f32[128,512]{1,0:T(8,128)S(1)}, u32[]{:S(2)}, u32[]{:S(2)}) collective-permute-start(f32[128,512]{1,0:T(8,128)} %get-tuple-element.34), channel_id=1, source_target_pairs={{0,1},{1,0},{2,3},{3,2},{4,5},{5,4},{6,7},{7,6},{8,9},{9,8},{10,11... | collective-permute-start | bytes 786440 | tf_op jit(solution)/shard_map/ppermute | solution.py:64
  96.5 1.7 %collective-permute-start.22 = (bf16[128,512]{1,0:T(8,128)(2,1)S(1)}, bf16[128,512]{1,0:T(8,128)(2,1)S(1)}, u32[]{:S(2)}, u32[]{:S(2)}) collective-permute-start(bf16[128,512]{1,0:T(8,128)(2,1)S(1)} %bitcast.483), channel_id=1, source_target_pairs={{0,1},{1,0},{2,3},{3,2},{4,5},{5,4},{6,7},{7,6},{8,9},{9,8},{10,11... | collective-permute-start | bytes 393224 | tf_op jit(solution)/shard_map/ppermute | solution.py:54
  97.1 10.1 %collective-permute-start.60 = (f32[128,512]{1,0:T(8,128)}, f32[128,512]{1,0:T(8,128)S(1)}, u32[]{:S(2)}, u32[]{:S(2)}) collective-permute-start(f32[128,512]{1,0:T(8,128)} %get-tuple-element.36), channel_id=1, source_target_pairs={{0,1},{1,0},{2,3},{3,2},{4,5},{5,4},{6,7},{7,6},{8,9},{9,8},{10,11... | collective-permute-start | bytes 786440 | tf_op jit(solution)/shard_map/ppermute | solution.py:64
  106.0 2.8 %collective-permute-start.24 = (f32[128,512]{1,0:T(8,128)}, f32[128,512]{1,0:T(8,128)S(1)}, u32[]{:S(2)}, u32[]{:S(2)}) collective-permute-start(f32[128,512]{1,0:T(8,128)} %get-tuple-element.26), channel_id=1, source_target_pairs={{0,1},{1,0},{2,3},{3,2},{4,5},{5,4},{6,7},{7,6},{8,9},{9,8},{10,11... | collective-permute-start | bytes 786440 | tf_op jit(solution)/shard_map/ppermute | solution.py:64
  106.2 4.3 %collective-permute-start.28 = (f32[128,512]{1,0:T(8,128)}, f32[128,512]{1,0:T(8,128)S(1)}, u32[]{:S(2)}, u32[]{:S(2)}) collective-permute-start(f32[128,512]{1,0:T(8,128)} %get-tuple-element.28), channel_id=1, source_target_pairs={{0,1},{1,0},{2,3},{3,2},{4,5},{5,4},{6,7},{7,6},{8,9},{9,8},{10,11... | collective-permute-start | bytes 786440 | tf_op jit(solution)/shard_map/ppermute | solution.py:64
  106.5 6.5 %collective-permute-start.57 = (f32[2,2,16,512]{3,2,1,0:T(8,128)S(1)}, f32[2,2,16,512]{3,2,1,0:T(8,128)S(1)}, u32[]{:S(2)}, u32[]{:S(2)}) collective-permute-start(f32[2,2,16,512]{3,2,1,0:T(8,128)S(1)} %bitcast_select_fusion.4), channel_id=1, source_target_pairs={{0,2},{1,5},{2,0},{3,7},{4,6},{5,1},{6,4},{7,3},{8,10},{9,13},{10,... | collective-permute-start | bytes 393224 | tf_op jit(solution)/shard_map/ppermute | solution.py:85
  107.3 6.7 %collective-permute-start.61 = (f32[2,2,16,512]{3,2,1,0:T(8,128)S(1)}, f32[2,2,16,512]{3,2,1,0:T(8,128)S(1)}, u32[]{:S(2)}, u32[]{:S(2)}) collective-permute-start(f32[2,2,16,512]{3,2,1,0:T(8,128)S(1)} %bitcast_select_fusion.2), channel_id=1, source_target_pairs={{0,2},{1,5},{2,0},{3,7},{4,6},{5,1},{6,4},{7,3},{8,10},{9,13},{10,... | collective-permute-start | bytes 393224 | tf_op jit(solution)/shard_map/ppermute | solution.py:85
  109.8 5.5 %collective-permute-start.25 = (f32[2,2,16,512]{3,2,1,0:T(8,128)S(1)}, f32[2,2,16,512]{3,2,1,0:T(8,128)S(1)}, u32[]{:S(2)}, u32[]{:S(2)}) collective-permute-start(f32[2,2,16,512]{3,2,1,0:T(8,128)S(1)} %bitcast_select_fusion.12), channel_id=1, source_target_pairs={{0,2},{1,5},{2,0},{3,7},{4,6},{5,1},{6,4},{7,3},{8,10},{9,13},{10,... | collective-permute-start | bytes 393224 | tf_op jit(solution)/shard_map/ppermute | solution.py:85
  111.5 6.4 %collective-permute-start.29 = (f32[2,2,16,512]{3,2,1,0:T(8,128)S(1)}, f32[2,2,16,512]{3,2,1,0:T(8,128)S(1)}, u32[]{:S(2)}, u32[]{:S(2)}) collective-permute-start(f32[2,2,16,512]{3,2,1,0:T(8,128)S(1)} %bitcast_select_fusion.10), channel_id=1, source_target_pairs={{0,2},{1,5},{2,0},{3,7},{4,6},{5,1},{6,4},{7,3},{8,10},{9,13},{10,... | collective-permute-start | bytes 393224 | tf_op jit(solution)/shard_map/ppermute | solution.py:85
  113.1 5.9 %collective-permute-start.58 = (f32[2,16,512]{2,1,0:T(8,128)S(1)}, f32[2,16,512]{2,1,0:T(8,128)S(1)}, u32[]{:S(2)}, u32[]{:S(2)}) collective-permute-start(f32[2,16,512]{2,1,0:T(8,128)S(1)} %dynamic-slice_bitcast_fusion.1), channel_id=1, source_target_pairs={{0,4},{1,3},{2,6},{3,1},{4,0},{5,7},{6,2},{7,5},{8,12},{9,11},{10,... | collective-permute-start | bytes 196616 | tf_op jit(solution)/shard_map/ppermute | solution.py:85
  114.1 7.1 %collective-permute-start.62 = (f32[2,16,512]{2,1,0:T(8,128)S(1)}, f32[2,16,512]{2,1,0:T(8,128)S(1)}, u32[]{:S(2)}, u32[]{:S(2)}) collective-permute-start(f32[2,16,512]{2,1,0:T(8,128)S(1)} %dynamic-slice_bitcast_fusion), channel_id=1, source_target_pairs={{0,4},{1,3},{2,6},{3,1},{4,0},{5,7},{6,2},{7,5},{8,12},{9,11},{10,... | collective-permute-start | bytes 196616 | tf_op jit(solution)/shard_map/ppermute | solution.py:85
  115.3 6.8 %collective-permute-start.26 = (f32[2,16,512]{2,1,0:T(8,128)S(1)}, f32[2,16,512]{2,1,0:T(8,128)S(1)}, u32[]{:S(2)}, u32[]{:S(2)}) collective-permute-start(f32[2,16,512]{2,1,0:T(8,128)S(1)} %dynamic-slice_bitcast_fusion.5), channel_id=1, source_target_pairs={{0,4},{1,3},{2,6},{3,1},{4,0},{5,7},{6,2},{7,5},{8,12},{9,11},{10,... | collective-permute-start | bytes 196616 | tf_op jit(solution)/shard_map/ppermute | solution.py:85
  118.0 6.2 %collective-permute-start.30 = (f32[2,16,512]{2,1,0:T(8,128)S(1)}, f32[2,16,512]{2,1,0:T(8,128)S(1)}, u32[]{:S(2)}, u32[]{:S(2)}) collective-permute-start(f32[2,16,512]{2,1,0:T(8,128)S(1)} %dynamic-slice_bitcast_fusion.4), channel_id=1, source_target_pairs={{0,4},{1,3},{2,6},{3,1},{4,0},{5,7},{6,2},{7,5},{8,12},{9,11},{10,... | collective-permute-start | bytes 196616 | tf_op jit(solution)/shard_map/ppermute | solution.py:85
  119.0 6.2 %collective-permute-start.59 = (f32[16,512]{1,0:T(8,128)S(1)}, f32[16,512]{1,0:T(8,128)S(1)}, u32[]{:S(2)}, u32[]{:S(2)}) collective-permute-start(f32[16,512]{1,0:T(8,128)S(1)} %dynamic-slice_bitcast_fusion.9), channel_id=1, source_target_pairs={{0,8},{1,9},{2,10},{3,11},{4,12},{5,13},{6,14},{7,15},{8,0},{9,1},... | collective-permute-start | bytes 98312 | tf_op jit(solution)/shard_map/ppermute | solution.py:85
  121.2 5.2 %collective-permute-start.63 = (f32[16,512]{1,0:T(8,128)S(1)}, f32[16,512]{1,0:T(8,128)S(1)}, u32[]{:S(2)}, u32[]{:S(2)}) collective-permute-start(f32[16,512]{1,0:T(8,128)S(1)} %dynamic-slice_bitcast_fusion.8), channel_id=1, source_target_pairs={{0,8},{1,9},{2,10},{3,11},{4,12},{5,13},{6,14},{7,15},{8,0},{9,1},... | collective-permute-start | bytes 98312 | tf_op jit(solution)/shard_map/ppermute | solution.py:85
  122.1 4.9 %collective-permute-start.27 = (f32[16,512]{1,0:T(8,128)S(1)}, f32[16,512]{1,0:T(8,128)S(1)}, u32[]{:S(2)}, u32[]{:S(2)}) collective-permute-start(f32[16,512]{1,0:T(8,128)S(1)} %dynamic-slice_bitcast_fusion.13), channel_id=1, source_target_pairs={{0,8},{1,9},{2,10},{3,11},{4,12},{5,13},{6,14},{7,15},{8,0},{9,1},... | collective-permute-start | bytes 98312 | tf_op jit(solution)/shard_map/ppermute | solution.py:85
  124.3 5.2 %collective-permute-start.31 = (f32[16,512]{1,0:T(8,128)S(1)}, f32[16,512]{1,0:T(8,128)S(1)}, u32[]{:S(2)}, u32[]{:S(2)}) collective-permute-start(f32[16,512]{1,0:T(8,128)S(1)} %dynamic-slice_bitcast_fusion.12), channel_id=1, source_target_pairs={{0,8},{1,9},{2,10},{3,11},{4,12},{5,13},{6,14},{7,15},{8,0},{9,1},... | collective-permute-start | bytes 98312 | tf_op jit(solution)/shard_map/ppermute | solution.py:85
  (21 other events, 119.4 us)

commit v10 on v9

--- a/solution.py
+++ b/solution.py
@@ -8,7 +8,6 @@
 from jax.sharding import PartitionSpec as P
 
 ITERS = 2
-PIECES = 2
 
 
 def bit_orders(m, descending):
@@ -88,49 +87,50 @@
     return acc
 
 
-def exchange_kernel(states, pieces, occ_ref, *refs):
-    mine, theirs = refs[:pieces], refs[pieces:2 * pieces]
-    vir_ref = refs[2 * pieces]
-    keep, send = refs[2 * pieces + 1:3 * pieces + 1], refs[3 * pieces + 1:4 * pieces + 1]
-    r_ref = refs[4 * pieces + 1]
+def exchange_kernel(states, occ_ref, *refs):
+    mine, theirs = refs[:states], refs[states:2 * states]
+    vir_ref = refs[2 * states]
+    keep, send = refs[2 * states + 1:3 * states + 1], refs[3 * states + 1:4 * states + 1]
+    r_ref = refs[4 * states + 1]
     split = mine[0].shape[0]
-    width = mine[0].shape[1]
+    nvir = vir_ref.shape[1]
 
     @pl.when(pl.program_id(0) == 0)
     def _():
-        for q in range(pieces):
-            keep[q][...] = jnp.zeros_like(keep[q])
-            send[q][...] = jnp.zeros_like(send[q])
-            r_ref[:split, q * width:(q + 1) * width] = mine[q][...]
-            r_ref[split:, q * width:(q + 1) * width] = theirs[q][...]
+        for s in range(states):
+            keep[s][...] = jnp.zeros_like(keep[s])
+            send[s][...] = jnp.zeros_like(send[s])
+            r_ref[:split, s * nvir:(s + 1) * nvir] = mine[s][...]
+            r_ref[split:, s * nvir:(s + 1) * nvir] = theirs[s][...]
 
     half = jnp.dot(occ_ref[0], r_ref[...], preferred_element_type=jnp.float32).astype(jnp.bfloat16)
     vir = vir_ref[0]
-    term = lax.dot_general(half, vir, (((1,), (1,)), ((), ())), preferred_element_type=jnp.float32)
-    for q in range(pieces):
-        keep[q][...] += term[:split, q * width:(q + 1) * width]
-        send[q][...] += term[split:, q * width:(q + 1) * width]
+    for s in range(states):
+        term = lax.dot_general(
+            half[:, s * nvir:(s + 1) * nvir], vir, (((1,), (1,)), ((), ())), preferred_element_type=jnp.float32
+        )
+        keep[s][...] += term[:split]
+        send[s][...] += term[split:]
 
 
 def exchange_part(occ_ints, mine, theirs, vir_ints):
     local_aux, nocc, _ = occ_ints.shape
     nvir = vir_ints.shape[1]
-    pieces = len(mine)
-    width = nvir // pieces
-    piece = pl.BlockSpec((nocc // 2, width), lambda p: (0, 0))
-    out = jax.ShapeDtypeStruct((nocc // 2, width), jnp.float32)
+    states = len(mine)
+    piece = pl.BlockSpec((nocc // 2, nvir), lambda p: (0, 0))
+    out = jax.ShapeDtypeStruct((nocc // 2, nvir), jnp.float32)
     results = pl.pallas_call(
-        functools.partial(exchange_kernel, 1, pieces),
+        functools.partial(exchange_kernel, states),
         grid=(local_aux,),
         in_specs=[pl.BlockSpec((1, nocc, nocc), lambda p: (p, 0, 0))]
-        + [piece] * (2 * pieces)
+        + [piece] * (2 * states)
         + [pl.BlockSpec((1, nvir, nvir), lambda p: (p, 0, 0))],
-        out_specs=[piece] * (2 * pieces),
-        out_shape=[out] * (2 * pieces),
-        scratch_shapes=[pltpu.VMEM((nocc, nvir), jnp.bfloat16)],
+        out_specs=[piece] * (2 * states),
+        out_shape=[out] * (2 * states),
+        scratch_shapes=[pltpu.VMEM((nocc, states * nvir), jnp.bfloat16)],
         compiler_params=pltpu.CompilerParams(dimension_semantics=("arbitrary",)),
     )(occ_ints, *mine, *theirs, vir_ints)
-    return results[:pieces], results[pieces:]
+    return results[:states], results[states:]
 
 
 def order_columns(occ_ints, n, core):
@@ -165,20 +165,15 @@
     my_occ = lax.dynamic_slice_in_dim(occ_energy, position * own_rows, own_rows, 0)
     denom = vir_energy[None, None, :] - my_occ[:, None, None]
     ordered_occ = order_columns(order_rows(occ_ints, n, position & 1), n, position & 1)
-    finals = []
-    for state in range(states):
-        own_rhs = rhs[:, state, :]
-        own_denom = denom[:, 0, :]
-        resp = own_rhs / own_denom
-        for step in range(ITERS):
-            rounded = resp.astype(jnp.bfloat16)
-            width = nvir // PIECES
-            got = [gather_rows(rounded[:, q * width:(q + 1) * width], n) for q in range(PIECES)]
-            keep, send = exchange_part(ordered_occ, [g[0] for g in got], [g[1] for g in got], vir_ints)
-            exchange = jnp.concatenate([scatter_sum(k, t, n) for k, t in zip(keep, send)], axis=1)
-            resp = 0.4 * resp + 0.6 * (own_rhs - exchange) / own_denom
-        finals.append(resp)
-    response = jnp.stack(finals, axis=1)
+    own_denom = denom[:, 0, :]
+    resps = [rhs[:, state, :] / own_denom for state in range(states)]
+    for step in range(ITERS):
+        got = [gather_rows(resp.astype(jnp.bfloat16), n) for resp in resps]
+        keep, send = exchange_part(ordered_occ, [g[0] for g in got], [g[1] for g in got], vir_ints)
+        for state in range(states):
+            exchange = scatter_sum(keep[state], send[state], n)
+            resps[state] = 0.4 * resps[state] + 0.6 * (rhs[:, state, :] - exchange) / own_denom
+    response = jnp.stack(resps, axis=1)
     return response
 
 

time: 131 us -> 116 us (0.89)
  starting transfers between devices: 64 us -> 35.7 us
  waiting for transfers between devices: 21.4 us -> 46 us
  Pallas kernels: 28.3 us -> 19.1 us
  local copies, waits for them, and re-layouts: 6.22 us -> 4.19 us
    ppermute x24 -> x12, starting transfers between devices: 29.8 us -> 16.2 us  [scatter_sum(): acc = kept + lax.ppermute(sent, 'aux', partners(n, b0, b1))]
    ppermute x24 -> x12, starting transfers between devices: 31.2 us -> 18.2 us  [gather_rows(): theirs = lax.ppermute(acc, 'aux', partners(n, b0, b1))]
    ppermute x24 -> x12, waiting for transfers between devices: 12.2 us -> 23.6 us  [scatter_sum(): acc = kept + lax.ppermute(sent, 'aux', partners(n, b0, b1))]
    ppermute x24 -> x12, waiting for transfers between devices: 7.05 us -> 17.4 us  [gather_rows(): theirs = lax.ppermute(acc, 'aux', partners(n, b0, b1))]
    pallas_call x4 -> x2, Pallas kernels: 28.3 us -> 19.1 us  [exchange_part(): pl.pallas_call(functools.partial(exchange_kernel, states), grid=(local_au...]
    ppermute x8 -> x4, waiting for transfers between devices: 0.02 us -> 3.23 us  [scatter_sum(): lax.ppermute(send, 'aux', partners(n, 0, 0)).reshape(shape)]
    unnamed x42 -> x18, local copies, waits for them, and re-layouts: 3.31 us -> 1.39 us
    ppermute x8 -> x4, starting transfers between devices: 1.65 us -> 0.28 us  [gather_rows(): return (flat, lax.ppermute(flat, 'aux', partners(n, 0, 0)))]
  transfers between devices with their start and end apart: 64 -> 32, of which waited for: 19 -> 25; matrix products, arithmetic and copies ran while one was open for 7% -> 8% of each run, Pallas kernels for 22% -> 0%
where the time goes in v10:
time: 116 us; the launch traced here: 115 us
  waiting for transfers between devices  46 us (40%)
  starting transfers between devices  35.7 us (31%)
  Pallas kernels  19.1 us (16%)
  other arithmetic  8.49 us (7%)
  local copies, waits for them, and re-layouts  4.19 us (4%)
    ppermute x12, waiting for transfers between devices, scatter_sum(): acc = kept + lax.ppermute(sent, 'aux', partners(n, b0, b1))  23.6 us
    pallas_call x2, Pallas kernels, exchange_part(): pl.pallas_call(functools.partial(exchange_kernel, states), grid=(local_au...  19.1 us
    ppermute x12, starting transfers between devices, gather_rows(): theirs = lax.ppermute(acc, 'aux', partners(n, b0, b1))  18.2 us
    ppermute x12, waiting for transfers between devices, gather_rows(): theirs = lax.ppermute(acc, 'aux', partners(n, b0, b1))  17.4 us
    ppermute x12, starting transfers between devices, scatter_sum(): acc = kept + lax.ppermute(sent, 'aux', partners(n, b0, b1))  16.2 us
    add x4, other arithmetic, scatter_sum(): keep.reshape(shape)  4.44 us
    ppermute x4, waiting for transfers between devices, scatter_sum(): lax.ppermute(send, 'aux', partners(n, 0, 0)).reshape(shape)  3.23 us
  transfers between devices with their start and end apart: 32, of which 25 were waited for; matrix products, arithmetic and copies ran while one was open for 8% of the time, Pallas kernels for 0%

profile of v10, /device:TPU:0, one launch (start us, length us, event | category | flops | bytes accessed | tf_op | source)
XLA Modules:
  0.0 115.1 jit_solution(15218072460613661771)
XLA Ops:
  0.0 1.1 fusion.32
  1.1 0.8 dynamic_slice.103
  1.9 0.8 fusion.8
  2.6 4.1 %collective-permute-start.3 = (bf16[1,16,1024]{2,1,0:T(8,128)(2,1)S(1)}, bf16[1,16,1024]{2,1,0:T(8,128)(2,1)S(1)}, u32[]{:S(2)}, u32[]{:S(2)}) collective-permute-start(bf16[1,16,1024]{2,1,0:T(8,128)(2,1)S(1)} %get-tuple-element.55), channel_id=1, source_target_pairs={{0,8},{1,9},{2,10},{3,11},{4,12},{5,13},{6,14},{7,15},{8,0},{9,1},... | collective-permute-start | bytes 98312 | tf_op jit(solution)/shard_map/ppermute | solution.py:36
  6.8 1.1 fusion.1
  7.9 1.1 fusion
  9.1 1.9 %collective-permute-start.4 = (bf16[2,16,1024]{2,1,0:T(8,128)(2,1)S(1)}, bf16[2,16,1024]{2,1,0:T(8,128)(2,1)S(1)}, u32[]{:S(2)}, u32[]{:S(2)}) collective-permute-start(bf16[2,16,1024]{2,1,0:T(8,128)(2,1)S(1)} %pad_maximum_fusion.7), channel_id=1, source_target_pairs={{0,4},{1,3},{2,6},{3,1},{4,0},{5,7},{6,2},{7,5},{8,12},{9,11},{10,... | collective-permute-start | bytes 196616 | tf_op jit(solution)/shard_map/ppermute | solution.py:36
  11.0 0.6 collective-permute-done
  11.6 1.6 %collective-permute-start.1 = (bf16[2,16,1024]{2,1,0:T(8,128)(2,1)S(1)}, bf16[2,16,1024]{2,1,0:T(8,128)(2,1)S(1)}, u32[]{:S(2)}, u32[]{:S(2)}) collective-permute-start(bf16[2,16,1024]{2,1,0:T(8,128)(2,1)S(1)} %pad_maximum_fusion.6), channel_id=1, source_target_pairs={{0,4},{1,3},{2,6},{3,1},{4,0},{5,7},{6,2},{7,5},{8,12},{9,11},{10,... | collective-permute-start | bytes 196616 | tf_op jit(solution)/shard_map/ppermute | solution.py:36
  13.5 1.8 %collective-permute-start.5 = (bf16[4,16,1024]{2,1,0:T(8,128)(2,1)S(1)}, bf16[4,16,1024]{2,1,0:T(8,128)(2,1)S(1)}, u32[]{:S(2)}, u32[]{:S(2)}) collective-permute-start(bf16[4,16,1024]{2,1,0:T(8,128)(2,1)S(1)} %bitcast.261), channel_id=1, source_target_pairs={{0,2},{1,5},{2,0},{3,7},{4,6},{5,1},{6,4},{7,3},{8,10},{9,13},{10,... | collective-permute-start | bytes 393224 | tf_op jit(solution)/shard_map/ppermute | solution.py:36
  15.3 1.3 %collective-permute-done.1 = bf16[2,16,1024]{2,1,0:T(8,128)(2,1)S(1)} collective-permute-done((bf16[2,16,1024]{2,1,0:T(8,128)(2,1)S(1)}, bf16[2,16,1024]{2,1,0:T(8,128)(2,1)S(1)}, u32[]{:S(2)}, u32[]{:S(2)}) %collective-permute-start.1) | collective-permute-done | bytes 65568 | tf_op jit(solution)/shard_map/ppermute | solution.py:36
  16.6 1.6 %collective-permute-start.2 = (bf16[4,16,1024]{2,1,0:T(8,128)(2,1)S(1)}, bf16[4,16,1024]{2,1,0:T(8,128)(2,1)S(1)}, u32[]{:S(2)}, u32[]{:S(2)}) collective-permute-start(bf16[4,16,1024]{2,1,0:T(8,128)(2,1)S(1)} %bitcast.262), channel_id=1, source_target_pairs={{0,2},{1,5},{2,0},{3,7},{4,6},{5,1},{6,4},{7,3},{8,10},{9,13},{10,... | collective-permute-start | bytes 393224 | tf_op jit(solution)/shard_map/ppermute | solution.py:36
  18.2 0.4 collective-permute-done.5
  18.7 2.9 %collective-permute-done.2 = bf16[4,16,1024]{2,1,0:T(8,128)(2,1)S(1)} collective-permute-done((bf16[4,16,1024]{2,1,0:T(8,128)(2,1)S(1)}, bf16[4,16,1024]{2,1,0:T(8,128)(2,1)S(1)}, u32[]{:S(2)}, u32[]{:S(2)}) %collective-permute-start.2) | collective-permute-done | bytes 131104 | tf_op jit(solution)/shard_map/ppermute | solution.py:36
  21.9 1.1 convolution_convert_fusion
  23.0 0.3 collective-permute-done.6.refs_2_
  23.3 0.3 copy-done.4
  23.7 0.3 copy-done.6
  24.0 9.5 %shard_map.55 = (f32[128,1024]{1,0:T(8,128)}, f32[128,1024]{1,0:T(8,128)}, f32[128,1024]{1,0:T(8,128)}, f32[128,1024]{1,0:T(8,128)}) custom-call(bf16[4,256,256]{2,1,0:T(8,128)(2,1)} %bitcast.224, bf16[128,1024]{1,0:T(8,128)(2,1)} %bitcast.258, bf16[128,1024]{1,0:T(8,128)(2,1)} %bitcast.254, bf16[128,1024]{1,0:T(8,128)(2,1)} %copy-done.6, ...), custom_call_target="tpu_custom_call" | custom-call | tf_op jit(solution)/shard_map/pallas_call | solution.py:122
  34.1 1.6 %collective-permute-done.8 = f32[128,1024]{1,0:T(8,128)S(1)} collective-permute-done((f32[128,1024]{1,0:T(8,128)}, f32[128,1024]{1,0:T(8,128)S(1)}, u32[]{:S(2)}, u32[]{:S(2)}) %collective-permute-start.8) | collective-permute-done | bytes 524320 | tf_op jit(solution)/shard_map/ppermute | solution.py:63
  35.7 1.1 add.178
  36.8 1.6 %collective-permute-start.9 = (f32[2,2,16,1024]{3,2,1,0:T(8,128)S(1)}, f32[2,2,16,1024]{3,2,1,0:T(8,128)S(1)}, u32[]{:S(2)}, u32[]{:S(2)}) collective-permute-start(f32[2,2,16,1024]{3,2,1,0:T(8,128)S(1)} %bitcast_select_fusion.8), channel_id=1, source_target_pairs={{0,2},{1,5},{2,0},{3,7},{4,6},{5,1},{6,4},{7,3},{8,10},{9,13},{10,... | collective-permute-start | bytes 786440 | tf_op jit(solution)/shard_map/ppermute | solution.py:84
  38.4 1.1 add.192
  39.5 0.6 collective-permute-start.16
  40.1 3.1 %collective-permute-done.9 = f32[2,2,16,1024]{3,2,1,0:T(8,128)S(1)} collective-permute-done((f32[2,2,16,1024]{3,2,1,0:T(8,128)S(1)}, f32[2,2,16,1024]{3,2,1,0:T(8,128)S(1)}, u32[]{:S(2)}, u32[]{:S(2)}) %collective-permute-start.9) | collective-permute-done | bytes 262176 | tf_op jit(solution)/shard_map/ppermute | solution.py:84
  43.3 1.6 %collective-permute-start.10 = (f32[2,16,1024]{2,1,0:T(8,128)S(1)}, f32[2,16,1024]{2,1,0:T(8,128)S(1)}, u32[]{:S(2)}, u32[]{:S(2)}) collective-permute-start(f32[2,16,1024]{2,1,0:T(8,128)S(1)} %dynamic-slice_bitcast_fusion.3), channel_id=1, source_target_pairs={{0,4},{1,3},{2,6},{3,1},{4,0},{5,7},{6,2},{7,5},{8,12},{9,11},{10,... | collective-permute-start | bytes 393224 | tf_op jit(solution)/shard_map/ppermute | solution.py:84
  45.0 1.7 %collective-permute-done.16 = f32[2,2,16,1024]{3,2,1,0:T(8,128)S(1)} collective-permute-done((f32[2,2,16,1024]{3,2,1,0:T(8,128)S(1)}, f32[2,2,16,1024]{3,2,1,0:T(8,128)S(1)}, u32[]{:S(2)}, u32[]{:S(2)}) %collective-permute-start.16) | collective-permute-done | bytes 262176 | tf_op jit(solution)/shard_map/ppermute | solution.py:84
  46.8 1.6 %collective-permute-start.17 = (f32[2,16,1024]{2,1,0:T(8,128)S(1)}, f32[2,16,1024]{2,1,0:T(8,128)S(1)}, u32[]{:S(2)}, u32[]{:S(2)}) collective-permute-start(f32[2,16,1024]{2,1,0:T(8,128)S(1)} %dynamic-slice_bitcast_fusion.2), channel_id=1, source_target_pairs={{0,4},{1,3},{2,6},{3,1},{4,0},{5,7},{6,2},{7,5},{8,12},{9,11},{10,... | collective-permute-start | bytes 393224 | tf_op jit(solution)/shard_map/ppermute | solution.py:84
  48.5 2.5 %collective-permute-start.11 = (f32[16,1024]{1,0:T(8,128)S(1)}, f32[16,1024]{1,0:T(8,128)S(1)}, u32[]{:S(2)}, u32[]{:S(2)}) collective-permute-start(f32[16,1024]{1,0:T(8,128)S(1)} %dynamic-slice_bitcast_fusion.7), channel_id=1, source_target_pairs={{0,8},{1,9},{2,10},{3,11},{4,12},{5,13},{6,14},{7,15},{8,0},{9,1},... | collective-permute-start | bytes 196616 | tf_op jit(solution)/shard_map/ppermute | solution.py:84
  51.0 1.5 %collective-permute-done.17 = f32[2,16,1024]{2,1,0:T(8,128)S(1)} collective-permute-done((f32[2,16,1024]{2,1,0:T(8,128)S(1)}, f32[2,16,1024]{2,1,0:T(8,128)S(1)}, u32[]{:S(2)}, u32[]{:S(2)}) %collective-permute-start.17) | collective-permute-done | bytes 131104 | tf_op jit(solution)/shard_map/ppermute | solution.py:84
  52.6 2.6 %collective-permute-start.18 = (f32[16,1024]{1,0:T(8,128)S(1)}, f32[16,1024]{1,0:T(8,128)S(1)}, u32[]{:S(2)}, u32[]{:S(2)}) collective-permute-start(f32[16,1024]{1,0:T(8,128)S(1)} %dynamic-slice_bitcast_fusion.6), channel_id=1, source_target_pairs={{0,8},{1,9},{2,10},{3,11},{4,12},{5,13},{6,14},{7,15},{8,0},{9,1},... | collective-permute-start | bytes 196616 | tf_op jit(solution)/shard_map/ppermute | solution.py:84
  55.2 2.6 %collective-permute-done.18 = f32[16,1024]{1,0:T(8,128)S(1)} collective-permute-done((f32[16,1024]{1,0:T(8,128)S(1)}, f32[16,1024]{1,0:T(8,128)S(1)}, u32[]{:S(2)}, u32[]{:S(2)}) %collective-permute-start.18) | collective-permute-done | bytes 65568 | tf_op jit(solution)/shard_map/ppermute | solution.py:84
  57.9 2.7 %collective-permute-start.19 = (bf16[1,16,1024]{2,1,0:T(8,128)(2,1)S(1)}, bf16[1,16,1024]{2,1,0:T(8,128)(2,1)S(1)}, u32[]{:S(2)}, u32[]{:S(2)}) collective-permute-start(bf16[1,16,1024]{2,1,0:T(8,128)(2,1)S(1)} %get-tuple-element.21), channel_id=1, source_target_pairs={{0,8},{1,9},{2,10},{3,11},{4,12},{5,13},{6,14},{7,15},{8,0},{9,1},... | collective-permute-start | bytes 98312 | tf_op jit(solution)/shard_map/ppermute | solution.py:36
  60.6 0.3 collective-permute-start.12
  60.9 2.0 %collective-permute-done.19 = bf16[1,16,1024]{2,1,0:T(8,128)(2,1)S(1)} collective-permute-done((bf16[1,16,1024]{2,1,0:T(8,128)(2,1)S(1)}, bf16[1,16,1024]{2,1,0:T(8,128)(2,1)S(1)}, u32[]{:S(2)}, u32[]{:S(2)}) %collective-permute-start.19) | collective-permute-done | bytes 32800 | tf_op jit(solution)/shard_map/ppermute | solution.py:36
  62.9 1.4 %collective-permute-start.20 = (bf16[2,16,1024]{2,1,0:T(8,128)(2,1)S(1)}, bf16[2,16,1024]{2,1,0:T(8,128)(2,1)S(1)}, u32[]{:S(2)}, u32[]{:S(2)}) collective-permute-start(bf16[2,16,1024]{2,1,0:T(8,128)(2,1)S(1)} %pad_maximum_fusion.9), channel_id=1, source_target_pairs={{0,4},{1,3},{2,6},{3,1},{4,0},{5,7},{6,2},{7,5},{8,12},{9,11},{10,... | collective-permute-start | bytes 196616 | tf_op jit(solution)/shard_map/ppermute | solution.py:36
  64.3 1.4 %collective-permute-done.12 = bf16[1,16,1024]{2,1,0:T(8,128)(2,1)S(1)} collective-permute-done((bf16[1,16,1024]{2,1,0:T(8,128)(2,1)S(1)}, bf16[1,16,1024]{2,1,0:T(8,128)(2,1)S(1)}, u32[]{:S(2)}, u32[]{:S(2)}) %collective-permute-start.12) | collective-permute-done | bytes 32800 | tf_op jit(solution)/shard_map/ppermute | solution.py:36
  65.8 0.6 collective-permute-start.13
  66.4 0.9 collective-permute-done.20
  67.3 3.5 %collective-permute-done.13 = bf16[2,16,1024]{2,1,0:T(8,128)(2,1)S(1)} collective-permute-done((bf16[2,16,1024]{2,1,0:T(8,128)(2,1)S(1)}, bf16[2,16,1024]{2,1,0:T(8,128)(2,1)S(1)}, u32[]{:S(2)}, u32[]{:S(2)}) %collective-permute-start.13) | collective-permute-done | bytes 65568 | tf_op jit(solution)/shard_map/ppermute | solution.py:36
  70.8 1.5 %collective-permute-start.21 = (bf16[4,16,1024]{2,1,0:T(8,128)(2,1)S(1)}, bf16[4,16,1024]{2,1,0:T(8,128)(2,1)S(1)}, u32[]{:S(2)}, u32[]{:S(2)}) collective-permute-start(bf16[4,16,1024]{2,1,0:T(8,128)(2,1)S(1)} %bitcast.264), channel_id=1, source_target_pairs={{0,2},{1,5},{2,0},{3,7},{4,6},{5,1},{6,4},{7,3},{8,10},{9,13},{10,... | collective-permute-start | bytes 393224 | tf_op jit(solution)/shard_map/ppermute | solution.py:36
  72.4 0.6 collective-permute-start.14
  73.0 2.8 %collective-permute-done.21 = bf16[4,16,1024]{2,1,0:T(8,128)(2,1)S(1)} collective-permute-done((bf16[4,16,1024]{2,1,0:T(8,128)(2,1)S(1)}, bf16[4,16,1024]{2,1,0:T(8,128)(2,1)S(1)}, u32[]{:S(2)}, u32[]{:S(2)}) %collective-permute-start.21) | collective-permute-done | bytes 131104 | tf_op jit(solution)/shard_map/ppermute | solution.py:36
  76.0 1.4 %collective-permute-done.14 = bf16[4,16,1024]{2,1,0:T(8,128)(2,1)S(1)} collective-permute-done((bf16[4,16,1024]{2,1,0:T(8,128)(2,1)S(1)}, bf16[4,16,1024]{2,1,0:T(8,128)(2,1)S(1)}, u32[]{:S(2)}, u32[]{:S(2)}) %collective-permute-start.14) | collective-permute-done | bytes 131104 | tf_op jit(solution)/shard_map/ppermute | solution.py:36
  77.6 1.5 %collective-permute-done.22.refs_2_ = bf16[128,1024]{1,0:T(8,128)(2,1)S(1)} collective-permute-done((bf16[128,1024]{1,0:T(8,128)(2,1)S(1)}, bf16[128,1024]{1,0:T(8,128)(2,1)S(1)}, u32[]{:S(2)}, u32[]{:S(2)}) %collective-permute-start.22) | collective-permute-done | bytes 262176 | tf_op jit(solution)/shard_map/ppermute | solution.py:53
  79.1 0.7 copy-done.7
  79.8 9.5 %shard_map.56 = (f32[128,1024]{1,0:T(8,128)}, f32[128,1024]{1,0:T(8,128)}, f32[128,1024]{1,0:T(8,128)}, f32[128,1024]{1,0:T(8,128)}) custom-call(bf16[4,256,256]{2,1,0:T(8,128)(2,1)} %bitcast.225, bf16[128,1024]{1,0:T(8,128)(2,1)} %bitcast.260, bf16[128,1024]{1,0:T(8,128)(2,1)} %bitcast.256, bf16[128,1024]{1,0:T(8,128)(2,1)} %copy-done.7, ...), custom_call_target="tpu_custom_call" | custom-call | tf_op jit(solution)/shard_map/pallas_call | solution.py:122
  89.5 0.4 collective-permute-start.28
  89.9 1.6 %collective-permute-done.24 = f32[128,1024]{1,0:T(8,128)S(1)} collective-permute-done((f32[128,1024]{1,0:T(8,128)}, f32[128,1024]{1,0:T(8,128)S(1)}, u32[]{:S(2)}, u32[]{:S(2)}) %collective-permute-start.24) | collective-permute-done | bytes 524320 | tf_op jit(solution)/shard_map/ppermute | solution.py:63
  91.5 1.1 add.198
  92.6 1.4 %collective-permute-start.25 = (f32[2,2,16,1024]{3,2,1,0:T(8,128)S(1)}, f32[2,2,16,1024]{3,2,1,0:T(8,128)S(1)}, u32[]{:S(2)}, u32[]{:S(2)}) collective-permute-start(f32[2,2,16,1024]{3,2,1,0:T(8,128)S(1)} %bitcast_select_fusion.4), channel_id=1, source_target_pairs={{0,2},{1,5},{2,0},{3,7},{4,6},{5,1},{6,4},{7,3},{8,10},{9,13},{10,... | collective-permute-start | bytes 786440 | tf_op jit(solution)/shard_map/ppermute | solution.py:84
  94.0 1.1 add.204
  95.2 0.8 collective-permute-start.29
  96.0 3.1 %collective-permute-done.25 = f32[2,2,16,1024]{3,2,1,0:T(8,128)S(1)} collective-permute-done((f32[2,2,16,1024]{3,2,1,0:T(8,128)S(1)}, f32[2,2,16,1024]{3,2,1,0:T(8,128)S(1)}, u32[]{:S(2)}, u32[]{:S(2)}) %collective-permute-start.25) | collective-permute-done | bytes 262176 | tf_op jit(solution)/shard_map/ppermute | solution.py:84
  99.1 0.5 collective-permute-start.26
  99.6 3.0 %collective-permute-done.29 = f32[2,2,16,1024]{3,2,1,0:T(8,128)S(1)} collective-permute-done((f32[2,2,16,1024]{3,2,1,0:T(8,128)S(1)}, f32[2,2,16,1024]{3,2,1,0:T(8,128)S(1)}, u32[]{:S(2)}, u32[]{:S(2)}) %collective-permute-start.29) | collective-permute-done | bytes 262176 | tf_op jit(solution)/shard_map/ppermute | solution.py:84
  102.7 0.5 collective-permute-start.30
  103.2 1.0 collective-permute-done.26
  104.2 1.1 collective-permute-start.27
  105.3 3.1 %collective-permute-done.30 = f32[2,16,1024]{2,1,0:T(8,128)S(1)} collective-permute-done((f32[2,16,1024]{2,1,0:T(8,128)S(1)}, f32[2,16,1024]{2,1,0:T(8,128)S(1)}, u32[]{:S(2)}, u32[]{:S(2)}) %collective-permute-start.30) | collective-permute-done | bytes 131104 | tf_op jit(solution)/shard_map/ppermute | solution.py:84
  108.4 1.4 %collective-permute-start.31 = (f32[16,1024]{1,0:T(8,128)S(1)}, f32[16,1024]{1,0:T(8,128)S(1)}, u32[]{:S(2)}, u32[]{:S(2)}) collective-permute-start(f32[16,1024]{1,0:T(8,128)S(1)} %dynamic-slice_bitcast_fusion.4), channel_id=1, source_target_pairs={{0,8},{1,9},{2,10},{3,11},{4,12},{5,13},{6,14},{7,15},{8,0},{9,1},... | collective-permute-start | bytes 196616 | tf_op jit(solution)/shard_map/ppermute | solution.py:84
  109.8 1.7 %collective-permute-done.27 = f32[16,1024]{1,0:T(8,128)S(1)} collective-permute-done((f32[16,1024]{1,0:T(8,128)S(1)}, f32[16,1024]{1,0:T(8,128)S(1)}, u32[]{:S(2)}, u32[]{:S(2)}) %collective-permute-start.27) | collective-permute-done | bytes 65568 | tf_op jit(solution)/shard_map/ppermute | solution.py:84
  111.5 2.8 %collective-permute-done.31 = f32[16,1024]{1,0:T(8,128)S(1)} collective-permute-done((f32[16,1024]{1,0:T(8,128)S(1)}, f32[16,1024]{1,0:T(8,128)S(1)}, u32[]{:S(2)}, u32[]{:S(2)}) %collective-permute-start.31) | collective-permute-done | bytes 65568 | tf_op jit(solution)/shard_map/ppermute | solution.py:84
  114.4 0.8 copy.64
  (83 shorter events, 2.6 us)
Async XLA Ops:
  2.6 6.4 %collective-permute-start.3 = (bf16[1,16,1024]{2,1,0:T(8,128)(2,1)S(1)}, bf16[1,16,1024]{2,1,0:T(8,128)(2,1)S(1)}, u32[]{:S(2)}, u32[]{:S(2)}) collective-permute-start(bf16[1,16,1024]{2,1,0:T(8,128)(2,1)S(1)} %get-tuple-element.55), channel_id=1, source_target_pairs={{0,8},{1,9},{2,10},{3,11},{4,12},{5,13},{6,14},{7,15},{8,0},{9,1},... | collective-permute-start | bytes 98312 | tf_op jit(solution)/shard_map/ppermute | solution.py:36
  6.7 4.8 %collective-permute-start = (bf16[1,16,1024]{2,1,0:T(8,128)(2,1)S(1)}, bf16[1,16,1024]{2,1,0:T(8,128)(2,1)S(1)}, u32[]{:S(2)}, u32[]{:S(2)}) collective-permute-start(bf16[1,16,1024]{2,1,0:T(8,128)(2,1)S(1)} %get-tuple-element.56), channel_id=1, source_target_pairs={{0,8},{1,9},{2,10},{3,11},{4,12},{5,13},{6,14},{7,15},{8,0},{9,1},... | collective-permute-start | bytes 98312 | tf_op jit(solution)/shard_map/ppermute | solution.py:36
  9.1 4.3 %collective-permute-start.4 = (bf16[2,16,1024]{2,1,0:T(8,128)(2,1)S(1)}, bf16[2,16,1024]{2,1,0:T(8,128)(2,1)S(1)}, u32[]{:S(2)}, u32[]{:S(2)}) collective-permute-start(bf16[2,16,1024]{2,1,0:T(8,128)(2,1)S(1)} %pad_maximum_fusion.7), channel_id=1, source_target_pairs={{0,4},{1,3},{2,6},{3,1},{4,0},{5,7},{6,2},{7,5},{8,12},{9,11},{10,... | collective-permute-start | bytes 196616 | tf_op jit(solution)/shard_map/ppermute | solution.py:36
  11.6 5.0 %collective-permute-start.1 = (bf16[2,16,1024]{2,1,0:T(8,128)(2,1)S(1)}, bf16[2,16,1024]{2,1,0:T(8,128)(2,1)S(1)}, u32[]{:S(2)}, u32[]{:S(2)}) collective-permute-start(bf16[2,16,1024]{2,1,0:T(8,128)(2,1)S(1)} %pad_maximum_fusion.6), channel_id=1, source_target_pairs={{0,4},{1,3},{2,6},{3,1},{4,0},{5,7},{6,2},{7,5},{8,12},{9,11},{10,... | collective-permute-start | bytes 196616 | tf_op jit(solution)/shard_map/ppermute | solution.py:36
  13.5 5.0 %collective-permute-start.5 = (bf16[4,16,1024]{2,1,0:T(8,128)(2,1)S(1)}, bf16[4,16,1024]{2,1,0:T(8,128)(2,1)S(1)}, u32[]{:S(2)}, u32[]{:S(2)}) collective-permute-start(bf16[4,16,1024]{2,1,0:T(8,128)(2,1)S(1)} %bitcast.261), channel_id=1, source_target_pairs={{0,2},{1,5},{2,0},{3,7},{4,6},{5,1},{6,4},{7,3},{8,10},{9,13},{10,... | collective-permute-start | bytes 393224 | tf_op jit(solution)/shard_map/ppermute | solution.py:36
  16.6 5.0 %collective-permute-start.2 = (bf16[4,16,1024]{2,1,0:T(8,128)(2,1)S(1)}, bf16[4,16,1024]{2,1,0:T(8,128)(2,1)S(1)}, u32[]{:S(2)}, u32[]{:S(2)}) collective-permute-start(bf16[4,16,1024]{2,1,0:T(8,128)(2,1)S(1)} %bitcast.262), channel_id=1, source_target_pairs={{0,2},{1,5},{2,0},{3,7},{4,6},{5,1},{6,4},{7,3},{8,10},{9,13},{10,... | collective-permute-start | bytes 393224 | tf_op jit(solution)/shard_map/ppermute | solution.py:36
  18.6 4.7 %copy-start = (bf16[2,2,2,16,1024]{4,3,2,1,0:T(8,128)(2,1)}, bf16[2,2,2,16,1024]{4,3,2,1,0:T(8,128)(2,1)S(1)}, u32[]{:S(2)}) copy-start(bf16[2,2,2,16,1024]{4,3,2,1,0:T(8,128)(2,1)S(1)} %maximum_select_fusion.1) | copy-start | bytes 786436
  18.6 4.4 %collective-permute-start.7 = (bf16[128,1024]{1,0:T(8,128)(2,1)S(1)}, bf16[128,1024]{1,0:T(8,128)(2,1)S(1)}, u32[]{:S(2)}, u32[]{:S(2)}) collective-permute-start(bf16[128,1024]{1,0:T(8,128)(2,1)S(1)} %bitcast.253), channel_id=1, source_target_pairs={{0,1},{1,0},{2,3},{3,2},{4,5},{5,4},{6,7},{7,6},{8,9},{9,8},{10,11... | collective-permute-start | bytes 786440 | tf_op jit(solution)/shard_map/ppermute | solution.py:53
  21.7 1.6 %copy-start.2 = (bf16[2,2,2,16,1024]{4,3,2,1,0:T(8,128)(2,1)}, bf16[2,2,2,16,1024]{4,3,2,1,0:T(8,128)(2,1)S(1)}, u32[]{:S(2)}) copy-start(bf16[2,2,2,16,1024]{4,3,2,1,0:T(8,128)(2,1)S(1)} %maximum_select_fusion) | copy-start | bytes 786436
  21.7 1.6 %collective-permute-start.6 = (bf16[128,1024]{1,0:T(8,128)(2,1)S(1)}, bf16[128,1024]{1,0:T(8,128)(2,1)S(1)}, u32[]{:S(2)}, u32[]{:S(2)}) collective-permute-start(bf16[128,1024]{1,0:T(8,128)(2,1)S(1)} %bitcast.257), channel_id=1, source_target_pairs={{0,1},{1,0},{2,3},{3,2},{4,5},{5,4},{6,7},{7,6},{8,9},{9,8},{10,11... | collective-permute-start | bytes 786440 | tf_op jit(solution)/shard_map/ppermute | solution.py:53
  23.0 0.7 copy-start.4
  23.3 0.7 copy-start.6
  24.0 33.8 %copy-start.8 = (f32[1024]{0:T(1024)S(1)}, f32[1024]{0:T(1024)}, u32[]{:S(2)}) copy-start(f32[1024]{0:T(1024)} %param.7) | copy-start | bytes 12292
  33.6 2.1 %collective-permute-start.8 = (f32[128,1024]{1,0:T(8,128)}, f32[128,1024]{1,0:T(8,128)S(1)}, u32[]{:S(2)}, u32[]{:S(2)}) collective-permute-start(f32[128,1024]{1,0:T(8,128)} %get-tuple-element.14), channel_id=1, source_target_pairs={{0,1},{1,0},{2,3},{3,2},{4,5},{5,4},{6,7},{7,6},{8,9},{9,8},{10,11... | collective-permute-start | bytes 1572872 | tf_op jit(solution)/shard_map/ppermute | solution.py:63
  33.8 4.6 %collective-permute-start.15 = (f32[128,1024]{1,0:T(8,128)}, f32[128,1024]{1,0:T(8,128)S(1)}, u32[]{:S(2)}, u32[]{:S(2)}) collective-permute-start(f32[128,1024]{1,0:T(8,128)} %get-tuple-element.16), channel_id=1, source_target_pairs={{0,1},{1,0},{2,3},{3,2},{4,5},{5,4},{6,7},{7,6},{8,9},{9,8},{10,11... | collective-permute-start | bytes 1572872 | tf_op jit(solution)/shard_map/ppermute | solution.py:63
  36.8 6.4 %collective-permute-start.9 = (f32[2,2,16,1024]{3,2,1,0:T(8,128)S(1)}, f32[2,2,16,1024]{3,2,1,0:T(8,128)S(1)}, u32[]{:S(2)}, u32[]{:S(2)}) collective-permute-start(f32[2,2,16,1024]{3,2,1,0:T(8,128)S(1)} %bitcast_select_fusion.8), channel_id=1, source_target_pairs={{0,2},{1,5},{2,0},{3,7},{4,6},{5,1},{6,4},{7,3},{8,10},{9,13},{10,... | collective-permute-start | bytes 786440 | tf_op jit(solution)/shard_map/ppermute | solution.py:84
  39.5 7.2 %collective-permute-start.16 = (f32[2,2,16,1024]{3,2,1,0:T(8,128)S(1)}, f32[2,2,16,1024]{3,2,1,0:T(8,128)S(1)}, u32[]{:S(2)}, u32[]{:S(2)}) collective-permute-start(f32[2,2,16,1024]{3,2,1,0:T(8,128)S(1)} %bitcast_select_fusion.6), channel_id=1, source_target_pairs={{0,2},{1,5},{2,0},{3,7},{4,6},{5,1},{6,4},{7,3},{8,10},{9,13},{10,... | collective-permute-start | bytes 786440 | tf_op jit(solution)/shard_map/ppermute | solution.py:84
  43.3 5.1 %collective-permute-start.10 = (f32[2,16,1024]{2,1,0:T(8,128)S(1)}, f32[2,16,1024]{2,1,0:T(8,128)S(1)}, u32[]{:S(2)}, u32[]{:S(2)}) collective-permute-start(f32[2,16,1024]{2,1,0:T(8,128)S(1)} %dynamic-slice_bitcast_fusion.3), channel_id=1, source_target_pairs={{0,4},{1,3},{2,6},{3,1},{4,0},{5,7},{6,2},{7,5},{8,12},{9,11},{10,... | collective-permute-start | bytes 393224 | tf_op jit(solution)/shard_map/ppermute | solution.py:84
  46.8 5.7 %collective-permute-start.17 = (f32[2,16,1024]{2,1,0:T(8,128)S(1)}, f32[2,16,1024]{2,1,0:T(8,128)S(1)}, u32[]{:S(2)}, u32[]{:S(2)}) collective-permute-start(f32[2,16,1024]{2,1,0:T(8,128)S(1)} %dynamic-slice_bitcast_fusion.2), channel_id=1, source_target_pairs={{0,4},{1,3},{2,6},{3,1},{4,0},{5,7},{6,2},{7,5},{8,12},{9,11},{10,... | collective-permute-start | bytes 393224 | tf_op jit(solution)/shard_map/ppermute | solution.py:84
  48.5 6.7 %collective-permute-start.11 = (f32[16,1024]{1,0:T(8,128)S(1)}, f32[16,1024]{1,0:T(8,128)S(1)}, u32[]{:S(2)}, u32[]{:S(2)}) collective-permute-start(f32[16,1024]{1,0:T(8,128)S(1)} %dynamic-slice_bitcast_fusion.7), channel_id=1, source_target_pairs={{0,8},{1,9},{2,10},{3,11},{4,12},{5,13},{6,14},{7,15},{8,0},{9,1},... | collective-permute-start | bytes 196616 | tf_op jit(solution)/shard_map/ppermute | solution.py:84
  52.6 5.2 %collective-permute-start.18 = (f32[16,1024]{1,0:T(8,128)S(1)}, f32[16,1024]{1,0:T(8,128)S(1)}, u32[]{:S(2)}, u32[]{:S(2)}) collective-permute-start(f32[16,1024]{1,0:T(8,128)S(1)} %dynamic-slice_bitcast_fusion.6), channel_id=1, source_target_pairs={{0,8},{1,9},{2,10},{3,11},{4,12},{5,13},{6,14},{7,15},{8,0},{9,1},... | collective-permute-start | bytes 196616 | tf_op jit(solution)/shard_map/ppermute | solution.py:84
  57.9 5.0 %collective-permute-start.19 = (bf16[1,16,1024]{2,1,0:T(8,128)(2,1)S(1)}, bf16[1,16,1024]{2,1,0:T(8,128)(2,1)S(1)}, u32[]{:S(2)}, u32[]{:S(2)}) collective-permute-start(bf16[1,16,1024]{2,1,0:T(8,128)(2,1)S(1)} %get-tuple-element.21), channel_id=1, source_target_pairs={{0,8},{1,9},{2,10},{3,11},{4,12},{5,13},{6,14},{7,15},{8,0},{9,1},... | collective-permute-start | bytes 98312 | tf_op jit(solution)/shard_map/ppermute | solution.py:36
  60.6 5.2 %collective-permute-start.12 = (bf16[1,16,1024]{2,1,0:T(8,128)(2,1)S(1)}, bf16[1,16,1024]{2,1,0:T(8,128)(2,1)S(1)}, u32[]{:S(2)}, u32[]{:S(2)}) collective-permute-start(bf16[1,16,1024]{2,1,0:T(8,128)(2,1)S(1)} %get-tuple-element.53), channel_id=1, source_target_pairs={{0,8},{1,9},{2,10},{3,11},{4,12},{5,13},{6,14},{7,15},{8,0},{9,1},... | collective-permute-start | bytes 98312 | tf_op jit(solution)/shard_map/ppermute | solution.py:36
  62.9 4.3 %collective-permute-start.20 = (bf16[2,16,1024]{2,1,0:T(8,128)(2,1)S(1)}, bf16[2,16,1024]{2,1,0:T(8,128)(2,1)S(1)}, u32[]{:S(2)}, u32[]{:S(2)}) collective-permute-start(bf16[2,16,1024]{2,1,0:T(8,128)(2,1)S(1)} %pad_maximum_fusion.9), channel_id=1, source_target_pairs={{0,4},{1,3},{2,6},{3,1},{4,0},{5,7},{6,2},{7,5},{8,12},{9,11},{10,... | collective-permute-start | bytes 196616 | tf_op jit(solution)/shard_map/ppermute | solution.py:36
  65.8 5.0 %collective-permute-start.13 = (bf16[2,16,1024]{2,1,0:T(8,128)(2,1)S(1)}, bf16[2,16,1024]{2,1,0:T(8,128)(2,1)S(1)}, u32[]{:S(2)}, u32[]{:S(2)}) collective-permute-start(bf16[2,16,1024]{2,1,0:T(8,128)(2,1)S(1)} %pad_maximum_fusion.8), channel_id=1, source_target_pairs={{0,4},{1,3},{2,6},{3,1},{4,0},{5,7},{6,2},{7,5},{8,12},{9,11},{10,... | collective-permute-start | bytes 196616 | tf_op jit(solution)/shard_map/ppermute | solution.py:36
  70.8 5.0 %collective-permute-start.21 = (bf16[4,16,1024]{2,1,0:T(8,128)(2,1)S(1)}, bf16[4,16,1024]{2,1,0:T(8,128)(2,1)S(1)}, u32[]{:S(2)}, u32[]{:S(2)}) collective-permute-start(bf16[4,16,1024]{2,1,0:T(8,128)(2,1)S(1)} %bitcast.264), channel_id=1, source_target_pairs={{0,2},{1,5},{2,0},{3,7},{4,6},{5,1},{6,4},{7,3},{8,10},{9,13},{10,... | collective-permute-start | bytes 393224 | tf_op jit(solution)/shard_map/ppermute | solution.py:36
  72.4 5.0 %collective-permute-start.14 = (bf16[4,16,1024]{2,1,0:T(8,128)(2,1)S(1)}, bf16[4,16,1024]{2,1,0:T(8,128)(2,1)S(1)}, u32[]{:S(2)}, u32[]{:S(2)}) collective-permute-start(bf16[4,16,1024]{2,1,0:T(8,128)(2,1)S(1)} %bitcast.263), channel_id=1, source_target_pairs={{0,2},{1,5},{2,0},{3,7},{4,6},{5,1},{6,4},{7,3},{8,10},{9,13},{10,... | collective-permute-start | bytes 393224 | tf_op jit(solution)/shard_map/ppermute | solution.py:36
  76.0 3.2 %copy-start.1 = (bf16[2,2,2,16,1024]{4,3,2,1,0:T(8,128)(2,1)}, bf16[2,2,2,16,1024]{4,3,2,1,0:T(8,128)(2,1)S(1)}, u32[]{:S(2)}) copy-start(bf16[2,2,2,16,1024]{4,3,2,1,0:T(8,128)(2,1)S(1)} %maximum_select_fusion.3) | copy-start | bytes 786436
  76.0 1.6 %collective-permute-start.23 = (bf16[128,1024]{1,0:T(8,128)(2,1)S(1)}, bf16[128,1024]{1,0:T(8,128)(2,1)S(1)}, u32[]{:S(2)}, u32[]{:S(2)}) collective-permute-start(bf16[128,1024]{1,0:T(8,128)(2,1)S(1)} %bitcast.255), channel_id=1, source_target_pairs={{0,1},{1,0},{2,3},{3,2},{4,5},{5,4},{6,7},{7,6},{8,9},{9,8},{10,11... | collective-permute-start | bytes 786440 | tf_op jit(solution)/shard_map/ppermute | solution.py:53
  77.5 1.6 %copy-start.3 = (bf16[2,2,2,16,1024]{4,3,2,1,0:T(8,128)(2,1)}, bf16[2,2,2,16,1024]{4,3,2,1,0:T(8,128)(2,1)S(1)}, u32[]{:S(2)}) copy-start(bf16[2,2,2,16,1024]{4,3,2,1,0:T(8,128)(2,1)S(1)} %maximum_select_fusion.2) | copy-start | bytes 786436
  77.5 1.6 %collective-permute-start.22 = (bf16[128,1024]{1,0:T(8,128)(2,1)S(1)}, bf16[128,1024]{1,0:T(8,128)(2,1)S(1)}, u32[]{:S(2)}, u32[]{:S(2)}) collective-permute-start(bf16[128,1024]{1,0:T(8,128)(2,1)S(1)} %bitcast.259), channel_id=1, source_target_pairs={{0,1},{1,0},{2,3},{3,2},{4,5},{5,4},{6,7},{7,6},{8,9},{9,8},{10,11... | collective-permute-start | bytes 786440 | tf_op jit(solution)/shard_map/ppermute | solution.py:53
  77.6 1.5 %copy-start.5 = (bf16[128,1024]{1,0:T(8,128)(2,1)}, bf16[128,1024]{1,0:T(8,128)(2,1)S(1)}, u32[]{:S(2)}) copy-start(bf16[128,1024]{1,0:T(8,128)(2,1)S(1)} %collective-permute-done.23.refs_3_) | copy-start | bytes 786436
  79.1 0.7 copy-start.7
  89.4 2.1 %collective-permute-start.24 = (f32[128,1024]{1,0:T(8,128)}, f32[128,1024]{1,0:T(8,128)S(1)}, u32[]{:S(2)}, u32[]{:S(2)}) collective-permute-start(f32[128,1024]{1,0:T(8,128)} %get-tuple-element.18), channel_id=1, source_target_pairs={{0,1},{1,0},{2,3},{3,2},{4,5},{5,4},{6,7},{7,6},{8,9},{9,8},{10,11... | collective-permute-start | bytes 1572872 | tf_op jit(solution)/shard_map/ppermute | solution.py:63
  89.5 4.5 %collective-permute-start.28 = (f32[128,1024]{1,0:T(8,128)}, f32[128,1024]{1,0:T(8,128)S(1)}, u32[]{:S(2)}, u32[]{:S(2)}) collective-permute-start(f32[128,1024]{1,0:T(8,128)} %get-tuple-element.20), channel_id=1, source_target_pairs={{0,1},{1,0},{2,3},{3,2},{4,5},{5,4},{6,7},{7,6},{8,9},{9,8},{10,11... | collective-permute-start | bytes 1572872 | tf_op jit(solution)/shard_map/ppermute | solution.py:63
  92.6 6.4 %collective-permute-start.25 = (f32[2,2,16,1024]{3,2,1,0:T(8,128)S(1)}, f32[2,2,16,1024]{3,2,1,0:T(8,128)S(1)}, u32[]{:S(2)}, u32[]{:S(2)}) collective-permute-start(f32[2,2,16,1024]{3,2,1,0:T(8,128)S(1)} %bitcast_select_fusion.4), channel_id=1, source_target_pairs={{0,2},{1,5},{2,0},{3,7},{4,6},{5,1},{6,4},{7,3},{8,10},{9,13},{10,... | collective-permute-start | bytes 786440 | tf_op jit(solution)/shard_map/ppermute | solution.py:84
  95.2 7.4 %collective-permute-start.29 = (f32[2,2,16,1024]{3,2,1,0:T(8,128)S(1)}, f32[2,2,16,1024]{3,2,1,0:T(8,128)S(1)}, u32[]{:S(2)}, u32[]{:S(2)}) collective-permute-start(f32[2,2,16,1024]{3,2,1,0:T(8,128)S(1)} %bitcast_select_fusion.2), channel_id=1, source_target_pairs={{0,2},{1,5},{2,0},{3,7},{4,6},{5,1},{6,4},{7,3},{8,10},{9,13},{10,... | collective-permute-start | bytes 786440 | tf_op jit(solution)/shard_map/ppermute | solution.py:84
  99.1 5.0 %collective-permute-start.26 = (f32[2,16,1024]{2,1,0:T(8,128)S(1)}, f32[2,16,1024]{2,1,0:T(8,128)S(1)}, u32[]{:S(2)}, u32[]{:S(2)}) collective-permute-start(f32[2,16,1024]{2,1,0:T(8,128)S(1)} %dynamic-slice_bitcast_fusion.1), channel_id=1, source_target_pairs={{0,4},{1,3},{2,6},{3,1},{4,0},{5,7},{6,2},{7,5},{8,12},{9,11},{10,... | collective-permute-start | bytes 393224 | tf_op jit(solution)/shard_map/ppermute | solution.py:84
  102.7 5.7 %collective-permute-start.30 = (f32[2,16,1024]{2,1,0:T(8,128)S(1)}, f32[2,16,1024]{2,1,0:T(8,128)S(1)}, u32[]{:S(2)}, u32[]{:S(2)}) collective-permute-start(f32[2,16,1024]{2,1,0:T(8,128)S(1)} %dynamic-slice_bitcast_fusion), channel_id=1, source_target_pairs={{0,4},{1,3},{2,6},{3,1},{4,0},{5,7},{6,2},{7,5},{8,12},{9,11},{10,... | collective-permute-start | bytes 393224 | tf_op jit(solution)/shard_map/ppermute | solution.py:84
  104.2 7.3 %collective-permute-start.27 = (f32[16,1024]{1,0:T(8,128)S(1)}, f32[16,1024]{1,0:T(8,128)S(1)}, u32[]{:S(2)}, u32[]{:S(2)}) collective-permute-start(f32[16,1024]{1,0:T(8,128)S(1)} %dynamic-slice_bitcast_fusion.5), channel_id=1, source_target_pairs={{0,8},{1,9},{2,10},{3,11},{4,12},{5,13},{6,14},{7,15},{8,0},{9,1},... | collective-permute-start | bytes 196616 | tf_op jit(solution)/shard_map/ppermute | solution.py:84
  108.4 5.9 %collective-permute-start.31 = (f32[16,1024]{1,0:T(8,128)S(1)}, f32[16,1024]{1,0:T(8,128)S(1)}, u32[]{:S(2)}, u32[]{:S(2)}) collective-permute-start(f32[16,1024]{1,0:T(8,128)S(1)} %dynamic-slice_bitcast_fusion.4), channel_id=1, source_target_pairs={{0,8},{1,9},{2,10},{3,11},{4,12},{5,13},{6,14},{7,15},{8,0},{9,1},... | collective-permute-start | bytes 196616 | tf_op jit(solution)/shard_map/ppermute | solution.py:84

commit v11 on v10

--- a/solution.py
+++ b/solution.py
@@ -60,30 +60,33 @@
     rows = 2 * keep.shape[0] // n
     order0, order1 = bit_orders(m, False)
     shape = (2,) * (m - 1) + (rows,) + keep.shape[1:]
-    acc = keep.reshape(shape) + lax.ppermute(send, "aux", partners(n, 0, 0)).reshape(shape)
+    parts = [keep.reshape(shape), lax.ppermute(send, "aux", partners(n, 0, 0)).reshape(shape)]
     axes0 = list(range(m - 1, 0, -1))
     axes1 = list(axes0)
     for b0, b1 in zip(order0[1:], order1[1:]):
         at0, at1 = axes0.index(b0), axes1.index(b1)
         bit0, bit1 = (me >> b0) & 1, (me >> b1) & 1
-        if at0 == at1:
-            bit = jnp.where(odd, bit1, bit0)
-            kept = lax.dynamic_index_in_dim(acc, bit, axis=at0, keepdims=False)
-            sent = lax.dynamic_index_in_dim(acc, 1 - bit, axis=at0, keepdims=False)
-        else:
-            kept = jnp.where(
-                odd,
-                lax.dynamic_index_in_dim(acc, bit1, axis=at1, keepdims=False),
-                lax.dynamic_index_in_dim(acc, bit0, axis=at0, keepdims=False),
-            )
-            sent = jnp.where(
-                odd,
-                lax.dynamic_index_in_dim(acc, 1 - bit1, axis=at1, keepdims=False),
-                lax.dynamic_index_in_dim(acc, 1 - bit0, axis=at0, keepdims=False),
-            )
-        acc = kept + lax.ppermute(sent, "aux", partners(n, b0, b1))
+
+        def pick(choice):
+            total = 0.0
+            for piece in parts:
+                if at0 == at1:
+                    bit = jnp.where(odd, bit1, bit0)
+                    got = lax.dynamic_index_in_dim(piece, bit ^ choice, axis=at0, keepdims=False)
+                else:
+                    got = jnp.where(
+                        odd,
+                        lax.dynamic_index_in_dim(piece, bit1 ^ choice, axis=at1, keepdims=False),
+                        lax.dynamic_index_in_dim(piece, bit0 ^ choice, axis=at0, keepdims=False),
+                    )
+                total = total + got
+            return total
+
+        kept, sent = pick(0), pick(1)
+        parts = [kept + lax.ppermute(sent, "aux", partners(n, b0, b1))]
         axes0.pop(at0)
         axes1.pop(at1)
+    acc = sum(parts[1:], parts[0])
     return acc
 
 
@@ -162,7 +165,8 @@
     n = nocc // own_rows
     assert n & (n - 1) == 0
     position = lax.axis_index("aux")
-    my_occ = lax.dynamic_slice_in_dim(occ_energy, position * own_rows, own_rows, 0)
+    wanted = position * own_rows + jnp.arange(own_rows)
+    my_occ = jnp.sum(jnp.where(jnp.arange(nocc)[None, :] == wanted[:, None], occ_energy[None, :], 0.0), axis=1)
     denom = vir_energy[None, None, :] - my_occ[:, None, None]
     ordered_occ = order_columns(order_rows(occ_ints, n, position & 1), n, position & 1)
     own_denom = denom[:, 0, :]

time: 116 us -> 115 us (level)
  waiting for transfers between devices: 46 us -> 36.2 us
  starting transfers between devices: 35.7 us -> 41.1 us
  other arithmetic: 8.49 us -> 13.5 us
    ppermute x12, waiting for transfers between devices: 23.6 us -> 15.6 us  [scatter_sum(): parts = [kept + lax.ppermute(sent, 'aux', partners(n, b0, b1))]]
    add x12 -> x13, other arithmetic: 4.68 us -> 8.94 us  [the longest x8 4.54 us: scatter_sum(): parts = [kept + lax.ppermute(sent, 'aux', partners(n, b0, b1))]]
    ppermute x12, starting transfers between devices: 16.2 us -> 20.4 us  [scatter_sum(): parts = [kept + lax.ppermute(sent, 'aux', partners(n, b0, b1))]]
    ppermute x12, waiting for transfers between devices: 17.4 us -> 15.5 us  [gather_rows(): theirs = lax.ppermute(acc, 'aux', partners(n, b0, b1))]
  transfers between devices with their start and end apart: 32 -> 32, of which waited for: 25 -> 26; matrix products, arithmetic and copies ran while one was open for 8% -> 11% of each run, Pallas kernels for 0% -> 0%
where the time goes in v11:
time: 115 us
  starting transfers between devices  41.1 us (36%)
  waiting for transfers between devices  36.2 us (31%)
  Pallas kernels  19.1 us (17%)
  other arithmetic  13.5 us (12%)
  local copies, waits for them, and re-layouts  3.42 us (3%)
    ppermute x12, starting transfers between devices, scatter_sum(): parts = [kept + lax.ppermute(sent, 'aux', partners(n, b0, b1))]  20.4 us
    ppermute x12, starting transfers between devices, gather_rows(): theirs = lax.ppermute(acc, 'aux', partners(n, b0, b1))  19.4 us
    pallas_call x2, Pallas kernels, exchange_part(): pl.pallas_call(functools.partial(exchange_kernel, states), grid=(local_au...  19.1 us
    ppermute x12, waiting for transfers between devices, scatter_sum(): parts = [kept + lax.ppermute(sent, 'aux', partners(n, b0, b1))]  15.6 us
    ppermute x12, waiting for transfers between devices, gather_rows(): theirs = lax.ppermute(acc, 'aux', partners(n, b0, b1))  15.5 us
    add x8, other arithmetic, scatter_sum(): parts = [kept + lax.ppermute(sent, 'aux', partners(n, b0, b1))]  4.54 us
    add x4, other arithmetic, pick(): total = total + got  4.4 us
    ppermute x4, waiting for transfers between devices, scatter_sum(): lax.ppermute(send, 'aux', partners(n, 0, 0)).reshape(shape)  3.23 us
  transfers between devices with their start and end apart: 32, of which 26 were waited for; matrix products, arithmetic and copies ran while one was open for 11% of the time, Pallas kernels for 0%

profile of v11, /device:TPU:0, one launch (start us, length us, event | category | flops | bytes accessed | tf_op | source)
XLA Modules:
  0.0 114.8 jit_solution(12877047180162028451)
XLA Ops:
  0.0 1.1 fusion.40
  1.1 0.9 select_reduce_fusion
  2.0 0.8 fusion.16
  2.7 4.1 %collective-permute-start.3 = (bf16[1,16,1024]{2,1,0:T(8,128)(2,1)S(1)}, bf16[1,16,1024]{2,1,0:T(8,128)(2,1)S(1)}, u32[]{:S(2)}, u32[]{:S(2)}) collective-permute-start(bf16[1,16,1024]{2,1,0:T(8,128)(2,1)S(1)} %get-tuple-element.55), channel_id=1, source_target_pairs={{0,8},{1,9},{2,10},{3,11},{4,12},{5,13},{6,14},{7,15},{8,0},{9,1},... | collective-permute-start | bytes 98312 | tf_op jit(solution)/shard_map/ppermute | solution.py:36
  6.9 1.1 fusion.1
  8.0 1.1 fusion
  9.2 1.9 %collective-permute-start.4 = (bf16[2,16,1024]{2,1,0:T(8,128)(2,1)S(1)}, bf16[2,16,1024]{2,1,0:T(8,128)(2,1)S(1)}, u32[]{:S(2)}, u32[]{:S(2)}) collective-permute-start(bf16[2,16,1024]{2,1,0:T(8,128)(2,1)S(1)} %pad_maximum_fusion.7), channel_id=1, source_target_pairs={{0,4},{1,3},{2,6},{3,1},{4,0},{5,7},{6,2},{7,5},{8,12},{9,11},{10,... | collective-permute-start | bytes 196616 | tf_op jit(solution)/shard_map/ppermute | solution.py:36
  11.1 0.6 collective-permute-done
  11.7 1.6 %collective-permute-start.1 = (bf16[2,16,1024]{2,1,0:T(8,128)(2,1)S(1)}, bf16[2,16,1024]{2,1,0:T(8,128)(2,1)S(1)}, u32[]{:S(2)}, u32[]{:S(2)}) collective-permute-start(bf16[2,16,1024]{2,1,0:T(8,128)(2,1)S(1)} %pad_maximum_fusion.6), channel_id=1, source_target_pairs={{0,4},{1,3},{2,6},{3,1},{4,0},{5,7},{6,2},{7,5},{8,12},{9,11},{10,... | collective-permute-start | bytes 196616 | tf_op jit(solution)/shard_map/ppermute | solution.py:36
  13.6 1.8 %collective-permute-start.5 = (bf16[4,16,1024]{2,1,0:T(8,128)(2,1)S(1)}, bf16[4,16,1024]{2,1,0:T(8,128)(2,1)S(1)}, u32[]{:S(2)}, u32[]{:S(2)}) collective-permute-start(bf16[4,16,1024]{2,1,0:T(8,128)(2,1)S(1)} %bitcast.337), channel_id=1, source_target_pairs={{0,2},{1,5},{2,0},{3,7},{4,6},{5,1},{6,4},{7,3},{8,10},{9,13},{10,... | collective-permute-start | bytes 393224 | tf_op jit(solution)/shard_map/ppermute | solution.py:36
  15.4 1.3 %collective-permute-done.1 = bf16[2,16,1024]{2,1,0:T(8,128)(2,1)S(1)} collective-permute-done((bf16[2,16,1024]{2,1,0:T(8,128)(2,1)S(1)}, bf16[2,16,1024]{2,1,0:T(8,128)(2,1)S(1)}, u32[]{:S(2)}, u32[]{:S(2)}) %collective-permute-start.1) | collective-permute-done | bytes 65568 | tf_op jit(solution)/shard_map/ppermute | solution.py:36
  16.7 1.6 %collective-permute-start.2 = (bf16[4,16,1024]{2,1,0:T(8,128)(2,1)S(1)}, bf16[4,16,1024]{2,1,0:T(8,128)(2,1)S(1)}, u32[]{:S(2)}, u32[]{:S(2)}) collective-permute-start(bf16[4,16,1024]{2,1,0:T(8,128)(2,1)S(1)} %bitcast.338), channel_id=1, source_target_pairs={{0,2},{1,5},{2,0},{3,7},{4,6},{5,1},{6,4},{7,3},{8,10},{9,13},{10,... | collective-permute-start | bytes 393224 | tf_op jit(solution)/shard_map/ppermute | solution.py:36
  18.8 2.9 %collective-permute-done.2 = bf16[4,16,1024]{2,1,0:T(8,128)(2,1)S(1)} collective-permute-done((bf16[4,16,1024]{2,1,0:T(8,128)(2,1)S(1)}, bf16[4,16,1024]{2,1,0:T(8,128)(2,1)S(1)}, u32[]{:S(2)}, u32[]{:S(2)}) %collective-permute-start.2) | collective-permute-done | bytes 131104 | tf_op jit(solution)/shard_map/ppermute | solution.py:36
  22.0 1.1 convolution_convert_fusion
  24.1 9.5 %shard_map.55 = (f32[128,1024]{1,0:T(8,128)}, f32[128,1024]{1,0:T(8,128)}, f32[128,1024]{1,0:T(8,128)}, f32[128,1024]{1,0:T(8,128)}) custom-call(bf16[4,256,256]{2,1,0:T(8,128)(2,1)} %bitcast.292, bf16[128,1024]{1,0:T(8,128)(2,1)} %bitcast.334, bf16[128,1024]{1,0:T(8,128)(2,1)} %bitcast.330, bf16[128,1024]{1,0:T(8,128)(2,1)} %copy-done.6, ...), custom_call_target="tpu_custom_call" | custom-call | tf_op jit(solution)/shard_map/pallas_call | solution.py:125
  34.2 1.6 %collective-permute-done.8 = f32[128,1024]{1,0:T(8,128)S(1)} collective-permute-done((f32[128,1024]{1,0:T(8,128)}, f32[128,1024]{1,0:T(8,128)S(1)}, u32[]{:S(2)}, u32[]{:S(2)}) %collective-permute-start.8) | collective-permute-done | bytes 524320 | tf_op jit(solution)/shard_map/ppermute | solution.py:63
  35.8 1.1 fusion.11
  36.9 1.6 %collective-permute-start.9 = (f32[2,2,16,1024]{3,2,1,0:T(8,128)S(1)}, f32[2,2,16,1024]{3,2,1,0:T(8,128)S(1)}, u32[]{:S(2)}, u32[]{:S(2)}) collective-permute-start(f32[2,2,16,1024]{3,2,1,0:T(8,128)S(1)} %fusion.11), channel_id=1, source_target_pairs={{0,2},{1,5},{2,0},{3,7},{4,6},{5,1},{6,4},{7,3},{8,10},{9,13},{10,... | collective-permute-start | bytes 786440 | tf_op jit(solution)/shard_map/ppermute | solution.py:86
  38.4 1.1 fusion.8
  39.5 0.6 collective-permute-start.16
  40.1 3.2 %collective-permute-done.9 = f32[2,2,16,1024]{3,2,1,0:T(8,128)S(1)} collective-permute-done((f32[2,2,16,1024]{3,2,1,0:T(8,128)S(1)}, f32[2,2,16,1024]{3,2,1,0:T(8,128)S(1)}, u32[]{:S(2)}, u32[]{:S(2)}) %collective-permute-start.9) | collective-permute-done | bytes 262176 | tf_op jit(solution)/shard_map/ppermute | solution.py:86
  43.3 1.1 fusion.13
  44.4 1.6 %collective-permute-start.10 = (f32[2,16,1024]{2,1,0:T(8,128)S(1)}, f32[2,16,1024]{2,1,0:T(8,128)S(1)}, u32[]{:S(2)}, u32[]{:S(2)}) collective-permute-start(f32[2,16,1024]{2,1,0:T(8,128)S(1)} %dynamic-slice_bitcast_fusion.3), channel_id=1, source_target_pairs={{0,4},{1,3},{2,6},{3,1},{4,0},{5,7},{6,2},{7,5},{8,12},{9,11},{10,... | collective-permute-start | bytes 393224 | tf_op jit(solution)/shard_map/ppermute | solution.py:86
  46.1 1.1 fusion.10
  47.3 1.6 %collective-permute-start.17 = (f32[2,16,1024]{2,1,0:T(8,128)S(1)}, f32[2,16,1024]{2,1,0:T(8,128)S(1)}, u32[]{:S(2)}, u32[]{:S(2)}) collective-permute-start(f32[2,16,1024]{2,1,0:T(8,128)S(1)} %dynamic-slice_bitcast_fusion.2), channel_id=1, source_target_pairs={{0,4},{1,3},{2,6},{3,1},{4,0},{5,7},{6,2},{7,5},{8,12},{9,11},{10,... | collective-permute-start | bytes 393224 | tf_op jit(solution)/shard_map/ppermute | solution.py:86
  48.9 0.6 collective-permute-done.10
  49.5 2.6 %collective-permute-start.11 = (f32[16,1024]{1,0:T(8,128)S(1)}, f32[16,1024]{1,0:T(8,128)S(1)}, u32[]{:S(2)}, u32[]{:S(2)}) collective-permute-start(f32[16,1024]{1,0:T(8,128)S(1)} %dynamic-slice_bitcast_fusion.7), channel_id=1, source_target_pairs={{0,8},{1,9},{2,10},{3,11},{4,12},{5,13},{6,14},{7,15},{8,0},{9,1},... | collective-permute-start | bytes 196616 | tf_op jit(solution)/shard_map/ppermute | solution.py:86
  52.1 0.9 collective-permute-done.17
  53.1 2.3 %collective-permute-start.18 = (f32[16,1024]{1,0:T(8,128)S(1)}, f32[16,1024]{1,0:T(8,128)S(1)}, u32[]{:S(2)}, u32[]{:S(2)}) collective-permute-start(f32[16,1024]{1,0:T(8,128)S(1)} %dynamic-slice_bitcast_fusion.6), channel_id=1, source_target_pairs={{0,8},{1,9},{2,10},{3,11},{4,12},{5,13},{6,14},{7,15},{8,0},{9,1},... | collective-permute-start | bytes 196616 | tf_op jit(solution)/shard_map/ppermute | solution.py:86
  55.3 1.4 %collective-permute-done.11 = f32[16,1024]{1,0:T(8,128)S(1)} collective-permute-done((f32[16,1024]{1,0:T(8,128)S(1)}, f32[16,1024]{1,0:T(8,128)S(1)}, u32[]{:S(2)}, u32[]{:S(2)}) %collective-permute-start.11) | collective-permute-done | bytes 65568 | tf_op jit(solution)/shard_map/ppermute | solution.py:86
  56.8 1.5 %collective-permute-done.18 = f32[16,1024]{1,0:T(8,128)S(1)} collective-permute-done((f32[16,1024]{1,0:T(8,128)S(1)}, f32[16,1024]{1,0:T(8,128)S(1)}, u32[]{:S(2)}, u32[]{:S(2)}) %collective-permute-start.18) | collective-permute-done | bytes 65568 | tf_op jit(solution)/shard_map/ppermute | solution.py:86
  58.4 2.4 %collective-permute-start.19 = (bf16[1,16,1024]{2,1,0:T(8,128)(2,1)S(1)}, bf16[1,16,1024]{2,1,0:T(8,128)(2,1)S(1)}, u32[]{:S(2)}, u32[]{:S(2)}) collective-permute-start(bf16[1,16,1024]{2,1,0:T(8,128)(2,1)S(1)} %get-tuple-element.21), channel_id=1, source_target_pairs={{0,8},{1,9},{2,10},{3,11},{4,12},{5,13},{6,14},{7,15},{8,0},{9,1},... | collective-permute-start | bytes 98312 | tf_op jit(solution)/shard_map/ppermute | solution.py:36
  60.8 0.6 collective-permute-start.12
  61.4 2.2 %collective-permute-done.19 = bf16[1,16,1024]{2,1,0:T(8,128)(2,1)S(1)} collective-permute-done((bf16[1,16,1024]{2,1,0:T(8,128)(2,1)S(1)}, bf16[1,16,1024]{2,1,0:T(8,128)(2,1)S(1)}, u32[]{:S(2)}, u32[]{:S(2)}) %collective-permute-start.19) | collective-permute-done | bytes 32800 | tf_op jit(solution)/shard_map/ppermute | solution.py:36
  63.7 1.3 %collective-permute-start.20 = (bf16[2,16,1024]{2,1,0:T(8,128)(2,1)S(1)}, bf16[2,16,1024]{2,1,0:T(8,128)(2,1)S(1)}, u32[]{:S(2)}, u32[]{:S(2)}) collective-permute-start(bf16[2,16,1024]{2,1,0:T(8,128)(2,1)S(1)} %pad_maximum_fusion.9), channel_id=1, source_target_pairs={{0,4},{1,3},{2,6},{3,1},{4,0},{5,7},{6,2},{7,5},{8,12},{9,11},{10,... | collective-permute-start | bytes 196616 | tf_op jit(solution)/shard_map/ppermute | solution.py:36
  64.9 0.7 collective-permute-done.12
  65.6 1.8 %collective-permute-start.13 = (bf16[2,16,1024]{2,1,0:T(8,128)(2,1)S(1)}, bf16[2,16,1024]{2,1,0:T(8,128)(2,1)S(1)}, u32[]{:S(2)}, u32[]{:S(2)}) collective-permute-start(bf16[2,16,1024]{2,1,0:T(8,128)(2,1)S(1)} %pad_maximum_fusion.8), channel_id=1, source_target_pairs={{0,4},{1,3},{2,6},{3,1},{4,0},{5,7},{6,2},{7,5},{8,12},{9,11},{10,... | collective-permute-start | bytes 196616 | tf_op jit(solution)/shard_map/ppermute | solution.py:36
  67.5 0.5 collective-permute-done.20
  68.0 2.6 %collective-permute-done.13 = bf16[2,16,1024]{2,1,0:T(8,128)(2,1)S(1)} collective-permute-done((bf16[2,16,1024]{2,1,0:T(8,128)(2,1)S(1)}, bf16[2,16,1024]{2,1,0:T(8,128)(2,1)S(1)}, u32[]{:S(2)}, u32[]{:S(2)}) %collective-permute-start.13) | collective-permute-done | bytes 65568 | tf_op jit(solution)/shard_map/ppermute | solution.py:36
  70.7 1.3 %collective-permute-start.21 = (bf16[4,16,1024]{2,1,0:T(8,128)(2,1)S(1)}, bf16[4,16,1024]{2,1,0:T(8,128)(2,1)S(1)}, u32[]{:S(2)}, u32[]{:S(2)}) collective-permute-start(bf16[4,16,1024]{2,1,0:T(8,128)(2,1)S(1)} %bitcast.340), channel_id=1, source_target_pairs={{0,2},{1,5},{2,0},{3,7},{4,6},{5,1},{6,4},{7,3},{8,10},{9,13},{10,... | collective-permute-start | bytes 393224 | tf_op jit(solution)/shard_map/ppermute | solution.py:36
  72.1 0.8 collective-permute-start.14
  72.9 2.8 %collective-permute-done.21 = bf16[4,16,1024]{2,1,0:T(8,128)(2,1)S(1)} collective-permute-done((bf16[4,16,1024]{2,1,0:T(8,128)(2,1)S(1)}, bf16[4,16,1024]{2,1,0:T(8,128)(2,1)S(1)}, u32[]{:S(2)}, u32[]{:S(2)}) %collective-permute-start.21) | collective-permute-done | bytes 131104 | tf_op jit(solution)/shard_map/ppermute | solution.py:36
  75.9 1.2 %collective-permute-done.14 = bf16[4,16,1024]{2,1,0:T(8,128)(2,1)S(1)} collective-permute-done((bf16[4,16,1024]{2,1,0:T(8,128)(2,1)S(1)}, bf16[4,16,1024]{2,1,0:T(8,128)(2,1)S(1)}, u32[]{:S(2)}, u32[]{:S(2)}) %collective-permute-start.14) | collective-permute-done | bytes 131104 | tf_op jit(solution)/shard_map/ppermute | solution.py:36
  77.4 1.4 %collective-permute-done.22.refs_2_ = bf16[128,1024]{1,0:T(8,128)(2,1)S(1)} collective-permute-done((bf16[128,1024]{1,0:T(8,128)(2,1)S(1)}, bf16[128,1024]{1,0:T(8,128)(2,1)S(1)}, u32[]{:S(2)}, u32[]{:S(2)}) %collective-permute-start.22) | collective-permute-done | bytes 262176 | tf_op jit(solution)/shard_map/ppermute | solution.py:53
  78.9 0.7 copy-done.7
  79.5 9.5 %shard_map.56 = (f32[128,1024]{1,0:T(8,128)}, f32[128,1024]{1,0:T(8,128)}, f32[128,1024]{1,0:T(8,128)}, f32[128,1024]{1,0:T(8,128)}) custom-call(bf16[4,256,256]{2,1,0:T(8,128)(2,1)} %bitcast.293, bf16[128,1024]{1,0:T(8,128)(2,1)} %bitcast.336, bf16[128,1024]{1,0:T(8,128)(2,1)} %bitcast.332, bf16[128,1024]{1,0:T(8,128)(2,1)} %copy-done.7, ...), custom_call_target="tpu_custom_call" | custom-call | tf_op jit(solution)/shard_map/pallas_call | solution.py:125
  89.2 0.4 collective-permute-start.28
  89.6 1.6 %collective-permute-done.24 = f32[128,1024]{1,0:T(8,128)S(1)} collective-permute-done((f32[128,1024]{1,0:T(8,128)}, f32[128,1024]{1,0:T(8,128)S(1)}, u32[]{:S(2)}, u32[]{:S(2)}) %collective-permute-start.24) | collective-permute-done | bytes 524320 | tf_op jit(solution)/shard_map/ppermute | solution.py:63
  91.2 1.1 fusion.5
  92.3 1.3 %collective-permute-start.25 = (f32[2,2,16,1024]{3,2,1,0:T(8,128)S(1)}, f32[2,2,16,1024]{3,2,1,0:T(8,128)S(1)}, u32[]{:S(2)}, u32[]{:S(2)}) collective-permute-start(f32[2,2,16,1024]{3,2,1,0:T(8,128)S(1)} %fusion.5), channel_id=1, source_target_pairs={{0,2},{1,5},{2,0},{3,7},{4,6},{5,1},{6,4},{7,3},{8,10},{9,13},{10,... | collective-permute-start | bytes 786440 | tf_op jit(solution)/shard_map/ppermute | solution.py:86
  93.6 1.1 fusion.2
  94.8 0.8 collective-permute-start.29
  95.6 3.2 %collective-permute-done.25 = f32[2,2,16,1024]{3,2,1,0:T(8,128)S(1)} collective-permute-done((f32[2,2,16,1024]{3,2,1,0:T(8,128)S(1)}, f32[2,2,16,1024]{3,2,1,0:T(8,128)S(1)}, u32[]{:S(2)}, u32[]{:S(2)}) %collective-permute-start.25) | collective-permute-done | bytes 262176 | tf_op jit(solution)/shard_map/ppermute | solution.py:86
  98.7 1.1 fusion.7
  99.9 1.8 %collective-permute-start.26 = (f32[2,16,1024]{2,1,0:T(8,128)S(1)}, f32[2,16,1024]{2,1,0:T(8,128)S(1)}, u32[]{:S(2)}, u32[]{:S(2)}) collective-permute-start(f32[2,16,1024]{2,1,0:T(8,128)S(1)} %dynamic-slice_bitcast_fusion.1), channel_id=1, source_target_pairs={{0,4},{1,3},{2,6},{3,1},{4,0},{5,7},{6,2},{7,5},{8,12},{9,11},{10,... | collective-permute-start | bytes 393224 | tf_op jit(solution)/shard_map/ppermute | solution.py:86
  101.7 1.1 fusion.4
  102.9 1.7 %collective-permute-start.30 = (f32[2,16,1024]{2,1,0:T(8,128)S(1)}, f32[2,16,1024]{2,1,0:T(8,128)S(1)}, u32[]{:S(2)}, u32[]{:S(2)}) collective-permute-start(f32[2,16,1024]{2,1,0:T(8,128)S(1)} %dynamic-slice_bitcast_fusion), channel_id=1, source_target_pairs={{0,4},{1,3},{2,6},{3,1},{4,0},{5,7},{6,2},{7,5},{8,12},{9,11},{10,... | collective-permute-start | bytes 393224 | tf_op jit(solution)/shard_map/ppermute | solution.py:86
  104.5 0.4 collective-permute-done.26
  105.0 2.4 %collective-permute-start.27 = (f32[16,1024]{1,0:T(8,128)S(1)}, f32[16,1024]{1,0:T(8,128)S(1)}, u32[]{:S(2)}, u32[]{:S(2)}) collective-permute-start(f32[16,1024]{1,0:T(8,128)S(1)} %dynamic-slice_bitcast_fusion.5), channel_id=1, source_target_pairs={{0,8},{1,9},{2,10},{3,11},{4,12},{5,13},{6,14},{7,15},{8,0},{9,1},... | collective-permute-start | bytes 196616 | tf_op jit(solution)/shard_map/ppermute | solution.py:86
  107.4 1.2 %collective-permute-done.30 = f32[2,16,1024]{2,1,0:T(8,128)S(1)} collective-permute-done((f32[2,16,1024]{2,1,0:T(8,128)S(1)}, f32[2,16,1024]{2,1,0:T(8,128)S(1)}, u32[]{:S(2)}, u32[]{:S(2)}) %collective-permute-start.30) | collective-permute-done | bytes 131104 | tf_op jit(solution)/shard_map/ppermute | solution.py:86
  108.7 2.0 %collective-permute-start.31 = (f32[16,1024]{1,0:T(8,128)S(1)}, f32[16,1024]{1,0:T(8,128)S(1)}, u32[]{:S(2)}, u32[]{:S(2)}) collective-permute-start(f32[16,1024]{1,0:T(8,128)S(1)} %dynamic-slice_bitcast_fusion.4), channel_id=1, source_target_pairs={{0,8},{1,9},{2,10},{3,11},{4,12},{5,13},{6,14},{7,15},{8,0},{9,1},... | collective-permute-start | bytes 196616 | tf_op jit(solution)/shard_map/ppermute | solution.py:86
  110.7 1.6 %collective-permute-done.27 = f32[16,1024]{1,0:T(8,128)S(1)} collective-permute-done((f32[16,1024]{1,0:T(8,128)S(1)}, f32[16,1024]{1,0:T(8,128)S(1)}, u32[]{:S(2)}, u32[]{:S(2)}) %collective-permute-start.27) | collective-permute-done | bytes 65568 | tf_op jit(solution)/shard_map/ppermute | solution.py:86
  112.3 1.6 %collective-permute-done.31 = f32[16,1024]{1,0:T(8,128)S(1)} collective-permute-done((f32[16,1024]{1,0:T(8,128)S(1)}, f32[16,1024]{1,0:T(8,128)S(1)}, u32[]{:S(2)}, u32[]{:S(2)}) %collective-permute-start.31) | collective-permute-done | bytes 65568 | tf_op jit(solution)/shard_map/ppermute | solution.py:86
  114.0 0.8 copy.92
  (80 shorter events, 3.8 us)
Async XLA Ops:
  2.7 6.4 %collective-permute-start.3 = (bf16[1,16,1024]{2,1,0:T(8,128)(2,1)S(1)}, bf16[1,16,1024]{2,1,0:T(8,128)(2,1)S(1)}, u32[]{:S(2)}, u32[]{:S(2)}) collective-permute-start(bf16[1,16,1024]{2,1,0:T(8,128)(2,1)S(1)} %get-tuple-element.55), channel_id=1, source_target_pairs={{0,8},{1,9},{2,10},{3,11},{4,12},{5,13},{6,14},{7,15},{8,0},{9,1},... | collective-permute-start | bytes 98312 | tf_op jit(solution)/shard_map/ppermute | solution.py:36
  6.8 4.8 %collective-permute-start = (bf16[1,16,1024]{2,1,0:T(8,128)(2,1)S(1)}, bf16[1,16,1024]{2,1,0:T(8,128)(2,1)S(1)}, u32[]{:S(2)}, u32[]{:S(2)}) collective-permute-start(bf16[1,16,1024]{2,1,0:T(8,128)(2,1)S(1)} %get-tuple-element.56), channel_id=1, source_target_pairs={{0,8},{1,9},{2,10},{3,11},{4,12},{5,13},{6,14},{7,15},{8,0},{9,1},... | collective-permute-start | bytes 98312 | tf_op jit(solution)/shard_map/ppermute | solution.py:36
  9.2 4.3 %collective-permute-start.4 = (bf16[2,16,1024]{2,1,0:T(8,128)(2,1)S(1)}, bf16[2,16,1024]{2,1,0:T(8,128)(2,1)S(1)}, u32[]{:S(2)}, u32[]{:S(2)}) collective-permute-start(bf16[2,16,1024]{2,1,0:T(8,128)(2,1)S(1)} %pad_maximum_fusion.7), channel_id=1, source_target_pairs={{0,4},{1,3},{2,6},{3,1},{4,0},{5,7},{6,2},{7,5},{8,12},{9,11},{10,... | collective-permute-start | bytes 196616 | tf_op jit(solution)/shard_map/ppermute | solution.py:36
  11.7 5.0 %collective-permute-start.1 = (bf16[2,16,1024]{2,1,0:T(8,128)(2,1)S(1)}, bf16[2,16,1024]{2,1,0:T(8,128)(2,1)S(1)}, u32[]{:S(2)}, u32[]{:S(2)}) collective-permute-start(bf16[2,16,1024]{2,1,0:T(8,128)(2,1)S(1)} %pad_maximum_fusion.6), channel_id=1, source_target_pairs={{0,4},{1,3},{2,6},{3,1},{4,0},{5,7},{6,2},{7,5},{8,12},{9,11},{10,... | collective-permute-start | bytes 196616 | tf_op jit(solution)/shard_map/ppermute | solution.py:36
  13.6 5.0 %collective-permute-start.5 = (bf16[4,16,1024]{2,1,0:T(8,128)(2,1)S(1)}, bf16[4,16,1024]{2,1,0:T(8,128)(2,1)S(1)}, u32[]{:S(2)}, u32[]{:S(2)}) collective-permute-start(bf16[4,16,1024]{2,1,0:T(8,128)(2,1)S(1)} %bitcast.337), channel_id=1, source_target_pairs={{0,2},{1,5},{2,0},{3,7},{4,6},{5,1},{6,4},{7,3},{8,10},{9,13},{10,... | collective-permute-start | bytes 393224 | tf_op jit(solution)/shard_map/ppermute | solution.py:36
  16.7 5.0 %collective-permute-start.2 = (bf16[4,16,1024]{2,1,0:T(8,128)(2,1)S(1)}, bf16[4,16,1024]{2,1,0:T(8,128)(2,1)S(1)}, u32[]{:S(2)}, u32[]{:S(2)}) collective-permute-start(bf16[4,16,1024]{2,1,0:T(8,128)(2,1)S(1)} %bitcast.338), channel_id=1, source_target_pairs={{0,2},{1,5},{2,0},{3,7},{4,6},{5,1},{6,4},{7,3},{8,10},{9,13},{10,... | collective-permute-start | bytes 393224 | tf_op jit(solution)/shard_map/ppermute | solution.py:36
  18.7 4.7 %copy-start = (bf16[2,2,2,16,1024]{4,3,2,1,0:T(8,128)(2,1)}, bf16[2,2,2,16,1024]{4,3,2,1,0:T(8,128)(2,1)S(1)}, u32[]{:S(2)}) copy-start(bf16[2,2,2,16,1024]{4,3,2,1,0:T(8,128)(2,1)S(1)} %maximum_select_fusion.1) | copy-start | bytes 786436
  18.7 4.4 %collective-permute-start.7 = (bf16[128,1024]{1,0:T(8,128)(2,1)S(1)}, bf16[128,1024]{1,0:T(8,128)(2,1)S(1)}, u32[]{:S(2)}, u32[]{:S(2)}) collective-permute-start(bf16[128,1024]{1,0:T(8,128)(2,1)S(1)} %bitcast.329), channel_id=1, source_target_pairs={{0,1},{1,0},{2,3},{3,2},{4,5},{5,4},{6,7},{7,6},{8,9},{9,8},{10,11... | collective-permute-start | bytes 786440 | tf_op jit(solution)/shard_map/ppermute | solution.py:53
  21.8 1.6 %copy-start.2 = (bf16[2,2,2,16,1024]{4,3,2,1,0:T(8,128)(2,1)}, bf16[2,2,2,16,1024]{4,3,2,1,0:T(8,128)(2,1)S(1)}, u32[]{:S(2)}) copy-start(bf16[2,2,2,16,1024]{4,3,2,1,0:T(8,128)(2,1)S(1)} %maximum_select_fusion) | copy-start | bytes 786436
  21.8 1.6 %collective-permute-start.6 = (bf16[128,1024]{1,0:T(8,128)(2,1)S(1)}, bf16[128,1024]{1,0:T(8,128)(2,1)S(1)}, u32[]{:S(2)}, u32[]{:S(2)}) collective-permute-start(bf16[128,1024]{1,0:T(8,128)(2,1)S(1)} %bitcast.333), channel_id=1, source_target_pairs={{0,1},{1,0},{2,3},{3,2},{4,5},{5,4},{6,7},{7,6},{8,9},{9,8},{10,11... | collective-permute-start | bytes 786440 | tf_op jit(solution)/shard_map/ppermute | solution.py:53
  23.1 0.7 copy-start.4
  23.4 0.7 copy-start.6
  24.1 34.2 %copy-start.8 = (f32[1024]{0:T(1024)S(1)}, f32[1024]{0:T(1024)}, u32[]{:S(2)}) copy-start(f32[1024]{0:T(1024)} %param.7) | copy-start | bytes 12292
  33.7 2.1 %collective-permute-start.8 = (f32[128,1024]{1,0:T(8,128)}, f32[128,1024]{1,0:T(8,128)S(1)}, u32[]{:S(2)}, u32[]{:S(2)}) collective-permute-start(f32[128,1024]{1,0:T(8,128)} %get-tuple-element.14), channel_id=1, source_target_pairs={{0,1},{1,0},{2,3},{3,2},{4,5},{5,4},{6,7},{7,6},{8,9},{9,8},{10,11... | collective-permute-start | bytes 1572872 | tf_op jit(solution)/shard_map/ppermute | solution.py:63
  33.9 4.5 %collective-permute-start.15 = (f32[128,1024]{1,0:T(8,128)}, f32[128,1024]{1,0:T(8,128)S(1)}, u32[]{:S(2)}, u32[]{:S(2)}) collective-permute-start(f32[128,1024]{1,0:T(8,128)} %get-tuple-element.16), channel_id=1, source_target_pairs={{0,1},{1,0},{2,3},{3,2},{4,5},{5,4},{6,7},{7,6},{8,9},{9,8},{10,11... | collective-permute-start | bytes 1572872 | tf_op jit(solution)/shard_map/ppermute | solution.py:63
  36.9 6.4 %collective-permute-start.9 = (f32[2,2,16,1024]{3,2,1,0:T(8,128)S(1)}, f32[2,2,16,1024]{3,2,1,0:T(8,128)S(1)}, u32[]{:S(2)}, u32[]{:S(2)}) collective-permute-start(f32[2,2,16,1024]{3,2,1,0:T(8,128)S(1)} %fusion.11), channel_id=1, source_target_pairs={{0,2},{1,5},{2,0},{3,7},{4,6},{5,1},{6,4},{7,3},{8,10},{9,13},{10,... | collective-permute-start | bytes 786440 | tf_op jit(solution)/shard_map/ppermute | solution.py:86
  39.5 6.6 %collective-permute-start.16 = (f32[2,2,16,1024]{3,2,1,0:T(8,128)S(1)}, f32[2,2,16,1024]{3,2,1,0:T(8,128)S(1)}, u32[]{:S(2)}, u32[]{:S(2)}) collective-permute-start(f32[2,2,16,1024]{3,2,1,0:T(8,128)S(1)} %fusion.8), channel_id=1, source_target_pairs={{0,2},{1,5},{2,0},{3,7},{4,6},{5,1},{6,4},{7,3},{8,10},{9,13},{10,... | collective-permute-start | bytes 786440 | tf_op jit(solution)/shard_map/ppermute | solution.py:86
  44.4 5.0 %collective-permute-start.10 = (f32[2,16,1024]{2,1,0:T(8,128)S(1)}, f32[2,16,1024]{2,1,0:T(8,128)S(1)}, u32[]{:S(2)}, u32[]{:S(2)}) collective-permute-start(f32[2,16,1024]{2,1,0:T(8,128)S(1)} %dynamic-slice_bitcast_fusion.3), channel_id=1, source_target_pairs={{0,4},{1,3},{2,6},{3,1},{4,0},{5,7},{6,2},{7,5},{8,12},{9,11},{10,... | collective-permute-start | bytes 393224 | tf_op jit(solution)/shard_map/ppermute | solution.py:86
  47.3 5.7 %collective-permute-start.17 = (f32[2,16,1024]{2,1,0:T(8,128)S(1)}, f32[2,16,1024]{2,1,0:T(8,128)S(1)}, u32[]{:S(2)}, u32[]{:S(2)}) collective-permute-start(f32[2,16,1024]{2,1,0:T(8,128)S(1)} %dynamic-slice_bitcast_fusion.2), channel_id=1, source_target_pairs={{0,4},{1,3},{2,6},{3,1},{4,0},{5,7},{6,2},{7,5},{8,12},{9,11},{10,... | collective-permute-start | bytes 393224 | tf_op jit(solution)/shard_map/ppermute | solution.py:86
  49.5 7.2 %collective-permute-start.11 = (f32[16,1024]{1,0:T(8,128)S(1)}, f32[16,1024]{1,0:T(8,128)S(1)}, u32[]{:S(2)}, u32[]{:S(2)}) collective-permute-start(f32[16,1024]{1,0:T(8,128)S(1)} %dynamic-slice_bitcast_fusion.7), channel_id=1, source_target_pairs={{0,8},{1,9},{2,10},{3,11},{4,12},{5,13},{6,14},{7,15},{8,0},{9,1},... | collective-permute-start | bytes 196616 | tf_op jit(solution)/shard_map/ppermute | solution.py:86
  53.1 5.2 %collective-permute-start.18 = (f32[16,1024]{1,0:T(8,128)S(1)}, f32[16,1024]{1,0:T(8,128)S(1)}, u32[]{:S(2)}, u32[]{:S(2)}) collective-permute-start(f32[16,1024]{1,0:T(8,128)S(1)} %dynamic-slice_bitcast_fusion.6), channel_id=1, source_target_pairs={{0,8},{1,9},{2,10},{3,11},{4,12},{5,13},{6,14},{7,15},{8,0},{9,1},... | collective-permute-start | bytes 196616 | tf_op jit(solution)/shard_map/ppermute | solution.py:86
  58.4 5.2 %collective-permute-start.19 = (bf16[1,16,1024]{2,1,0:T(8,128)(2,1)S(1)}, bf16[1,16,1024]{2,1,0:T(8,128)(2,1)S(1)}, u32[]{:S(2)}, u32[]{:S(2)}) collective-permute-start(bf16[1,16,1024]{2,1,0:T(8,128)(2,1)S(1)} %get-tuple-element.21), channel_id=1, source_target_pairs={{0,8},{1,9},{2,10},{3,11},{4,12},{5,13},{6,14},{7,15},{8,0},{9,1},... | collective-permute-start | bytes 98312 | tf_op jit(solution)/shard_map/ppermute | solution.py:36
  60.8 4.8 %collective-permute-start.12 = (bf16[1,16,1024]{2,1,0:T(8,128)(2,1)S(1)}, bf16[1,16,1024]{2,1,0:T(8,128)(2,1)S(1)}, u32[]{:S(2)}, u32[]{:S(2)}) collective-permute-start(bf16[1,16,1024]{2,1,0:T(8,128)(2,1)S(1)} %get-tuple-element.53), channel_id=1, source_target_pairs={{0,8},{1,9},{2,10},{3,11},{4,12},{5,13},{6,14},{7,15},{8,0},{9,1},... | collective-permute-start | bytes 98312 | tf_op jit(solution)/shard_map/ppermute | solution.py:36
  63.7 4.3 %collective-permute-start.20 = (bf16[2,16,1024]{2,1,0:T(8,128)(2,1)S(1)}, bf16[2,16,1024]{2,1,0:T(8,128)(2,1)S(1)}, u32[]{:S(2)}, u32[]{:S(2)}) collective-permute-start(bf16[2,16,1024]{2,1,0:T(8,128)(2,1)S(1)} %pad_maximum_fusion.9), channel_id=1, source_target_pairs={{0,4},{1,3},{2,6},{3,1},{4,0},{5,7},{6,2},{7,5},{8,12},{9,11},{10,... | collective-permute-start | bytes 196616 | tf_op jit(solution)/shard_map/ppermute | solution.py:36
  65.6 5.0 %collective-permute-start.13 = (bf16[2,16,1024]{2,1,0:T(8,128)(2,1)S(1)}, bf16[2,16,1024]{2,1,0:T(8,128)(2,1)S(1)}, u32[]{:S(2)}, u32[]{:S(2)}) collective-permute-start(bf16[2,16,1024]{2,1,0:T(8,128)(2,1)S(1)} %pad_maximum_fusion.8), channel_id=1, source_target_pairs={{0,4},{1,3},{2,6},{3,1},{4,0},{5,7},{6,2},{7,5},{8,12},{9,11},{10,... | collective-permute-start | bytes 196616 | tf_op jit(solution)/shard_map/ppermute | solution.py:36
  70.7 5.0 %collective-permute-start.21 = (bf16[4,16,1024]{2,1,0:T(8,128)(2,1)S(1)}, bf16[4,16,1024]{2,1,0:T(8,128)(2,1)S(1)}, u32[]{:S(2)}, u32[]{:S(2)}) collective-permute-start(bf16[4,16,1024]{2,1,0:T(8,128)(2,1)S(1)} %bitcast.340), channel_id=1, source_target_pairs={{0,2},{1,5},{2,0},{3,7},{4,6},{5,1},{6,4},{7,3},{8,10},{9,13},{10,... | collective-permute-start | bytes 393224 | tf_op jit(solution)/shard_map/ppermute | solution.py:36
  72.1 5.1 %collective-permute-start.14 = (bf16[4,16,1024]{2,1,0:T(8,128)(2,1)S(1)}, bf16[4,16,1024]{2,1,0:T(8,128)(2,1)S(1)}, u32[]{:S(2)}, u32[]{:S(2)}) collective-permute-start(bf16[4,16,1024]{2,1,0:T(8,128)(2,1)S(1)} %bitcast.339), channel_id=1, source_target_pairs={{0,2},{1,5},{2,0},{3,7},{4,6},{5,1},{6,4},{7,3},{8,10},{9,13},{10,... | collective-permute-start | bytes 393224 | tf_op jit(solution)/shard_map/ppermute | solution.py:36
  75.8 3.0 %copy-start.1 = (bf16[2,2,2,16,1024]{4,3,2,1,0:T(8,128)(2,1)}, bf16[2,2,2,16,1024]{4,3,2,1,0:T(8,128)(2,1)S(1)}, u32[]{:S(2)}) copy-start(bf16[2,2,2,16,1024]{4,3,2,1,0:T(8,128)(2,1)S(1)} %maximum_select_fusion.3) | copy-start | bytes 786436
  75.8 1.6 %collective-permute-start.23 = (bf16[128,1024]{1,0:T(8,128)(2,1)S(1)}, bf16[128,1024]{1,0:T(8,128)(2,1)S(1)}, u32[]{:S(2)}, u32[]{:S(2)}) collective-permute-start(bf16[128,1024]{1,0:T(8,128)(2,1)S(1)} %bitcast.331), channel_id=1, source_target_pairs={{0,1},{1,0},{2,3},{3,2},{4,5},{5,4},{6,7},{7,6},{8,9},{9,8},{10,11... | collective-permute-start | bytes 786440 | tf_op jit(solution)/shard_map/ppermute | solution.py:53
  77.2 1.6 %copy-start.3 = (bf16[2,2,2,16,1024]{4,3,2,1,0:T(8,128)(2,1)}, bf16[2,2,2,16,1024]{4,3,2,1,0:T(8,128)(2,1)S(1)}, u32[]{:S(2)}) copy-start(bf16[2,2,2,16,1024]{4,3,2,1,0:T(8,128)(2,1)S(1)} %maximum_select_fusion.2) | copy-start | bytes 786436
  77.2 1.6 %collective-permute-start.22 = (bf16[128,1024]{1,0:T(8,128)(2,1)S(1)}, bf16[128,1024]{1,0:T(8,128)(2,1)S(1)}, u32[]{:S(2)}, u32[]{:S(2)}) collective-permute-start(bf16[128,1024]{1,0:T(8,128)(2,1)S(1)} %bitcast.335), channel_id=1, source_target_pairs={{0,1},{1,0},{2,3},{3,2},{4,5},{5,4},{6,7},{7,6},{8,9},{9,8},{10,11... | collective-permute-start | bytes 786440 | tf_op jit(solution)/shard_map/ppermute | solution.py:53
  77.4 1.4 %copy-start.5 = (bf16[128,1024]{1,0:T(8,128)(2,1)}, bf16[128,1024]{1,0:T(8,128)(2,1)S(1)}, u32[]{:S(2)}) copy-start(bf16[128,1024]{1,0:T(8,128)(2,1)S(1)} %collective-permute-done.23.refs_3_) | copy-start | bytes 786436
  78.8 0.7 copy-start.7
  89.1 2.1 %collective-permute-start.24 = (f32[128,1024]{1,0:T(8,128)}, f32[128,1024]{1,0:T(8,128)S(1)}, u32[]{:S(2)}, u32[]{:S(2)}) collective-permute-start(f32[128,1024]{1,0:T(8,128)} %get-tuple-element.18), channel_id=1, source_target_pairs={{0,1},{1,0},{2,3},{3,2},{4,5},{5,4},{6,7},{7,6},{8,9},{9,8},{10,11... | collective-permute-start | bytes 1572872 | tf_op jit(solution)/shard_map/ppermute | solution.py:63
  89.2 4.4 %collective-permute-start.28 = (f32[128,1024]{1,0:T(8,128)}, f32[128,1024]{1,0:T(8,128)S(1)}, u32[]{:S(2)}, u32[]{:S(2)}) collective-permute-start(f32[128,1024]{1,0:T(8,128)} %get-tuple-element.20), channel_id=1, source_target_pairs={{0,1},{1,0},{2,3},{3,2},{4,5},{5,4},{6,7},{7,6},{8,9},{9,8},{10,11... | collective-permute-start | bytes 1572872 | tf_op jit(solution)/shard_map/ppermute | solution.py:63
  92.3 6.4 %collective-permute-start.25 = (f32[2,2,16,1024]{3,2,1,0:T(8,128)S(1)}, f32[2,2,16,1024]{3,2,1,0:T(8,128)S(1)}, u32[]{:S(2)}, u32[]{:S(2)}) collective-permute-start(f32[2,2,16,1024]{3,2,1,0:T(8,128)S(1)} %fusion.5), channel_id=1, source_target_pairs={{0,2},{1,5},{2,0},{3,7},{4,6},{5,1},{6,4},{7,3},{8,10},{9,13},{10,... | collective-permute-start | bytes 786440 | tf_op jit(solution)/shard_map/ppermute | solution.py:86
  94.8 7.0 %collective-permute-start.29 = (f32[2,2,16,1024]{3,2,1,0:T(8,128)S(1)}, f32[2,2,16,1024]{3,2,1,0:T(8,128)S(1)}, u32[]{:S(2)}, u32[]{:S(2)}) collective-permute-start(f32[2,2,16,1024]{3,2,1,0:T(8,128)S(1)} %fusion.2), channel_id=1, source_target_pairs={{0,2},{1,5},{2,0},{3,7},{4,6},{5,1},{6,4},{7,3},{8,10},{9,13},{10,... | collective-permute-start | bytes 786440 | tf_op jit(solution)/shard_map/ppermute | solution.py:86
  99.9 5.0 %collective-permute-start.26 = (f32[2,16,1024]{2,1,0:T(8,128)S(1)}, f32[2,16,1024]{2,1,0:T(8,128)S(1)}, u32[]{:S(2)}, u32[]{:S(2)}) collective-permute-start(f32[2,16,1024]{2,1,0:T(8,128)S(1)} %dynamic-slice_bitcast_fusion.1), channel_id=1, source_target_pairs={{0,4},{1,3},{2,6},{3,1},{4,0},{5,7},{6,2},{7,5},{8,12},{9,11},{10,... | collective-permute-start | bytes 393224 | tf_op jit(solution)/shard_map/ppermute | solution.py:86
  102.9 5.7 %collective-permute-start.30 = (f32[2,16,1024]{2,1,0:T(8,128)S(1)}, f32[2,16,1024]{2,1,0:T(8,128)S(1)}, u32[]{:S(2)}, u32[]{:S(2)}) collective-permute-start(f32[2,16,1024]{2,1,0:T(8,128)S(1)} %dynamic-slice_bitcast_fusion), channel_id=1, source_target_pairs={{0,4},{1,3},{2,6},{3,1},{4,0},{5,7},{6,2},{7,5},{8,12},{9,11},{10,... | collective-permute-start | bytes 393224 | tf_op jit(solution)/shard_map/ppermute | solution.py:86
  105.0 7.3 %collective-permute-start.27 = (f32[16,1024]{1,0:T(8,128)S(1)}, f32[16,1024]{1,0:T(8,128)S(1)}, u32[]{:S(2)}, u32[]{:S(2)}) collective-permute-start(f32[16,1024]{1,0:T(8,128)S(1)} %dynamic-slice_bitcast_fusion.5), channel_id=1, source_target_pairs={{0,8},{1,9},{2,10},{3,11},{4,12},{5,13},{6,14},{7,15},{8,0},{9,1},... | collective-permute-start | bytes 196616 | tf_op jit(solution)/shard_map/ppermute | solution.py:86
  108.7 5.2 %collective-permute-start.31 = (f32[16,1024]{1,0:T(8,128)S(1)}, f32[16,1024]{1,0:T(8,128)S(1)}, u32[]{:S(2)}, u32[]{:S(2)}) collective-permute-start(f32[16,1024]{1,0:T(8,128)S(1)} %dynamic-slice_bitcast_fusion.4), channel_id=1, source_target_pairs={{0,8},{1,9},{2,10},{3,11},{4,12},{5,13},{6,14},{7,15},{8,0},{9,1},... | collective-permute-start | bytes 196616 | tf_op jit(solution)/shard_map/ppermute | solution.py:86

commit v12 on v10

--- a/solution.py
+++ b/solution.py
@@ -8,6 +8,7 @@
 from jax.sharding import PartitionSpec as P
 
 ITERS = 2
+JOINT = 2
 
 
 def bit_orders(m, descending):
@@ -24,67 +25,86 @@
     return [(d, d ^ (1 << (b1 if d & 1 else b0))) for d in range(n)]
 
 
-def gather_rows(x, n):
+def gather_step(acc, item, have0, have1, b0, b1, n, me, odd):
+    bit = jnp.where(odd, (me >> b1) & 1, (me >> b0) & 1)
+    theirs = lax.ppermute(acc, "aux", partners(n, b0, b1))
+    lo = jnp.where(bit == 0, acc, theirs)
+    hi = jnp.where(bit == 0, theirs, acc)
+    at0 = sum(1 for b in have0 if b > b0)
+    at1 = sum(1 for b in have1 if b > b1)
+    lead = len(have0)
+    lo = lo.reshape((2,) * lead + item) if lead else lo[0]
+    hi = hi.reshape((2,) * lead + item) if lead else hi[0]
+    new0 = jnp.stack([lo, hi], axis=at0)
+    acc = new0 if at1 == at0 else jnp.where(odd, jnp.stack([lo, hi], axis=at1), new0)
+    return acc.reshape((-1,) + item), sorted(have0 + [b0], reverse=True), sorted(have1 + [b1], reverse=True)
+
+
+def gather_rows(xs, n, joint):
     m = n.bit_length() - 1
     me = lax.axis_index("aux")
     odd = (me & 1) == 1
     order0, order1 = bit_orders(m, True)
-    acc = x[None]
+    steps = list(zip(order0[:-1], order1[:-1]))
+    item = (len(xs),) + xs[0].shape
+    acc = jnp.stack(xs)[None]
     have0, have1 = [], []
-    for b0, b1 in zip(order0[:-1], order1[:-1]):
-        bit = jnp.where(odd, (me >> b1) & 1, (me >> b0) & 1)
-        theirs = lax.ppermute(acc, "aux", partners(n, b0, b1))
-        lo = jnp.where(bit == 0, acc, theirs)
-        hi = jnp.where(bit == 0, theirs, acc)
-        at0 = sum(1 for b in have0 if b > b0)
-        at1 = sum(1 for b in have1 if b > b1)
-        lead = len(have0)
-        lo = lo.reshape((2,) * lead + x.shape) if lead else lo[0]
-        hi = hi.reshape((2,) * lead + x.shape) if lead else hi[0]
-        new0 = jnp.stack([lo, hi], axis=at0)
-        if at1 == at0:
-            acc = new0
-        else:
-            acc = jnp.where(odd, jnp.stack([lo, hi], axis=at1), new0)
-        have0 = sorted(have0 + [b0], reverse=True)
-        have1 = sorted(have1 + [b1], reverse=True)
-        acc = acc.reshape((-1,) + x.shape)
-    flat = acc.reshape((n // 2 * x.shape[0],) + x.shape[1:])
-    return flat, lax.ppermute(flat, "aux", partners(n, 0, 0))
-
-
-def scatter_sum(keep, send, n):
+    for b0, b1 in steps[:joint]:
+        acc, have0, have1 = gather_step(acc, item, have0, have1, b0, b1, n, me, odd)
+    result = []
+    for state in range(len(xs)):
+        own = acc[:, state]
+        h0, h1 = have0, have1
+        for b0, b1 in steps[joint:]:
+            own, h0, h1 = gather_step(own, xs[0].shape, h0, h1, b0, b1, n, me, odd)
+        flat = own.reshape((n // 2 * xs[0].shape[0],) + xs[0].shape[1:])
+        result.append((flat, lax.ppermute(flat, "aux", partners(n, 0, 0))))
+    return result
+
+
+def reduce_step(acc, axes0, axes1, b0, b1, n, me, odd):
+    at0, at1 = axes0.index(b0), axes1.index(b1)
+    bit0, bit1 = (me >> b0) & 1, (me >> b1) & 1
+    if at0 == at1:
+        bit = jnp.where(odd, bit1, bit0)
+        kept = lax.dynamic_index_in_dim(acc, bit, axis=at0, keepdims=False)
+        sent = lax.dynamic_index_in_dim(acc, 1 - bit, axis=at0, keepdims=False)
+    else:
+        kept = jnp.where(
+            odd,
+            lax.dynamic_index_in_dim(acc, bit1, axis=at1, keepdims=False),
+            lax.dynamic_index_in_dim(acc, bit0, axis=at0, keepdims=False),
+        )
+        sent = jnp.where(
+            odd,
+            lax.dynamic_index_in_dim(acc, 1 - bit1, axis=at1, keepdims=False),
+            lax.dynamic_index_in_dim(acc, 1 - bit0, axis=at0, keepdims=False),
+        )
+    acc = kept + lax.ppermute(sent, "aux", partners(n, b0, b1))
+    return acc, axes0[:at0] + axes0[at0 + 1:], axes1[:at1] + axes1[at1 + 1:]
+
+
+def scatter_sum(keeps, sends, n, joint):
     m = n.bit_length() - 1
     me = lax.axis_index("aux")
     odd = (me & 1) == 1
-    rows = 2 * keep.shape[0] // n
+    rows = 2 * keeps[0].shape[0] // n
     order0, order1 = bit_orders(m, False)
-    shape = (2,) * (m - 1) + (rows,) + keep.shape[1:]
-    acc = keep.reshape(shape) + lax.ppermute(send, "aux", partners(n, 0, 0)).reshape(shape)
-    axes0 = list(range(m - 1, 0, -1))
-    axes1 = list(axes0)
-    for b0, b1 in zip(order0[1:], order1[1:]):
-        at0, at1 = axes0.index(b0), axes1.index(b1)
-        bit0, bit1 = (me >> b0) & 1, (me >> b1) & 1
-        if at0 == at1:
-            bit = jnp.where(odd, bit1, bit0)
-            kept = lax.dynamic_index_in_dim(acc, bit, axis=at0, keepdims=False)
-            sent = lax.dynamic_index_in_dim(acc, 1 - bit, axis=at0, keepdims=False)
-        else:
-            kept = jnp.where(
-                odd,
-                lax.dynamic_index_in_dim(acc, bit1, axis=at1, keepdims=False),
-                lax.dynamic_index_in_dim(acc, bit0, axis=at0, keepdims=False),
-            )
-            sent = jnp.where(
-                odd,
-                lax.dynamic_index_in_dim(acc, 1 - bit1, axis=at1, keepdims=False),
-                lax.dynamic_index_in_dim(acc, 1 - bit0, axis=at0, keepdims=False),
-            )
-        acc = kept + lax.ppermute(sent, "aux", partners(n, b0, b1))
-        axes0.pop(at0)
-        axes1.pop(at1)
-    return acc
+    steps = list(zip(order0[1:], order1[1:]))
+    split = len(steps) - joint
+    shape = (2,) * (m - 1) + (rows,) + keeps[0].shape[1:]
+    accs = []
+    for keep, send in zip(keeps, sends):
+        acc = keep.reshape(shape) + lax.ppermute(send, "aux", partners(n, 0, 0)).reshape(shape)
+        axes0 = list(range(m - 1, 0, -1))
+        axes1 = list(axes0)
+        for b0, b1 in steps[:split]:
+            acc, axes0, axes1 = reduce_step(acc, axes0, axes1, b0, b1, n, me, odd)
+        accs.append(acc)
+    acc = jnp.stack(accs, axis=len(axes0))
+    for b0, b1 in steps[split:]:
+        acc, axes0, axes1 = reduce_step(acc, axes0, axes1, b0, b1, n, me, odd)
+    return [acc[state] for state in range(len(keeps))]
 
 
 def exchange_kernel(states, occ_ref, *refs):
@@ -168,11 +188,11 @@
     own_denom = denom[:, 0, :]
     resps = [rhs[:, state, :] / own_denom for state in range(states)]
     for step in range(ITERS):
-        got = [gather_rows(resp.astype(jnp.bfloat16), n) for resp in resps]
+        got = gather_rows([resp.astype(jnp.bfloat16) for resp in resps], n, JOINT)
         keep, send = exchange_part(ordered_occ, [g[0] for g in got], [g[1] for g in got], vir_ints)
+        exchange = scatter_sum(keep, send, n, JOINT)
         for state in range(states):
-            exchange = scatter_sum(keep[state], send[state], n)
-            resps[state] = 0.4 * resps[state] + 0.6 * (rhs[:, state, :] - exchange) / own_denom
+            resps[state] = 0.4 * resps[state] + 0.6 * (rhs[:, state, :] - exchange[state]) / own_denom
     response = jnp.stack(resps, axis=1)
     return response
 

time: 116 us -> 120 us (1.034)
  waiting for transfers between devices: 46 us -> 67.7 us
  starting transfers between devices: 35.7 us -> 18 us
    ppermute x28 -> x20, waiting for transfers between devices: 42.8 us -> 64.5 us  [the longest x8 37.3 us: reduce_step(): acc = kept + lax.ppermute(sent, 'aux', partners(n, b0, b1))]
    ppermute x28 -> x20, starting transfers between devices: 34.7 us -> 17 us  [the longest x8 9.06 us: gather_step(): theirs = lax.ppermute(acc, 'aux', partners(n, b0, b1))]
  transfers between devices with their start and end apart: 32 -> 24, of which waited for: 25 -> 21; matrix products, arithmetic and copies ran while one was open for 8% -> 7% of each run, Pallas kernels for 0% -> 0%
where the time goes in v12:
time: 120 us
  waiting for transfers between devices  67.7 us (56%)
  Pallas kernels  19.1 us (16%)
  starting transfers between devices  18 us (15%)
  other arithmetic  8.61 us (7%)
  local copies, waits for them, and re-layouts  4.52 us (4%)
    ppermute x8, waiting for transfers between devices, reduce_step(): acc = kept + lax.ppermute(sent, 'aux', partners(n, b0, b1))  37.3 us
    ppermute x8, waiting for transfers between devices, gather_step(): theirs = lax.ppermute(acc, 'aux', partners(n, b0, b1))  25.9 us
    pallas_call x2, Pallas kernels, exchange_part(): pl.pallas_call(functools.partial(exchange_kernel, states), grid=(local_au...  19.1 us
    ppermute x8, starting transfers between devices, gather_step(): theirs = lax.ppermute(acc, 'aux', partners(n, b0, b1))  9.06 us
    ppermute x8, starting transfers between devices, reduce_step(): acc = kept + lax.ppermute(sent, 'aux', partners(n, b0, b1))  6.7 us
    add x4, other arithmetic, scatter_sum(): keep.reshape(shape)  4.41 us
    ppermute x4, waiting for transfers between devices, scatter_sum(): lax.ppermute(send, 'aux', partners(n, 0, 0)).reshape(shape)  3.23 us
  transfers between devices with their start and end apart: 24, of which 21 were waited for; matrix products, arithmetic and copies ran while one was open for 7% of the time, Pallas kernels for 0%

profile of v12, /device:TPU:0, one launch (start us, length us, event | category | flops | bytes accessed | tf_op | source)
XLA Modules:
  0.0 119.5 jit_solution(10189394503215809644)
XLA Ops:
  0.0 1.1 fusion.42
  1.1 0.8 dynamic_slice.78
  1.9 0.8 fusion.35
  2.6 4.1 %collective-permute-start = (bf16[1,2,16,1024]{3,2,1,0:T(8,128)(2,1)S(1)}, bf16[1,2,16,1024]{3,2,1,0:T(8,128)(2,1)S(1)}, u32[]{:S(2)}, u32[]{:S(2)}) collective-permute-start(bf16[1,2,16,1024]{3,2,1,0:T(8,128)(2,1)S(1)} %maximum_bitcast_fusion), channel_id=1, source_target_pairs={{0,8},{1,9},{2,10},{3,11},{4,12},{5,13},{6,14},{7,15},{8,0},{9,1},... | collective-permute-start | bytes 196616 | tf_op jit(solution)/shard_map/ppermute | solution.py:30
  6.7 3.6 %collective-permute-done = bf16[1,2,16,1024]{3,2,1,0:T(8,128)(2,1)S(1)} collective-permute-done((bf16[1,2,16,1024]{3,2,1,0:T(8,128)(2,1)S(1)}, bf16[1,2,16,1024]{3,2,1,0:T(8,128)(2,1)S(1)}, u32[]{:S(2)}, u32[]{:S(2)}) %collective-permute-start) | collective-permute-done | bytes 65568 | tf_op jit(solution)/shard_map/ppermute | solution.py:30
  10.4 0.6 collective-permute-start.1
  11.1 1.1 fusion.5
  12.1 3.3 %collective-permute-done.1 = bf16[2,2,16,1024]{3,2,1,0:T(8,128)(2,1)S(1)} collective-permute-done((bf16[2,2,16,1024]{3,2,1,0:T(8,128)(2,1)S(1)}, bf16[2,2,16,1024]{3,2,1,0:T(8,128)(2,1)S(1)}, u32[]{:S(2)}, u32[]{:S(2)}) %collective-permute-start.1) | collective-permute-done | bytes 131104 | tf_op jit(solution)/shard_map/ppermute | solution.py:30
  15.6 2.0 %collective-permute-start.3 = (bf16[4,16,1024]{2,1,0:T(8,128)(2,1)S(1)}, bf16[4,16,1024]{2,1,0:T(8,128)(2,1)S(1)}, u32[]{:S(2)}, u32[]{:S(2)}) collective-permute-start(bf16[4,16,1024]{2,1,0:T(8,128)(2,1)S(1)} %get-tuple-element.43), channel_id=1, source_target_pairs={{0,2},{1,5},{2,0},{3,7},{4,6},{5,1},{6,4},{7,3},{8,10},{9,13},{10,... | collective-permute-start | bytes 393224 | tf_op jit(solution)/shard_map/ppermute | solution.py:30
  17.6 0.1 collective-permute-start.2
  17.7 1.1 fusion
  18.8 1.8 %collective-permute-done.3 = bf16[4,16,1024]{2,1,0:T(8,128)(2,1)S(1)} collective-permute-done((bf16[4,16,1024]{2,1,0:T(8,128)(2,1)S(1)}, bf16[4,16,1024]{2,1,0:T(8,128)(2,1)S(1)}, u32[]{:S(2)}, u32[]{:S(2)}) %collective-permute-start.3) | collective-permute-done | bytes 131104 | tf_op jit(solution)/shard_map/ppermute | solution.py:30
  20.6 1.9 %collective-permute-done.2 = bf16[4,16,1024]{2,1,0:T(8,128)(2,1)S(1)} collective-permute-done((bf16[4,16,1024]{2,1,0:T(8,128)(2,1)S(1)}, bf16[4,16,1024]{2,1,0:T(8,128)(2,1)S(1)}, u32[]{:S(2)}, u32[]{:S(2)}) %collective-permute-start.2) | collective-permute-done | bytes 131104 | tf_op jit(solution)/shard_map/ppermute | solution.py:30
  22.6 0.1 collective-permute-start.4
  22.8 0.6 collective-permute-start.5
  23.4 1.1 convolution_convert_fusion
  24.5 0.1 collective-permute-done.5.refs_3_
  24.6 0.6 copy-done.4
  25.2 0.1 copy-done.5
  25.3 9.6 %shard_map.55 = (f32[128,1024]{1,0:T(8,128)}, f32[128,1024]{1,0:T(8,128)}, f32[128,1024]{1,0:T(8,128)}, f32[128,1024]{1,0:T(8,128)}) custom-call(bf16[4,256,256]{2,1,0:T(8,128)(2,1)} %bitcast.254, bf16[128,1024]{1,0:T(8,128)(2,1)} %bitcast.288, bf16[128,1024]{1,0:T(8,128)(2,1)} %bitcast.290, bf16[128,1024]{1,0:T(8,128)(2,1)} %copy-done.4, ...), custom_call_target="tpu_custom_call" | custom-call | tf_op jit(solution)/shard_map/pallas_call | solution.py:142
  34.9 0.2 collective-permute-start.6
  35.1 0.3 collective-permute-start.8
  35.4 1.6 %collective-permute-done.6 = f32[128,1024]{1,0:T(8,128)S(1)} collective-permute-done((f32[128,1024]{1,0:T(8,128)}, f32[128,1024]{1,0:T(8,128)S(1)}, u32[]{:S(2)}, u32[]{:S(2)}) %collective-permute-start.6) | collective-permute-done | bytes 524320 | tf_op jit(solution)/shard_map/ppermute | solution.py:98
  37.0 1.1 add.167
  38.1 1.5 %collective-permute-start.7 = (f32[2,2,16,1024]{3,2,1,0:T(8,128)S(1)}, f32[2,2,16,1024]{3,2,1,0:T(8,128)S(1)}, u32[]{:S(2)}, u32[]{:S(2)}) collective-permute-start(f32[2,2,16,1024]{3,2,1,0:T(8,128)S(1)} %bitcast_select_fusion.8), channel_id=1, source_target_pairs={{0,2},{1,5},{2,0},{3,7},{4,6},{5,1},{6,4},{7,3},{8,10},{9,13},{10,... | collective-permute-start | bytes 786440 | tf_op jit(solution)/shard_map/ppermute | solution.py:83
  39.6 1.1 add.174
  40.8 0.7 collective-permute-start.9
  41.5 3.1 %collective-permute-done.7 = f32[2,2,16,1024]{3,2,1,0:T(8,128)S(1)} collective-permute-done((f32[2,2,16,1024]{3,2,1,0:T(8,128)S(1)}, f32[2,2,16,1024]{3,2,1,0:T(8,128)S(1)}, u32[]{:S(2)}, u32[]{:S(2)}) %collective-permute-start.7) | collective-permute-done | bytes 262176 | tf_op jit(solution)/shard_map/ppermute | solution.py:83
  44.6 2.8 %collective-permute-done.9 = f32[2,2,16,1024]{3,2,1,0:T(8,128)S(1)} collective-permute-done((f32[2,2,16,1024]{3,2,1,0:T(8,128)S(1)}, f32[2,2,16,1024]{3,2,1,0:T(8,128)S(1)}, u32[]{:S(2)}, u32[]{:S(2)}) %collective-permute-start.9) | collective-permute-done | bytes 262176 | tf_op jit(solution)/shard_map/ppermute | solution.py:83
  47.5 0.2 collective-permute-start.10
  47.7 6.2 %collective-permute-done.10 = f32[2,2,16,1024]{3,2,1,0:T(8,128)S(1)} collective-permute-done((f32[2,2,16,1024]{3,2,1,0:T(8,128)S(1)}, f32[2,2,16,1024]{3,2,1,0:T(8,128)S(1)}, u32[]{:S(2)}, u32[]{:S(2)}) %collective-permute-start.10) | collective-permute-done | bytes 262176 | tf_op jit(solution)/shard_map/ppermute | solution.py:83
  54.0 1.5 %collective-permute-start.11 = (f32[2,16,1024]{2,1,0:T(8,128)S(1)}, f32[2,16,1024]{2,1,0:T(8,128)S(1)}, u32[]{:S(2)}, u32[]{:S(2)}) collective-permute-start(f32[2,16,1024]{2,1,0:T(8,128)S(1)} %dynamic-slice_bitcast_fusion.1), channel_id=1, source_target_pairs={{0,8},{1,9},{2,10},{3,11},{4,12},{5,13},{6,14},{7,15},{8,0},{9,1},... | collective-permute-start | bytes 393224 | tf_op jit(solution)/shard_map/ppermute | solution.py:83
  55.6 6.2 %collective-permute-done.11 = f32[2,16,1024]{2,1,0:T(8,128)S(1)} collective-permute-done((f32[2,16,1024]{2,1,0:T(8,128)S(1)}, f32[2,16,1024]{2,1,0:T(8,128)S(1)}, u32[]{:S(2)}, u32[]{:S(2)}) %collective-permute-start.11) | collective-permute-done | bytes 131104 | tf_op jit(solution)/shard_map/ppermute | solution.py:83
  61.8 0.1 fusion.16
  61.9 0.1 collective-permute-start.12
  62.0 5.6 %collective-permute-done.12 = bf16[1,2,16,1024]{3,2,1,0:T(8,128)(2,1)S(1)} collective-permute-done((bf16[1,2,16,1024]{3,2,1,0:T(8,128)(2,1)S(1)}, bf16[1,2,16,1024]{3,2,1,0:T(8,128)(2,1)S(1)}, u32[]{:S(2)}, u32[]{:S(2)}) %collective-permute-start.12) | collective-permute-done | bytes 65568 | tf_op jit(solution)/shard_map/ppermute | solution.py:30
  67.6 0.1 collective-permute-start.13
  67.7 5.2 %collective-permute-done.13 = bf16[2,2,16,1024]{3,2,1,0:T(8,128)(2,1)S(1)} collective-permute-done((bf16[2,2,16,1024]{3,2,1,0:T(8,128)(2,1)S(1)}, bf16[2,2,16,1024]{3,2,1,0:T(8,128)(2,1)S(1)}, u32[]{:S(2)}, u32[]{:S(2)}) %collective-permute-start.13) | collective-permute-done | bytes 131104 | tf_op jit(solution)/shard_map/ppermute | solution.py:30
  73.0 1.5 %collective-permute-start.15 = (bf16[4,16,1024]{2,1,0:T(8,128)(2,1)S(1)}, bf16[4,16,1024]{2,1,0:T(8,128)(2,1)S(1)}, u32[]{:S(2)}, u32[]{:S(2)}) collective-permute-start(bf16[4,16,1024]{2,1,0:T(8,128)(2,1)S(1)} %get-tuple-element.37), channel_id=1, source_target_pairs={{0,2},{1,5},{2,0},{3,7},{4,6},{5,1},{6,4},{7,3},{8,10},{9,13},{10,... | collective-permute-start | bytes 393224 | tf_op jit(solution)/shard_map/ppermute | solution.py:30
  74.5 0.6 collective-permute-start.14
  75.1 2.9 %collective-permute-done.15 = bf16[4,16,1024]{2,1,0:T(8,128)(2,1)S(1)} collective-permute-done((bf16[4,16,1024]{2,1,0:T(8,128)(2,1)S(1)}, bf16[4,16,1024]{2,1,0:T(8,128)(2,1)S(1)}, u32[]{:S(2)}, u32[]{:S(2)}) %collective-permute-start.15) | collective-permute-done | bytes 131104 | tf_op jit(solution)/shard_map/ppermute | solution.py:30
  78.0 1.4 %collective-permute-done.14 = bf16[4,16,1024]{2,1,0:T(8,128)(2,1)S(1)} collective-permute-done((bf16[4,16,1024]{2,1,0:T(8,128)(2,1)S(1)}, bf16[4,16,1024]{2,1,0:T(8,128)(2,1)S(1)}, u32[]{:S(2)}, u32[]{:S(2)}) %collective-permute-start.14) | collective-permute-done | bytes 131104 | tf_op jit(solution)/shard_map/ppermute | solution.py:30
  79.5 0.1 collective-permute-start.16
  79.7 0.6 collective-permute-start.17
  80.2 0.9 collective-permute-done.16.refs_2_
  81.1 0.4 collective-permute-done.17.refs_3_
  81.5 0.3 copy-done.6
  81.9 0.7 copy-done.7
  82.5 9.5 %shard_map.56 = (f32[128,1024]{1,0:T(8,128)}, f32[128,1024]{1,0:T(8,128)}, f32[128,1024]{1,0:T(8,128)}, f32[128,1024]{1,0:T(8,128)}) custom-call(bf16[4,256,256]{2,1,0:T(8,128)(2,1)} %bitcast.255, bf16[128,1024]{1,0:T(8,128)(2,1)} %bitcast.292, bf16[128,1024]{1,0:T(8,128)(2,1)} %bitcast.294, bf16[128,1024]{1,0:T(8,128)(2,1)} %copy-done.6, ...), custom_call_target="tpu_custom_call" | custom-call | tf_op jit(solution)/shard_map/pallas_call | solution.py:142
  92.1 0.1 collective-permute-start.18
  92.2 0.4 collective-permute-start.20
  92.6 1.6 %collective-permute-done.18 = f32[128,1024]{1,0:T(8,128)S(1)} collective-permute-done((f32[128,1024]{1,0:T(8,128)}, f32[128,1024]{1,0:T(8,128)S(1)}, u32[]{:S(2)}, u32[]{:S(2)}) %collective-permute-start.18) | collective-permute-done | bytes 524320 | tf_op jit(solution)/shard_map/ppermute | solution.py:98
  94.2 1.1 add.186
  95.4 1.5 %collective-permute-start.19 = (f32[2,2,16,1024]{3,2,1,0:T(8,128)S(1)}, f32[2,2,16,1024]{3,2,1,0:T(8,128)S(1)}, u32[]{:S(2)}, u32[]{:S(2)}) collective-permute-start(f32[2,2,16,1024]{3,2,1,0:T(8,128)S(1)} %bitcast_select_fusion.4), channel_id=1, source_target_pairs={{0,2},{1,5},{2,0},{3,7},{4,6},{5,1},{6,4},{7,3},{8,10},{9,13},{10,... | collective-permute-start | bytes 786440 | tf_op jit(solution)/shard_map/ppermute | solution.py:83
  96.8 1.1 add.189
  98.0 0.7 collective-permute-start.21
  98.7 3.1 %collective-permute-done.19 = f32[2,2,16,1024]{3,2,1,0:T(8,128)S(1)} collective-permute-done((f32[2,2,16,1024]{3,2,1,0:T(8,128)S(1)}, f32[2,2,16,1024]{3,2,1,0:T(8,128)S(1)}, u32[]{:S(2)}, u32[]{:S(2)}) %collective-permute-start.19) | collective-permute-done | bytes 262176 | tf_op jit(solution)/shard_map/ppermute | solution.py:83
  101.9 2.8 %collective-permute-done.21 = f32[2,2,16,1024]{3,2,1,0:T(8,128)S(1)} collective-permute-done((f32[2,2,16,1024]{3,2,1,0:T(8,128)S(1)}, f32[2,2,16,1024]{3,2,1,0:T(8,128)S(1)}, u32[]{:S(2)}, u32[]{:S(2)}) %collective-permute-start.21) | collective-permute-done | bytes 262176 | tf_op jit(solution)/shard_map/ppermute | solution.py:83
  104.8 0.1 collective-permute-start.22
  104.8 6.4 %collective-permute-done.22 = f32[2,2,16,1024]{3,2,1,0:T(8,128)S(1)} collective-permute-done((f32[2,2,16,1024]{3,2,1,0:T(8,128)S(1)}, f32[2,2,16,1024]{3,2,1,0:T(8,128)S(1)}, u32[]{:S(2)}, u32[]{:S(2)}) %collective-permute-start.22) | collective-permute-done | bytes 262176 | tf_op jit(solution)/shard_map/ppermute | solution.py:83
  111.3 0.6 collective-permute-start.23
  111.8 6.7 %collective-permute-done.23 = f32[2,16,1024]{2,1,0:T(8,128)S(1)} collective-permute-done((f32[2,16,1024]{2,1,0:T(8,128)S(1)}, f32[2,16,1024]{2,1,0:T(8,128)S(1)}, u32[]{:S(2)}, u32[]{:S(2)}) %collective-permute-start.23) | collective-permute-done | bytes 131104 | tf_op jit(solution)/shard_map/ppermute | solution.py:83
  118.6 0.1 fusion.22
  118.7 0.8 copy.75
  (58 shorter events, 1.3 us)
Async XLA Ops:
  2.6 7.8 %collective-permute-start = (bf16[1,2,16,1024]{3,2,1,0:T(8,128)(2,1)S(1)}, bf16[1,2,16,1024]{3,2,1,0:T(8,128)(2,1)S(1)}, u32[]{:S(2)}, u32[]{:S(2)}) collective-permute-start(bf16[1,2,16,1024]{3,2,1,0:T(8,128)(2,1)S(1)} %maximum_bitcast_fusion), channel_id=1, source_target_pairs={{0,8},{1,9},{2,10},{3,11},{4,12},{5,13},{6,14},{7,15},{8,0},{9,1},... | collective-permute-start | bytes 196616 | tf_op jit(solution)/shard_map/ppermute | solution.py:30
  10.4 5.0 %collective-permute-start.1 = (bf16[2,2,16,1024]{3,2,1,0:T(8,128)(2,1)S(1)}, bf16[2,2,16,1024]{3,2,1,0:T(8,128)(2,1)S(1)}, u32[]{:S(2)}, u32[]{:S(2)}) collective-permute-start(bf16[2,2,16,1024]{3,2,1,0:T(8,128)(2,1)S(1)} %pad_maximum_fusion.3), channel_id=1, source_target_pairs={{0,4},{1,3},{2,6},{3,1},{4,0},{5,7},{6,2},{7,5},{8,12},{9,11},{10,... | collective-permute-start | bytes 393224 | tf_op jit(solution)/shard_map/ppermute | solution.py:30
  15.6 5.0 %collective-permute-start.3 = (bf16[4,16,1024]{2,1,0:T(8,128)(2,1)S(1)}, bf16[4,16,1024]{2,1,0:T(8,128)(2,1)S(1)}, u32[]{:S(2)}, u32[]{:S(2)}) collective-permute-start(bf16[4,16,1024]{2,1,0:T(8,128)(2,1)S(1)} %get-tuple-element.43), channel_id=1, source_target_pairs={{0,2},{1,5},{2,0},{3,7},{4,6},{5,1},{6,4},{7,3},{8,10},{9,13},{10,... | collective-permute-start | bytes 393224 | tf_op jit(solution)/shard_map/ppermute | solution.py:30
  17.6 5.0 %collective-permute-start.2 = (bf16[4,16,1024]{2,1,0:T(8,128)(2,1)S(1)}, bf16[4,16,1024]{2,1,0:T(8,128)(2,1)S(1)}, u32[]{:S(2)}, u32[]{:S(2)}) collective-permute-start(bf16[4,16,1024]{2,1,0:T(8,128)(2,1)S(1)} %get-tuple-element.44), channel_id=1, source_target_pairs={{0,2},{1,5},{2,0},{3,7},{4,6},{5,1},{6,4},{7,3},{8,10},{9,13},{10,... | collective-permute-start | bytes 393224 | tf_op jit(solution)/shard_map/ppermute | solution.py:30
  22.6 2.0 %copy-start = (bf16[2,2,2,16,1024]{4,3,2,1,0:T(8,128)(2,1)}, bf16[2,2,2,16,1024]{4,3,2,1,0:T(8,128)(2,1)S(1)}, u32[]{:S(2)}) copy-start(bf16[2,2,2,16,1024]{4,3,2,1,0:T(8,128)(2,1)S(1)} %maximum_select_fusion) | copy-start | bytes 786436
  22.6 1.9 %collective-permute-start.4 = (bf16[128,1024]{1,0:T(8,128)(2,1)S(1)}, bf16[128,1024]{1,0:T(8,128)(2,1)S(1)}, u32[]{:S(2)}, u32[]{:S(2)}) collective-permute-start(bf16[128,1024]{1,0:T(8,128)(2,1)S(1)} %bitcast.287), channel_id=1, source_target_pairs={{0,1},{1,0},{2,3},{3,2},{4,5},{5,4},{6,7},{7,6},{8,9},{9,8},{10,11... | collective-permute-start | bytes 786440 | tf_op jit(solution)/shard_map/ppermute | solution.py:61
  22.8 1.9 %copy-start.1 = (bf16[2,2,2,16,1024]{4,3,2,1,0:T(8,128)(2,1)}, bf16[2,2,2,16,1024]{4,3,2,1,0:T(8,128)(2,1)S(1)}, u32[]{:S(2)}) copy-start(bf16[2,2,2,16,1024]{4,3,2,1,0:T(8,128)(2,1)S(1)} %maximum_select_fusion.1) | copy-start | bytes 786436
  22.8 1.8 %collective-permute-start.5 = (bf16[128,1024]{1,0:T(8,128)(2,1)S(1)}, bf16[128,1024]{1,0:T(8,128)(2,1)S(1)}, u32[]{:S(2)}, u32[]{:S(2)}) collective-permute-start(bf16[128,1024]{1,0:T(8,128)(2,1)S(1)} %bitcast.289), channel_id=1, source_target_pairs={{0,1},{1,0},{2,3},{3,2},{4,5},{5,4},{6,7},{7,6},{8,9},{9,8},{10,11... | collective-permute-start | bytes 786440 | tf_op jit(solution)/shard_map/ppermute | solution.py:61
  24.5 0.7 copy-start.4
  24.6 0.7 copy-start.5
  25.3 36.4 %copy-start.8 = (f32[1024]{0:T(1024)S(1)}, f32[1024]{0:T(1024)}, u32[]{:S(2)}) copy-start(f32[1024]{0:T(1024)} %param.7) | copy-start | bytes 12292
  34.9 2.1 %collective-permute-start.6 = (f32[128,1024]{1,0:T(8,128)}, f32[128,1024]{1,0:T(8,128)S(1)}, u32[]{:S(2)}, u32[]{:S(2)}) collective-permute-start(f32[128,1024]{1,0:T(8,128)} %get-tuple-element.14), channel_id=1, source_target_pairs={{0,1},{1,0},{2,3},{3,2},{4,5},{5,4},{6,7},{7,6},{8,9},{9,8},{10,11... | collective-permute-start | bytes 1572872 | tf_op jit(solution)/shard_map/ppermute | solution.py:98
  35.1 4.5 %collective-permute-start.8 = (f32[128,1024]{1,0:T(8,128)}, f32[128,1024]{1,0:T(8,128)S(1)}, u32[]{:S(2)}, u32[]{:S(2)}) collective-permute-start(f32[128,1024]{1,0:T(8,128)} %get-tuple-element.16), channel_id=1, source_target_pairs={{0,1},{1,0},{2,3},{3,2},{4,5},{5,4},{6,7},{7,6},{8,9},{9,8},{10,11... | collective-permute-start | bytes 1572872 | tf_op jit(solution)/shard_map/ppermute | solution.py:98
  38.1 6.4 %collective-permute-start.7 = (f32[2,2,16,1024]{3,2,1,0:T(8,128)S(1)}, f32[2,2,16,1024]{3,2,1,0:T(8,128)S(1)}, u32[]{:S(2)}, u32[]{:S(2)}) collective-permute-start(f32[2,2,16,1024]{3,2,1,0:T(8,128)S(1)} %bitcast_select_fusion.8), channel_id=1, source_target_pairs={{0,2},{1,5},{2,0},{3,7},{4,6},{5,1},{6,4},{7,3},{8,10},{9,13},{10,... | collective-permute-start | bytes 786440 | tf_op jit(solution)/shard_map/ppermute | solution.py:83
  40.8 6.6 %collective-permute-start.9 = (f32[2,2,16,1024]{3,2,1,0:T(8,128)S(1)}, f32[2,2,16,1024]{3,2,1,0:T(8,128)S(1)}, u32[]{:S(2)}, u32[]{:S(2)}) collective-permute-start(f32[2,2,16,1024]{3,2,1,0:T(8,128)S(1)} %bitcast_select_fusion.6), channel_id=1, source_target_pairs={{0,2},{1,5},{2,0},{3,7},{4,6},{5,1},{6,4},{7,3},{8,10},{9,13},{10,... | collective-permute-start | bytes 786440 | tf_op jit(solution)/shard_map/ppermute | solution.py:83
  47.5 6.4 %collective-permute-start.10 = (f32[2,2,16,1024]{3,2,1,0:T(8,128)S(1)}, f32[2,2,16,1024]{3,2,1,0:T(8,128)S(1)}, u32[]{:S(2)}, u32[]{:S(2)}) collective-permute-start(f32[2,2,16,1024]{3,2,1,0:T(8,128)S(1)} %bitcast.295), channel_id=1, source_target_pairs={{0,4},{1,3},{2,6},{3,1},{4,0},{5,7},{6,2},{7,5},{8,12},{9,11},{10,... | collective-permute-start | bytes 786440 | tf_op jit(solution)/shard_map/ppermute | solution.py:83
  54.0 7.7 %collective-permute-start.11 = (f32[2,16,1024]{2,1,0:T(8,128)S(1)}, f32[2,16,1024]{2,1,0:T(8,128)S(1)}, u32[]{:S(2)}, u32[]{:S(2)}) collective-permute-start(f32[2,16,1024]{2,1,0:T(8,128)S(1)} %dynamic-slice_bitcast_fusion.1), channel_id=1, source_target_pairs={{0,8},{1,9},{2,10},{3,11},{4,12},{5,13},{6,14},{7,15},{8,0},{9,1},... | collective-permute-start | bytes 393224 | tf_op jit(solution)/shard_map/ppermute | solution.py:83
  61.9 5.7 %collective-permute-start.12 = (bf16[1,2,16,1024]{3,2,1,0:T(8,128)(2,1)S(1)}, bf16[1,2,16,1024]{3,2,1,0:T(8,128)(2,1)S(1)}, u32[]{:S(2)}, u32[]{:S(2)}) collective-permute-start(bf16[1,2,16,1024]{3,2,1,0:T(8,128)(2,1)S(1)} %maximum_bitcast_fusion.1), channel_id=1, source_target_pairs={{0,8},{1,9},{2,10},{3,11},{4,12},{5,13},{6,14},{7,15},{8,0},{9,1},... | collective-permute-start | bytes 196616 | tf_op jit(solution)/shard_map/ppermute | solution.py:30
  67.6 5.3 %collective-permute-start.13 = (bf16[2,2,16,1024]{3,2,1,0:T(8,128)(2,1)S(1)}, bf16[2,2,16,1024]{3,2,1,0:T(8,128)(2,1)S(1)}, u32[]{:S(2)}, u32[]{:S(2)}) collective-permute-start(bf16[2,2,16,1024]{3,2,1,0:T(8,128)(2,1)S(1)} %pad_maximum_fusion.4), channel_id=1, source_target_pairs={{0,4},{1,3},{2,6},{3,1},{4,0},{5,7},{6,2},{7,5},{8,12},{9,11},{10,... | collective-permute-start | bytes 393224 | tf_op jit(solution)/shard_map/ppermute | solution.py:30
  73.0 5.0 %collective-permute-start.15 = (bf16[4,16,1024]{2,1,0:T(8,128)(2,1)S(1)}, bf16[4,16,1024]{2,1,0:T(8,128)(2,1)S(1)}, u32[]{:S(2)}, u32[]{:S(2)}) collective-permute-start(bf16[4,16,1024]{2,1,0:T(8,128)(2,1)S(1)} %get-tuple-element.37), channel_id=1, source_target_pairs={{0,2},{1,5},{2,0},{3,7},{4,6},{5,1},{6,4},{7,3},{8,10},{9,13},{10,... | collective-permute-start | bytes 393224 | tf_op jit(solution)/shard_map/ppermute | solution.py:30
  74.5 5.0 %collective-permute-start.14 = (bf16[4,16,1024]{2,1,0:T(8,128)(2,1)S(1)}, bf16[4,16,1024]{2,1,0:T(8,128)(2,1)S(1)}, u32[]{:S(2)}, u32[]{:S(2)}) collective-permute-start(bf16[4,16,1024]{2,1,0:T(8,128)(2,1)S(1)} %get-tuple-element.38), channel_id=1, source_target_pairs={{0,2},{1,5},{2,0},{3,7},{4,6},{5,1},{6,4},{7,3},{8,10},{9,13},{10,... | collective-permute-start | bytes 393224 | tf_op jit(solution)/shard_map/ppermute | solution.py:30
  79.5 2.0 %copy-start.2 = (bf16[2,2,2,16,1024]{4,3,2,1,0:T(8,128)(2,1)}, bf16[2,2,2,16,1024]{4,3,2,1,0:T(8,128)(2,1)S(1)}, u32[]{:S(2)}) copy-start(bf16[2,2,2,16,1024]{4,3,2,1,0:T(8,128)(2,1)S(1)} %maximum_select_fusion.2) | copy-start | bytes 786436
  79.5 1.6 %collective-permute-start.16 = (bf16[128,1024]{1,0:T(8,128)(2,1)S(1)}, bf16[128,1024]{1,0:T(8,128)(2,1)S(1)}, u32[]{:S(2)}, u32[]{:S(2)}) collective-permute-start(bf16[128,1024]{1,0:T(8,128)(2,1)S(1)} %bitcast.291), channel_id=1, source_target_pairs={{0,1},{1,0},{2,3},{3,2},{4,5},{5,4},{6,7},{7,6},{8,9},{9,8},{10,11... | collective-permute-start | bytes 786440 | tf_op jit(solution)/shard_map/ppermute | solution.py:61
  79.7 1.8 %copy-start.3 = (bf16[2,2,2,16,1024]{4,3,2,1,0:T(8,128)(2,1)}, bf16[2,2,2,16,1024]{4,3,2,1,0:T(8,128)(2,1)S(1)}, u32[]{:S(2)}) copy-start(bf16[2,2,2,16,1024]{4,3,2,1,0:T(8,128)(2,1)S(1)} %maximum_select_fusion.3) | copy-start | bytes 786436
  79.7 1.8 %collective-permute-start.17 = (bf16[128,1024]{1,0:T(8,128)(2,1)S(1)}, bf16[128,1024]{1,0:T(8,128)(2,1)S(1)}, u32[]{:S(2)}, u32[]{:S(2)}) collective-permute-start(bf16[128,1024]{1,0:T(8,128)(2,1)S(1)} %bitcast.293), channel_id=1, source_target_pairs={{0,1},{1,0},{2,3},{3,2},{4,5},{5,4},{6,7},{7,6},{8,9},{9,8},{10,11... | collective-permute-start | bytes 786440 | tf_op jit(solution)/shard_map/ppermute | solution.py:61
  81.1 0.7 copy-start.6
  81.9 0.7 copy-start.7
  92.1 2.1 %collective-permute-start.18 = (f32[128,1024]{1,0:T(8,128)}, f32[128,1024]{1,0:T(8,128)S(1)}, u32[]{:S(2)}, u32[]{:S(2)}) collective-permute-start(f32[128,1024]{1,0:T(8,128)} %get-tuple-element.18), channel_id=1, source_target_pairs={{0,1},{1,0},{2,3},{3,2},{4,5},{5,4},{6,7},{7,6},{8,9},{9,8},{10,11... | collective-permute-start | bytes 1572872 | tf_op jit(solution)/shard_map/ppermute | solution.py:98
  92.2 4.6 %collective-permute-start.20 = (f32[128,1024]{1,0:T(8,128)}, f32[128,1024]{1,0:T(8,128)S(1)}, u32[]{:S(2)}, u32[]{:S(2)}) collective-permute-start(f32[128,1024]{1,0:T(8,128)} %get-tuple-element.20), channel_id=1, source_target_pairs={{0,1},{1,0},{2,3},{3,2},{4,5},{5,4},{6,7},{7,6},{8,9},{9,8},{10,11... | collective-permute-start | bytes 1572872 | tf_op jit(solution)/shard_map/ppermute | solution.py:98
  95.4 6.4 %collective-permute-start.19 = (f32[2,2,16,1024]{3,2,1,0:T(8,128)S(1)}, f32[2,2,16,1024]{3,2,1,0:T(8,128)S(1)}, u32[]{:S(2)}, u32[]{:S(2)}) collective-permute-start(f32[2,2,16,1024]{3,2,1,0:T(8,128)S(1)} %bitcast_select_fusion.4), channel_id=1, source_target_pairs={{0,2},{1,5},{2,0},{3,7},{4,6},{5,1},{6,4},{7,3},{8,10},{9,13},{10,... | collective-permute-start | bytes 786440 | tf_op jit(solution)/shard_map/ppermute | solution.py:83
  98.0 6.6 %collective-permute-start.21 = (f32[2,2,16,1024]{3,2,1,0:T(8,128)S(1)}, f32[2,2,16,1024]{3,2,1,0:T(8,128)S(1)}, u32[]{:S(2)}, u32[]{:S(2)}) collective-permute-start(f32[2,2,16,1024]{3,2,1,0:T(8,128)S(1)} %bitcast_select_fusion.2), channel_id=1, source_target_pairs={{0,2},{1,5},{2,0},{3,7},{4,6},{5,1},{6,4},{7,3},{8,10},{9,13},{10,... | collective-permute-start | bytes 786440 | tf_op jit(solution)/shard_map/ppermute | solution.py:83
  104.8 6.4 %collective-permute-start.22 = (f32[2,2,16,1024]{3,2,1,0:T(8,128)S(1)}, f32[2,2,16,1024]{3,2,1,0:T(8,128)S(1)}, u32[]{:S(2)}, u32[]{:S(2)}) collective-permute-start(f32[2,2,16,1024]{3,2,1,0:T(8,128)S(1)} %bitcast.296), channel_id=1, source_target_pairs={{0,4},{1,3},{2,6},{3,1},{4,0},{5,7},{6,2},{7,5},{8,12},{9,11},{10,... | collective-permute-start | bytes 786440 | tf_op jit(solution)/shard_map/ppermute | solution.py:83
  111.3 7.3 %collective-permute-start.23 = (f32[2,16,1024]{2,1,0:T(8,128)S(1)}, f32[2,16,1024]{2,1,0:T(8,128)S(1)}, u32[]{:S(2)}, u32[]{:S(2)}) collective-permute-start(f32[2,16,1024]{2,1,0:T(8,128)S(1)} %dynamic-slice_bitcast_fusion), channel_id=1, source_target_pairs={{0,8},{1,9},{2,10},{3,11},{4,12},{5,13},{6,14},{7,15},{8,0},{9,1},... | collective-permute-start | bytes 393224 | tf_op jit(solution)/shard_map/ppermute | solution.py:83

commit v13 on v10

--- a/solution.py
+++ b/solution.py
@@ -24,7 +24,7 @@
     return [(d, d ^ (1 << (b1 if d & 1 else b0))) for d in range(n)]
 
 
-def gather_rows(x, n):
+def gather_rows(x, n, tie=None):
     m = n.bit_length() - 1
     me = lax.axis_index("aux")
     odd = (me & 1) == 1
@@ -50,6 +50,9 @@
         have1 = sorted(have1 + [b1], reverse=True)
         acc = acc.reshape((-1,) + x.shape)
     flat = acc.reshape((n // 2 * x.shape[0],) + x.shape[1:])
+    if tie is not None:
+        flat, tie = lax.optimization_barrier((flat, tie))
+        return flat, lax.ppermute(flat, "aux", partners(n, 0, 0)), tie
     return flat, lax.ppermute(flat, "aux", partners(n, 0, 0))
 
 
@@ -168,7 +171,13 @@
     own_denom = denom[:, 0, :]
     resps = [rhs[:, state, :] / own_denom for state in range(states)]
     for step in range(ITERS):
-        got = [gather_rows(resp.astype(jnp.bfloat16), n) for resp in resps]
+        got = []
+        for state, resp in enumerate(resps):
+            if step == 0 and state == 0:
+                mine, theirs, ordered_occ = gather_rows(resp.astype(jnp.bfloat16), n, ordered_occ)
+                got.append((mine, theirs))
+            else:
+                got.append(gather_rows(resp.astype(jnp.bfloat16), n))
         keep, send = exchange_part(ordered_occ, [g[0] for g in got], [g[1] for g in got], vir_ints)
         for state in range(states):
             exchange = scatter_sum(keep[state], send[state], n)

time: 116 us -> 117 us (level)
  waiting for transfers between devices: 46 us -> 50.8 us
  starting transfers between devices: 35.7 us -> 32.1 us
    ppermute x12, starting transfers between devices: 18.2 us -> 15.8 us  [gather_rows(): theirs = lax.ppermute(acc, 'aux', partners(n, b0, b1))]
    ppermute x12, waiting for transfers between devices: 23.6 us -> 25.7 us  [scatter_sum(): acc = kept + lax.ppermute(sent, 'aux', partners(n, b0, b1))]
    ppermute x12, waiting for transfers between devices: 17.4 us -> 18.9 us  [gather_rows(): theirs = lax.ppermute(acc, 'aux', partners(n, b0, b1))]
    ppermute x12, starting transfers between devices: 16.2 us -> 15 us  [scatter_sum(): acc = kept + lax.ppermute(sent, 'aux', partners(n, b0, b1))]
    ppermute x4 -> x3, waiting for transfers between devices: 1.85 us -> 3.02 us  [gather_rows(): return (flat, lax.ppermute(flat, 'aux', partners(n, 0, 0)))]
  transfers between devices with their start and end apart: 32 -> 32, of which waited for: 25 -> 28; matrix products, arithmetic and copies ran while one was open for 8% -> 8% of each run, Pallas kernels for 0% -> 0%
where the time goes in v13:
time: 117 us; the launch traced here: 116 us
  waiting for transfers between devices  50.8 us (43%)
  starting transfers between devices  32.1 us (27%)
  Pallas kernels  19.1 us (16%)
  other arithmetic  8.5 us (7%)
  local copies, waits for them, and re-layouts  4.2 us (4%)
    ppermute x12, waiting for transfers between devices, scatter_sum(): acc = kept + lax.ppermute(sent, 'aux', partners(n, b0, b1))  25.7 us
    pallas_call x2, Pallas kernels, exchange_part(): pl.pallas_call(functools.partial(exchange_kernel, states), grid=(local_au...  19.1 us
    ppermute x12, waiting for transfers between devices, gather_rows(): theirs = lax.ppermute(acc, 'aux', partners(n, b0, b1))  18.9 us
    ppermute x12, starting transfers between devices, gather_rows(): theirs = lax.ppermute(acc, 'aux', partners(n, b0, b1))  15.8 us
    ppermute x12, starting transfers between devices, scatter_sum(): acc = kept + lax.ppermute(sent, 'aux', partners(n, b0, b1))  15 us
    add x4, other arithmetic, scatter_sum(): keep.reshape(shape)  4.44 us
    ppermute x4, waiting for transfers between devices, scatter_sum(): lax.ppermute(send, 'aux', partners(n, 0, 0)).reshape(shape)  3.23 us
    ppermute x3, waiting for transfers between devices, gather_rows(): return (flat, lax.ppermute(flat, 'aux', partners(n, 0, 0)))  3.02 us
  transfers between devices with their start and end apart: 32, of which 28 were waited for; matrix products, arithmetic and copies ran while one was open for 8% of the time, Pallas kernels for 0%

profile of v13, /device:TPU:0, one launch (start us, length us, event | category | flops | bytes accessed | tf_op | source)
XLA Modules:
  0.0 116.3 jit_solution(1813003323291459062)
XLA Ops:
  0.0 1.1 fusion.32
  1.1 0.8 dynamic_slice.103
  1.9 0.8 fusion.8
  2.6 4.1 %collective-permute-start.3 = (bf16[1,16,1024]{2,1,0:T(8,128)(2,1)S(1)}, bf16[1,16,1024]{2,1,0:T(8,128)(2,1)S(1)}, u32[]{:S(2)}, u32[]{:S(2)}) collective-permute-start(bf16[1,16,1024]{2,1,0:T(8,128)(2,1)S(1)} %get-tuple-element.59), channel_id=1, source_target_pairs={{0,8},{1,9},{2,10},{3,11},{4,12},{5,13},{6,14},{7,15},{8,0},{9,1},... | collective-permute-start | bytes 98312 | tf_op jit(solution)/shard_map/ppermute | solution.py:36
  6.8 1.1 fusion.1
  7.9 1.1 fusion
  9.1 1.1 convolution_convert_fusion
  10.2 1.4 %collective-permute-done = bf16[1,16,1024]{2,1,0:T(8,128)(2,1)S(1)} collective-permute-done((bf16[1,16,1024]{2,1,0:T(8,128)(2,1)S(1)}, bf16[1,16,1024]{2,1,0:T(8,128)(2,1)S(1)}, u32[]{:S(2)}, u32[]{:S(2)}) %collective-permute-start) | collective-permute-done | bytes 32800 | tf_op jit(solution)/shard_map/ppermute | solution.py:36
  11.6 1.6 %collective-permute-start.1 = (bf16[2,16,1024]{2,1,0:T(8,128)(2,1)S(1)}, bf16[2,16,1024]{2,1,0:T(8,128)(2,1)S(1)}, u32[]{:S(2)}, u32[]{:S(2)}) collective-permute-start(bf16[2,16,1024]{2,1,0:T(8,128)(2,1)S(1)} %pad_maximum_fusion.6), channel_id=1, source_target_pairs={{0,4},{1,3},{2,6},{3,1},{4,0},{5,7},{6,2},{7,5},{8,12},{9,11},{10,... | collective-permute-start | bytes 196616 | tf_op jit(solution)/shard_map/ppermute | solution.py:36
  13.3 0.5 collective-permute-start.4
  13.8 2.1 %collective-permute-done.1 = bf16[2,16,1024]{2,1,0:T(8,128)(2,1)S(1)} collective-permute-done((bf16[2,16,1024]{2,1,0:T(8,128)(2,1)S(1)}, bf16[2,16,1024]{2,1,0:T(8,128)(2,1)S(1)}, u32[]{:S(2)}, u32[]{:S(2)}) %collective-permute-start.1) | collective-permute-done | bytes 65568 | tf_op jit(solution)/shard_map/ppermute | solution.py:36
  15.9 1.6 %collective-permute-start.2 = (bf16[4,16,1024]{2,1,0:T(8,128)(2,1)S(1)}, bf16[4,16,1024]{2,1,0:T(8,128)(2,1)S(1)}, u32[]{:S(2)}, u32[]{:S(2)}) collective-permute-start(bf16[4,16,1024]{2,1,0:T(8,128)(2,1)S(1)} %bitcast.261), channel_id=1, source_target_pairs={{0,2},{1,5},{2,0},{3,7},{4,6},{5,1},{6,4},{7,3},{8,10},{9,13},{10,... | collective-permute-start | bytes 393224 | tf_op jit(solution)/shard_map/ppermute | solution.py:36
  17.5 0.7 collective-permute-done.4
  18.3 1.6 %collective-permute-start.5 = (bf16[4,16,1024]{2,1,0:T(8,128)(2,1)S(1)}, bf16[4,16,1024]{2,1,0:T(8,128)(2,1)S(1)}, u32[]{:S(2)}, u32[]{:S(2)}) collective-permute-start(bf16[4,16,1024]{2,1,0:T(8,128)(2,1)S(1)} %bitcast.263), channel_id=1, source_target_pairs={{0,2},{1,5},{2,0},{3,7},{4,6},{5,1},{6,4},{7,3},{8,10},{9,13},{10,... | collective-permute-start | bytes 393224 | tf_op jit(solution)/shard_map/ppermute | solution.py:36
  19.9 1.1 collective-permute-done.2
  21.2 2.2 %collective-permute-done.5 = bf16[4,16,1024]{2,1,0:T(8,128)(2,1)S(1)} collective-permute-done((bf16[4,16,1024]{2,1,0:T(8,128)(2,1)S(1)}, bf16[4,16,1024]{2,1,0:T(8,128)(2,1)S(1)}, u32[]{:S(2)}, u32[]{:S(2)}) %collective-permute-start.5) | collective-permute-done | bytes 131104 | tf_op jit(solution)/shard_map/ppermute | solution.py:36
  23.6 1.5 %collective-permute-done.7.refs_3_ = bf16[128,1024]{1,0:T(8,128)(2,1)S(1)} collective-permute-done((bf16[128,1024]{1,0:T(8,128)(2,1)S(1)}, bf16[128,1024]{1,0:T(8,128)(2,1)S(1)}, u32[]{:S(2)}, u32[]{:S(2)}) %collective-permute-start.7) | collective-permute-done | bytes 262176 | tf_op jit(solution)/shard_map/ppermute | solution.py:56
  25.1 0.7 copy-done.7
  25.8 9.5 %shard_map.55 = (f32[128,1024]{1,0:T(8,128)}, f32[128,1024]{1,0:T(8,128)}, f32[128,1024]{1,0:T(8,128)}, f32[128,1024]{1,0:T(8,128)}) custom-call(bf16[4,256,256]{2,1,0:T(8,128)(2,1)} %bitcast.224, bf16[128,1024]{1,0:T(8,128)(2,1)} %bitcast.256, bf16[128,1024]{1,0:T(8,128)(2,1)} %bitcast.260, bf16[128,1024]{1,0:T(8,128)(2,1)} %copy-done.5, ...), custom_call_target="tpu_custom_call" | custom-call | tf_op jit(solution)/shard_map/pallas_call | solution.py:125
  35.8 1.6 %collective-permute-done.8 = f32[128,1024]{1,0:T(8,128)S(1)} collective-permute-done((f32[128,1024]{1,0:T(8,128)}, f32[128,1024]{1,0:T(8,128)S(1)}, u32[]{:S(2)}, u32[]{:S(2)}) %collective-permute-start.8) | collective-permute-done | bytes 524320 | tf_op jit(solution)/shard_map/ppermute | solution.py:66
  37.4 1.1 add.178
  38.6 1.6 %collective-permute-start.9 = (f32[2,2,16,1024]{3,2,1,0:T(8,128)S(1)}, f32[2,2,16,1024]{3,2,1,0:T(8,128)S(1)}, u32[]{:S(2)}, u32[]{:S(2)}) collective-permute-start(f32[2,2,16,1024]{3,2,1,0:T(8,128)S(1)} %bitcast_select_fusion.8), channel_id=1, source_target_pairs={{0,2},{1,5},{2,0},{3,7},{4,6},{5,1},{6,4},{7,3},{8,10},{9,13},{10,... | collective-permute-start | bytes 786440 | tf_op jit(solution)/shard_map/ppermute | solution.py:87
  40.1 1.1 add.192
  41.3 0.6 collective-permute-start.16
  41.9 3.1 %collective-permute-done.9 = f32[2,2,16,1024]{3,2,1,0:T(8,128)S(1)} collective-permute-done((f32[2,2,16,1024]{3,2,1,0:T(8,128)S(1)}, f32[2,2,16,1024]{3,2,1,0:T(8,128)S(1)}, u32[]{:S(2)}, u32[]{:S(2)}) %collective-permute-start.9) | collective-permute-done | bytes 262176 | tf_op jit(solution)/shard_map/ppermute | solution.py:87
  45.1 1.0 collective-permute-start.10
  46.1 2.5 %collective-permute-done.16 = f32[2,2,16,1024]{3,2,1,0:T(8,128)S(1)} collective-permute-done((f32[2,2,16,1024]{3,2,1,0:T(8,128)S(1)}, f32[2,2,16,1024]{3,2,1,0:T(8,128)S(1)}, u32[]{:S(2)}, u32[]{:S(2)}) %collective-permute-start.16) | collective-permute-done | bytes 262176 | tf_op jit(solution)/shard_map/ppermute | solution.py:87
  48.6 1.0 collective-permute-start.17
  49.6 0.5 collective-permute-done.10
  50.2 1.6 %collective-permute-start.11 = (f32[16,1024]{1,0:T(8,128)S(1)}, f32[16,1024]{1,0:T(8,128)S(1)}, u32[]{:S(2)}, u32[]{:S(2)}) collective-permute-start(f32[16,1024]{1,0:T(8,128)S(1)} %dynamic-slice_bitcast_fusion.7), channel_id=1, source_target_pairs={{0,8},{1,9},{2,10},{3,11},{4,12},{5,13},{6,14},{7,15},{8,0},{9,1},... | collective-permute-start | bytes 196616 | tf_op jit(solution)/shard_map/ppermute | solution.py:87
  51.7 2.6 %collective-permute-done.17 = f32[2,16,1024]{2,1,0:T(8,128)S(1)} collective-permute-done((f32[2,16,1024]{2,1,0:T(8,128)S(1)}, f32[2,16,1024]{2,1,0:T(8,128)S(1)}, u32[]{:S(2)}, u32[]{:S(2)}) %collective-permute-start.17) | collective-permute-done | bytes 131104 | tf_op jit(solution)/shard_map/ppermute | solution.py:87
  54.4 1.8 %collective-permute-start.18 = (f32[16,1024]{1,0:T(8,128)S(1)}, f32[16,1024]{1,0:T(8,128)S(1)}, u32[]{:S(2)}, u32[]{:S(2)}) collective-permute-start(f32[16,1024]{1,0:T(8,128)S(1)} %dynamic-slice_bitcast_fusion.6), channel_id=1, source_target_pairs={{0,8},{1,9},{2,10},{3,11},{4,12},{5,13},{6,14},{7,15},{8,0},{9,1},... | collective-permute-start | bytes 196616 | tf_op jit(solution)/shard_map/ppermute | solution.py:87
  56.2 1.3 %collective-permute-done.11 = f32[16,1024]{1,0:T(8,128)S(1)} collective-permute-done((f32[16,1024]{1,0:T(8,128)S(1)}, f32[16,1024]{1,0:T(8,128)S(1)}, u32[]{:S(2)}, u32[]{:S(2)}) %collective-permute-start.11) | collective-permute-done | bytes 65568 | tf_op jit(solution)/shard_map/ppermute | solution.py:87
  57.5 2.8 %collective-permute-done.18 = f32[16,1024]{1,0:T(8,128)S(1)} collective-permute-done((f32[16,1024]{1,0:T(8,128)S(1)}, f32[16,1024]{1,0:T(8,128)S(1)}, u32[]{:S(2)}, u32[]{:S(2)}) %collective-permute-start.18) | collective-permute-done | bytes 65568 | tf_op jit(solution)/shard_map/ppermute | solution.py:87
  60.4 1.1 collective-permute-start.19
  61.6 1.9 %collective-permute-start.12 = (bf16[1,16,1024]{2,1,0:T(8,128)(2,1)S(1)}, bf16[1,16,1024]{2,1,0:T(8,128)(2,1)S(1)}, u32[]{:S(2)}, u32[]{:S(2)}) collective-permute-start(bf16[1,16,1024]{2,1,0:T(8,128)(2,1)S(1)} %get-tuple-element.57), channel_id=1, source_target_pairs={{0,8},{1,9},{2,10},{3,11},{4,12},{5,13},{6,14},{7,15},{8,0},{9,1},... | collective-permute-start | bytes 98312 | tf_op jit(solution)/shard_map/ppermute | solution.py:36
  63.4 2.0 %collective-permute-done.19 = bf16[1,16,1024]{2,1,0:T(8,128)(2,1)S(1)} collective-permute-done((bf16[1,16,1024]{2,1,0:T(8,128)(2,1)S(1)}, bf16[1,16,1024]{2,1,0:T(8,128)(2,1)S(1)}, u32[]{:S(2)}, u32[]{:S(2)}) %collective-permute-start.19) | collective-permute-done | bytes 32800 | tf_op jit(solution)/shard_map/ppermute | solution.py:36
  65.8 1.0 collective-permute-done.12
  66.8 0.9 collective-permute-start.13
  67.7 2.8 %collective-permute-done.20 = bf16[2,16,1024]{2,1,0:T(8,128)(2,1)S(1)} collective-permute-done((bf16[2,16,1024]{2,1,0:T(8,128)(2,1)S(1)}, bf16[2,16,1024]{2,1,0:T(8,128)(2,1)S(1)}, u32[]{:S(2)}, u32[]{:S(2)}) %collective-permute-start.20) | collective-permute-done | bytes 65568 | tf_op jit(solution)/shard_map/ppermute | solution.py:36
  70.5 1.4 %collective-permute-done.13 = bf16[2,16,1024]{2,1,0:T(8,128)(2,1)S(1)} collective-permute-done((bf16[2,16,1024]{2,1,0:T(8,128)(2,1)S(1)}, bf16[2,16,1024]{2,1,0:T(8,128)(2,1)S(1)}, u32[]{:S(2)}, u32[]{:S(2)}) %collective-permute-start.13) | collective-permute-done | bytes 65568 | tf_op jit(solution)/shard_map/ppermute | solution.py:36
  72.0 1.4 %collective-permute-start.21 = (bf16[4,16,1024]{2,1,0:T(8,128)(2,1)S(1)}, bf16[4,16,1024]{2,1,0:T(8,128)(2,1)S(1)}, u32[]{:S(2)}, u32[]{:S(2)}) collective-permute-start(bf16[4,16,1024]{2,1,0:T(8,128)(2,1)S(1)} %bitcast.264), channel_id=1, source_target_pairs={{0,2},{1,5},{2,0},{3,7},{4,6},{5,1},{6,4},{7,3},{8,10},{9,13},{10,... | collective-permute-start | bytes 393224 | tf_op jit(solution)/shard_map/ppermute | solution.py:36
  73.4 0.7 collective-permute-start.14
  74.2 2.8 %collective-permute-done.21 = bf16[4,16,1024]{2,1,0:T(8,128)(2,1)S(1)} collective-permute-done((bf16[4,16,1024]{2,1,0:T(8,128)(2,1)S(1)}, bf16[4,16,1024]{2,1,0:T(8,128)(2,1)S(1)}, u32[]{:S(2)}, u32[]{:S(2)}) %collective-permute-start.21) | collective-permute-done | bytes 131104 | tf_op jit(solution)/shard_map/ppermute | solution.py:36
  77.2 1.3 %collective-permute-done.14 = bf16[4,16,1024]{2,1,0:T(8,128)(2,1)S(1)} collective-permute-done((bf16[4,16,1024]{2,1,0:T(8,128)(2,1)S(1)}, bf16[4,16,1024]{2,1,0:T(8,128)(2,1)S(1)}, u32[]{:S(2)}, u32[]{:S(2)}) %collective-permute-start.14) | collective-permute-done | bytes 131104 | tf_op jit(solution)/shard_map/ppermute | solution.py:36
  78.7 1.4 %collective-permute-done.22.refs_2_ = bf16[128,1024]{1,0:T(8,128)(2,1)S(1)} collective-permute-done((bf16[128,1024]{1,0:T(8,128)(2,1)S(1)}, bf16[128,1024]{1,0:T(8,128)(2,1)S(1)}, u32[]{:S(2)}, u32[]{:S(2)}) %collective-permute-start.22) | collective-permute-done | bytes 262176 | tf_op jit(solution)/shard_map/ppermute | solution.py:56
  80.2 0.7 copy-done.6
  80.9 9.5 %shard_map.56 = (f32[128,1024]{1,0:T(8,128)}, f32[128,1024]{1,0:T(8,128)}, f32[128,1024]{1,0:T(8,128)}, f32[128,1024]{1,0:T(8,128)}) custom-call(bf16[4,256,256]{2,1,0:T(8,128)(2,1)} %bitcast.225, bf16[128,1024]{1,0:T(8,128)(2,1)} %bitcast.258, bf16[128,1024]{1,0:T(8,128)(2,1)} %bitcast.254, bf16[128,1024]{1,0:T(8,128)(2,1)} %copy-done.6, ...), custom_call_target="tpu_custom_call" | custom-call | tf_op jit(solution)/shard_map/pallas_call | solution.py:125
  90.9 1.6 %collective-permute-done.24 = f32[128,1024]{1,0:T(8,128)S(1)} collective-permute-done((f32[128,1024]{1,0:T(8,128)}, f32[128,1024]{1,0:T(8,128)S(1)}, u32[]{:S(2)}, u32[]{:S(2)}) %collective-permute-start.24) | collective-permute-done | bytes 524320 | tf_op jit(solution)/shard_map/ppermute | solution.py:66
  92.5 1.1 add.198
  93.7 1.4 %collective-permute-start.25 = (f32[2,2,16,1024]{3,2,1,0:T(8,128)S(1)}, f32[2,2,16,1024]{3,2,1,0:T(8,128)S(1)}, u32[]{:S(2)}, u32[]{:S(2)}) collective-permute-start(f32[2,2,16,1024]{3,2,1,0:T(8,128)S(1)} %bitcast_select_fusion.4), channel_id=1, source_target_pairs={{0,2},{1,5},{2,0},{3,7},{4,6},{5,1},{6,4},{7,3},{8,10},{9,13},{10,... | collective-permute-start | bytes 786440 | tf_op jit(solution)/shard_map/ppermute | solution.py:87
  95.1 1.1 add.204
  96.2 0.8 collective-permute-start.29
  97.0 3.1 %collective-permute-done.25 = f32[2,2,16,1024]{3,2,1,0:T(8,128)S(1)} collective-permute-done((f32[2,2,16,1024]{3,2,1,0:T(8,128)S(1)}, f32[2,2,16,1024]{3,2,1,0:T(8,128)S(1)}, u32[]{:S(2)}, u32[]{:S(2)}) %collective-permute-start.25) | collective-permute-done | bytes 262176 | tf_op jit(solution)/shard_map/ppermute | solution.py:87
  100.2 0.9 collective-permute-start.26
  101.1 2.6 %collective-permute-done.29 = f32[2,2,16,1024]{3,2,1,0:T(8,128)S(1)} collective-permute-done((f32[2,2,16,1024]{3,2,1,0:T(8,128)S(1)}, f32[2,2,16,1024]{3,2,1,0:T(8,128)S(1)}, u32[]{:S(2)}, u32[]{:S(2)}) %collective-permute-start.29) | collective-permute-done | bytes 262176 | tf_op jit(solution)/shard_map/ppermute | solution.py:87
  103.7 0.9 collective-permute-start.30
  104.6 0.6 collective-permute-done.26
  105.3 1.7 %collective-permute-start.27 = (f32[16,1024]{1,0:T(8,128)S(1)}, f32[16,1024]{1,0:T(8,128)S(1)}, u32[]{:S(2)}, u32[]{:S(2)}) collective-permute-start(f32[16,1024]{1,0:T(8,128)S(1)} %dynamic-slice_bitcast_fusion.5), channel_id=1, source_target_pairs={{0,8},{1,9},{2,10},{3,11},{4,12},{5,13},{6,14},{7,15},{8,0},{9,1},... | collective-permute-start | bytes 196616 | tf_op jit(solution)/shard_map/ppermute | solution.py:87
  106.9 2.5 %collective-permute-done.30 = f32[2,16,1024]{2,1,0:T(8,128)S(1)} collective-permute-done((f32[2,16,1024]{2,1,0:T(8,128)S(1)}, f32[2,16,1024]{2,1,0:T(8,128)S(1)}, u32[]{:S(2)}, u32[]{:S(2)}) %collective-permute-start.30) | collective-permute-done | bytes 131104 | tf_op jit(solution)/shard_map/ppermute | solution.py:87
  109.5 1.9 %collective-permute-start.31 = (f32[16,1024]{1,0:T(8,128)S(1)}, f32[16,1024]{1,0:T(8,128)S(1)}, u32[]{:S(2)}, u32[]{:S(2)}) collective-permute-start(f32[16,1024]{1,0:T(8,128)S(1)} %dynamic-slice_bitcast_fusion.4), channel_id=1, source_target_pairs={{0,8},{1,9},{2,10},{3,11},{4,12},{5,13},{6,14},{7,15},{8,0},{9,1},... | collective-permute-start | bytes 196616 | tf_op jit(solution)/shard_map/ppermute | solution.py:87
  111.4 1.2 %collective-permute-done.27 = f32[16,1024]{1,0:T(8,128)S(1)} collective-permute-done((f32[16,1024]{1,0:T(8,128)S(1)}, f32[16,1024]{1,0:T(8,128)S(1)}, u32[]{:S(2)}, u32[]{:S(2)}) %collective-permute-start.27) | collective-permute-done | bytes 65568 | tf_op jit(solution)/shard_map/ppermute | solution.py:87
  112.6 2.9 %collective-permute-done.31 = f32[16,1024]{1,0:T(8,128)S(1)} collective-permute-done((f32[16,1024]{1,0:T(8,128)S(1)}, f32[16,1024]{1,0:T(8,128)S(1)}, u32[]{:S(2)}, u32[]{:S(2)}) %collective-permute-start.31) | collective-permute-done | bytes 65568 | tf_op jit(solution)/shard_map/ppermute | solution.py:87
  115.5 0.8 copy.64
  (83 shorter events, 3.1 us)
Async XLA Ops:
  2.6 10.6 %collective-permute-start.3 = (bf16[1,16,1024]{2,1,0:T(8,128)(2,1)S(1)}, bf16[1,16,1024]{2,1,0:T(8,128)(2,1)S(1)}, u32[]{:S(2)}, u32[]{:S(2)}) collective-permute-start(bf16[1,16,1024]{2,1,0:T(8,128)(2,1)S(1)} %get-tuple-element.59), channel_id=1, source_target_pairs={{0,8},{1,9},{2,10},{3,11},{4,12},{5,13},{6,14},{7,15},{8,0},{9,1},... | collective-permute-start | bytes 98312 | tf_op jit(solution)/shard_map/ppermute | solution.py:36
  6.7 4.8 %collective-permute-start = (bf16[1,16,1024]{2,1,0:T(8,128)(2,1)S(1)}, bf16[1,16,1024]{2,1,0:T(8,128)(2,1)S(1)}, u32[]{:S(2)}, u32[]{:S(2)}) collective-permute-start(bf16[1,16,1024]{2,1,0:T(8,128)(2,1)S(1)} %get-tuple-element.60), channel_id=1, source_target_pairs={{0,8},{1,9},{2,10},{3,11},{4,12},{5,13},{6,14},{7,15},{8,0},{9,1},... | collective-permute-start | bytes 98312 | tf_op jit(solution)/shard_map/ppermute | solution.py:36
  11.6 4.3 %collective-permute-start.1 = (bf16[2,16,1024]{2,1,0:T(8,128)(2,1)S(1)}, bf16[2,16,1024]{2,1,0:T(8,128)(2,1)S(1)}, u32[]{:S(2)}, u32[]{:S(2)}) collective-permute-start(bf16[2,16,1024]{2,1,0:T(8,128)(2,1)S(1)} %pad_maximum_fusion.6), channel_id=1, source_target_pairs={{0,4},{1,3},{2,6},{3,1},{4,0},{5,7},{6,2},{7,5},{8,12},{9,11},{10,... | collective-permute-start | bytes 196616 | tf_op jit(solution)/shard_map/ppermute | solution.py:36
  13.3 5.0 %collective-permute-start.4 = (bf16[2,16,1024]{2,1,0:T(8,128)(2,1)S(1)}, bf16[2,16,1024]{2,1,0:T(8,128)(2,1)S(1)}, u32[]{:S(2)}, u32[]{:S(2)}) collective-permute-start(bf16[2,16,1024]{2,1,0:T(8,128)(2,1)S(1)} %pad_maximum_fusion.7), channel_id=1, source_target_pairs={{0,4},{1,3},{2,6},{3,1},{4,0},{5,7},{6,2},{7,5},{8,12},{9,11},{10,... | collective-permute-start | bytes 196616 | tf_op jit(solution)/shard_map/ppermute | solution.py:36
  15.9 5.0 %collective-permute-start.2 = (bf16[4,16,1024]{2,1,0:T(8,128)(2,1)S(1)}, bf16[4,16,1024]{2,1,0:T(8,128)(2,1)S(1)}, u32[]{:S(2)}, u32[]{:S(2)}) collective-permute-start(bf16[4,16,1024]{2,1,0:T(8,128)(2,1)S(1)} %bitcast.261), channel_id=1, source_target_pairs={{0,2},{1,5},{2,0},{3,7},{4,6},{5,1},{6,4},{7,3},{8,10},{9,13},{10,... | collective-permute-start | bytes 393224 | tf_op jit(solution)/shard_map/ppermute | solution.py:36
  18.3 5.0 %collective-permute-start.5 = (bf16[4,16,1024]{2,1,0:T(8,128)(2,1)S(1)}, bf16[4,16,1024]{2,1,0:T(8,128)(2,1)S(1)}, u32[]{:S(2)}, u32[]{:S(2)}) collective-permute-start(bf16[4,16,1024]{2,1,0:T(8,128)(2,1)S(1)} %bitcast.263), channel_id=1, source_target_pairs={{0,2},{1,5},{2,0},{3,7},{4,6},{5,1},{6,4},{7,3},{8,10},{9,13},{10,... | collective-permute-start | bytes 393224 | tf_op jit(solution)/shard_map/ppermute | solution.py:36
  21.1 4.0 %copy-start.1 = (bf16[2,2,2,16,1024]{4,3,2,1,0:T(8,128)(2,1)}, bf16[2,2,2,16,1024]{4,3,2,1,0:T(8,128)(2,1)S(1)}, u32[]{:S(2)}) copy-start(bf16[2,2,2,16,1024]{4,3,2,1,0:T(8,128)(2,1)S(1)} %maximum_select_fusion) | copy-start | bytes 786436
  21.1 2.5 %collective-permute-start.6 = (bf16[128,1024]{1,0:T(8,128)(2,1)S(1)}, bf16[128,1024]{1,0:T(8,128)(2,1)S(1)}, u32[]{:S(2)}, u32[]{:S(2)}) collective-permute-start(bf16[128,1024]{1,0:T(8,128)(2,1)S(1)} %bitcast.255), channel_id=1, source_target_pairs={{0,1},{1,0},{2,3},{3,2},{4,5},{5,4},{6,7},{7,6},{8,9},{9,8},{10,11... | collective-permute-start | bytes 786440 | tf_op jit(solution)/shard_map/ppermute | solution.py:55
  23.4 1.6 %copy-start.3 = (bf16[2,2,2,16,1024]{4,3,2,1,0:T(8,128)(2,1)}, bf16[2,2,2,16,1024]{4,3,2,1,0:T(8,128)(2,1)S(1)}, u32[]{:S(2)}) copy-start(bf16[2,2,2,16,1024]{4,3,2,1,0:T(8,128)(2,1)S(1)} %maximum_select_fusion.1) | copy-start | bytes 786436
  23.4 36.9 %copy-start.8 = (f32[1024]{0:T(1024)S(1)}, f32[1024]{0:T(1024)}, u32[]{:S(2)}) copy-start(f32[1024]{0:T(1024)} %param.7) | copy-start | bytes 12292
  23.5 1.6 %collective-permute-start.7 = (bf16[128,1024]{1,0:T(8,128)(2,1)S(1)}, bf16[128,1024]{1,0:T(8,128)(2,1)S(1)}, u32[]{:S(2)}, u32[]{:S(2)}) collective-permute-start(bf16[128,1024]{1,0:T(8,128)(2,1)S(1)} %bitcast.259), channel_id=1, source_target_pairs={{0,1},{1,0},{2,3},{3,2},{4,5},{5,4},{6,7},{7,6},{8,9},{9,8},{10,11... | collective-permute-start | bytes 786440 | tf_op jit(solution)/shard_map/ppermute | solution.py:56
  23.5 1.5 %copy-start.5 = (bf16[128,1024]{1,0:T(8,128)(2,1)}, bf16[128,1024]{1,0:T(8,128)(2,1)S(1)}, u32[]{:S(2)}) copy-start(bf16[128,1024]{1,0:T(8,128)(2,1)S(1)} %collective-permute-done.6.refs_2_) | copy-start | bytes 786436
  25.1 0.7 copy-start.7
  35.3 2.1 %collective-permute-start.8 = (f32[128,1024]{1,0:T(8,128)}, f32[128,1024]{1,0:T(8,128)S(1)}, u32[]{:S(2)}, u32[]{:S(2)}) collective-permute-start(f32[128,1024]{1,0:T(8,128)} %get-tuple-element.18), channel_id=1, source_target_pairs={{0,1},{1,0},{2,3},{3,2},{4,5},{5,4},{6,7},{7,6},{8,9},{9,8},{10,11... | collective-permute-start | bytes 1572872 | tf_op jit(solution)/shard_map/ppermute | solution.py:66
  35.4 4.7 %collective-permute-start.15 = (f32[128,1024]{1,0:T(8,128)}, f32[128,1024]{1,0:T(8,128)S(1)}, u32[]{:S(2)}, u32[]{:S(2)}) collective-permute-start(f32[128,1024]{1,0:T(8,128)} %get-tuple-element.20), channel_id=1, source_target_pairs={{0,1},{1,0},{2,3},{3,2},{4,5},{5,4},{6,7},{7,6},{8,9},{9,8},{10,11... | collective-permute-start | bytes 1572872 | tf_op jit(solution)/shard_map/ppermute | solution.py:66
  38.6 6.4 %collective-permute-start.9 = (f32[2,2,16,1024]{3,2,1,0:T(8,128)S(1)}, f32[2,2,16,1024]{3,2,1,0:T(8,128)S(1)}, u32[]{:S(2)}, u32[]{:S(2)}) collective-permute-start(f32[2,2,16,1024]{3,2,1,0:T(8,128)S(1)} %bitcast_select_fusion.8), channel_id=1, source_target_pairs={{0,2},{1,5},{2,0},{3,7},{4,6},{5,1},{6,4},{7,3},{8,10},{9,13},{10,... | collective-permute-start | bytes 786440 | tf_op jit(solution)/shard_map/ppermute | solution.py:87
  41.3 7.3 %collective-permute-start.16 = (f32[2,2,16,1024]{3,2,1,0:T(8,128)S(1)}, f32[2,2,16,1024]{3,2,1,0:T(8,128)S(1)}, u32[]{:S(2)}, u32[]{:S(2)}) collective-permute-start(f32[2,2,16,1024]{3,2,1,0:T(8,128)S(1)} %bitcast_select_fusion.6), channel_id=1, source_target_pairs={{0,2},{1,5},{2,0},{3,7},{4,6},{5,1},{6,4},{7,3},{8,10},{9,13},{10,... | collective-permute-start | bytes 786440 | tf_op jit(solution)/shard_map/ppermute | solution.py:87
  45.1 5.0 %collective-permute-start.10 = (f32[2,16,1024]{2,1,0:T(8,128)S(1)}, f32[2,16,1024]{2,1,0:T(8,128)S(1)}, u32[]{:S(2)}, u32[]{:S(2)}) collective-permute-start(f32[2,16,1024]{2,1,0:T(8,128)S(1)} %dynamic-slice_bitcast_fusion.3), channel_id=1, source_target_pairs={{0,4},{1,3},{2,6},{3,1},{4,0},{5,7},{6,2},{7,5},{8,12},{9,11},{10,... | collective-permute-start | bytes 393224 | tf_op jit(solution)/shard_map/ppermute | solution.py:87
  48.6 5.7 %collective-permute-start.17 = (f32[2,16,1024]{2,1,0:T(8,128)S(1)}, f32[2,16,1024]{2,1,0:T(8,128)S(1)}, u32[]{:S(2)}, u32[]{:S(2)}) collective-permute-start(f32[2,16,1024]{2,1,0:T(8,128)S(1)} %dynamic-slice_bitcast_fusion.2), channel_id=1, source_target_pairs={{0,4},{1,3},{2,6},{3,1},{4,0},{5,7},{6,2},{7,5},{8,12},{9,11},{10,... | collective-permute-start | bytes 393224 | tf_op jit(solution)/shard_map/ppermute | solution.py:87
  50.2 7.3 %collective-permute-start.11 = (f32[16,1024]{1,0:T(8,128)S(1)}, f32[16,1024]{1,0:T(8,128)S(1)}, u32[]{:S(2)}, u32[]{:S(2)}) collective-permute-start(f32[16,1024]{1,0:T(8,128)S(1)} %dynamic-slice_bitcast_fusion.7), channel_id=1, source_target_pairs={{0,8},{1,9},{2,10},{3,11},{4,12},{5,13},{6,14},{7,15},{8,0},{9,1},... | collective-permute-start | bytes 196616 | tf_op jit(solution)/shard_map/ppermute | solution.py:87
  54.4 5.9 %collective-permute-start.18 = (f32[16,1024]{1,0:T(8,128)S(1)}, f32[16,1024]{1,0:T(8,128)S(1)}, u32[]{:S(2)}, u32[]{:S(2)}) collective-permute-start(f32[16,1024]{1,0:T(8,128)S(1)} %dynamic-slice_bitcast_fusion.6), channel_id=1, source_target_pairs={{0,8},{1,9},{2,10},{3,11},{4,12},{5,13},{6,14},{7,15},{8,0},{9,1},... | collective-permute-start | bytes 196616 | tf_op jit(solution)/shard_map/ppermute | solution.py:87
  60.4 5.0 %collective-permute-start.19 = (bf16[1,16,1024]{2,1,0:T(8,128)(2,1)S(1)}, bf16[1,16,1024]{2,1,0:T(8,128)(2,1)S(1)}, u32[]{:S(2)}, u32[]{:S(2)}) collective-permute-start(bf16[1,16,1024]{2,1,0:T(8,128)(2,1)S(1)} %get-tuple-element.25), channel_id=1, source_target_pairs={{0,8},{1,9},{2,10},{3,11},{4,12},{5,13},{6,14},{7,15},{8,0},{9,1},... | collective-permute-start | bytes 98312 | tf_op jit(solution)/shard_map/ppermute | solution.py:36
  61.6 5.2 %collective-permute-start.12 = (bf16[1,16,1024]{2,1,0:T(8,128)(2,1)S(1)}, bf16[1,16,1024]{2,1,0:T(8,128)(2,1)S(1)}, u32[]{:S(2)}, u32[]{:S(2)}) collective-permute-start(bf16[1,16,1024]{2,1,0:T(8,128)(2,1)S(1)} %get-tuple-element.57), channel_id=1, source_target_pairs={{0,8},{1,9},{2,10},{3,11},{4,12},{5,13},{6,14},{7,15},{8,0},{9,1},... | collective-permute-start | bytes 98312 | tf_op jit(solution)/shard_map/ppermute | solution.py:36
  65.5 5.0 %collective-permute-start.20 = (bf16[2,16,1024]{2,1,0:T(8,128)(2,1)S(1)}, bf16[2,16,1024]{2,1,0:T(8,128)(2,1)S(1)}, u32[]{:S(2)}, u32[]{:S(2)}) collective-permute-start(bf16[2,16,1024]{2,1,0:T(8,128)(2,1)S(1)} %pad_maximum_fusion.9), channel_id=1, source_target_pairs={{0,4},{1,3},{2,6},{3,1},{4,0},{5,7},{6,2},{7,5},{8,12},{9,11},{10,... | collective-permute-start | bytes 196616 | tf_op jit(solution)/shard_map/ppermute | solution.py:36
  66.8 5.1 %collective-permute-start.13 = (bf16[2,16,1024]{2,1,0:T(8,128)(2,1)S(1)}, bf16[2,16,1024]{2,1,0:T(8,128)(2,1)S(1)}, u32[]{:S(2)}, u32[]{:S(2)}) collective-permute-start(bf16[2,16,1024]{2,1,0:T(8,128)(2,1)S(1)} %pad_maximum_fusion.8), channel_id=1, source_target_pairs={{0,4},{1,3},{2,6},{3,1},{4,0},{5,7},{6,2},{7,5},{8,12},{9,11},{10,... | collective-permute-start | bytes 196616 | tf_op jit(solution)/shard_map/ppermute | solution.py:36
  72.0 5.0 %collective-permute-start.21 = (bf16[4,16,1024]{2,1,0:T(8,128)(2,1)S(1)}, bf16[4,16,1024]{2,1,0:T(8,128)(2,1)S(1)}, u32[]{:S(2)}, u32[]{:S(2)}) collective-permute-start(bf16[4,16,1024]{2,1,0:T(8,128)(2,1)S(1)} %bitcast.264), channel_id=1, source_target_pairs={{0,2},{1,5},{2,0},{3,7},{4,6},{5,1},{6,4},{7,3},{8,10},{9,13},{10,... | collective-permute-start | bytes 393224 | tf_op jit(solution)/shard_map/ppermute | solution.py:36
  73.4 5.0 %collective-permute-start.14 = (bf16[4,16,1024]{2,1,0:T(8,128)(2,1)S(1)}, bf16[4,16,1024]{2,1,0:T(8,128)(2,1)S(1)}, u32[]{:S(2)}, u32[]{:S(2)}) collective-permute-start(bf16[4,16,1024]{2,1,0:T(8,128)(2,1)S(1)} %bitcast.262), channel_id=1, source_target_pairs={{0,2},{1,5},{2,0},{3,7},{4,6},{5,1},{6,4},{7,3},{8,10},{9,13},{10,... | collective-permute-start | bytes 393224 | tf_op jit(solution)/shard_map/ppermute | solution.py:36
  77.1 3.1 %copy-start = (bf16[2,2,2,16,1024]{4,3,2,1,0:T(8,128)(2,1)}, bf16[2,2,2,16,1024]{4,3,2,1,0:T(8,128)(2,1)S(1)}, u32[]{:S(2)}) copy-start(bf16[2,2,2,16,1024]{4,3,2,1,0:T(8,128)(2,1)S(1)} %maximum_select_fusion.3) | copy-start | bytes 786436
  77.1 1.6 %collective-permute-start.23 = (bf16[128,1024]{1,0:T(8,128)(2,1)S(1)}, bf16[128,1024]{1,0:T(8,128)(2,1)S(1)}, u32[]{:S(2)}, u32[]{:S(2)}) collective-permute-start(bf16[128,1024]{1,0:T(8,128)(2,1)S(1)} %bitcast.253), channel_id=1, source_target_pairs={{0,1},{1,0},{2,3},{3,2},{4,5},{5,4},{6,7},{7,6},{8,9},{9,8},{10,11... | collective-permute-start | bytes 786440 | tf_op jit(solution)/shard_map/ppermute | solution.py:56
  78.5 1.6 %copy-start.2 = (bf16[2,2,2,16,1024]{4,3,2,1,0:T(8,128)(2,1)}, bf16[2,2,2,16,1024]{4,3,2,1,0:T(8,128)(2,1)S(1)}, u32[]{:S(2)}) copy-start(bf16[2,2,2,16,1024]{4,3,2,1,0:T(8,128)(2,1)S(1)} %maximum_select_fusion.2) | copy-start | bytes 786436
  78.6 1.6 %collective-permute-start.22 = (bf16[128,1024]{1,0:T(8,128)(2,1)S(1)}, bf16[128,1024]{1,0:T(8,128)(2,1)S(1)}, u32[]{:S(2)}, u32[]{:S(2)}) collective-permute-start(bf16[128,1024]{1,0:T(8,128)(2,1)S(1)} %bitcast.257), channel_id=1, source_target_pairs={{0,1},{1,0},{2,3},{3,2},{4,5},{5,4},{6,7},{7,6},{8,9},{9,8},{10,11... | collective-permute-start | bytes 786440 | tf_op jit(solution)/shard_map/ppermute | solution.py:56
  78.7 1.5 %copy-start.4 = (bf16[128,1024]{1,0:T(8,128)(2,1)}, bf16[128,1024]{1,0:T(8,128)(2,1)S(1)}, u32[]{:S(2)}) copy-start(bf16[128,1024]{1,0:T(8,128)(2,1)S(1)} %collective-permute-done.23.refs_3_) | copy-start | bytes 786436
  80.2 0.7 copy-start.6
  90.4 2.1 %collective-permute-start.24 = (f32[128,1024]{1,0:T(8,128)}, f32[128,1024]{1,0:T(8,128)S(1)}, u32[]{:S(2)}, u32[]{:S(2)}) collective-permute-start(f32[128,1024]{1,0:T(8,128)} %get-tuple-element.22), channel_id=1, source_target_pairs={{0,1},{1,0},{2,3},{3,2},{4,5},{5,4},{6,7},{7,6},{8,9},{9,8},{10,11... | collective-permute-start | bytes 1572872 | tf_op jit(solution)/shard_map/ppermute | solution.py:66
  90.5 4.5 %collective-permute-start.28 = (f32[128,1024]{1,0:T(8,128)}, f32[128,1024]{1,0:T(8,128)S(1)}, u32[]{:S(2)}, u32[]{:S(2)}) collective-permute-start(f32[128,1024]{1,0:T(8,128)} %get-tuple-element.24), channel_id=1, source_target_pairs={{0,1},{1,0},{2,3},{3,2},{4,5},{5,4},{6,7},{7,6},{8,9},{9,8},{10,11... | collective-permute-start | bytes 1572872 | tf_op jit(solution)/shard_map/ppermute | solution.py:66
  93.7 6.4 %collective-permute-start.25 = (f32[2,2,16,1024]{3,2,1,0:T(8,128)S(1)}, f32[2,2,16,1024]{3,2,1,0:T(8,128)S(1)}, u32[]{:S(2)}, u32[]{:S(2)}) collective-permute-start(f32[2,2,16,1024]{3,2,1,0:T(8,128)S(1)} %bitcast_select_fusion.4), channel_id=1, source_target_pairs={{0,2},{1,5},{2,0},{3,7},{4,6},{5,1},{6,4},{7,3},{8,10},{9,13},{10,... | collective-permute-start | bytes 786440 | tf_op jit(solution)/shard_map/ppermute | solution.py:87
  96.2 7.4 %collective-permute-start.29 = (f32[2,2,16,1024]{3,2,1,0:T(8,128)S(1)}, f32[2,2,16,1024]{3,2,1,0:T(8,128)S(1)}, u32[]{:S(2)}, u32[]{:S(2)}) collective-permute-start(f32[2,2,16,1024]{3,2,1,0:T(8,128)S(1)} %bitcast_select_fusion.2), channel_id=1, source_target_pairs={{0,2},{1,5},{2,0},{3,7},{4,6},{5,1},{6,4},{7,3},{8,10},{9,13},{10,... | collective-permute-start | bytes 786440 | tf_op jit(solution)/shard_map/ppermute | solution.py:87
  100.2 5.0 %collective-permute-start.26 = (f32[2,16,1024]{2,1,0:T(8,128)S(1)}, f32[2,16,1024]{2,1,0:T(8,128)S(1)}, u32[]{:S(2)}, u32[]{:S(2)}) collective-permute-start(f32[2,16,1024]{2,1,0:T(8,128)S(1)} %dynamic-slice_bitcast_fusion.1), channel_id=1, source_target_pairs={{0,4},{1,3},{2,6},{3,1},{4,0},{5,7},{6,2},{7,5},{8,12},{9,11},{10,... | collective-permute-start | bytes 393224 | tf_op jit(solution)/shard_map/ppermute | solution.py:87
  103.7 5.7 %collective-permute-start.30 = (f32[2,16,1024]{2,1,0:T(8,128)S(1)}, f32[2,16,1024]{2,1,0:T(8,128)S(1)}, u32[]{:S(2)}, u32[]{:S(2)}) collective-permute-start(f32[2,16,1024]{2,1,0:T(8,128)S(1)} %dynamic-slice_bitcast_fusion), channel_id=1, source_target_pairs={{0,4},{1,3},{2,6},{3,1},{4,0},{5,7},{6,2},{7,5},{8,12},{9,11},{10,... | collective-permute-start | bytes 393224 | tf_op jit(solution)/shard_map/ppermute | solution.py:87
  105.3 7.3 %collective-permute-start.27 = (f32[16,1024]{1,0:T(8,128)S(1)}, f32[16,1024]{1,0:T(8,128)S(1)}, u32[]{:S(2)}, u32[]{:S(2)}) collective-permute-start(f32[16,1024]{1,0:T(8,128)S(1)} %dynamic-slice_bitcast_fusion.5), channel_id=1, source_target_pairs={{0,8},{1,9},{2,10},{3,11},{4,12},{5,13},{6,14},{7,15},{8,0},{9,1},... | collective-permute-start | bytes 196616 | tf_op jit(solution)/shard_map/ppermute | solution.py:87
  109.5 5.9 %collective-permute-start.31 = (f32[16,1024]{1,0:T(8,128)S(1)}, f32[16,1024]{1,0:T(8,128)S(1)}, u32[]{:S(2)}, u32[]{:S(2)}) collective-permute-start(f32[16,1024]{1,0:T(8,128)S(1)} %dynamic-slice_bitcast_fusion.4), channel_id=1, source_target_pairs={{0,8},{1,9},{2,10},{3,11},{4,12},{5,13},{6,14},{7,15},{8,0},{9,1},... | collective-permute-start | bytes 196616 | tf_op jit(solution)/shard_map/ppermute | solution.py:87

commit v14 on v10

--- a/solution.py
+++ b/solution.py
@@ -87,7 +87,7 @@
     return acc
 
 
-def exchange_kernel(states, occ_ref, *refs):
+def exchange_kernel(states, rows, core_ref, occ_ref, *refs):
     mine, theirs = refs[:states], refs[states:2 * states]
     vir_ref = refs[2 * states]
     keep, send = refs[2 * states + 1:3 * states + 1], refs[3 * states + 1:4 * states + 1]
@@ -98,10 +98,19 @@
     @pl.when(pl.program_id(0) == 0)
     def _():
         for s in range(states):
+            cols = slice(s * nvir, (s + 1) * nvir)
             keep[s][...] = jnp.zeros_like(keep[s])
             send[s][...] = jnp.zeros_like(send[s])
-            r_ref[:split, s * nvir:(s + 1) * nvir] = mine[s][...]
-            r_ref[split:, s * nvir:(s + 1) * nvir] = theirs[s][...]
+            if rows:
+                core = core_ref[0]
+                for b in range(split // rows):
+                    at_mine = pl.multiple_of((2 * b + core) * rows, rows)
+                    at_theirs = pl.multiple_of((2 * b + 1 - core) * rows, rows)
+                    r_ref[pl.ds(at_mine, rows), cols] = mine[s][b * rows:(b + 1) * rows]
+                    r_ref[pl.ds(at_theirs, rows), cols] = theirs[s][b * rows:(b + 1) * rows]
+            else:
+                r_ref[:split, cols] = mine[s][...]
+                r_ref[split:, cols] = theirs[s][...]
 
     half = jnp.dot(occ_ref[0], r_ref[...], preferred_element_type=jnp.float32).astype(jnp.bfloat16)
     vir = vir_ref[0]
@@ -113,23 +122,23 @@
         send[s][...] += term[split:]
 
 
-def exchange_part(occ_ints, mine, theirs, vir_ints):
+def exchange_part(core, occ_ints, mine, theirs, vir_ints, rows):
     local_aux, nocc, _ = occ_ints.shape
     nvir = vir_ints.shape[1]
     states = len(mine)
     piece = pl.BlockSpec((nocc // 2, nvir), lambda p: (0, 0))
     out = jax.ShapeDtypeStruct((nocc // 2, nvir), jnp.float32)
     results = pl.pallas_call(
-        functools.partial(exchange_kernel, states),
+        functools.partial(exchange_kernel, states, rows),
         grid=(local_aux,),
-        in_specs=[pl.BlockSpec((1, nocc, nocc), lambda p: (p, 0, 0))]
+        in_specs=[pl.BlockSpec(memory_space=pltpu.SMEM), pl.BlockSpec((1, nocc, nocc), lambda p: (p, 0, 0))]
         + [piece] * (2 * states)
         + [pl.BlockSpec((1, nvir, nvir), lambda p: (p, 0, 0))],
         out_specs=[piece] * (2 * states),
         out_shape=[out] * (2 * states),
         scratch_shapes=[pltpu.VMEM((nocc, states * nvir), jnp.bfloat16)],
         compiler_params=pltpu.CompilerParams(dimension_semantics=("arbitrary",)),
-    )(occ_ints, *mine, *theirs, vir_ints)
+    )(core, occ_ints, *mine, *theirs, vir_ints)
     return results[:states], results[states:]
 
 
@@ -164,12 +173,16 @@
     position = lax.axis_index("aux")
     my_occ = lax.dynamic_slice_in_dim(occ_energy, position * own_rows, own_rows, 0)
     denom = vir_energy[None, None, :] - my_occ[:, None, None]
-    ordered_occ = order_columns(order_rows(occ_ints, n, position & 1), n, position & 1)
+    rows = own_rows if own_rows % 16 == 0 else 0
+    ordered_occ = order_rows(occ_ints, n, position & 1)
+    if not rows:
+        ordered_occ = order_columns(ordered_occ, n, position & 1)
+    core = (position & 1).astype(jnp.int32).reshape(1)
     own_denom = denom[:, 0, :]
     resps = [rhs[:, state, :] / own_denom for state in range(states)]
     for step in range(ITERS):
         got = [gather_rows(resp.astype(jnp.bfloat16), n) for resp in resps]
-        keep, send = exchange_part(ordered_occ, [g[0] for g in got], [g[1] for g in got], vir_ints)
+        keep, send = exchange_part(core, ordered_occ, [g[0] for g in got], [g[1] for g in got], vir_ints, rows)
         for state in range(states):
             exchange = scatter_sum(keep[state], send[state], n)
             resps[state] = 0.4 * resps[state] + 0.6 * (rhs[:, state, :] - exchange) / own_denom

time: 116 us -> 115 us (level)
  starting transfers between devices: 35.7 us -> 40 us
  waiting for transfers between devices: 46 us -> 42.2 us
    ppermute x12, waiting for transfers between devices: 23.6 us -> 19 us  [scatter_sum(): acc = kept + lax.ppermute(sent, 'aux', partners(n, b0, b1))]
    ppermute x12, starting transfers between devices: 16.2 us -> 20.6 us  [scatter_sum(): acc = kept + lax.ppermute(sent, 'aux', partners(n, b0, b1))]
  transfers between devices with their start and end apart: 32 -> 32, of which waited for: 25 -> 25; matrix products, arithmetic and copies ran while one was open for 8% -> 6% of each run, Pallas kernels for 0% -> 0%
where the time goes in v14:
time: 115 us; the launch traced here: 114 us
  waiting for transfers between devices  42.2 us (37%)
  starting transfers between devices  40 us (35%)
  Pallas kernels  19.1 us (17%)
  other arithmetic  8.23 us (7%)
  local copies, waits for them, and re-layouts  4.22 us (4%)
    ppermute x12, starting transfers between devices, scatter_sum(): acc = kept + lax.ppermute(sent, 'aux', partners(n, b0, b1))  20.6 us
    pallas_call x2, Pallas kernels, exchange_part(): pl.pallas_call(functools.partial(exchange_kernel, states, rows), grid=(lo...  19.1 us
    ppermute x12, waiting for transfers between devices, scatter_sum(): acc = kept + lax.ppermute(sent, 'aux', partners(n, b0, b1))  19 us
    ppermute x12, waiting for transfers between devices, gather_rows(): theirs = lax.ppermute(acc, 'aux', partners(n, b0, b1))  18.3 us
    ppermute x12, starting transfers between devices, gather_rows(): theirs = lax.ppermute(acc, 'aux', partners(n, b0, b1))  18.1 us
    add x4, other arithmetic, scatter_sum(): keep.reshape(shape)  4.44 us
    ppermute x4, waiting for transfers between devices, scatter_sum(): lax.ppermute(send, 'aux', partners(n, 0, 0)).reshape(shape)  3.3 us
  transfers between devices with their start and end apart: 32, of which 25 were waited for; matrix products, arithmetic and copies ran while one was open for 6% of the time, Pallas kernels for 0%

profile of v14, /device:TPU:0, one launch (start us, length us, event | category | flops | bytes accessed | tf_op | source)
XLA Modules:
  0.0 114.2 jit_solution(11417386687058816443)
XLA Ops:
  0.0 1.1 fusion.24
  1.1 0.8 dynamic_slice.103
  1.9 0.8 fusion.5
  2.6 4.1 %collective-permute-start.3 = (bf16[1,16,1024]{2,1,0:T(8,128)(2,1)S(1)}, bf16[1,16,1024]{2,1,0:T(8,128)(2,1)S(1)}, u32[]{:S(2)}, u32[]{:S(2)}) collective-permute-start(bf16[1,16,1024]{2,1,0:T(8,128)(2,1)S(1)} %get-tuple-element.57), channel_id=1, source_target_pairs={{0,8},{1,9},{2,10},{3,11},{4,12},{5,13},{6,14},{7,15},{8,0},{9,1},... | collective-permute-start | bytes 98312 | tf_op jit(solution)/shard_map/ppermute | solution.py:36
  6.8 2.2 %collective-permute-done.3 = bf16[1,16,1024]{2,1,0:T(8,128)(2,1)S(1)} collective-permute-done((bf16[1,16,1024]{2,1,0:T(8,128)(2,1)S(1)}, bf16[1,16,1024]{2,1,0:T(8,128)(2,1)S(1)}, u32[]{:S(2)}, u32[]{:S(2)}) %collective-permute-start.3) | collective-permute-done | bytes 32800 | tf_op jit(solution)/shard_map/ppermute | solution.py:36
  9.0 1.7 %collective-permute-start.4 = (bf16[2,16,1024]{2,1,0:T(8,128)(2,1)S(1)}, bf16[2,16,1024]{2,1,0:T(8,128)(2,1)S(1)}, u32[]{:S(2)}, u32[]{:S(2)}) collective-permute-start(bf16[2,16,1024]{2,1,0:T(8,128)(2,1)S(1)} %pad_maximum_fusion.7), channel_id=1, source_target_pairs={{0,4},{1,3},{2,6},{3,1},{4,0},{5,7},{6,2},{7,5},{8,12},{9,11},{10,... | collective-permute-start | bytes 196616 | tf_op jit(solution)/shard_map/ppermute | solution.py:36
  10.7 0.9 collective-permute-done
  11.6 1.6 %collective-permute-start.1 = (bf16[2,16,1024]{2,1,0:T(8,128)(2,1)S(1)}, bf16[2,16,1024]{2,1,0:T(8,128)(2,1)S(1)}, u32[]{:S(2)}, u32[]{:S(2)}) collective-permute-start(bf16[2,16,1024]{2,1,0:T(8,128)(2,1)S(1)} %pad_maximum_fusion.6), channel_id=1, source_target_pairs={{0,4},{1,3},{2,6},{3,1},{4,0},{5,7},{6,2},{7,5},{8,12},{9,11},{10,... | collective-permute-start | bytes 196616 | tf_op jit(solution)/shard_map/ppermute | solution.py:36
  13.4 1.8 %collective-permute-start.5 = (bf16[4,16,1024]{2,1,0:T(8,128)(2,1)S(1)}, bf16[4,16,1024]{2,1,0:T(8,128)(2,1)S(1)}, u32[]{:S(2)}, u32[]{:S(2)}) collective-permute-start(bf16[4,16,1024]{2,1,0:T(8,128)(2,1)S(1)} %bitcast.259), channel_id=1, source_target_pairs={{0,2},{1,5},{2,0},{3,7},{4,6},{5,1},{6,4},{7,3},{8,10},{9,13},{10,... | collective-permute-start | bytes 393224 | tf_op jit(solution)/shard_map/ppermute | solution.py:36
  15.2 1.2 %collective-permute-done.1 = bf16[2,16,1024]{2,1,0:T(8,128)(2,1)S(1)} collective-permute-done((bf16[2,16,1024]{2,1,0:T(8,128)(2,1)S(1)}, bf16[2,16,1024]{2,1,0:T(8,128)(2,1)S(1)}, u32[]{:S(2)}, u32[]{:S(2)}) %collective-permute-start.1) | collective-permute-done | bytes 65568 | tf_op jit(solution)/shard_map/ppermute | solution.py:36
  16.4 1.1 collective-permute-start.2
  17.5 0.9 collective-permute-done.5
  18.6 2.9 %collective-permute-done.2 = bf16[4,16,1024]{2,1,0:T(8,128)(2,1)S(1)} collective-permute-done((bf16[4,16,1024]{2,1,0:T(8,128)(2,1)S(1)}, bf16[4,16,1024]{2,1,0:T(8,128)(2,1)S(1)}, u32[]{:S(2)}, u32[]{:S(2)}) %collective-permute-start.2) | collective-permute-done | bytes 131104 | tf_op jit(solution)/shard_map/ppermute | solution.py:36
  21.7 1.1 select_bitcast_fusion.1
  22.8 0.9 pad_maximum_fusion
  23.6 0.7 copy-done.4
  24.4 9.5 %shard_map.55 = (f32[128,1024]{1,0:T(8,128)}, f32[128,1024]{1,0:T(8,128)}, f32[128,1024]{1,0:T(8,128)}, f32[128,1024]{1,0:T(8,128)}) custom-call(s32[1]{0:T(128)} %bitcast.1.core_ref, bf16[4,256,256]{2,1,0:T(8,128)(2,1)} %bitcast.225, bf16[128,1024]{1,0:T(8,128)(2,1)} %bitcast.256, bf16[128,1024]{1,0:T(8,128)(2,1)} %bitcast.252, ...), custom_call_target="tpu_custom_call" | custom-call | tf_op jit(solution)/shard_map/pallas_call | solution.py:131
  33.9 0.5 collective-permute-start.8
  34.5 1.7 %collective-permute-done.8 = f32[128,1024]{1,0:T(8,128)S(1)} collective-permute-done((f32[128,1024]{1,0:T(8,128)}, f32[128,1024]{1,0:T(8,128)S(1)}, u32[]{:S(2)}, u32[]{:S(2)}) %collective-permute-start.8) | collective-permute-done | bytes 524320 | tf_op jit(solution)/shard_map/ppermute | solution.py:63
  36.2 1.1 add.132
  37.3 1.1 collective-permute-start.9
  38.4 1.1 add.146
  39.5 1.1 collective-permute-start.16
  40.6 3.1 %collective-permute-done.9 = f32[2,2,16,1024]{3,2,1,0:T(8,128)S(1)} collective-permute-done((f32[2,2,16,1024]{3,2,1,0:T(8,128)S(1)}, f32[2,2,16,1024]{3,2,1,0:T(8,128)S(1)}, u32[]{:S(2)}, u32[]{:S(2)}) %collective-permute-start.9) | collective-permute-done | bytes 262176 | tf_op jit(solution)/shard_map/ppermute | solution.py:84
  43.8 1.3 %collective-permute-start.10 = (f32[2,16,1024]{2,1,0:T(8,128)S(1)}, f32[2,16,1024]{2,1,0:T(8,128)S(1)}, u32[]{:S(2)}, u32[]{:S(2)}) collective-permute-start(f32[2,16,1024]{2,1,0:T(8,128)S(1)} %dynamic-slice_bitcast_fusion.3), channel_id=1, source_target_pairs={{0,4},{1,3},{2,6},{3,1},{4,0},{5,7},{6,2},{7,5},{8,12},{9,11},{10,... | collective-permute-start | bytes 393224 | tf_op jit(solution)/shard_map/ppermute | solution.py:84
  45.1 1.9 %collective-permute-done.16 = f32[2,2,16,1024]{3,2,1,0:T(8,128)S(1)} collective-permute-done((f32[2,2,16,1024]{3,2,1,0:T(8,128)S(1)}, f32[2,2,16,1024]{3,2,1,0:T(8,128)S(1)}, u32[]{:S(2)}, u32[]{:S(2)}) %collective-permute-start.16) | collective-permute-done | bytes 262176 | tf_op jit(solution)/shard_map/ppermute | solution.py:84
  47.1 1.3 %collective-permute-start.17 = (f32[2,16,1024]{2,1,0:T(8,128)S(1)}, f32[2,16,1024]{2,1,0:T(8,128)S(1)}, u32[]{:S(2)}, u32[]{:S(2)}) collective-permute-start(f32[2,16,1024]{2,1,0:T(8,128)S(1)} %dynamic-slice_bitcast_fusion.2), channel_id=1, source_target_pairs={{0,4},{1,3},{2,6},{3,1},{4,0},{5,7},{6,2},{7,5},{8,12},{9,11},{10,... | collective-permute-start | bytes 393224 | tf_op jit(solution)/shard_map/ppermute | solution.py:84
  48.5 0.4 collective-permute-done.10
  48.9 2.8 %collective-permute-start.11 = (f32[16,1024]{1,0:T(8,128)S(1)}, f32[16,1024]{1,0:T(8,128)S(1)}, u32[]{:S(2)}, u32[]{:S(2)}) collective-permute-start(f32[16,1024]{1,0:T(8,128)S(1)} %dynamic-slice_bitcast_fusion.7), channel_id=1, source_target_pairs={{0,8},{1,9},{2,10},{3,11},{4,12},{5,13},{6,14},{7,15},{8,0},{9,1},... | collective-permute-start | bytes 196616 | tf_op jit(solution)/shard_map/ppermute | solution.py:84
  51.7 1.1 collective-permute-done.17
  52.9 2.3 %collective-permute-start.18 = (f32[16,1024]{1,0:T(8,128)S(1)}, f32[16,1024]{1,0:T(8,128)S(1)}, u32[]{:S(2)}, u32[]{:S(2)}) collective-permute-start(f32[16,1024]{1,0:T(8,128)S(1)} %dynamic-slice_bitcast_fusion.6), channel_id=1, source_target_pairs={{0,8},{1,9},{2,10},{3,11},{4,12},{5,13},{6,14},{7,15},{8,0},{9,1},... | collective-permute-start | bytes 196616 | tf_op jit(solution)/shard_map/ppermute | solution.py:84
  55.2 3.7 %collective-permute-done.18 = f32[16,1024]{1,0:T(8,128)S(1)} collective-permute-done((f32[16,1024]{1,0:T(8,128)S(1)}, f32[16,1024]{1,0:T(8,128)S(1)}, u32[]{:S(2)}, u32[]{:S(2)}) %collective-permute-start.18) | collective-permute-done | bytes 65568 | tf_op jit(solution)/shard_map/ppermute | solution.py:84
  58.9 1.7 %collective-permute-start.19 = (bf16[1,16,1024]{2,1,0:T(8,128)(2,1)S(1)}, bf16[1,16,1024]{2,1,0:T(8,128)(2,1)S(1)}, u32[]{:S(2)}, u32[]{:S(2)}) collective-permute-start(bf16[1,16,1024]{2,1,0:T(8,128)(2,1)S(1)} %get-tuple-element.21), channel_id=1, source_target_pairs={{0,8},{1,9},{2,10},{3,11},{4,12},{5,13},{6,14},{7,15},{8,0},{9,1},... | collective-permute-start | bytes 98312 | tf_op jit(solution)/shard_map/ppermute | solution.py:36
  60.6 1.3 %collective-permute-start.12 = (bf16[1,16,1024]{2,1,0:T(8,128)(2,1)S(1)}, bf16[1,16,1024]{2,1,0:T(8,128)(2,1)S(1)}, u32[]{:S(2)}, u32[]{:S(2)}) collective-permute-start(bf16[1,16,1024]{2,1,0:T(8,128)(2,1)S(1)} %get-tuple-element.55), channel_id=1, source_target_pairs={{0,8},{1,9},{2,10},{3,11},{4,12},{5,13},{6,14},{7,15},{8,0},{9,1},... | collective-permute-start | bytes 98312 | tf_op jit(solution)/shard_map/ppermute | solution.py:36
  61.9 2.2 %collective-permute-done.19 = bf16[1,16,1024]{2,1,0:T(8,128)(2,1)S(1)} collective-permute-done((bf16[1,16,1024]{2,1,0:T(8,128)(2,1)S(1)}, bf16[1,16,1024]{2,1,0:T(8,128)(2,1)S(1)}, u32[]{:S(2)}, u32[]{:S(2)}) %collective-permute-start.19) | collective-permute-done | bytes 32800 | tf_op jit(solution)/shard_map/ppermute | solution.py:36
  64.2 0.5 collective-permute-start.20
  64.7 0.7 collective-permute-done.12
  65.4 2.1 %collective-permute-start.13 = (bf16[2,16,1024]{2,1,0:T(8,128)(2,1)S(1)}, bf16[2,16,1024]{2,1,0:T(8,128)(2,1)S(1)}, u32[]{:S(2)}, u32[]{:S(2)}) collective-permute-start(bf16[2,16,1024]{2,1,0:T(8,128)(2,1)S(1)} %pad_maximum_fusion.8), channel_id=1, source_target_pairs={{0,4},{1,3},{2,6},{3,1},{4,0},{5,7},{6,2},{7,5},{8,12},{9,11},{10,... | collective-permute-start | bytes 196616 | tf_op jit(solution)/shard_map/ppermute | solution.py:36
  67.5 1.6 %collective-permute-done.20 = bf16[2,16,1024]{2,1,0:T(8,128)(2,1)S(1)} collective-permute-done((bf16[2,16,1024]{2,1,0:T(8,128)(2,1)S(1)}, bf16[2,16,1024]{2,1,0:T(8,128)(2,1)S(1)}, u32[]{:S(2)}, u32[]{:S(2)}) %collective-permute-start.20) | collective-permute-done | bytes 65568 | tf_op jit(solution)/shard_map/ppermute | solution.py:36
  69.1 1.4 %collective-permute-done.13 = bf16[2,16,1024]{2,1,0:T(8,128)(2,1)S(1)} collective-permute-done((bf16[2,16,1024]{2,1,0:T(8,128)(2,1)S(1)}, bf16[2,16,1024]{2,1,0:T(8,128)(2,1)S(1)}, u32[]{:S(2)}, u32[]{:S(2)}) %collective-permute-start.13) | collective-permute-done | bytes 65568 | tf_op jit(solution)/shard_map/ppermute | solution.py:36
  70.6 1.5 %collective-permute-start.21 = (bf16[4,16,1024]{2,1,0:T(8,128)(2,1)S(1)}, bf16[4,16,1024]{2,1,0:T(8,128)(2,1)S(1)}, u32[]{:S(2)}, u32[]{:S(2)}) collective-permute-start(bf16[4,16,1024]{2,1,0:T(8,128)(2,1)S(1)} %bitcast.262), channel_id=1, source_target_pairs={{0,2},{1,5},{2,0},{3,7},{4,6},{5,1},{6,4},{7,3},{8,10},{9,13},{10,... | collective-permute-start | bytes 393224 | tf_op jit(solution)/shard_map/ppermute | solution.py:36
  72.2 0.6 collective-permute-start.14
  72.8 2.8 %collective-permute-done.21 = bf16[4,16,1024]{2,1,0:T(8,128)(2,1)S(1)} collective-permute-done((bf16[4,16,1024]{2,1,0:T(8,128)(2,1)S(1)}, bf16[4,16,1024]{2,1,0:T(8,128)(2,1)S(1)}, u32[]{:S(2)}, u32[]{:S(2)}) %collective-permute-start.21) | collective-permute-done | bytes 131104 | tf_op jit(solution)/shard_map/ppermute | solution.py:36
  75.8 1.4 %collective-permute-done.14 = bf16[4,16,1024]{2,1,0:T(8,128)(2,1)S(1)} collective-permute-done((bf16[4,16,1024]{2,1,0:T(8,128)(2,1)S(1)}, bf16[4,16,1024]{2,1,0:T(8,128)(2,1)S(1)}, u32[]{:S(2)}, u32[]{:S(2)}) %collective-permute-start.14) | collective-permute-done | bytes 131104 | tf_op jit(solution)/shard_map/ppermute | solution.py:36
  77.4 1.5 %collective-permute-done.22.refs_2_ = bf16[128,1024]{1,0:T(8,128)(2,1)S(1)} collective-permute-done((bf16[128,1024]{1,0:T(8,128)(2,1)S(1)}, bf16[128,1024]{1,0:T(8,128)(2,1)S(1)}, u32[]{:S(2)}, u32[]{:S(2)}) %collective-permute-start.22) | collective-permute-done | bytes 262176 | tf_op jit(solution)/shard_map/ppermute | solution.py:53
  78.9 0.7 copy-done.7
  79.6 9.5 %shard_map.56 = (f32[128,1024]{1,0:T(8,128)}, f32[128,1024]{1,0:T(8,128)}, f32[128,1024]{1,0:T(8,128)}, f32[128,1024]{1,0:T(8,128)}) custom-call(s32[1]{0:T(128)} %bitcast.1.core_ref, bf16[4,256,256]{2,1,0:T(8,128)(2,1)} %bitcast.226, bf16[128,1024]{1,0:T(8,128)(2,1)} %bitcast.258, bf16[128,1024]{1,0:T(8,128)(2,1)} %bitcast.254, ...), custom_call_target="tpu_custom_call" | custom-call | tf_op jit(solution)/shard_map/pallas_call | solution.py:131
  89.1 0.1 collective-permute-start.24
  89.3 0.4 collective-permute-start.28
  89.6 1.6 %collective-permute-done.24 = f32[128,1024]{1,0:T(8,128)S(1)} collective-permute-done((f32[128,1024]{1,0:T(8,128)}, f32[128,1024]{1,0:T(8,128)S(1)}, u32[]{:S(2)}, u32[]{:S(2)}) %collective-permute-start.24) | collective-permute-done | bytes 524320 | tf_op jit(solution)/shard_map/ppermute | solution.py:63
  91.2 1.1 add.152
  92.4 1.4 %collective-permute-start.25 = (f32[2,2,16,1024]{3,2,1,0:T(8,128)S(1)}, f32[2,2,16,1024]{3,2,1,0:T(8,128)S(1)}, u32[]{:S(2)}, u32[]{:S(2)}) collective-permute-start(f32[2,2,16,1024]{3,2,1,0:T(8,128)S(1)} %bitcast_select_fusion.2), channel_id=1, source_target_pairs={{0,2},{1,5},{2,0},{3,7},{4,6},{5,1},{6,4},{7,3},{8,10},{9,13},{10,... | collective-permute-start | bytes 786440 | tf_op jit(solution)/shard_map/ppermute | solution.py:84
  93.8 1.1 add.158
  94.9 0.8 collective-permute-start.29
  95.7 3.1 %collective-permute-done.25 = f32[2,2,16,1024]{3,2,1,0:T(8,128)S(1)} collective-permute-done((f32[2,2,16,1024]{3,2,1,0:T(8,128)S(1)}, f32[2,2,16,1024]{3,2,1,0:T(8,128)S(1)}, u32[]{:S(2)}, u32[]{:S(2)}) %collective-permute-start.25) | collective-permute-done | bytes 262176 | tf_op jit(solution)/shard_map/ppermute | solution.py:84
  98.9 2.0 %collective-permute-start.26 = (f32[2,16,1024]{2,1,0:T(8,128)S(1)}, f32[2,16,1024]{2,1,0:T(8,128)S(1)}, u32[]{:S(2)}, u32[]{:S(2)}) collective-permute-start(f32[2,16,1024]{2,1,0:T(8,128)S(1)} %dynamic-slice_bitcast_fusion.1), channel_id=1, source_target_pairs={{0,4},{1,3},{2,6},{3,1},{4,0},{5,7},{6,2},{7,5},{8,12},{9,11},{10,... | collective-permute-start | bytes 393224 | tf_op jit(solution)/shard_map/ppermute | solution.py:84
  100.9 1.4 %collective-permute-done.29 = f32[2,2,16,1024]{3,2,1,0:T(8,128)S(1)} collective-permute-done((f32[2,2,16,1024]{3,2,1,0:T(8,128)S(1)}, f32[2,2,16,1024]{3,2,1,0:T(8,128)S(1)}, u32[]{:S(2)}, u32[]{:S(2)}) %collective-permute-start.29) | collective-permute-done | bytes 262176 | tf_op jit(solution)/shard_map/ppermute | solution.py:84
  102.3 2.1 %collective-permute-start.30 = (f32[2,16,1024]{2,1,0:T(8,128)S(1)}, f32[2,16,1024]{2,1,0:T(8,128)S(1)}, u32[]{:S(2)}, u32[]{:S(2)}) collective-permute-start(f32[2,16,1024]{2,1,0:T(8,128)S(1)} %dynamic-slice_bitcast_fusion), channel_id=1, source_target_pairs={{0,4},{1,3},{2,6},{3,1},{4,0},{5,7},{6,2},{7,5},{8,12},{9,11},{10,... | collective-permute-start | bytes 393224 | tf_op jit(solution)/shard_map/ppermute | solution.py:84
  104.5 1.9 %collective-permute-start.27 = (f32[16,1024]{1,0:T(8,128)S(1)}, f32[16,1024]{1,0:T(8,128)S(1)}, u32[]{:S(2)}, u32[]{:S(2)}) collective-permute-start(f32[16,1024]{1,0:T(8,128)S(1)} %dynamic-slice_bitcast_fusion.5), channel_id=1, source_target_pairs={{0,8},{1,9},{2,10},{3,11},{4,12},{5,13},{6,14},{7,15},{8,0},{9,1},... | collective-permute-start | bytes 196616 | tf_op jit(solution)/shard_map/ppermute | solution.py:84
  106.4 1.7 %collective-permute-done.30 = f32[2,16,1024]{2,1,0:T(8,128)S(1)} collective-permute-done((f32[2,16,1024]{2,1,0:T(8,128)S(1)}, f32[2,16,1024]{2,1,0:T(8,128)S(1)}, u32[]{:S(2)}, u32[]{:S(2)}) %collective-permute-start.30) | collective-permute-done | bytes 131104 | tf_op jit(solution)/shard_map/ppermute | solution.py:84
  108.1 2.6 %collective-permute-start.31 = (f32[16,1024]{1,0:T(8,128)S(1)}, f32[16,1024]{1,0:T(8,128)S(1)}, u32[]{:S(2)}, u32[]{:S(2)}) collective-permute-start(f32[16,1024]{1,0:T(8,128)S(1)} %dynamic-slice_bitcast_fusion.4), channel_id=1, source_target_pairs={{0,8},{1,9},{2,10},{3,11},{4,12},{5,13},{6,14},{7,15},{8,0},{9,1},... | collective-permute-start | bytes 196616 | tf_op jit(solution)/shard_map/ppermute | solution.py:84
  110.7 1.3 %collective-permute-done.27 = f32[16,1024]{1,0:T(8,128)S(1)} collective-permute-done((f32[16,1024]{1,0:T(8,128)S(1)}, f32[16,1024]{1,0:T(8,128)S(1)}, u32[]{:S(2)}, u32[]{:S(2)}) %collective-permute-start.27) | collective-permute-done | bytes 65568 | tf_op jit(solution)/shard_map/ppermute | solution.py:84
  112.0 1.3 %collective-permute-done.31 = f32[16,1024]{1,0:T(8,128)S(1)} collective-permute-done((f32[16,1024]{1,0:T(8,128)S(1)}, f32[16,1024]{1,0:T(8,128)S(1)}, u32[]{:S(2)}, u32[]{:S(2)}) %collective-permute-start.31) | collective-permute-done | bytes 65568 | tf_op jit(solution)/shard_map/ppermute | solution.py:84
  113.4 0.8 copy.37
  (79 shorter events, 1.9 us)
Async XLA Ops:
  2.6 6.3 %collective-permute-start.3 = (bf16[1,16,1024]{2,1,0:T(8,128)(2,1)S(1)}, bf16[1,16,1024]{2,1,0:T(8,128)(2,1)S(1)}, u32[]{:S(2)}, u32[]{:S(2)}) collective-permute-start(bf16[1,16,1024]{2,1,0:T(8,128)(2,1)S(1)} %get-tuple-element.57), channel_id=1, source_target_pairs={{0,8},{1,9},{2,10},{3,11},{4,12},{5,13},{6,14},{7,15},{8,0},{9,1},... | collective-permute-start | bytes 98312 | tf_op jit(solution)/shard_map/ppermute | solution.py:36
  6.7 4.8 %collective-permute-start = (bf16[1,16,1024]{2,1,0:T(8,128)(2,1)S(1)}, bf16[1,16,1024]{2,1,0:T(8,128)(2,1)S(1)}, u32[]{:S(2)}, u32[]{:S(2)}) collective-permute-start(bf16[1,16,1024]{2,1,0:T(8,128)(2,1)S(1)} %get-tuple-element.58), channel_id=1, source_target_pairs={{0,8},{1,9},{2,10},{3,11},{4,12},{5,13},{6,14},{7,15},{8,0},{9,1},... | collective-permute-start | bytes 98312 | tf_op jit(solution)/shard_map/ppermute | solution.py:36
  9.0 4.3 %collective-permute-start.4 = (bf16[2,16,1024]{2,1,0:T(8,128)(2,1)S(1)}, bf16[2,16,1024]{2,1,0:T(8,128)(2,1)S(1)}, u32[]{:S(2)}, u32[]{:S(2)}) collective-permute-start(bf16[2,16,1024]{2,1,0:T(8,128)(2,1)S(1)} %pad_maximum_fusion.7), channel_id=1, source_target_pairs={{0,4},{1,3},{2,6},{3,1},{4,0},{5,7},{6,2},{7,5},{8,12},{9,11},{10,... | collective-permute-start | bytes 196616 | tf_op jit(solution)/shard_map/ppermute | solution.py:36
  11.6 4.8 %collective-permute-start.1 = (bf16[2,16,1024]{2,1,0:T(8,128)(2,1)S(1)}, bf16[2,16,1024]{2,1,0:T(8,128)(2,1)S(1)}, u32[]{:S(2)}, u32[]{:S(2)}) collective-permute-start(bf16[2,16,1024]{2,1,0:T(8,128)(2,1)S(1)} %pad_maximum_fusion.6), channel_id=1, source_target_pairs={{0,4},{1,3},{2,6},{3,1},{4,0},{5,7},{6,2},{7,5},{8,12},{9,11},{10,... | collective-permute-start | bytes 196616 | tf_op jit(solution)/shard_map/ppermute | solution.py:36
  13.4 5.0 %collective-permute-start.5 = (bf16[4,16,1024]{2,1,0:T(8,128)(2,1)S(1)}, bf16[4,16,1024]{2,1,0:T(8,128)(2,1)S(1)}, u32[]{:S(2)}, u32[]{:S(2)}) collective-permute-start(bf16[4,16,1024]{2,1,0:T(8,128)(2,1)S(1)} %bitcast.259), channel_id=1, source_target_pairs={{0,2},{1,5},{2,0},{3,7},{4,6},{5,1},{6,4},{7,3},{8,10},{9,13},{10,... | collective-permute-start | bytes 393224 | tf_op jit(solution)/shard_map/ppermute | solution.py:36
  16.4 5.0 %collective-permute-start.2 = (bf16[4,16,1024]{2,1,0:T(8,128)(2,1)S(1)}, bf16[4,16,1024]{2,1,0:T(8,128)(2,1)S(1)}, u32[]{:S(2)}, u32[]{:S(2)}) collective-permute-start(bf16[4,16,1024]{2,1,0:T(8,128)(2,1)S(1)} %bitcast.260), channel_id=1, source_target_pairs={{0,2},{1,5},{2,0},{3,7},{4,6},{5,1},{6,4},{7,3},{8,10},{9,13},{10,... | collective-permute-start | bytes 393224 | tf_op jit(solution)/shard_map/ppermute | solution.py:36
  18.5 5.1 %copy-start = (bf16[2,2,2,16,1024]{4,3,2,1,0:T(8,128)(2,1)}, bf16[2,2,2,16,1024]{4,3,2,1,0:T(8,128)(2,1)S(1)}, u32[]{:S(2)}) copy-start(bf16[2,2,2,16,1024]{4,3,2,1,0:T(8,128)(2,1)S(1)} %maximum_select_fusion.1) | copy-start | bytes 786436
  18.5 5.1 %collective-permute-start.7 = (bf16[128,1024]{1,0:T(8,128)(2,1)S(1)}, bf16[128,1024]{1,0:T(8,128)(2,1)S(1)}, u32[]{:S(2)}, u32[]{:S(2)}) collective-permute-start(bf16[128,1024]{1,0:T(8,128)(2,1)S(1)} %bitcast.251), channel_id=1, source_target_pairs={{0,1},{1,0},{2,3},{3,2},{4,5},{5,4},{6,7},{7,6},{8,9},{9,8},{10,11... | collective-permute-start | bytes 786440 | tf_op jit(solution)/shard_map/ppermute | solution.py:53
  21.6 2.1 %copy-start.2 = (bf16[2,2,2,16,1024]{4,3,2,1,0:T(8,128)(2,1)}, bf16[2,2,2,16,1024]{4,3,2,1,0:T(8,128)(2,1)S(1)}, u32[]{:S(2)}) copy-start(bf16[2,2,2,16,1024]{4,3,2,1,0:T(8,128)(2,1)S(1)} %maximum_select_fusion) | copy-start | bytes 786436
  21.6 2.0 %collective-permute-start.6 = (bf16[128,1024]{1,0:T(8,128)(2,1)S(1)}, bf16[128,1024]{1,0:T(8,128)(2,1)S(1)}, u32[]{:S(2)}, u32[]{:S(2)}) collective-permute-start(bf16[128,1024]{1,0:T(8,128)(2,1)S(1)} %bitcast.255), channel_id=1, source_target_pairs={{0,1},{1,0},{2,3},{3,2},{4,5},{5,4},{6,7},{7,6},{8,9},{9,8},{10,11... | collective-permute-start | bytes 786440 | tf_op jit(solution)/shard_map/ppermute | solution.py:53
  23.6 0.7 copy-start.4
  23.6 0.8 copy-start.6
  24.4 34.4 %copy-start.8 = (f32[1024]{0:T(1024)S(1)}, f32[1024]{0:T(1024)}, u32[]{:S(2)}) copy-start(f32[1024]{0:T(1024)} %param.7) | copy-start | bytes 12292
  33.9 2.2 %collective-permute-start.8 = (f32[128,1024]{1,0:T(8,128)}, f32[128,1024]{1,0:T(8,128)S(1)}, u32[]{:S(2)}, u32[]{:S(2)}) collective-permute-start(f32[128,1024]{1,0:T(8,128)} %get-tuple-element.14), channel_id=1, source_target_pairs={{0,1},{1,0},{2,3},{3,2},{4,5},{5,4},{6,7},{7,6},{8,9},{9,8},{10,11... | collective-permute-start | bytes 1572872 | tf_op jit(solution)/shard_map/ppermute | solution.py:63
  34.4 4.0 %collective-permute-start.15 = (f32[128,1024]{1,0:T(8,128)}, f32[128,1024]{1,0:T(8,128)S(1)}, u32[]{:S(2)}, u32[]{:S(2)}) collective-permute-start(f32[128,1024]{1,0:T(8,128)} %get-tuple-element.16), channel_id=1, source_target_pairs={{0,1},{1,0},{2,3},{3,2},{4,5},{5,4},{6,7},{7,6},{8,9},{9,8},{10,11... | collective-permute-start | bytes 1572872 | tf_op jit(solution)/shard_map/ppermute | solution.py:63
  37.3 6.4 %collective-permute-start.9 = (f32[2,2,16,1024]{3,2,1,0:T(8,128)S(1)}, f32[2,2,16,1024]{3,2,1,0:T(8,128)S(1)}, u32[]{:S(2)}, u32[]{:S(2)}) collective-permute-start(f32[2,2,16,1024]{3,2,1,0:T(8,128)S(1)} %bitcast_select_fusion.6), channel_id=1, source_target_pairs={{0,2},{1,5},{2,0},{3,7},{4,6},{5,1},{6,4},{7,3},{8,10},{9,13},{10,... | collective-permute-start | bytes 786440 | tf_op jit(solution)/shard_map/ppermute | solution.py:84
  39.5 7.5 %collective-permute-start.16 = (f32[2,2,16,1024]{3,2,1,0:T(8,128)S(1)}, f32[2,2,16,1024]{3,2,1,0:T(8,128)S(1)}, u32[]{:S(2)}, u32[]{:S(2)}) collective-permute-start(f32[2,2,16,1024]{3,2,1,0:T(8,128)S(1)} %bitcast_select_fusion.4), channel_id=1, source_target_pairs={{0,2},{1,5},{2,0},{3,7},{4,6},{5,1},{6,4},{7,3},{8,10},{9,13},{10,... | collective-permute-start | bytes 786440 | tf_op jit(solution)/shard_map/ppermute | solution.py:84
  43.8 5.0 %collective-permute-start.10 = (f32[2,16,1024]{2,1,0:T(8,128)S(1)}, f32[2,16,1024]{2,1,0:T(8,128)S(1)}, u32[]{:S(2)}, u32[]{:S(2)}) collective-permute-start(f32[2,16,1024]{2,1,0:T(8,128)S(1)} %dynamic-slice_bitcast_fusion.3), channel_id=1, source_target_pairs={{0,4},{1,3},{2,6},{3,1},{4,0},{5,7},{6,2},{7,5},{8,12},{9,11},{10,... | collective-permute-start | bytes 393224 | tf_op jit(solution)/shard_map/ppermute | solution.py:84
  47.1 5.7 %collective-permute-start.17 = (f32[2,16,1024]{2,1,0:T(8,128)S(1)}, f32[2,16,1024]{2,1,0:T(8,128)S(1)}, u32[]{:S(2)}, u32[]{:S(2)}) collective-permute-start(f32[2,16,1024]{2,1,0:T(8,128)S(1)} %dynamic-slice_bitcast_fusion.2), channel_id=1, source_target_pairs={{0,4},{1,3},{2,6},{3,1},{4,0},{5,7},{6,2},{7,5},{8,12},{9,11},{10,... | collective-permute-start | bytes 393224 | tf_op jit(solution)/shard_map/ppermute | solution.py:84
  48.9 6.3 %collective-permute-start.11 = (f32[16,1024]{1,0:T(8,128)S(1)}, f32[16,1024]{1,0:T(8,128)S(1)}, u32[]{:S(2)}, u32[]{:S(2)}) collective-permute-start(f32[16,1024]{1,0:T(8,128)S(1)} %dynamic-slice_bitcast_fusion.7), channel_id=1, source_target_pairs={{0,8},{1,9},{2,10},{3,11},{4,12},{5,13},{6,14},{7,15},{8,0},{9,1},... | collective-permute-start | bytes 196616 | tf_op jit(solution)/shard_map/ppermute | solution.py:84
  52.9 5.9 %collective-permute-start.18 = (f32[16,1024]{1,0:T(8,128)S(1)}, f32[16,1024]{1,0:T(8,128)S(1)}, u32[]{:S(2)}, u32[]{:S(2)}) collective-permute-start(f32[16,1024]{1,0:T(8,128)S(1)} %dynamic-slice_bitcast_fusion.6), channel_id=1, source_target_pairs={{0,8},{1,9},{2,10},{3,11},{4,12},{5,13},{6,14},{7,15},{8,0},{9,1},... | collective-permute-start | bytes 196616 | tf_op jit(solution)/shard_map/ppermute | solution.py:84
  58.9 5.2 %collective-permute-start.19 = (bf16[1,16,1024]{2,1,0:T(8,128)(2,1)S(1)}, bf16[1,16,1024]{2,1,0:T(8,128)(2,1)S(1)}, u32[]{:S(2)}, u32[]{:S(2)}) collective-permute-start(bf16[1,16,1024]{2,1,0:T(8,128)(2,1)S(1)} %get-tuple-element.21), channel_id=1, source_target_pairs={{0,8},{1,9},{2,10},{3,11},{4,12},{5,13},{6,14},{7,15},{8,0},{9,1},... | collective-permute-start | bytes 98312 | tf_op jit(solution)/shard_map/ppermute | solution.py:36
  60.6 4.8 %collective-permute-start.12 = (bf16[1,16,1024]{2,1,0:T(8,128)(2,1)S(1)}, bf16[1,16,1024]{2,1,0:T(8,128)(2,1)S(1)}, u32[]{:S(2)}, u32[]{:S(2)}) collective-permute-start(bf16[1,16,1024]{2,1,0:T(8,128)(2,1)S(1)} %get-tuple-element.55), channel_id=1, source_target_pairs={{0,8},{1,9},{2,10},{3,11},{4,12},{5,13},{6,14},{7,15},{8,0},{9,1},... | collective-permute-start | bytes 98312 | tf_op jit(solution)/shard_map/ppermute | solution.py:36
  64.2 4.9 %collective-permute-start.20 = (bf16[2,16,1024]{2,1,0:T(8,128)(2,1)S(1)}, bf16[2,16,1024]{2,1,0:T(8,128)(2,1)S(1)}, u32[]{:S(2)}, u32[]{:S(2)}) collective-permute-start(bf16[2,16,1024]{2,1,0:T(8,128)(2,1)S(1)} %pad_maximum_fusion.9), channel_id=1, source_target_pairs={{0,4},{1,3},{2,6},{3,1},{4,0},{5,7},{6,2},{7,5},{8,12},{9,11},{10,... | collective-permute-start | bytes 196616 | tf_op jit(solution)/shard_map/ppermute | solution.py:36
  65.4 5.1 %collective-permute-start.13 = (bf16[2,16,1024]{2,1,0:T(8,128)(2,1)S(1)}, bf16[2,16,1024]{2,1,0:T(8,128)(2,1)S(1)}, u32[]{:S(2)}, u32[]{:S(2)}) collective-permute-start(bf16[2,16,1024]{2,1,0:T(8,128)(2,1)S(1)} %pad_maximum_fusion.8), channel_id=1, source_target_pairs={{0,4},{1,3},{2,6},{3,1},{4,0},{5,7},{6,2},{7,5},{8,12},{9,11},{10,... | collective-permute-start | bytes 196616 | tf_op jit(solution)/shard_map/ppermute | solution.py:36
  70.6 5.0 %collective-permute-start.21 = (bf16[4,16,1024]{2,1,0:T(8,128)(2,1)S(1)}, bf16[4,16,1024]{2,1,0:T(8,128)(2,1)S(1)}, u32[]{:S(2)}, u32[]{:S(2)}) collective-permute-start(bf16[4,16,1024]{2,1,0:T(8,128)(2,1)S(1)} %bitcast.262), channel_id=1, source_target_pairs={{0,2},{1,5},{2,0},{3,7},{4,6},{5,1},{6,4},{7,3},{8,10},{9,13},{10,... | collective-permute-start | bytes 393224 | tf_op jit(solution)/shard_map/ppermute | solution.py:36
  72.2 5.0 %collective-permute-start.14 = (bf16[4,16,1024]{2,1,0:T(8,128)(2,1)S(1)}, bf16[4,16,1024]{2,1,0:T(8,128)(2,1)S(1)}, u32[]{:S(2)}, u32[]{:S(2)}) collective-permute-start(bf16[4,16,1024]{2,1,0:T(8,128)(2,1)S(1)} %bitcast.261), channel_id=1, source_target_pairs={{0,2},{1,5},{2,0},{3,7},{4,6},{5,1},{6,4},{7,3},{8,10},{9,13},{10,... | collective-permute-start | bytes 393224 | tf_op jit(solution)/shard_map/ppermute | solution.py:36
  75.7 3.2 %copy-start.1 = (bf16[2,2,2,16,1024]{4,3,2,1,0:T(8,128)(2,1)}, bf16[2,2,2,16,1024]{4,3,2,1,0:T(8,128)(2,1)S(1)}, u32[]{:S(2)}) copy-start(bf16[2,2,2,16,1024]{4,3,2,1,0:T(8,128)(2,1)S(1)} %maximum_select_fusion.3) | copy-start | bytes 786436
  75.7 1.6 %collective-permute-start.23 = (bf16[128,1024]{1,0:T(8,128)(2,1)S(1)}, bf16[128,1024]{1,0:T(8,128)(2,1)S(1)}, u32[]{:S(2)}, u32[]{:S(2)}) collective-permute-start(bf16[128,1024]{1,0:T(8,128)(2,1)S(1)} %bitcast.253), channel_id=1, source_target_pairs={{0,1},{1,0},{2,3},{3,2},{4,5},{5,4},{6,7},{7,6},{8,9},{9,8},{10,11... | collective-permute-start | bytes 786440 | tf_op jit(solution)/shard_map/ppermute | solution.py:53
  77.3 1.6 %copy-start.3 = (bf16[2,2,2,16,1024]{4,3,2,1,0:T(8,128)(2,1)}, bf16[2,2,2,16,1024]{4,3,2,1,0:T(8,128)(2,1)S(1)}, u32[]{:S(2)}) copy-start(bf16[2,2,2,16,1024]{4,3,2,1,0:T(8,128)(2,1)S(1)} %maximum_select_fusion.2) | copy-start | bytes 786436
  77.3 1.6 %collective-permute-start.22 = (bf16[128,1024]{1,0:T(8,128)(2,1)S(1)}, bf16[128,1024]{1,0:T(8,128)(2,1)S(1)}, u32[]{:S(2)}, u32[]{:S(2)}) collective-permute-start(bf16[128,1024]{1,0:T(8,128)(2,1)S(1)} %bitcast.257), channel_id=1, source_target_pairs={{0,1},{1,0},{2,3},{3,2},{4,5},{5,4},{6,7},{7,6},{8,9},{9,8},{10,11... | collective-permute-start | bytes 786440 | tf_op jit(solution)/shard_map/ppermute | solution.py:53
  77.4 1.5 %copy-start.5 = (bf16[128,1024]{1,0:T(8,128)(2,1)}, bf16[128,1024]{1,0:T(8,128)(2,1)S(1)}, u32[]{:S(2)}) copy-start(bf16[128,1024]{1,0:T(8,128)(2,1)S(1)} %collective-permute-done.23.refs_3_) | copy-start | bytes 786436
  78.9 0.7 copy-start.7
  89.1 2.1 %collective-permute-start.24 = (f32[128,1024]{1,0:T(8,128)}, f32[128,1024]{1,0:T(8,128)S(1)}, u32[]{:S(2)}, u32[]{:S(2)}) collective-permute-start(f32[128,1024]{1,0:T(8,128)} %get-tuple-element.18), channel_id=1, source_target_pairs={{0,1},{1,0},{2,3},{3,2},{4,5},{5,4},{6,7},{7,6},{8,9},{9,8},{10,11... | collective-permute-start | bytes 1572872 | tf_op jit(solution)/shard_map/ppermute | solution.py:63
  89.3 4.5 %collective-permute-start.28 = (f32[128,1024]{1,0:T(8,128)}, f32[128,1024]{1,0:T(8,128)S(1)}, u32[]{:S(2)}, u32[]{:S(2)}) collective-permute-start(f32[128,1024]{1,0:T(8,128)} %get-tuple-element.20), channel_id=1, source_target_pairs={{0,1},{1,0},{2,3},{3,2},{4,5},{5,4},{6,7},{7,6},{8,9},{9,8},{10,11... | collective-permute-start | bytes 1572872 | tf_op jit(solution)/shard_map/ppermute | solution.py:63
  92.4 6.4 %collective-permute-start.25 = (f32[2,2,16,1024]{3,2,1,0:T(8,128)S(1)}, f32[2,2,16,1024]{3,2,1,0:T(8,128)S(1)}, u32[]{:S(2)}, u32[]{:S(2)}) collective-permute-start(f32[2,2,16,1024]{3,2,1,0:T(8,128)S(1)} %bitcast_select_fusion.2), channel_id=1, source_target_pairs={{0,2},{1,5},{2,0},{3,7},{4,6},{5,1},{6,4},{7,3},{8,10},{9,13},{10,... | collective-permute-start | bytes 786440 | tf_op jit(solution)/shard_map/ppermute | solution.py:84
  94.9 7.3 %collective-permute-start.29 = (f32[2,2,16,1024]{3,2,1,0:T(8,128)S(1)}, f32[2,2,16,1024]{3,2,1,0:T(8,128)S(1)}, u32[]{:S(2)}, u32[]{:S(2)}) collective-permute-start(f32[2,2,16,1024]{3,2,1,0:T(8,128)S(1)} %bitcast_select_fusion), channel_id=1, source_target_pairs={{0,2},{1,5},{2,0},{3,7},{4,6},{5,1},{6,4},{7,3},{8,10},{9,13},{10,... | collective-permute-start | bytes 786440 | tf_op jit(solution)/shard_map/ppermute | solution.py:84
  98.9 5.5 %collective-permute-start.26 = (f32[2,16,1024]{2,1,0:T(8,128)S(1)}, f32[2,16,1024]{2,1,0:T(8,128)S(1)}, u32[]{:S(2)}, u32[]{:S(2)}) collective-permute-start(f32[2,16,1024]{2,1,0:T(8,128)S(1)} %dynamic-slice_bitcast_fusion.1), channel_id=1, source_target_pairs={{0,4},{1,3},{2,6},{3,1},{4,0},{5,7},{6,2},{7,5},{8,12},{9,11},{10,... | collective-permute-start | bytes 393224 | tf_op jit(solution)/shard_map/ppermute | solution.py:84
  102.3 5.8 %collective-permute-start.30 = (f32[2,16,1024]{2,1,0:T(8,128)S(1)}, f32[2,16,1024]{2,1,0:T(8,128)S(1)}, u32[]{:S(2)}, u32[]{:S(2)}) collective-permute-start(f32[2,16,1024]{2,1,0:T(8,128)S(1)} %dynamic-slice_bitcast_fusion), channel_id=1, source_target_pairs={{0,4},{1,3},{2,6},{3,1},{4,0},{5,7},{6,2},{7,5},{8,12},{9,11},{10,... | collective-permute-start | bytes 393224 | tf_op jit(solution)/shard_map/ppermute | solution.py:84
  104.5 7.6 %collective-permute-start.27 = (f32[16,1024]{1,0:T(8,128)S(1)}, f32[16,1024]{1,0:T(8,128)S(1)}, u32[]{:S(2)}, u32[]{:S(2)}) collective-permute-start(f32[16,1024]{1,0:T(8,128)S(1)} %dynamic-slice_bitcast_fusion.5), channel_id=1, source_target_pairs={{0,8},{1,9},{2,10},{3,11},{4,12},{5,13},{6,14},{7,15},{8,0},{9,1},... | collective-permute-start | bytes 196616 | tf_op jit(solution)/shard_map/ppermute | solution.py:84
  108.1 5.2 %collective-permute-start.31 = (f32[16,1024]{1,0:T(8,128)S(1)}, f32[16,1024]{1,0:T(8,128)S(1)}, u32[]{:S(2)}, u32[]{:S(2)}) collective-permute-start(f32[16,1024]{1,0:T(8,128)S(1)} %dynamic-slice_bitcast_fusion.4), channel_id=1, source_target_pairs={{0,8},{1,9},{2,10},{3,11},{4,12},{5,13},{6,14},{7,15},{8,0},{9,1},... | collective-permute-start | bytes 196616 | tf_op jit(solution)/shard_map/ppermute | solution.py:84

commit v15 on v14

--- a/solution.py
+++ b/solution.py
@@ -91,12 +91,20 @@
     mine, theirs = refs[:states], refs[states:2 * states]
     vir_ref = refs[2 * states]
     keep, send = refs[2 * states + 1:3 * states + 1], refs[3 * states + 1:4 * states + 1]
-    r_ref = refs[4 * states + 1]
+    r_ref, occ_buf = refs[4 * states + 1], refs[4 * states + 2]
     split = mine[0].shape[0]
     nvir = vir_ref.shape[1]
 
     @pl.when(pl.program_id(0) == 0)
     def _():
+        if rows:
+            core = core_ref[0]
+            for p in range(occ_ref.shape[0]):
+                for b in range(split // rows):
+                    at_mine = pl.multiple_of((2 * b + core) * rows, rows)
+                    at_theirs = pl.multiple_of((2 * b + 1 - core) * rows, rows)
+                    occ_buf[p, b * rows:(b + 1) * rows] = occ_ref[p, pl.ds(at_mine, rows)]
+                    occ_buf[p, split + b * rows:split + (b + 1) * rows] = occ_ref[p, pl.ds(at_theirs, rows)]
         for s in range(states):
             cols = slice(s * nvir, (s + 1) * nvir)
             keep[s][...] = jnp.zeros_like(keep[s])
@@ -112,7 +120,8 @@
                 r_ref[:split, cols] = mine[s][...]
                 r_ref[split:, cols] = theirs[s][...]
 
-    half = jnp.dot(occ_ref[0], r_ref[...], preferred_element_type=jnp.float32).astype(jnp.bfloat16)
+    occ = occ_buf[pl.program_id(0)] if rows else occ_ref[pl.program_id(0)]
+    half = jnp.dot(occ, r_ref[...], preferred_element_type=jnp.float32).astype(jnp.bfloat16)
     vir = vir_ref[0]
     for s in range(states):
         term = lax.dot_general(
@@ -131,12 +140,15 @@
     results = pl.pallas_call(
         functools.partial(exchange_kernel, states, rows),
         grid=(local_aux,),
-        in_specs=[pl.BlockSpec(memory_space=pltpu.SMEM), pl.BlockSpec((1, nocc, nocc), lambda p: (p, 0, 0))]
+        in_specs=[pl.BlockSpec(memory_space=pltpu.SMEM), pl.BlockSpec((local_aux, nocc, nocc), lambda p: (0, 0, 0))]
         + [piece] * (2 * states)
         + [pl.BlockSpec((1, nvir, nvir), lambda p: (p, 0, 0))],
         out_specs=[piece] * (2 * states),
         out_shape=[out] * (2 * states),
-        scratch_shapes=[pltpu.VMEM((nocc, states * nvir), jnp.bfloat16)],
+        scratch_shapes=[
+            pltpu.VMEM((nocc, states * nvir), jnp.bfloat16),
+            pltpu.VMEM((local_aux, nocc, nocc) if rows else (1, 8, 128), jnp.bfloat16),
+        ],
         compiler_params=pltpu.CompilerParams(dimension_semantics=("arbitrary",)),
     )(core, occ_ints, *mine, *theirs, vir_ints)
     return results[:states], results[states:]
@@ -174,9 +186,9 @@
     my_occ = lax.dynamic_slice_in_dim(occ_energy, position * own_rows, own_rows, 0)
     denom = vir_energy[None, None, :] - my_occ[:, None, None]
     rows = own_rows if own_rows % 16 == 0 else 0
-    ordered_occ = order_rows(occ_ints, n, position & 1)
+    ordered_occ = occ_ints
     if not rows:
-        ordered_occ = order_columns(ordered_occ, n, position & 1)
+        ordered_occ = order_columns(order_rows(occ_ints, n, position & 1), n, position & 1)
     core = (position & 1).astype(jnp.int32).reshape(1)
     own_denom = denom[:, 0, :]
     resps = [rhs[:, state, :] / own_denom for state in range(states)]

time: 115 us -> 115 us (level)
  waiting for transfers between devices: 42.2 us -> 45.5 us
  other arithmetic: 8.23 us -> 6.29 us
  starting transfers between devices: 40 us -> 38.6 us
    ppermute x12, waiting for transfers between devices: 19 us -> 20.8 us  [scatter_sum(): acc = kept + lax.ppermute(sent, 'aux', partners(n, b0, b1))]
    ppermute x4, waiting for transfers between devices: 1.51 us -> 3.01 us  [gather_rows(): return (flat, lax.ppermute(flat, 'aux', partners(n, 0, 0)))]
    ppermute x12, starting transfers between devices: 20.6 us -> 19.2 us  [scatter_sum(): acc = kept + lax.ppermute(sent, 'aux', partners(n, b0, b1))]
  transfers between devices with their start and end apart: 32 -> 32, of which waited for: 25 -> 26; matrix products, arithmetic and copies ran while one was open for 6% -> 5% of each run, Pallas kernels for 0% -> 0%
where the time goes in v15:
time: 115 us; the launch traced here: 114 us
  waiting for transfers between devices  45.5 us (40%)
  starting transfers between devices  38.6 us (34%)
  Pallas kernels  19.2 us (17%)
  other arithmetic  6.29 us (5%)
  local copies, waits for them, and re-layouts  4.16 us (4%)
    ppermute x12, waiting for transfers between devices, scatter_sum(): acc = kept + lax.ppermute(sent, 'aux', partners(n, b0, b1))  20.8 us
    ppermute x12, starting transfers between devices, scatter_sum(): acc = kept + lax.ppermute(sent, 'aux', partners(n, b0, b1))  19.2 us
    pallas_call x2, Pallas kernels, exchange_part(): pl.pallas_call(functools.partial(exchange_kernel, states, rows), grid=(lo...  19.2 us
    ppermute x12, waiting for transfers between devices, gather_rows(): theirs = lax.ppermute(acc, 'aux', partners(n, b0, b1))  18.5 us
    ppermute x12, starting transfers between devices, gather_rows(): theirs = lax.ppermute(acc, 'aux', partners(n, b0, b1))  18.1 us
    add x4, other arithmetic, scatter_sum(): keep.reshape(shape)  4.44 us
    ppermute x4, waiting for transfers between devices, scatter_sum(): lax.ppermute(send, 'aux', partners(n, 0, 0)).reshape(shape)  3.23 us
    ppermute x4, waiting for transfers between devices, gather_rows(): return (flat, lax.ppermute(flat, 'aux', partners(n, 0, 0)))  3.01 us
  transfers between devices with their start and end apart: 32, of which 26 were waited for; matrix products, arithmetic and copies ran while one was open for 5% of the time, Pallas kernels for 0%

profile of v15, /device:TPU:0, one launch (start us, length us, event | category | flops | bytes accessed | tf_op | source)
XLA Modules:
  0.0 114.1 jit_solution(8101812320765557997)
XLA Ops:
  0.0 1.1 fusion.24
  1.1 0.8 dynamic_slice.103
  1.9 0.8 fusion.5
  2.6 4.1 %collective-permute-start.3 = (bf16[1,16,1024]{2,1,0:T(8,128)(2,1)S(1)}, bf16[1,16,1024]{2,1,0:T(8,128)(2,1)S(1)}, u32[]{:S(2)}, u32[]{:S(2)}) collective-permute-start(bf16[1,16,1024]{2,1,0:T(8,128)(2,1)S(1)} %get-tuple-element.55), channel_id=1, source_target_pairs={{0,8},{1,9},{2,10},{3,11},{4,12},{5,13},{6,14},{7,15},{8,0},{9,1},... | collective-permute-start | bytes 98312 | tf_op jit(solution)/shard_map/ppermute | solution.py:36
  6.8 2.2 %collective-permute-done.3 = bf16[1,16,1024]{2,1,0:T(8,128)(2,1)S(1)} collective-permute-done((bf16[1,16,1024]{2,1,0:T(8,128)(2,1)S(1)}, bf16[1,16,1024]{2,1,0:T(8,128)(2,1)S(1)}, u32[]{:S(2)}, u32[]{:S(2)}) %collective-permute-start.3) | collective-permute-done | bytes 32800 | tf_op jit(solution)/shard_map/ppermute | solution.py:36
  9.0 1.7 %collective-permute-start.4 = (bf16[2,16,1024]{2,1,0:T(8,128)(2,1)S(1)}, bf16[2,16,1024]{2,1,0:T(8,128)(2,1)S(1)}, u32[]{:S(2)}, u32[]{:S(2)}) collective-permute-start(bf16[2,16,1024]{2,1,0:T(8,128)(2,1)S(1)} %pad_maximum_fusion.6), channel_id=1, source_target_pairs={{0,4},{1,3},{2,6},{3,1},{4,0},{5,7},{6,2},{7,5},{8,12},{9,11},{10,... | collective-permute-start | bytes 196616 | tf_op jit(solution)/shard_map/ppermute | solution.py:36
  10.7 0.9 collective-permute-done
  11.6 1.6 %collective-permute-start.1 = (bf16[2,16,1024]{2,1,0:T(8,128)(2,1)S(1)}, bf16[2,16,1024]{2,1,0:T(8,128)(2,1)S(1)}, u32[]{:S(2)}, u32[]{:S(2)}) collective-permute-start(bf16[2,16,1024]{2,1,0:T(8,128)(2,1)S(1)} %pad_maximum_fusion.5), channel_id=1, source_target_pairs={{0,4},{1,3},{2,6},{3,1},{4,0},{5,7},{6,2},{7,5},{8,12},{9,11},{10,... | collective-permute-start | bytes 196616 | tf_op jit(solution)/shard_map/ppermute | solution.py:36
  13.4 1.8 %collective-permute-start.5 = (bf16[4,16,1024]{2,1,0:T(8,128)(2,1)S(1)}, bf16[4,16,1024]{2,1,0:T(8,128)(2,1)S(1)}, u32[]{:S(2)}, u32[]{:S(2)}) collective-permute-start(bf16[4,16,1024]{2,1,0:T(8,128)(2,1)S(1)} %bitcast.237), channel_id=1, source_target_pairs={{0,2},{1,5},{2,0},{3,7},{4,6},{5,1},{6,4},{7,3},{8,10},{9,13},{10,... | collective-permute-start | bytes 393224 | tf_op jit(solution)/shard_map/ppermute | solution.py:36
  15.2 1.2 %collective-permute-done.1 = bf16[2,16,1024]{2,1,0:T(8,128)(2,1)S(1)} collective-permute-done((bf16[2,16,1024]{2,1,0:T(8,128)(2,1)S(1)}, bf16[2,16,1024]{2,1,0:T(8,128)(2,1)S(1)}, u32[]{:S(2)}, u32[]{:S(2)}) %collective-permute-start.1) | collective-permute-done | bytes 65568 | tf_op jit(solution)/shard_map/ppermute | solution.py:36
  16.4 1.1 collective-permute-start.2
  17.5 0.9 collective-permute-done.5
  18.6 2.9 %collective-permute-done.2 = bf16[4,16,1024]{2,1,0:T(8,128)(2,1)S(1)} collective-permute-done((bf16[4,16,1024]{2,1,0:T(8,128)(2,1)S(1)}, bf16[4,16,1024]{2,1,0:T(8,128)(2,1)S(1)}, u32[]{:S(2)}, u32[]{:S(2)}) %collective-permute-start.2) | collective-permute-done | bytes 131104 | tf_op jit(solution)/shard_map/ppermute | solution.py:36
  21.7 1.5 %collective-permute-done.6.refs_2_ = bf16[128,1024]{1,0:T(8,128)(2,1)S(1)} collective-permute-done((bf16[128,1024]{1,0:T(8,128)(2,1)S(1)}, bf16[128,1024]{1,0:T(8,128)(2,1)S(1)}, u32[]{:S(2)}, u32[]{:S(2)}) %collective-permute-start.6) | collective-permute-done | bytes 262176 | tf_op jit(solution)/shard_map/ppermute | solution.py:53
  23.2 0.7 copy-done.7
  23.9 9.6 %shard_map.55 = (f32[128,1024]{1,0:T(8,128)}, f32[128,1024]{1,0:T(8,128)}, f32[128,1024]{1,0:T(8,128)}, f32[128,1024]{1,0:T(8,128)}) custom-call(s32[1]{0:T(128)} %bitcast.1.core_ref, bf16[4,256,256]{2,1,0:T(8,128)(2,1)} %occ_ref.3, bf16[128,1024]{1,0:T(8,128)(2,1)} %bitcast.236, bf16[128,1024]{1,0:T(8,128)(2,1)} %bitcast.232, bf16[128,1024]{1,0:T(8,128)(2,1)} %copy-done.7, ...), custom_call_target="tpu_custom_call" | custom-call | tf_op jit(solution)/shard_map/pallas_call | solution.py:140
  33.5 0.1 collective-permute-start.8
  33.6 0.4 collective-permute-start.15
  34.0 1.6 %collective-permute-done.8 = f32[128,1024]{1,0:T(8,128)S(1)} collective-permute-done((f32[128,1024]{1,0:T(8,128)}, f32[128,1024]{1,0:T(8,128)S(1)}, u32[]{:S(2)}, u32[]{:S(2)}) %collective-permute-start.8) | collective-permute-done | bytes 524320 | tf_op jit(solution)/shard_map/ppermute | solution.py:63
  35.6 1.1 add.132
  36.7 1.1 collective-permute-start.9
  37.8 1.1 add.146
  38.9 1.1 collective-permute-start.16
  40.0 3.1 %collective-permute-done.9 = f32[2,2,16,1024]{3,2,1,0:T(8,128)S(1)} collective-permute-done((f32[2,2,16,1024]{3,2,1,0:T(8,128)S(1)}, f32[2,2,16,1024]{3,2,1,0:T(8,128)S(1)}, u32[]{:S(2)}, u32[]{:S(2)}) %collective-permute-start.9) | collective-permute-done | bytes 262176 | tf_op jit(solution)/shard_map/ppermute | solution.py:84
  43.2 1.3 %collective-permute-start.10 = (f32[2,16,1024]{2,1,0:T(8,128)S(1)}, f32[2,16,1024]{2,1,0:T(8,128)S(1)}, u32[]{:S(2)}, u32[]{:S(2)}) collective-permute-start(f32[2,16,1024]{2,1,0:T(8,128)S(1)} %dynamic-slice_bitcast_fusion.3), channel_id=1, source_target_pairs={{0,4},{1,3},{2,6},{3,1},{4,0},{5,7},{6,2},{7,5},{8,12},{9,11},{10,... | collective-permute-start | bytes 393224 | tf_op jit(solution)/shard_map/ppermute | solution.py:84
  44.6 2.1 %collective-permute-done.16 = f32[2,2,16,1024]{3,2,1,0:T(8,128)S(1)} collective-permute-done((f32[2,2,16,1024]{3,2,1,0:T(8,128)S(1)}, f32[2,2,16,1024]{3,2,1,0:T(8,128)S(1)}, u32[]{:S(2)}, u32[]{:S(2)}) %collective-permute-start.16) | collective-permute-done | bytes 262176 | tf_op jit(solution)/shard_map/ppermute | solution.py:84
  46.8 1.3 %collective-permute-start.17 = (f32[2,16,1024]{2,1,0:T(8,128)S(1)}, f32[2,16,1024]{2,1,0:T(8,128)S(1)}, u32[]{:S(2)}, u32[]{:S(2)}) collective-permute-start(f32[2,16,1024]{2,1,0:T(8,128)S(1)} %dynamic-slice_bitcast_fusion.2), channel_id=1, source_target_pairs={{0,4},{1,3},{2,6},{3,1},{4,0},{5,7},{6,2},{7,5},{8,12},{9,11},{10,... | collective-permute-start | bytes 393224 | tf_op jit(solution)/shard_map/ppermute | solution.py:84
  48.1 0.2 collective-permute-done.10
  48.3 2.8 %collective-permute-start.11 = (f32[16,1024]{1,0:T(8,128)S(1)}, f32[16,1024]{1,0:T(8,128)S(1)}, u32[]{:S(2)}, u32[]{:S(2)}) collective-permute-start(f32[16,1024]{1,0:T(8,128)S(1)} %dynamic-slice_bitcast_fusion.7), channel_id=1, source_target_pairs={{0,8},{1,9},{2,10},{3,11},{4,12},{5,13},{6,14},{7,15},{8,0},{9,1},... | collective-permute-start | bytes 196616 | tf_op jit(solution)/shard_map/ppermute | solution.py:84
  51.1 1.4 %collective-permute-done.17 = f32[2,16,1024]{2,1,0:T(8,128)S(1)} collective-permute-done((f32[2,16,1024]{2,1,0:T(8,128)S(1)}, f32[2,16,1024]{2,1,0:T(8,128)S(1)}, u32[]{:S(2)}, u32[]{:S(2)}) %collective-permute-start.17) | collective-permute-done | bytes 131104 | tf_op jit(solution)/shard_map/ppermute | solution.py:84
  52.5 2.1 %collective-permute-start.18 = (f32[16,1024]{1,0:T(8,128)S(1)}, f32[16,1024]{1,0:T(8,128)S(1)}, u32[]{:S(2)}, u32[]{:S(2)}) collective-permute-start(f32[16,1024]{1,0:T(8,128)S(1)} %dynamic-slice_bitcast_fusion.6), channel_id=1, source_target_pairs={{0,8},{1,9},{2,10},{3,11},{4,12},{5,13},{6,14},{7,15},{8,0},{9,1},... | collective-permute-start | bytes 196616 | tf_op jit(solution)/shard_map/ppermute | solution.py:84
  54.7 3.8 %collective-permute-done.18 = f32[16,1024]{1,0:T(8,128)S(1)} collective-permute-done((f32[16,1024]{1,0:T(8,128)S(1)}, f32[16,1024]{1,0:T(8,128)S(1)}, u32[]{:S(2)}, u32[]{:S(2)}) %collective-permute-start.18) | collective-permute-done | bytes 65568 | tf_op jit(solution)/shard_map/ppermute | solution.py:84
  58.6 1.5 %collective-permute-start.19 = (bf16[1,16,1024]{2,1,0:T(8,128)(2,1)S(1)}, bf16[1,16,1024]{2,1,0:T(8,128)(2,1)S(1)}, u32[]{:S(2)}, u32[]{:S(2)}) collective-permute-start(bf16[1,16,1024]{2,1,0:T(8,128)(2,1)S(1)} %get-tuple-element.21), channel_id=1, source_target_pairs={{0,8},{1,9},{2,10},{3,11},{4,12},{5,13},{6,14},{7,15},{8,0},{9,1},... | collective-permute-start | bytes 98312 | tf_op jit(solution)/shard_map/ppermute | solution.py:36
  60.1 1.5 %collective-permute-start.12 = (bf16[1,16,1024]{2,1,0:T(8,128)(2,1)S(1)}, bf16[1,16,1024]{2,1,0:T(8,128)(2,1)S(1)}, u32[]{:S(2)}, u32[]{:S(2)}) collective-permute-start(bf16[1,16,1024]{2,1,0:T(8,128)(2,1)S(1)} %get-tuple-element.53), channel_id=1, source_target_pairs={{0,8},{1,9},{2,10},{3,11},{4,12},{5,13},{6,14},{7,15},{8,0},{9,1},... | collective-permute-start | bytes 98312 | tf_op jit(solution)/shard_map/ppermute | solution.py:36
  61.6 2.2 %collective-permute-done.19 = bf16[1,16,1024]{2,1,0:T(8,128)(2,1)S(1)} collective-permute-done((bf16[1,16,1024]{2,1,0:T(8,128)(2,1)S(1)}, bf16[1,16,1024]{2,1,0:T(8,128)(2,1)S(1)}, u32[]{:S(2)}, u32[]{:S(2)}) %collective-permute-start.19) | collective-permute-done | bytes 32800 | tf_op jit(solution)/shard_map/ppermute | solution.py:36
  63.9 0.4 collective-permute-start.20
  64.3 0.6 collective-permute-done.12
  64.9 2.2 %collective-permute-start.13 = (bf16[2,16,1024]{2,1,0:T(8,128)(2,1)S(1)}, bf16[2,16,1024]{2,1,0:T(8,128)(2,1)S(1)}, u32[]{:S(2)}, u32[]{:S(2)}) collective-permute-start(bf16[2,16,1024]{2,1,0:T(8,128)(2,1)S(1)} %pad_maximum_fusion.7), channel_id=1, source_target_pairs={{0,4},{1,3},{2,6},{3,1},{4,0},{5,7},{6,2},{7,5},{8,12},{9,11},{10,... | collective-permute-start | bytes 196616 | tf_op jit(solution)/shard_map/ppermute | solution.py:36
  67.1 1.7 %collective-permute-done.20 = bf16[2,16,1024]{2,1,0:T(8,128)(2,1)S(1)} collective-permute-done((bf16[2,16,1024]{2,1,0:T(8,128)(2,1)S(1)}, bf16[2,16,1024]{2,1,0:T(8,128)(2,1)S(1)}, u32[]{:S(2)}, u32[]{:S(2)}) %collective-permute-start.20) | collective-permute-done | bytes 65568 | tf_op jit(solution)/shard_map/ppermute | solution.py:36
  68.8 1.4 %collective-permute-done.13 = bf16[2,16,1024]{2,1,0:T(8,128)(2,1)S(1)} collective-permute-done((bf16[2,16,1024]{2,1,0:T(8,128)(2,1)S(1)}, bf16[2,16,1024]{2,1,0:T(8,128)(2,1)S(1)}, u32[]{:S(2)}, u32[]{:S(2)}) %collective-permute-start.13) | collective-permute-done | bytes 65568 | tf_op jit(solution)/shard_map/ppermute | solution.py:36
  70.3 1.6 %collective-permute-start.21 = (bf16[4,16,1024]{2,1,0:T(8,128)(2,1)S(1)}, bf16[4,16,1024]{2,1,0:T(8,128)(2,1)S(1)}, u32[]{:S(2)}, u32[]{:S(2)}) collective-permute-start(bf16[4,16,1024]{2,1,0:T(8,128)(2,1)S(1)} %bitcast.240), channel_id=1, source_target_pairs={{0,2},{1,5},{2,0},{3,7},{4,6},{5,1},{6,4},{7,3},{8,10},{9,13},{10,... | collective-permute-start | bytes 393224 | tf_op jit(solution)/shard_map/ppermute | solution.py:36
  71.9 0.5 collective-permute-start.14
  72.5 2.8 %collective-permute-done.21 = bf16[4,16,1024]{2,1,0:T(8,128)(2,1)S(1)} collective-permute-done((bf16[4,16,1024]{2,1,0:T(8,128)(2,1)S(1)}, bf16[4,16,1024]{2,1,0:T(8,128)(2,1)S(1)}, u32[]{:S(2)}, u32[]{:S(2)}) %collective-permute-start.21) | collective-permute-done | bytes 131104 | tf_op jit(solution)/shard_map/ppermute | solution.py:36
  75.5 1.5 %collective-permute-done.14 = bf16[4,16,1024]{2,1,0:T(8,128)(2,1)S(1)} collective-permute-done((bf16[4,16,1024]{2,1,0:T(8,128)(2,1)S(1)}, bf16[4,16,1024]{2,1,0:T(8,128)(2,1)S(1)}, u32[]{:S(2)}, u32[]{:S(2)}) %collective-permute-start.14) | collective-permute-done | bytes 131104 | tf_op jit(solution)/shard_map/ppermute | solution.py:36
  77.2 1.5 %collective-permute-done.22.refs_2_ = bf16[128,1024]{1,0:T(8,128)(2,1)S(1)} collective-permute-done((bf16[128,1024]{1,0:T(8,128)(2,1)S(1)}, bf16[128,1024]{1,0:T(8,128)(2,1)S(1)}, u32[]{:S(2)}, u32[]{:S(2)}) %collective-permute-start.22) | collective-permute-done | bytes 262176 | tf_op jit(solution)/shard_map/ppermute | solution.py:53
  78.7 0.7 copy-done.6
  79.4 9.6 %shard_map.56 = (f32[128,1024]{1,0:T(8,128)}, f32[128,1024]{1,0:T(8,128)}, f32[128,1024]{1,0:T(8,128)}, f32[128,1024]{1,0:T(8,128)}) custom-call(s32[1]{0:T(128)} %bitcast.1.core_ref, bf16[4,256,256]{2,1,0:T(8,128)(2,1)} %occ_ref.3, bf16[128,1024]{1,0:T(8,128)(2,1)} %bitcast.234, bf16[128,1024]{1,0:T(8,128)(2,1)} %bitcast.230, bf16[128,1024]{1,0:T(8,128)(2,1)} %copy-done.6, ...), custom_call_target="tpu_custom_call" | custom-call | tf_op jit(solution)/shard_map/pallas_call | solution.py:140
  88.9 0.1 collective-permute-start.24
  89.1 0.4 collective-permute-start.28
  89.4 1.6 %collective-permute-done.24 = f32[128,1024]{1,0:T(8,128)S(1)} collective-permute-done((f32[128,1024]{1,0:T(8,128)}, f32[128,1024]{1,0:T(8,128)S(1)}, u32[]{:S(2)}, u32[]{:S(2)}) %collective-permute-start.24) | collective-permute-done | bytes 524320 | tf_op jit(solution)/shard_map/ppermute | solution.py:63
  91.1 1.1 add.152
  92.2 1.4 %collective-permute-start.25 = (f32[2,2,16,1024]{3,2,1,0:T(8,128)S(1)}, f32[2,2,16,1024]{3,2,1,0:T(8,128)S(1)}, u32[]{:S(2)}, u32[]{:S(2)}) collective-permute-start(f32[2,2,16,1024]{3,2,1,0:T(8,128)S(1)} %bitcast_select_fusion.2), channel_id=1, source_target_pairs={{0,2},{1,5},{2,0},{3,7},{4,6},{5,1},{6,4},{7,3},{8,10},{9,13},{10,... | collective-permute-start | bytes 786440 | tf_op jit(solution)/shard_map/ppermute | solution.py:84
  93.6 1.1 add.158
  94.8 0.8 collective-permute-start.29
  95.5 3.1 %collective-permute-done.25 = f32[2,2,16,1024]{3,2,1,0:T(8,128)S(1)} collective-permute-done((f32[2,2,16,1024]{3,2,1,0:T(8,128)S(1)}, f32[2,2,16,1024]{3,2,1,0:T(8,128)S(1)}, u32[]{:S(2)}, u32[]{:S(2)}) %collective-permute-start.25) | collective-permute-done | bytes 262176 | tf_op jit(solution)/shard_map/ppermute | solution.py:84
  98.7 1.8 %collective-permute-start.26 = (f32[2,16,1024]{2,1,0:T(8,128)S(1)}, f32[2,16,1024]{2,1,0:T(8,128)S(1)}, u32[]{:S(2)}, u32[]{:S(2)}) collective-permute-start(f32[2,16,1024]{2,1,0:T(8,128)S(1)} %dynamic-slice_bitcast_fusion.1), channel_id=1, source_target_pairs={{0,4},{1,3},{2,6},{3,1},{4,0},{5,7},{6,2},{7,5},{8,12},{9,11},{10,... | collective-permute-start | bytes 393224 | tf_op jit(solution)/shard_map/ppermute | solution.py:84
  100.6 1.6 %collective-permute-done.29 = f32[2,2,16,1024]{3,2,1,0:T(8,128)S(1)} collective-permute-done((f32[2,2,16,1024]{3,2,1,0:T(8,128)S(1)}, f32[2,2,16,1024]{3,2,1,0:T(8,128)S(1)}, u32[]{:S(2)}, u32[]{:S(2)}) %collective-permute-start.29) | collective-permute-done | bytes 262176 | tf_op jit(solution)/shard_map/ppermute | solution.py:84
  102.3 1.8 %collective-permute-start.30 = (f32[2,16,1024]{2,1,0:T(8,128)S(1)}, f32[2,16,1024]{2,1,0:T(8,128)S(1)}, u32[]{:S(2)}, u32[]{:S(2)}) collective-permute-start(f32[2,16,1024]{2,1,0:T(8,128)S(1)} %dynamic-slice_bitcast_fusion), channel_id=1, source_target_pairs={{0,4},{1,3},{2,6},{3,1},{4,0},{5,7},{6,2},{7,5},{8,12},{9,11},{10,... | collective-permute-start | bytes 393224 | tf_op jit(solution)/shard_map/ppermute | solution.py:84
  104.1 1.6 %collective-permute-start.27 = (f32[16,1024]{1,0:T(8,128)S(1)}, f32[16,1024]{1,0:T(8,128)S(1)}, u32[]{:S(2)}, u32[]{:S(2)}) collective-permute-start(f32[16,1024]{1,0:T(8,128)S(1)} %dynamic-slice_bitcast_fusion.5), channel_id=1, source_target_pairs={{0,8},{1,9},{2,10},{3,11},{4,12},{5,13},{6,14},{7,15},{8,0},{9,1},... | collective-permute-start | bytes 196616 | tf_op jit(solution)/shard_map/ppermute | solution.py:84
  105.8 2.2 %collective-permute-done.30 = f32[2,16,1024]{2,1,0:T(8,128)S(1)} collective-permute-done((f32[2,16,1024]{2,1,0:T(8,128)S(1)}, f32[2,16,1024]{2,1,0:T(8,128)S(1)}, u32[]{:S(2)}, u32[]{:S(2)}) %collective-permute-start.30) | collective-permute-done | bytes 131104 | tf_op jit(solution)/shard_map/ppermute | solution.py:84
  108.0 2.0 %collective-permute-start.31 = (f32[16,1024]{1,0:T(8,128)S(1)}, f32[16,1024]{1,0:T(8,128)S(1)}, u32[]{:S(2)}, u32[]{:S(2)}) collective-permute-start(f32[16,1024]{1,0:T(8,128)S(1)} %dynamic-slice_bitcast_fusion.4), channel_id=1, source_target_pairs={{0,8},{1,9},{2,10},{3,11},{4,12},{5,13},{6,14},{7,15},{8,0},{9,1},... | collective-permute-start | bytes 196616 | tf_op jit(solution)/shard_map/ppermute | solution.py:84
  110.0 1.5 %collective-permute-done.27 = f32[16,1024]{1,0:T(8,128)S(1)} collective-permute-done((f32[16,1024]{1,0:T(8,128)S(1)}, f32[16,1024]{1,0:T(8,128)S(1)}, u32[]{:S(2)}, u32[]{:S(2)}) %collective-permute-start.27) | collective-permute-done | bytes 65568 | tf_op jit(solution)/shard_map/ppermute | solution.py:84
  111.5 1.7 %collective-permute-done.31 = f32[16,1024]{1,0:T(8,128)S(1)} collective-permute-done((f32[16,1024]{1,0:T(8,128)S(1)}, f32[16,1024]{1,0:T(8,128)S(1)}, u32[]{:S(2)}, u32[]{:S(2)}) %collective-permute-start.31) | collective-permute-done | bytes 65568 | tf_op jit(solution)/shard_map/ppermute | solution.py:84
  113.4 0.8 copy.31
  (77 shorter events, 1.8 us)
Async XLA Ops:
  2.6 6.3 %collective-permute-start.3 = (bf16[1,16,1024]{2,1,0:T(8,128)(2,1)S(1)}, bf16[1,16,1024]{2,1,0:T(8,128)(2,1)S(1)}, u32[]{:S(2)}, u32[]{:S(2)}) collective-permute-start(bf16[1,16,1024]{2,1,0:T(8,128)(2,1)S(1)} %get-tuple-element.55), channel_id=1, source_target_pairs={{0,8},{1,9},{2,10},{3,11},{4,12},{5,13},{6,14},{7,15},{8,0},{9,1},... | collective-permute-start | bytes 98312 | tf_op jit(solution)/shard_map/ppermute | solution.py:36
  6.7 4.8 %collective-permute-start = (bf16[1,16,1024]{2,1,0:T(8,128)(2,1)S(1)}, bf16[1,16,1024]{2,1,0:T(8,128)(2,1)S(1)}, u32[]{:S(2)}, u32[]{:S(2)}) collective-permute-start(bf16[1,16,1024]{2,1,0:T(8,128)(2,1)S(1)} %get-tuple-element.56), channel_id=1, source_target_pairs={{0,8},{1,9},{2,10},{3,11},{4,12},{5,13},{6,14},{7,15},{8,0},{9,1},... | collective-permute-start | bytes 98312 | tf_op jit(solution)/shard_map/ppermute | solution.py:36
  9.0 4.3 %collective-permute-start.4 = (bf16[2,16,1024]{2,1,0:T(8,128)(2,1)S(1)}, bf16[2,16,1024]{2,1,0:T(8,128)(2,1)S(1)}, u32[]{:S(2)}, u32[]{:S(2)}) collective-permute-start(bf16[2,16,1024]{2,1,0:T(8,128)(2,1)S(1)} %pad_maximum_fusion.6), channel_id=1, source_target_pairs={{0,4},{1,3},{2,6},{3,1},{4,0},{5,7},{6,2},{7,5},{8,12},{9,11},{10,... | collective-permute-start | bytes 196616 | tf_op jit(solution)/shard_map/ppermute | solution.py:36
  11.6 4.8 %collective-permute-start.1 = (bf16[2,16,1024]{2,1,0:T(8,128)(2,1)S(1)}, bf16[2,16,1024]{2,1,0:T(8,128)(2,1)S(1)}, u32[]{:S(2)}, u32[]{:S(2)}) collective-permute-start(bf16[2,16,1024]{2,1,0:T(8,128)(2,1)S(1)} %pad_maximum_fusion.5), channel_id=1, source_target_pairs={{0,4},{1,3},{2,6},{3,1},{4,0},{5,7},{6,2},{7,5},{8,12},{9,11},{10,... | collective-permute-start | bytes 196616 | tf_op jit(solution)/shard_map/ppermute | solution.py:36
  13.4 5.0 %collective-permute-start.5 = (bf16[4,16,1024]{2,1,0:T(8,128)(2,1)S(1)}, bf16[4,16,1024]{2,1,0:T(8,128)(2,1)S(1)}, u32[]{:S(2)}, u32[]{:S(2)}) collective-permute-start(bf16[4,16,1024]{2,1,0:T(8,128)(2,1)S(1)} %bitcast.237), channel_id=1, source_target_pairs={{0,2},{1,5},{2,0},{3,7},{4,6},{5,1},{6,4},{7,3},{8,10},{9,13},{10,... | collective-permute-start | bytes 393224 | tf_op jit(solution)/shard_map/ppermute | solution.py:36
  16.4 5.0 %collective-permute-start.2 = (bf16[4,16,1024]{2,1,0:T(8,128)(2,1)S(1)}, bf16[4,16,1024]{2,1,0:T(8,128)(2,1)S(1)}, u32[]{:S(2)}, u32[]{:S(2)}) collective-permute-start(bf16[4,16,1024]{2,1,0:T(8,128)(2,1)S(1)} %bitcast.238), channel_id=1, source_target_pairs={{0,2},{1,5},{2,0},{3,7},{4,6},{5,1},{6,4},{7,3},{8,10},{9,13},{10,... | collective-permute-start | bytes 393224 | tf_op jit(solution)/shard_map/ppermute | solution.py:36
  18.5 4.7 %copy-start.1 = (bf16[2,2,2,16,1024]{4,3,2,1,0:T(8,128)(2,1)}, bf16[2,2,2,16,1024]{4,3,2,1,0:T(8,128)(2,1)S(1)}, u32[]{:S(2)}) copy-start(bf16[2,2,2,16,1024]{4,3,2,1,0:T(8,128)(2,1)S(1)} %maximum_select_fusion.1) | copy-start | bytes 786436
  18.5 3.1 %collective-permute-start.7 = (bf16[128,1024]{1,0:T(8,128)(2,1)S(1)}, bf16[128,1024]{1,0:T(8,128)(2,1)S(1)}, u32[]{:S(2)}, u32[]{:S(2)}) collective-permute-start(bf16[128,1024]{1,0:T(8,128)(2,1)S(1)} %bitcast.231), channel_id=1, source_target_pairs={{0,1},{1,0},{2,3},{3,2},{4,5},{5,4},{6,7},{7,6},{8,9},{9,8},{10,11... | collective-permute-start | bytes 786440 | tf_op jit(solution)/shard_map/ppermute | solution.py:53
  21.6 1.6 %copy-start.3 = (bf16[2,2,2,16,1024]{4,3,2,1,0:T(8,128)(2,1)}, bf16[2,2,2,16,1024]{4,3,2,1,0:T(8,128)(2,1)S(1)}, u32[]{:S(2)}) copy-start(bf16[2,2,2,16,1024]{4,3,2,1,0:T(8,128)(2,1)S(1)} %maximum_select_fusion) | copy-start | bytes 786436
  21.6 1.6 %collective-permute-start.6 = (bf16[128,1024]{1,0:T(8,128)(2,1)S(1)}, bf16[128,1024]{1,0:T(8,128)(2,1)S(1)}, u32[]{:S(2)}, u32[]{:S(2)}) collective-permute-start(bf16[128,1024]{1,0:T(8,128)(2,1)S(1)} %bitcast.235), channel_id=1, source_target_pairs={{0,1},{1,0},{2,3},{3,2},{4,5},{5,4},{6,7},{7,6},{8,9},{9,8},{10,11... | collective-permute-start | bytes 786440 | tf_op jit(solution)/shard_map/ppermute | solution.py:53
  21.7 1.5 %copy-start.5 = (bf16[128,1024]{1,0:T(8,128)(2,1)}, bf16[128,1024]{1,0:T(8,128)(2,1)S(1)}, u32[]{:S(2)}) copy-start(bf16[128,1024]{1,0:T(8,128)(2,1)S(1)} %collective-permute-done.7.refs_3_) | copy-start | bytes 786436
  23.2 0.7 copy-start.7
  23.9 34.6 %copy-start.8 = (f32[1024]{0:T(1024)S(1)}, f32[1024]{0:T(1024)}, u32[]{:S(2)}) copy-start(f32[1024]{0:T(1024)} %param.7) | copy-start | bytes 12292
  33.5 2.1 %collective-permute-start.8 = (f32[128,1024]{1,0:T(8,128)}, f32[128,1024]{1,0:T(8,128)S(1)}, u32[]{:S(2)}, u32[]{:S(2)}) collective-permute-start(f32[128,1024]{1,0:T(8,128)} %get-tuple-element.14), channel_id=1, source_target_pairs={{0,1},{1,0},{2,3},{3,2},{4,5},{5,4},{6,7},{7,6},{8,9},{9,8},{10,11... | collective-permute-start | bytes 1572872 | tf_op jit(solution)/shard_map/ppermute | solution.py:63
  33.6 4.2 %collective-permute-start.15 = (f32[128,1024]{1,0:T(8,128)}, f32[128,1024]{1,0:T(8,128)S(1)}, u32[]{:S(2)}, u32[]{:S(2)}) collective-permute-start(f32[128,1024]{1,0:T(8,128)} %get-tuple-element.16), channel_id=1, source_target_pairs={{0,1},{1,0},{2,3},{3,2},{4,5},{5,4},{6,7},{7,6},{8,9},{9,8},{10,11... | collective-permute-start | bytes 1572872 | tf_op jit(solution)/shard_map/ppermute | solution.py:63
  36.7 6.4 %collective-permute-start.9 = (f32[2,2,16,1024]{3,2,1,0:T(8,128)S(1)}, f32[2,2,16,1024]{3,2,1,0:T(8,128)S(1)}, u32[]{:S(2)}, u32[]{:S(2)}) collective-permute-start(f32[2,2,16,1024]{3,2,1,0:T(8,128)S(1)} %bitcast_select_fusion.6), channel_id=1, source_target_pairs={{0,2},{1,5},{2,0},{3,7},{4,6},{5,1},{6,4},{7,3},{8,10},{9,13},{10,... | collective-permute-start | bytes 786440 | tf_op jit(solution)/shard_map/ppermute | solution.py:84
  38.9 7.8 %collective-permute-start.16 = (f32[2,2,16,1024]{3,2,1,0:T(8,128)S(1)}, f32[2,2,16,1024]{3,2,1,0:T(8,128)S(1)}, u32[]{:S(2)}, u32[]{:S(2)}) collective-permute-start(f32[2,2,16,1024]{3,2,1,0:T(8,128)S(1)} %bitcast_select_fusion.4), channel_id=1, source_target_pairs={{0,2},{1,5},{2,0},{3,7},{4,6},{5,1},{6,4},{7,3},{8,10},{9,13},{10,... | collective-permute-start | bytes 786440 | tf_op jit(solution)/shard_map/ppermute | solution.py:84
  43.2 5.0 %collective-permute-start.10 = (f32[2,16,1024]{2,1,0:T(8,128)S(1)}, f32[2,16,1024]{2,1,0:T(8,128)S(1)}, u32[]{:S(2)}, u32[]{:S(2)}) collective-permute-start(f32[2,16,1024]{2,1,0:T(8,128)S(1)} %dynamic-slice_bitcast_fusion.3), channel_id=1, source_target_pairs={{0,4},{1,3},{2,6},{3,1},{4,0},{5,7},{6,2},{7,5},{8,12},{9,11},{10,... | collective-permute-start | bytes 393224 | tf_op jit(solution)/shard_map/ppermute | solution.py:84
  46.8 5.7 %collective-permute-start.17 = (f32[2,16,1024]{2,1,0:T(8,128)S(1)}, f32[2,16,1024]{2,1,0:T(8,128)S(1)}, u32[]{:S(2)}, u32[]{:S(2)}) collective-permute-start(f32[2,16,1024]{2,1,0:T(8,128)S(1)} %dynamic-slice_bitcast_fusion.2), channel_id=1, source_target_pairs={{0,4},{1,3},{2,6},{3,1},{4,0},{5,7},{6,2},{7,5},{8,12},{9,11},{10,... | collective-permute-start | bytes 393224 | tf_op jit(solution)/shard_map/ppermute | solution.py:84
  48.3 6.4 %collective-permute-start.11 = (f32[16,1024]{1,0:T(8,128)S(1)}, f32[16,1024]{1,0:T(8,128)S(1)}, u32[]{:S(2)}, u32[]{:S(2)}) collective-permute-start(f32[16,1024]{1,0:T(8,128)S(1)} %dynamic-slice_bitcast_fusion.7), channel_id=1, source_target_pairs={{0,8},{1,9},{2,10},{3,11},{4,12},{5,13},{6,14},{7,15},{8,0},{9,1},... | collective-permute-start | bytes 196616 | tf_op jit(solution)/shard_map/ppermute | solution.py:84
  52.5 5.9 %collective-permute-start.18 = (f32[16,1024]{1,0:T(8,128)S(1)}, f32[16,1024]{1,0:T(8,128)S(1)}, u32[]{:S(2)}, u32[]{:S(2)}) collective-permute-start(f32[16,1024]{1,0:T(8,128)S(1)} %dynamic-slice_bitcast_fusion.6), channel_id=1, source_target_pairs={{0,8},{1,9},{2,10},{3,11},{4,12},{5,13},{6,14},{7,15},{8,0},{9,1},... | collective-permute-start | bytes 196616 | tf_op jit(solution)/shard_map/ppermute | solution.py:84
  58.6 5.2 %collective-permute-start.19 = (bf16[1,16,1024]{2,1,0:T(8,128)(2,1)S(1)}, bf16[1,16,1024]{2,1,0:T(8,128)(2,1)S(1)}, u32[]{:S(2)}, u32[]{:S(2)}) collective-permute-start(bf16[1,16,1024]{2,1,0:T(8,128)(2,1)S(1)} %get-tuple-element.21), channel_id=1, source_target_pairs={{0,8},{1,9},{2,10},{3,11},{4,12},{5,13},{6,14},{7,15},{8,0},{9,1},... | collective-permute-start | bytes 98312 | tf_op jit(solution)/shard_map/ppermute | solution.py:36
  60.1 4.8 %collective-permute-start.12 = (bf16[1,16,1024]{2,1,0:T(8,128)(2,1)S(1)}, bf16[1,16,1024]{2,1,0:T(8,128)(2,1)S(1)}, u32[]{:S(2)}, u32[]{:S(2)}) collective-permute-start(bf16[1,16,1024]{2,1,0:T(8,128)(2,1)S(1)} %get-tuple-element.53), channel_id=1, source_target_pairs={{0,8},{1,9},{2,10},{3,11},{4,12},{5,13},{6,14},{7,15},{8,0},{9,1},... | collective-permute-start | bytes 98312 | tf_op jit(solution)/shard_map/ppermute | solution.py:36
  63.9 4.9 %collective-permute-start.20 = (bf16[2,16,1024]{2,1,0:T(8,128)(2,1)S(1)}, bf16[2,16,1024]{2,1,0:T(8,128)(2,1)S(1)}, u32[]{:S(2)}, u32[]{:S(2)}) collective-permute-start(bf16[2,16,1024]{2,1,0:T(8,128)(2,1)S(1)} %pad_maximum_fusion.8), channel_id=1, source_target_pairs={{0,4},{1,3},{2,6},{3,1},{4,0},{5,7},{6,2},{7,5},{8,12},{9,11},{10,... | collective-permute-start | bytes 196616 | tf_op jit(solution)/shard_map/ppermute | solution.py:36
  64.9 5.3 %collective-permute-start.13 = (bf16[2,16,1024]{2,1,0:T(8,128)(2,1)S(1)}, bf16[2,16,1024]{2,1,0:T(8,128)(2,1)S(1)}, u32[]{:S(2)}, u32[]{:S(2)}) collective-permute-start(bf16[2,16,1024]{2,1,0:T(8,128)(2,1)S(1)} %pad_maximum_fusion.7), channel_id=1, source_target_pairs={{0,4},{1,3},{2,6},{3,1},{4,0},{5,7},{6,2},{7,5},{8,12},{9,11},{10,... | collective-permute-start | bytes 196616 | tf_op jit(solution)/shard_map/ppermute | solution.py:36
  70.3 5.0 %collective-permute-start.21 = (bf16[4,16,1024]{2,1,0:T(8,128)(2,1)S(1)}, bf16[4,16,1024]{2,1,0:T(8,128)(2,1)S(1)}, u32[]{:S(2)}, u32[]{:S(2)}) collective-permute-start(bf16[4,16,1024]{2,1,0:T(8,128)(2,1)S(1)} %bitcast.240), channel_id=1, source_target_pairs={{0,2},{1,5},{2,0},{3,7},{4,6},{5,1},{6,4},{7,3},{8,10},{9,13},{10,... | collective-permute-start | bytes 393224 | tf_op jit(solution)/shard_map/ppermute | solution.py:36
  71.9 5.0 %collective-permute-start.14 = (bf16[4,16,1024]{2,1,0:T(8,128)(2,1)S(1)}, bf16[4,16,1024]{2,1,0:T(8,128)(2,1)S(1)}, u32[]{:S(2)}, u32[]{:S(2)}) collective-permute-start(bf16[4,16,1024]{2,1,0:T(8,128)(2,1)S(1)} %bitcast.239), channel_id=1, source_target_pairs={{0,2},{1,5},{2,0},{3,7},{4,6},{5,1},{6,4},{7,3},{8,10},{9,13},{10,... | collective-permute-start | bytes 393224 | tf_op jit(solution)/shard_map/ppermute | solution.py:36
  75.4 3.3 %copy-start = (bf16[2,2,2,16,1024]{4,3,2,1,0:T(8,128)(2,1)}, bf16[2,2,2,16,1024]{4,3,2,1,0:T(8,128)(2,1)S(1)}, u32[]{:S(2)}) copy-start(bf16[2,2,2,16,1024]{4,3,2,1,0:T(8,128)(2,1)S(1)} %maximum_select_fusion.3) | copy-start | bytes 786436
  75.4 1.7 %collective-permute-start.23 = (bf16[128,1024]{1,0:T(8,128)(2,1)S(1)}, bf16[128,1024]{1,0:T(8,128)(2,1)S(1)}, u32[]{:S(2)}, u32[]{:S(2)}) collective-permute-start(bf16[128,1024]{1,0:T(8,128)(2,1)S(1)} %bitcast.229), channel_id=1, source_target_pairs={{0,1},{1,0},{2,3},{3,2},{4,5},{5,4},{6,7},{7,6},{8,9},{9,8},{10,11... | collective-permute-start | bytes 786440 | tf_op jit(solution)/shard_map/ppermute | solution.py:53
  77.0 1.6 %copy-start.2 = (bf16[2,2,2,16,1024]{4,3,2,1,0:T(8,128)(2,1)}, bf16[2,2,2,16,1024]{4,3,2,1,0:T(8,128)(2,1)S(1)}, u32[]{:S(2)}) copy-start(bf16[2,2,2,16,1024]{4,3,2,1,0:T(8,128)(2,1)S(1)} %maximum_select_fusion.2) | copy-start | bytes 786436
  77.1 1.6 %collective-permute-start.22 = (bf16[128,1024]{1,0:T(8,128)(2,1)S(1)}, bf16[128,1024]{1,0:T(8,128)(2,1)S(1)}, u32[]{:S(2)}, u32[]{:S(2)}) collective-permute-start(bf16[128,1024]{1,0:T(8,128)(2,1)S(1)} %bitcast.233), channel_id=1, source_target_pairs={{0,1},{1,0},{2,3},{3,2},{4,5},{5,4},{6,7},{7,6},{8,9},{9,8},{10,11... | collective-permute-start | bytes 786440 | tf_op jit(solution)/shard_map/ppermute | solution.py:53
  77.1 1.5 %copy-start.4 = (bf16[128,1024]{1,0:T(8,128)(2,1)}, bf16[128,1024]{1,0:T(8,128)(2,1)S(1)}, u32[]{:S(2)}) copy-start(bf16[128,1024]{1,0:T(8,128)(2,1)S(1)} %collective-permute-done.23.refs_3_) | copy-start | bytes 786436
  78.7 0.7 copy-start.6
  88.9 2.1 %collective-permute-start.24 = (f32[128,1024]{1,0:T(8,128)}, f32[128,1024]{1,0:T(8,128)S(1)}, u32[]{:S(2)}, u32[]{:S(2)}) collective-permute-start(f32[128,1024]{1,0:T(8,128)} %get-tuple-element.18), channel_id=1, source_target_pairs={{0,1},{1,0},{2,3},{3,2},{4,5},{5,4},{6,7},{7,6},{8,9},{9,8},{10,11... | collective-permute-start | bytes 1572872 | tf_op jit(solution)/shard_map/ppermute | solution.py:63
  89.1 4.5 %collective-permute-start.28 = (f32[128,1024]{1,0:T(8,128)}, f32[128,1024]{1,0:T(8,128)S(1)}, u32[]{:S(2)}, u32[]{:S(2)}) collective-permute-start(f32[128,1024]{1,0:T(8,128)} %get-tuple-element.20), channel_id=1, source_target_pairs={{0,1},{1,0},{2,3},{3,2},{4,5},{5,4},{6,7},{7,6},{8,9},{9,8},{10,11... | collective-permute-start | bytes 1572872 | tf_op jit(solution)/shard_map/ppermute | solution.py:63
  92.2 6.4 %collective-permute-start.25 = (f32[2,2,16,1024]{3,2,1,0:T(8,128)S(1)}, f32[2,2,16,1024]{3,2,1,0:T(8,128)S(1)}, u32[]{:S(2)}, u32[]{:S(2)}) collective-permute-start(f32[2,2,16,1024]{3,2,1,0:T(8,128)S(1)} %bitcast_select_fusion.2), channel_id=1, source_target_pairs={{0,2},{1,5},{2,0},{3,7},{4,6},{5,1},{6,4},{7,3},{8,10},{9,13},{10,... | collective-permute-start | bytes 786440 | tf_op jit(solution)/shard_map/ppermute | solution.py:84
  94.8 7.4 %collective-permute-start.29 = (f32[2,2,16,1024]{3,2,1,0:T(8,128)S(1)}, f32[2,2,16,1024]{3,2,1,0:T(8,128)S(1)}, u32[]{:S(2)}, u32[]{:S(2)}) collective-permute-start(f32[2,2,16,1024]{3,2,1,0:T(8,128)S(1)} %bitcast_select_fusion), channel_id=1, source_target_pairs={{0,2},{1,5},{2,0},{3,7},{4,6},{5,1},{6,4},{7,3},{8,10},{9,13},{10,... | collective-permute-start | bytes 786440 | tf_op jit(solution)/shard_map/ppermute | solution.py:84
  98.7 5.4 %collective-permute-start.26 = (f32[2,16,1024]{2,1,0:T(8,128)S(1)}, f32[2,16,1024]{2,1,0:T(8,128)S(1)}, u32[]{:S(2)}, u32[]{:S(2)}) collective-permute-start(f32[2,16,1024]{2,1,0:T(8,128)S(1)} %dynamic-slice_bitcast_fusion.1), channel_id=1, source_target_pairs={{0,4},{1,3},{2,6},{3,1},{4,0},{5,7},{6,2},{7,5},{8,12},{9,11},{10,... | collective-permute-start | bytes 393224 | tf_op jit(solution)/shard_map/ppermute | solution.py:84
  102.3 5.7 %collective-permute-start.30 = (f32[2,16,1024]{2,1,0:T(8,128)S(1)}, f32[2,16,1024]{2,1,0:T(8,128)S(1)}, u32[]{:S(2)}, u32[]{:S(2)}) collective-permute-start(f32[2,16,1024]{2,1,0:T(8,128)S(1)} %dynamic-slice_bitcast_fusion), channel_id=1, source_target_pairs={{0,4},{1,3},{2,6},{3,1},{4,0},{5,7},{6,2},{7,5},{8,12},{9,11},{10,... | collective-permute-start | bytes 393224 | tf_op jit(solution)/shard_map/ppermute | solution.py:84
  104.1 7.4 %collective-permute-start.27 = (f32[16,1024]{1,0:T(8,128)S(1)}, f32[16,1024]{1,0:T(8,128)S(1)}, u32[]{:S(2)}, u32[]{:S(2)}) collective-permute-start(f32[16,1024]{1,0:T(8,128)S(1)} %dynamic-slice_bitcast_fusion.5), channel_id=1, source_target_pairs={{0,8},{1,9},{2,10},{3,11},{4,12},{5,13},{6,14},{7,15},{8,0},{9,1},... | collective-permute-start | bytes 196616 | tf_op jit(solution)/shard_map/ppermute | solution.py:84
  108.0 5.2 %collective-permute-start.31 = (f32[16,1024]{1,0:T(8,128)S(1)}, f32[16,1024]{1,0:T(8,128)S(1)}, u32[]{:S(2)}, u32[]{:S(2)}) collective-permute-start(f32[16,1024]{1,0:T(8,128)S(1)} %dynamic-slice_bitcast_fusion.4), channel_id=1, source_target_pairs={{0,8},{1,9},{2,10},{3,11},{4,12},{5,13},{6,14},{7,15},{8,0},{9,1},... | collective-permute-start | bytes 196616 | tf_op jit(solution)/shard_map/ppermute | solution.py:84

commit v16 on v15

--- a/solution.py
+++ b/solution.py
@@ -183,7 +183,8 @@
     n = nocc // own_rows
     assert n & (n - 1) == 0
     position = lax.axis_index("aux")
-    my_occ = lax.dynamic_slice_in_dim(occ_energy, position * own_rows, own_rows, 0)
+    wanted = position * own_rows + jnp.arange(own_rows)
+    my_occ = jnp.sum(jnp.where(jnp.arange(nocc)[None, :] == wanted[:, None], occ_energy[None, :], 0.0), axis=1)
     denom = vir_energy[None, None, :] - my_occ[:, None, None]
     rows = own_rows if own_rows % 16 == 0 else 0
     ordered_occ = occ_ints

time: 115 us -> 115 us (level)
  no operation moved by 1% of the time
where the time goes in v16:
time: 115 us; the launch traced here: 114 us
  waiting for transfers between devices  45.5 us (40%)
  starting transfers between devices  38.6 us (34%)
  Pallas kernels  19.2 us (17%)
  other arithmetic  7.16 us (6%)
  local copies, waits for them, and re-layouts  3.39 us (3%)
    ppermute x12, waiting for transfers between devices, scatter_sum(): acc = kept + lax.ppermute(sent, 'aux', partners(n, b0, b1))  20.8 us
    ppermute x12, starting transfers between devices, scatter_sum(): acc = kept + lax.ppermute(sent, 'aux', partners(n, b0, b1))  19.2 us
    pallas_call x2, Pallas kernels, exchange_part(): pl.pallas_call(functools.partial(exchange_kernel, states, rows), grid=(lo...  19.2 us
    ppermute x12, waiting for transfers between devices, gather_rows(): theirs = lax.ppermute(acc, 'aux', partners(n, b0, b1))  18.5 us
    ppermute x12, starting transfers between devices, gather_rows(): theirs = lax.ppermute(acc, 'aux', partners(n, b0, b1))  18.1 us
    add x4, other arithmetic, scatter_sum(): keep.reshape(shape)  4.44 us
    ppermute x4, waiting for transfers between devices, scatter_sum(): lax.ppermute(send, 'aux', partners(n, 0, 0)).reshape(shape)  3.23 us
    ppermute x4, waiting for transfers between devices, gather_rows(): return (flat, lax.ppermute(flat, 'aux', partners(n, 0, 0)))  3.01 us
  transfers between devices with their start and end apart: 32, of which 26 were waited for; matrix products, arithmetic and copies ran while one was open for 5% of the time, Pallas kernels for 0%

profile of v16, /device:TPU:0, one launch (start us, length us, event | category | flops | bytes accessed | tf_op | source)
XLA Modules:
  0.0 114.2 jit_solution(500317170011828164)
XLA Ops:
  0.0 1.1 fusion.24
  1.1 0.9 select_reduce_fusion
  2.0 0.8 fusion.5
  2.7 4.1 %collective-permute-start.3 = (bf16[1,16,1024]{2,1,0:T(8,128)(2,1)S(1)}, bf16[1,16,1024]{2,1,0:T(8,128)(2,1)S(1)}, u32[]{:S(2)}, u32[]{:S(2)}) collective-permute-start(bf16[1,16,1024]{2,1,0:T(8,128)(2,1)S(1)} %get-tuple-element.55), channel_id=1, source_target_pairs={{0,8},{1,9},{2,10},{3,11},{4,12},{5,13},{6,14},{7,15},{8,0},{9,1},... | collective-permute-start | bytes 98312 | tf_op jit(solution)/shard_map/ppermute | solution.py:36
  6.9 2.2 %collective-permute-done.3 = bf16[1,16,1024]{2,1,0:T(8,128)(2,1)S(1)} collective-permute-done((bf16[1,16,1024]{2,1,0:T(8,128)(2,1)S(1)}, bf16[1,16,1024]{2,1,0:T(8,128)(2,1)S(1)}, u32[]{:S(2)}, u32[]{:S(2)}) %collective-permute-start.3) | collective-permute-done | bytes 32800 | tf_op jit(solution)/shard_map/ppermute | solution.py:36
  9.1 1.7 %collective-permute-start.4 = (bf16[2,16,1024]{2,1,0:T(8,128)(2,1)S(1)}, bf16[2,16,1024]{2,1,0:T(8,128)(2,1)S(1)}, u32[]{:S(2)}, u32[]{:S(2)}) collective-permute-start(bf16[2,16,1024]{2,1,0:T(8,128)(2,1)S(1)} %pad_maximum_fusion.6), channel_id=1, source_target_pairs={{0,4},{1,3},{2,6},{3,1},{4,0},{5,7},{6,2},{7,5},{8,12},{9,11},{10,... | collective-permute-start | bytes 196616 | tf_op jit(solution)/shard_map/ppermute | solution.py:36
  10.8 0.9 collective-permute-done
  11.7 1.6 %collective-permute-start.1 = (bf16[2,16,1024]{2,1,0:T(8,128)(2,1)S(1)}, bf16[2,16,1024]{2,1,0:T(8,128)(2,1)S(1)}, u32[]{:S(2)}, u32[]{:S(2)}) collective-permute-start(bf16[2,16,1024]{2,1,0:T(8,128)(2,1)S(1)} %pad_maximum_fusion.5), channel_id=1, source_target_pairs={{0,4},{1,3},{2,6},{3,1},{4,0},{5,7},{6,2},{7,5},{8,12},{9,11},{10,... | collective-permute-start | bytes 196616 | tf_op jit(solution)/shard_map/ppermute | solution.py:36
  13.5 1.8 %collective-permute-start.5 = (bf16[4,16,1024]{2,1,0:T(8,128)(2,1)S(1)}, bf16[4,16,1024]{2,1,0:T(8,128)(2,1)S(1)}, u32[]{:S(2)}, u32[]{:S(2)}) collective-permute-start(bf16[4,16,1024]{2,1,0:T(8,128)(2,1)S(1)} %bitcast.237), channel_id=1, source_target_pairs={{0,2},{1,5},{2,0},{3,7},{4,6},{5,1},{6,4},{7,3},{8,10},{9,13},{10,... | collective-permute-start | bytes 393224 | tf_op jit(solution)/shard_map/ppermute | solution.py:36
  15.3 1.2 %collective-permute-done.1 = bf16[2,16,1024]{2,1,0:T(8,128)(2,1)S(1)} collective-permute-done((bf16[2,16,1024]{2,1,0:T(8,128)(2,1)S(1)}, bf16[2,16,1024]{2,1,0:T(8,128)(2,1)S(1)}, u32[]{:S(2)}, u32[]{:S(2)}) %collective-permute-start.1) | collective-permute-done | bytes 65568 | tf_op jit(solution)/shard_map/ppermute | solution.py:36
  16.6 1.1 collective-permute-start.2
  17.6 0.9 collective-permute-done.5
  18.7 2.9 %collective-permute-done.2 = bf16[4,16,1024]{2,1,0:T(8,128)(2,1)S(1)} collective-permute-done((bf16[4,16,1024]{2,1,0:T(8,128)(2,1)S(1)}, bf16[4,16,1024]{2,1,0:T(8,128)(2,1)S(1)}, u32[]{:S(2)}, u32[]{:S(2)}) %collective-permute-start.2) | collective-permute-done | bytes 131104 | tf_op jit(solution)/shard_map/ppermute | solution.py:36
  21.8 1.5 %collective-permute-done.6.refs_2_ = bf16[128,1024]{1,0:T(8,128)(2,1)S(1)} collective-permute-done((bf16[128,1024]{1,0:T(8,128)(2,1)S(1)}, bf16[128,1024]{1,0:T(8,128)(2,1)S(1)}, u32[]{:S(2)}, u32[]{:S(2)}) %collective-permute-start.6) | collective-permute-done | bytes 262176 | tf_op jit(solution)/shard_map/ppermute | solution.py:53
  23.3 0.7 copy-done.7
  24.0 9.6 %shard_map.55 = (f32[128,1024]{1,0:T(8,128)}, f32[128,1024]{1,0:T(8,128)}, f32[128,1024]{1,0:T(8,128)}, f32[128,1024]{1,0:T(8,128)}) custom-call(s32[1]{0:T(128)} %bitcast.1.core_ref, bf16[4,256,256]{2,1,0:T(8,128)(2,1)} %occ_ref.3, bf16[128,1024]{1,0:T(8,128)(2,1)} %bitcast.236, bf16[128,1024]{1,0:T(8,128)(2,1)} %bitcast.232, bf16[128,1024]{1,0:T(8,128)(2,1)} %copy-done.7, ...), custom_call_target="tpu_custom_call" | custom-call | tf_op jit(solution)/shard_map/pallas_call | solution.py:140
  33.6 0.1 collective-permute-start.8
  33.7 0.4 collective-permute-start.15
  34.1 1.6 %collective-permute-done.8 = f32[128,1024]{1,0:T(8,128)S(1)} collective-permute-done((f32[128,1024]{1,0:T(8,128)}, f32[128,1024]{1,0:T(8,128)S(1)}, u32[]{:S(2)}, u32[]{:S(2)}) %collective-permute-start.8) | collective-permute-done | bytes 524320 | tf_op jit(solution)/shard_map/ppermute | solution.py:63
  35.7 1.1 add.140
  36.8 1.1 collective-permute-start.9
  37.9 1.1 add.154
  39.0 1.1 collective-permute-start.16
  40.1 3.1 %collective-permute-done.9 = f32[2,2,16,1024]{3,2,1,0:T(8,128)S(1)} collective-permute-done((f32[2,2,16,1024]{3,2,1,0:T(8,128)S(1)}, f32[2,2,16,1024]{3,2,1,0:T(8,128)S(1)}, u32[]{:S(2)}, u32[]{:S(2)}) %collective-permute-start.9) | collective-permute-done | bytes 262176 | tf_op jit(solution)/shard_map/ppermute | solution.py:84
  43.3 1.3 %collective-permute-start.10 = (f32[2,16,1024]{2,1,0:T(8,128)S(1)}, f32[2,16,1024]{2,1,0:T(8,128)S(1)}, u32[]{:S(2)}, u32[]{:S(2)}) collective-permute-start(f32[2,16,1024]{2,1,0:T(8,128)S(1)} %dynamic-slice_bitcast_fusion.3), channel_id=1, source_target_pairs={{0,4},{1,3},{2,6},{3,1},{4,0},{5,7},{6,2},{7,5},{8,12},{9,11},{10,... | collective-permute-start | bytes 393224 | tf_op jit(solution)/shard_map/ppermute | solution.py:84
  44.7 2.1 %collective-permute-done.16 = f32[2,2,16,1024]{3,2,1,0:T(8,128)S(1)} collective-permute-done((f32[2,2,16,1024]{3,2,1,0:T(8,128)S(1)}, f32[2,2,16,1024]{3,2,1,0:T(8,128)S(1)}, u32[]{:S(2)}, u32[]{:S(2)}) %collective-permute-start.16) | collective-permute-done | bytes 262176 | tf_op jit(solution)/shard_map/ppermute | solution.py:84
  46.9 1.3 %collective-permute-start.17 = (f32[2,16,1024]{2,1,0:T(8,128)S(1)}, f32[2,16,1024]{2,1,0:T(8,128)S(1)}, u32[]{:S(2)}, u32[]{:S(2)}) collective-permute-start(f32[2,16,1024]{2,1,0:T(8,128)S(1)} %dynamic-slice_bitcast_fusion.2), channel_id=1, source_target_pairs={{0,4},{1,3},{2,6},{3,1},{4,0},{5,7},{6,2},{7,5},{8,12},{9,11},{10,... | collective-permute-start | bytes 393224 | tf_op jit(solution)/shard_map/ppermute | solution.py:84
  48.2 0.2 collective-permute-done.10
  48.4 2.8 %collective-permute-start.11 = (f32[16,1024]{1,0:T(8,128)S(1)}, f32[16,1024]{1,0:T(8,128)S(1)}, u32[]{:S(2)}, u32[]{:S(2)}) collective-permute-start(f32[16,1024]{1,0:T(8,128)S(1)} %dynamic-slice_bitcast_fusion.7), channel_id=1, source_target_pairs={{0,8},{1,9},{2,10},{3,11},{4,12},{5,13},{6,14},{7,15},{8,0},{9,1},... | collective-permute-start | bytes 196616 | tf_op jit(solution)/shard_map/ppermute | solution.py:84
  51.2 1.4 %collective-permute-done.17 = f32[2,16,1024]{2,1,0:T(8,128)S(1)} collective-permute-done((f32[2,16,1024]{2,1,0:T(8,128)S(1)}, f32[2,16,1024]{2,1,0:T(8,128)S(1)}, u32[]{:S(2)}, u32[]{:S(2)}) %collective-permute-start.17) | collective-permute-done | bytes 131104 | tf_op jit(solution)/shard_map/ppermute | solution.py:84
  52.6 2.1 %collective-permute-start.18 = (f32[16,1024]{1,0:T(8,128)S(1)}, f32[16,1024]{1,0:T(8,128)S(1)}, u32[]{:S(2)}, u32[]{:S(2)}) collective-permute-start(f32[16,1024]{1,0:T(8,128)S(1)} %dynamic-slice_bitcast_fusion.6), channel_id=1, source_target_pairs={{0,8},{1,9},{2,10},{3,11},{4,12},{5,13},{6,14},{7,15},{8,0},{9,1},... | collective-permute-start | bytes 196616 | tf_op jit(solution)/shard_map/ppermute | solution.py:84
  54.8 3.8 %collective-permute-done.18 = f32[16,1024]{1,0:T(8,128)S(1)} collective-permute-done((f32[16,1024]{1,0:T(8,128)S(1)}, f32[16,1024]{1,0:T(8,128)S(1)}, u32[]{:S(2)}, u32[]{:S(2)}) %collective-permute-start.18) | collective-permute-done | bytes 65568 | tf_op jit(solution)/shard_map/ppermute | solution.py:84
  58.7 1.5 %collective-permute-start.19 = (bf16[1,16,1024]{2,1,0:T(8,128)(2,1)S(1)}, bf16[1,16,1024]{2,1,0:T(8,128)(2,1)S(1)}, u32[]{:S(2)}, u32[]{:S(2)}) collective-permute-start(bf16[1,16,1024]{2,1,0:T(8,128)(2,1)S(1)} %get-tuple-element.21), channel_id=1, source_target_pairs={{0,8},{1,9},{2,10},{3,11},{4,12},{5,13},{6,14},{7,15},{8,0},{9,1},... | collective-permute-start | bytes 98312 | tf_op jit(solution)/shard_map/ppermute | solution.py:36
  60.2 1.5 %collective-permute-start.12 = (bf16[1,16,1024]{2,1,0:T(8,128)(2,1)S(1)}, bf16[1,16,1024]{2,1,0:T(8,128)(2,1)S(1)}, u32[]{:S(2)}, u32[]{:S(2)}) collective-permute-start(bf16[1,16,1024]{2,1,0:T(8,128)(2,1)S(1)} %get-tuple-element.53), channel_id=1, source_target_pairs={{0,8},{1,9},{2,10},{3,11},{4,12},{5,13},{6,14},{7,15},{8,0},{9,1},... | collective-permute-start | bytes 98312 | tf_op jit(solution)/shard_map/ppermute | solution.py:36
  61.7 2.2 %collective-permute-done.19 = bf16[1,16,1024]{2,1,0:T(8,128)(2,1)S(1)} collective-permute-done((bf16[1,16,1024]{2,1,0:T(8,128)(2,1)S(1)}, bf16[1,16,1024]{2,1,0:T(8,128)(2,1)S(1)}, u32[]{:S(2)}, u32[]{:S(2)}) %collective-permute-start.19) | collective-permute-done | bytes 32800 | tf_op jit(solution)/shard_map/ppermute | solution.py:36
  63.9 0.4 collective-permute-start.20
  64.4 0.6 collective-permute-done.12
  65.0 2.2 %collective-permute-start.13 = (bf16[2,16,1024]{2,1,0:T(8,128)(2,1)S(1)}, bf16[2,16,1024]{2,1,0:T(8,128)(2,1)S(1)}, u32[]{:S(2)}, u32[]{:S(2)}) collective-permute-start(bf16[2,16,1024]{2,1,0:T(8,128)(2,1)S(1)} %pad_maximum_fusion.7), channel_id=1, source_target_pairs={{0,4},{1,3},{2,6},{3,1},{4,0},{5,7},{6,2},{7,5},{8,12},{9,11},{10,... | collective-permute-start | bytes 196616 | tf_op jit(solution)/shard_map/ppermute | solution.py:36
  67.2 1.7 %collective-permute-done.20 = bf16[2,16,1024]{2,1,0:T(8,128)(2,1)S(1)} collective-permute-done((bf16[2,16,1024]{2,1,0:T(8,128)(2,1)S(1)}, bf16[2,16,1024]{2,1,0:T(8,128)(2,1)S(1)}, u32[]{:S(2)}, u32[]{:S(2)}) %collective-permute-start.20) | collective-permute-done | bytes 65568 | tf_op jit(solution)/shard_map/ppermute | solution.py:36
  68.9 1.4 %collective-permute-done.13 = bf16[2,16,1024]{2,1,0:T(8,128)(2,1)S(1)} collective-permute-done((bf16[2,16,1024]{2,1,0:T(8,128)(2,1)S(1)}, bf16[2,16,1024]{2,1,0:T(8,128)(2,1)S(1)}, u32[]{:S(2)}, u32[]{:S(2)}) %collective-permute-start.13) | collective-permute-done | bytes 65568 | tf_op jit(solution)/shard_map/ppermute | solution.py:36
  70.4 1.6 %collective-permute-start.21 = (bf16[4,16,1024]{2,1,0:T(8,128)(2,1)S(1)}, bf16[4,16,1024]{2,1,0:T(8,128)(2,1)S(1)}, u32[]{:S(2)}, u32[]{:S(2)}) collective-permute-start(bf16[4,16,1024]{2,1,0:T(8,128)(2,1)S(1)} %bitcast.240), channel_id=1, source_target_pairs={{0,2},{1,5},{2,0},{3,7},{4,6},{5,1},{6,4},{7,3},{8,10},{9,13},{10,... | collective-permute-start | bytes 393224 | tf_op jit(solution)/shard_map/ppermute | solution.py:36
  72.0 0.5 collective-permute-start.14
  72.6 2.8 %collective-permute-done.21 = bf16[4,16,1024]{2,1,0:T(8,128)(2,1)S(1)} collective-permute-done((bf16[4,16,1024]{2,1,0:T(8,128)(2,1)S(1)}, bf16[4,16,1024]{2,1,0:T(8,128)(2,1)S(1)}, u32[]{:S(2)}, u32[]{:S(2)}) %collective-permute-start.21) | collective-permute-done | bytes 131104 | tf_op jit(solution)/shard_map/ppermute | solution.py:36
  75.6 1.5 %collective-permute-done.14 = bf16[4,16,1024]{2,1,0:T(8,128)(2,1)S(1)} collective-permute-done((bf16[4,16,1024]{2,1,0:T(8,128)(2,1)S(1)}, bf16[4,16,1024]{2,1,0:T(8,128)(2,1)S(1)}, u32[]{:S(2)}, u32[]{:S(2)}) %collective-permute-start.14) | collective-permute-done | bytes 131104 | tf_op jit(solution)/shard_map/ppermute | solution.py:36
  77.2 1.5 %collective-permute-done.22.refs_2_ = bf16[128,1024]{1,0:T(8,128)(2,1)S(1)} collective-permute-done((bf16[128,1024]{1,0:T(8,128)(2,1)S(1)}, bf16[128,1024]{1,0:T(8,128)(2,1)S(1)}, u32[]{:S(2)}, u32[]{:S(2)}) %collective-permute-start.22) | collective-permute-done | bytes 262176 | tf_op jit(solution)/shard_map/ppermute | solution.py:53
  78.8 0.7 copy-done.6
  79.4 9.6 %shard_map.56 = (f32[128,1024]{1,0:T(8,128)}, f32[128,1024]{1,0:T(8,128)}, f32[128,1024]{1,0:T(8,128)}, f32[128,1024]{1,0:T(8,128)}) custom-call(s32[1]{0:T(128)} %bitcast.1.core_ref, bf16[4,256,256]{2,1,0:T(8,128)(2,1)} %occ_ref.3, bf16[128,1024]{1,0:T(8,128)(2,1)} %bitcast.234, bf16[128,1024]{1,0:T(8,128)(2,1)} %bitcast.230, bf16[128,1024]{1,0:T(8,128)(2,1)} %copy-done.6, ...), custom_call_target="tpu_custom_call" | custom-call | tf_op jit(solution)/shard_map/pallas_call | solution.py:140
  89.0 0.1 collective-permute-start.24
  89.2 0.4 collective-permute-start.28
  89.5 1.6 %collective-permute-done.24 = f32[128,1024]{1,0:T(8,128)S(1)} collective-permute-done((f32[128,1024]{1,0:T(8,128)}, f32[128,1024]{1,0:T(8,128)S(1)}, u32[]{:S(2)}, u32[]{:S(2)}) %collective-permute-start.24) | collective-permute-done | bytes 524320 | tf_op jit(solution)/shard_map/ppermute | solution.py:63
  91.1 1.1 add.160
  92.3 1.4 %collective-permute-start.25 = (f32[2,2,16,1024]{3,2,1,0:T(8,128)S(1)}, f32[2,2,16,1024]{3,2,1,0:T(8,128)S(1)}, u32[]{:S(2)}, u32[]{:S(2)}) collective-permute-start(f32[2,2,16,1024]{3,2,1,0:T(8,128)S(1)} %bitcast_select_fusion.2), channel_id=1, source_target_pairs={{0,2},{1,5},{2,0},{3,7},{4,6},{5,1},{6,4},{7,3},{8,10},{9,13},{10,... | collective-permute-start | bytes 786440 | tf_op jit(solution)/shard_map/ppermute | solution.py:84
  93.7 1.1 add.166
  94.8 0.8 collective-permute-start.29
  95.6 3.1 %collective-permute-done.25 = f32[2,2,16,1024]{3,2,1,0:T(8,128)S(1)} collective-permute-done((f32[2,2,16,1024]{3,2,1,0:T(8,128)S(1)}, f32[2,2,16,1024]{3,2,1,0:T(8,128)S(1)}, u32[]{:S(2)}, u32[]{:S(2)}) %collective-permute-start.25) | collective-permute-done | bytes 262176 | tf_op jit(solution)/shard_map/ppermute | solution.py:84
  98.8 1.8 %collective-permute-start.26 = (f32[2,16,1024]{2,1,0:T(8,128)S(1)}, f32[2,16,1024]{2,1,0:T(8,128)S(1)}, u32[]{:S(2)}, u32[]{:S(2)}) collective-permute-start(f32[2,16,1024]{2,1,0:T(8,128)S(1)} %dynamic-slice_bitcast_fusion.1), channel_id=1, source_target_pairs={{0,4},{1,3},{2,6},{3,1},{4,0},{5,7},{6,2},{7,5},{8,12},{9,11},{10,... | collective-permute-start | bytes 393224 | tf_op jit(solution)/shard_map/ppermute | solution.py:84
  100.6 1.6 %collective-permute-done.29 = f32[2,2,16,1024]{3,2,1,0:T(8,128)S(1)} collective-permute-done((f32[2,2,16,1024]{3,2,1,0:T(8,128)S(1)}, f32[2,2,16,1024]{3,2,1,0:T(8,128)S(1)}, u32[]{:S(2)}, u32[]{:S(2)}) %collective-permute-start.29) | collective-permute-done | bytes 262176 | tf_op jit(solution)/shard_map/ppermute | solution.py:84
  102.3 1.8 %collective-permute-start.30 = (f32[2,16,1024]{2,1,0:T(8,128)S(1)}, f32[2,16,1024]{2,1,0:T(8,128)S(1)}, u32[]{:S(2)}, u32[]{:S(2)}) collective-permute-start(f32[2,16,1024]{2,1,0:T(8,128)S(1)} %dynamic-slice_bitcast_fusion), channel_id=1, source_target_pairs={{0,4},{1,3},{2,6},{3,1},{4,0},{5,7},{6,2},{7,5},{8,12},{9,11},{10,... | collective-permute-start | bytes 393224 | tf_op jit(solution)/shard_map/ppermute | solution.py:84
  104.2 1.6 %collective-permute-start.27 = (f32[16,1024]{1,0:T(8,128)S(1)}, f32[16,1024]{1,0:T(8,128)S(1)}, u32[]{:S(2)}, u32[]{:S(2)}) collective-permute-start(f32[16,1024]{1,0:T(8,128)S(1)} %dynamic-slice_bitcast_fusion.5), channel_id=1, source_target_pairs={{0,8},{1,9},{2,10},{3,11},{4,12},{5,13},{6,14},{7,15},{8,0},{9,1},... | collective-permute-start | bytes 196616 | tf_op jit(solution)/shard_map/ppermute | solution.py:84
  105.9 2.2 %collective-permute-done.30 = f32[2,16,1024]{2,1,0:T(8,128)S(1)} collective-permute-done((f32[2,16,1024]{2,1,0:T(8,128)S(1)}, f32[2,16,1024]{2,1,0:T(8,128)S(1)}, u32[]{:S(2)}, u32[]{:S(2)}) %collective-permute-start.30) | collective-permute-done | bytes 131104 | tf_op jit(solution)/shard_map/ppermute | solution.py:84
  108.1 2.0 %collective-permute-start.31 = (f32[16,1024]{1,0:T(8,128)S(1)}, f32[16,1024]{1,0:T(8,128)S(1)}, u32[]{:S(2)}, u32[]{:S(2)}) collective-permute-start(f32[16,1024]{1,0:T(8,128)S(1)} %dynamic-slice_bitcast_fusion.4), channel_id=1, source_target_pairs={{0,8},{1,9},{2,10},{3,11},{4,12},{5,13},{6,14},{7,15},{8,0},{9,1},... | collective-permute-start | bytes 196616 | tf_op jit(solution)/shard_map/ppermute | solution.py:84
  110.1 1.5 %collective-permute-done.27 = f32[16,1024]{1,0:T(8,128)S(1)} collective-permute-done((f32[16,1024]{1,0:T(8,128)S(1)}, f32[16,1024]{1,0:T(8,128)S(1)}, u32[]{:S(2)}, u32[]{:S(2)}) %collective-permute-start.27) | collective-permute-done | bytes 65568 | tf_op jit(solution)/shard_map/ppermute | solution.py:84
  111.6 1.7 %collective-permute-done.31 = f32[16,1024]{1,0:T(8,128)S(1)} collective-permute-done((f32[16,1024]{1,0:T(8,128)S(1)}, f32[16,1024]{1,0:T(8,128)S(1)}, u32[]{:S(2)}, u32[]{:S(2)}) %collective-permute-start.31) | collective-permute-done | bytes 65568 | tf_op jit(solution)/shard_map/ppermute | solution.py:84
  113.4 0.8 copy.54
  (78 shorter events, 1.8 us)
Async XLA Ops:
  2.7 6.3 %collective-permute-start.3 = (bf16[1,16,1024]{2,1,0:T(8,128)(2,1)S(1)}, bf16[1,16,1024]{2,1,0:T(8,128)(2,1)S(1)}, u32[]{:S(2)}, u32[]{:S(2)}) collective-permute-start(bf16[1,16,1024]{2,1,0:T(8,128)(2,1)S(1)} %get-tuple-element.55), channel_id=1, source_target_pairs={{0,8},{1,9},{2,10},{3,11},{4,12},{5,13},{6,14},{7,15},{8,0},{9,1},... | collective-permute-start | bytes 98312 | tf_op jit(solution)/shard_map/ppermute | solution.py:36
  6.8 4.8 %collective-permute-start = (bf16[1,16,1024]{2,1,0:T(8,128)(2,1)S(1)}, bf16[1,16,1024]{2,1,0:T(8,128)(2,1)S(1)}, u32[]{:S(2)}, u32[]{:S(2)}) collective-permute-start(bf16[1,16,1024]{2,1,0:T(8,128)(2,1)S(1)} %get-tuple-element.56), channel_id=1, source_target_pairs={{0,8},{1,9},{2,10},{3,11},{4,12},{5,13},{6,14},{7,15},{8,0},{9,1},... | collective-permute-start | bytes 98312 | tf_op jit(solution)/shard_map/ppermute | solution.py:36
  9.1 4.3 %collective-permute-start.4 = (bf16[2,16,1024]{2,1,0:T(8,128)(2,1)S(1)}, bf16[2,16,1024]{2,1,0:T(8,128)(2,1)S(1)}, u32[]{:S(2)}, u32[]{:S(2)}) collective-permute-start(bf16[2,16,1024]{2,1,0:T(8,128)(2,1)S(1)} %pad_maximum_fusion.6), channel_id=1, source_target_pairs={{0,4},{1,3},{2,6},{3,1},{4,0},{5,7},{6,2},{7,5},{8,12},{9,11},{10,... | collective-permute-start | bytes 196616 | tf_op jit(solution)/shard_map/ppermute | solution.py:36
  11.7 4.8 %collective-permute-start.1 = (bf16[2,16,1024]{2,1,0:T(8,128)(2,1)S(1)}, bf16[2,16,1024]{2,1,0:T(8,128)(2,1)S(1)}, u32[]{:S(2)}, u32[]{:S(2)}) collective-permute-start(bf16[2,16,1024]{2,1,0:T(8,128)(2,1)S(1)} %pad_maximum_fusion.5), channel_id=1, source_target_pairs={{0,4},{1,3},{2,6},{3,1},{4,0},{5,7},{6,2},{7,5},{8,12},{9,11},{10,... | collective-permute-start | bytes 196616 | tf_op jit(solution)/shard_map/ppermute | solution.py:36
  13.5 5.0 %collective-permute-start.5 = (bf16[4,16,1024]{2,1,0:T(8,128)(2,1)S(1)}, bf16[4,16,1024]{2,1,0:T(8,128)(2,1)S(1)}, u32[]{:S(2)}, u32[]{:S(2)}) collective-permute-start(bf16[4,16,1024]{2,1,0:T(8,128)(2,1)S(1)} %bitcast.237), channel_id=1, source_target_pairs={{0,2},{1,5},{2,0},{3,7},{4,6},{5,1},{6,4},{7,3},{8,10},{9,13},{10,... | collective-permute-start | bytes 393224 | tf_op jit(solution)/shard_map/ppermute | solution.py:36
  16.6 5.0 %collective-permute-start.2 = (bf16[4,16,1024]{2,1,0:T(8,128)(2,1)S(1)}, bf16[4,16,1024]{2,1,0:T(8,128)(2,1)S(1)}, u32[]{:S(2)}, u32[]{:S(2)}) collective-permute-start(bf16[4,16,1024]{2,1,0:T(8,128)(2,1)S(1)} %bitcast.238), channel_id=1, source_target_pairs={{0,2},{1,5},{2,0},{3,7},{4,6},{5,1},{6,4},{7,3},{8,10},{9,13},{10,... | collective-permute-start | bytes 393224 | tf_op jit(solution)/shard_map/ppermute | solution.py:36
  18.6 4.7 %copy-start.1 = (bf16[2,2,2,16,1024]{4,3,2,1,0:T(8,128)(2,1)}, bf16[2,2,2,16,1024]{4,3,2,1,0:T(8,128)(2,1)S(1)}, u32[]{:S(2)}) copy-start(bf16[2,2,2,16,1024]{4,3,2,1,0:T(8,128)(2,1)S(1)} %maximum_select_fusion.1) | copy-start | bytes 786436
  18.6 3.1 %collective-permute-start.7 = (bf16[128,1024]{1,0:T(8,128)(2,1)S(1)}, bf16[128,1024]{1,0:T(8,128)(2,1)S(1)}, u32[]{:S(2)}, u32[]{:S(2)}) collective-permute-start(bf16[128,1024]{1,0:T(8,128)(2,1)S(1)} %bitcast.231), channel_id=1, source_target_pairs={{0,1},{1,0},{2,3},{3,2},{4,5},{5,4},{6,7},{7,6},{8,9},{9,8},{10,11... | collective-permute-start | bytes 786440 | tf_op jit(solution)/shard_map/ppermute | solution.py:53
  21.7 1.6 %copy-start.3 = (bf16[2,2,2,16,1024]{4,3,2,1,0:T(8,128)(2,1)}, bf16[2,2,2,16,1024]{4,3,2,1,0:T(8,128)(2,1)S(1)}, u32[]{:S(2)}) copy-start(bf16[2,2,2,16,1024]{4,3,2,1,0:T(8,128)(2,1)S(1)} %maximum_select_fusion) | copy-start | bytes 786436
  21.7 1.6 %collective-permute-start.6 = (bf16[128,1024]{1,0:T(8,128)(2,1)S(1)}, bf16[128,1024]{1,0:T(8,128)(2,1)S(1)}, u32[]{:S(2)}, u32[]{:S(2)}) collective-permute-start(bf16[128,1024]{1,0:T(8,128)(2,1)S(1)} %bitcast.235), channel_id=1, source_target_pairs={{0,1},{1,0},{2,3},{3,2},{4,5},{5,4},{6,7},{7,6},{8,9},{9,8},{10,11... | collective-permute-start | bytes 786440 | tf_op jit(solution)/shard_map/ppermute | solution.py:53
  21.8 1.5 %copy-start.5 = (bf16[128,1024]{1,0:T(8,128)(2,1)}, bf16[128,1024]{1,0:T(8,128)(2,1)S(1)}, u32[]{:S(2)}) copy-start(bf16[128,1024]{1,0:T(8,128)(2,1)S(1)} %collective-permute-done.7.refs_3_) | copy-start | bytes 786436
  23.3 0.7 copy-start.7
  24.0 34.6 %copy-start.8 = (f32[1024]{0:T(1024)S(1)}, f32[1024]{0:T(1024)}, u32[]{:S(2)}) copy-start(f32[1024]{0:T(1024)} %param.7) | copy-start | bytes 12292
  33.6 2.1 %collective-permute-start.8 = (f32[128,1024]{1,0:T(8,128)}, f32[128,1024]{1,0:T(8,128)S(1)}, u32[]{:S(2)}, u32[]{:S(2)}) collective-permute-start(f32[128,1024]{1,0:T(8,128)} %get-tuple-element.14), channel_id=1, source_target_pairs={{0,1},{1,0},{2,3},{3,2},{4,5},{5,4},{6,7},{7,6},{8,9},{9,8},{10,11... | collective-permute-start | bytes 1572872 | tf_op jit(solution)/shard_map/ppermute | solution.py:63
  33.7 4.2 %collective-permute-start.15 = (f32[128,1024]{1,0:T(8,128)}, f32[128,1024]{1,0:T(8,128)S(1)}, u32[]{:S(2)}, u32[]{:S(2)}) collective-permute-start(f32[128,1024]{1,0:T(8,128)} %get-tuple-element.16), channel_id=1, source_target_pairs={{0,1},{1,0},{2,3},{3,2},{4,5},{5,4},{6,7},{7,6},{8,9},{9,8},{10,11... | collective-permute-start | bytes 1572872 | tf_op jit(solution)/shard_map/ppermute | solution.py:63
  36.8 6.4 %collective-permute-start.9 = (f32[2,2,16,1024]{3,2,1,0:T(8,128)S(1)}, f32[2,2,16,1024]{3,2,1,0:T(8,128)S(1)}, u32[]{:S(2)}, u32[]{:S(2)}) collective-permute-start(f32[2,2,16,1024]{3,2,1,0:T(8,128)S(1)} %bitcast_select_fusion.6), channel_id=1, source_target_pairs={{0,2},{1,5},{2,0},{3,7},{4,6},{5,1},{6,4},{7,3},{8,10},{9,13},{10,... | collective-permute-start | bytes 786440 | tf_op jit(solution)/shard_map/ppermute | solution.py:84
  39.0 7.8 %collective-permute-start.16 = (f32[2,2,16,1024]{3,2,1,0:T(8,128)S(1)}, f32[2,2,16,1024]{3,2,1,0:T(8,128)S(1)}, u32[]{:S(2)}, u32[]{:S(2)}) collective-permute-start(f32[2,2,16,1024]{3,2,1,0:T(8,128)S(1)} %bitcast_select_fusion.4), channel_id=1, source_target_pairs={{0,2},{1,5},{2,0},{3,7},{4,6},{5,1},{6,4},{7,3},{8,10},{9,13},{10,... | collective-permute-start | bytes 786440 | tf_op jit(solution)/shard_map/ppermute | solution.py:84
  43.3 5.0 %collective-permute-start.10 = (f32[2,16,1024]{2,1,0:T(8,128)S(1)}, f32[2,16,1024]{2,1,0:T(8,128)S(1)}, u32[]{:S(2)}, u32[]{:S(2)}) collective-permute-start(f32[2,16,1024]{2,1,0:T(8,128)S(1)} %dynamic-slice_bitcast_fusion.3), channel_id=1, source_target_pairs={{0,4},{1,3},{2,6},{3,1},{4,0},{5,7},{6,2},{7,5},{8,12},{9,11},{10,... | collective-permute-start | bytes 393224 | tf_op jit(solution)/shard_map/ppermute | solution.py:84
  46.9 5.7 %collective-permute-start.17 = (f32[2,16,1024]{2,1,0:T(8,128)S(1)}, f32[2,16,1024]{2,1,0:T(8,128)S(1)}, u32[]{:S(2)}, u32[]{:S(2)}) collective-permute-start(f32[2,16,1024]{2,1,0:T(8,128)S(1)} %dynamic-slice_bitcast_fusion.2), channel_id=1, source_target_pairs={{0,4},{1,3},{2,6},{3,1},{4,0},{5,7},{6,2},{7,5},{8,12},{9,11},{10,... | collective-permute-start | bytes 393224 | tf_op jit(solution)/shard_map/ppermute | solution.py:84
  48.4 6.4 %collective-permute-start.11 = (f32[16,1024]{1,0:T(8,128)S(1)}, f32[16,1024]{1,0:T(8,128)S(1)}, u32[]{:S(2)}, u32[]{:S(2)}) collective-permute-start(f32[16,1024]{1,0:T(8,128)S(1)} %dynamic-slice_bitcast_fusion.7), channel_id=1, source_target_pairs={{0,8},{1,9},{2,10},{3,11},{4,12},{5,13},{6,14},{7,15},{8,0},{9,1},... | collective-permute-start | bytes 196616 | tf_op jit(solution)/shard_map/ppermute | solution.py:84
  52.6 5.9 %collective-permute-start.18 = (f32[16,1024]{1,0:T(8,128)S(1)}, f32[16,1024]{1,0:T(8,128)S(1)}, u32[]{:S(2)}, u32[]{:S(2)}) collective-permute-start(f32[16,1024]{1,0:T(8,128)S(1)} %dynamic-slice_bitcast_fusion.6), channel_id=1, source_target_pairs={{0,8},{1,9},{2,10},{3,11},{4,12},{5,13},{6,14},{7,15},{8,0},{9,1},... | collective-permute-start | bytes 196616 | tf_op jit(solution)/shard_map/ppermute | solution.py:84
  58.7 5.2 %collective-permute-start.19 = (bf16[1,16,1024]{2,1,0:T(8,128)(2,1)S(1)}, bf16[1,16,1024]{2,1,0:T(8,128)(2,1)S(1)}, u32[]{:S(2)}, u32[]{:S(2)}) collective-permute-start(bf16[1,16,1024]{2,1,0:T(8,128)(2,1)S(1)} %get-tuple-element.21), channel_id=1, source_target_pairs={{0,8},{1,9},{2,10},{3,11},{4,12},{5,13},{6,14},{7,15},{8,0},{9,1},... | collective-permute-start | bytes 98312 | tf_op jit(solution)/shard_map/ppermute | solution.py:36
  60.2 4.8 %collective-permute-start.12 = (bf16[1,16,1024]{2,1,0:T(8,128)(2,1)S(1)}, bf16[1,16,1024]{2,1,0:T(8,128)(2,1)S(1)}, u32[]{:S(2)}, u32[]{:S(2)}) collective-permute-start(bf16[1,16,1024]{2,1,0:T(8,128)(2,1)S(1)} %get-tuple-element.53), channel_id=1, source_target_pairs={{0,8},{1,9},{2,10},{3,11},{4,12},{5,13},{6,14},{7,15},{8,0},{9,1},... | collective-permute-start | bytes 98312 | tf_op jit(solution)/shard_map/ppermute | solution.py:36
  63.9 4.9 %collective-permute-start.20 = (bf16[2,16,1024]{2,1,0:T(8,128)(2,1)S(1)}, bf16[2,16,1024]{2,1,0:T(8,128)(2,1)S(1)}, u32[]{:S(2)}, u32[]{:S(2)}) collective-permute-start(bf16[2,16,1024]{2,1,0:T(8,128)(2,1)S(1)} %pad_maximum_fusion.8), channel_id=1, source_target_pairs={{0,4},{1,3},{2,6},{3,1},{4,0},{5,7},{6,2},{7,5},{8,12},{9,11},{10,... | collective-permute-start | bytes 196616 | tf_op jit(solution)/shard_map/ppermute | solution.py:36
  65.0 5.3 %collective-permute-start.13 = (bf16[2,16,1024]{2,1,0:T(8,128)(2,1)S(1)}, bf16[2,16,1024]{2,1,0:T(8,128)(2,1)S(1)}, u32[]{:S(2)}, u32[]{:S(2)}) collective-permute-start(bf16[2,16,1024]{2,1,0:T(8,128)(2,1)S(1)} %pad_maximum_fusion.7), channel_id=1, source_target_pairs={{0,4},{1,3},{2,6},{3,1},{4,0},{5,7},{6,2},{7,5},{8,12},{9,11},{10,... | collective-permute-start | bytes 196616 | tf_op jit(solution)/shard_map/ppermute | solution.py:36
  70.4 5.0 %collective-permute-start.21 = (bf16[4,16,1024]{2,1,0:T(8,128)(2,1)S(1)}, bf16[4,16,1024]{2,1,0:T(8,128)(2,1)S(1)}, u32[]{:S(2)}, u32[]{:S(2)}) collective-permute-start(bf16[4,16,1024]{2,1,0:T(8,128)(2,1)S(1)} %bitcast.240), channel_id=1, source_target_pairs={{0,2},{1,5},{2,0},{3,7},{4,6},{5,1},{6,4},{7,3},{8,10},{9,13},{10,... | collective-permute-start | bytes 393224 | tf_op jit(solution)/shard_map/ppermute | solution.py:36
  72.0 5.0 %collective-permute-start.14 = (bf16[4,16,1024]{2,1,0:T(8,128)(2,1)S(1)}, bf16[4,16,1024]{2,1,0:T(8,128)(2,1)S(1)}, u32[]{:S(2)}, u32[]{:S(2)}) collective-permute-start(bf16[4,16,1024]{2,1,0:T(8,128)(2,1)S(1)} %bitcast.239), channel_id=1, source_target_pairs={{0,2},{1,5},{2,0},{3,7},{4,6},{5,1},{6,4},{7,3},{8,10},{9,13},{10,... | collective-permute-start | bytes 393224 | tf_op jit(solution)/shard_map/ppermute | solution.py:36
  75.5 3.3 %copy-start = (bf16[2,2,2,16,1024]{4,3,2,1,0:T(8,128)(2,1)}, bf16[2,2,2,16,1024]{4,3,2,1,0:T(8,128)(2,1)S(1)}, u32[]{:S(2)}) copy-start(bf16[2,2,2,16,1024]{4,3,2,1,0:T(8,128)(2,1)S(1)} %maximum_select_fusion.3) | copy-start | bytes 786436
  75.5 1.7 %collective-permute-start.23 = (bf16[128,1024]{1,0:T(8,128)(2,1)S(1)}, bf16[128,1024]{1,0:T(8,128)(2,1)S(1)}, u32[]{:S(2)}, u32[]{:S(2)}) collective-permute-start(bf16[128,1024]{1,0:T(8,128)(2,1)S(1)} %bitcast.229), channel_id=1, source_target_pairs={{0,1},{1,0},{2,3},{3,2},{4,5},{5,4},{6,7},{7,6},{8,9},{9,8},{10,11... | collective-permute-start | bytes 786440 | tf_op jit(solution)/shard_map/ppermute | solution.py:53
  77.1 1.6 %copy-start.2 = (bf16[2,2,2,16,1024]{4,3,2,1,0:T(8,128)(2,1)}, bf16[2,2,2,16,1024]{4,3,2,1,0:T(8,128)(2,1)S(1)}, u32[]{:S(2)}) copy-start(bf16[2,2,2,16,1024]{4,3,2,1,0:T(8,128)(2,1)S(1)} %maximum_select_fusion.2) | copy-start | bytes 786436
  77.1 1.6 %collective-permute-start.22 = (bf16[128,1024]{1,0:T(8,128)(2,1)S(1)}, bf16[128,1024]{1,0:T(8,128)(2,1)S(1)}, u32[]{:S(2)}, u32[]{:S(2)}) collective-permute-start(bf16[128,1024]{1,0:T(8,128)(2,1)S(1)} %bitcast.233), channel_id=1, source_target_pairs={{0,1},{1,0},{2,3},{3,2},{4,5},{5,4},{6,7},{7,6},{8,9},{9,8},{10,11... | collective-permute-start | bytes 786440 | tf_op jit(solution)/shard_map/ppermute | solution.py:53
  77.2 1.5 %copy-start.4 = (bf16[128,1024]{1,0:T(8,128)(2,1)}, bf16[128,1024]{1,0:T(8,128)(2,1)S(1)}, u32[]{:S(2)}) copy-start(bf16[128,1024]{1,0:T(8,128)(2,1)S(1)} %collective-permute-done.23.refs_3_) | copy-start | bytes 786436
  78.8 0.7 copy-start.6
  89.0 2.1 %collective-permute-start.24 = (f32[128,1024]{1,0:T(8,128)}, f32[128,1024]{1,0:T(8,128)S(1)}, u32[]{:S(2)}, u32[]{:S(2)}) collective-permute-start(f32[128,1024]{1,0:T(8,128)} %get-tuple-element.18), channel_id=1, source_target_pairs={{0,1},{1,0},{2,3},{3,2},{4,5},{5,4},{6,7},{7,6},{8,9},{9,8},{10,11... | collective-permute-start | bytes 1572872 | tf_op jit(solution)/shard_map/ppermute | solution.py:63
  89.2 4.5 %collective-permute-start.28 = (f32[128,1024]{1,0:T(8,128)}, f32[128,1024]{1,0:T(8,128)S(1)}, u32[]{:S(2)}, u32[]{:S(2)}) collective-permute-start(f32[128,1024]{1,0:T(8,128)} %get-tuple-element.20), channel_id=1, source_target_pairs={{0,1},{1,0},{2,3},{3,2},{4,5},{5,4},{6,7},{7,6},{8,9},{9,8},{10,11... | collective-permute-start | bytes 1572872 | tf_op jit(solution)/shard_map/ppermute | solution.py:63
  92.3 6.4 %collective-permute-start.25 = (f32[2,2,16,1024]{3,2,1,0:T(8,128)S(1)}, f32[2,2,16,1024]{3,2,1,0:T(8,128)S(1)}, u32[]{:S(2)}, u32[]{:S(2)}) collective-permute-start(f32[2,2,16,1024]{3,2,1,0:T(8,128)S(1)} %bitcast_select_fusion.2), channel_id=1, source_target_pairs={{0,2},{1,5},{2,0},{3,7},{4,6},{5,1},{6,4},{7,3},{8,10},{9,13},{10,... | collective-permute-start | bytes 786440 | tf_op jit(solution)/shard_map/ppermute | solution.py:84
  94.8 7.4 %collective-permute-start.29 = (f32[2,2,16,1024]{3,2,1,0:T(8,128)S(1)}, f32[2,2,16,1024]{3,2,1,0:T(8,128)S(1)}, u32[]{:S(2)}, u32[]{:S(2)}) collective-permute-start(f32[2,2,16,1024]{3,2,1,0:T(8,128)S(1)} %bitcast_select_fusion), channel_id=1, source_target_pairs={{0,2},{1,5},{2,0},{3,7},{4,6},{5,1},{6,4},{7,3},{8,10},{9,13},{10,... | collective-permute-start | bytes 786440 | tf_op jit(solution)/shard_map/ppermute | solution.py:84
  98.8 5.4 %collective-permute-start.26 = (f32[2,16,1024]{2,1,0:T(8,128)S(1)}, f32[2,16,1024]{2,1,0:T(8,128)S(1)}, u32[]{:S(2)}, u32[]{:S(2)}) collective-permute-start(f32[2,16,1024]{2,1,0:T(8,128)S(1)} %dynamic-slice_bitcast_fusion.1), channel_id=1, source_target_pairs={{0,4},{1,3},{2,6},{3,1},{4,0},{5,7},{6,2},{7,5},{8,12},{9,11},{10,... | collective-permute-start | bytes 393224 | tf_op jit(solution)/shard_map/ppermute | solution.py:84
  102.3 5.7 %collective-permute-start.30 = (f32[2,16,1024]{2,1,0:T(8,128)S(1)}, f32[2,16,1024]{2,1,0:T(8,128)S(1)}, u32[]{:S(2)}, u32[]{:S(2)}) collective-permute-start(f32[2,16,1024]{2,1,0:T(8,128)S(1)} %dynamic-slice_bitcast_fusion), channel_id=1, source_target_pairs={{0,4},{1,3},{2,6},{3,1},{4,0},{5,7},{6,2},{7,5},{8,12},{9,11},{10,... | collective-permute-start | bytes 393224 | tf_op jit(solution)/shard_map/ppermute | solution.py:84
  104.2 7.4 %collective-permute-start.27 = (f32[16,1024]{1,0:T(8,128)S(1)}, f32[16,1024]{1,0:T(8,128)S(1)}, u32[]{:S(2)}, u32[]{:S(2)}) collective-permute-start(f32[16,1024]{1,0:T(8,128)S(1)} %dynamic-slice_bitcast_fusion.5), channel_id=1, source_target_pairs={{0,8},{1,9},{2,10},{3,11},{4,12},{5,13},{6,14},{7,15},{8,0},{9,1},... | collective-permute-start | bytes 196616 | tf_op jit(solution)/shard_map/ppermute | solution.py:84
  108.1 5.2 %collective-permute-start.31 = (f32[16,1024]{1,0:T(8,128)S(1)}, f32[16,1024]{1,0:T(8,128)S(1)}, u32[]{:S(2)}, u32[]{:S(2)}) collective-permute-start(f32[16,1024]{1,0:T(8,128)S(1)} %dynamic-slice_bitcast_fusion.4), channel_id=1, source_target_pairs={{0,8},{1,9},{2,10},{3,11},{4,12},{5,13},{6,14},{7,15},{8,0},{9,1},... | collective-permute-start | bytes 196616 | tf_op jit(solution)/shard_map/ppermute | solution.py:84

commit v17 on v16

--- a/solution.py
+++ b/solution.py
@@ -193,8 +193,12 @@
     core = (position & 1).astype(jnp.int32).reshape(1)
     own_denom = denom[:, 0, :]
     resps = [rhs[:, state, :] / own_denom for state in range(states)]
+    first = (rhs / denom).astype(jnp.bfloat16)
     for step in range(ITERS):
-        got = [gather_rows(resp.astype(jnp.bfloat16), n) for resp in resps]
+        rounded = [first[:, state, :] for state in range(states)] if step == 0 else [
+            resp.astype(jnp.bfloat16) for resp in resps
+        ]
+        got = [gather_rows(r, n) for r in rounded]
         keep, send = exchange_part(core, ordered_occ, [g[0] for g in got], [g[1] for g in got], vir_ints, rows)
         for state in range(states):
             exchange = scatter_sum(keep[state], send[state], n)

time: 115 us -> 118 us (1.026)
  waiting for transfers between devices: 45.5 us -> 54.9 us
  starting transfers between devices: 38.6 us -> 32.2 us
    ppermute x12, waiting for transfers between devices: 20.8 us -> 27.4 us  [scatter_sum(): acc = kept + lax.ppermute(sent, 'aux', partners(n, b0, b1))]
    ppermute x12, starting transfers between devices: 19.2 us -> 12.7 us  [scatter_sum(): acc = kept + lax.ppermute(sent, 'aux', partners(n, b0, b1))]
    ppermute x12, waiting for transfers between devices: 18.5 us -> 21.3 us  [gather_rows(): theirs = lax.ppermute(acc, 'aux', partners(n, b0, b1))]
  transfers between devices with their start and end apart: 32 -> 32, of which waited for: 26 -> 27; matrix products, arithmetic and copies ran while one was open for 5% -> 5% of each run, Pallas kernels for 0% -> 0%
where the time goes in v17:
time: 118 us; the launch traced here: 117 us
  waiting for transfers between devices  54.9 us (47%)
  starting transfers between devices  32.2 us (27%)
  Pallas kernels  19.2 us (16%)
  other arithmetic  8.09 us (7%)
  local copies, waits for them, and re-layouts  2.33 us (2%)
    ppermute x12, waiting for transfers between devices, scatter_sum(): acc = kept + lax.ppermute(sent, 'aux', partners(n, b0, b1))  27.4 us
    ppermute x12, waiting for transfers between devices, gather_rows(): theirs = lax.ppermute(acc, 'aux', partners(n, b0, b1))  21.3 us
    pallas_call x2, Pallas kernels, exchange_part(): pl.pallas_call(functools.partial(exchange_kernel, states, rows), grid=(lo...  19.2 us
    ppermute x12, starting transfers between devices, gather_rows(): theirs = lax.ppermute(acc, 'aux', partners(n, b0, b1))  18.2 us
    ppermute x12, starting transfers between devices, scatter_sum(): acc = kept + lax.ppermute(sent, 'aux', partners(n, b0, b1))  12.7 us
    add x4, other arithmetic, scatter_sum(): keep.reshape(shape)  4.44 us
    ppermute x4, waiting for transfers between devices, scatter_sum(): lax.ppermute(send, 'aux', partners(n, 0, 0)).reshape(shape)  3.23 us
    ppermute x4, waiting for transfers between devices, gather_rows(): return (flat, lax.ppermute(flat, 'aux', partners(n, 0, 0)))  3.01 us
  transfers between devices with their start and end apart: 32, of which 27 were waited for; matrix products, arithmetic and copies ran while one was open for 5% of the time, Pallas kernels for 0%

profile of v17, /device:TPU:0, one launch (start us, length us, event | category | flops | bytes accessed | tf_op | source)
XLA Modules:
  0.0 117.1 jit_solution(8131580619909431145)
XLA Ops:
  0.0 0.9 select_reduce_fusion
  0.9 0.8 broadcast_subtract_fusion
  1.6 1.0 fusion.22
  2.6 4.1 %collective-permute-start.3 = (bf16[1,16,1024]{2,1,0:T(8,128)(2,1)S(1)}, bf16[1,16,1024]{2,1,0:T(8,128)(2,1)S(1)}, u32[]{:S(2)}, u32[]{:S(2)}) collective-permute-start(bf16[1,16,1024]{2,1,0:T(8,128)(2,1)S(1)} %get-tuple-element.57), channel_id=1, source_target_pairs={{0,8},{1,9},{2,10},{3,11},{4,12},{5,13},{6,14},{7,15},{8,0},{9,1},... | collective-permute-start | bytes 98312 | tf_op jit(solution)/shard_map/ppermute | solution.py:36
  6.8 2.2 %collective-permute-done.3 = bf16[1,16,1024]{2,1,0:T(8,128)(2,1)S(1)} collective-permute-done((bf16[1,16,1024]{2,1,0:T(8,128)(2,1)S(1)}, bf16[1,16,1024]{2,1,0:T(8,128)(2,1)S(1)}, u32[]{:S(2)}, u32[]{:S(2)}) %collective-permute-start.3) | collective-permute-done | bytes 32800 | tf_op jit(solution)/shard_map/ppermute | solution.py:36
  8.9 2.6 %collective-permute-done = bf16[1,16,1024]{2,1,0:T(8,128)(2,1)S(1)} collective-permute-done((bf16[1,16,1024]{2,1,0:T(8,128)(2,1)S(1)}, bf16[1,16,1024]{2,1,0:T(8,128)(2,1)S(1)}, u32[]{:S(2)}, u32[]{:S(2)}) %collective-permute-start) | collective-permute-done | bytes 32800 | tf_op jit(solution)/shard_map/ppermute | solution.py:36
  11.5 1.6 %collective-permute-start.1 = (bf16[2,16,1024]{2,1,0:T(8,128)(2,1)S(1)}, bf16[2,16,1024]{2,1,0:T(8,128)(2,1)S(1)}, u32[]{:S(2)}, u32[]{:S(2)}) collective-permute-start(bf16[2,16,1024]{2,1,0:T(8,128)(2,1)S(1)} %pad_maximum_fusion.5), channel_id=1, source_target_pairs={{0,4},{1,3},{2,6},{3,1},{4,0},{5,7},{6,2},{7,5},{8,12},{9,11},{10,... | collective-permute-start | bytes 196616 | tf_op jit(solution)/shard_map/ppermute | solution.py:36
  13.2 0.5 collective-permute-start.4
  13.7 2.2 %collective-permute-done.1 = bf16[2,16,1024]{2,1,0:T(8,128)(2,1)S(1)} collective-permute-done((bf16[2,16,1024]{2,1,0:T(8,128)(2,1)S(1)}, bf16[2,16,1024]{2,1,0:T(8,128)(2,1)S(1)}, u32[]{:S(2)}, u32[]{:S(2)}) %collective-permute-start.1) | collective-permute-done | bytes 65568 | tf_op jit(solution)/shard_map/ppermute | solution.py:36
  15.9 1.6 %collective-permute-start.2 = (bf16[4,16,1024]{2,1,0:T(8,128)(2,1)S(1)}, bf16[4,16,1024]{2,1,0:T(8,128)(2,1)S(1)}, u32[]{:S(2)}, u32[]{:S(2)}) collective-permute-start(bf16[4,16,1024]{2,1,0:T(8,128)(2,1)S(1)} %bitcast.251), channel_id=1, source_target_pairs={{0,2},{1,5},{2,0},{3,7},{4,6},{5,1},{6,4},{7,3},{8,10},{9,13},{10,... | collective-permute-start | bytes 393224 | tf_op jit(solution)/shard_map/ppermute | solution.py:36
  17.5 0.7 collective-permute-done.4
  18.3 1.6 %collective-permute-start.5 = (bf16[4,16,1024]{2,1,0:T(8,128)(2,1)S(1)}, bf16[4,16,1024]{2,1,0:T(8,128)(2,1)S(1)}, u32[]{:S(2)}, u32[]{:S(2)}) collective-permute-start(bf16[4,16,1024]{2,1,0:T(8,128)(2,1)S(1)} %bitcast.253), channel_id=1, source_target_pairs={{0,2},{1,5},{2,0},{3,7},{4,6},{5,1},{6,4},{7,3},{8,10},{9,13},{10,... | collective-permute-start | bytes 393224 | tf_op jit(solution)/shard_map/ppermute | solution.py:36
  19.8 1.1 collective-permute-done.2
  21.1 2.2 %collective-permute-done.5 = bf16[4,16,1024]{2,1,0:T(8,128)(2,1)S(1)} collective-permute-done((bf16[4,16,1024]{2,1,0:T(8,128)(2,1)S(1)}, bf16[4,16,1024]{2,1,0:T(8,128)(2,1)S(1)}, u32[]{:S(2)}, u32[]{:S(2)}) %collective-permute-start.5) | collective-permute-done | bytes 131104 | tf_op jit(solution)/shard_map/ppermute | solution.py:36
  23.5 1.5 %collective-permute-done.7.refs_3_ = bf16[128,1024]{1,0:T(8,128)(2,1)S(1)} collective-permute-done((bf16[128,1024]{1,0:T(8,128)(2,1)S(1)}, bf16[128,1024]{1,0:T(8,128)(2,1)S(1)}, u32[]{:S(2)}, u32[]{:S(2)}) %collective-permute-start.7) | collective-permute-done | bytes 262176 | tf_op jit(solution)/shard_map/ppermute | solution.py:53
  25.0 0.7 copy-done.7
  25.7 9.6 %shard_map.55 = (f32[128,1024]{1,0:T(8,128)}, f32[128,1024]{1,0:T(8,128)}, f32[128,1024]{1,0:T(8,128)}, f32[128,1024]{1,0:T(8,128)}) custom-call(s32[1]{0:T(128)} %bitcast.1.core_ref, bf16[4,256,256]{2,1,0:T(8,128)(2,1)} %occ_ref.3, bf16[128,1024]{1,0:T(8,128)(2,1)} %bitcast.246, bf16[128,1024]{1,0:T(8,128)(2,1)} %bitcast.250, bf16[128,1024]{1,0:T(8,128)(2,1)} %copy-done.5, ...), custom_call_target="tpu_custom_call" | custom-call | tf_op jit(solution)/shard_map/pallas_call | solution.py:140
  35.4 0.4 collective-permute-start.15
  35.8 1.6 %collective-permute-done.8 = f32[128,1024]{1,0:T(8,128)S(1)} collective-permute-done((f32[128,1024]{1,0:T(8,128)}, f32[128,1024]{1,0:T(8,128)S(1)}, u32[]{:S(2)}, u32[]{:S(2)}) %collective-permute-start.8) | collective-permute-done | bytes 524320 | tf_op jit(solution)/shard_map/ppermute | solution.py:63
  37.4 1.1 add.140
  38.5 1.6 %collective-permute-start.9 = (f32[2,2,16,1024]{3,2,1,0:T(8,128)S(1)}, f32[2,2,16,1024]{3,2,1,0:T(8,128)S(1)}, u32[]{:S(2)}, u32[]{:S(2)}) collective-permute-start(f32[2,2,16,1024]{3,2,1,0:T(8,128)S(1)} %bitcast_select_fusion.6), channel_id=1, source_target_pairs={{0,2},{1,5},{2,0},{3,7},{4,6},{5,1},{6,4},{7,3},{8,10},{9,13},{10,... | collective-permute-start | bytes 786440 | tf_op jit(solution)/shard_map/ppermute | solution.py:84
  40.1 1.1 add.154
  41.2 0.6 collective-permute-start.16
  41.9 3.1 %collective-permute-done.9 = f32[2,2,16,1024]{3,2,1,0:T(8,128)S(1)} collective-permute-done((f32[2,2,16,1024]{3,2,1,0:T(8,128)S(1)}, f32[2,2,16,1024]{3,2,1,0:T(8,128)S(1)}, u32[]{:S(2)}, u32[]{:S(2)}) %collective-permute-start.9) | collective-permute-done | bytes 262176 | tf_op jit(solution)/shard_map/ppermute | solution.py:84
  45.1 1.0 collective-permute-start.10
  46.1 2.4 %collective-permute-done.16 = f32[2,2,16,1024]{3,2,1,0:T(8,128)S(1)} collective-permute-done((f32[2,2,16,1024]{3,2,1,0:T(8,128)S(1)}, f32[2,2,16,1024]{3,2,1,0:T(8,128)S(1)}, u32[]{:S(2)}, u32[]{:S(2)}) %collective-permute-start.16) | collective-permute-done | bytes 262176 | tf_op jit(solution)/shard_map/ppermute | solution.py:84
  48.6 1.0 collective-permute-start.17
  49.6 0.5 collective-permute-done.10
  50.1 1.2 %collective-permute-start.11 = (f32[16,1024]{1,0:T(8,128)S(1)}, f32[16,1024]{1,0:T(8,128)S(1)}, u32[]{:S(2)}, u32[]{:S(2)}) collective-permute-start(f32[16,1024]{1,0:T(8,128)S(1)} %dynamic-slice_bitcast_fusion.7), channel_id=1, source_target_pairs={{0,8},{1,9},{2,10},{3,11},{4,12},{5,13},{6,14},{7,15},{8,0},{9,1},... | collective-permute-start | bytes 196616 | tf_op jit(solution)/shard_map/ppermute | solution.py:84
  51.3 3.0 %collective-permute-done.17 = f32[2,16,1024]{2,1,0:T(8,128)S(1)} collective-permute-done((f32[2,16,1024]{2,1,0:T(8,128)S(1)}, f32[2,16,1024]{2,1,0:T(8,128)S(1)}, u32[]{:S(2)}, u32[]{:S(2)}) %collective-permute-start.17) | collective-permute-done | bytes 131104 | tf_op jit(solution)/shard_map/ppermute | solution.py:84
  54.4 1.2 %collective-permute-start.18 = (f32[16,1024]{1,0:T(8,128)S(1)}, f32[16,1024]{1,0:T(8,128)S(1)}, u32[]{:S(2)}, u32[]{:S(2)}) collective-permute-start(f32[16,1024]{1,0:T(8,128)S(1)} %dynamic-slice_bitcast_fusion.6), channel_id=1, source_target_pairs={{0,8},{1,9},{2,10},{3,11},{4,12},{5,13},{6,14},{7,15},{8,0},{9,1},... | collective-permute-start | bytes 196616 | tf_op jit(solution)/shard_map/ppermute | solution.py:84
  55.6 1.9 %collective-permute-done.11 = f32[16,1024]{1,0:T(8,128)S(1)} collective-permute-done((f32[16,1024]{1,0:T(8,128)S(1)}, f32[16,1024]{1,0:T(8,128)S(1)}, u32[]{:S(2)}, u32[]{:S(2)}) %collective-permute-start.11) | collective-permute-done | bytes 65568 | tf_op jit(solution)/shard_map/ppermute | solution.py:84
  57.4 2.2 %collective-permute-done.18 = f32[16,1024]{1,0:T(8,128)S(1)} collective-permute-done((f32[16,1024]{1,0:T(8,128)S(1)}, f32[16,1024]{1,0:T(8,128)S(1)}, u32[]{:S(2)}, u32[]{:S(2)}) %collective-permute-start.18) | collective-permute-done | bytes 65568 | tf_op jit(solution)/shard_map/ppermute | solution.py:84
  59.7 1.3 %collective-permute-start.19 = (bf16[1,16,1024]{2,1,0:T(8,128)(2,1)S(1)}, bf16[1,16,1024]{2,1,0:T(8,128)(2,1)S(1)}, u32[]{:S(2)}, u32[]{:S(2)}) collective-permute-start(bf16[1,16,1024]{2,1,0:T(8,128)(2,1)S(1)} %get-tuple-element.21), channel_id=1, source_target_pairs={{0,8},{1,9},{2,10},{3,11},{4,12},{5,13},{6,14},{7,15},{8,0},{9,1},... | collective-permute-start | bytes 98312 | tf_op jit(solution)/shard_map/ppermute | solution.py:36
  61.0 1.7 %collective-permute-start.12 = (bf16[1,16,1024]{2,1,0:T(8,128)(2,1)S(1)}, bf16[1,16,1024]{2,1,0:T(8,128)(2,1)S(1)}, u32[]{:S(2)}, u32[]{:S(2)}) collective-permute-start(bf16[1,16,1024]{2,1,0:T(8,128)(2,1)S(1)} %get-tuple-element.35), channel_id=1, source_target_pairs={{0,8},{1,9},{2,10},{3,11},{4,12},{5,13},{6,14},{7,15},{8,0},{9,1},... | collective-permute-start | bytes 98312 | tf_op jit(solution)/shard_map/ppermute | solution.py:36
  62.7 1.9 %collective-permute-done.19 = bf16[1,16,1024]{2,1,0:T(8,128)(2,1)S(1)} collective-permute-done((bf16[1,16,1024]{2,1,0:T(8,128)(2,1)S(1)}, bf16[1,16,1024]{2,1,0:T(8,128)(2,1)S(1)}, u32[]{:S(2)}, u32[]{:S(2)}) %collective-permute-start.19) | collective-permute-done | bytes 32800 | tf_op jit(solution)/shard_map/ppermute | solution.py:36
  64.6 1.4 %collective-permute-start.20 = (bf16[2,16,1024]{2,1,0:T(8,128)(2,1)S(1)}, bf16[2,16,1024]{2,1,0:T(8,128)(2,1)S(1)}, u32[]{:S(2)}, u32[]{:S(2)}) collective-permute-start(bf16[2,16,1024]{2,1,0:T(8,128)(2,1)S(1)} %pad_maximum_fusion.8), channel_id=1, source_target_pairs={{0,4},{1,3},{2,6},{3,1},{4,0},{5,7},{6,2},{7,5},{8,12},{9,11},{10,... | collective-permute-start | bytes 196616 | tf_op jit(solution)/shard_map/ppermute | solution.py:36
  66.1 1.3 %collective-permute-start.13 = (bf16[2,16,1024]{2,1,0:T(8,128)(2,1)S(1)}, bf16[2,16,1024]{2,1,0:T(8,128)(2,1)S(1)}, u32[]{:S(2)}, u32[]{:S(2)}) collective-permute-start(bf16[2,16,1024]{2,1,0:T(8,128)(2,1)S(1)} %pad_maximum_fusion.7), channel_id=1, source_target_pairs={{0,4},{1,3},{2,6},{3,1},{4,0},{5,7},{6,2},{7,5},{8,12},{9,11},{10,... | collective-permute-start | bytes 196616 | tf_op jit(solution)/shard_map/ppermute | solution.py:36
  67.5 1.9 %collective-permute-done.20 = bf16[2,16,1024]{2,1,0:T(8,128)(2,1)S(1)} collective-permute-done((bf16[2,16,1024]{2,1,0:T(8,128)(2,1)S(1)}, bf16[2,16,1024]{2,1,0:T(8,128)(2,1)S(1)}, u32[]{:S(2)}, u32[]{:S(2)}) %collective-permute-start.20) | collective-permute-done | bytes 65568 | tf_op jit(solution)/shard_map/ppermute | solution.py:36
  69.3 1.8 %collective-permute-done.13 = bf16[2,16,1024]{2,1,0:T(8,128)(2,1)S(1)} collective-permute-done((bf16[2,16,1024]{2,1,0:T(8,128)(2,1)S(1)}, bf16[2,16,1024]{2,1,0:T(8,128)(2,1)S(1)}, u32[]{:S(2)}, u32[]{:S(2)}) %collective-permute-start.13) | collective-permute-done | bytes 65568 | tf_op jit(solution)/shard_map/ppermute | solution.py:36
  71.2 2.9 %collective-permute-start.21 = (bf16[4,16,1024]{2,1,0:T(8,128)(2,1)S(1)}, bf16[4,16,1024]{2,1,0:T(8,128)(2,1)S(1)}, u32[]{:S(2)}, u32[]{:S(2)}) collective-permute-start(bf16[4,16,1024]{2,1,0:T(8,128)(2,1)S(1)} %bitcast.254), channel_id=1, source_target_pairs={{0,2},{1,5},{2,0},{3,7},{4,6},{5,1},{6,4},{7,3},{8,10},{9,13},{10,... | collective-permute-start | bytes 393224 | tf_op jit(solution)/shard_map/ppermute | solution.py:36
  74.3 2.8 %collective-permute-done.21 = bf16[4,16,1024]{2,1,0:T(8,128)(2,1)S(1)} collective-permute-done((bf16[4,16,1024]{2,1,0:T(8,128)(2,1)S(1)}, bf16[4,16,1024]{2,1,0:T(8,128)(2,1)S(1)}, u32[]{:S(2)}, u32[]{:S(2)}) %collective-permute-start.21) | collective-permute-done | bytes 131104 | tf_op jit(solution)/shard_map/ppermute | solution.py:36
  77.3 1.9 %collective-permute-done.14 = bf16[4,16,1024]{2,1,0:T(8,128)(2,1)S(1)} collective-permute-done((bf16[4,16,1024]{2,1,0:T(8,128)(2,1)S(1)}, bf16[4,16,1024]{2,1,0:T(8,128)(2,1)S(1)}, u32[]{:S(2)}, u32[]{:S(2)}) %collective-permute-start.14) | collective-permute-done | bytes 131104 | tf_op jit(solution)/shard_map/ppermute | solution.py:36
  79.4 1.5 %collective-permute-done.22.refs_2_ = bf16[128,1024]{1,0:T(8,128)(2,1)S(1)} collective-permute-done((bf16[128,1024]{1,0:T(8,128)(2,1)S(1)}, bf16[128,1024]{1,0:T(8,128)(2,1)S(1)}, u32[]{:S(2)}, u32[]{:S(2)}) %collective-permute-start.22) | collective-permute-done | bytes 262176 | tf_op jit(solution)/shard_map/ppermute | solution.py:53
  80.9 0.7 copy-done.6
  81.6 9.6 %shard_map.56 = (f32[128,1024]{1,0:T(8,128)}, f32[128,1024]{1,0:T(8,128)}, f32[128,1024]{1,0:T(8,128)}, f32[128,1024]{1,0:T(8,128)}) custom-call(s32[1]{0:T(128)} %bitcast.1.core_ref, bf16[4,256,256]{2,1,0:T(8,128)(2,1)} %occ_ref.3, bf16[128,1024]{1,0:T(8,128)(2,1)} %bitcast.248, bf16[128,1024]{1,0:T(8,128)(2,1)} %bitcast.244, bf16[128,1024]{1,0:T(8,128)(2,1)} %copy-done.6, ...), custom_call_target="tpu_custom_call" | custom-call | tf_op jit(solution)/shard_map/pallas_call | solution.py:140
  91.2 0.1 collective-permute-start.24
  91.3 0.4 collective-permute-start.28
  91.7 1.6 %collective-permute-done.24 = f32[128,1024]{1,0:T(8,128)S(1)} collective-permute-done((f32[128,1024]{1,0:T(8,128)}, f32[128,1024]{1,0:T(8,128)S(1)}, u32[]{:S(2)}, u32[]{:S(2)}) %collective-permute-start.24) | collective-permute-done | bytes 524320 | tf_op jit(solution)/shard_map/ppermute | solution.py:63
  93.3 1.1 add.160
  94.5 1.4 %collective-permute-start.25 = (f32[2,2,16,1024]{3,2,1,0:T(8,128)S(1)}, f32[2,2,16,1024]{3,2,1,0:T(8,128)S(1)}, u32[]{:S(2)}, u32[]{:S(2)}) collective-permute-start(f32[2,2,16,1024]{3,2,1,0:T(8,128)S(1)} %bitcast_select_fusion.2), channel_id=1, source_target_pairs={{0,2},{1,5},{2,0},{3,7},{4,6},{5,1},{6,4},{7,3},{8,10},{9,13},{10,... | collective-permute-start | bytes 786440 | tf_op jit(solution)/shard_map/ppermute | solution.py:84
  95.8 1.1 add.166
  97.0 0.8 collective-permute-start.29
  97.8 3.1 %collective-permute-done.25 = f32[2,2,16,1024]{3,2,1,0:T(8,128)S(1)} collective-permute-done((f32[2,2,16,1024]{3,2,1,0:T(8,128)S(1)}, f32[2,2,16,1024]{3,2,1,0:T(8,128)S(1)}, u32[]{:S(2)}, u32[]{:S(2)}) %collective-permute-start.25) | collective-permute-done | bytes 262176 | tf_op jit(solution)/shard_map/ppermute | solution.py:84
  101.0 0.8 collective-permute-start.26
  101.8 2.7 %collective-permute-done.29 = f32[2,2,16,1024]{3,2,1,0:T(8,128)S(1)} collective-permute-done((f32[2,2,16,1024]{3,2,1,0:T(8,128)S(1)}, f32[2,2,16,1024]{3,2,1,0:T(8,128)S(1)}, u32[]{:S(2)}, u32[]{:S(2)}) %collective-permute-start.29) | collective-permute-done | bytes 262176 | tf_op jit(solution)/shard_map/ppermute | solution.py:84
  104.5 0.8 collective-permute-start.30
  105.3 0.7 collective-permute-done.26
  106.1 1.2 collective-permute-start.27
  107.2 3.0 %collective-permute-done.30 = f32[2,16,1024]{2,1,0:T(8,128)S(1)} collective-permute-done((f32[2,16,1024]{2,1,0:T(8,128)S(1)}, f32[2,16,1024]{2,1,0:T(8,128)S(1)}, u32[]{:S(2)}, u32[]{:S(2)}) %collective-permute-start.30) | collective-permute-done | bytes 131104 | tf_op jit(solution)/shard_map/ppermute | solution.py:84
  110.3 1.2 collective-permute-start.31
  111.4 1.9 %collective-permute-done.27 = f32[16,1024]{1,0:T(8,128)S(1)} collective-permute-done((f32[16,1024]{1,0:T(8,128)S(1)}, f32[16,1024]{1,0:T(8,128)S(1)}, u32[]{:S(2)}, u32[]{:S(2)}) %collective-permute-start.27) | collective-permute-done | bytes 65568 | tf_op jit(solution)/shard_map/ppermute | solution.py:84
  113.4 2.9 %collective-permute-done.31 = f32[16,1024]{1,0:T(8,128)S(1)} collective-permute-done((f32[16,1024]{1,0:T(8,128)S(1)}, f32[16,1024]{1,0:T(8,128)S(1)}, u32[]{:S(2)}, u32[]{:S(2)}) %collective-permute-start.31) | collective-permute-done | bytes 65568 | tf_op jit(solution)/shard_map/ppermute | solution.py:84
  116.3 0.8 copy.57
  (78 shorter events, 1.9 us)
Async XLA Ops:
  2.6 6.3 %collective-permute-start.3 = (bf16[1,16,1024]{2,1,0:T(8,128)(2,1)S(1)}, bf16[1,16,1024]{2,1,0:T(8,128)(2,1)S(1)}, u32[]{:S(2)}, u32[]{:S(2)}) collective-permute-start(bf16[1,16,1024]{2,1,0:T(8,128)(2,1)S(1)} %get-tuple-element.57), channel_id=1, source_target_pairs={{0,8},{1,9},{2,10},{3,11},{4,12},{5,13},{6,14},{7,15},{8,0},{9,1},... | collective-permute-start | bytes 98312 | tf_op jit(solution)/shard_map/ppermute | solution.py:36
  6.7 4.8 %collective-permute-start = (bf16[1,16,1024]{2,1,0:T(8,128)(2,1)S(1)}, bf16[1,16,1024]{2,1,0:T(8,128)(2,1)S(1)}, u32[]{:S(2)}, u32[]{:S(2)}) collective-permute-start(bf16[1,16,1024]{2,1,0:T(8,128)(2,1)S(1)} %get-tuple-element.58), channel_id=1, source_target_pairs={{0,8},{1,9},{2,10},{3,11},{4,12},{5,13},{6,14},{7,15},{8,0},{9,1},... | collective-permute-start | bytes 98312 | tf_op jit(solution)/shard_map/ppermute | solution.py:36
  11.5 4.3 %collective-permute-start.1 = (bf16[2,16,1024]{2,1,0:T(8,128)(2,1)S(1)}, bf16[2,16,1024]{2,1,0:T(8,128)(2,1)S(1)}, u32[]{:S(2)}, u32[]{:S(2)}) collective-permute-start(bf16[2,16,1024]{2,1,0:T(8,128)(2,1)S(1)} %pad_maximum_fusion.5), channel_id=1, source_target_pairs={{0,4},{1,3},{2,6},{3,1},{4,0},{5,7},{6,2},{7,5},{8,12},{9,11},{10,... | collective-permute-start | bytes 196616 | tf_op jit(solution)/shard_map/ppermute | solution.py:36
  13.2 5.0 %collective-permute-start.4 = (bf16[2,16,1024]{2,1,0:T(8,128)(2,1)S(1)}, bf16[2,16,1024]{2,1,0:T(8,128)(2,1)S(1)}, u32[]{:S(2)}, u32[]{:S(2)}) collective-permute-start(bf16[2,16,1024]{2,1,0:T(8,128)(2,1)S(1)} %pad_maximum_fusion.6), channel_id=1, source_target_pairs={{0,4},{1,3},{2,6},{3,1},{4,0},{5,7},{6,2},{7,5},{8,12},{9,11},{10,... | collective-permute-start | bytes 196616 | tf_op jit(solution)/shard_map/ppermute | solution.py:36
  15.9 5.0 %collective-permute-start.2 = (bf16[4,16,1024]{2,1,0:T(8,128)(2,1)S(1)}, bf16[4,16,1024]{2,1,0:T(8,128)(2,1)S(1)}, u32[]{:S(2)}, u32[]{:S(2)}) collective-permute-start(bf16[4,16,1024]{2,1,0:T(8,128)(2,1)S(1)} %bitcast.251), channel_id=1, source_target_pairs={{0,2},{1,5},{2,0},{3,7},{4,6},{5,1},{6,4},{7,3},{8,10},{9,13},{10,... | collective-permute-start | bytes 393224 | tf_op jit(solution)/shard_map/ppermute | solution.py:36
  18.3 5.0 %collective-permute-start.5 = (bf16[4,16,1024]{2,1,0:T(8,128)(2,1)S(1)}, bf16[4,16,1024]{2,1,0:T(8,128)(2,1)S(1)}, u32[]{:S(2)}, u32[]{:S(2)}) collective-permute-start(bf16[4,16,1024]{2,1,0:T(8,128)(2,1)S(1)} %bitcast.253), channel_id=1, source_target_pairs={{0,2},{1,5},{2,0},{3,7},{4,6},{5,1},{6,4},{7,3},{8,10},{9,13},{10,... | collective-permute-start | bytes 393224 | tf_op jit(solution)/shard_map/ppermute | solution.py:36
  21.0 3.9 %copy-start.1 = (bf16[2,2,2,16,1024]{4,3,2,1,0:T(8,128)(2,1)}, bf16[2,2,2,16,1024]{4,3,2,1,0:T(8,128)(2,1)S(1)}, u32[]{:S(2)}) copy-start(bf16[2,2,2,16,1024]{4,3,2,1,0:T(8,128)(2,1)S(1)} %maximum_select_fusion) | copy-start | bytes 786436
  21.1 2.4 %collective-permute-start.6 = (bf16[128,1024]{1,0:T(8,128)(2,1)S(1)}, bf16[128,1024]{1,0:T(8,128)(2,1)S(1)}, u32[]{:S(2)}, u32[]{:S(2)}) collective-permute-start(bf16[128,1024]{1,0:T(8,128)(2,1)S(1)} %bitcast.245), channel_id=1, source_target_pairs={{0,1},{1,0},{2,3},{3,2},{4,5},{5,4},{6,7},{7,6},{8,9},{9,8},{10,11... | collective-permute-start | bytes 786440 | tf_op jit(solution)/shard_map/ppermute | solution.py:53
  23.4 1.6 %copy-start.3 = (bf16[2,2,2,16,1024]{4,3,2,1,0:T(8,128)(2,1)}, bf16[2,2,2,16,1024]{4,3,2,1,0:T(8,128)(2,1)S(1)}, u32[]{:S(2)}) copy-start(bf16[2,2,2,16,1024]{4,3,2,1,0:T(8,128)(2,1)S(1)} %maximum_select_fusion.1) | copy-start | bytes 786436
  23.4 1.6 %collective-permute-start.7 = (bf16[128,1024]{1,0:T(8,128)(2,1)S(1)}, bf16[128,1024]{1,0:T(8,128)(2,1)S(1)}, u32[]{:S(2)}, u32[]{:S(2)}) collective-permute-start(bf16[128,1024]{1,0:T(8,128)(2,1)S(1)} %bitcast.249), channel_id=1, source_target_pairs={{0,1},{1,0},{2,3},{3,2},{4,5},{5,4},{6,7},{7,6},{8,9},{9,8},{10,11... | collective-permute-start | bytes 786440 | tf_op jit(solution)/shard_map/ppermute | solution.py:53
  23.5 1.5 %copy-start.5 = (bf16[128,1024]{1,0:T(8,128)(2,1)}, bf16[128,1024]{1,0:T(8,128)(2,1)S(1)}, u32[]{:S(2)}) copy-start(bf16[128,1024]{1,0:T(8,128)(2,1)S(1)} %collective-permute-done.6.refs_2_) | copy-start | bytes 786436
  25.0 0.7 copy-start.7
  25.7 33.9 %copy-start.8 = (f32[1024]{0:T(1024)S(1)}, f32[1024]{0:T(1024)}, u32[]{:S(2)}) copy-start(f32[1024]{0:T(1024)} %param.7) | copy-start | bytes 12292
  35.3 2.1 %collective-permute-start.8 = (f32[128,1024]{1,0:T(8,128)}, f32[128,1024]{1,0:T(8,128)S(1)}, u32[]{:S(2)}, u32[]{:S(2)}) collective-permute-start(f32[128,1024]{1,0:T(8,128)} %get-tuple-element.14), channel_id=1, source_target_pairs={{0,1},{1,0},{2,3},{3,2},{4,5},{5,4},{6,7},{7,6},{8,9},{9,8},{10,11... | collective-permute-start | bytes 1572872 | tf_op jit(solution)/shard_map/ppermute | solution.py:63
  35.4 4.7 %collective-permute-start.15 = (f32[128,1024]{1,0:T(8,128)}, f32[128,1024]{1,0:T(8,128)S(1)}, u32[]{:S(2)}, u32[]{:S(2)}) collective-permute-start(f32[128,1024]{1,0:T(8,128)} %get-tuple-element.16), channel_id=1, source_target_pairs={{0,1},{1,0},{2,3},{3,2},{4,5},{5,4},{6,7},{7,6},{8,9},{9,8},{10,11... | collective-permute-start | bytes 1572872 | tf_op jit(solution)/shard_map/ppermute | solution.py:63
  38.5 6.4 %collective-permute-start.9 = (f32[2,2,16,1024]{3,2,1,0:T(8,128)S(1)}, f32[2,2,16,1024]{3,2,1,0:T(8,128)S(1)}, u32[]{:S(2)}, u32[]{:S(2)}) collective-permute-start(f32[2,2,16,1024]{3,2,1,0:T(8,128)S(1)} %bitcast_select_fusion.6), channel_id=1, source_target_pairs={{0,2},{1,5},{2,0},{3,7},{4,6},{5,1},{6,4},{7,3},{8,10},{9,13},{10,... | collective-permute-start | bytes 786440 | tf_op jit(solution)/shard_map/ppermute | solution.py:84
  41.2 7.3 %collective-permute-start.16 = (f32[2,2,16,1024]{3,2,1,0:T(8,128)S(1)}, f32[2,2,16,1024]{3,2,1,0:T(8,128)S(1)}, u32[]{:S(2)}, u32[]{:S(2)}) collective-permute-start(f32[2,2,16,1024]{3,2,1,0:T(8,128)S(1)} %bitcast_select_fusion.4), channel_id=1, source_target_pairs={{0,2},{1,5},{2,0},{3,7},{4,6},{5,1},{6,4},{7,3},{8,10},{9,13},{10,... | collective-permute-start | bytes 786440 | tf_op jit(solution)/shard_map/ppermute | solution.py:84
  45.1 5.0 %collective-permute-start.10 = (f32[2,16,1024]{2,1,0:T(8,128)S(1)}, f32[2,16,1024]{2,1,0:T(8,128)S(1)}, u32[]{:S(2)}, u32[]{:S(2)}) collective-permute-start(f32[2,16,1024]{2,1,0:T(8,128)S(1)} %dynamic-slice_bitcast_fusion.3), channel_id=1, source_target_pairs={{0,4},{1,3},{2,6},{3,1},{4,0},{5,7},{6,2},{7,5},{8,12},{9,11},{10,... | collective-permute-start | bytes 393224 | tf_op jit(solution)/shard_map/ppermute | solution.py:84
  48.6 5.7 %collective-permute-start.17 = (f32[2,16,1024]{2,1,0:T(8,128)S(1)}, f32[2,16,1024]{2,1,0:T(8,128)S(1)}, u32[]{:S(2)}, u32[]{:S(2)}) collective-permute-start(f32[2,16,1024]{2,1,0:T(8,128)S(1)} %dynamic-slice_bitcast_fusion.2), channel_id=1, source_target_pairs={{0,4},{1,3},{2,6},{3,1},{4,0},{5,7},{6,2},{7,5},{8,12},{9,11},{10,... | collective-permute-start | bytes 393224 | tf_op jit(solution)/shard_map/ppermute | solution.py:84
  50.1 7.3 %collective-permute-start.11 = (f32[16,1024]{1,0:T(8,128)S(1)}, f32[16,1024]{1,0:T(8,128)S(1)}, u32[]{:S(2)}, u32[]{:S(2)}) collective-permute-start(f32[16,1024]{1,0:T(8,128)S(1)} %dynamic-slice_bitcast_fusion.7), channel_id=1, source_target_pairs={{0,8},{1,9},{2,10},{3,11},{4,12},{5,13},{6,14},{7,15},{8,0},{9,1},... | collective-permute-start | bytes 196616 | tf_op jit(solution)/shard_map/ppermute | solution.py:84
  54.4 5.2 %collective-permute-start.18 = (f32[16,1024]{1,0:T(8,128)S(1)}, f32[16,1024]{1,0:T(8,128)S(1)}, u32[]{:S(2)}, u32[]{:S(2)}) collective-permute-start(f32[16,1024]{1,0:T(8,128)S(1)} %dynamic-slice_bitcast_fusion.6), channel_id=1, source_target_pairs={{0,8},{1,9},{2,10},{3,11},{4,12},{5,13},{6,14},{7,15},{8,0},{9,1},... | collective-permute-start | bytes 196616 | tf_op jit(solution)/shard_map/ppermute | solution.py:84
  59.7 4.9 %collective-permute-start.19 = (bf16[1,16,1024]{2,1,0:T(8,128)(2,1)S(1)}, bf16[1,16,1024]{2,1,0:T(8,128)(2,1)S(1)}, u32[]{:S(2)}, u32[]{:S(2)}) collective-permute-start(bf16[1,16,1024]{2,1,0:T(8,128)(2,1)S(1)} %get-tuple-element.21), channel_id=1, source_target_pairs={{0,8},{1,9},{2,10},{3,11},{4,12},{5,13},{6,14},{7,15},{8,0},{9,1},... | collective-permute-start | bytes 98312 | tf_op jit(solution)/shard_map/ppermute | solution.py:36
  61.0 5.1 %collective-permute-start.12 = (bf16[1,16,1024]{2,1,0:T(8,128)(2,1)S(1)}, bf16[1,16,1024]{2,1,0:T(8,128)(2,1)S(1)}, u32[]{:S(2)}, u32[]{:S(2)}) collective-permute-start(bf16[1,16,1024]{2,1,0:T(8,128)(2,1)S(1)} %get-tuple-element.35), channel_id=1, source_target_pairs={{0,8},{1,9},{2,10},{3,11},{4,12},{5,13},{6,14},{7,15},{8,0},{9,1},... | collective-permute-start | bytes 98312 | tf_op jit(solution)/shard_map/ppermute | solution.py:36
  64.6 4.7 %collective-permute-start.20 = (bf16[2,16,1024]{2,1,0:T(8,128)(2,1)S(1)}, bf16[2,16,1024]{2,1,0:T(8,128)(2,1)S(1)}, u32[]{:S(2)}, u32[]{:S(2)}) collective-permute-start(bf16[2,16,1024]{2,1,0:T(8,128)(2,1)S(1)} %pad_maximum_fusion.8), channel_id=1, source_target_pairs={{0,4},{1,3},{2,6},{3,1},{4,0},{5,7},{6,2},{7,5},{8,12},{9,11},{10,... | collective-permute-start | bytes 196616 | tf_op jit(solution)/shard_map/ppermute | solution.py:36
  66.1 5.0 %collective-permute-start.13 = (bf16[2,16,1024]{2,1,0:T(8,128)(2,1)S(1)}, bf16[2,16,1024]{2,1,0:T(8,128)(2,1)S(1)}, u32[]{:S(2)}, u32[]{:S(2)}) collective-permute-start(bf16[2,16,1024]{2,1,0:T(8,128)(2,1)S(1)} %pad_maximum_fusion.7), channel_id=1, source_target_pairs={{0,4},{1,3},{2,6},{3,1},{4,0},{5,7},{6,2},{7,5},{8,12},{9,11},{10,... | collective-permute-start | bytes 196616 | tf_op jit(solution)/shard_map/ppermute | solution.py:36
  71.2 5.9 %collective-permute-start.21 = (bf16[4,16,1024]{2,1,0:T(8,128)(2,1)S(1)}, bf16[4,16,1024]{2,1,0:T(8,128)(2,1)S(1)}, u32[]{:S(2)}, u32[]{:S(2)}) collective-permute-start(bf16[4,16,1024]{2,1,0:T(8,128)(2,1)S(1)} %bitcast.254), channel_id=1, source_target_pairs={{0,2},{1,5},{2,0},{3,7},{4,6},{5,1},{6,4},{7,3},{8,10},{9,13},{10,... | collective-permute-start | bytes 393224 | tf_op jit(solution)/shard_map/ppermute | solution.py:36
  74.2 5.0 %collective-permute-start.14 = (bf16[4,16,1024]{2,1,0:T(8,128)(2,1)S(1)}, bf16[4,16,1024]{2,1,0:T(8,128)(2,1)S(1)}, u32[]{:S(2)}, u32[]{:S(2)}) collective-permute-start(bf16[4,16,1024]{2,1,0:T(8,128)(2,1)S(1)} %bitcast.252), channel_id=1, source_target_pairs={{0,2},{1,5},{2,0},{3,7},{4,6},{5,1},{6,4},{7,3},{8,10},{9,13},{10,... | collective-permute-start | bytes 393224 | tf_op jit(solution)/shard_map/ppermute | solution.py:36
  77.2 3.7 %copy-start = (bf16[2,2,2,16,1024]{4,3,2,1,0:T(8,128)(2,1)}, bf16[2,2,2,16,1024]{4,3,2,1,0:T(8,128)(2,1)S(1)}, u32[]{:S(2)}) copy-start(bf16[2,2,2,16,1024]{4,3,2,1,0:T(8,128)(2,1)S(1)} %maximum_select_fusion.3) | copy-start | bytes 786436
  77.2 2.2 %collective-permute-start.23 = (bf16[128,1024]{1,0:T(8,128)(2,1)S(1)}, bf16[128,1024]{1,0:T(8,128)(2,1)S(1)}, u32[]{:S(2)}, u32[]{:S(2)}) collective-permute-start(bf16[128,1024]{1,0:T(8,128)(2,1)S(1)} %bitcast.243), channel_id=1, source_target_pairs={{0,1},{1,0},{2,3},{3,2},{4,5},{5,4},{6,7},{7,6},{8,9},{9,8},{10,11... | collective-permute-start | bytes 786440 | tf_op jit(solution)/shard_map/ppermute | solution.py:53
  79.3 1.6 %copy-start.2 = (bf16[2,2,2,16,1024]{4,3,2,1,0:T(8,128)(2,1)}, bf16[2,2,2,16,1024]{4,3,2,1,0:T(8,128)(2,1)S(1)}, u32[]{:S(2)}) copy-start(bf16[2,2,2,16,1024]{4,3,2,1,0:T(8,128)(2,1)S(1)} %maximum_select_fusion.2) | copy-start | bytes 786436
  79.3 1.6 %collective-permute-start.22 = (bf16[128,1024]{1,0:T(8,128)(2,1)S(1)}, bf16[128,1024]{1,0:T(8,128)(2,1)S(1)}, u32[]{:S(2)}, u32[]{:S(2)}) collective-permute-start(bf16[128,1024]{1,0:T(8,128)(2,1)S(1)} %bitcast.247), channel_id=1, source_target_pairs={{0,1},{1,0},{2,3},{3,2},{4,5},{5,4},{6,7},{7,6},{8,9},{9,8},{10,11... | collective-permute-start | bytes 786440 | tf_op jit(solution)/shard_map/ppermute | solution.py:53
  79.4 1.5 %copy-start.4 = (bf16[128,1024]{1,0:T(8,128)(2,1)}, bf16[128,1024]{1,0:T(8,128)(2,1)S(1)}, u32[]{:S(2)}) copy-start(bf16[128,1024]{1,0:T(8,128)(2,1)S(1)} %collective-permute-done.23.refs_3_) | copy-start | bytes 786436
  80.9 0.7 copy-start.6
  91.2 2.1 %collective-permute-start.24 = (f32[128,1024]{1,0:T(8,128)}, f32[128,1024]{1,0:T(8,128)S(1)}, u32[]{:S(2)}, u32[]{:S(2)}) collective-permute-start(f32[128,1024]{1,0:T(8,128)} %get-tuple-element.18), channel_id=1, source_target_pairs={{0,1},{1,0},{2,3},{3,2},{4,5},{5,4},{6,7},{7,6},{8,9},{9,8},{10,11... | collective-permute-start | bytes 1572872 | tf_op jit(solution)/shard_map/ppermute | solution.py:63
  91.3 4.5 %collective-permute-start.28 = (f32[128,1024]{1,0:T(8,128)}, f32[128,1024]{1,0:T(8,128)S(1)}, u32[]{:S(2)}, u32[]{:S(2)}) collective-permute-start(f32[128,1024]{1,0:T(8,128)} %get-tuple-element.20), channel_id=1, source_target_pairs={{0,1},{1,0},{2,3},{3,2},{4,5},{5,4},{6,7},{7,6},{8,9},{9,8},{10,11... | collective-permute-start | bytes 1572872 | tf_op jit(solution)/shard_map/ppermute | solution.py:63
  94.5 6.4 %collective-permute-start.25 = (f32[2,2,16,1024]{3,2,1,0:T(8,128)S(1)}, f32[2,2,16,1024]{3,2,1,0:T(8,128)S(1)}, u32[]{:S(2)}, u32[]{:S(2)}) collective-permute-start(f32[2,2,16,1024]{3,2,1,0:T(8,128)S(1)} %bitcast_select_fusion.2), channel_id=1, source_target_pairs={{0,2},{1,5},{2,0},{3,7},{4,6},{5,1},{6,4},{7,3},{8,10},{9,13},{10,... | collective-permute-start | bytes 786440 | tf_op jit(solution)/shard_map/ppermute | solution.py:84
  97.0 7.4 %collective-permute-start.29 = (f32[2,2,16,1024]{3,2,1,0:T(8,128)S(1)}, f32[2,2,16,1024]{3,2,1,0:T(8,128)S(1)}, u32[]{:S(2)}, u32[]{:S(2)}) collective-permute-start(f32[2,2,16,1024]{3,2,1,0:T(8,128)S(1)} %bitcast_select_fusion), channel_id=1, source_target_pairs={{0,2},{1,5},{2,0},{3,7},{4,6},{5,1},{6,4},{7,3},{8,10},{9,13},{10,... | collective-permute-start | bytes 786440 | tf_op jit(solution)/shard_map/ppermute | solution.py:84
  101.0 5.0 %collective-permute-start.26 = (f32[2,16,1024]{2,1,0:T(8,128)S(1)}, f32[2,16,1024]{2,1,0:T(8,128)S(1)}, u32[]{:S(2)}, u32[]{:S(2)}) collective-permute-start(f32[2,16,1024]{2,1,0:T(8,128)S(1)} %dynamic-slice_bitcast_fusion.1), channel_id=1, source_target_pairs={{0,4},{1,3},{2,6},{3,1},{4,0},{5,7},{6,2},{7,5},{8,12},{9,11},{10,... | collective-permute-start | bytes 393224 | tf_op jit(solution)/shard_map/ppermute | solution.py:84
  104.5 5.7 %collective-permute-start.30 = (f32[2,16,1024]{2,1,0:T(8,128)S(1)}, f32[2,16,1024]{2,1,0:T(8,128)S(1)}, u32[]{:S(2)}, u32[]{:S(2)}) collective-permute-start(f32[2,16,1024]{2,1,0:T(8,128)S(1)} %dynamic-slice_bitcast_fusion), channel_id=1, source_target_pairs={{0,4},{1,3},{2,6},{3,1},{4,0},{5,7},{6,2},{7,5},{8,12},{9,11},{10,... | collective-permute-start | bytes 393224 | tf_op jit(solution)/shard_map/ppermute | solution.py:84
  106.1 7.3 %collective-permute-start.27 = (f32[16,1024]{1,0:T(8,128)S(1)}, f32[16,1024]{1,0:T(8,128)S(1)}, u32[]{:S(2)}, u32[]{:S(2)}) collective-permute-start(f32[16,1024]{1,0:T(8,128)S(1)} %dynamic-slice_bitcast_fusion.5), channel_id=1, source_target_pairs={{0,8},{1,9},{2,10},{3,11},{4,12},{5,13},{6,14},{7,15},{8,0},{9,1},... | collective-permute-start | bytes 196616 | tf_op jit(solution)/shard_map/ppermute | solution.py:84
  110.3 5.9 %collective-permute-start.31 = (f32[16,1024]{1,0:T(8,128)S(1)}, f32[16,1024]{1,0:T(8,128)S(1)}, u32[]{:S(2)}, u32[]{:S(2)}) collective-permute-start(f32[16,1024]{1,0:T(8,128)S(1)} %dynamic-slice_bitcast_fusion.4), channel_id=1, source_target_pairs={{0,8},{1,9},{2,10},{3,11},{4,12},{5,13},{6,14},{7,15},{8,0},{9,1},... | collective-permute-start | bytes 196616 | tf_op jit(solution)/shard_map/ppermute | solution.py:84

commit v18 on v16

--- a/solution.py
+++ b/solution.py
@@ -195,7 +195,11 @@
     resps = [rhs[:, state, :] / own_denom for state in range(states)]
     for step in range(ITERS):
         got = [gather_rows(resp.astype(jnp.bfloat16), n) for resp in resps]
-        keep, send = exchange_part(core, ordered_occ, [g[0] for g in got], [g[1] for g in got], vir_ints, rows)
+        if step < ITERS - 1:
+            calls = [exchange_part(core, ordered_occ, [g[0]], [g[1]], vir_ints, rows) for g in got]
+            keep, send = [c[0][0] for c in calls], [c[1][0] for c in calls]
+        else:
+            keep, send = exchange_part(core, ordered_occ, [g[0] for g in got], [g[1] for g in got], vir_ints, rows)
         for state in range(states):
             exchange = scatter_sum(keep[state], send[state], n)
             resps[state] = 0.4 * resps[state] + 0.6 * (rhs[:, state, :] - exchange) / own_denom

time: 115 us -> 116 us (level)
  Pallas kernels: 19.2 us -> 24.1 us
  waiting for transfers between devices: 45.5 us -> 40.7 us
  starting transfers between devices: 38.6 us -> 40.4 us
    pallas_call x2 -> x3, Pallas kernels: 19.2 us -> 24.1 us  [exchange_part(): pl.pallas_call(functools.partial(exchange_kernel, states, rows), grid=(lo...]
    ppermute x12, waiting for transfers between devices: 20.8 us -> 19.2 us  [scatter_sum(): acc = kept + lax.ppermute(sent, 'aux', partners(n, b0, b1))]
    ppermute x4, waiting for transfers between devices: 3.01 us -> 1.52 us  [gather_rows(): return (flat, lax.ppermute(flat, 'aux', partners(n, 0, 0)))]
  transfers between devices with their start and end apart: 32 -> 32, of which waited for: 26 -> 25; matrix products, arithmetic and copies ran while one was open for 5% -> 4% of each run, Pallas kernels for 0% -> 13%
where the time goes in v18:
time: 116 us
  waiting for transfers between devices  40.7 us (35%)
  starting transfers between devices  40.4 us (35%)
  Pallas kernels  24.1 us (21%)
  other arithmetic  6.12 us (5%)
  local copies, waits for them, and re-layouts  4.13 us (4%)
    pallas_call x3, Pallas kernels, exchange_part(): pl.pallas_call(functools.partial(exchange_kernel, states, rows), grid=(lo...  24.1 us
    ppermute x12, starting transfers between devices, scatter_sum(): acc = kept + lax.ppermute(sent, 'aux', partners(n, b0, b1))  20.1 us
    ppermute x12, waiting for transfers between devices, scatter_sum(): acc = kept + lax.ppermute(sent, 'aux', partners(n, b0, b1))  19.2 us
    ppermute x12, starting transfers between devices, gather_rows(): theirs = lax.ppermute(acc, 'aux', partners(n, b0, b1))  19 us
    ppermute x12, waiting for transfers between devices, gather_rows(): theirs = lax.ppermute(acc, 'aux', partners(n, b0, b1))  17.5 us
    add x4, other arithmetic, scatter_sum(): keep.reshape(shape)  3.4 us
    ppermute x4, waiting for transfers between devices, scatter_sum(): lax.ppermute(send, 'aux', partners(n, 0, 0)).reshape(shape)  2.51 us
  transfers between devices with their start and end apart: 32, of which 25 were waited for; matrix products, arithmetic and copies ran while one was open for 4% of the time, Pallas kernels for 13%

profile of v18, /device:TPU:0, one launch (start us, length us, event | category | flops | bytes accessed | tf_op | source)
XLA Modules:
  0.0 116.0 jit_solution(15557565669126751509)
XLA Ops:
  0.0 1.1 fusion.24
  1.1 0.9 select_reduce_fusion
  2.0 0.8 fusion.5
  2.7 4.1 %collective-permute-start.11 = (bf16[1,16,1024]{2,1,0:T(8,128)(2,1)S(1)}, bf16[1,16,1024]{2,1,0:T(8,128)(2,1)S(1)}, u32[]{:S(2)}, u32[]{:S(2)}) collective-permute-start(bf16[1,16,1024]{2,1,0:T(8,128)(2,1)S(1)} %get-tuple-element.55), channel_id=1, source_target_pairs={{0,8},{1,9},{2,10},{3,11},{4,12},{5,13},{6,14},{7,15},{8,0},{9,1},... | collective-permute-start | bytes 98312 | tf_op jit(solution)/shard_map/ppermute | solution.py:36
  6.9 2.2 %collective-permute-done.11 = bf16[1,16,1024]{2,1,0:T(8,128)(2,1)S(1)} collective-permute-done((bf16[1,16,1024]{2,1,0:T(8,128)(2,1)S(1)}, bf16[1,16,1024]{2,1,0:T(8,128)(2,1)S(1)}, u32[]{:S(2)}, u32[]{:S(2)}) %collective-permute-start.11) | collective-permute-done | bytes 32800 | tf_op jit(solution)/shard_map/ppermute | solution.py:36
  9.1 1.7 %collective-permute-start.12 = (bf16[2,16,1024]{2,1,0:T(8,128)(2,1)S(1)}, bf16[2,16,1024]{2,1,0:T(8,128)(2,1)S(1)}, u32[]{:S(2)}, u32[]{:S(2)}) collective-permute-start(bf16[2,16,1024]{2,1,0:T(8,128)(2,1)S(1)} %pad_maximum_fusion.7), channel_id=1, source_target_pairs={{0,4},{1,3},{2,6},{3,1},{4,0},{5,7},{6,2},{7,5},{8,12},{9,11},{10,... | collective-permute-start | bytes 196616 | tf_op jit(solution)/shard_map/ppermute | solution.py:36
  10.8 0.9 collective-permute-done
  11.7 1.6 %collective-permute-start.1 = (bf16[2,16,1024]{2,1,0:T(8,128)(2,1)S(1)}, bf16[2,16,1024]{2,1,0:T(8,128)(2,1)S(1)}, u32[]{:S(2)}, u32[]{:S(2)}) collective-permute-start(bf16[2,16,1024]{2,1,0:T(8,128)(2,1)S(1)} %pad_maximum_fusion.5), channel_id=1, source_target_pairs={{0,4},{1,3},{2,6},{3,1},{4,0},{5,7},{6,2},{7,5},{8,12},{9,11},{10,... | collective-permute-start | bytes 196616 | tf_op jit(solution)/shard_map/ppermute | solution.py:36
  13.3 0.1 collective-permute-done.12
  13.5 1.8 %collective-permute-start.13 = (bf16[4,16,1024]{2,1,0:T(8,128)(2,1)S(1)}, bf16[4,16,1024]{2,1,0:T(8,128)(2,1)S(1)}, u32[]{:S(2)}, u32[]{:S(2)}) collective-permute-start(bf16[4,16,1024]{2,1,0:T(8,128)(2,1)S(1)} %bitcast.237), channel_id=1, source_target_pairs={{0,2},{1,5},{2,0},{3,7},{4,6},{5,1},{6,4},{7,3},{8,10},{9,13},{10,... | collective-permute-start | bytes 393224 | tf_op jit(solution)/shard_map/ppermute | solution.py:36
  15.3 1.2 %collective-permute-done.1 = bf16[2,16,1024]{2,1,0:T(8,128)(2,1)S(1)} collective-permute-done((bf16[2,16,1024]{2,1,0:T(8,128)(2,1)S(1)}, bf16[2,16,1024]{2,1,0:T(8,128)(2,1)S(1)}, u32[]{:S(2)}, u32[]{:S(2)}) %collective-permute-start.1) | collective-permute-done | bytes 65568 | tf_op jit(solution)/shard_map/ppermute | solution.py:36
  16.6 1.1 collective-permute-start.2
  17.6 0.9 collective-permute-done.13
  18.7 2.9 %collective-permute-done.2 = bf16[4,16,1024]{2,1,0:T(8,128)(2,1)S(1)} collective-permute-done((bf16[4,16,1024]{2,1,0:T(8,128)(2,1)S(1)}, bf16[4,16,1024]{2,1,0:T(8,128)(2,1)S(1)}, u32[]{:S(2)}, u32[]{:S(2)}) %collective-permute-start.2) | collective-permute-done | bytes 131104 | tf_op jit(solution)/shard_map/ppermute | solution.py:36
  21.8 0.7 copy-done.6
  22.5 7.3 %shard_map.56 = (f32[128,1024]{1,0:T(8,128)}, f32[128,1024]{1,0:T(8,128)}) custom-call(s32[1]{0:T(128)} %bitcast.1.core_ref, bf16[4,256,256]{2,1,0:T(8,128)(2,1)} %occ_ref.5, bf16[128,1024]{1,0:T(8,128)(2,1)} %bitcast.232, bf16[128,1024]{1,0:T(8,128)(2,1)} %copy-done.6, bf16[4,1024,1024]{2,1,0:T(8,128)(2,1)} %refs_4_.1), custom_call_target="tpu_custom_call" | custom-call | tf_op jit(solution)/shard_map/pallas_call | solution.py:140
  29.8 0.5 collective-permute-start.15
  30.3 0.7 copy-done.7
  31.0 7.3 %shard_map.55 = (f32[128,1024]{1,0:T(8,128)}, f32[128,1024]{1,0:T(8,128)}) custom-call(s32[1]{0:T(128)} %bitcast.1.core_ref, bf16[4,256,256]{2,1,0:T(8,128)(2,1)} %occ_ref.5, bf16[128,1024]{1,0:T(8,128)(2,1)} %bitcast.234, bf16[128,1024]{1,0:T(8,128)(2,1)} %copy-done.7, bf16[4,1024,1024]{2,1,0:T(8,128)(2,1)} %refs_4_.1), custom_call_target="tpu_custom_call" | custom-call | tf_op jit(solution)/shard_map/pallas_call | solution.py:140
  38.4 1.1 collective-permute-start.16
  39.5 0.9 collective-permute-done.4
  40.4 1.1 add.140
  41.5 1.1 collective-permute-start.5
  42.6 2.3 %collective-permute-done.16 = f32[2,2,16,1024]{3,2,1,0:T(8,128)S(1)} collective-permute-done((f32[2,2,16,1024]{3,2,1,0:T(8,128)S(1)}, f32[2,2,16,1024]{3,2,1,0:T(8,128)S(1)}, u32[]{:S(2)}, u32[]{:S(2)}) %collective-permute-start.16) | collective-permute-done | bytes 262176 | tf_op jit(solution)/shard_map/ppermute | solution.py:84
  44.9 1.3 %collective-permute-start.17 = (f32[2,16,1024]{2,1,0:T(8,128)S(1)}, f32[2,16,1024]{2,1,0:T(8,128)S(1)}, u32[]{:S(2)}, u32[]{:S(2)}) collective-permute-start(f32[2,16,1024]{2,1,0:T(8,128)S(1)} %dynamic-slice_bitcast_fusion.2), channel_id=1, source_target_pairs={{0,4},{1,3},{2,6},{3,1},{4,0},{5,7},{6,2},{7,5},{8,12},{9,11},{10,... | collective-permute-start | bytes 393224 | tf_op jit(solution)/shard_map/ppermute | solution.py:84
  46.2 2.4 %collective-permute-done.5 = f32[2,2,16,1024]{3,2,1,0:T(8,128)S(1)} collective-permute-done((f32[2,2,16,1024]{3,2,1,0:T(8,128)S(1)}, f32[2,2,16,1024]{3,2,1,0:T(8,128)S(1)}, u32[]{:S(2)}, u32[]{:S(2)}) %collective-permute-start.5) | collective-permute-done | bytes 262176 | tf_op jit(solution)/shard_map/ppermute | solution.py:84
  48.7 1.3 %collective-permute-start.6 = (f32[2,16,1024]{2,1,0:T(8,128)S(1)}, f32[2,16,1024]{2,1,0:T(8,128)S(1)}, u32[]{:S(2)}, u32[]{:S(2)}) collective-permute-start(f32[2,16,1024]{2,1,0:T(8,128)S(1)} %dynamic-slice_bitcast_fusion.3), channel_id=1, source_target_pairs={{0,4},{1,3},{2,6},{3,1},{4,0},{5,7},{6,2},{7,5},{8,12},{9,11},{10,... | collective-permute-start | bytes 393224 | tf_op jit(solution)/shard_map/ppermute | solution.py:84
  50.1 2.7 %collective-permute-start.18 = (f32[16,1024]{1,0:T(8,128)S(1)}, f32[16,1024]{1,0:T(8,128)S(1)}, u32[]{:S(2)}, u32[]{:S(2)}) collective-permute-start(f32[16,1024]{1,0:T(8,128)S(1)} %dynamic-slice_bitcast_fusion.6), channel_id=1, source_target_pairs={{0,8},{1,9},{2,10},{3,11},{4,12},{5,13},{6,14},{7,15},{8,0},{9,1},... | collective-permute-start | bytes 196616 | tf_op jit(solution)/shard_map/ppermute | solution.py:84
  52.8 1.6 %collective-permute-done.6 = f32[2,16,1024]{2,1,0:T(8,128)S(1)} collective-permute-done((f32[2,16,1024]{2,1,0:T(8,128)S(1)}, f32[2,16,1024]{2,1,0:T(8,128)S(1)}, u32[]{:S(2)}, u32[]{:S(2)}) %collective-permute-start.6) | collective-permute-done | bytes 131104 | tf_op jit(solution)/shard_map/ppermute | solution.py:84
  54.5 2.1 %collective-permute-start.7 = (f32[16,1024]{1,0:T(8,128)S(1)}, f32[16,1024]{1,0:T(8,128)S(1)}, u32[]{:S(2)}, u32[]{:S(2)}) collective-permute-start(f32[16,1024]{1,0:T(8,128)S(1)} %dynamic-slice_bitcast_fusion.7), channel_id=1, source_target_pairs={{0,8},{1,9},{2,10},{3,11},{4,12},{5,13},{6,14},{7,15},{8,0},{9,1},... | collective-permute-start | bytes 196616 | tf_op jit(solution)/shard_map/ppermute | solution.py:84
  56.6 3.8 %collective-permute-done.7 = f32[16,1024]{1,0:T(8,128)S(1)} collective-permute-done((f32[16,1024]{1,0:T(8,128)S(1)}, f32[16,1024]{1,0:T(8,128)S(1)}, u32[]{:S(2)}, u32[]{:S(2)}) %collective-permute-start.7) | collective-permute-done | bytes 65568 | tf_op jit(solution)/shard_map/ppermute | solution.py:84
  60.5 1.5 %collective-permute-start.19 = (bf16[1,16,1024]{2,1,0:T(8,128)(2,1)S(1)}, bf16[1,16,1024]{2,1,0:T(8,128)(2,1)S(1)}, u32[]{:S(2)}, u32[]{:S(2)}) collective-permute-start(bf16[1,16,1024]{2,1,0:T(8,128)(2,1)S(1)} %get-tuple-element.21), channel_id=1, source_target_pairs={{0,8},{1,9},{2,10},{3,11},{4,12},{5,13},{6,14},{7,15},{8,0},{9,1},... | collective-permute-start | bytes 98312 | tf_op jit(solution)/shard_map/ppermute | solution.py:36
  62.0 1.5 %collective-permute-start.8 = (bf16[1,16,1024]{2,1,0:T(8,128)(2,1)S(1)}, bf16[1,16,1024]{2,1,0:T(8,128)(2,1)S(1)}, u32[]{:S(2)}, u32[]{:S(2)}) collective-permute-start(bf16[1,16,1024]{2,1,0:T(8,128)(2,1)S(1)} %get-tuple-element.53), channel_id=1, source_target_pairs={{0,8},{1,9},{2,10},{3,11},{4,12},{5,13},{6,14},{7,15},{8,0},{9,1},... | collective-permute-start | bytes 98312 | tf_op jit(solution)/shard_map/ppermute | solution.py:36
  63.5 1.9 %collective-permute-done.19 = bf16[1,16,1024]{2,1,0:T(8,128)(2,1)S(1)} collective-permute-done((bf16[1,16,1024]{2,1,0:T(8,128)(2,1)S(1)}, bf16[1,16,1024]{2,1,0:T(8,128)(2,1)S(1)}, u32[]{:S(2)}, u32[]{:S(2)}) %collective-permute-start.19) | collective-permute-done | bytes 32800 | tf_op jit(solution)/shard_map/ppermute | solution.py:36
  65.4 1.0 collective-permute-start.20
  66.4 0.4 collective-permute-done.8
  66.8 2.5 %collective-permute-start.9 = (bf16[2,16,1024]{2,1,0:T(8,128)(2,1)S(1)}, bf16[2,16,1024]{2,1,0:T(8,128)(2,1)S(1)}, u32[]{:S(2)}, u32[]{:S(2)}) collective-permute-start(bf16[2,16,1024]{2,1,0:T(8,128)(2,1)S(1)} %pad_maximum_fusion.6), channel_id=1, source_target_pairs={{0,4},{1,3},{2,6},{3,1},{4,0},{5,7},{6,2},{7,5},{8,12},{9,11},{10,... | collective-permute-start | bytes 196616 | tf_op jit(solution)/shard_map/ppermute | solution.py:36
  69.4 0.9 collective-permute-done.20
  70.2 2.1 %collective-permute-done.9 = bf16[2,16,1024]{2,1,0:T(8,128)(2,1)S(1)} collective-permute-done((bf16[2,16,1024]{2,1,0:T(8,128)(2,1)S(1)}, bf16[2,16,1024]{2,1,0:T(8,128)(2,1)S(1)}, u32[]{:S(2)}, u32[]{:S(2)}) %collective-permute-start.9) | collective-permute-done | bytes 65568 | tf_op jit(solution)/shard_map/ppermute | solution.py:36
  72.4 1.3 %collective-permute-start.21 = (bf16[4,16,1024]{2,1,0:T(8,128)(2,1)S(1)}, bf16[4,16,1024]{2,1,0:T(8,128)(2,1)S(1)}, u32[]{:S(2)}, u32[]{:S(2)}) collective-permute-start(bf16[4,16,1024]{2,1,0:T(8,128)(2,1)S(1)} %bitcast.240), channel_id=1, source_target_pairs={{0,2},{1,5},{2,0},{3,7},{4,6},{5,1},{6,4},{7,3},{8,10},{9,13},{10,... | collective-permute-start | bytes 393224 | tf_op jit(solution)/shard_map/ppermute | solution.py:36
  73.8 0.8 collective-permute-start.10
  74.6 2.8 %collective-permute-done.21 = bf16[4,16,1024]{2,1,0:T(8,128)(2,1)S(1)} collective-permute-done((bf16[4,16,1024]{2,1,0:T(8,128)(2,1)S(1)}, bf16[4,16,1024]{2,1,0:T(8,128)(2,1)S(1)}, u32[]{:S(2)}, u32[]{:S(2)}) %collective-permute-start.21) | collective-permute-done | bytes 131104 | tf_op jit(solution)/shard_map/ppermute | solution.py:36
  77.7 1.2 %collective-permute-done.10 = bf16[4,16,1024]{2,1,0:T(8,128)(2,1)S(1)} collective-permute-done((bf16[4,16,1024]{2,1,0:T(8,128)(2,1)S(1)}, bf16[4,16,1024]{2,1,0:T(8,128)(2,1)S(1)}, u32[]{:S(2)}, u32[]{:S(2)}) %collective-permute-start.10) | collective-permute-done | bytes 131104 | tf_op jit(solution)/shard_map/ppermute | solution.py:36
  79.1 0.1 collective-permute-done.23.refs_3_
  79.2 1.4 %collective-permute-done.22.refs_2_ = bf16[128,1024]{1,0:T(8,128)(2,1)S(1)} collective-permute-done((bf16[128,1024]{1,0:T(8,128)(2,1)S(1)}, bf16[128,1024]{1,0:T(8,128)(2,1)S(1)}, u32[]{:S(2)}, u32[]{:S(2)}) %collective-permute-start.22) | collective-permute-done | bytes 262176 | tf_op jit(solution)/shard_map/ppermute | solution.py:53
  80.6 0.7 copy-done.8
  81.3 9.6 %shard_map.57 = (f32[128,1024]{1,0:T(8,128)}, f32[128,1024]{1,0:T(8,128)}, f32[128,1024]{1,0:T(8,128)}, f32[128,1024]{1,0:T(8,128)}) custom-call(s32[1]{0:T(128)} %bitcast.1.core_ref, bf16[4,256,256]{2,1,0:T(8,128)(2,1)} %occ_ref.5, bf16[128,1024]{1,0:T(8,128)(2,1)} %bitcast.236, bf16[128,1024]{1,0:T(8,128)(2,1)} %bitcast.230, bf16[128,1024]{1,0:T(8,128)(2,1)} %copy-done.8, ...), custom_call_target="tpu_custom_call" | custom-call | tf_op jit(solution)/shard_map/pallas_call | solution.py:140
  90.9 0.1 collective-permute-start.24
  91.0 0.4 collective-permute-start.28
  91.4 1.6 %collective-permute-done.24 = f32[128,1024]{1,0:T(8,128)S(1)} collective-permute-done((f32[128,1024]{1,0:T(8,128)}, f32[128,1024]{1,0:T(8,128)S(1)}, u32[]{:S(2)}, u32[]{:S(2)}) %collective-permute-start.24) | collective-permute-done | bytes 524320 | tf_op jit(solution)/shard_map/ppermute | solution.py:63
  93.0 1.1 add.160
  94.1 1.3 %collective-permute-start.25 = (f32[2,2,16,1024]{3,2,1,0:T(8,128)S(1)}, f32[2,2,16,1024]{3,2,1,0:T(8,128)S(1)}, u32[]{:S(2)}, u32[]{:S(2)}) collective-permute-start(f32[2,2,16,1024]{3,2,1,0:T(8,128)S(1)} %bitcast_select_fusion.2), channel_id=1, source_target_pairs={{0,2},{1,5},{2,0},{3,7},{4,6},{5,1},{6,4},{7,3},{8,10},{9,13},{10,... | collective-permute-start | bytes 786440 | tf_op jit(solution)/shard_map/ppermute | solution.py:84
  95.5 1.1 add.166
  96.6 0.8 collective-permute-start.29
  97.5 3.1 %collective-permute-done.25 = f32[2,2,16,1024]{3,2,1,0:T(8,128)S(1)} collective-permute-done((f32[2,2,16,1024]{3,2,1,0:T(8,128)S(1)}, f32[2,2,16,1024]{3,2,1,0:T(8,128)S(1)}, u32[]{:S(2)}, u32[]{:S(2)}) %collective-permute-start.25) | collective-permute-done | bytes 262176 | tf_op jit(solution)/shard_map/ppermute | solution.py:84
  100.7 2.0 %collective-permute-start.26 = (f32[2,16,1024]{2,1,0:T(8,128)S(1)}, f32[2,16,1024]{2,1,0:T(8,128)S(1)}, u32[]{:S(2)}, u32[]{:S(2)}) collective-permute-start(f32[2,16,1024]{2,1,0:T(8,128)S(1)} %dynamic-slice_bitcast_fusion.1), channel_id=1, source_target_pairs={{0,4},{1,3},{2,6},{3,1},{4,0},{5,7},{6,2},{7,5},{8,12},{9,11},{10,... | collective-permute-start | bytes 393224 | tf_op jit(solution)/shard_map/ppermute | solution.py:84
  102.7 1.3 %collective-permute-done.29 = f32[2,2,16,1024]{3,2,1,0:T(8,128)S(1)} collective-permute-done((f32[2,2,16,1024]{3,2,1,0:T(8,128)S(1)}, f32[2,2,16,1024]{3,2,1,0:T(8,128)S(1)}, u32[]{:S(2)}, u32[]{:S(2)}) %collective-permute-start.29) | collective-permute-done | bytes 262176 | tf_op jit(solution)/shard_map/ppermute | solution.py:84
  104.0 2.2 %collective-permute-start.30 = (f32[2,16,1024]{2,1,0:T(8,128)S(1)}, f32[2,16,1024]{2,1,0:T(8,128)S(1)}, u32[]{:S(2)}, u32[]{:S(2)}) collective-permute-start(f32[2,16,1024]{2,1,0:T(8,128)S(1)} %dynamic-slice_bitcast_fusion), channel_id=1, source_target_pairs={{0,4},{1,3},{2,6},{3,1},{4,0},{5,7},{6,2},{7,5},{8,12},{9,11},{10,... | collective-permute-start | bytes 393224 | tf_op jit(solution)/shard_map/ppermute | solution.py:84
  106.2 1.8 %collective-permute-start.27 = (f32[16,1024]{1,0:T(8,128)S(1)}, f32[16,1024]{1,0:T(8,128)S(1)}, u32[]{:S(2)}, u32[]{:S(2)}) collective-permute-start(f32[16,1024]{1,0:T(8,128)S(1)} %dynamic-slice_bitcast_fusion.5), channel_id=1, source_target_pairs={{0,8},{1,9},{2,10},{3,11},{4,12},{5,13},{6,14},{7,15},{8,0},{9,1},... | collective-permute-start | bytes 196616 | tf_op jit(solution)/shard_map/ppermute | solution.py:84
  108.0 1.8 %collective-permute-done.30 = f32[2,16,1024]{2,1,0:T(8,128)S(1)} collective-permute-done((f32[2,16,1024]{2,1,0:T(8,128)S(1)}, f32[2,16,1024]{2,1,0:T(8,128)S(1)}, u32[]{:S(2)}, u32[]{:S(2)}) %collective-permute-start.30) | collective-permute-done | bytes 131104 | tf_op jit(solution)/shard_map/ppermute | solution.py:84
  109.9 2.4 %collective-permute-start.31 = (f32[16,1024]{1,0:T(8,128)S(1)}, f32[16,1024]{1,0:T(8,128)S(1)}, u32[]{:S(2)}, u32[]{:S(2)}) collective-permute-start(f32[16,1024]{1,0:T(8,128)S(1)} %dynamic-slice_bitcast_fusion.4), channel_id=1, source_target_pairs={{0,8},{1,9},{2,10},{3,11},{4,12},{5,13},{6,14},{7,15},{8,0},{9,1},... | collective-permute-start | bytes 196616 | tf_op jit(solution)/shard_map/ppermute | solution.py:84
  112.3 1.4 %collective-permute-done.27 = f32[16,1024]{1,0:T(8,128)S(1)} collective-permute-done((f32[16,1024]{1,0:T(8,128)S(1)}, f32[16,1024]{1,0:T(8,128)S(1)}, u32[]{:S(2)}, u32[]{:S(2)}) %collective-permute-start.27) | collective-permute-done | bytes 65568 | tf_op jit(solution)/shard_map/ppermute | solution.py:84
  113.7 1.4 %collective-permute-done.31 = f32[16,1024]{1,0:T(8,128)S(1)} collective-permute-done((f32[16,1024]{1,0:T(8,128)S(1)}, f32[16,1024]{1,0:T(8,128)S(1)}, u32[]{:S(2)}, u32[]{:S(2)}) %collective-permute-start.31) | collective-permute-done | bytes 65568 | tf_op jit(solution)/shard_map/ppermute | solution.py:84
  115.2 0.8 copy.54
  (81 shorter events, 1.8 us)
Async XLA Ops:
  2.7 6.3 %collective-permute-start.11 = (bf16[1,16,1024]{2,1,0:T(8,128)(2,1)S(1)}, bf16[1,16,1024]{2,1,0:T(8,128)(2,1)S(1)}, u32[]{:S(2)}, u32[]{:S(2)}) collective-permute-start(bf16[1,16,1024]{2,1,0:T(8,128)(2,1)S(1)} %get-tuple-element.55), channel_id=1, source_target_pairs={{0,8},{1,9},{2,10},{3,11},{4,12},{5,13},{6,14},{7,15},{8,0},{9,1},... | collective-permute-start | bytes 98312 | tf_op jit(solution)/shard_map/ppermute | solution.py:36
  6.8 4.8 %collective-permute-start = (bf16[1,16,1024]{2,1,0:T(8,128)(2,1)S(1)}, bf16[1,16,1024]{2,1,0:T(8,128)(2,1)S(1)}, u32[]{:S(2)}, u32[]{:S(2)}) collective-permute-start(bf16[1,16,1024]{2,1,0:T(8,128)(2,1)S(1)} %get-tuple-element.56), channel_id=1, source_target_pairs={{0,8},{1,9},{2,10},{3,11},{4,12},{5,13},{6,14},{7,15},{8,0},{9,1},... | collective-permute-start | bytes 98312 | tf_op jit(solution)/shard_map/ppermute | solution.py:36
  9.1 4.3 %collective-permute-start.12 = (bf16[2,16,1024]{2,1,0:T(8,128)(2,1)S(1)}, bf16[2,16,1024]{2,1,0:T(8,128)(2,1)S(1)}, u32[]{:S(2)}, u32[]{:S(2)}) collective-permute-start(bf16[2,16,1024]{2,1,0:T(8,128)(2,1)S(1)} %pad_maximum_fusion.7), channel_id=1, source_target_pairs={{0,4},{1,3},{2,6},{3,1},{4,0},{5,7},{6,2},{7,5},{8,12},{9,11},{10,... | collective-permute-start | bytes 196616 | tf_op jit(solution)/shard_map/ppermute | solution.py:36
  11.7 4.8 %collective-permute-start.1 = (bf16[2,16,1024]{2,1,0:T(8,128)(2,1)S(1)}, bf16[2,16,1024]{2,1,0:T(8,128)(2,1)S(1)}, u32[]{:S(2)}, u32[]{:S(2)}) collective-permute-start(bf16[2,16,1024]{2,1,0:T(8,128)(2,1)S(1)} %pad_maximum_fusion.5), channel_id=1, source_target_pairs={{0,4},{1,3},{2,6},{3,1},{4,0},{5,7},{6,2},{7,5},{8,12},{9,11},{10,... | collective-permute-start | bytes 196616 | tf_op jit(solution)/shard_map/ppermute | solution.py:36
  13.5 5.0 %collective-permute-start.13 = (bf16[4,16,1024]{2,1,0:T(8,128)(2,1)S(1)}, bf16[4,16,1024]{2,1,0:T(8,128)(2,1)S(1)}, u32[]{:S(2)}, u32[]{:S(2)}) collective-permute-start(bf16[4,16,1024]{2,1,0:T(8,128)(2,1)S(1)} %bitcast.237), channel_id=1, source_target_pairs={{0,2},{1,5},{2,0},{3,7},{4,6},{5,1},{6,4},{7,3},{8,10},{9,13},{10,... | collective-permute-start | bytes 393224 | tf_op jit(solution)/shard_map/ppermute | solution.py:36
  16.6 5.0 %collective-permute-start.2 = (bf16[4,16,1024]{2,1,0:T(8,128)(2,1)S(1)}, bf16[4,16,1024]{2,1,0:T(8,128)(2,1)S(1)}, u32[]{:S(2)}, u32[]{:S(2)}) collective-permute-start(bf16[4,16,1024]{2,1,0:T(8,128)(2,1)S(1)} %bitcast.238), channel_id=1, source_target_pairs={{0,2},{1,5},{2,0},{3,7},{4,6},{5,1},{6,4},{7,3},{8,10},{9,13},{10,... | collective-permute-start | bytes 393224 | tf_op jit(solution)/shard_map/ppermute | solution.py:36
  18.6 3.2 %copy-start.1 = (bf16[2,2,2,16,1024]{4,3,2,1,0:T(8,128)(2,1)}, bf16[2,2,2,16,1024]{4,3,2,1,0:T(8,128)(2,1)S(1)}, u32[]{:S(2)}) copy-start(bf16[2,2,2,16,1024]{4,3,2,1,0:T(8,128)(2,1)S(1)} %maximum_select_fusion.2) | copy-start | bytes 786436
  18.6 3.1 %collective-permute-start.14 = (bf16[128,1024]{1,0:T(8,128)(2,1)S(1)}, bf16[128,1024]{1,0:T(8,128)(2,1)S(1)}, u32[]{:S(2)}, u32[]{:S(2)}) collective-permute-start(bf16[128,1024]{1,0:T(8,128)(2,1)S(1)} %bitcast.231), channel_id=1, source_target_pairs={{0,1},{1,0},{2,3},{3,2},{4,5},{5,4},{6,7},{7,6},{8,9},{9,8},{10,11... | collective-permute-start | bytes 786440 | tf_op jit(solution)/shard_map/ppermute | solution.py:53
  21.7 8.6 %copy-start.2 = (bf16[2,2,2,16,1024]{4,3,2,1,0:T(8,128)(2,1)}, bf16[2,2,2,16,1024]{4,3,2,1,0:T(8,128)(2,1)S(1)}, u32[]{:S(2)}) copy-start(bf16[2,2,2,16,1024]{4,3,2,1,0:T(8,128)(2,1)S(1)} %maximum_select_fusion) | copy-start | bytes 786436
  21.7 8.6 %collective-permute-start.3 = (bf16[128,1024]{1,0:T(8,128)(2,1)S(1)}, bf16[128,1024]{1,0:T(8,128)(2,1)S(1)}, u32[]{:S(2)}, u32[]{:S(2)}) collective-permute-start(bf16[128,1024]{1,0:T(8,128)(2,1)S(1)} %bitcast.233), channel_id=1, source_target_pairs={{0,1},{1,0},{2,3},{3,2},{4,5},{5,4},{6,7},{7,6},{8,9},{9,8},{10,11... | collective-permute-start | bytes 786440 | tf_op jit(solution)/shard_map/ppermute | solution.py:53
  21.8 0.7 copy-start.6
  29.8 8.5 %copy-start.4 = (f32[128,1024]{1,0:T(8,128)S(1)}, f32[128,1024]{1,0:T(8,128)}, u32[]{:S(2)}) copy-start(f32[128,1024]{1,0:T(8,128)} %get-tuple-element.15) | copy-start | bytes 1572868
  29.8 30.6 %copy-start.9 = (f32[1024]{0:T(1024)S(1)}, f32[1024]{0:T(1024)}, u32[]{:S(2)}) copy-start(f32[1024]{0:T(1024)} %param.7) | copy-start | bytes 12292
  29.8 8.5 %collective-permute-start.15 = (f32[128,1024]{1,0:T(8,128)}, f32[128,1024]{1,0:T(8,128)S(1)}, u32[]{:S(2)}, u32[]{:S(2)}) collective-permute-start(f32[128,1024]{1,0:T(8,128)} %get-tuple-element.16), channel_id=1, source_target_pairs={{0,1},{1,0},{2,3},{3,2},{4,5},{5,4},{6,7},{7,6},{8,9},{9,8},{10,11... | collective-permute-start | bytes 1572872 | tf_op jit(solution)/shard_map/ppermute | solution.py:63
  30.3 0.7 copy-start.7
  38.2 2.1 %collective-permute-start.4 = (f32[128,1024]{1,0:T(8,128)}, f32[128,1024]{1,0:T(8,128)S(1)}, u32[]{:S(2)}, u32[]{:S(2)}) collective-permute-start(f32[128,1024]{1,0:T(8,128)} %get-tuple-element.14), channel_id=1, source_target_pairs={{0,1},{1,0},{2,3},{3,2},{4,5},{5,4},{6,7},{7,6},{8,9},{9,8},{10,11... | collective-permute-start | bytes 1572872 | tf_op jit(solution)/shard_map/ppermute | solution.py:63
  38.4 6.4 %collective-permute-start.16 = (f32[2,2,16,1024]{3,2,1,0:T(8,128)S(1)}, f32[2,2,16,1024]{3,2,1,0:T(8,128)S(1)}, u32[]{:S(2)}, u32[]{:S(2)}) collective-permute-start(f32[2,2,16,1024]{3,2,1,0:T(8,128)S(1)} %bitcast_select_fusion.4), channel_id=1, source_target_pairs={{0,2},{1,5},{2,0},{3,7},{4,6},{5,1},{6,4},{7,3},{8,10},{9,13},{10,... | collective-permute-start | bytes 786440 | tf_op jit(solution)/shard_map/ppermute | solution.py:84
  41.5 7.1 %collective-permute-start.5 = (f32[2,2,16,1024]{3,2,1,0:T(8,128)S(1)}, f32[2,2,16,1024]{3,2,1,0:T(8,128)S(1)}, u32[]{:S(2)}, u32[]{:S(2)}) collective-permute-start(f32[2,2,16,1024]{3,2,1,0:T(8,128)S(1)} %bitcast_select_fusion.6), channel_id=1, source_target_pairs={{0,2},{1,5},{2,0},{3,7},{4,6},{5,1},{6,4},{7,3},{8,10},{9,13},{10,... | collective-permute-start | bytes 786440 | tf_op jit(solution)/shard_map/ppermute | solution.py:84
  44.9 5.1 %collective-permute-start.17 = (f32[2,16,1024]{2,1,0:T(8,128)S(1)}, f32[2,16,1024]{2,1,0:T(8,128)S(1)}, u32[]{:S(2)}, u32[]{:S(2)}) collective-permute-start(f32[2,16,1024]{2,1,0:T(8,128)S(1)} %dynamic-slice_bitcast_fusion.2), channel_id=1, source_target_pairs={{0,4},{1,3},{2,6},{3,1},{4,0},{5,7},{6,2},{7,5},{8,12},{9,11},{10,... | collective-permute-start | bytes 393224 | tf_op jit(solution)/shard_map/ppermute | solution.py:84
  48.7 5.7 %collective-permute-start.6 = (f32[2,16,1024]{2,1,0:T(8,128)S(1)}, f32[2,16,1024]{2,1,0:T(8,128)S(1)}, u32[]{:S(2)}, u32[]{:S(2)}) collective-permute-start(f32[2,16,1024]{2,1,0:T(8,128)S(1)} %dynamic-slice_bitcast_fusion.3), channel_id=1, source_target_pairs={{0,4},{1,3},{2,6},{3,1},{4,0},{5,7},{6,2},{7,5},{8,12},{9,11},{10,... | collective-permute-start | bytes 393224 | tf_op jit(solution)/shard_map/ppermute | solution.py:84
  50.1 6.5 %collective-permute-start.18 = (f32[16,1024]{1,0:T(8,128)S(1)}, f32[16,1024]{1,0:T(8,128)S(1)}, u32[]{:S(2)}, u32[]{:S(2)}) collective-permute-start(f32[16,1024]{1,0:T(8,128)S(1)} %dynamic-slice_bitcast_fusion.6), channel_id=1, source_target_pairs={{0,8},{1,9},{2,10},{3,11},{4,12},{5,13},{6,14},{7,15},{8,0},{9,1},... | collective-permute-start | bytes 196616 | tf_op jit(solution)/shard_map/ppermute | solution.py:84
  54.5 5.9 %collective-permute-start.7 = (f32[16,1024]{1,0:T(8,128)S(1)}, f32[16,1024]{1,0:T(8,128)S(1)}, u32[]{:S(2)}, u32[]{:S(2)}) collective-permute-start(f32[16,1024]{1,0:T(8,128)S(1)} %dynamic-slice_bitcast_fusion.7), channel_id=1, source_target_pairs={{0,8},{1,9},{2,10},{3,11},{4,12},{5,13},{6,14},{7,15},{8,0},{9,1},... | collective-permute-start | bytes 196616 | tf_op jit(solution)/shard_map/ppermute | solution.py:84
  60.5 4.9 %collective-permute-start.19 = (bf16[1,16,1024]{2,1,0:T(8,128)(2,1)S(1)}, bf16[1,16,1024]{2,1,0:T(8,128)(2,1)S(1)}, u32[]{:S(2)}, u32[]{:S(2)}) collective-permute-start(bf16[1,16,1024]{2,1,0:T(8,128)(2,1)S(1)} %get-tuple-element.21), channel_id=1, source_target_pairs={{0,8},{1,9},{2,10},{3,11},{4,12},{5,13},{6,14},{7,15},{8,0},{9,1},... | collective-permute-start | bytes 98312 | tf_op jit(solution)/shard_map/ppermute | solution.py:36
  62.0 4.8 %collective-permute-start.8 = (bf16[1,16,1024]{2,1,0:T(8,128)(2,1)S(1)}, bf16[1,16,1024]{2,1,0:T(8,128)(2,1)S(1)}, u32[]{:S(2)}, u32[]{:S(2)}) collective-permute-start(bf16[1,16,1024]{2,1,0:T(8,128)(2,1)S(1)} %get-tuple-element.53), channel_id=1, source_target_pairs={{0,8},{1,9},{2,10},{3,11},{4,12},{5,13},{6,14},{7,15},{8,0},{9,1},... | collective-permute-start | bytes 98312 | tf_op jit(solution)/shard_map/ppermute | solution.py:36
  65.4 4.8 %collective-permute-start.20 = (bf16[2,16,1024]{2,1,0:T(8,128)(2,1)S(1)}, bf16[2,16,1024]{2,1,0:T(8,128)(2,1)S(1)}, u32[]{:S(2)}, u32[]{:S(2)}) collective-permute-start(bf16[2,16,1024]{2,1,0:T(8,128)(2,1)S(1)} %pad_maximum_fusion.8), channel_id=1, source_target_pairs={{0,4},{1,3},{2,6},{3,1},{4,0},{5,7},{6,2},{7,5},{8,12},{9,11},{10,... | collective-permute-start | bytes 196616 | tf_op jit(solution)/shard_map/ppermute | solution.py:36
  66.8 5.5 %collective-permute-start.9 = (bf16[2,16,1024]{2,1,0:T(8,128)(2,1)S(1)}, bf16[2,16,1024]{2,1,0:T(8,128)(2,1)S(1)}, u32[]{:S(2)}, u32[]{:S(2)}) collective-permute-start(bf16[2,16,1024]{2,1,0:T(8,128)(2,1)S(1)} %pad_maximum_fusion.6), channel_id=1, source_target_pairs={{0,4},{1,3},{2,6},{3,1},{4,0},{5,7},{6,2},{7,5},{8,12},{9,11},{10,... | collective-permute-start | bytes 196616 | tf_op jit(solution)/shard_map/ppermute | solution.py:36
  72.4 5.0 %collective-permute-start.21 = (bf16[4,16,1024]{2,1,0:T(8,128)(2,1)S(1)}, bf16[4,16,1024]{2,1,0:T(8,128)(2,1)S(1)}, u32[]{:S(2)}, u32[]{:S(2)}) collective-permute-start(bf16[4,16,1024]{2,1,0:T(8,128)(2,1)S(1)} %bitcast.240), channel_id=1, source_target_pairs={{0,2},{1,5},{2,0},{3,7},{4,6},{5,1},{6,4},{7,3},{8,10},{9,13},{10,... | collective-permute-start | bytes 393224 | tf_op jit(solution)/shard_map/ppermute | solution.py:36
  73.8 5.1 %collective-permute-start.10 = (bf16[4,16,1024]{2,1,0:T(8,128)(2,1)S(1)}, bf16[4,16,1024]{2,1,0:T(8,128)(2,1)S(1)}, u32[]{:S(2)}, u32[]{:S(2)}) collective-permute-start(bf16[4,16,1024]{2,1,0:T(8,128)(2,1)S(1)} %bitcast.239), channel_id=1, source_target_pairs={{0,2},{1,5},{2,0},{3,7},{4,6},{5,1},{6,4},{7,3},{8,10},{9,13},{10,... | collective-permute-start | bytes 393224 | tf_op jit(solution)/shard_map/ppermute | solution.py:36
  77.6 3.0 %copy-start = (bf16[2,2,2,16,1024]{4,3,2,1,0:T(8,128)(2,1)}, bf16[2,2,2,16,1024]{4,3,2,1,0:T(8,128)(2,1)S(1)}, u32[]{:S(2)}) copy-start(bf16[2,2,2,16,1024]{4,3,2,1,0:T(8,128)(2,1)S(1)} %maximum_select_fusion.3) | copy-start | bytes 786436
  77.6 1.6 %collective-permute-start.23 = (bf16[128,1024]{1,0:T(8,128)(2,1)S(1)}, bf16[128,1024]{1,0:T(8,128)(2,1)S(1)}, u32[]{:S(2)}, u32[]{:S(2)}) collective-permute-start(bf16[128,1024]{1,0:T(8,128)(2,1)S(1)} %bitcast.229), channel_id=1, source_target_pairs={{0,1},{1,0},{2,3},{3,2},{4,5},{5,4},{6,7},{7,6},{8,9},{9,8},{10,11... | collective-permute-start | bytes 786440 | tf_op jit(solution)/shard_map/ppermute | solution.py:53
  79.0 1.6 %copy-start.3 = (bf16[2,2,2,16,1024]{4,3,2,1,0:T(8,128)(2,1)}, bf16[2,2,2,16,1024]{4,3,2,1,0:T(8,128)(2,1)S(1)}, u32[]{:S(2)}) copy-start(bf16[2,2,2,16,1024]{4,3,2,1,0:T(8,128)(2,1)S(1)} %maximum_select_fusion.1) | copy-start | bytes 786436
  79.0 1.6 %collective-permute-start.22 = (bf16[128,1024]{1,0:T(8,128)(2,1)S(1)}, bf16[128,1024]{1,0:T(8,128)(2,1)S(1)}, u32[]{:S(2)}, u32[]{:S(2)}) collective-permute-start(bf16[128,1024]{1,0:T(8,128)(2,1)S(1)} %bitcast.235), channel_id=1, source_target_pairs={{0,1},{1,0},{2,3},{3,2},{4,5},{5,4},{6,7},{7,6},{8,9},{9,8},{10,11... | collective-permute-start | bytes 786440 | tf_op jit(solution)/shard_map/ppermute | solution.py:53
  79.2 1.4 %copy-start.5 = (bf16[128,1024]{1,0:T(8,128)(2,1)}, bf16[128,1024]{1,0:T(8,128)(2,1)S(1)}, u32[]{:S(2)}) copy-start(bf16[128,1024]{1,0:T(8,128)(2,1)S(1)} %collective-permute-done.23.refs_3_) | copy-start | bytes 786436
  80.6 0.7 copy-start.8
  90.9 2.1 %collective-permute-start.24 = (f32[128,1024]{1,0:T(8,128)}, f32[128,1024]{1,0:T(8,128)S(1)}, u32[]{:S(2)}, u32[]{:S(2)}) collective-permute-start(f32[128,1024]{1,0:T(8,128)} %get-tuple-element.18), channel_id=1, source_target_pairs={{0,1},{1,0},{2,3},{3,2},{4,5},{5,4},{6,7},{7,6},{8,9},{9,8},{10,11... | collective-permute-start | bytes 1572872 | tf_op jit(solution)/shard_map/ppermute | solution.py:63
  91.0 4.5 %collective-permute-start.28 = (f32[128,1024]{1,0:T(8,128)}, f32[128,1024]{1,0:T(8,128)S(1)}, u32[]{:S(2)}, u32[]{:S(2)}) collective-permute-start(f32[128,1024]{1,0:T(8,128)} %get-tuple-element.20), channel_id=1, source_target_pairs={{0,1},{1,0},{2,3},{3,2},{4,5},{5,4},{6,7},{7,6},{8,9},{9,8},{10,11... | collective-permute-start | bytes 1572872 | tf_op jit(solution)/shard_map/ppermute | solution.py:63
  94.1 6.4 %collective-permute-start.25 = (f32[2,2,16,1024]{3,2,1,0:T(8,128)S(1)}, f32[2,2,16,1024]{3,2,1,0:T(8,128)S(1)}, u32[]{:S(2)}, u32[]{:S(2)}) collective-permute-start(f32[2,2,16,1024]{3,2,1,0:T(8,128)S(1)} %bitcast_select_fusion.2), channel_id=1, source_target_pairs={{0,2},{1,5},{2,0},{3,7},{4,6},{5,1},{6,4},{7,3},{8,10},{9,13},{10,... | collective-permute-start | bytes 786440 | tf_op jit(solution)/shard_map/ppermute | solution.py:84
  96.6 7.3 %collective-permute-start.29 = (f32[2,2,16,1024]{3,2,1,0:T(8,128)S(1)}, f32[2,2,16,1024]{3,2,1,0:T(8,128)S(1)}, u32[]{:S(2)}, u32[]{:S(2)}) collective-permute-start(f32[2,2,16,1024]{3,2,1,0:T(8,128)S(1)} %bitcast_select_fusion), channel_id=1, source_target_pairs={{0,2},{1,5},{2,0},{3,7},{4,6},{5,1},{6,4},{7,3},{8,10},{9,13},{10,... | collective-permute-start | bytes 786440 | tf_op jit(solution)/shard_map/ppermute | solution.py:84
  100.7 5.5 %collective-permute-start.26 = (f32[2,16,1024]{2,1,0:T(8,128)S(1)}, f32[2,16,1024]{2,1,0:T(8,128)S(1)}, u32[]{:S(2)}, u32[]{:S(2)}) collective-permute-start(f32[2,16,1024]{2,1,0:T(8,128)S(1)} %dynamic-slice_bitcast_fusion.1), channel_id=1, source_target_pairs={{0,4},{1,3},{2,6},{3,1},{4,0},{5,7},{6,2},{7,5},{8,12},{9,11},{10,... | collective-permute-start | bytes 393224 | tf_op jit(solution)/shard_map/ppermute | solution.py:84
  104.0 5.9 %collective-permute-start.30 = (f32[2,16,1024]{2,1,0:T(8,128)S(1)}, f32[2,16,1024]{2,1,0:T(8,128)S(1)}, u32[]{:S(2)}, u32[]{:S(2)}) collective-permute-start(f32[2,16,1024]{2,1,0:T(8,128)S(1)} %dynamic-slice_bitcast_fusion), channel_id=1, source_target_pairs={{0,4},{1,3},{2,6},{3,1},{4,0},{5,7},{6,2},{7,5},{8,12},{9,11},{10,... | collective-permute-start | bytes 393224 | tf_op jit(solution)/shard_map/ppermute | solution.py:84
  106.2 7.5 %collective-permute-start.27 = (f32[16,1024]{1,0:T(8,128)S(1)}, f32[16,1024]{1,0:T(8,128)S(1)}, u32[]{:S(2)}, u32[]{:S(2)}) collective-permute-start(f32[16,1024]{1,0:T(8,128)S(1)} %dynamic-slice_bitcast_fusion.5), channel_id=1, source_target_pairs={{0,8},{1,9},{2,10},{3,11},{4,12},{5,13},{6,14},{7,15},{8,0},{9,1},... | collective-permute-start | bytes 196616 | tf_op jit(solution)/shard_map/ppermute | solution.py:84
  109.9 5.2 %collective-permute-start.31 = (f32[16,1024]{1,0:T(8,128)S(1)}, f32[16,1024]{1,0:T(8,128)S(1)}, u32[]{:S(2)}, u32[]{:S(2)}) collective-permute-start(f32[16,1024]{1,0:T(8,128)S(1)} %dynamic-slice_bitcast_fusion.4), channel_id=1, source_target_pairs={{0,8},{1,9},{2,10},{3,11},{4,12},{5,13},{6,14},{7,15},{8,0},{9,1},... | collective-permute-start | bytes 196616 | tf_op jit(solution)/shard_map/ppermute | solution.py:84

commit v19 on v16

--- a/solution.py
+++ b/solution.py
@@ -107,8 +107,6 @@
                     occ_buf[p, split + b * rows:split + (b + 1) * rows] = occ_ref[p, pl.ds(at_theirs, rows)]
         for s in range(states):
             cols = slice(s * nvir, (s + 1) * nvir)
-            keep[s][...] = jnp.zeros_like(keep[s])
-            send[s][...] = jnp.zeros_like(send[s])
             if rows:
                 core = core_ref[0]
                 for b in range(split // rows):
@@ -127,8 +125,16 @@
         term = lax.dot_general(
             half[:, s * nvir:(s + 1) * nvir], vir, (((1,), (1,)), ((), ())), preferred_element_type=jnp.float32
         )
-        keep[s][...] += term[:split]
-        send[s][...] += term[split:]
+
+        @pl.when(pl.program_id(0) == 0)
+        def _():
+            keep[s][...] = term[:split]
+            send[s][...] = term[split:]
+
+        @pl.when(pl.program_id(0) > 0)
+        def _():
+            keep[s][...] += term[:split]
+            send[s][...] += term[split:]
 
 
 def exchange_part(core, occ_ints, mine, theirs, vir_ints, rows):

time: 115 us -> 118 us (1.026)
  Pallas kernels: 19.2 us -> 22.2 us
    pallas_call x2, Pallas kernels: 19.2 us -> 22.2 us  [exchange_part(): pl.pallas_call(functools.partial(exchange_kernel, states, rows), grid=(lo...]
where the time goes in v19:
time: 118 us; the launch traced here: 117 us
  waiting for transfers between devices  45.4 us (38%)
  starting transfers between devices  38.6 us (33%)
  Pallas kernels  22.2 us (19%)
  other arithmetic  7.16 us (6%)
  local copies, waits for them, and re-layouts  3.39 us (3%)
    pallas_call x2, Pallas kernels, exchange_part(): pl.pallas_call(functools.partial(exchange_kernel, states, rows), grid=(lo...  22.2 us
    ppermute x12, waiting for transfers between devices, scatter_sum(): acc = kept + lax.ppermute(sent, 'aux', partners(n, b0, b1))  20.7 us
    ppermute x12, starting transfers between devices, scatter_sum(): acc = kept + lax.ppermute(sent, 'aux', partners(n, b0, b1))  19.2 us
    ppermute x12, waiting for transfers between devices, gather_rows(): theirs = lax.ppermute(acc, 'aux', partners(n, b0, b1))  18.4 us
    ppermute x12, starting transfers between devices, gather_rows(): theirs = lax.ppermute(acc, 'aux', partners(n, b0, b1))  18 us
    add x4, other arithmetic, scatter_sum(): keep.reshape(shape)  4.44 us
    ppermute x4, waiting for transfers between devices, scatter_sum(): lax.ppermute(send, 'aux', partners(n, 0, 0)).reshape(shape)  3.23 us
    ppermute x4, waiting for transfers between devices, gather_rows(): return (flat, lax.ppermute(flat, 'aux', partners(n, 0, 0)))  3.01 us
  transfers between devices with their start and end apart: 32, of which 26 were waited for; matrix products, arithmetic and copies ran while one was open for 5% of the time, Pallas kernels for 0%

profile of v19, /device:TPU:0, one launch (start us, length us, event | category | flops | bytes accessed | tf_op | source)
XLA Modules:
  0.0 117.2 jit_solution(1068164723177938849)
XLA Ops:
  0.0 1.1 fusion.24
  1.1 0.9 select_reduce_fusion
  2.0 0.8 fusion.5
  2.7 4.1 %collective-permute-start.3 = (bf16[1,16,1024]{2,1,0:T(8,128)(2,1)S(1)}, bf16[1,16,1024]{2,1,0:T(8,128)(2,1)S(1)}, u32[]{:S(2)}, u32[]{:S(2)}) collective-permute-start(bf16[1,16,1024]{2,1,0:T(8,128)(2,1)S(1)} %get-tuple-element.55), channel_id=1, source_target_pairs={{0,8},{1,9},{2,10},{3,11},{4,12},{5,13},{6,14},{7,15},{8,0},{9,1},... | collective-permute-start | bytes 98312 | tf_op jit(solution)/shard_map/ppermute | solution.py:36
  6.9 2.2 %collective-permute-done.3 = bf16[1,16,1024]{2,1,0:T(8,128)(2,1)S(1)} collective-permute-done((bf16[1,16,1024]{2,1,0:T(8,128)(2,1)S(1)}, bf16[1,16,1024]{2,1,0:T(8,128)(2,1)S(1)}, u32[]{:S(2)}, u32[]{:S(2)}) %collective-permute-start.3) | collective-permute-done | bytes 32800 | tf_op jit(solution)/shard_map/ppermute | solution.py:36
  9.1 1.7 %collective-permute-start.4 = (bf16[2,16,1024]{2,1,0:T(8,128)(2,1)S(1)}, bf16[2,16,1024]{2,1,0:T(8,128)(2,1)S(1)}, u32[]{:S(2)}, u32[]{:S(2)}) collective-permute-start(bf16[2,16,1024]{2,1,0:T(8,128)(2,1)S(1)} %pad_maximum_fusion.6), channel_id=1, source_target_pairs={{0,4},{1,3},{2,6},{3,1},{4,0},{5,7},{6,2},{7,5},{8,12},{9,11},{10,... | collective-permute-start | bytes 196616 | tf_op jit(solution)/shard_map/ppermute | solution.py:36
  10.8 0.9 collective-permute-done
  11.7 1.6 %collective-permute-start.1 = (bf16[2,16,1024]{2,1,0:T(8,128)(2,1)S(1)}, bf16[2,16,1024]{2,1,0:T(8,128)(2,1)S(1)}, u32[]{:S(2)}, u32[]{:S(2)}) collective-permute-start(bf16[2,16,1024]{2,1,0:T(8,128)(2,1)S(1)} %pad_maximum_fusion.5), channel_id=1, source_target_pairs={{0,4},{1,3},{2,6},{3,1},{4,0},{5,7},{6,2},{7,5},{8,12},{9,11},{10,... | collective-permute-start | bytes 196616 | tf_op jit(solution)/shard_map/ppermute | solution.py:36
  13.5 1.8 %collective-permute-start.5 = (bf16[4,16,1024]{2,1,0:T(8,128)(2,1)S(1)}, bf16[4,16,1024]{2,1,0:T(8,128)(2,1)S(1)}, u32[]{:S(2)}, u32[]{:S(2)}) collective-permute-start(bf16[4,16,1024]{2,1,0:T(8,128)(2,1)S(1)} %bitcast.237), channel_id=1, source_target_pairs={{0,2},{1,5},{2,0},{3,7},{4,6},{5,1},{6,4},{7,3},{8,10},{9,13},{10,... | collective-permute-start | bytes 393224 | tf_op jit(solution)/shard_map/ppermute | solution.py:36
  15.3 1.2 %collective-permute-done.1 = bf16[2,16,1024]{2,1,0:T(8,128)(2,1)S(1)} collective-permute-done((bf16[2,16,1024]{2,1,0:T(8,128)(2,1)S(1)}, bf16[2,16,1024]{2,1,0:T(8,128)(2,1)S(1)}, u32[]{:S(2)}, u32[]{:S(2)}) %collective-permute-start.1) | collective-permute-done | bytes 65568 | tf_op jit(solution)/shard_map/ppermute | solution.py:36
  16.6 1.1 collective-permute-start.2
  17.6 0.9 collective-permute-done.5
  18.7 2.9 %collective-permute-done.2 = bf16[4,16,1024]{2,1,0:T(8,128)(2,1)S(1)} collective-permute-done((bf16[4,16,1024]{2,1,0:T(8,128)(2,1)S(1)}, bf16[4,16,1024]{2,1,0:T(8,128)(2,1)S(1)}, u32[]{:S(2)}, u32[]{:S(2)}) %collective-permute-start.2) | collective-permute-done | bytes 131104 | tf_op jit(solution)/shard_map/ppermute | solution.py:36
  21.8 1.5 %collective-permute-done.6.refs_2_ = bf16[128,1024]{1,0:T(8,128)(2,1)S(1)} collective-permute-done((bf16[128,1024]{1,0:T(8,128)(2,1)S(1)}, bf16[128,1024]{1,0:T(8,128)(2,1)S(1)}, u32[]{:S(2)}, u32[]{:S(2)}) %collective-permute-start.6) | collective-permute-done | bytes 262176 | tf_op jit(solution)/shard_map/ppermute | solution.py:53
  23.3 0.7 copy-done.7
  24.0 11.1 %shard_map.55 = (f32[128,1024]{1,0:T(8,128)}, f32[128,1024]{1,0:T(8,128)}, f32[128,1024]{1,0:T(8,128)}, f32[128,1024]{1,0:T(8,128)}) custom-call(s32[1]{0:T(128)} %bitcast.1.core_ref, bf16[4,256,256]{2,1,0:T(8,128)(2,1)} %occ_ref.3, bf16[128,1024]{1,0:T(8,128)(2,1)} %bitcast.236, bf16[128,1024]{1,0:T(8,128)(2,1)} %bitcast.232, bf16[128,1024]{1,0:T(8,128)(2,1)} %copy-done.7, ...), custom_call_target="tpu_custom_call" | custom-call | tf_op jit(solution)/shard_map/pallas_call | solution.py:146
  35.1 0.1 collective-permute-start.8
  35.2 0.4 collective-permute-start.15
  35.6 1.6 %collective-permute-done.8 = f32[128,1024]{1,0:T(8,128)S(1)} collective-permute-done((f32[128,1024]{1,0:T(8,128)}, f32[128,1024]{1,0:T(8,128)S(1)}, u32[]{:S(2)}, u32[]{:S(2)}) %collective-permute-start.8) | collective-permute-done | bytes 524320 | tf_op jit(solution)/shard_map/ppermute | solution.py:63
  37.2 1.1 add.140
  38.4 1.1 collective-permute-start.9
  39.4 1.1 add.154
  40.6 1.1 collective-permute-start.16
  41.7 3.1 %collective-permute-done.9 = f32[2,2,16,1024]{3,2,1,0:T(8,128)S(1)} collective-permute-done((f32[2,2,16,1024]{3,2,1,0:T(8,128)S(1)}, f32[2,2,16,1024]{3,2,1,0:T(8,128)S(1)}, u32[]{:S(2)}, u32[]{:S(2)}) %collective-permute-start.9) | collective-permute-done | bytes 262176 | tf_op jit(solution)/shard_map/ppermute | solution.py:84
  44.9 1.3 %collective-permute-start.10 = (f32[2,16,1024]{2,1,0:T(8,128)S(1)}, f32[2,16,1024]{2,1,0:T(8,128)S(1)}, u32[]{:S(2)}, u32[]{:S(2)}) collective-permute-start(f32[2,16,1024]{2,1,0:T(8,128)S(1)} %dynamic-slice_bitcast_fusion.3), channel_id=1, source_target_pairs={{0,4},{1,3},{2,6},{3,1},{4,0},{5,7},{6,2},{7,5},{8,12},{9,11},{10,... | collective-permute-start | bytes 393224 | tf_op jit(solution)/shard_map/ppermute | solution.py:84
  46.2 2.1 %collective-permute-done.16 = f32[2,2,16,1024]{3,2,1,0:T(8,128)S(1)} collective-permute-done((f32[2,2,16,1024]{3,2,1,0:T(8,128)S(1)}, f32[2,2,16,1024]{3,2,1,0:T(8,128)S(1)}, u32[]{:S(2)}, u32[]{:S(2)}) %collective-permute-start.16) | collective-permute-done | bytes 262176 | tf_op jit(solution)/shard_map/ppermute | solution.py:84
  48.4 1.3 %collective-permute-start.17 = (f32[2,16,1024]{2,1,0:T(8,128)S(1)}, f32[2,16,1024]{2,1,0:T(8,128)S(1)}, u32[]{:S(2)}, u32[]{:S(2)}) collective-permute-start(f32[2,16,1024]{2,1,0:T(8,128)S(1)} %dynamic-slice_bitcast_fusion.2), channel_id=1, source_target_pairs={{0,4},{1,3},{2,6},{3,1},{4,0},{5,7},{6,2},{7,5},{8,12},{9,11},{10,... | collective-permute-start | bytes 393224 | tf_op jit(solution)/shard_map/ppermute | solution.py:84
  49.7 0.2 collective-permute-done.10
  50.0 2.8 %collective-permute-start.11 = (f32[16,1024]{1,0:T(8,128)S(1)}, f32[16,1024]{1,0:T(8,128)S(1)}, u32[]{:S(2)}, u32[]{:S(2)}) collective-permute-start(f32[16,1024]{1,0:T(8,128)S(1)} %dynamic-slice_bitcast_fusion.7), channel_id=1, source_target_pairs={{0,8},{1,9},{2,10},{3,11},{4,12},{5,13},{6,14},{7,15},{8,0},{9,1},... | collective-permute-start | bytes 196616 | tf_op jit(solution)/shard_map/ppermute | solution.py:84
  52.8 1.4 %collective-permute-done.17 = f32[2,16,1024]{2,1,0:T(8,128)S(1)} collective-permute-done((f32[2,16,1024]{2,1,0:T(8,128)S(1)}, f32[2,16,1024]{2,1,0:T(8,128)S(1)}, u32[]{:S(2)}, u32[]{:S(2)}) %collective-permute-start.17) | collective-permute-done | bytes 131104 | tf_op jit(solution)/shard_map/ppermute | solution.py:84
  54.2 2.1 %collective-permute-start.18 = (f32[16,1024]{1,0:T(8,128)S(1)}, f32[16,1024]{1,0:T(8,128)S(1)}, u32[]{:S(2)}, u32[]{:S(2)}) collective-permute-start(f32[16,1024]{1,0:T(8,128)S(1)} %dynamic-slice_bitcast_fusion.6), channel_id=1, source_target_pairs={{0,8},{1,9},{2,10},{3,11},{4,12},{5,13},{6,14},{7,15},{8,0},{9,1},... | collective-permute-start | bytes 196616 | tf_op jit(solution)/shard_map/ppermute | solution.py:84
  56.3 3.8 %collective-permute-done.18 = f32[16,1024]{1,0:T(8,128)S(1)} collective-permute-done((f32[16,1024]{1,0:T(8,128)S(1)}, f32[16,1024]{1,0:T(8,128)S(1)}, u32[]{:S(2)}, u32[]{:S(2)}) %collective-permute-start.18) | collective-permute-done | bytes 65568 | tf_op jit(solution)/shard_map/ppermute | solution.py:84
  60.2 1.5 %collective-permute-start.19 = (bf16[1,16,1024]{2,1,0:T(8,128)(2,1)S(1)}, bf16[1,16,1024]{2,1,0:T(8,128)(2,1)S(1)}, u32[]{:S(2)}, u32[]{:S(2)}) collective-permute-start(bf16[1,16,1024]{2,1,0:T(8,128)(2,1)S(1)} %get-tuple-element.21), channel_id=1, source_target_pairs={{0,8},{1,9},{2,10},{3,11},{4,12},{5,13},{6,14},{7,15},{8,0},{9,1},... | collective-permute-start | bytes 98312 | tf_op jit(solution)/shard_map/ppermute | solution.py:36
  61.7 1.5 %collective-permute-start.12 = (bf16[1,16,1024]{2,1,0:T(8,128)(2,1)S(1)}, bf16[1,16,1024]{2,1,0:T(8,128)(2,1)S(1)}, u32[]{:S(2)}, u32[]{:S(2)}) collective-permute-start(bf16[1,16,1024]{2,1,0:T(8,128)(2,1)S(1)} %get-tuple-element.53), channel_id=1, source_target_pairs={{0,8},{1,9},{2,10},{3,11},{4,12},{5,13},{6,14},{7,15},{8,0},{9,1},... | collective-permute-start | bytes 98312 | tf_op jit(solution)/shard_map/ppermute | solution.py:36
  63.2 2.2 %collective-permute-done.19 = bf16[1,16,1024]{2,1,0:T(8,128)(2,1)S(1)} collective-permute-done((bf16[1,16,1024]{2,1,0:T(8,128)(2,1)S(1)}, bf16[1,16,1024]{2,1,0:T(8,128)(2,1)S(1)}, u32[]{:S(2)}, u32[]{:S(2)}) %collective-permute-start.19) | collective-permute-done | bytes 32800 | tf_op jit(solution)/shard_map/ppermute | solution.py:36
  65.5 0.4 collective-permute-start.20
  65.9 0.6 collective-permute-done.12
  66.5 2.2 %collective-permute-start.13 = (bf16[2,16,1024]{2,1,0:T(8,128)(2,1)S(1)}, bf16[2,16,1024]{2,1,0:T(8,128)(2,1)S(1)}, u32[]{:S(2)}, u32[]{:S(2)}) collective-permute-start(bf16[2,16,1024]{2,1,0:T(8,128)(2,1)S(1)} %pad_maximum_fusion.7), channel_id=1, source_target_pairs={{0,4},{1,3},{2,6},{3,1},{4,0},{5,7},{6,2},{7,5},{8,12},{9,11},{10,... | collective-permute-start | bytes 196616 | tf_op jit(solution)/shard_map/ppermute | solution.py:36
  68.7 1.7 %collective-permute-done.20 = bf16[2,16,1024]{2,1,0:T(8,128)(2,1)S(1)} collective-permute-done((bf16[2,16,1024]{2,1,0:T(8,128)(2,1)S(1)}, bf16[2,16,1024]{2,1,0:T(8,128)(2,1)S(1)}, u32[]{:S(2)}, u32[]{:S(2)}) %collective-permute-start.20) | collective-permute-done | bytes 65568 | tf_op jit(solution)/shard_map/ppermute | solution.py:36
  70.4 1.4 %collective-permute-done.13 = bf16[2,16,1024]{2,1,0:T(8,128)(2,1)S(1)} collective-permute-done((bf16[2,16,1024]{2,1,0:T(8,128)(2,1)S(1)}, bf16[2,16,1024]{2,1,0:T(8,128)(2,1)S(1)}, u32[]{:S(2)}, u32[]{:S(2)}) %collective-permute-start.13) | collective-permute-done | bytes 65568 | tf_op jit(solution)/shard_map/ppermute | solution.py:36
  71.9 1.6 %collective-permute-start.21 = (bf16[4,16,1024]{2,1,0:T(8,128)(2,1)S(1)}, bf16[4,16,1024]{2,1,0:T(8,128)(2,1)S(1)}, u32[]{:S(2)}, u32[]{:S(2)}) collective-permute-start(bf16[4,16,1024]{2,1,0:T(8,128)(2,1)S(1)} %bitcast.240), channel_id=1, source_target_pairs={{0,2},{1,5},{2,0},{3,7},{4,6},{5,1},{6,4},{7,3},{8,10},{9,13},{10,... | collective-permute-start | bytes 393224 | tf_op jit(solution)/shard_map/ppermute | solution.py:36
  73.5 0.6 collective-permute-start.14
  74.1 2.8 %collective-permute-done.21 = bf16[4,16,1024]{2,1,0:T(8,128)(2,1)S(1)} collective-permute-done((bf16[4,16,1024]{2,1,0:T(8,128)(2,1)S(1)}, bf16[4,16,1024]{2,1,0:T(8,128)(2,1)S(1)}, u32[]{:S(2)}, u32[]{:S(2)}) %collective-permute-start.21) | collective-permute-done | bytes 131104 | tf_op jit(solution)/shard_map/ppermute | solution.py:36
  77.1 1.4 %collective-permute-done.14 = bf16[4,16,1024]{2,1,0:T(8,128)(2,1)S(1)} collective-permute-done((bf16[4,16,1024]{2,1,0:T(8,128)(2,1)S(1)}, bf16[4,16,1024]{2,1,0:T(8,128)(2,1)S(1)}, u32[]{:S(2)}, u32[]{:S(2)}) %collective-permute-start.14) | collective-permute-done | bytes 131104 | tf_op jit(solution)/shard_map/ppermute | solution.py:36
  78.7 1.5 %collective-permute-done.22.refs_2_ = bf16[128,1024]{1,0:T(8,128)(2,1)S(1)} collective-permute-done((bf16[128,1024]{1,0:T(8,128)(2,1)S(1)}, bf16[128,1024]{1,0:T(8,128)(2,1)S(1)}, u32[]{:S(2)}, u32[]{:S(2)}) %collective-permute-start.22) | collective-permute-done | bytes 262176 | tf_op jit(solution)/shard_map/ppermute | solution.py:53
  80.3 0.7 copy-done.6
  80.9 11.1 %shard_map.56 = (f32[128,1024]{1,0:T(8,128)}, f32[128,1024]{1,0:T(8,128)}, f32[128,1024]{1,0:T(8,128)}, f32[128,1024]{1,0:T(8,128)}) custom-call(s32[1]{0:T(128)} %bitcast.1.core_ref, bf16[4,256,256]{2,1,0:T(8,128)(2,1)} %occ_ref.3, bf16[128,1024]{1,0:T(8,128)(2,1)} %bitcast.234, bf16[128,1024]{1,0:T(8,128)(2,1)} %bitcast.230, bf16[128,1024]{1,0:T(8,128)(2,1)} %copy-done.6, ...), custom_call_target="tpu_custom_call" | custom-call | tf_op jit(solution)/shard_map/pallas_call | solution.py:146
  92.0 0.1 collective-permute-start.24
  92.2 0.4 collective-permute-start.28
  92.6 1.6 %collective-permute-done.24 = f32[128,1024]{1,0:T(8,128)S(1)} collective-permute-done((f32[128,1024]{1,0:T(8,128)}, f32[128,1024]{1,0:T(8,128)S(1)}, u32[]{:S(2)}, u32[]{:S(2)}) %collective-permute-start.24) | collective-permute-done | bytes 524320 | tf_op jit(solution)/shard_map/ppermute | solution.py:63
  94.2 1.1 add.160
  95.3 1.4 %collective-permute-start.25 = (f32[2,2,16,1024]{3,2,1,0:T(8,128)S(1)}, f32[2,2,16,1024]{3,2,1,0:T(8,128)S(1)}, u32[]{:S(2)}, u32[]{:S(2)}) collective-permute-start(f32[2,2,16,1024]{3,2,1,0:T(8,128)S(1)} %bitcast_select_fusion.2), channel_id=1, source_target_pairs={{0,2},{1,5},{2,0},{3,7},{4,6},{5,1},{6,4},{7,3},{8,10},{9,13},{10,... | collective-permute-start | bytes 786440 | tf_op jit(solution)/shard_map/ppermute | solution.py:84
  96.7 1.1 add.166
  97.9 0.8 collective-permute-start.29
  98.7 3.1 %collective-permute-done.25 = f32[2,2,16,1024]{3,2,1,0:T(8,128)S(1)} collective-permute-done((f32[2,2,16,1024]{3,2,1,0:T(8,128)S(1)}, f32[2,2,16,1024]{3,2,1,0:T(8,128)S(1)}, u32[]{:S(2)}, u32[]{:S(2)}) %collective-permute-start.25) | collective-permute-done | bytes 262176 | tf_op jit(solution)/shard_map/ppermute | solution.py:84
  101.8 1.8 %collective-permute-start.26 = (f32[2,16,1024]{2,1,0:T(8,128)S(1)}, f32[2,16,1024]{2,1,0:T(8,128)S(1)}, u32[]{:S(2)}, u32[]{:S(2)}) collective-permute-start(f32[2,16,1024]{2,1,0:T(8,128)S(1)} %dynamic-slice_bitcast_fusion.1), channel_id=1, source_target_pairs={{0,4},{1,3},{2,6},{3,1},{4,0},{5,7},{6,2},{7,5},{8,12},{9,11},{10,... | collective-permute-start | bytes 393224 | tf_op jit(solution)/shard_map/ppermute | solution.py:84
  103.7 1.6 %collective-permute-done.29 = f32[2,2,16,1024]{3,2,1,0:T(8,128)S(1)} collective-permute-done((f32[2,2,16,1024]{3,2,1,0:T(8,128)S(1)}, f32[2,2,16,1024]{3,2,1,0:T(8,128)S(1)}, u32[]{:S(2)}, u32[]{:S(2)}) %collective-permute-start.29) | collective-permute-done | bytes 262176 | tf_op jit(solution)/shard_map/ppermute | solution.py:84
  105.3 1.9 %collective-permute-start.30 = (f32[2,16,1024]{2,1,0:T(8,128)S(1)}, f32[2,16,1024]{2,1,0:T(8,128)S(1)}, u32[]{:S(2)}, u32[]{:S(2)}) collective-permute-start(f32[2,16,1024]{2,1,0:T(8,128)S(1)} %dynamic-slice_bitcast_fusion), channel_id=1, source_target_pairs={{0,4},{1,3},{2,6},{3,1},{4,0},{5,7},{6,2},{7,5},{8,12},{9,11},{10,... | collective-permute-start | bytes 393224 | tf_op jit(solution)/shard_map/ppermute | solution.py:84
  107.2 1.6 %collective-permute-start.27 = (f32[16,1024]{1,0:T(8,128)S(1)}, f32[16,1024]{1,0:T(8,128)S(1)}, u32[]{:S(2)}, u32[]{:S(2)}) collective-permute-start(f32[16,1024]{1,0:T(8,128)S(1)} %dynamic-slice_bitcast_fusion.5), channel_id=1, source_target_pairs={{0,8},{1,9},{2,10},{3,11},{4,12},{5,13},{6,14},{7,15},{8,0},{9,1},... | collective-permute-start | bytes 196616 | tf_op jit(solution)/shard_map/ppermute | solution.py:84
  108.9 2.2 %collective-permute-done.30 = f32[2,16,1024]{2,1,0:T(8,128)S(1)} collective-permute-done((f32[2,16,1024]{2,1,0:T(8,128)S(1)}, f32[2,16,1024]{2,1,0:T(8,128)S(1)}, u32[]{:S(2)}, u32[]{:S(2)}) %collective-permute-start.30) | collective-permute-done | bytes 131104 | tf_op jit(solution)/shard_map/ppermute | solution.py:84
  111.1 2.0 %collective-permute-start.31 = (f32[16,1024]{1,0:T(8,128)S(1)}, f32[16,1024]{1,0:T(8,128)S(1)}, u32[]{:S(2)}, u32[]{:S(2)}) collective-permute-start(f32[16,1024]{1,0:T(8,128)S(1)} %dynamic-slice_bitcast_fusion.4), channel_id=1, source_target_pairs={{0,8},{1,9},{2,10},{3,11},{4,12},{5,13},{6,14},{7,15},{8,0},{9,1},... | collective-permute-start | bytes 196616 | tf_op jit(solution)/shard_map/ppermute | solution.py:84
  113.1 1.6 %collective-permute-done.27 = f32[16,1024]{1,0:T(8,128)S(1)} collective-permute-done((f32[16,1024]{1,0:T(8,128)S(1)}, f32[16,1024]{1,0:T(8,128)S(1)}, u32[]{:S(2)}, u32[]{:S(2)}) %collective-permute-start.27) | collective-permute-done | bytes 65568 | tf_op jit(solution)/shard_map/ppermute | solution.py:84
  114.7 1.6 %collective-permute-done.31 = f32[16,1024]{1,0:T(8,128)S(1)} collective-permute-done((f32[16,1024]{1,0:T(8,128)S(1)}, f32[16,1024]{1,0:T(8,128)S(1)}, u32[]{:S(2)}, u32[]{:S(2)}) %collective-permute-start.31) | collective-permute-done | bytes 65568 | tf_op jit(solution)/shard_map/ppermute | solution.py:84
  116.4 0.8 copy.54
  (78 shorter events, 1.8 us)
Async XLA Ops:
  2.7 6.3 %collective-permute-start.3 = (bf16[1,16,1024]{2,1,0:T(8,128)(2,1)S(1)}, bf16[1,16,1024]{2,1,0:T(8,128)(2,1)S(1)}, u32[]{:S(2)}, u32[]{:S(2)}) collective-permute-start(bf16[1,16,1024]{2,1,0:T(8,128)(2,1)S(1)} %get-tuple-element.55), channel_id=1, source_target_pairs={{0,8},{1,9},{2,10},{3,11},{4,12},{5,13},{6,14},{7,15},{8,0},{9,1},... | collective-permute-start | bytes 98312 | tf_op jit(solution)/shard_map/ppermute | solution.py:36
  6.8 4.8 %collective-permute-start = (bf16[1,16,1024]{2,1,0:T(8,128)(2,1)S(1)}, bf16[1,16,1024]{2,1,0:T(8,128)(2,1)S(1)}, u32[]{:S(2)}, u32[]{:S(2)}) collective-permute-start(bf16[1,16,1024]{2,1,0:T(8,128)(2,1)S(1)} %get-tuple-element.56), channel_id=1, source_target_pairs={{0,8},{1,9},{2,10},{3,11},{4,12},{5,13},{6,14},{7,15},{8,0},{9,1},... | collective-permute-start | bytes 98312 | tf_op jit(solution)/shard_map/ppermute | solution.py:36
  9.1 4.3 %collective-permute-start.4 = (bf16[2,16,1024]{2,1,0:T(8,128)(2,1)S(1)}, bf16[2,16,1024]{2,1,0:T(8,128)(2,1)S(1)}, u32[]{:S(2)}, u32[]{:S(2)}) collective-permute-start(bf16[2,16,1024]{2,1,0:T(8,128)(2,1)S(1)} %pad_maximum_fusion.6), channel_id=1, source_target_pairs={{0,4},{1,3},{2,6},{3,1},{4,0},{5,7},{6,2},{7,5},{8,12},{9,11},{10,... | collective-permute-start | bytes 196616 | tf_op jit(solution)/shard_map/ppermute | solution.py:36
  11.7 4.8 %collective-permute-start.1 = (bf16[2,16,1024]{2,1,0:T(8,128)(2,1)S(1)}, bf16[2,16,1024]{2,1,0:T(8,128)(2,1)S(1)}, u32[]{:S(2)}, u32[]{:S(2)}) collective-permute-start(bf16[2,16,1024]{2,1,0:T(8,128)(2,1)S(1)} %pad_maximum_fusion.5), channel_id=1, source_target_pairs={{0,4},{1,3},{2,6},{3,1},{4,0},{5,7},{6,2},{7,5},{8,12},{9,11},{10,... | collective-permute-start | bytes 196616 | tf_op jit(solution)/shard_map/ppermute | solution.py:36
  13.5 5.0 %collective-permute-start.5 = (bf16[4,16,1024]{2,1,0:T(8,128)(2,1)S(1)}, bf16[4,16,1024]{2,1,0:T(8,128)(2,1)S(1)}, u32[]{:S(2)}, u32[]{:S(2)}) collective-permute-start(bf16[4,16,1024]{2,1,0:T(8,128)(2,1)S(1)} %bitcast.237), channel_id=1, source_target_pairs={{0,2},{1,5},{2,0},{3,7},{4,6},{5,1},{6,4},{7,3},{8,10},{9,13},{10,... | collective-permute-start | bytes 393224 | tf_op jit(solution)/shard_map/ppermute | solution.py:36
  16.6 5.0 %collective-permute-start.2 = (bf16[4,16,1024]{2,1,0:T(8,128)(2,1)S(1)}, bf16[4,16,1024]{2,1,0:T(8,128)(2,1)S(1)}, u32[]{:S(2)}, u32[]{:S(2)}) collective-permute-start(bf16[4,16,1024]{2,1,0:T(8,128)(2,1)S(1)} %bitcast.238), channel_id=1, source_target_pairs={{0,2},{1,5},{2,0},{3,7},{4,6},{5,1},{6,4},{7,3},{8,10},{9,13},{10,... | collective-permute-start | bytes 393224 | tf_op jit(solution)/shard_map/ppermute | solution.py:36
  18.6 4.7 %copy-start.1 = (bf16[2,2,2,16,1024]{4,3,2,1,0:T(8,128)(2,1)}, bf16[2,2,2,16,1024]{4,3,2,1,0:T(8,128)(2,1)S(1)}, u32[]{:S(2)}) copy-start(bf16[2,2,2,16,1024]{4,3,2,1,0:T(8,128)(2,1)S(1)} %maximum_select_fusion.1) | copy-start | bytes 786436
  18.6 3.1 %collective-permute-start.7 = (bf16[128,1024]{1,0:T(8,128)(2,1)S(1)}, bf16[128,1024]{1,0:T(8,128)(2,1)S(1)}, u32[]{:S(2)}, u32[]{:S(2)}) collective-permute-start(bf16[128,1024]{1,0:T(8,128)(2,1)S(1)} %bitcast.231), channel_id=1, source_target_pairs={{0,1},{1,0},{2,3},{3,2},{4,5},{5,4},{6,7},{7,6},{8,9},{9,8},{10,11... | collective-permute-start | bytes 786440 | tf_op jit(solution)/shard_map/ppermute | solution.py:53
  21.7 1.6 %copy-start.3 = (bf16[2,2,2,16,1024]{4,3,2,1,0:T(8,128)(2,1)}, bf16[2,2,2,16,1024]{4,3,2,1,0:T(8,128)(2,1)S(1)}, u32[]{:S(2)}) copy-start(bf16[2,2,2,16,1024]{4,3,2,1,0:T(8,128)(2,1)S(1)} %maximum_select_fusion) | copy-start | bytes 786436
  21.7 1.6 %collective-permute-start.6 = (bf16[128,1024]{1,0:T(8,128)(2,1)S(1)}, bf16[128,1024]{1,0:T(8,128)(2,1)S(1)}, u32[]{:S(2)}, u32[]{:S(2)}) collective-permute-start(bf16[128,1024]{1,0:T(8,128)(2,1)S(1)} %bitcast.235), channel_id=1, source_target_pairs={{0,1},{1,0},{2,3},{3,2},{4,5},{5,4},{6,7},{7,6},{8,9},{9,8},{10,11... | collective-permute-start | bytes 786440 | tf_op jit(solution)/shard_map/ppermute | solution.py:53
  21.8 1.5 %copy-start.5 = (bf16[128,1024]{1,0:T(8,128)(2,1)}, bf16[128,1024]{1,0:T(8,128)(2,1)S(1)}, u32[]{:S(2)}) copy-start(bf16[128,1024]{1,0:T(8,128)(2,1)S(1)} %collective-permute-done.7.refs_3_) | copy-start | bytes 786436
  23.3 0.7 copy-start.7
  24.0 36.1 %copy-start.8 = (f32[1024]{0:T(1024)S(1)}, f32[1024]{0:T(1024)}, u32[]{:S(2)}) copy-start(f32[1024]{0:T(1024)} %param.7) | copy-start | bytes 12292
  35.1 2.1 %collective-permute-start.8 = (f32[128,1024]{1,0:T(8,128)}, f32[128,1024]{1,0:T(8,128)S(1)}, u32[]{:S(2)}, u32[]{:S(2)}) collective-permute-start(f32[128,1024]{1,0:T(8,128)} %get-tuple-element.14), channel_id=1, source_target_pairs={{0,1},{1,0},{2,3},{3,2},{4,5},{5,4},{6,7},{7,6},{8,9},{9,8},{10,11... | collective-permute-start | bytes 1572872 | tf_op jit(solution)/shard_map/ppermute | solution.py:63
  35.2 4.2 %collective-permute-start.15 = (f32[128,1024]{1,0:T(8,128)}, f32[128,1024]{1,0:T(8,128)S(1)}, u32[]{:S(2)}, u32[]{:S(2)}) collective-permute-start(f32[128,1024]{1,0:T(8,128)} %get-tuple-element.16), channel_id=1, source_target_pairs={{0,1},{1,0},{2,3},{3,2},{4,5},{5,4},{6,7},{7,6},{8,9},{9,8},{10,11... | collective-permute-start | bytes 1572872 | tf_op jit(solution)/shard_map/ppermute | solution.py:63
  38.4 6.4 %collective-permute-start.9 = (f32[2,2,16,1024]{3,2,1,0:T(8,128)S(1)}, f32[2,2,16,1024]{3,2,1,0:T(8,128)S(1)}, u32[]{:S(2)}, u32[]{:S(2)}) collective-permute-start(f32[2,2,16,1024]{3,2,1,0:T(8,128)S(1)} %bitcast_select_fusion.6), channel_id=1, source_target_pairs={{0,2},{1,5},{2,0},{3,7},{4,6},{5,1},{6,4},{7,3},{8,10},{9,13},{10,... | collective-permute-start | bytes 786440 | tf_op jit(solution)/shard_map/ppermute | solution.py:84
  40.6 7.8 %collective-permute-start.16 = (f32[2,2,16,1024]{3,2,1,0:T(8,128)S(1)}, f32[2,2,16,1024]{3,2,1,0:T(8,128)S(1)}, u32[]{:S(2)}, u32[]{:S(2)}) collective-permute-start(f32[2,2,16,1024]{3,2,1,0:T(8,128)S(1)} %bitcast_select_fusion.4), channel_id=1, source_target_pairs={{0,2},{1,5},{2,0},{3,7},{4,6},{5,1},{6,4},{7,3},{8,10},{9,13},{10,... | collective-permute-start | bytes 786440 | tf_op jit(solution)/shard_map/ppermute | solution.py:84
  44.9 5.0 %collective-permute-start.10 = (f32[2,16,1024]{2,1,0:T(8,128)S(1)}, f32[2,16,1024]{2,1,0:T(8,128)S(1)}, u32[]{:S(2)}, u32[]{:S(2)}) collective-permute-start(f32[2,16,1024]{2,1,0:T(8,128)S(1)} %dynamic-slice_bitcast_fusion.3), channel_id=1, source_target_pairs={{0,4},{1,3},{2,6},{3,1},{4,0},{5,7},{6,2},{7,5},{8,12},{9,11},{10,... | collective-permute-start | bytes 393224 | tf_op jit(solution)/shard_map/ppermute | solution.py:84
  48.4 5.7 %collective-permute-start.17 = (f32[2,16,1024]{2,1,0:T(8,128)S(1)}, f32[2,16,1024]{2,1,0:T(8,128)S(1)}, u32[]{:S(2)}, u32[]{:S(2)}) collective-permute-start(f32[2,16,1024]{2,1,0:T(8,128)S(1)} %dynamic-slice_bitcast_fusion.2), channel_id=1, source_target_pairs={{0,4},{1,3},{2,6},{3,1},{4,0},{5,7},{6,2},{7,5},{8,12},{9,11},{10,... | collective-permute-start | bytes 393224 | tf_op jit(solution)/shard_map/ppermute | solution.py:84
  50.0 6.4 %collective-permute-start.11 = (f32[16,1024]{1,0:T(8,128)S(1)}, f32[16,1024]{1,0:T(8,128)S(1)}, u32[]{:S(2)}, u32[]{:S(2)}) collective-permute-start(f32[16,1024]{1,0:T(8,128)S(1)} %dynamic-slice_bitcast_fusion.7), channel_id=1, source_target_pairs={{0,8},{1,9},{2,10},{3,11},{4,12},{5,13},{6,14},{7,15},{8,0},{9,1},... | collective-permute-start | bytes 196616 | tf_op jit(solution)/shard_map/ppermute | solution.py:84
  54.2 5.9 %collective-permute-start.18 = (f32[16,1024]{1,0:T(8,128)S(1)}, f32[16,1024]{1,0:T(8,128)S(1)}, u32[]{:S(2)}, u32[]{:S(2)}) collective-permute-start(f32[16,1024]{1,0:T(8,128)S(1)} %dynamic-slice_bitcast_fusion.6), channel_id=1, source_target_pairs={{0,8},{1,9},{2,10},{3,11},{4,12},{5,13},{6,14},{7,15},{8,0},{9,1},... | collective-permute-start | bytes 196616 | tf_op jit(solution)/shard_map/ppermute | solution.py:84
  60.2 5.2 %collective-permute-start.19 = (bf16[1,16,1024]{2,1,0:T(8,128)(2,1)S(1)}, bf16[1,16,1024]{2,1,0:T(8,128)(2,1)S(1)}, u32[]{:S(2)}, u32[]{:S(2)}) collective-permute-start(bf16[1,16,1024]{2,1,0:T(8,128)(2,1)S(1)} %get-tuple-element.21), channel_id=1, source_target_pairs={{0,8},{1,9},{2,10},{3,11},{4,12},{5,13},{6,14},{7,15},{8,0},{9,1},... | collective-permute-start | bytes 98312 | tf_op jit(solution)/shard_map/ppermute | solution.py:36
  61.7 4.8 %collective-permute-start.12 = (bf16[1,16,1024]{2,1,0:T(8,128)(2,1)S(1)}, bf16[1,16,1024]{2,1,0:T(8,128)(2,1)S(1)}, u32[]{:S(2)}, u32[]{:S(2)}) collective-permute-start(bf16[1,16,1024]{2,1,0:T(8,128)(2,1)S(1)} %get-tuple-element.53), channel_id=1, source_target_pairs={{0,8},{1,9},{2,10},{3,11},{4,12},{5,13},{6,14},{7,15},{8,0},{9,1},... | collective-permute-start | bytes 98312 | tf_op jit(solution)/shard_map/ppermute | solution.py:36
  65.5 4.9 %collective-permute-start.20 = (bf16[2,16,1024]{2,1,0:T(8,128)(2,1)S(1)}, bf16[2,16,1024]{2,1,0:T(8,128)(2,1)S(1)}, u32[]{:S(2)}, u32[]{:S(2)}) collective-permute-start(bf16[2,16,1024]{2,1,0:T(8,128)(2,1)S(1)} %pad_maximum_fusion.8), channel_id=1, source_target_pairs={{0,4},{1,3},{2,6},{3,1},{4,0},{5,7},{6,2},{7,5},{8,12},{9,11},{10,... | collective-permute-start | bytes 196616 | tf_op jit(solution)/shard_map/ppermute | solution.py:36
  66.5 5.3 %collective-permute-start.13 = (bf16[2,16,1024]{2,1,0:T(8,128)(2,1)S(1)}, bf16[2,16,1024]{2,1,0:T(8,128)(2,1)S(1)}, u32[]{:S(2)}, u32[]{:S(2)}) collective-permute-start(bf16[2,16,1024]{2,1,0:T(8,128)(2,1)S(1)} %pad_maximum_fusion.7), channel_id=1, source_target_pairs={{0,4},{1,3},{2,6},{3,1},{4,0},{5,7},{6,2},{7,5},{8,12},{9,11},{10,... | collective-permute-start | bytes 196616 | tf_op jit(solution)/shard_map/ppermute | solution.py:36
  71.9 5.0 %collective-permute-start.21 = (bf16[4,16,1024]{2,1,0:T(8,128)(2,1)S(1)}, bf16[4,16,1024]{2,1,0:T(8,128)(2,1)S(1)}, u32[]{:S(2)}, u32[]{:S(2)}) collective-permute-start(bf16[4,16,1024]{2,1,0:T(8,128)(2,1)S(1)} %bitcast.240), channel_id=1, source_target_pairs={{0,2},{1,5},{2,0},{3,7},{4,6},{5,1},{6,4},{7,3},{8,10},{9,13},{10,... | collective-permute-start | bytes 393224 | tf_op jit(solution)/shard_map/ppermute | solution.py:36
  73.5 5.0 %collective-permute-start.14 = (bf16[4,16,1024]{2,1,0:T(8,128)(2,1)S(1)}, bf16[4,16,1024]{2,1,0:T(8,128)(2,1)S(1)}, u32[]{:S(2)}, u32[]{:S(2)}) collective-permute-start(bf16[4,16,1024]{2,1,0:T(8,128)(2,1)S(1)} %bitcast.239), channel_id=1, source_target_pairs={{0,2},{1,5},{2,0},{3,7},{4,6},{5,1},{6,4},{7,3},{8,10},{9,13},{10,... | collective-permute-start | bytes 393224 | tf_op jit(solution)/shard_map/ppermute | solution.py:36
  77.0 3.2 %copy-start = (bf16[2,2,2,16,1024]{4,3,2,1,0:T(8,128)(2,1)}, bf16[2,2,2,16,1024]{4,3,2,1,0:T(8,128)(2,1)S(1)}, u32[]{:S(2)}) copy-start(bf16[2,2,2,16,1024]{4,3,2,1,0:T(8,128)(2,1)S(1)} %maximum_select_fusion.3) | copy-start | bytes 786436
  77.0 1.7 %collective-permute-start.23 = (bf16[128,1024]{1,0:T(8,128)(2,1)S(1)}, bf16[128,1024]{1,0:T(8,128)(2,1)S(1)}, u32[]{:S(2)}, u32[]{:S(2)}) collective-permute-start(bf16[128,1024]{1,0:T(8,128)(2,1)S(1)} %bitcast.229), channel_id=1, source_target_pairs={{0,1},{1,0},{2,3},{3,2},{4,5},{5,4},{6,7},{7,6},{8,9},{9,8},{10,11... | collective-permute-start | bytes 786440 | tf_op jit(solution)/shard_map/ppermute | solution.py:53
  78.6 1.6 %copy-start.2 = (bf16[2,2,2,16,1024]{4,3,2,1,0:T(8,128)(2,1)}, bf16[2,2,2,16,1024]{4,3,2,1,0:T(8,128)(2,1)S(1)}, u32[]{:S(2)}) copy-start(bf16[2,2,2,16,1024]{4,3,2,1,0:T(8,128)(2,1)S(1)} %maximum_select_fusion.2) | copy-start | bytes 786436
  78.6 1.6 %collective-permute-start.22 = (bf16[128,1024]{1,0:T(8,128)(2,1)S(1)}, bf16[128,1024]{1,0:T(8,128)(2,1)S(1)}, u32[]{:S(2)}, u32[]{:S(2)}) collective-permute-start(bf16[128,1024]{1,0:T(8,128)(2,1)S(1)} %bitcast.233), channel_id=1, source_target_pairs={{0,1},{1,0},{2,3},{3,2},{4,5},{5,4},{6,7},{7,6},{8,9},{9,8},{10,11... | collective-permute-start | bytes 786440 | tf_op jit(solution)/shard_map/ppermute | solution.py:53
  78.7 1.5 %copy-start.4 = (bf16[128,1024]{1,0:T(8,128)(2,1)}, bf16[128,1024]{1,0:T(8,128)(2,1)S(1)}, u32[]{:S(2)}) copy-start(bf16[128,1024]{1,0:T(8,128)(2,1)S(1)} %collective-permute-done.23.refs_3_) | copy-start | bytes 786436
  80.2 0.7 copy-start.6
  92.0 2.1 %collective-permute-start.24 = (f32[128,1024]{1,0:T(8,128)}, f32[128,1024]{1,0:T(8,128)S(1)}, u32[]{:S(2)}, u32[]{:S(2)}) collective-permute-start(f32[128,1024]{1,0:T(8,128)} %get-tuple-element.18), channel_id=1, source_target_pairs={{0,1},{1,0},{2,3},{3,2},{4,5},{5,4},{6,7},{7,6},{8,9},{9,8},{10,11... | collective-permute-start | bytes 1572872 | tf_op jit(solution)/shard_map/ppermute | solution.py:63
  92.2 4.5 %collective-permute-start.28 = (f32[128,1024]{1,0:T(8,128)}, f32[128,1024]{1,0:T(8,128)S(1)}, u32[]{:S(2)}, u32[]{:S(2)}) collective-permute-start(f32[128,1024]{1,0:T(8,128)} %get-tuple-element.20), channel_id=1, source_target_pairs={{0,1},{1,0},{2,3},{3,2},{4,5},{5,4},{6,7},{7,6},{8,9},{9,8},{10,11... | collective-permute-start | bytes 1572872 | tf_op jit(solution)/shard_map/ppermute | solution.py:63
  95.3 6.4 %collective-permute-start.25 = (f32[2,2,16,1024]{3,2,1,0:T(8,128)S(1)}, f32[2,2,16,1024]{3,2,1,0:T(8,128)S(1)}, u32[]{:S(2)}, u32[]{:S(2)}) collective-permute-start(f32[2,2,16,1024]{3,2,1,0:T(8,128)S(1)} %bitcast_select_fusion.2), channel_id=1, source_target_pairs={{0,2},{1,5},{2,0},{3,7},{4,6},{5,1},{6,4},{7,3},{8,10},{9,13},{10,... | collective-permute-start | bytes 786440 | tf_op jit(solution)/shard_map/ppermute | solution.py:84
  97.9 7.4 %collective-permute-start.29 = (f32[2,2,16,1024]{3,2,1,0:T(8,128)S(1)}, f32[2,2,16,1024]{3,2,1,0:T(8,128)S(1)}, u32[]{:S(2)}, u32[]{:S(2)}) collective-permute-start(f32[2,2,16,1024]{3,2,1,0:T(8,128)S(1)} %bitcast_select_fusion), channel_id=1, source_target_pairs={{0,2},{1,5},{2,0},{3,7},{4,6},{5,1},{6,4},{7,3},{8,10},{9,13},{10,... | collective-permute-start | bytes 786440 | tf_op jit(solution)/shard_map/ppermute | solution.py:84
  101.8 5.3 %collective-permute-start.26 = (f32[2,16,1024]{2,1,0:T(8,128)S(1)}, f32[2,16,1024]{2,1,0:T(8,128)S(1)}, u32[]{:S(2)}, u32[]{:S(2)}) collective-permute-start(f32[2,16,1024]{2,1,0:T(8,128)S(1)} %dynamic-slice_bitcast_fusion.1), channel_id=1, source_target_pairs={{0,4},{1,3},{2,6},{3,1},{4,0},{5,7},{6,2},{7,5},{8,12},{9,11},{10,... | collective-permute-start | bytes 393224 | tf_op jit(solution)/shard_map/ppermute | solution.py:84
  105.3 5.7 %collective-permute-start.30 = (f32[2,16,1024]{2,1,0:T(8,128)S(1)}, f32[2,16,1024]{2,1,0:T(8,128)S(1)}, u32[]{:S(2)}, u32[]{:S(2)}) collective-permute-start(f32[2,16,1024]{2,1,0:T(8,128)S(1)} %dynamic-slice_bitcast_fusion), channel_id=1, source_target_pairs={{0,4},{1,3},{2,6},{3,1},{4,0},{5,7},{6,2},{7,5},{8,12},{9,11},{10,... | collective-permute-start | bytes 393224 | tf_op jit(solution)/shard_map/ppermute | solution.py:84
  107.2 7.5 %collective-permute-start.27 = (f32[16,1024]{1,0:T(8,128)S(1)}, f32[16,1024]{1,0:T(8,128)S(1)}, u32[]{:S(2)}, u32[]{:S(2)}) collective-permute-start(f32[16,1024]{1,0:T(8,128)S(1)} %dynamic-slice_bitcast_fusion.5), channel_id=1, source_target_pairs={{0,8},{1,9},{2,10},{3,11},{4,12},{5,13},{6,14},{7,15},{8,0},{9,1},... | collective-permute-start | bytes 196616 | tf_op jit(solution)/shard_map/ppermute | solution.py:84
  111.1 5.2 %collective-permute-start.31 = (f32[16,1024]{1,0:T(8,128)S(1)}, f32[16,1024]{1,0:T(8,128)S(1)}, u32[]{:S(2)}, u32[]{:S(2)}) collective-permute-start(f32[16,1024]{1,0:T(8,128)S(1)} %dynamic-slice_bitcast_fusion.4), channel_id=1, source_target_pairs={{0,8},{1,9},{2,10},{3,11},{4,12},{5,13},{6,14},{7,15},{8,0},{9,1},... | collective-permute-start | bytes 196616 | tf_op jit(solution)/shard_map/ppermute | solution.py:84
